TPU v7x, 32 devices: a whole 2x2x4 slice. The times are simulated.
32 devices in a mesh: req: 2 (over x), seq: 16 (over z, y, core).
Axes of the slice: x: 2, y: 2, z: 4, core: 2. Of those that a mesh axis runs over, the one named last changes fastest.
Arguments:
- states: bfloat16 [4, 4, 4544], P(None, 'req', 'seq'), may hold values from -6 to 6
- kv_cache: bfloat16 [4, 8192, 128], P('req', 'seq'), may hold values from -48 to 48, as said below
- lengths: int32 [4], replicated, may hold values from 1 to 8188, as said below
- placement: int32 [4], replicated, may hold values from 0 to 3, each once
- norm_gain: bfloat16 [4544], replicated, may hold values from 0.25 to 1.75
- norm_bias: bfloat16 [4544], replicated, may hold values from -1.5 to 1.5
- w_query: bfloat16 [4544, 4544], P('req', 'seq'), may hold values from -0.09375 to 0.09375
- w_keyval: bfloat16 [4544, 128], P('req'), may hold values from -0.09375 to 0.09375
- w_out: bfloat16 [4544, 4544], P('seq', 'req'), may hold values from -0.09375 to 0.09375
- w_up: bfloat16 [4544, 18176], P('req', 'seq'), may hold values from -0.09375 to 0.09375
- w_down: bfloat16 [18176, 4544], P('seq', 'req'), may hold values from -0.046875 to 0.046875
Outputs:
- new_states: bfloat16 [4, 4, 4544], P(None, 'req', 'seq')
- new_cache: bfloat16 [4, 8192, 128], P('req', 'seq')
Inputs may be any that keep to these rules, and one draw needn't show every extreme that they name: Request r's cache holds its first lengths[r] positions; some request has exactly 8188. `kv_cache`: row i is the cache of request placement[i]; positions at or beyond that request's length hold arbitrary values. `placement`: each request is served by exactly one slot.
All inputs are finite; a program needn't handle non-finite values.
Results may differ from a plain program's by a relative error of at most 0.012.
The roundings to bfloat16 on the way count: a program that leaves them out, or rounds other values in their place, can miss the bound.
Values may be sent and summed in bfloat16 or wider, within the bound.
No kernel may reach another device: no remote copies, remote signals or barrier semaphores. Data moves between devices by JAX's collectives and lax.ppermute only.
A program may use at most 192 MiB of HBM per device.

v0:
```python
import jax
import jax.numpy as jnp
from jax import lax
from jax.sharding import PartitionSpec as P

STEPS = 4


EPSILON = 1e-05
NEGATIVE = -1e30


def joined_2(part, axis, combine):
    gathered = jax.tree.map(lambda a: lax.all_gather(a, axis), part)

    def take(source):
        return jax.tree.map(lambda a: lax.dynamic_index_in_dim(a, source, 0, False), gathered)

    return lax.fori_loop(
        1, lax.axis_size(axis), lambda source, state: combine(state, take(source)), take(0)
    )


def layer_norm(row_block, norm_gain, norm_bias):
    values = row_block.astype(jnp.float32)
    average = jnp.mean(values, axis=-1, keepdims=True)
    centered = values - average
    spread = jnp.mean(centered * centered, axis=-1, keepdims=True)
    scaled = centered * lax.rsqrt(spread + EPSILON)
    return (scaled * norm_gain.astype(jnp.float32) + norm_bias.astype(jnp.float32)).astype(
        jnp.bfloat16
    )


def rotate(vectors, positions):
    head_width = vectors.shape[-1]
    half_width = head_width // 2
    frequency = 10000.0 ** (-(jnp.arange(half_width, dtype=jnp.float32) * 2.0) / head_width)
    angles = positions.astype(jnp.float32)[:, None] * frequency[None, :]
    cosine = jnp.concatenate([jnp.cos(angles), jnp.cos(angles)], axis=-1)[:, None, :]
    sine_wave = jnp.concatenate([jnp.sin(angles), jnp.sin(angles)], axis=-1)[:, None, :]
    turned = jnp.concatenate([-vectors[..., half_width:], vectors[..., :half_width]], axis=-1)
    return vectors * cosine + turned * sine_wave


def combine_parts(earlier, later):
    peak_first, total_first, weighted_first = earlier
    peak_second, total_second, weighted_second = later
    peak_score = jnp.maximum(peak_first, peak_second)
    scale_first = jnp.exp(peak_first - peak_score)
    scale_second = jnp.exp(peak_second - peak_score)
    weight_total = total_first * scale_first + total_second * scale_second
    weighted = weighted_first * scale_first[:, :, None] + weighted_second * scale_second[:, :, None]
    return (peak_score, weight_total, weighted)


def shards(
    states,
    kv_cache,
    lengths,
    placement,
    norm_gain,
    norm_bias,
    w_query,
    w_keyval,
    w_out,
    w_up,
    w_down,
):
    group_rows = kv_cache.shape[0]
    seg_length = kv_cache.shape[1]
    head_width = kv_cache.shape[2] // 2
    model_width = norm_gain.shape[0]
    head_count = model_width // head_width
    slice_width = states.shape[2]
    group_index = lax.axis_index("req")
    shard_index = lax.axis_index("seq")
    own_requests = lax.dynamic_slice_in_dim(placement, group_index * group_rows, group_rows, 0)
    slot_lengths = jnp.take(lengths, own_requests)
    every_request = lax.all_gather(states, "req", axis=1, tiled=True)
    own_states = jnp.take(every_request, own_requests, axis=1)
    full_states = lax.all_gather(own_states, "seq", axis=2, tiled=True)
    query_cols, keyval_cols, up_cols, out_rows, down_rows = (
        lax.all_gather(w_query, "req", axis=0, tiled=True),
        lax.all_gather(w_keyval, "req", axis=0, tiled=True),
        lax.all_gather(w_up, "req", axis=0, tiled=True),
        lax.all_gather(w_out, "req", axis=1, tiled=True),
        lax.all_gather(w_down, "req", axis=1, tiled=True),
    )
    first_matrix = jnp.concatenate([query_cols, keyval_cols, up_cols], axis=1)
    second_matrix = jnp.concatenate([out_rows, down_rows], axis=0)
    local_slots = jnp.arange(seg_length, dtype=jnp.int32)
    global_positions = shard_index * seg_length + local_slots
    cache_now = kv_cache
    outputs = []
    for step_index in range(STEPS):
        current = own_states[step_index]
        normed = layer_norm(full_states[step_index], norm_gain, norm_bias)
        first_out = jnp.dot(normed, first_matrix, preferred_element_type=jnp.float32)
        query_part = first_out[:, :slice_width].astype(jnp.bfloat16)
        keyval = first_out[:, slice_width : slice_width + 2 * head_width]
        up_part = first_out[:, slice_width + 2 * head_width :]
        positions = slot_lengths + step_index
        query_all = lax.all_gather(query_part, "seq", axis=1, tiled=True)
        query_rows = rotate(
            query_all.astype(jnp.float32).reshape(group_rows, head_count, head_width), positions
        ).astype(jnp.bfloat16)
        new_key = rotate(keyval[:, None, :head_width], positions)[:, 0, :]
        new_entry = jnp.concatenate([new_key, keyval[:, head_width:]], axis=-1).astype(jnp.bfloat16)
        write_mask = local_slots[None, :] == (positions - shard_index * seg_length)[:, None]
        cache_now = jnp.where(write_mask[:, :, None], new_entry[:, None, :], cache_now)
        key_rows = cache_now[:, :, :head_width]
        value_rows = cache_now[:, :, head_width:]
        scores = jnp.einsum(
            "ghd,gsd->ghs", query_rows, key_rows, preferred_element_type=jnp.float32
        ) * head_width ** (-0.5)
        valid_mask = (global_positions[None, :] <= positions[:, None])[:, None, :]
        highest = jnp.max(jnp.where(valid_mask, scores, NEGATIVE), axis=-1)
        weights = jnp.where(valid_mask, jnp.exp(scores - highest[:, :, None]), 0.0)
        weight_total = jnp.sum(weights, axis=-1)
        weighted = jnp.einsum(
            "ghs,gsd->ghd", weights, value_rows, preferred_element_type=jnp.float32
        )
        peak_score, denominator, numerator = joined_2(
            (highest, weight_total, weighted), "seq", combine_parts
        )
        mixed_all = (
            (numerator / denominator[:, :, None])
            .reshape(group_rows, model_width)
            .astype(jnp.bfloat16)
        )
        mixed_part = lax.dynamic_slice_in_dim(mixed_all, shard_index * slice_width, slice_width, 1)
        hidden = jax.nn.gelu(up_part, approximate=False).astype(jnp.bfloat16)
        joined = jnp.concatenate([mixed_part, hidden], axis=1)
        partial_sum = jnp.dot(joined, second_matrix, preferred_element_type=jnp.float32)
        update = lax.psum_scatter(partial_sum, "seq", scatter_dimension=1, tiled=True)
        outputs.append((current.astype(jnp.float32) + update).astype(jnp.bfloat16))
    stacked = jnp.stack(outputs)
    slot_states = lax.all_gather(stacked, "req", axis=1, tiled=True)
    request_total = placement.shape[0]
    inverse = (
        jnp.zeros((request_total,), jnp.int32)
        .at[placement]
        .set(jnp.arange(request_total, dtype=jnp.int32))
    )
    own_inverse = lax.dynamic_slice_in_dim(inverse, group_index * group_rows, group_rows, 0)
    return (jnp.take(slot_states, own_inverse, axis=1), cache_now)


def solution(mesh):
    in_specs = (
        P(None, "req", "seq"),
        P("req", "seq", None),
        P(),
        P(),
        P(),
        P(),
        P("req", "seq"),
        P("req", None),
        P("seq", "req"),
        P("req", "seq"),
        P("seq", "req"),
    )
    out_specs = (P(None, "req", "seq"), P("req", "seq", None))
    return jax.shard_map(shards, mesh=mesh, in_specs=in_specs, out_specs=out_specs, check_vma=False)
```

profile of v0, /device:TPU:2, one launch (start us, length us, event | category | flops | bytes accessed | tf_op | source)
XLA Modules:
  0.0 747.2 jit_solution(15381080556855086247)
XLA Ops:
  10.0 8.6 %copy.124 = bf16[1136,2272]{0,1:T(8,128)(2,1)} copy(bf16[1136,2272]{1,0:T(8,128)(2,1)} %param.31) | data formatting | bytes 10323968 | tf_op args[10]
  18.7 4.5 all_gather.108
  24.1 31.8 %all_gather.109 = bf16[4,2,4544]{0,1,2:T(2,128)(2,1)S(1)} all-gather(bf16[4,2,284]{0,1,2:T(2,128)(2,1)S(1)} %copy.114), channel_id=1, replica_groups=mesh['req'=2,'seq'=16] {'seq'}, dimensions={2}, use_global_device_ids=true | all-gather | bytes 77248 | tf_op jit(solution)/shard_map/all_gather | solution.py:82
  55.9 10.2 %fusion.177 = (bf16[1,2,4544]{0,1,2:T(2,128)(2,1)S(1)}, bf16[1,2,4544]{0,1,2:T(2,128)(2,1)}, f32[1,2,4544]{0,1,2:T(2,128)}, bf16[1,2,4544]{0,1,2:T(2,128)(2,1)}) fusion(bf16[4,2,4544]{0,1,2:T(2,128)(2,1)S(1)} %all_gather.109), kind=kLoop, calls=%fused_computation.365 | loop fusion | flops 9088 | bytes 163584 | tf_op jit(solution)/shard_map/slice | solution.py:98
  66.1 5.3 fusion.48
  72.0 5.5 copy.138
  79.0 5.1 copy.167
  85.2 5.1 copy.166
  91.3 0.9 copy.119
  92.2 2.4 copy.165
  100.7 6.1 copy.123
  106.8 5.8 reshape.547
  112.7 3.0 copy.125
  115.6 3.9 copy.150
  119.5 125.6 %all-gather.34.cloned.1.call-done = bf16[4544,1136]{1,0:T(8,128)(2,1)} async-done(((bf16[2272,1136]{1,0:T(8,128)(2,1)}), bf16[4544,1136]{1,0:T(8,128)(2,1)}) %all-gather.34.cloned.1.call-update) | async-done | bytes 10323984 | tf_op jit(solution)/shard_map/all_gather | solution.py:86
  245.1 25.6 %concatenate.126 = bf16[4544,1548]{1,0:T(8,128)(2,1)} concatenate(bf16[4544,284]{1,0:T(8,128)(2,1)S(1)} %bitcast.276, bf16[4544,128]{1,0:T(8,128)(2,1)} %all-gather.32.cloned.1.call-done, bf16[4544,1136]{1,0:T(8,128)(2,1)} %all-gather.34.cloned.1.call-done), dimensions={1} | concatenate | bytes 28136448 | tf_op jit(solution)/shard_map/concatenate | solution.py:90
  270.7 7.6 %fusion.179 = (bf16[2,1548]{1,0:T(2,128)(2,1)S(1)}, f32[2,1548]{1,0:T(2,128)S(1)}) fusion(bf16[4544,1548]{1,0:T(8,128)(2,1)} %concatenate.126, f32[1,2,4544]{2,1,0:T(2,128)} %copy-done.6, f32[2]{0:T(128)} %add_rsqrt_fusion, f32[2]{0:T(128)} %copy-done.26, f32[4544]{0:T(1024)S(1)} %convert_element_type.189, f32[4544]{0:T(1024)S(1)} %convert_element_type.188), kind=kOutput, calls=%fused_computation.367 | convolution fusion | flops 28184984 | bytes 14159520 | tf_op jit(solution)/shard_map/dot_general | solution.py:99
  278.5 1.8 copy-done.2
  280.3 2.1 fusion.180
  282.7 2.1 fusion.181
  285.2 2.1 fusion.182
  287.5 21.6 %all-gather.23 = bf16[16,284,2]{1,2,0:T(2,128)(2,1)S(1)} all-gather(bf16[1,284,2]{1,2,0:T(2,128)(2,1)S(1)} %slice_bitcast_fusion), channel_id=1, replica_groups=mesh['req'=2,'seq'=16] {'seq'}, dimensions={0}, use_global_device_ids=true | all-gather | bytes 19312 | tf_op jit(solution)/shard_map/all_gather | solution.py:104
  311.4 17.5 %all-gather.20 = bf16[16,284,2]{1,2,0:T(2,128)(2,1)S(1)} all-gather(bf16[1,284,2]{1,2,0:T(2,128)(2,1)S(1)} %slice_bitcast_fusion.1), channel_id=1, replica_groups=mesh['req'=2,'seq'=16] {'seq'}, dimensions={0}, use_global_device_ids=true | all-gather | bytes 19312 | tf_op jit(solution)/shard_map/all_gather | solution.py:104
  330.0 19.1 %all-gather.17 = bf16[16,284,2]{1,2,0:T(2,128)(2,1)S(1)} all-gather(bf16[1,284,2]{1,2,0:T(2,128)(2,1)S(1)} %slice_bitcast_fusion.2), channel_id=1, replica_groups=mesh['req'=2,'seq'=16] {'seq'}, dimensions={0}, use_global_device_ids=true | all-gather | bytes 19312 | tf_op jit(solution)/shard_map/all_gather | solution.py:104
  350.3 17.5 %all-gather.13 = bf16[16,284,2]{1,2,0:T(2,128)(2,1)S(1)} all-gather(bf16[1,284,2]{1,2,0:T(2,128)(2,1)S(1)} %slice_bitcast_fusion.3), channel_id=1, replica_groups=mesh['req'=2,'seq'=16] {'seq'}, dimensions={0}, use_global_device_ids=true | all-gather | bytes 19312 | tf_op jit(solution)/shard_map/all_gather | solution.py:104
  368.9 18.8 %all-gather.24 = f32[16,2,71]{2,1,0:T(2,128)S(1)} all-gather(f32[1,2,71]{2,1,0:T(2,128)S(1)} %bitcast.291), channel_id=11, replica_groups=mesh['req'=2,'seq'=16] {'seq'}, dimensions={0}, use_global_device_ids=true | all-gather | bytes 9656 | tf_op jit(solution)/shard_map/all_gather | solution.py:14
  387.7 17.4 %all-gather.25 = f32[16,2,71]{2,1,0:T(2,128)S(1)} all-gather(f32[1,2,71]{2,1,0:T(2,128)S(1)} %bitcast.295), channel_id=12, replica_groups=mesh['req'=2,'seq'=16] {'seq'}, dimensions={0}, use_global_device_ids=true | all-gather | bytes 9656 | tf_op jit(solution)/shard_map/all_gather | solution.py:14
  405.1 21.9 %all-gather.11 = f32[32,71,64]{1,2,0:T(8,128)S(1)} all-gather(f32[2,71,64]{1,2,0:T(8,128)S(1)} %fusion.18), channel_id=13, replica_groups=mesh['req'=2,'seq'=16] {'seq'}, dimensions={0}, use_global_device_ids=true | all-gather | bytes 617984 | tf_op jit(solution)/shard_map/all_gather | solution.py:14
  427.1 4.4 while.79
  431.7 18.0 %all-gather.21 = f32[16,2,71]{2,1,0:T(2,128)S(1)} all-gather(f32[1,2,71]{2,1,0:T(2,128)S(1)} %bitcast.290), channel_id=8, replica_groups=mesh['req'=2,'seq'=16] {'seq'}, dimensions={0}, use_global_device_ids=true | all-gather | bytes 9656 | tf_op jit(solution)/shard_map/all_gather | solution.py:14
  449.8 18.2 %all-gather.22 = f32[16,2,71]{2,1,0:T(2,128)S(1)} all-gather(f32[1,2,71]{2,1,0:T(2,128)S(1)} %bitcast.294), channel_id=9, replica_groups=mesh['req'=2,'seq'=16] {'seq'}, dimensions={0}, use_global_device_ids=true | all-gather | bytes 9656 | tf_op jit(solution)/shard_map/all_gather | solution.py:14
  468.0 21.1 %all-gather.8 = f32[32,71,64]{1,2,0:T(8,128)S(1)} all-gather(f32[2,71,64]{1,2,0:T(8,128)S(1)} %fusion.16), channel_id=10, replica_groups=mesh['req'=2,'seq'=16] {'seq'}, dimensions={0}, use_global_device_ids=true | all-gather | bytes 617984 | tf_op jit(solution)/shard_map/all_gather | solution.py:14
  489.1 4.4 while.78
  493.8 18.5 %all-gather.18 = f32[16,2,71]{2,1,0:T(2,128)S(1)} all-gather(f32[1,2,71]{2,1,0:T(2,128)S(1)} %bitcast.289), channel_id=5, replica_groups=mesh['req'=2,'seq'=16] {'seq'}, dimensions={0}, use_global_device_ids=true | all-gather | bytes 9656 | tf_op jit(solution)/shard_map/all_gather | solution.py:14
  512.2 17.7 %all-gather.19 = f32[16,2,71]{2,1,0:T(2,128)S(1)} all-gather(f32[1,2,71]{2,1,0:T(2,128)S(1)} %bitcast.293), channel_id=6, replica_groups=mesh['req'=2,'seq'=16] {'seq'}, dimensions={0}, use_global_device_ids=true | all-gather | bytes 9656 | tf_op jit(solution)/shard_map/all_gather | solution.py:14
  530.0 21.5 %all-gather.5 = f32[32,71,64]{1,2,0:T(8,128)S(1)} all-gather(f32[2,71,64]{1,2,0:T(8,128)S(1)} %fusion.14), channel_id=7, replica_groups=mesh['req'=2,'seq'=16] {'seq'}, dimensions={0}, use_global_device_ids=true | all-gather | bytes 617984 | tf_op jit(solution)/shard_map/all_gather | solution.py:14
  551.6 4.4 while.77
  556.2 18.2 %all-gather.14 = f32[16,2,71]{2,1,0:T(2,128)S(1)} all-gather(f32[1,2,71]{2,1,0:T(2,128)S(1)} %bitcast.288), channel_id=2, replica_groups=mesh['req'=2,'seq'=16] {'seq'}, dimensions={0}, use_global_device_ids=true | all-gather | bytes 9656 | tf_op jit(solution)/shard_map/all_gather | solution.py:14
  574.5 18.0 %all-gather.15 = f32[16,2,71]{2,1,0:T(2,128)S(1)} all-gather(f32[1,2,71]{2,1,0:T(2,128)S(1)} %bitcast.292), channel_id=3, replica_groups=mesh['req'=2,'seq'=16] {'seq'}, dimensions={0}, use_global_device_ids=true | all-gather | bytes 9656 | tf_op jit(solution)/shard_map/all_gather | solution.py:14
  592.4 21.3 %all-gather.2 = f32[32,71,64]{1,2,0:T(8,128)S(1)} all-gather(f32[2,71,64]{1,2,0:T(8,128)S(1)} %fusion.12), channel_id=4, replica_groups=mesh['req'=2,'seq'=16] {'seq'}, dimensions={0}, use_global_device_ids=true | all-gather | bytes 617984 | tf_op jit(solution)/shard_map/all_gather | solution.py:14
  613.9 4.4 while.76
  619.5 10.7 %fusion.136 = f32[2,4544]{1,0:T(2,128)} fusion(bf16[2,1136]{1,0:T(2,128)(2,1)S(1)} %fusion.115, bf16[2,284]{1,0:T(2,128)(2,1)S(1)} %constant_dynamic-slice_fusion.8, bf16[1136,4544]{0,1:T(8,128)(2,1)} %all-gather.36.cloned.1.call-done, bf16[284,4544]{0,1:T(8,128)(2,1)} %copy.125), kind=kOutput, calls=%fused_computation.232 | convolution fusion | flops 51631200 | bytes 12946992 | tf_op jit(solution)/shard_map/dot_general | solution.py:135
  630.2 4.8 fusion.132
  635.1 4.8 fusion.128
  639.9 4.8 fusion.124
  644.8 1.8 copy.145
  646.6 84.6 %all-reduce.7.cloned.1.call-done = (f32[2,4544]{1,0:T(2,128)}, f32[2,4544]{1,0:T(2,128)}, f32[2,4544]{1,0:T(2,128)}, f32[2,4544]{1,0:T(2,128)}) async-done(((f32[2,4544]{1,0:T(2,128)}, f32[2,4544]{1,0:T(2,128)}, f32[2,4544]{1,0:T(2,128)}, f32[2,4544]{1,0:T(2,128)}), (f32[2,4544]{1,0:T(2,128)}, f32[2,4544]{1,0:T(2,128)}, f32[2,4544]{1,0:T(2,128)}, f32[2,4544]{1,0:T(2,128)})) %all-reduce.7.cloned.1.call-update) | async-done | bytes 145424
  734.2 4.4 all_gather.143
  (486 shorter events, 41.9 us)
Async XLA Ops:
  7.2 71.2 %copy-start = (s32[4]{0:T(128)S(1)}, s32[4]{0:T(128)}, u32[]{:S(2)}) copy-start(s32[4]{0:T(128)} %param.23) | copy-start | bytes 52
  7.2 93.5 %all-gather.40.cloned.1.call-start = ((), (), s32[]{:S(2)}) async-start(), calls=%async_computation.4 | async-start | bytes 3981312 | tf_op jit(solution)/shard_map/all_gather | solution.py:87
  7.9 107.7 %all-gather.38.cloned.1.call-start = ((), (), s32[]{:S(2)}) async-start(), calls=%async_computation.3 | async-start | bytes 3981312 | tf_op jit(solution)/shard_map/all_gather | solution.py:84
  8.7 110.9 %all-gather.32.cloned.1.call-start = ((), (), s32[]{:S(2)}) async-start(), calls=%async_computation | async-start | bytes 1744896 | tf_op jit(solution)/shard_map/all_gather | solution.py:85
  9.4 9.3 %copy-start.25 = (bf16[4,2,284]{2,1,0:T(2,128)(2,1)S(1)}, bf16[4,2,284]{2,1,0:T(2,128)(2,1)}, u32[]{:S(2)}) copy-start(bf16[4,2,284]{2,1,0:T(2,128)(2,1)} %param.21) | copy-start | bytes 13636
  9.4 13.8 %copy-start.46 = (s32[4]{0:T(128)S(1)}, s32[4]{0:T(128)}, u32[]{:S(2)}) copy-start(s32[4]{0:T(128)} %param.24) | copy-start | bytes 52
  9.4 235.7 %all-gather.34.cloned.1.call-start = ((), (), s32[]{:S(2)}) async-start(), calls=%async_computation.1 | async-start | bytes 15704064 | tf_op jit(solution)/shard_map/all_gather | solution.py:86
  10.0 609.5 %all-gather.36.cloned.1.call-start = ((), (), s32[]{:S(2)}) async-start(), calls=%async_computation.2 | async-start | bytes 15704064 | tf_op jit(solution)/shard_map/all_gather | solution.py:88
  18.7 712.5 %all-reduce.7.cloned.1.call-start = ((), (), s32[]{:S(2)}) async-start(), calls=%async_computation.5 | async-start | bytes 294912
  55.9 22.4 %copy-start.19 = (bf16[4544]{0:T(1024)(128)(2,1)S(1)}, bf16[4544]{0:T(1024)(128)(2,1)}, u32[]{:S(2)}) copy-start(bf16[4544]{0:T(1024)(128)(2,1)} %param.26) | copy-start | bytes 27268
  55.9 22.4 %copy-start.20 = (bf16[4544]{0:T(1024)(128)(2,1)S(1)}, bf16[4544]{0:T(1024)(128)(2,1)}, u32[]{:S(2)}) copy-start(bf16[4544]{0:T(1024)(128)(2,1)} %param.25) | copy-start | bytes 27268
  66.1 25.2 %copy-start.11 = (bf16[2,512,128]{2,1,0:T(8,128)(2,1)S(1)}, bf16[2,512,128]{2,1,0:T(8,128)(2,1)}, u32[]{:S(2)}) copy-start(bf16[2,512,128]{2,1,0:T(8,128)(2,1)} %param.22) | copy-start | bytes 786436
  66.1 31.9 %copy-start.48 = (u32[32]{0:T(128)S(1)}, u32[32]{0:T(128)}, u32[]{:S(2)}) copy-start(u32[32]{0:T(128)} %constant.327) | copy-start | bytes 388
  77.5 23.2 %copy-start.6 = (f32[1,2,4544]{2,1,0:T(2,128)}, f32[1,2,4544]{2,1,0:T(2,128)S(1)}, u32[]{:S(2)}) copy-start(f32[1,2,4544]{2,1,0:T(2,128)S(1)} %copy.138) | copy-start | bytes 109060
  84.4 6.0 copy-start.31
  90.3 10.4 %copy-start.7 = (bf16[1,2,4544]{2,1,0:T(2,128)(2,1)}, bf16[1,2,4544]{2,1,0:T(2,128)(2,1)S(1)}, u32[]{:S(2)}) copy-start(bf16[1,2,4544]{2,1,0:T(2,128)(2,1)S(1)} %copy.166) | copy-start | bytes 54532
  90.5 4.1 copy-start.29
  94.7 4.6 copy-start.27
  270.7 9.6 %copy-start.2 = (bf16[4544,1548]{1,0:T(8,128)(2,1)S(1)}, bf16[4544,1548]{1,0:T(8,128)(2,1)}, u32[]{:S(2)}) copy-start(bf16[4544,1548]{1,0:T(8,128)(2,1)} %concatenate.126) | copy-start | bytes 42204676
  270.7 9.6 %copy-start.10 = (bf16[1,2,4544]{2,1,0:T(2,128)(2,1)S(1)}, bf16[1,2,4544]{2,1,0:T(2,128)(2,1)}, u32[]{:S(2)}) copy-start(bf16[1,2,4544]{2,1,0:T(2,128)(2,1)} %copy-done.9) | copy-start | bytes 54532
  270.7 9.6 %copy-start.32 = (f32[2]{0:T(128)S(1)}, f32[2]{0:T(128)}, u32[]{:S(2)}) copy-start(f32[2]{0:T(128)} %copy-done.31) | copy-start | bytes 28
  270.7 9.6 %copy-start.43 = (f32[2]{0:T(128)S(1)}, f32[2]{0:T(128)}, u32[]{:S(2)}) copy-start(f32[2]{0:T(128)} %add_rsqrt_fusion.1) | copy-start | bytes 28
  280.3 2.4 copy-start.8
  285.0 24.4 %copy-start.39 = (f32[2,32]{1,0:T(2,128)S(1)}, f32[2,32]{1,0:T(2,128)}, u32[]{:S(2)}) copy-start(f32[2,32]{1,0:T(2,128)} %get-tuple-element.1017) | copy-start | bytes 772
  285.0 24.4 %copy-start.40 = (f32[2,32]{1,0:T(2,128)S(1)}, f32[2,32]{1,0:T(2,128)}, u32[]{:S(2)}) copy-start(f32[2,32]{1,0:T(2,128)} %get-tuple-element.1018) | copy-start | bytes 772
  285.0 24.6 %copy-start.37 = (f32[2,32]{1,0:T(2,128)S(1)}, f32[2,32]{1,0:T(2,128)}, u32[]{:S(2)}) copy-start(f32[2,32]{1,0:T(2,128)} %get-tuple-element.1015) | copy-start | bytes 772
  285.1 24.6 %copy-start.38 = (f32[2,32]{1,0:T(2,128)S(1)}, f32[2,32]{1,0:T(2,128)}, u32[]{:S(2)}) copy-start(f32[2,32]{1,0:T(2,128)} %get-tuple-element.1016) | copy-start | bytes 772
  285.1 24.7 %copy-start.35 = (f32[2,32]{1,0:T(2,128)S(1)}, f32[2,32]{1,0:T(2,128)}, u32[]{:S(2)}) copy-start(f32[2,32]{1,0:T(2,128)} %get-tuple-element.1013) | copy-start | bytes 772
  285.1 24.7 %copy-start.36 = (f32[2,32]{1,0:T(2,128)S(1)}, f32[2,32]{1,0:T(2,128)}, u32[]{:S(2)}) copy-start(f32[2,32]{1,0:T(2,128)} %get-tuple-element.1014) | copy-start | bytes 772
  285.1 24.9 %copy-start.33 = (f32[2,32]{1,0:T(2,128)S(1)}, f32[2,32]{1,0:T(2,128)}, u32[]{:S(2)}) copy-start(f32[2,32]{1,0:T(2,128)} %get-tuple-element.987) | copy-start | bytes 772
  285.1 24.9 %copy-start.34 = (f32[2,32]{1,0:T(2,128)S(1)}, f32[2,32]{1,0:T(2,128)}, u32[]{:S(2)}) copy-start(f32[2,32]{1,0:T(2,128)} %get-tuple-element.988) | copy-start | bytes 772
  285.1 25.0 %copy-start.5 = (bf16[2,512,128]{1,2,0:T(8,128)(2,1)S(1)}, bf16[2,512,128]{1,2,0:T(8,128)(2,1)}, u32[]{:S(2)}) copy-start(bf16[2,512,128]{1,2,0:T(8,128)(2,1)} %copy.119) | copy-start | bytes 786436
  285.1 25.0 %copy-start.21 = (pred[2,512]{1,0:T(4,128)(4,1)S(1)}, pred[2,512]{1,0:T(4,128)(4,1)}, u32[]{:S(2)}) copy-start(pred[2,512]{1,0:T(4,128)(4,1)} %get-tuple-element.1035) | copy-start | bytes 3076
  285.1 25.0 %copy-start.22 = (pred[2,512]{1,0:T(4,128)(4,1)S(1)}, pred[2,512]{1,0:T(4,128)(4,1)}, u32[]{:S(2)}) copy-start(pred[2,512]{1,0:T(4,128)(4,1)} %get-tuple-element.1036) | copy-start | bytes 3076
  285.1 25.0 %copy-start.23 = (pred[2,512]{1,0:T(4,128)(4,1)S(1)}, pred[2,512]{1,0:T(4,128)(4,1)}, u32[]{:S(2)}) copy-start(pred[2,512]{1,0:T(4,128)(4,1)} %get-tuple-element.1037) | copy-start | bytes 3076
  285.1 25.0 %copy-start.24 = (pred[2,512]{1,0:T(4,128)(4,1)S(1)}, pred[2,512]{1,0:T(4,128)(4,1)}, u32[]{:S(2)}) copy-start(pred[2,512]{1,0:T(4,128)(4,1)} %get-tuple-element.1038) | copy-start | bytes 3076
  285.2 25.2 %copy-start.14 = (pred[2,512]{1,0:T(4,128)(4,1)S(1)}, pred[2,512]{1,0:T(4,128)(4,1)}, u32[]{:S(2)}) copy-start(pred[2,512]{1,0:T(4,128)(4,1)} %get-tuple-element.974) | copy-start | bytes 3076
  285.2 44.0 %copy-start.13 = (pred[2,512]{1,0:T(4,128)(4,1)S(1)}, pred[2,512]{1,0:T(4,128)(4,1)}, u32[]{:S(2)}) copy-start(pred[2,512]{1,0:T(4,128)(4,1)} %get-tuple-element.973) | copy-start | bytes 3076
  285.2 64.2 %copy-start.12 = (pred[2,512]{1,0:T(4,128)(4,1)S(1)}, pred[2,512]{1,0:T(4,128)(4,1)}, u32[]{:S(2)}) copy-start(pred[2,512]{1,0:T(4,128)(4,1)} %get-tuple-element.972) | copy-start | bytes 3076
  619.4 10.8 %copy-start.3 = (bf16[284,4544]{0,1:T(8,128)(2,1)S(1)}, bf16[284,4544]{0,1:T(8,128)(2,1)}, u32[]{:S(2)}) copy-start(bf16[284,4544]{0,1:T(8,128)(2,1)} %copy.125) | copy-start | bytes 7742980
  619.5 10.8 %copy-start.47 = (bf16[1136,4544]{0,1:T(8,128)(2,1)S(1)}, bf16[1136,4544]{0,1:T(8,128)(2,1)}, u32[]{:S(2)}) copy-start(bf16[1136,4544]{0,1:T(8,128)(2,1)} %all-gather.36.cloned.1.call-done) | copy-start | bytes 30971908
  635.1 104.8 %copy-start.1 = (s32[4]{0:T(128)S(1)}, s32[4]{0:T(128)}, u32[]{:S(2)}) copy-start(s32[4]{0:T(128)} %param.23) | copy-start | bytes 52
  639.9 4.9 copy-start.45
  639.9 91.3 %copy-start.18 = (f32[1,2,284]{2,0,1:T(1,128)S(1)}, f32[1,2,284]{2,0,1:T(1,128)}, u32[]{:S(2)}) copy-start(f32[1,2,284]{2,0,1:T(1,128)} %get-tuple-element.969) | copy-start | bytes 6820
  639.9 92.1 %copy-start.17 = (bf16[1,2,284]{2,0,1:T(2,128)(2,1)S(1)}, bf16[1,2,284]{2,0,1:T(2,128)(2,1)}, u32[]{:S(2)}) copy-start(bf16[1,2,284]{2,0,1:T(2,128)(2,1)} %get-tuple-element.970) | copy-start | bytes 3412
  639.9 92.8 %copy-start.16 = (bf16[1,2,284]{2,0,1:T(2,128)(2,1)S(1)}, bf16[1,2,284]{2,0,1:T(2,128)(2,1)}, u32[]{:S(2)}) copy-start(bf16[1,2,284]{2,0,1:T(2,128)(2,1)} %get-tuple-element.968) | copy-start | bytes 3412
  639.9 93.6 %copy-start.15 = (bf16[1,2,284]{2,0,1:T(2,128)(2,1)S(1)}, bf16[1,2,284]{2,0,1:T(2,128)(2,1)}, u32[]{:S(2)}) copy-start(bf16[1,2,284]{2,0,1:T(2,128)(2,1)} %get-tuple-element.967) | copy-start | bytes 3412
  639.9 99.3 %copy-start.44 = (pred[2]{0:T(512)(128)(4,1)S(1)}, pred[2]{0:T(512)(128)(4,1)}, u32[]{:S(2)}) copy-start(pred[2]{0:T(512)(128)(4,1)} %get-tuple-element.945) | copy-start | bytes 10
  (7 other events, 12.5 us)
Sparse Core Ops, SparseCore 0:
  9.6 39.5 all-gather.39
  50.7 39.3 all-gather.37
  91.7 22.5 all-gather.31
  115.8 129.3 all-gather.33
  246.5 129.3 all-gather.35
  644.9 86.2 all-reduce.6
where the time goes:
time: 757 us; the launch traced here: 747 us
  blocking collectives  347 us (46%)
  waiting for transfers between devices  213 us (28%)
  local copies, waits for them, and re-layouts  88.9 us (12%)
  matrix products  41.5 us (5%)
  other arithmetic  38.8 us (5%)
  between operations  16 us (2%)
    all_gather x12, blocking collectives, joined_2(): gathered = jax.tree.map(lambda a: lax.all_gather(a, axis), part)  231 us
    all_gather x1, waiting for transfers between devices, shards(): lax.all_gather(w_up, 'req', axis=0, tiled=True)  126 us
    unnamed x7, waiting for transfers between devices  87.2 us
    all_gather x4, blocking collectives, shards(): query_all = lax.all_gather(query_part, 'seq', axis=1, tiled=True)  75.6 us
    unnamed x114, local copies, waits for them, and re-layouts  39.9 us
    all_gather x1, blocking collectives, shards(): full_states = lax.all_gather(own_states, 'seq', axis=2, tiled=True)  31.8 us
    concatenate x1, local copies, waits for them, and re-layouts, shards(): first_matrix = jnp.concatenate([query_cols, keyval_cols, up_cols], axis=1)  25.6 us
    dot_general x4, matrix products, shards(): jnp.dot(joined, second_matrix, preferred_element_type=jnp.float32)  25.2 us
  transfers between devices with their start and end apart: 6, of which 2 were waited for; matrix products, arithmetic and copies ran while one was open for 18% of the time, Pallas kernels for 0%

commit v1 on v0

v1 whole, which is shorter than its diff:
```python
import jax
import jax.numpy as jnp
from jax import lax
from jax.sharding import PartitionSpec as P


EPSILON = 1e-05
NEGATIVE = -1e30
ALL = ("req", "seq")


def layer_norm(row_block, norm_gain, norm_bias):
    values = row_block.astype(jnp.float32)
    average = jnp.mean(values, axis=-1, keepdims=True)
    centered = values - average
    spread = jnp.mean(centered * centered, axis=-1, keepdims=True)
    scaled = centered * lax.rsqrt(spread + EPSILON)
    return (scaled * norm_gain.astype(jnp.float32) + norm_bias.astype(jnp.float32)).astype(
        jnp.bfloat16
    )


def rotate(vectors, positions):
    head_width = vectors.shape[-1]
    half_width = head_width // 2
    frequency = 10000.0 ** (-(jnp.arange(half_width, dtype=jnp.float32) * 2.0) / head_width)
    angles = positions.astype(jnp.float32)[:, None] * frequency[None, :]
    cosine = jnp.concatenate([jnp.cos(angles), jnp.cos(angles)], axis=-1)[:, None, :]
    sine_wave = jnp.concatenate([jnp.sin(angles), jnp.sin(angles)], axis=-1)[:, None, :]
    turned = jnp.concatenate([-vectors[..., half_width:], vectors[..., :half_width]], axis=-1)
    return vectors * cosine + turned * sine_wave


def shards(
    states,
    kv_cache,
    lengths,
    placement,
    norm_gain,
    norm_bias,
    w_query,
    w_keyval,
    w_out,
    w_up,
    w_down,
):
    steps = states.shape[0]
    group_rows = kv_cache.shape[0]
    seg_length = kv_cache.shape[1]
    head_width = kv_cache.shape[2] // 2
    model_width = norm_gain.shape[0]
    head_count = model_width // head_width
    slice_width = states.shape[2]
    part_width = w_query.shape[0]
    total = placement.shape[0]
    req_size = total // group_rows
    seq_size = model_width // slice_width
    rows = steps * total
    group_index = lax.axis_index("req")
    shard_index = lax.axis_index("seq")

    own_requests = lax.dynamic_slice_in_dim(placement, group_index * group_rows, group_rows, 0)
    slot_lengths = jnp.take(lengths, own_requests)
    step_offsets = jnp.arange(steps, dtype=jnp.int32)
    positions = slot_lengths[None, :] + step_offsets[:, None]

    every = lax.all_gather(states, ALL, axis=0, tiled=False)
    every = every.reshape(req_size, seq_size, steps, group_rows, slice_width)
    every = every.transpose(2, 0, 3, 1, 4).reshape(steps, total, model_width)
    current_all = jnp.take(every, placement, axis=1)
    normed = layer_norm(current_all.reshape(rows, model_width), norm_gain, norm_bias)
    normed_part = lax.dynamic_slice_in_dim(normed, group_index * part_width, part_width, 1)

    part_query = jnp.dot(normed_part, w_query, preferred_element_type=jnp.float32)
    part_keyval = jnp.dot(normed_part, w_keyval, preferred_element_type=jnp.float32)
    part_up = jnp.dot(normed_part, w_up, preferred_element_type=jnp.float32)
    first = lax.psum(jnp.concatenate([part_query, part_keyval, part_up], axis=1), "req")
    query_raw = first[:, :slice_width].astype(jnp.bfloat16).reshape(steps, total, slice_width)
    keyval = first[:, slice_width : slice_width + 2 * head_width].reshape(steps, total, 2 * head_width)
    up_part = first[:, slice_width + 2 * head_width :]

    own_query = lax.dynamic_slice_in_dim(query_raw, group_index * group_rows, group_rows, 1)
    query_all = lax.all_gather(own_query, "seq", axis=2, tiled=True)
    flat_positions = positions.reshape(-1)
    query_rows = rotate(
        query_all.astype(jnp.float32).reshape(steps * group_rows, head_count, head_width),
        flat_positions,
    ).astype(jnp.bfloat16)
    own_keyval = lax.dynamic_slice_in_dim(keyval, group_index * group_rows, group_rows, 1)
    own_keyval = own_keyval.reshape(steps * group_rows, 2 * head_width)
    new_key = rotate(own_keyval[:, None, :head_width], flat_positions)[:, 0, :]
    new_entry = jnp.concatenate([new_key, own_keyval[:, head_width:]], axis=-1).astype(jnp.bfloat16)
    new_entry = new_entry.reshape(steps, group_rows, 2 * head_width)

    local_slots = jnp.arange(seg_length, dtype=jnp.int32)
    global_positions = shard_index * seg_length + local_slots
    cache_now = kv_cache
    for step_index in range(steps):
        write_mask = global_positions[None, :] == positions[step_index][:, None]
        cache_now = jnp.where(write_mask[:, :, None], new_entry[step_index][:, None, :], cache_now)

    key_rows = cache_now[:, :, :head_width]
    value_rows = cache_now[:, :, head_width:]
    query_heads = (
        query_rows.reshape(steps, group_rows, head_count, head_width)
        .transpose(1, 0, 2, 3)
        .reshape(group_rows, steps * head_count, head_width)
    )
    scores = jnp.einsum(
        "gqd,gsd->gqs", query_heads, key_rows, preferred_element_type=jnp.float32
    ) * head_width ** (-0.5)
    valid = global_positions[None, None, :] <= positions.T[:, :, None]
    valid = jnp.broadcast_to(
        valid[:, :, None, :], (group_rows, steps, head_count, seg_length)
    ).reshape(group_rows, steps * head_count, seg_length)
    local_peak = jnp.max(jnp.where(valid, scores, NEGATIVE), axis=-1)
    weights = jnp.where(valid, jnp.exp(scores - local_peak[:, :, None]), 0.0)
    local_total = jnp.sum(weights, axis=-1)
    local_weighted = jnp.einsum(
        "gqs,gsd->gqd", weights, value_rows, preferred_element_type=jnp.float32
    )

    peak_buffer = jnp.full((total, steps * head_count), NEGATIVE, jnp.float32)
    peak_buffer = lax.dynamic_update_slice_in_dim(
        peak_buffer, local_peak, group_index * group_rows, 0
    )
    peak = lax.pmax(peak_buffer, ALL)
    own_peak = lax.dynamic_slice_in_dim(peak, group_index * group_rows, group_rows, 0)
    scale = jnp.exp(local_peak - own_peak)
    packed = jnp.concatenate(
        [local_weighted * scale[:, :, None], (local_total * scale)[:, :, None]], axis=-1
    )
    packed_buffer = jnp.zeros((total, steps * head_count, head_width + 1), jnp.float32)
    packed_buffer = lax.dynamic_update_slice_in_dim(
        packed_buffer, packed, group_index * group_rows, 0
    )
    summed = lax.psum(packed_buffer, ALL)
    mixed = summed[:, :, :head_width] / summed[:, :, head_width:]
    mixed = (
        mixed.reshape(total, steps, model_width)
        .transpose(1, 0, 2)
        .reshape(rows, model_width)
        .astype(jnp.bfloat16)
    )
    mixed_part = lax.dynamic_slice_in_dim(mixed, shard_index * slice_width, slice_width, 1)

    hidden = jax.nn.gelu(up_part, approximate=False).astype(jnp.bfloat16)
    partial_sum = jnp.dot(mixed_part, w_out, preferred_element_type=jnp.float32) + jnp.dot(
        hidden, w_down, preferred_element_type=jnp.float32
    )
    out_buffer = jnp.zeros((rows, model_width), jnp.float32)
    out_buffer = lax.dynamic_update_slice_in_dim(
        out_buffer, partial_sum, group_index * part_width, 1
    )
    branch = lax.psum(out_buffer, ALL).reshape(steps, total, model_width)

    inverse = (
        jnp.zeros((total,), jnp.int32).at[placement].set(jnp.arange(total, dtype=jnp.int32))
    )
    own_inverse = lax.dynamic_slice_in_dim(inverse, group_index * group_rows, group_rows, 0)
    own_branch = jnp.take(branch, own_inverse, axis=1)
    own_branch = lax.dynamic_slice_in_dim(own_branch, shard_index * slice_width, slice_width, 2)
    new_states = (states.astype(jnp.float32) + own_branch).astype(jnp.bfloat16)
    return (new_states, cache_now)


def solution(mesh):
    in_specs = (
        P(None, "req", "seq"),
        P("req", "seq", None),
        P(),
        P(),
        P(),
        P(),
        P("req", "seq"),
        P("req", None),
        P("seq", "req"),
        P("req", "seq"),
        P("seq", "req"),
    )
    out_specs = (P(None, "req", "seq"), P("req", "seq", None))
    return jax.shard_map(shards, mesh=mesh, in_specs=in_specs, out_specs=out_specs, check_vma=False)
```

time: 757 us -> 438 us (0.58)
  blocking collectives: 347 us -> 119 us
  local copies, waits for them, and re-layouts: 88.9 us -> 22 us
  waiting for transfers between devices: 213 us -> 266 us
  other arithmetic: 38.8 us -> 5.32 us
  matrix products: 41.5 us -> 8.89 us
    all_gather x19 -> x2, blocking collectives: 347 us -> 74.6 us  [the longest x1 41.6 us: shards(): every = lax.all_gather(states, ALL, axis=0, tiled=False)]
    psum x0 -> x3, waiting for transfers between devices: none -> 266 us  [the longest x1 126 us: shards(): summed = lax.psum(packed_buffer, ALL)]
    all_gather x5 -> x0, waiting for transfers between devices: 126 us -> none  [the longest x1 126 us: shards(): lax.all_gather(w_up, 'req', axis=0, tiled=True)]
    unnamed x7 -> x3, waiting for transfers between devices: 87.2 us -> 0.05 us
    pmax x0 -> x1, blocking collectives: none -> 44 us  [shards(): peak = lax.pmax(peak_buffer, ALL)]
    unnamed x114 -> x23, local copies, waits for them, and re-layouts: 39.9 us -> 2.97 us
    dot_general x16 -> x7, matrix products: 41.5 us -> 8.89 us  [the longest x1 3.46 us: shards(): part_up = jnp.dot(normed_part, w_up, preferred_element_type=jnp.float32)]
    concatenate x1 -> x3, local copies, waits for them, and re-layouts: 25.6 us -> 1.11 us  [the longest x1 0.78 us: shards(): jnp.concatenate([part_query, part_keyval, part_up], axis=1)]
  transfers between devices with their start and end apart: 6 -> 3, of which waited for: 2 -> 3; matrix products, arithmetic and copies ran while one was open for 18% -> 1% of each run, Pallas kernels for 0% -> 0%
where the time goes in v1:
time: 438 us; the launch traced here: 436 us
  waiting for transfers between devices  266 us (61%)
  blocking collectives  119 us (27%)
  local copies, waits for them, and re-layouts  22 us (5%)
  between operations  14.2 us (3%)
  matrix products  8.89 us (2%)
  other arithmetic  5.32 us (1%)
    psum x1, waiting for transfers between devices, shards(): summed = lax.psum(packed_buffer, ALL)  126 us
    psum x1, waiting for transfers between devices, shards(): branch = lax.psum(out_buffer, ALL).reshape(steps, total, model_width)  125 us
    pmax x1, blocking collectives, shards(): peak = lax.pmax(peak_buffer, ALL)  44 us
    all_gather x1, blocking collectives, shards(): every = lax.all_gather(states, ALL, axis=0, tiled=False)  41.6 us
    all_gather x1, blocking collectives, shards(): query_all = lax.all_gather(own_query, 'seq', axis=2, tiled=True)  33 us
    psum x1, waiting for transfers between devices, shards(): lax.psum(jnp.concatenate([part_query, part_keyval, part_up], axis=1), 'req')  15.4 us
  transfers between devices with their start and end apart: 3, of which 3 were waited for; matrix products, arithmetic and copies ran while one was open for 1% of the time, Pallas kernels for 0%

profile of v1, /device:TPU:2, one launch (start us, length us, event | category | flops | bytes accessed | tf_op | source)
XLA Modules:
  0.0 435.6 jit_solution(13402356280962080718)
XLA Ops:
  7.2 0.8 compare_select_fusion.2
  8.0 0.7 compare_and_fusion
  8.6 0.8 dynamic-slice.1
  9.4 0.8 dynamic-slice.2
  10.2 41.6 %all-gather = bf16[128,2,284]{2,1,0:T(2,128)(2,1)S(1)} all-gather(bf16[4,2,284]{2,1,0:T(2,128)(2,1)} %param.11), channel_id=2, replica_groups=mesh['req'=2,'seq'=16] {'req','seq'}, dimensions={0}, use_global_device_ids=true | all-gather | bytes 149952 | tf_op jit(solution)/shard_map/all_gather | solution.py:67
  51.8 0.3 reshape.348
  52.1 0.7 gather_fusion.1
  52.8 0.3 convert_reduce_fusion
  53.2 0.3 fusion.5
  54.1 3.5 fusion.96
  57.6 0.3 fusion.94
  57.8 0.4 fusion.95
  58.3 0.8 concatenate.40
  59.3 0.6 gather_fusion
  60.4 0.1 copy.81
  60.7 0.2 reshape.346
  61.1 15.4 %all-reduce.4.cloned.1.call-done = f32[16,1548]{1,0:T(8,128)} async-done(((f32[16,1548]{1,0:T(8,128)}), f32[16,1548]{1,0:T(8,128)}) %all-reduce.4.cloned.1.call-update) | async-done | bytes 99088 | tf_op jit(solution)/shard_map/psum | solution.py:77
  76.5 0.8 slice.99
  77.3 0.7 slice.124
  78.1 0.2 copy.88
  78.3 33.0 %all_gather.11 = bf16[4,2,4544]{0,1,2:T(2,128)(2,1)} all-gather(bf16[4,2,284]{0,1,2:T(2,128)(2,1)S(1)} %copy.88), channel_id=1, replica_groups=mesh['req'=2,'seq'=16] {'seq'}, dimensions={2}, use_global_device_ids=true | all-gather | bytes 77248 | tf_op jit(solution)/shard_map/all_gather | solution.py:83
  111.3 5.2 %copy.73 = bf16[4,2,4544]{2,0,1:T(4,128)(2,1)S(1)} copy(bf16[4,2,4544]{0,1,2:T(2,128)(2,1)} %all_gather.11) | data formatting | bytes 145408 | tf_op jit(solution)/shard_map/all_gather | solution.py:83
  116.5 0.2 reshape.351
  116.8 0.2 reshape.350
  117.6 0.2 copy.78
  117.8 0.2 fusion.8
  118.0 0.2 copy.80
  118.3 0.2 select_select_fusion
  118.5 0.5 select_reduce_fusion
  119.0 44.0 %pmax.7 = f32[4,284]{1,0:T(4,128)S(1)} all-reduce(f32[4,284]{1,0:T(4,128)S(1)} %constant_dynamic-update-slice_fusion.1), channel_id=1, replica_groups=mesh['req'=2,'seq'=16] {'req','seq'}, use_global_device_ids=true, to_apply=%region_5.6 | all-reduce | flops 1136 | bytes 9088 | tf_op jit(solution)/shard_map/pmax | solution.py:127
  163.0 0.4 fusion
  163.4 0.4 convolution_multiply_fusion.1
  163.9 0.2 copy.82
  164.2 0.8 copy-done.2
  165.1 0.6 scatter_custom_fusion
  165.7 125.7 %all-reduce.6.cloned.1.call-done = f32[4,284,65]{2,1,0:T(8,128)} async-done(((f32[4,284,65]{2,1,0:T(8,128)}), f32[4,284,65]{2,1,0:T(8,128)}) %all-reduce.6.cloned.1.call-update) | async-done | bytes 295376 | tf_op jit(solution)/shard_map/psum | solution.py:137
  291.3 1.5 slice_reduce_fusion
  292.8 1.3 fusion.1
  294.1 0.2 convert_element_type.69
  294.4 0.4 fusion.55
  294.8 0.2 copy-done.6
  295.0 3.4 convolution_add_fusion
  298.5 1.1 dynamic_update_slice.11
  299.7 0.8 copy.84
  300.6 0.8 copy.86
  301.4 125.3 %all-reduce.8.cloned.1.call-done = f32[4,4,4544]{2,0,1:T(4,128)} async-done(((f32[4,4,4544]{2,0,1:T(4,128)}), f32[4,4,4544]{2,0,1:T(4,128)}) %all-reduce.8.cloned.1.call-update) | async-done | bytes 290832 | tf_op jit(solution)/shard_map/psum | solution.py:155
  426.8 1.6 gather_fusion.2
  428.5 0.6 copy.85
  (81 shorter events, 3.2 us)
Async XLA Ops:
  7.2 287.3 %copy-start = (bf16[284,2272]{1,0:T(8,128)(2,1)S(1)}, bf16[284,2272]{1,0:T(8,128)(2,1)}, u32[]{:S(2)}) copy-start(bf16[284,2272]{1,0:T(8,128)(2,1)} %param.19) | copy-start | bytes 3871492
  7.2 69.3 %all-reduce.4.cloned.1.call-start = ((), (), s32[]{:S(2)}) async-start(), calls=%async_computation | async-start | bytes 212992 | tf_op jit(solution)/shard_map/psum | solution.py:77
  54.0 3.5 copy-start.4
  54.0 3.8 copy-start.3
  57.5 1.6 copy-start.8
  57.5 1.7 copy-start.1
  57.8 2.6 copy-start.5
  59.1 232.2 %all-reduce.6.cloned.1.call-start = ((), (), s32[]{:S(2)}) async-start(), calls=%async_computation.1 | async-start | bytes 1179648 | tf_op jit(solution)/shard_map/psum | solution.py:137
  164.2 0.8 copy-start.2
  165.0 261.8 %all-reduce.8.cloned.1.call-start = ((), (), s32[]{:S(2)}) async-start(), calls=%async_computation.2 | async-start | bytes 589824 | tf_op jit(solution)/shard_map/psum | solution.py:155
  294.1 0.9 copy-start.6
  299.6 128.8 %copy-start.7 = (bf16[4,2,284]{2,1,0:T(2,128)(2,1)S(1)}, bf16[4,2,284]{2,1,0:T(2,128)(2,1)}, u32[]{:S(2)}) copy-start(bf16[4,2,284]{2,1,0:T(2,128)(2,1)} %param.11) | copy-start | bytes 13636
Sparse Core Ops, SparseCore 0:
  59.2 17.2 all-reduce.3
  165.1 126.1 all-reduce.5
  300.6 126.0 all-reduce.7

commit v2 on v1

--- a/solution.py
+++ b/solution.py
@@ -7,6 +7,59 @@
 EPSILON = 1e-05
 NEGATIVE = -1e30
 ALL = ("req", "seq")
+
+
+def xor_pairs(size, bit):
+    return [(index, index ^ bit) for index in range(size)]
+
+
+def gather_blocks(block, axis, size):
+    index = lax.axis_index(axis)
+    blocks = block[None]
+    bit = 1
+    while bit < size:
+        other = lax.ppermute(blocks, axis, xor_pairs(size, bit))
+        low = (index // bit) % 2 == 0
+        blocks = jnp.where(
+            low, jnp.concatenate([blocks, other]), jnp.concatenate([other, blocks])
+        )
+        bit *= 2
+    return blocks
+
+
+def sum_over(value, axis, size):
+    bit = 1
+    while bit < size:
+        value = value + lax.ppermute(value, axis, xor_pairs(size, bit))
+        bit *= 2
+    return value
+
+
+def scatter_sum(blocks, axis, size):
+    index = lax.axis_index(axis)
+    bit = size // 2
+    while bit >= 1:
+        half = blocks.shape[0] // 2
+        high = (index // bit) % 2 == 1
+        keep = jnp.where(high, blocks[half:], blocks[:half])
+        send = jnp.where(high, blocks[:half], blocks[half:])
+        blocks = keep + lax.ppermute(send, axis, xor_pairs(size, bit))
+        bit //= 2
+    return blocks[0]
+
+
+def merge_over(packed, axis, size):
+    bit = 1
+    while bit < size:
+        other = lax.ppermute(packed, axis, xor_pairs(size, bit))
+        peak_first, peak_second = packed[..., 0], other[..., 0]
+        peak = jnp.maximum(peak_first, peak_second)
+        scale_first = jnp.exp(peak_first - peak)[..., None]
+        scale_second = jnp.exp(peak_second - peak)[..., None]
+        merged = packed[..., 1:] * scale_first + other[..., 1:] * scale_second
+        packed = jnp.concatenate([peak[..., None], merged], axis=-1)
+        bit *= 2
+    return packed
 
 
 def layer_norm(row_block, norm_gain, norm_bias):
@@ -64,8 +117,7 @@
     step_offsets = jnp.arange(steps, dtype=jnp.int32)
     positions = slot_lengths[None, :] + step_offsets[:, None]
 
-    every = lax.all_gather(states, ALL, axis=0, tiled=False)
-    every = every.reshape(req_size, seq_size, steps, group_rows, slice_width)
+    every = gather_blocks(gather_blocks(states, "seq", seq_size), "req", req_size)
     every = every.transpose(2, 0, 3, 1, 4).reshape(steps, total, model_width)
     current_all = jnp.take(every, placement, axis=1)
     normed = layer_norm(current_all.reshape(rows, model_width), norm_gain, norm_bias)
@@ -74,13 +126,14 @@
     part_query = jnp.dot(normed_part, w_query, preferred_element_type=jnp.float32)
     part_keyval = jnp.dot(normed_part, w_keyval, preferred_element_type=jnp.float32)
     part_up = jnp.dot(normed_part, w_up, preferred_element_type=jnp.float32)
-    first = lax.psum(jnp.concatenate([part_query, part_keyval, part_up], axis=1), "req")
+    first = sum_over(jnp.concatenate([part_query, part_keyval, part_up], axis=1), "req", req_size)
     query_raw = first[:, :slice_width].astype(jnp.bfloat16).reshape(steps, total, slice_width)
     keyval = first[:, slice_width : slice_width + 2 * head_width].reshape(steps, total, 2 * head_width)
     up_part = first[:, slice_width + 2 * head_width :]
 
     own_query = lax.dynamic_slice_in_dim(query_raw, group_index * group_rows, group_rows, 1)
-    query_all = lax.all_gather(own_query, "seq", axis=2, tiled=True)
+    query_all = gather_blocks(own_query, "seq", seq_size)
+    query_all = query_all.transpose(1, 2, 0, 3).reshape(steps, group_rows, model_width)
     flat_positions = positions.reshape(-1)
     query_rows = rotate(
         query_all.astype(jnp.float32).reshape(steps * group_rows, head_count, head_width),
@@ -120,46 +173,38 @@
         "gqs,gsd->gqd", weights, value_rows, preferred_element_type=jnp.float32
     )
 
-    peak_buffer = jnp.full((total, steps * head_count), NEGATIVE, jnp.float32)
-    peak_buffer = lax.dynamic_update_slice_in_dim(
-        peak_buffer, local_peak, group_index * group_rows, 0
-    )
-    peak = lax.pmax(peak_buffer, ALL)
-    own_peak = lax.dynamic_slice_in_dim(peak, group_index * group_rows, group_rows, 0)
-    scale = jnp.exp(local_peak - own_peak)
     packed = jnp.concatenate(
-        [local_weighted * scale[:, :, None], (local_total * scale)[:, :, None]], axis=-1
-    )
-    packed_buffer = jnp.zeros((total, steps * head_count, head_width + 1), jnp.float32)
-    packed_buffer = lax.dynamic_update_slice_in_dim(
-        packed_buffer, packed, group_index * group_rows, 0
-    )
-    summed = lax.psum(packed_buffer, ALL)
-    mixed = summed[:, :, :head_width] / summed[:, :, head_width:]
+        [local_peak[:, :, None], local_total[:, :, None], local_weighted], axis=-1
+    )
+    packed = merge_over(packed, "seq", seq_size)
+    mixed = packed[:, :, 2:] / packed[:, :, 1:2]
     mixed = (
-        mixed.reshape(total, steps, model_width)
+        mixed.reshape(group_rows, steps, model_width)
         .transpose(1, 0, 2)
-        .reshape(rows, model_width)
         .astype(jnp.bfloat16)
     )
-    mixed_part = lax.dynamic_slice_in_dim(mixed, shard_index * slice_width, slice_width, 1)
+    own_mixed = lax.dynamic_slice_in_dim(mixed, shard_index * slice_width, slice_width, 2)
+    every_mixed = gather_blocks(own_mixed, "req", req_size)
+    mixed_part = every_mixed.transpose(1, 0, 2, 3).reshape(rows, slice_width)
 
     hidden = jax.nn.gelu(up_part, approximate=False).astype(jnp.bfloat16)
     partial_sum = jnp.dot(mixed_part, w_out, preferred_element_type=jnp.float32) + jnp.dot(
         hidden, w_down, preferred_element_type=jnp.float32
     )
-    out_buffer = jnp.zeros((rows, model_width), jnp.float32)
-    out_buffer = lax.dynamic_update_slice_in_dim(
-        out_buffer, partial_sum, group_index * part_width, 1
-    )
-    branch = lax.psum(out_buffer, ALL).reshape(steps, total, model_width)
-
     inverse = (
         jnp.zeros((total,), jnp.int32).at[placement].set(jnp.arange(total, dtype=jnp.int32))
     )
-    own_inverse = lax.dynamic_slice_in_dim(inverse, group_index * group_rows, group_rows, 0)
-    own_branch = jnp.take(branch, own_inverse, axis=1)
-    own_branch = lax.dynamic_slice_in_dim(own_branch, shard_index * slice_width, slice_width, 2)
+    chunks = seq_size // req_size
+    by_request = jnp.take(partial_sum.reshape(steps, total, part_width), inverse, axis=1)
+    blocks = by_request.reshape(steps, req_size, group_rows, chunks, slice_width)
+    blocks = blocks.transpose(1, 3, 0, 2, 4).reshape(seq_size, steps, group_rows, slice_width)
+    reduced = scatter_sum(blocks, "seq", seq_size)
+    routes = []
+    for source_group in range(req_size):
+        for block in range(seq_size):
+            target = (block // chunks) * seq_size + source_group * chunks + block % chunks
+            routes.append((source_group * seq_size + block, target))
+    own_branch = lax.ppermute(reduced, ALL, routes)
     new_states = (states.astype(jnp.float32) + own_branch).astype(jnp.bfloat16)
     return (new_states, cache_now)
 

time: 438 us -> 114 us (0.26)
  waiting for transfers between devices: 266 us -> 61.1 us
  blocking collectives: 119 us -> 0 us
  starting transfers between devices: 0.12 us -> 24.2 us
  between operations: 14.2 us -> 1.35 us
  local copies, waits for them, and re-layouts: 22 us -> 9.38 us
    psum x3 -> x0, waiting for transfers between devices: 266 us -> none  [the longest x1 126 us: shards(): summed = lax.psum(packed_buffer, ALL)]
    all_gather x2 -> x0, blocking collectives: 74.6 us -> none  [the longest x1 41.6 us: shards(): every = lax.all_gather(states, ALL, axis=0, tiled=False)]
    ppermute x0 -> x20, waiting for transfers between devices: none -> 61.1 us  [the longest x4 20.8 us: merge_over(): other = lax.ppermute(packed, axis, xor_pairs(size, bit))]
    pmax x1 -> x0, blocking collectives: 44 us -> none  [shards(): peak = lax.pmax(peak_buffer, ALL)]
    ppermute x0 -> x20, starting transfers between devices: none -> 24.2 us  [the longest x10 12.8 us: gather_blocks(): other = lax.ppermute(blocks, axis, xor_pairs(size, bit))]
    all_gather x1 -> x0, local copies, waits for them, and re-layouts: 5.18 us -> none  [shards(): query_all = lax.all_gather(own_query, 'seq', axis=2, tiled=True)]
  transfers between devices with their start and end apart: 3 -> 20, of which waited for: 3 -> 18; matrix products, arithmetic and copies ran while one was open for 1% -> 8% of each run, Pallas kernels for 0% -> 0%
where the time goes in v2:
time: 114 us; the launch traced here: 113 us
  waiting for transfers between devices  61.1 us (54%)
  starting transfers between devices  24.2 us (21%)
  local copies, waits for them, and re-layouts  9.38 us (8%)
  matrix products  8.83 us (8%)
  other arithmetic  8.37 us (7%)
  between operations  1.35 us (1%)
    ppermute x4, waiting for transfers between devices, merge_over(): other = lax.ppermute(packed, axis, xor_pairs(size, bit))  20.8 us
    ppermute x10, waiting for transfers between devices, gather_blocks(): other = lax.ppermute(blocks, axis, xor_pairs(size, bit))  18.6 us
    ppermute x4, waiting for transfers between devices, scatter_sum(): blocks = keep + lax.ppermute(send, axis, xor_pairs(size, bit))  13.9 us
    ppermute x10, starting transfers between devices, gather_blocks(): other = lax.ppermute(blocks, axis, xor_pairs(size, bit))  12.8 us
    ppermute x4, starting transfers between devices, merge_over(): other = lax.ppermute(packed, axis, xor_pairs(size, bit))  5.92 us
    ppermute x1, waiting for transfers between devices, sum_over(): value = value + lax.ppermute(value, axis, xor_pairs(size, bit))  4.08 us
    ppermute x1, waiting for transfers between devices, shards(): own_branch = lax.ppermute(reduced, ALL, routes)  3.64 us
    dot_general x1, matrix products, shards(): part_up = jnp.dot(normed_part, w_up, preferred_element_type=jnp.float32)  3.46 us
  transfers between devices with their start and end apart: 20, of which 18 were waited for; matrix products, arithmetic and copies ran while one was open for 8% of the time, Pallas kernels for 0%

profile of v2, /device:TPU:2, one launch (start us, length us, event | category | flops | bytes accessed | tf_op | source)
XLA Modules:
  0.0 113.2 jit_solution(9680536117939728943)
XLA Ops:
  0.8 0.8 compare_select_fusion
  1.6 1.3 %gather_fusion = s32[2]{0:T(128)S(1)} fusion(s32[4]{0:T(128)} %param.13, s32[1024]{0:T(1024)S(1)} %pad_clamp_fusion.2), kind=kCustom, calls=%fused_computation | custom fusion | bytes 24 | tf_op jit(solution)/shard_map/jit(_take)/gather | solution.py:116
  2.9 0.7 and_select_fusion
  4.2 0.8 broadcast_select_fusion.10
  5.0 1.6 %collective-permute-start.1 = (bf16[2,4,2,284]{3,2,1,0:T(2,128)(2,1)S(1)}, bf16[2,4,2,284]{3,2,1,0:T(2,128)(2,1)S(1)}, u32[]{:S(2)}, u32[]{:S(2)}) collective-permute-start(bf16[2,4,2,284]{3,2,1,0:T(2,128)(2,1)S(1)} %broadcast_select_fusion.10), channel_id=1, source_target_pairs={{0,2},{1,3},{2,0},{3,1},{4,6},{5,7},{6,4},{7,5},{8,10},{9,11},{10,... | collective-permute-start | bytes 27272 | tf_op jit(solution)/shard_map/ppermute | solution.py:21
  6.6 2.1 %collective-permute-done.1 = bf16[2,4,2,284]{3,2,1,0:T(2,128)(2,1)S(1)} collective-permute-done((bf16[2,4,2,284]{3,2,1,0:T(2,128)(2,1)S(1)}, bf16[2,4,2,284]{3,2,1,0:T(2,128)(2,1)S(1)}, u32[]{:S(2)}, u32[]{:S(2)}) %collective-permute-start.1) | collective-permute-done | bytes 9120 | tf_op jit(solution)/shard_map/ppermute | solution.py:21
  8.8 1.6 %collective-permute-start.2 = (bf16[4,4,2,284]{3,2,1,0:T(2,128)(2,1)S(1)}, bf16[4,4,2,284]{3,2,1,0:T(2,128)(2,1)S(1)}, u32[]{:S(2)}, u32[]{:S(2)}) collective-permute-start(bf16[4,4,2,284]{3,2,1,0:T(2,128)(2,1)S(1)} %broadcast_select_fusion.8), channel_id=1, source_target_pairs={{0,4},{1,5},{2,6},{3,7},{4,0},{5,1},{6,2},{7,3},{8,12},{9,13},{10,... | collective-permute-start | bytes 54536 | tf_op jit(solution)/shard_map/ppermute | solution.py:21
  10.4 0.7 compare_select_fusion.2
  11.1 1.6 %collective-permute-done.2 = bf16[4,4,2,284]{3,2,1,0:T(2,128)(2,1)S(1)} collective-permute-done((bf16[4,4,2,284]{3,2,1,0:T(2,128)(2,1)S(1)}, bf16[4,4,2,284]{3,2,1,0:T(2,128)(2,1)S(1)}, u32[]{:S(2)}, u32[]{:S(2)}) %collective-permute-start.2) | collective-permute-done | bytes 18208 | tf_op jit(solution)/shard_map/ppermute | solution.py:21
  12.8 2.7 %collective-permute-start.3 = (bf16[8,4,2,284]{3,2,1,0:T(2,128)(2,1)S(1)}, bf16[8,4,2,284]{3,2,1,0:T(2,128)(2,1)S(1)}, u32[]{:S(2)}, u32[]{:S(2)}) collective-permute-start(bf16[8,4,2,284]{3,2,1,0:T(2,128)(2,1)S(1)} %broadcast_select_fusion.6), channel_id=1, source_target_pairs={{0,8},{1,9},{2,10},{3,11},{4,12},{5,13},{6,14},{7,15},{8,0},{9,1},... | collective-permute-start | bytes 109064 | tf_op jit(solution)/shard_map/ppermute | solution.py:21
  15.5 0.7 compare_and_fusion
  16.2 0.8 dynamic-slice.4
  17.0 0.8 dynamic-slice.5
  18.5 0.6 collective-permute-start.4
  19.1 4.1 %collective-permute-done.4 = bf16[1,16,4,2,284]{4,3,2,1,0:T(2,128)(2,1)S(1)} collective-permute-done((bf16[1,16,4,2,284]{4,3,2,1,0:T(2,128)(2,1)S(1)}, bf16[1,16,4,2,284]{4,3,2,1,0:T(2,128)(2,1)S(1)}, u32[]{:S(2)}, u32[]{:S(2)}) %collective-permute-start.4) | collective-permute-done | bytes 72736 | tf_op jit(solution)/shard_map/ppermute | solution.py:21
  23.8 0.7 gather_fusion.1
  25.6 3.5 %fusion.102 = f32[16,1136]{1,0:T(8,128)S(1)} fusion(bf16[2272,1136]{1,0:T(8,128)(2,1)} %param.20, f32[2272]{0:T(1024)S(1)} %dynamic-slice.5, f32[2272]{0:T(1024)S(1)} %dynamic-slice.4, f32[16]{0:T(128)S(1)} %rsqrt.12, f32[16]{0:T(128)S(1)} %div.67, bf16[16,4544]{1,0:T(8,128)(2,1)S(1)} %broadcast_select_fusion.4, s32[]{:T(128)S(6)} %select_n.293), kind=kOutput, calls=%fused_computation.217 | convolution fusion | flops 82809856 | bytes 5334020 | tf_op jit(solution)/shard_map/dot_general | solution.py:128
  29.9 0.6 collective-permute-start.5
  30.6 4.1 %collective-permute-done.5 = f32[16,1548]{1,0:T(8,128)S(1)} collective-permute-done((f32[16,1548]{1,0:T(8,128)S(1)}, f32[16,1548]{1,0:T(8,128)S(1)}, u32[]{:S(2)}, u32[]{:S(2)}) %collective-permute-start.5) | collective-permute-done | bytes 99104 | tf_op jit(solution)/shard_map/ppermute | solution.py:33
  35.2 1.0 collective-permute-done.6
  36.2 1.6 %collective-permute-start.7 = (bf16[2,4,2,284]{3,2,1,0:T(2,128)(2,1)S(1)}, bf16[2,4,2,284]{3,2,1,0:T(2,128)(2,1)S(1)}, u32[]{:S(2)}, u32[]{:S(2)}) collective-permute-start(bf16[2,4,2,284]{3,2,1,0:T(2,128)(2,1)S(1)} %broadcast_select_fusion.9), channel_id=1, source_target_pairs={{0,2},{1,3},{2,0},{3,1},{4,6},{5,7},{6,4},{7,5},{8,10},{9,11},{10,... | collective-permute-start | bytes 27272 | tf_op jit(solution)/shard_map/ppermute | solution.py:21
  37.8 2.1 %collective-permute-done.7 = bf16[2,4,2,284]{3,2,1,0:T(2,128)(2,1)S(1)} collective-permute-done((bf16[2,4,2,284]{3,2,1,0:T(2,128)(2,1)S(1)}, bf16[2,4,2,284]{3,2,1,0:T(2,128)(2,1)S(1)}, u32[]{:S(2)}, u32[]{:S(2)}) %collective-permute-start.7) | collective-permute-done | bytes 9120 | tf_op jit(solution)/shard_map/ppermute | solution.py:21
  40.0 1.6 %collective-permute-start.8 = (bf16[4,4,2,284]{3,2,1,0:T(2,128)(2,1)S(1)}, bf16[4,4,2,284]{3,2,1,0:T(2,128)(2,1)S(1)}, u32[]{:S(2)}, u32[]{:S(2)}) collective-permute-start(bf16[4,4,2,284]{3,2,1,0:T(2,128)(2,1)S(1)} %broadcast_select_fusion.7), channel_id=1, source_target_pairs={{0,4},{1,5},{2,6},{3,7},{4,0},{5,1},{6,2},{7,3},{8,12},{9,13},{10,... | collective-permute-start | bytes 54536 | tf_op jit(solution)/shard_map/ppermute | solution.py:21
  41.6 2.2 %collective-permute-done.8 = bf16[4,4,2,284]{3,2,1,0:T(2,128)(2,1)S(1)} collective-permute-done((bf16[4,4,2,284]{3,2,1,0:T(2,128)(2,1)S(1)}, bf16[4,4,2,284]{3,2,1,0:T(2,128)(2,1)S(1)}, u32[]{:S(2)}, u32[]{:S(2)}) %collective-permute-start.8) | collective-permute-done | bytes 18208 | tf_op jit(solution)/shard_map/ppermute | solution.py:21
  44.0 2.4 %collective-permute-start.9 = (bf16[8,4,2,284]{3,2,1,0:T(2,128)(2,1)S(1)}, bf16[8,4,2,284]{3,2,1,0:T(2,128)(2,1)S(1)}, u32[]{:S(2)}, u32[]{:S(2)}) collective-permute-start(bf16[8,4,2,284]{3,2,1,0:T(2,128)(2,1)S(1)} %broadcast_select_fusion.5), channel_id=1, source_target_pairs={{0,8},{1,9},{2,10},{3,11},{4,12},{5,13},{6,14},{7,15},{8,0},{9,1},... | collective-permute-start | bytes 109064 | tf_op jit(solution)/shard_map/ppermute | solution.py:21
  46.6 2.5 %collective-permute-done.9 = bf16[8,4,2,284]{3,2,1,0:T(2,128)(2,1)S(1)} collective-permute-done((bf16[8,4,2,284]{3,2,1,0:T(2,128)(2,1)S(1)}, bf16[8,4,2,284]{3,2,1,0:T(2,128)(2,1)S(1)}, u32[]{:S(2)}, u32[]{:S(2)}) %collective-permute-start.9) | collective-permute-done | bytes 36384 | tf_op jit(solution)/shard_map/ppermute | solution.py:21
  50.8 0.5 select_reduce_fusion
  52.3 1.5 %collective-permute-done.10 = f32[2,284,66]{1,2,0:T(8,128)S(1)} collective-permute-done((f32[2,284,66]{1,2,0:T(8,128)S(1)}, f32[2,284,66]{1,2,0:T(8,128)S(1)}, u32[]{:S(2)}, u32[]{:S(2)}) %collective-permute-start.10) | collective-permute-done | bytes 149984 | tf_op jit(solution)/shard_map/ppermute | solution.py:54
  53.9 1.6 %collective-permute-start.11 = (f32[2,284,66]{1,2,0:T(8,128)S(1)}, f32[2,284,66]{1,2,0:T(8,128)S(1)}, u32[]{:S(2)}, u32[]{:S(2)}) collective-permute-start(f32[2,284,66]{1,2,0:T(8,128)S(1)} %pad_maximum_fusion.1), channel_id=1, source_target_pairs={{0,2},{1,3},{2,0},{3,1},{4,6},{5,7},{6,4},{7,5},{8,10},{9,11},{10,... | collective-permute-start | bytes 449864 | tf_op jit(solution)/shard_map/ppermute | solution.py:54
  55.5 0.6 scatter_custom_fusion
  56.1 5.3 %collective-permute-done.11 = f32[2,284,66]{1,2,0:T(8,128)S(1)} collective-permute-done((f32[2,284,66]{1,2,0:T(8,128)S(1)}, f32[2,284,66]{1,2,0:T(8,128)S(1)}, u32[]{:S(2)}, u32[]{:S(2)}) %collective-permute-start.11) | collective-permute-done | bytes 149984 | tf_op jit(solution)/shard_map/ppermute | solution.py:54
  61.6 1.6 %collective-permute-start.12 = (f32[2,284,66]{1,2,0:T(8,128)S(1)}, f32[2,284,66]{1,2,0:T(8,128)S(1)}, u32[]{:S(2)}, u32[]{:S(2)}) collective-permute-start(f32[2,284,66]{1,2,0:T(8,128)S(1)} %pad_maximum_fusion.2), channel_id=1, source_target_pairs={{0,4},{1,5},{2,6},{3,7},{4,0},{5,1},{6,2},{7,3},{8,12},{9,13},{10,... | collective-permute-start | bytes 449864 | tf_op jit(solution)/shard_map/ppermute | solution.py:54
  63.2 5.1 %collective-permute-done.12 = f32[2,284,66]{1,2,0:T(8,128)S(1)} collective-permute-done((f32[2,284,66]{1,2,0:T(8,128)S(1)}, f32[2,284,66]{1,2,0:T(8,128)S(1)}, u32[]{:S(2)}, u32[]{:S(2)}) %collective-permute-start.12) | collective-permute-done | bytes 149984 | tf_op jit(solution)/shard_map/ppermute | solution.py:54
  68.4 2.6 %collective-permute-start.13 = (f32[2,284,66]{1,2,0:T(8,128)S(1)}, f32[2,284,66]{1,2,0:T(8,128)S(1)}, u32[]{:S(2)}, u32[]{:S(2)}) collective-permute-start(f32[2,284,66]{1,2,0:T(8,128)S(1)} %pad_maximum_fusion.3), channel_id=1, source_target_pairs={{0,8},{1,9},{2,10},{3,11},{4,12},{5,13},{6,14},{7,15},{8,0},{9,1},... | collective-permute-start | bytes 449864 | tf_op jit(solution)/shard_map/ppermute | solution.py:54
  71.0 9.0 %collective-permute-done.13 = f32[2,284,66]{1,2,0:T(8,128)S(1)} collective-permute-done((f32[2,284,66]{1,2,0:T(8,128)S(1)}, f32[2,284,66]{1,2,0:T(8,128)S(1)}, u32[]{:S(2)}, u32[]{:S(2)}) %collective-permute-start.13) | collective-permute-done | bytes 149984 | tf_op jit(solution)/shard_map/ppermute | solution.py:54
  80.6 0.6 collective-permute-start.14
  81.2 3.0 %collective-permute-done.14 = bf16[1,4,2,284]{3,1,2,0:T(4,128)(2,1)S(1)} collective-permute-done((bf16[1,4,2,284]{3,1,2,0:T(4,128)(2,1)S(1)}, bf16[1,4,2,284]{3,1,2,0:T(4,128)(2,1)S(1)}, u32[]{:S(2)}, u32[]{:S(2)}) %collective-permute-start.14) | collective-permute-done | bytes 4576 | tf_op jit(solution)/shard_map/ppermute | solution.py:21
  84.6 3.4 %convolution_add_fusion = f32[16,2272]{1,0:T(8,128)S(1)} fusion(f32[16,2272]{1,0:T(8,128)S(1)} %fusion.105, bf16[1136,2272]{1,0:T(8,128)(2,1)} %param.21, f32[16,1548]{1,0:T(8,128)S(1)} %add.175), kind=kOutput, calls=%fused_computation.4 | convolution fusion | flops 83809536 | bytes 5528576 | tf_op jit(solution)/shard_map/dot_general | solution.py:191
  88.1 0.6 gather_fusion.2
  89.2 6.6 %collective-permute-done.15 = f32[8,4,2,284]{3,0,2,1:T(8,128)S(1)} collective-permute-done((f32[8,4,2,284]{3,0,2,1:T(8,128)S(1)}, f32[8,4,2,284]{3,0,2,1:T(8,128)S(1)}, u32[]{:S(2)}, u32[]{:S(2)}) %collective-permute-start.15) | collective-permute-done | bytes 72736 | tf_op jit(solution)/shard_map/ppermute | solution.py:46
  96.0 3.9 %collective-permute-done.16 = f32[4,4,2,284]{3,0,2,1:T(4,128)S(1)} collective-permute-done((f32[4,4,2,284]{3,0,2,1:T(4,128)S(1)}, f32[4,4,2,284]{3,0,2,1:T(4,128)S(1)}, u32[]{:S(2)}, u32[]{:S(2)}) %collective-permute-start.16) | collective-permute-done | bytes 36384 | tf_op jit(solution)/shard_map/ppermute | solution.py:46
  100.0 1.6 %collective-permute-start.17 = (f32[2,4,2,284]{3,0,2,1:T(2,128)S(1)}, f32[2,4,2,284]{3,0,2,1:T(2,128)S(1)}, u32[]{:S(2)}, u32[]{:S(2)}) collective-permute-start(f32[2,4,2,284]{3,0,2,1:T(2,128)S(1)} %broadcast_select_fusion.11), channel_id=1, source_target_pairs={{0,2},{1,3},{2,0},{3,1},{4,6},{5,7},{6,4},{7,5},{8,10},{9,11},{10,... | collective-permute-start | bytes 54536 | tf_op jit(solution)/shard_map/ppermute | solution.py:46
  101.6 2.3 %collective-permute-done.17 = f32[2,4,2,284]{3,0,2,1:T(2,128)S(1)} collective-permute-done((f32[2,4,2,284]{3,0,2,1:T(2,128)S(1)}, f32[2,4,2,284]{3,0,2,1:T(2,128)S(1)}, u32[]{:S(2)}, u32[]{:S(2)}) %collective-permute-start.17) | collective-permute-done | bytes 18208 | tf_op jit(solution)/shard_map/ppermute | solution.py:46
  104.0 1.2 %collective-permute-done.18 = f32[1,4,2,284]{3,0,2,1:T(1,128)S(1)} collective-permute-done((f32[1,4,2,284]{3,0,2,1:T(1,128)S(1)}, f32[1,4,2,284]{3,0,2,1:T(1,128)S(1)}, u32[]{:S(2)}, u32[]{:S(2)}) %collective-permute-start.18) | collective-permute-done | bytes 9120 | tf_op jit(solution)/shard_map/ppermute | solution.py:46
  105.2 2.9 %collective-permute-start.19 = (f32[4,2,284]{2,1,0:T(2,128)S(1)}, f32[4,2,284]{2,1,0:T(2,128)S(1)}, u32[]{:S(2)}, u32[]{:S(2)}) collective-permute-start(f32[4,2,284]{2,1,0:T(2,128)S(1)} %bitcast.127), channel_id=1, source_target_pairs={{0,0},{1,1},{2,2},{3,3},{4,4},{5,5},{6,6},{7,7},{8,16},{9,17},{10,... | collective-permute-start | bytes 27272 | tf_op jit(solution)/shard_map/ppermute | solution.py:207
  108.1 0.8 copy.99
  108.9 3.6 %collective-permute-done.19 = f32[4,2,284]{2,1,0:T(2,128)S(1)} collective-permute-done((f32[4,2,284]{2,1,0:T(2,128)S(1)}, f32[4,2,284]{2,1,0:T(2,128)S(1)}, u32[]{:S(2)}, u32[]{:S(2)}) %collective-permute-start.19) | collective-permute-done | bytes 9120 | tf_op jit(solution)/shard_map/ppermute | solution.py:207
  112.6 0.6 add_convert_fusion.1
  (140 shorter events, 10.0 us)
Async XLA Ops:
  0.6 83.6 %copy-start = (bf16[284,2272]{1,0:T(8,128)(2,1)S(1)}, bf16[284,2272]{1,0:T(8,128)(2,1)}, u32[]{:S(2)}) copy-start(bf16[284,2272]{1,0:T(8,128)(2,1)} %param.19) | copy-start | bytes 3871492
  0.6 17.1 %copy-start.3 = (bf16[2,512,128]{2,1,0:T(8,128)(2,1)S(1)}, bf16[2,512,128]{2,1,0:T(8,128)(2,1)}, u32[]{:S(2)}) copy-start(bf16[2,512,128]{2,1,0:T(8,128)(2,1)} %param.12) | copy-start | bytes 786436
  0.7 3.5 %collective-permute-start = (bf16[1,4,2,284]{3,2,1,0:T(2,128)(2,1)}, bf16[1,4,2,284]{3,2,1,0:T(2,128)(2,1)S(1)}, u32[]{:S(2)}, u32[]{:S(2)}) collective-permute-start(bf16[1,4,2,284]{3,2,1,0:T(2,128)(2,1)} %bitcast.115), channel_id=1, source_target_pairs={{0,1},{1,0},{2,3},{3,2},{4,5},{5,4},{6,7},{7,6},{8,9},{9,8},{10,11... | collective-permute-start | bytes 13640 | tf_op jit(solution)/shard_map/ppermute | solution.py:21
  5.0 3.8 %collective-permute-start.1 = (bf16[2,4,2,284]{3,2,1,0:T(2,128)(2,1)S(1)}, bf16[2,4,2,284]{3,2,1,0:T(2,128)(2,1)S(1)}, u32[]{:S(2)}, u32[]{:S(2)}) collective-permute-start(bf16[2,4,2,284]{3,2,1,0:T(2,128)(2,1)S(1)} %broadcast_select_fusion.10), channel_id=1, source_target_pairs={{0,2},{1,3},{2,0},{3,1},{4,6},{5,7},{6,4},{7,5},{8,10},{9,11},{10,... | collective-permute-start | bytes 27272 | tf_op jit(solution)/shard_map/ppermute | solution.py:21
  8.8 3.9 %collective-permute-start.2 = (bf16[4,4,2,284]{3,2,1,0:T(2,128)(2,1)S(1)}, bf16[4,4,2,284]{3,2,1,0:T(2,128)(2,1)S(1)}, u32[]{:S(2)}, u32[]{:S(2)}) collective-permute-start(bf16[4,4,2,284]{3,2,1,0:T(2,128)(2,1)S(1)} %broadcast_select_fusion.8), channel_id=1, source_target_pairs={{0,4},{1,5},{2,6},{3,7},{4,0},{5,1},{6,2},{7,3},{8,12},{9,13},{10,... | collective-permute-start | bytes 54536 | tf_op jit(solution)/shard_map/ppermute | solution.py:21
  12.8 5.4 %collective-permute-start.3 = (bf16[8,4,2,284]{3,2,1,0:T(2,128)(2,1)S(1)}, bf16[8,4,2,284]{3,2,1,0:T(2,128)(2,1)S(1)}, u32[]{:S(2)}, u32[]{:S(2)}) collective-permute-start(bf16[8,4,2,284]{3,2,1,0:T(2,128)(2,1)S(1)} %broadcast_select_fusion.6), channel_id=1, source_target_pairs={{0,8},{1,9},{2,10},{3,11},{4,12},{5,13},{6,14},{7,15},{8,0},{9,1},... | collective-permute-start | bytes 109064 | tf_op jit(solution)/shard_map/ppermute | solution.py:21
  18.5 4.7 %collective-permute-start.4 = (bf16[1,16,4,2,284]{4,3,2,1,0:T(2,128)(2,1)S(1)}, bf16[1,16,4,2,284]{4,3,2,1,0:T(2,128)(2,1)S(1)}, u32[]{:S(2)}, u32[]{:S(2)}) collective-permute-start(bf16[1,16,4,2,284]{4,3,2,1,0:T(2,128)(2,1)S(1)} %broadcast_select_fusion.1), channel_id=1, source_target_pairs={{0,16},{16,0},{1,17},{17,1},{2,18},{18,2},{3,19},{19,3},{4,20},{20... | collective-permute-start | bytes 218120 | tf_op jit(solution)/shard_map/ppermute | solution.py:21
  25.6 3.5 %copy-start.2 = (bf16[2272,128]{1,0:T(8,128)(2,1)S(1)}, bf16[2272,128]{1,0:T(8,128)(2,1)}, u32[]{:S(2)}) copy-start(bf16[2272,128]{1,0:T(8,128)(2,1)} %param.18) | copy-start | bytes 1744900
  25.6 3.8 %copy-start.1 = (bf16[2272,284]{0,1:T(8,128)(2,1)S(1)}, bf16[2272,284]{0,1:T(8,128)(2,1)}, u32[]{:S(2)}) copy-start(bf16[2272,284]{0,1:T(8,128)(2,1)} %param.17) | copy-start | bytes 3871492
  29.9 4.8 %collective-permute-start.5 = (f32[16,1548]{1,0:T(8,128)S(1)}, f32[16,1548]{1,0:T(8,128)S(1)}, u32[]{:S(2)}, u32[]{:S(2)}) collective-permute-start(f32[16,1548]{1,0:T(8,128)S(1)} %concatenate.160), channel_id=1, source_target_pairs={{0,16},{16,0},{1,17},{17,1},{2,18},{18,2},{3,19},{19,3},{4,20},{20... | collective-permute-start | bytes 297224 | tf_op jit(solution)/shard_map/ppermute | solution.py:33
  34.9 1.2 %collective-permute-start.6 = (bf16[1,4,2,284]{3,2,1,0:T(2,128)(2,1)S(1)}, bf16[1,4,2,284]{3,2,1,0:T(2,128)(2,1)S(1)}, u32[]{:S(2)}, u32[]{:S(2)}) collective-permute-start(bf16[1,4,2,284]{3,2,1,0:T(2,128)(2,1)S(1)} %dynamic-slice_bitcast_fusion.1), channel_id=1, source_target_pairs={{0,1},{1,0},{2,3},{3,2},{4,5},{5,4},{6,7},{7,6},{8,9},{9,8},{10,11... | collective-permute-start | bytes 13640 | tf_op jit(solution)/shard_map/ppermute | solution.py:21
  36.2 3.8 %collective-permute-start.7 = (bf16[2,4,2,284]{3,2,1,0:T(2,128)(2,1)S(1)}, bf16[2,4,2,284]{3,2,1,0:T(2,128)(2,1)S(1)}, u32[]{:S(2)}, u32[]{:S(2)}) collective-permute-start(bf16[2,4,2,284]{3,2,1,0:T(2,128)(2,1)S(1)} %broadcast_select_fusion.9), channel_id=1, source_target_pairs={{0,2},{1,3},{2,0},{3,1},{4,6},{5,7},{6,4},{7,5},{8,10},{9,11},{10,... | collective-permute-start | bytes 27272 | tf_op jit(solution)/shard_map/ppermute | solution.py:21
  40.0 3.9 %collective-permute-start.8 = (bf16[4,4,2,284]{3,2,1,0:T(2,128)(2,1)S(1)}, bf16[4,4,2,284]{3,2,1,0:T(2,128)(2,1)S(1)}, u32[]{:S(2)}, u32[]{:S(2)}) collective-permute-start(bf16[4,4,2,284]{3,2,1,0:T(2,128)(2,1)S(1)} %broadcast_select_fusion.7), channel_id=1, source_target_pairs={{0,4},{1,5},{2,6},{3,7},{4,0},{5,1},{6,2},{7,3},{8,12},{9,13},{10,... | collective-permute-start | bytes 54536 | tf_op jit(solution)/shard_map/ppermute | solution.py:21
  44.0 5.1 %collective-permute-start.9 = (bf16[8,4,2,284]{3,2,1,0:T(2,128)(2,1)S(1)}, bf16[8,4,2,284]{3,2,1,0:T(2,128)(2,1)S(1)}, u32[]{:S(2)}, u32[]{:S(2)}) collective-permute-start(bf16[8,4,2,284]{3,2,1,0:T(2,128)(2,1)S(1)} %broadcast_select_fusion.5), channel_id=1, source_target_pairs={{0,8},{1,9},{2,10},{3,11},{4,12},{5,13},{6,14},{7,15},{8,0},{9,1},... | collective-permute-start | bytes 109064 | tf_op jit(solution)/shard_map/ppermute | solution.py:21
  52.2 1.5 %collective-permute-start.10 = (f32[2,284,66]{1,2,0:T(8,128)S(1)}, f32[2,284,66]{1,2,0:T(8,128)S(1)}, u32[]{:S(2)}, u32[]{:S(2)}) collective-permute-start(f32[2,284,66]{1,2,0:T(8,128)S(1)} %pad_maximum_fusion), channel_id=1, source_target_pairs={{0,1},{1,0},{2,3},{3,2},{4,5},{5,4},{6,7},{7,6},{8,9},{9,8},{10,11... | collective-permute-start | bytes 449864 | tf_op jit(solution)/shard_map/ppermute | solution.py:54
  53.9 7.5 %collective-permute-start.11 = (f32[2,284,66]{1,2,0:T(8,128)S(1)}, f32[2,284,66]{1,2,0:T(8,128)S(1)}, u32[]{:S(2)}, u32[]{:S(2)}) collective-permute-start(f32[2,284,66]{1,2,0:T(8,128)S(1)} %pad_maximum_fusion.1), channel_id=1, source_target_pairs={{0,2},{1,3},{2,0},{3,1},{4,6},{5,7},{6,4},{7,5},{8,10},{9,11},{10,... | collective-permute-start | bytes 449864 | tf_op jit(solution)/shard_map/ppermute | solution.py:54
  61.6 6.7 %collective-permute-start.12 = (f32[2,284,66]{1,2,0:T(8,128)S(1)}, f32[2,284,66]{1,2,0:T(8,128)S(1)}, u32[]{:S(2)}, u32[]{:S(2)}) collective-permute-start(f32[2,284,66]{1,2,0:T(8,128)S(1)} %pad_maximum_fusion.2), channel_id=1, source_target_pairs={{0,4},{1,5},{2,6},{3,7},{4,0},{5,1},{6,2},{7,3},{8,12},{9,13},{10,... | collective-permute-start | bytes 449864 | tf_op jit(solution)/shard_map/ppermute | solution.py:54
  68.4 11.6 %collective-permute-start.13 = (f32[2,284,66]{1,2,0:T(8,128)S(1)}, f32[2,284,66]{1,2,0:T(8,128)S(1)}, u32[]{:S(2)}, u32[]{:S(2)}) collective-permute-start(f32[2,284,66]{1,2,0:T(8,128)S(1)} %pad_maximum_fusion.3), channel_id=1, source_target_pairs={{0,8},{1,9},{2,10},{3,11},{4,12},{5,13},{6,14},{7,15},{8,0},{9,1},... | collective-permute-start | bytes 449864 | tf_op jit(solution)/shard_map/ppermute | solution.py:54
  80.6 3.6 %collective-permute-start.14 = (bf16[1,4,2,284]{3,1,2,0:T(4,128)(2,1)S(1)}, bf16[1,4,2,284]{3,1,2,0:T(4,128)(2,1)S(1)}, u32[]{:S(2)}, u32[]{:S(2)}) collective-permute-start(bf16[1,4,2,284]{3,1,2,0:T(4,128)(2,1)S(1)} %dynamic-slice_bitcast_fusion), channel_id=1, source_target_pairs={{0,16},{16,0},{1,17},{17,1},{2,18},{18,2},{3,19},{19,3},{4,20},{20... | collective-permute-start | bytes 13640 | tf_op jit(solution)/shard_map/ppermute | solution.py:21
  89.0 23.6 %copy-start.4 = (bf16[4,2,284]{2,1,0:T(2,128)(2,1)S(1)}, bf16[4,2,284]{2,1,0:T(2,128)(2,1)}, u32[]{:S(2)}) copy-start(bf16[4,2,284]{2,1,0:T(2,128)(2,1)} %param.11) | copy-start | bytes 13636
  89.1 6.7 %collective-permute-start.15 = (f32[8,4,2,284]{3,0,2,1:T(8,128)S(1)}, f32[8,4,2,284]{3,0,2,1:T(8,128)S(1)}, u32[]{:S(2)}, u32[]{:S(2)}) collective-permute-start(f32[8,4,2,284]{3,0,2,1:T(8,128)S(1)} %select_bitcast_fusion.1), channel_id=1, source_target_pairs={{0,8},{1,9},{2,10},{3,11},{4,12},{5,13},{6,14},{7,15},{8,0},{9,1},... | collective-permute-start | bytes 218120 | tf_op jit(solution)/shard_map/ppermute | solution.py:46
  95.8 4.2 %collective-permute-start.16 = (f32[4,4,2,284]{3,0,2,1:T(4,128)S(1)}, f32[4,4,2,284]{3,0,2,1:T(4,128)S(1)}, u32[]{:S(2)}, u32[]{:S(2)}) collective-permute-start(f32[4,4,2,284]{3,0,2,1:T(4,128)S(1)} %slice_select_fusion), channel_id=1, source_target_pairs={{0,4},{1,5},{2,6},{3,7},{4,0},{5,1},{6,2},{7,3},{8,12},{9,13},{10,... | collective-permute-start | bytes 109064 | tf_op jit(solution)/shard_map/ppermute | solution.py:46
  100.0 3.9 %collective-permute-start.17 = (f32[2,4,2,284]{3,0,2,1:T(2,128)S(1)}, f32[2,4,2,284]{3,0,2,1:T(2,128)S(1)}, u32[]{:S(2)}, u32[]{:S(2)}) collective-permute-start(f32[2,4,2,284]{3,0,2,1:T(2,128)S(1)} %broadcast_select_fusion.11), channel_id=1, source_target_pairs={{0,2},{1,3},{2,0},{3,1},{4,6},{5,7},{6,4},{7,5},{8,10},{9,11},{10,... | collective-permute-start | bytes 54536 | tf_op jit(solution)/shard_map/ppermute | solution.py:46
  103.9 1.2 %collective-permute-start.18 = (f32[1,4,2,284]{3,0,2,1:T(1,128)S(1)}, f32[1,4,2,284]{3,0,2,1:T(1,128)S(1)}, u32[]{:S(2)}, u32[]{:S(2)}) collective-permute-start(f32[1,4,2,284]{3,0,2,1:T(1,128)S(1)} %broadcast_select_fusion.12), channel_id=1, source_target_pairs={{0,1},{1,0},{2,3},{3,2},{4,5},{5,4},{6,7},{7,6},{8,9},{9,8},{10,11... | collective-permute-start | bytes 27272 | tf_op jit(solution)/shard_map/ppermute | solution.py:46
  105.2 7.4 %collective-permute-start.19 = (f32[4,2,284]{2,1,0:T(2,128)S(1)}, f32[4,2,284]{2,1,0:T(2,128)S(1)}, u32[]{:S(2)}, u32[]{:S(2)}) collective-permute-start(f32[4,2,284]{2,1,0:T(2,128)S(1)} %bitcast.127), channel_id=1, source_target_pairs={{0,0},{1,1},{2,2},{3,3},{4,4},{5,5},{6,6},{7,7},{8,16},{9,17},{10,... | collective-permute-start | bytes 27272 | tf_op jit(solution)/shard_map/ppermute | solution.py:207

commit v3 on v2

--- a/solution.py
+++ b/solution.py
@@ -15,16 +15,18 @@
 
 def gather_blocks(block, axis, size):
     index = lax.axis_index(axis)
-    blocks = block[None]
-    bit = 1
-    while bit < size:
+    levels = size.bit_length() - 1
+    blocks = block.reshape((1,) * levels + block.shape)
+    for level in range(levels):
+        bit = 2 ** (levels - 1 - level)
         other = lax.ppermute(blocks, axis, xor_pairs(size, bit))
         low = (index // bit) % 2 == 0
         blocks = jnp.where(
-            low, jnp.concatenate([blocks, other]), jnp.concatenate([other, blocks])
+            low,
+            jnp.concatenate([blocks, other], axis=level),
+            jnp.concatenate([other, blocks], axis=level),
         )
-        bit *= 2
-    return blocks
+    return blocks.reshape((size,) + block.shape)
 
 
 def sum_over(value, axis, size):
@@ -37,29 +39,52 @@
 
 def scatter_sum(blocks, axis, size):
     index = lax.axis_index(axis)
-    bit = size // 2
-    while bit >= 1:
-        half = blocks.shape[0] // 2
+    levels = size.bit_length() - 1
+    blocks = blocks.reshape((2,) * levels + blocks.shape[1:])
+    for level in range(levels):
+        bit = 2 ** level
+        place = levels - 1 - level
         high = (index // bit) % 2 == 1
-        keep = jnp.where(high, blocks[half:], blocks[:half])
-        send = jnp.where(high, blocks[:half], blocks[half:])
+        lower = lax.index_in_dim(blocks, 0, place, keepdims=False)
+        upper = lax.index_in_dim(blocks, 1, place, keepdims=False)
+        keep = jnp.where(high, upper, lower)
+        send = jnp.where(high, lower, upper)
         blocks = keep + lax.ppermute(send, axis, xor_pairs(size, bit))
-        bit //= 2
-    return blocks[0]
-
-
-def merge_over(packed, axis, size):
+    return blocks
+
+
+def split_exact(value):
+    high = lax.reduce_precision(value, exponent_bits=8, mantissa_bits=7)
+    rest = value - high
+    middle = lax.reduce_precision(rest, exponent_bits=8, mantissa_bits=7)
+    low = rest - middle
+    return [part.astype(jnp.bfloat16) for part in (high, middle, low)]
+
+
+def join_exact(pieces):
+    pieces = pieces.astype(jnp.float32)
+    return (pieces[..., 0] + pieces[..., 1]) + pieces[..., 2]
+
+
+def merge_over(peak, total, weighted, axis, size):
     bit = 1
     while bit < size:
-        other = lax.ppermute(packed, axis, xor_pairs(size, bit))
-        peak_first, peak_second = packed[..., 0], other[..., 0]
-        peak = jnp.maximum(peak_first, peak_second)
-        scale_first = jnp.exp(peak_first - peak)[..., None]
-        scale_second = jnp.exp(peak_second - peak)[..., None]
-        merged = packed[..., 1:] * scale_first + other[..., 1:] * scale_second
-        packed = jnp.concatenate([peak[..., None], merged], axis=-1)
+        sent = jnp.concatenate(
+            [jnp.stack(split_exact(peak) + split_exact(total), axis=-1), weighted.astype(jnp.bfloat16)],
+            axis=-1,
+        )
+        other = lax.ppermute(sent, axis, xor_pairs(size, bit))
+        peak_second = join_exact(other[..., 0:3])
+        total_second = join_exact(other[..., 3:6])
+        weighted_second = other[..., 6:].astype(jnp.float32)
+        merged_peak = jnp.maximum(peak, peak_second)
+        scale_first = jnp.exp(peak - merged_peak)
+        scale_second = jnp.exp(peak_second - merged_peak)
+        total = total * scale_first + total_second * scale_second
+        weighted = weighted * scale_first[..., None] + weighted_second * scale_second[..., None]
+        peak = merged_peak
         bit *= 2
-    return packed
+    return peak, total, weighted
 
 
 def layer_norm(row_block, norm_gain, norm_bias):
@@ -117,19 +142,21 @@
     step_offsets = jnp.arange(steps, dtype=jnp.int32)
     positions = slot_lengths[None, :] + step_offsets[:, None]
 
-    every = gather_blocks(gather_blocks(states, "seq", seq_size), "req", req_size)
-    every = every.transpose(2, 0, 3, 1, 4).reshape(steps, total, model_width)
+    every = gather_blocks(gather_blocks(states, "req", req_size), "seq", seq_size)
+    every = every.transpose(2, 1, 3, 0, 4).reshape(steps, total, model_width)
     current_all = jnp.take(every, placement, axis=1)
     normed = layer_norm(current_all.reshape(rows, model_width), norm_gain, norm_bias)
     normed_part = lax.dynamic_slice_in_dim(normed, group_index * part_width, part_width, 1)
 
     part_query = jnp.dot(normed_part, w_query, preferred_element_type=jnp.float32)
     part_keyval = jnp.dot(normed_part, w_keyval, preferred_element_type=jnp.float32)
+    first = sum_over(jnp.concatenate([part_query, part_keyval], axis=1), "req", req_size)
+    query_raw = first[:, :slice_width].astype(jnp.bfloat16).reshape(steps, total, slice_width)
+    keyval = first[:, slice_width:].reshape(steps, total, 2 * head_width)
     part_up = jnp.dot(normed_part, w_up, preferred_element_type=jnp.float32)
-    first = sum_over(jnp.concatenate([part_query, part_keyval, part_up], axis=1), "req", req_size)
-    query_raw = first[:, :slice_width].astype(jnp.bfloat16).reshape(steps, total, slice_width)
-    keyval = first[:, slice_width : slice_width + 2 * head_width].reshape(steps, total, 2 * head_width)
-    up_part = first[:, slice_width + 2 * head_width :]
+    up_part = sum_over(part_up, "req", req_size)
+    hidden = jax.nn.gelu(up_part, approximate=False).astype(jnp.bfloat16)
+    down_part = jnp.dot(hidden, w_down, preferred_element_type=jnp.float32)
 
     own_query = lax.dynamic_slice_in_dim(query_raw, group_index * group_rows, group_rows, 1)
     query_all = gather_blocks(own_query, "seq", seq_size)
@@ -173,11 +200,10 @@
         "gqs,gsd->gqd", weights, value_rows, preferred_element_type=jnp.float32
     )
 
-    packed = jnp.concatenate(
-        [local_peak[:, :, None], local_total[:, :, None], local_weighted], axis=-1
-    )
-    packed = merge_over(packed, "seq", seq_size)
-    mixed = packed[:, :, 2:] / packed[:, :, 1:2]
+    _, merged_total, merged_weighted = merge_over(
+        local_peak, local_total, local_weighted, "seq", seq_size
+    )
+    mixed = merged_weighted / merged_total[:, :, None]
     mixed = (
         mixed.reshape(group_rows, steps, model_width)
         .transpose(1, 0, 2)
@@ -187,10 +213,7 @@
     every_mixed = gather_blocks(own_mixed, "req", req_size)
     mixed_part = every_mixed.transpose(1, 0, 2, 3).reshape(rows, slice_width)
 
-    hidden = jax.nn.gelu(up_part, approximate=False).astype(jnp.bfloat16)
-    partial_sum = jnp.dot(mixed_part, w_out, preferred_element_type=jnp.float32) + jnp.dot(
-        hidden, w_down, preferred_element_type=jnp.float32
-    )
+    partial_sum = jnp.dot(mixed_part, w_out, preferred_element_type=jnp.float32) + down_part
     inverse = (
         jnp.zeros((total,), jnp.int32).at[placement].set(jnp.arange(total, dtype=jnp.int32))
     )

time: 114 us -> 106 us (0.930)
  waiting for transfers between devices: 61.1 us -> 39.6 us
  starting transfers between devices: 24.2 us -> 33.2 us
  other arithmetic: 8.37 us -> 10.6 us
  local copies, waits for them, and re-layouts: 9.38 us -> 11.6 us
    ppermute x4, waiting for transfers between devices: 20.8 us -> 9.5 us  [merge_over(): other = lax.ppermute(sent, axis, xor_pairs(size, bit))]
    ppermute x10, waiting for transfers between devices: 18.6 us -> 12.3 us  [gather_blocks(): other = lax.ppermute(blocks, axis, xor_pairs(size, bit))]
    ppermute x4, waiting for transfers between devices: 13.9 us -> 9.57 us  [scatter_sum(): blocks = keep + lax.ppermute(send, axis, xor_pairs(size, bit))]
    ppermute x10, starting transfers between devices: 12.8 us -> 16.3 us  [gather_blocks(): other = lax.ppermute(blocks, axis, xor_pairs(size, bit))]
    ppermute x4, starting transfers between devices: 2 us -> 4.49 us  [scatter_sum(): blocks = keep + lax.ppermute(send, axis, xor_pairs(size, bit))]
    concatenate x4 -> x10, other arithmetic: 0.11 us -> 1.97 us  [the longest x9 1.88 us: gather_blocks(): jnp.concatenate([blocks, other], axis=level)]
    ppermute x1 -> x2, waiting for transfers between devices: 4.08 us -> 5.66 us  [sum_over(): value = value + lax.ppermute(value, axis, xor_pairs(size, bit))]
    concatenate x1 -> x5, local copies, waits for them, and re-layouts: 0.15 us -> 1.65 us  [the longest x4 1.64 us: merge_over(): jnp.concatenate([jnp.stack(split_exact(peak) + split_exact(total), axis=-...]
  transfers between devices with their start and end apart: 20 -> 21, of which waited for: 18 -> 19; matrix products, arithmetic and copies ran while one was open for 8% -> 14% of each run, Pallas kernels for 0% -> 0%
where the time goes in v3:
time: 106 us; the launch traced here: 105 us
  waiting for transfers between devices  39.6 us (37%)
  starting transfers between devices  33.2 us (31%)
  local copies, waits for them, and re-layouts  11.6 us (11%)
  other arithmetic  10.6 us (10%)
  matrix products  8.64 us (8%)
  between operations  1.49 us (1%)
    ppermute x10, starting transfers between devices, gather_blocks(): other = lax.ppermute(blocks, axis, xor_pairs(size, bit))  16.3 us
    ppermute x10, waiting for transfers between devices, gather_blocks(): other = lax.ppermute(blocks, axis, xor_pairs(size, bit))  12.3 us
    ppermute x4, waiting for transfers between devices, scatter_sum(): blocks = keep + lax.ppermute(send, axis, xor_pairs(size, bit))  9.57 us
    ppermute x4, waiting for transfers between devices, merge_over(): other = lax.ppermute(sent, axis, xor_pairs(size, bit))  9.5 us
    ppermute x4, starting transfers between devices, merge_over(): other = lax.ppermute(sent, axis, xor_pairs(size, bit))  6.71 us
    ppermute x2, waiting for transfers between devices, sum_over(): value = value + lax.ppermute(value, axis, xor_pairs(size, bit))  5.66 us
    ppermute x4, starting transfers between devices, scatter_sum(): blocks = keep + lax.ppermute(send, axis, xor_pairs(size, bit))  4.49 us
    ppermute x1, starting transfers between devices, shards(): own_branch = lax.ppermute(reduced, ALL, routes)  3.9 us
  transfers between devices with their start and end apart: 21, of which 19 were waited for; matrix products, arithmetic and copies ran while one was open for 14% of the time, Pallas kernels for 0%

profile of v3, /device:TPU:2, one launch (start us, length us, event | category | flops | bytes accessed | tf_op | source)
XLA Modules:
  0.0 105.1 jit_solution(17504488323497756925)
XLA Ops:
  0.7 0.7 compare_select_fusion.2
  1.5 0.7 compare_and_fusion
  2.2 0.7 compare_select_fusion
  2.9 1.3 %gather_fusion = s32[2]{0:T(128)S(1)} fusion(s32[4]{0:T(128)} %param.13, s32[1024]{0:T(1024)S(1)} %pad_clamp_fusion.2), kind=kCustom, calls=%fused_computation | custom fusion | bytes 24 | tf_op jit(solution)/shard_map/jit(_take)/gather | solution.py:141
  4.2 0.7 and_select_fusion
  5.7 0.8 dynamic-slice.4
  6.5 0.8 dynamic-slice.5
  7.3 0.8 broadcast_select_fusion.13
  8.1 3.1 %collective-permute-start.1 = (bf16[1,1,1,1,2,4,2,284]{7,6,5,4,3,2,1,0:T(2,128)(2,1)S(1)}, bf16[1,1,1,1,2,4,2,284]{7,6,5,4,3,2,1,0:T(2,128)(2,1)S(1)}, u32[]{:S(2)}, u32[]{:S(2)}) collective-permute-start(bf16[1,1,1,1,2,4,2,284]{7,6,5,4,3,2,1,0:T(2,128)(2,1)S(1)} %broadcast_select_fusion.13), channel_id=1, source_target_pairs={{0,8},{1,9},{2,10},{3,11},{4,12},{5,13},{6,14},{7,15},{8,0},{9,1},... | collective-permute-start | bytes 27272 | tf_op jit(solution)/shard_map/ppermute | solution.py:22
  11.2 0.8 fusion.144
  12.0 0.8 fusion.146
  13.1 1.8 %collective-permute-start.2 = (bf16[2,1,1,1,2,4,2,284]{7,6,5,4,3,2,1,0:T(2,128)(2,1)S(1)}, bf16[2,1,1,1,2,4,2,284]{7,6,5,4,3,2,1,0:T(2,128)(2,1)S(1)}, u32[]{:S(2)}, u32[]{:S(2)}) collective-permute-start(bf16[2,1,1,1,2,4,2,284]{7,6,5,4,3,2,1,0:T(2,128)(2,1)S(1)} %broadcast_select_fusion.9), channel_id=1, source_target_pairs={{0,4},{1,5},{2,6},{3,7},{4,0},{5,1},{6,2},{7,3},{8,12},{9,13},{10,... | collective-permute-start | bytes 54536 | tf_op jit(solution)/shard_map/ppermute | solution.py:22
  15.0 2.0 %collective-permute-done.2 = bf16[2,1,1,1,2,4,2,284]{7,6,5,4,3,2,1,0:T(2,128)(2,1)S(1)} collective-permute-done((bf16[2,1,1,1,2,4,2,284]{7,6,5,4,3,2,1,0:T(2,128)(2,1)S(1)}, bf16[2,1,1,1,2,4,2,284]{7,6,5,4,3,2,1,0:T(2,128)(2,1)S(1)}, u32[]{:S(2)}, u32[]{:S(2)}) %collective-permute-start.2) | collective-permute-done | bytes 18208 | tf_op jit(solution)/shard_map/ppermute | solution.py:22
  17.1 1.8 %collective-permute-start.3 = (bf16[2,2,1,1,2,4,2,284]{7,6,5,4,3,2,1,0:T(2,128)(2,1)S(1)}, bf16[2,2,1,1,2,4,2,284]{7,6,5,4,3,2,1,0:T(2,128)(2,1)S(1)}, u32[]{:S(2)}, u32[]{:S(2)}) collective-permute-start(bf16[2,2,1,1,2,4,2,284]{7,6,5,4,3,2,1,0:T(2,128)(2,1)S(1)} %broadcast_select_fusion.5), channel_id=1, source_target_pairs={{0,2},{1,3},{2,0},{3,1},{4,6},{5,7},{6,4},{7,5},{8,10},{9,11},{10,... | collective-permute-start | bytes 109064 | tf_op jit(solution)/shard_map/ppermute | solution.py:22
  19.0 2.3 %collective-permute-done.3 = bf16[2,2,1,1,2,4,2,284]{7,6,5,4,3,2,1,0:T(2,128)(2,1)S(1)} collective-permute-done((bf16[2,2,1,1,2,4,2,284]{7,6,5,4,3,2,1,0:T(2,128)(2,1)S(1)}, bf16[2,2,1,1,2,4,2,284]{7,6,5,4,3,2,1,0:T(2,128)(2,1)S(1)}, u32[]{:S(2)}, u32[]{:S(2)}) %collective-permute-start.3) | collective-permute-done | bytes 36384 | tf_op jit(solution)/shard_map/ppermute | solution.py:22
  21.5 1.3 %collective-permute-done.4 = bf16[2,2,2,1,2,4,2,284]{7,6,5,4,3,2,1,0:T(2,128)(2,1)S(1)} collective-permute-done((bf16[2,2,2,1,2,4,2,284]{7,6,5,4,3,2,1,0:T(2,128)(2,1)S(1)}, bf16[2,2,2,1,2,4,2,284]{7,6,5,4,3,2,1,0:T(2,128)(2,1)S(1)}, u32[]{:S(2)}, u32[]{:S(2)}) %collective-permute-start.4) | collective-permute-done | bytes 72736 | tf_op jit(solution)/shard_map/ppermute | solution.py:22
  23.5 0.7 gather_fusion.1
  26.6 1.7 %collective-permute-start.5 = (f32[16,412]{1,0:T(8,128)S(1)}, f32[16,412]{1,0:T(8,128)S(1)}, u32[]{:S(2)}, u32[]{:S(2)}) collective-permute-start(f32[16,412]{1,0:T(8,128)S(1)} %pad_maximum_fusion.1), channel_id=1, source_target_pairs={{0,16},{16,0},{1,17},{17,1},{2,18},{18,2},{3,19},{19,3},{4,20},{20... | collective-permute-start | bytes 79112 | tf_op jit(solution)/shard_map/ppermute | solution.py:35
  28.8 1.7 %collective-permute-done.5 = f32[16,412]{1,0:T(8,128)S(1)} collective-permute-done((f32[16,412]{1,0:T(8,128)S(1)}, f32[16,412]{1,0:T(8,128)S(1)}, u32[]{:S(2)}, u32[]{:S(2)}) %collective-permute-start.5) | collective-permute-done | bytes 26400 | tf_op jit(solution)/shard_map/ppermute | solution.py:35
  30.9 2.9 %collective-permute-start.6 = (bf16[1,1,1,1,4,2,284]{6,5,4,3,2,1,0:T(2,128)(2,1)S(1)}, bf16[1,1,1,1,4,2,284]{6,5,4,3,2,1,0:T(2,128)(2,1)S(1)}, u32[]{:S(2)}, u32[]{:S(2)}) collective-permute-start(bf16[1,1,1,1,4,2,284]{6,5,4,3,2,1,0:T(2,128)(2,1)S(1)} %get-tuple-element.45), channel_id=1, source_target_pairs={{0,8},{1,9},{2,10},{3,11},{4,12},{5,13},{6,14},{7,15},{8,0},{9,1},... | collective-permute-start | bytes 13640 | tf_op jit(solution)/shard_map/ppermute | solution.py:22
  33.9 1.6 %collective-permute-done.6 = bf16[1,1,1,1,4,2,284]{6,5,4,3,2,1,0:T(2,128)(2,1)S(1)} collective-permute-done((bf16[1,1,1,1,4,2,284]{6,5,4,3,2,1,0:T(2,128)(2,1)S(1)}, bf16[1,1,1,1,4,2,284]{6,5,4,3,2,1,0:T(2,128)(2,1)S(1)}, u32[]{:S(2)}, u32[]{:S(2)}) %collective-permute-start.6) | collective-permute-done | bytes 4576 | tf_op jit(solution)/shard_map/ppermute | solution.py:22
  35.5 1.8 %collective-permute-start.7 = (bf16[2,1,1,1,4,2,284]{6,5,4,3,2,1,0:T(2,128)(2,1)S(1)}, bf16[2,1,1,1,4,2,284]{6,5,4,3,2,1,0:T(2,128)(2,1)S(1)}, u32[]{:S(2)}, u32[]{:S(2)}) collective-permute-start(bf16[2,1,1,1,4,2,284]{6,5,4,3,2,1,0:T(2,128)(2,1)S(1)} %broadcast_select_fusion.12), channel_id=1, source_target_pairs={{0,4},{1,5},{2,6},{3,7},{4,0},{5,1},{6,2},{7,3},{8,12},{9,13},{10,... | collective-permute-start | bytes 27272 | tf_op jit(solution)/shard_map/ppermute | solution.py:22
  37.4 1.9 %collective-permute-done.7 = bf16[2,1,1,1,4,2,284]{6,5,4,3,2,1,0:T(2,128)(2,1)S(1)} collective-permute-done((bf16[2,1,1,1,4,2,284]{6,5,4,3,2,1,0:T(2,128)(2,1)S(1)}, bf16[2,1,1,1,4,2,284]{6,5,4,3,2,1,0:T(2,128)(2,1)S(1)}, u32[]{:S(2)}, u32[]{:S(2)}) %collective-permute-start.7) | collective-permute-done | bytes 9120 | tf_op jit(solution)/shard_map/ppermute | solution.py:22
  39.3 1.8 %collective-permute-start.8 = (bf16[2,2,1,1,4,2,284]{6,5,4,3,2,1,0:T(2,128)(2,1)S(1)}, bf16[2,2,1,1,4,2,284]{6,5,4,3,2,1,0:T(2,128)(2,1)S(1)}, u32[]{:S(2)}, u32[]{:S(2)}) collective-permute-start(bf16[2,2,1,1,4,2,284]{6,5,4,3,2,1,0:T(2,128)(2,1)S(1)} %broadcast_select_fusion.8), channel_id=1, source_target_pairs={{0,2},{1,3},{2,0},{3,1},{4,6},{5,7},{6,4},{7,5},{8,10},{9,11},{10,... | collective-permute-start | bytes 54536 | tf_op jit(solution)/shard_map/ppermute | solution.py:22
  41.1 2.1 %collective-permute-done.8 = bf16[2,2,1,1,4,2,284]{6,5,4,3,2,1,0:T(2,128)(2,1)S(1)} collective-permute-done((bf16[2,2,1,1,4,2,284]{6,5,4,3,2,1,0:T(2,128)(2,1)S(1)}, bf16[2,2,1,1,4,2,284]{6,5,4,3,2,1,0:T(2,128)(2,1)S(1)}, u32[]{:S(2)}, u32[]{:S(2)}) %collective-permute-start.8) | collective-permute-done | bytes 18208 | tf_op jit(solution)/shard_map/ppermute | solution.py:22
  43.6 1.0 collective-permute-done.9
  48.4 0.8 scatter_custom_fusion
  50.1 1.8 %collective-permute-start.11 = (bf16[2,284,70]{1,2,0:T(8,128)(2,1)S(1)}, bf16[2,284,70]{1,2,0:T(8,128)(2,1)S(1)}, u32[]{:S(2)}, u32[]{:S(2)}) collective-permute-start(bf16[2,284,70]{1,2,0:T(8,128)(2,1)S(1)} %concatenate.555), channel_id=1, source_target_pairs={{0,2},{1,3},{2,0},{3,1},{4,6},{5,7},{6,4},{7,5},{8,10},{9,11},{10,... | collective-permute-start | bytes 238568 | tf_op jit(solution)/shard_map/ppermute | solution.py:76
  51.9 3.4 %collective-permute-done.11 = bf16[2,284,70]{1,2,0:T(8,128)(2,1)S(1)} collective-permute-done((bf16[2,284,70]{1,2,0:T(8,128)(2,1)S(1)}, bf16[2,284,70]{1,2,0:T(8,128)(2,1)S(1)}, u32[]{:S(2)}, u32[]{:S(2)}) %collective-permute-start.11) | collective-permute-done | bytes 79552 | tf_op jit(solution)/shard_map/ppermute | solution.py:76
  55.9 1.8 %collective-permute-start.12 = (bf16[2,284,70]{1,2,0:T(8,128)(2,1)S(1)}, bf16[2,284,70]{1,2,0:T(8,128)(2,1)S(1)}, u32[]{:S(2)}, u32[]{:S(2)}) collective-permute-start(bf16[2,284,70]{1,2,0:T(8,128)(2,1)S(1)} %concatenate.556), channel_id=1, source_target_pairs={{0,4},{1,5},{2,6},{3,7},{4,0},{5,1},{6,2},{7,3},{8,12},{9,13},{10,... | collective-permute-start | bytes 238568 | tf_op jit(solution)/shard_map/ppermute | solution.py:76
  57.8 2.9 %collective-permute-done.12 = bf16[2,284,70]{1,2,0:T(8,128)(2,1)S(1)} collective-permute-done((bf16[2,284,70]{1,2,0:T(8,128)(2,1)S(1)}, bf16[2,284,70]{1,2,0:T(8,128)(2,1)S(1)}, u32[]{:S(2)}, u32[]{:S(2)}) %collective-permute-start.12) | collective-permute-done | bytes 79552 | tf_op jit(solution)/shard_map/ppermute | solution.py:76
  61.3 2.9 %collective-permute-start.13 = (bf16[2,284,70]{1,2,0:T(8,128)(2,1)S(1)}, bf16[2,284,70]{1,2,0:T(8,128)(2,1)S(1)}, u32[]{:S(2)}, u32[]{:S(2)}) collective-permute-start(bf16[2,284,70]{1,2,0:T(8,128)(2,1)S(1)} %concatenate.557), channel_id=1, source_target_pairs={{0,8},{1,9},{2,10},{3,11},{4,12},{5,13},{6,14},{7,15},{8,0},{9,1},... | collective-permute-start | bytes 238568 | tf_op jit(solution)/shard_map/ppermute | solution.py:76
  64.2 2.8 %collective-permute-done.13 = bf16[2,284,70]{1,2,0:T(8,128)(2,1)S(1)} collective-permute-done((bf16[2,284,70]{1,2,0:T(8,128)(2,1)S(1)}, bf16[2,284,70]{1,2,0:T(8,128)(2,1)S(1)}, u32[]{:S(2)}, u32[]{:S(2)}) %collective-permute-start.13) | collective-permute-done | bytes 79552 | tf_op jit(solution)/shard_map/ppermute | solution.py:76
  67.6 2.9 %collective-permute-start.14 = (bf16[1,4,2,284]{3,1,2,0:T(4,128)(2,1)S(1)}, bf16[1,4,2,284]{3,1,2,0:T(4,128)(2,1)S(1)}, u32[]{:S(2)}, u32[]{:S(2)}) collective-permute-start(bf16[1,4,2,284]{3,1,2,0:T(4,128)(2,1)S(1)} %dynamic-slice_bitcast_fusion), channel_id=1, source_target_pairs={{0,16},{16,0},{1,17},{17,1},{2,18},{18,2},{3,19},{19,3},{4,20},{20... | collective-permute-start | bytes 13640 | tf_op jit(solution)/shard_map/ppermute | solution.py:22
  70.5 3.3 %fusion.122 = f32[16,1136]{1,0:T(8,128)S(1)} fusion(bf16[2272,1136]{1,0:T(8,128)(2,1)} %param.20, f32[2272]{0:T(1024)S(1)} %dynamic-slice.5, f32[2272]{0:T(1024)S(1)} %dynamic-slice.4, f32[16]{0:T(128)S(1)} %rsqrt.12, f32[16]{0:T(128)S(1)} %div.67, bf16[16,4544]{1,0:T(8,128)(2,1)S(1)} %broadcast_select_fusion.4, s32[]{:T(128)S(6)} %select_n.512), kind=kOutput, calls=%fused_computation.294 | convolution fusion | flops 82809856 | bytes 5334020 | tf_op jit(solution)/shard_map/dot_general | solution.py:156
  74.3 4.0 %collective-permute-done.15 = f32[16,1136]{1,0:T(8,128)S(1)} collective-permute-done((f32[16,1136]{1,0:T(8,128)S(1)}, f32[16,1136]{1,0:T(8,128)S(1)}, u32[]{:S(2)}, u32[]{:S(2)}) %collective-permute-start.15) | collective-permute-done | bytes 72736 | tf_op jit(solution)/shard_map/ppermute | solution.py:35
  78.2 3.4 %convolution_add_fusion = f32[16,2272]{1,0:T(8,128)S(1)} fusion(f32[16,2272]{1,0:T(8,128)S(1)} %fusion.132, bf16[1136,2272]{1,0:T(8,128)(2,1)} %param.21, f32[16,1136]{1,0:T(8,128)S(1)} %fusion.122, f32[16,1136]{1,0:T(8,128)S(1)} %collective-permute-done.15), kind=kOutput, calls=%fused_computation.4 | convolution fusion | flops 83827712 | bytes 5598208 | tf_op jit(solution)/shard_map/dot_general | solution.py:159
  81.7 0.6 gather_fusion.2
  82.9 1.3 %collective-permute-done.16 = f32[2,2,2,4,2,284]{5,4,3,2,1,0:T(2,128)S(1)} collective-permute-done((f32[2,2,2,4,2,284]{5,4,3,2,1,0:T(2,128)S(1)}, f32[2,2,2,4,2,284]{5,4,3,2,1,0:T(2,128)S(1)}, u32[]{:S(2)}, u32[]{:S(2)}) %collective-permute-start.16) | collective-permute-done | bytes 72736 | tf_op jit(solution)/shard_map/ppermute | solution.py:52
  84.3 1.6 %collective-permute-start.17 = (f32[2,2,4,2,284]{4,3,2,1,0:T(2,128)S(1)}, f32[2,2,4,2,284]{4,3,2,1,0:T(2,128)S(1)}, u32[]{:S(2)}, u32[]{:S(2)}) collective-permute-start(f32[2,2,4,2,284]{4,3,2,1,0:T(2,128)S(1)} %fusion.27), channel_id=1, source_target_pairs={{0,2},{1,3},{2,0},{3,1},{4,6},{5,7},{6,4},{7,5},{8,10},{9,11},{10,... | collective-permute-start | bytes 109064 | tf_op jit(solution)/shard_map/ppermute | solution.py:52
  85.9 2.6 %collective-permute-done.17 = f32[2,2,4,2,284]{4,3,2,1,0:T(2,128)S(1)} collective-permute-done((f32[2,2,4,2,284]{4,3,2,1,0:T(2,128)S(1)}, f32[2,2,4,2,284]{4,3,2,1,0:T(2,128)S(1)}, u32[]{:S(2)}, u32[]{:S(2)}) %collective-permute-start.17) | collective-permute-done | bytes 36384 | tf_op jit(solution)/shard_map/ppermute | solution.py:52
  88.5 0.7 collective-permute-start.18
  89.3 3.2 %collective-permute-done.18 = f32[2,4,2,284]{3,2,1,0:T(2,128)S(1)} collective-permute-done((f32[2,4,2,284]{3,2,1,0:T(2,128)S(1)}, f32[2,4,2,284]{3,2,1,0:T(2,128)S(1)}, u32[]{:S(2)}, u32[]{:S(2)}) %collective-permute-start.18) | collective-permute-done | bytes 18208 | tf_op jit(solution)/shard_map/ppermute | solution.py:52
  92.5 2.1 %collective-permute-start.19 = (f32[4,2,284]{2,1,0:T(2,128)S(1)}, f32[4,2,284]{2,1,0:T(2,128)S(1)}, u32[]{:S(2)}, u32[]{:S(2)}) collective-permute-start(f32[4,2,284]{2,1,0:T(2,128)S(1)} %select_bitcast_fusion), channel_id=1, source_target_pairs={{0,8},{1,9},{2,10},{3,11},{4,12},{5,13},{6,14},{7,15},{8,0},{9,1},... | collective-permute-start | bytes 27272 | tf_op jit(solution)/shard_map/ppermute | solution.py:52
  94.6 2.6 %collective-permute-done.19 = f32[4,2,284]{2,1,0:T(2,128)S(1)} collective-permute-done((f32[4,2,284]{2,1,0:T(2,128)S(1)}, f32[4,2,284]{2,1,0:T(2,128)S(1)}, u32[]{:S(2)}, u32[]{:S(2)}) %collective-permute-start.19) | collective-permute-done | bytes 9120 | tf_op jit(solution)/shard_map/ppermute | solution.py:52
  97.1 3.9 %collective-permute-start.20 = (f32[4,2,284]{2,1,0:T(2,128)S(1)}, f32[4,2,284]{2,1,0:T(2,128)S(1)}, u32[]{:S(2)}, u32[]{:S(2)}) collective-permute-start(f32[4,2,284]{2,1,0:T(2,128)S(1)} %bitcast_add_fusion), channel_id=1, source_target_pairs={{0,0},{1,1},{2,2},{3,3},{4,4},{5,5},{6,6},{7,7},{8,16},{9,17},{10,... | collective-permute-start | bytes 27272 | tf_op jit(solution)/shard_map/ppermute | solution.py:230
  101.1 0.8 copy.150
  101.9 2.6 %collective-permute-done.20 = f32[4,2,284]{2,1,0:T(2,128)S(1)} collective-permute-done((f32[4,2,284]{2,1,0:T(2,128)S(1)}, f32[4,2,284]{2,1,0:T(2,128)S(1)}, u32[]{:S(2)}, u32[]{:S(2)}) %collective-permute-start.20) | collective-permute-done | bytes 9120 | tf_op jit(solution)/shard_map/ppermute | solution.py:230
  (156 shorter events, 14.3 us)
Async XLA Ops:
  0.6 73.3 %copy-start = (bf16[284,2272]{1,0:T(8,128)(2,1)S(1)}, bf16[284,2272]{1,0:T(8,128)(2,1)}, u32[]{:S(2)}) copy-start(bf16[284,2272]{1,0:T(8,128)(2,1)} %param.19) | copy-start | bytes 3871492
  0.6 6.6 %collective-permute-start = (bf16[1,4,2,284]{3,2,1,0:T(2,128)(2,1)}, bf16[1,4,2,284]{3,2,1,0:T(2,128)(2,1)S(1)}, u32[]{:S(2)}, u32[]{:S(2)}) collective-permute-start(bf16[1,4,2,284]{3,2,1,0:T(2,128)(2,1)} %bitcast.196), channel_id=1, source_target_pairs={{0,16},{16,0},{1,17},{17,1},{2,18},{18,2},{3,19},{19,3},{4,20},{20... | collective-permute-start | bytes 13640 | tf_op jit(solution)/shard_map/ppermute | solution.py:22
  8.1 4.9 %collective-permute-start.1 = (bf16[1,1,1,1,2,4,2,284]{7,6,5,4,3,2,1,0:T(2,128)(2,1)S(1)}, bf16[1,1,1,1,2,4,2,284]{7,6,5,4,3,2,1,0:T(2,128)(2,1)S(1)}, u32[]{:S(2)}, u32[]{:S(2)}) collective-permute-start(bf16[1,1,1,1,2,4,2,284]{7,6,5,4,3,2,1,0:T(2,128)(2,1)S(1)} %broadcast_select_fusion.13), channel_id=1, source_target_pairs={{0,8},{1,9},{2,10},{3,11},{4,12},{5,13},{6,14},{7,15},{8,0},{9,1},... | collective-permute-start | bytes 27272 | tf_op jit(solution)/shard_map/ppermute | solution.py:22
  13.1 3.9 %collective-permute-start.2 = (bf16[2,1,1,1,2,4,2,284]{7,6,5,4,3,2,1,0:T(2,128)(2,1)S(1)}, bf16[2,1,1,1,2,4,2,284]{7,6,5,4,3,2,1,0:T(2,128)(2,1)S(1)}, u32[]{:S(2)}, u32[]{:S(2)}) collective-permute-start(bf16[2,1,1,1,2,4,2,284]{7,6,5,4,3,2,1,0:T(2,128)(2,1)S(1)} %broadcast_select_fusion.9), channel_id=1, source_target_pairs={{0,4},{1,5},{2,6},{3,7},{4,0},{5,1},{6,2},{7,3},{8,12},{9,13},{10,... | collective-permute-start | bytes 54536 | tf_op jit(solution)/shard_map/ppermute | solution.py:22
  17.1 4.2 %collective-permute-start.3 = (bf16[2,2,1,1,2,4,2,284]{7,6,5,4,3,2,1,0:T(2,128)(2,1)S(1)}, bf16[2,2,1,1,2,4,2,284]{7,6,5,4,3,2,1,0:T(2,128)(2,1)S(1)}, u32[]{:S(2)}, u32[]{:S(2)}) collective-permute-start(bf16[2,2,1,1,2,4,2,284]{7,6,5,4,3,2,1,0:T(2,128)(2,1)S(1)} %broadcast_select_fusion.5), channel_id=1, source_target_pairs={{0,2},{1,3},{2,0},{3,1},{4,6},{5,7},{6,4},{7,5},{8,10},{9,11},{10,... | collective-permute-start | bytes 109064 | tf_op jit(solution)/shard_map/ppermute | solution.py:22
  21.4 1.4 %collective-permute-start.4 = (bf16[2,2,2,1,2,4,2,284]{7,6,5,4,3,2,1,0:T(2,128)(2,1)S(1)}, bf16[2,2,2,1,2,4,2,284]{7,6,5,4,3,2,1,0:T(2,128)(2,1)S(1)}, u32[]{:S(2)}, u32[]{:S(2)}) collective-permute-start(bf16[2,2,2,1,2,4,2,284]{7,6,5,4,3,2,1,0:T(2,128)(2,1)S(1)} %broadcast_select_fusion.1), channel_id=1, source_target_pairs={{0,1},{1,0},{2,3},{3,2},{4,5},{5,4},{6,7},{7,6},{8,9},{9,8},{10,11... | collective-permute-start | bytes 218120 | tf_op jit(solution)/shard_map/ppermute | solution.py:22
  23.1 2.1 %copy-start.1 = (bf16[2272,284]{0,1:T(8,128)(2,1)S(1)}, bf16[2272,284]{0,1:T(8,128)(2,1)}, u32[]{:S(2)}) copy-start(bf16[2272,284]{0,1:T(8,128)(2,1)} %param.17) | copy-start | bytes 3871492
  25.2 1.1 %copy-start.2 = (bf16[2272,128]{1,0:T(8,128)(2,1)S(1)}, bf16[2272,128]{1,0:T(8,128)(2,1)}, u32[]{:S(2)}) copy-start(bf16[2272,128]{1,0:T(8,128)(2,1)} %param.18) | copy-start | bytes 1744900
  25.3 3.1 %copy-start.3 = (bf16[2,512,128]{2,1,0:T(8,128)(2,1)S(1)}, bf16[2,512,128]{2,1,0:T(8,128)(2,1)}, u32[]{:S(2)}) copy-start(bf16[2,512,128]{2,1,0:T(8,128)(2,1)} %param.12) | copy-start | bytes 786436
  26.6 3.9 %collective-permute-start.5 = (f32[16,412]{1,0:T(8,128)S(1)}, f32[16,412]{1,0:T(8,128)S(1)}, u32[]{:S(2)}, u32[]{:S(2)}) collective-permute-start(f32[16,412]{1,0:T(8,128)S(1)} %pad_maximum_fusion.1), channel_id=1, source_target_pairs={{0,16},{16,0},{1,17},{17,1},{2,18},{18,2},{3,19},{19,3},{4,20},{20... | collective-permute-start | bytes 79112 | tf_op jit(solution)/shard_map/ppermute | solution.py:35
  30.9 4.6 %collective-permute-start.6 = (bf16[1,1,1,1,4,2,284]{6,5,4,3,2,1,0:T(2,128)(2,1)S(1)}, bf16[1,1,1,1,4,2,284]{6,5,4,3,2,1,0:T(2,128)(2,1)S(1)}, u32[]{:S(2)}, u32[]{:S(2)}) collective-permute-start(bf16[1,1,1,1,4,2,284]{6,5,4,3,2,1,0:T(2,128)(2,1)S(1)} %get-tuple-element.45), channel_id=1, source_target_pairs={{0,8},{1,9},{2,10},{3,11},{4,12},{5,13},{6,14},{7,15},{8,0},{9,1},... | collective-permute-start | bytes 13640 | tf_op jit(solution)/shard_map/ppermute | solution.py:22
  35.5 3.8 %collective-permute-start.7 = (bf16[2,1,1,1,4,2,284]{6,5,4,3,2,1,0:T(2,128)(2,1)S(1)}, bf16[2,1,1,1,4,2,284]{6,5,4,3,2,1,0:T(2,128)(2,1)S(1)}, u32[]{:S(2)}, u32[]{:S(2)}) collective-permute-start(bf16[2,1,1,1,4,2,284]{6,5,4,3,2,1,0:T(2,128)(2,1)S(1)} %broadcast_select_fusion.12), channel_id=1, source_target_pairs={{0,4},{1,5},{2,6},{3,7},{4,0},{5,1},{6,2},{7,3},{8,12},{9,13},{10,... | collective-permute-start | bytes 27272 | tf_op jit(solution)/shard_map/ppermute | solution.py:22
  39.3 3.9 %collective-permute-start.8 = (bf16[2,2,1,1,4,2,284]{6,5,4,3,2,1,0:T(2,128)(2,1)S(1)}, bf16[2,2,1,1,4,2,284]{6,5,4,3,2,1,0:T(2,128)(2,1)S(1)}, u32[]{:S(2)}, u32[]{:S(2)}) collective-permute-start(bf16[2,2,1,1,4,2,284]{6,5,4,3,2,1,0:T(2,128)(2,1)S(1)} %broadcast_select_fusion.8), channel_id=1, source_target_pairs={{0,2},{1,3},{2,0},{3,1},{4,6},{5,7},{6,4},{7,5},{8,10},{9,11},{10,... | collective-permute-start | bytes 54536 | tf_op jit(solution)/shard_map/ppermute | solution.py:22
  43.3 1.3 %collective-permute-start.9 = (bf16[2,2,2,1,4,2,284]{6,5,4,3,2,1,0:T(2,128)(2,1)S(1)}, bf16[2,2,2,1,4,2,284]{6,5,4,3,2,1,0:T(2,128)(2,1)S(1)}, u32[]{:S(2)}, u32[]{:S(2)}) collective-permute-start(bf16[2,2,2,1,4,2,284]{6,5,4,3,2,1,0:T(2,128)(2,1)S(1)} %broadcast_select_fusion.7), channel_id=1, source_target_pairs={{0,1},{1,0},{2,3},{3,2},{4,5},{5,4},{6,7},{7,6},{8,9},{9,8},{10,11... | collective-permute-start | bytes 109064 | tf_op jit(solution)/shard_map/ppermute | solution.py:22
  48.1 1.4 %collective-permute-start.10 = (bf16[2,284,70]{1,2,0:T(8,128)(2,1)S(1)}, bf16[2,284,70]{1,2,0:T(8,128)(2,1)S(1)}, u32[]{:S(2)}, u32[]{:S(2)}) collective-permute-start(bf16[2,284,70]{1,2,0:T(8,128)(2,1)S(1)} %concatenate.554), channel_id=1, source_target_pairs={{0,1},{1,0},{2,3},{3,2},{4,5},{5,4},{6,7},{7,6},{8,9},{9,8},{10,11... | collective-permute-start | bytes 238568 | tf_op jit(solution)/shard_map/ppermute | solution.py:76
  50.1 5.2 %collective-permute-start.11 = (bf16[2,284,70]{1,2,0:T(8,128)(2,1)S(1)}, bf16[2,284,70]{1,2,0:T(8,128)(2,1)S(1)}, u32[]{:S(2)}, u32[]{:S(2)}) collective-permute-start(bf16[2,284,70]{1,2,0:T(8,128)(2,1)S(1)} %concatenate.555), channel_id=1, source_target_pairs={{0,2},{1,3},{2,0},{3,1},{4,6},{5,7},{6,4},{7,5},{8,10},{9,11},{10,... | collective-permute-start | bytes 238568 | tf_op jit(solution)/shard_map/ppermute | solution.py:76
  55.9 4.8 %collective-permute-start.12 = (bf16[2,284,70]{1,2,0:T(8,128)(2,1)S(1)}, bf16[2,284,70]{1,2,0:T(8,128)(2,1)S(1)}, u32[]{:S(2)}, u32[]{:S(2)}) collective-permute-start(bf16[2,284,70]{1,2,0:T(8,128)(2,1)S(1)} %concatenate.556), channel_id=1, source_target_pairs={{0,4},{1,5},{2,6},{3,7},{4,0},{5,1},{6,2},{7,3},{8,12},{9,13},{10,... | collective-permute-start | bytes 238568 | tf_op jit(solution)/shard_map/ppermute | solution.py:76
  61.3 5.7 %collective-permute-start.13 = (bf16[2,284,70]{1,2,0:T(8,128)(2,1)S(1)}, bf16[2,284,70]{1,2,0:T(8,128)(2,1)S(1)}, u32[]{:S(2)}, u32[]{:S(2)}) collective-permute-start(bf16[2,284,70]{1,2,0:T(8,128)(2,1)S(1)} %concatenate.557), channel_id=1, source_target_pairs={{0,8},{1,9},{2,10},{3,11},{4,12},{5,13},{6,14},{7,15},{8,0},{9,1},... | collective-permute-start | bytes 238568 | tf_op jit(solution)/shard_map/ppermute | solution.py:76
  67.6 6.3 %collective-permute-start.14 = (bf16[1,4,2,284]{3,1,2,0:T(4,128)(2,1)S(1)}, bf16[1,4,2,284]{3,1,2,0:T(4,128)(2,1)S(1)}, u32[]{:S(2)}, u32[]{:S(2)}) collective-permute-start(bf16[1,4,2,284]{3,1,2,0:T(4,128)(2,1)S(1)} %dynamic-slice_bitcast_fusion), channel_id=1, source_target_pairs={{0,16},{16,0},{1,17},{17,1},{2,18},{18,2},{3,19},{19,3},{4,20},{20... | collective-permute-start | bytes 13640 | tf_op jit(solution)/shard_map/ppermute | solution.py:22
  73.8 4.4 %collective-permute-start.15 = (f32[16,1136]{1,0:T(8,128)S(1)}, f32[16,1136]{1,0:T(8,128)S(1)}, u32[]{:S(2)}, u32[]{:S(2)}) collective-permute-start(f32[16,1136]{1,0:T(8,128)S(1)} %fusion.122), channel_id=1, source_target_pairs={{0,16},{16,0},{1,17},{17,1},{2,18},{18,2},{3,19},{19,3},{4,20},{20... | collective-permute-start | bytes 218120 | tf_op jit(solution)/shard_map/ppermute | solution.py:35
  82.5 22.0 %copy-start.4 = (bf16[4,2,284]{2,1,0:T(2,128)(2,1)S(1)}, bf16[4,2,284]{2,1,0:T(2,128)(2,1)}, u32[]{:S(2)}) copy-start(bf16[4,2,284]{2,1,0:T(2,128)(2,1)} %param.11) | copy-start | bytes 13636
  82.8 1.4 %collective-permute-start.16 = (f32[2,2,2,4,2,284]{5,4,3,2,1,0:T(2,128)S(1)}, f32[2,2,2,4,2,284]{5,4,3,2,1,0:T(2,128)S(1)}, u32[]{:S(2)}, u32[]{:S(2)}) collective-permute-start(f32[2,2,2,4,2,284]{5,4,3,2,1,0:T(2,128)S(1)} %fusion.13), channel_id=1, source_target_pairs={{0,1},{1,0},{2,3},{3,2},{4,5},{5,4},{6,7},{7,6},{8,9},{9,8},{10,11... | collective-permute-start | bytes 218120 | tf_op jit(solution)/shard_map/ppermute | solution.py:52
  84.3 4.2 %collective-permute-start.17 = (f32[2,2,4,2,284]{4,3,2,1,0:T(2,128)S(1)}, f32[2,2,4,2,284]{4,3,2,1,0:T(2,128)S(1)}, u32[]{:S(2)}, u32[]{:S(2)}) collective-permute-start(f32[2,2,4,2,284]{4,3,2,1,0:T(2,128)S(1)} %fusion.27), channel_id=1, source_target_pairs={{0,2},{1,3},{2,0},{3,1},{4,6},{5,7},{6,4},{7,5},{8,10},{9,11},{10,... | collective-permute-start | bytes 109064 | tf_op jit(solution)/shard_map/ppermute | solution.py:52
  88.5 3.9 %collective-permute-start.18 = (f32[2,4,2,284]{3,2,1,0:T(2,128)S(1)}, f32[2,4,2,284]{3,2,1,0:T(2,128)S(1)}, u32[]{:S(2)}, u32[]{:S(2)}) collective-permute-start(f32[2,4,2,284]{3,2,1,0:T(2,128)S(1)} %fusion.61), channel_id=1, source_target_pairs={{0,4},{1,5},{2,6},{3,7},{4,0},{5,1},{6,2},{7,3},{8,12},{9,13},{10,... | collective-permute-start | bytes 54536 | tf_op jit(solution)/shard_map/ppermute | solution.py:52
  92.5 4.7 %collective-permute-start.19 = (f32[4,2,284]{2,1,0:T(2,128)S(1)}, f32[4,2,284]{2,1,0:T(2,128)S(1)}, u32[]{:S(2)}, u32[]{:S(2)}) collective-permute-start(f32[4,2,284]{2,1,0:T(2,128)S(1)} %select_bitcast_fusion), channel_id=1, source_target_pairs={{0,8},{1,9},{2,10},{3,11},{4,12},{5,13},{6,14},{7,15},{8,0},{9,1},... | collective-permute-start | bytes 27272 | tf_op jit(solution)/shard_map/ppermute | solution.py:52
  97.1 7.4 %collective-permute-start.20 = (f32[4,2,284]{2,1,0:T(2,128)S(1)}, f32[4,2,284]{2,1,0:T(2,128)S(1)}, u32[]{:S(2)}, u32[]{:S(2)}) collective-permute-start(f32[4,2,284]{2,1,0:T(2,128)S(1)} %bitcast_add_fusion), channel_id=1, source_target_pairs={{0,0},{1,1},{2,2},{3,3},{4,4},{5,5},{6,6},{7,7},{8,16},{9,17},{10,... | collective-permute-start | bytes 27272 | tf_op jit(solution)/shard_map/ppermute | solution.py:230

commit v4 on v3

--- a/solution.py
+++ b/solution.py
@@ -13,20 +13,22 @@
     return [(index, index ^ bit) for index in range(size)]
 
 
-def gather_blocks(block, axis, size):
-    index = lax.axis_index(axis)
+def gather_xor(block, axis, size):
     levels = size.bit_length() - 1
-    blocks = block.reshape((1,) * levels + block.shape)
+    stacked = block
     for level in range(levels):
         bit = 2 ** (levels - 1 - level)
-        other = lax.ppermute(blocks, axis, xor_pairs(size, bit))
-        low = (index // bit) % 2 == 0
-        blocks = jnp.where(
-            low,
-            jnp.concatenate([blocks, other], axis=level),
-            jnp.concatenate([other, blocks], axis=level),
-        )
-    return blocks.reshape((size,) + block.shape)
+        stacked = jnp.stack([stacked, lax.ppermute(stacked, axis, xor_pairs(size, bit))])
+    return stacked.reshape((size,) + block.shape)
+
+
+def xor_slot(offset, size):
+    levels = size.bit_length() - 1
+    position = jnp.zeros_like(offset)
+    for level in range(levels):
+        bit = 2 ** (levels - 1 - level)
+        position = position + ((offset // bit) % 2) * (2 ** level)
+    return position
 
 
 def sum_over(value, axis, size):
@@ -66,9 +68,13 @@
     return (pieces[..., 0] + pieces[..., 1]) + pieces[..., 2]
 
 
-def merge_over(peak, total, weighted, axis, size):
+def merge_over(peak, total, weighted, axis, size, carried):
     bit = 1
     while bit < size:
+        if bit == 4:
+            carried, peak, total, weighted = lax.optimization_barrier(
+                (carried, peak, total, weighted)
+            )
         sent = jnp.concatenate(
             [jnp.stack(split_exact(peak) + split_exact(total), axis=-1), weighted.astype(jnp.bfloat16)],
             axis=-1,
@@ -84,7 +90,7 @@
         weighted = weighted * scale_first[..., None] + weighted_second * scale_second[..., None]
         peak = merged_peak
         bit *= 2
-    return peak, total, weighted
+    return peak, total, weighted, carried
 
 
 def layer_norm(row_block, norm_gain, norm_bias):
@@ -137,29 +143,37 @@
     group_index = lax.axis_index("req")
     shard_index = lax.axis_index("seq")
 
-    own_requests = lax.dynamic_slice_in_dim(placement, group_index * group_rows, group_rows, 0)
-    slot_lengths = jnp.take(lengths, own_requests)
+    request_ids = jnp.arange(total, dtype=jnp.int32)
+    serves = placement[:, None] == request_ids[None, :]
+    own_serves = lax.dynamic_slice_in_dim(serves, group_index * group_rows, group_rows, 0)
+    slot_lengths = jnp.sum(jnp.where(own_serves, lengths[None, :], 0), axis=1)
     step_offsets = jnp.arange(steps, dtype=jnp.int32)
     positions = slot_lengths[None, :] + step_offsets[:, None]
-
-    every = gather_blocks(gather_blocks(states, "req", req_size), "seq", seq_size)
-    every = every.transpose(2, 1, 3, 0, 4).reshape(steps, total, model_width)
-    current_all = jnp.take(every, placement, axis=1)
+    seq_ids = jnp.arange(seq_size, dtype=jnp.int32)
+    req_ids = jnp.arange(req_size, dtype=jnp.int32)
+    seq_slots = xor_slot(shard_index ^ seq_ids, seq_size)
+    req_slots = xor_slot(group_index ^ req_ids, req_size)
+
+    every = gather_xor(gather_xor(states, "req", req_size), "seq", seq_size)
+    slot_req = xor_slot(group_index ^ (placement // group_rows), req_size)
+    current_all = every[seq_slots[None, :], slot_req[:, None], :, (placement % group_rows)[:, None], :]
+    current_all = current_all.transpose(2, 0, 1, 3).reshape(steps, total, model_width)
     normed = layer_norm(current_all.reshape(rows, model_width), norm_gain, norm_bias)
     normed_part = lax.dynamic_slice_in_dim(normed, group_index * part_width, part_width, 1)
 
     part_query = jnp.dot(normed_part, w_query, preferred_element_type=jnp.float32)
     part_keyval = jnp.dot(normed_part, w_keyval, preferred_element_type=jnp.float32)
     first = sum_over(jnp.concatenate([part_query, part_keyval], axis=1), "req", req_size)
+    part_up = jnp.dot(normed_part, w_up, preferred_element_type=jnp.float32)
+    first, part_up = lax.optimization_barrier((first, part_up))
     query_raw = first[:, :slice_width].astype(jnp.bfloat16).reshape(steps, total, slice_width)
     keyval = first[:, slice_width:].reshape(steps, total, 2 * head_width)
-    part_up = jnp.dot(normed_part, w_up, preferred_element_type=jnp.float32)
     up_part = sum_over(part_up, "req", req_size)
     hidden = jax.nn.gelu(up_part, approximate=False).astype(jnp.bfloat16)
     down_part = jnp.dot(hidden, w_down, preferred_element_type=jnp.float32)
 
     own_query = lax.dynamic_slice_in_dim(query_raw, group_index * group_rows, group_rows, 1)
-    query_all = gather_blocks(own_query, "seq", seq_size)
+    query_all = jnp.take(gather_xor(own_query, "seq", seq_size), seq_slots, axis=0)
     query_all = query_all.transpose(1, 2, 0, 3).reshape(steps, group_rows, model_width)
     flat_positions = positions.reshape(-1)
     query_rows = rotate(
@@ -200,8 +214,8 @@
         "gqs,gsd->gqd", weights, value_rows, preferred_element_type=jnp.float32
     )
 
-    _, merged_total, merged_weighted = merge_over(
-        local_peak, local_total, local_weighted, "seq", seq_size
+    _, merged_total, merged_weighted, down_part = merge_over(
+        local_peak, local_total, local_weighted, "seq", seq_size, down_part
     )
     mixed = merged_weighted / merged_total[:, :, None]
     mixed = (
@@ -210,13 +224,11 @@
         .astype(jnp.bfloat16)
     )
     own_mixed = lax.dynamic_slice_in_dim(mixed, shard_index * slice_width, slice_width, 2)
-    every_mixed = gather_blocks(own_mixed, "req", req_size)
+    every_mixed = jnp.take(gather_xor(own_mixed, "req", req_size), req_slots, axis=0)
     mixed_part = every_mixed.transpose(1, 0, 2, 3).reshape(rows, slice_width)
 
     partial_sum = jnp.dot(mixed_part, w_out, preferred_element_type=jnp.float32) + down_part
-    inverse = (
-        jnp.zeros((total,), jnp.int32).at[placement].set(jnp.arange(total, dtype=jnp.int32))
-    )
+    inverse = jnp.sum(jnp.where(serves, request_ids[:, None], 0), axis=0)
     chunks = seq_size // req_size
     by_request = jnp.take(partial_sum.reshape(steps, total, part_width), inverse, axis=1)
     blocks = by_request.reshape(steps, req_size, group_rows, chunks, slice_width)

time: 106 us -> 102 us (0.962)
  starting transfers between devices: 33.2 us -> 30.5 us
  other arithmetic: 10.6 us -> 8.59 us
  local copies, waits for them, and re-layouts: 11.6 us -> 13.3 us
    ppermute x10, waiting for transfers between devices: 12.3 us -> 17.2 us  [gather_xor(): lax.ppermute(stacked, axis, xor_pairs(size, bit))]
    ppermute x2, waiting for transfers between devices: 5.66 us -> 1.35 us  [sum_over(): value = value + lax.ppermute(value, axis, xor_pairs(size, bit))]
    select_n x13 -> x3, other arithmetic: 3.98 us -> 0.12 us  [the longest x2 0.09 us: shards(): jnp.take(gather_xor(own_mixed, 'req', req_size), req_slots, axis=0)]
    ppermute x10, starting transfers between devices: 16.3 us -> 13.6 us  [gather_xor(): lax.ppermute(stacked, axis, xor_pairs(size, bit))]
    unnamed x22 -> x15, local copies, waits for them, and re-layouts: 1.69 us -> 4.26 us
    ppermute x4, waiting for transfers between devices: 9.5 us -> 7.94 us  [merge_over(): other = lax.ppermute(sent, axis, xor_pairs(size, bit))]
    reduce_sum x0 -> x2, other arithmetic: none -> 1.52 us  [the longest x1 0.78 us: shards(): slot_lengths = jnp.sum(jnp.where(own_serves, lengths[None, :], 0), axis=1)]
    another operation x2 -> x22, other arithmetic: 0.08 us -> 1.45 us  [the longest x17 1.33 us: gather_xor(): jnp.stack([stacked, lax.ppermute(stacked, axis, xor_pairs(size, bit))])]
  transfers between devices with their start and end apart: 21 -> 21, of which waited for: 19 -> 18; matrix products, arithmetic and copies ran while one was open for 14% -> 17% of each run, Pallas kernels for 0% -> 0%
where the time goes in v4:
time: 102 us; the launch traced here: 101 us
  waiting for transfers between devices  38.6 us (38%)
  starting transfers between devices  30.5 us (30%)
  local copies, waits for them, and re-layouts  13.3 us (13%)
  matrix products  8.63 us (8%)
  other arithmetic  8.59 us (8%)
  between operations  1.46 us (1%)
    ppermute x10, waiting for transfers between devices, gather_xor(): lax.ppermute(stacked, axis, xor_pairs(size, bit))  17.2 us
    ppermute x10, starting transfers between devices, gather_xor(): lax.ppermute(stacked, axis, xor_pairs(size, bit))  13.6 us
    ppermute x4, waiting for transfers between devices, scatter_sum(): blocks = keep + lax.ppermute(send, axis, xor_pairs(size, bit))  9.54 us
    ppermute x4, waiting for transfers between devices, merge_over(): other = lax.ppermute(sent, axis, xor_pairs(size, bit))  7.94 us
    ppermute x4, starting transfers between devices, merge_over(): other = lax.ppermute(sent, axis, xor_pairs(size, bit))  6.09 us
    ppermute x4, starting transfers between devices, scatter_sum(): blocks = keep + lax.ppermute(send, axis, xor_pairs(size, bit))  4.49 us
    unnamed x15, local copies, waits for them, and re-layouts  4.26 us
    ppermute x1, starting transfers between devices, shards(): own_branch = lax.ppermute(reduced, ALL, routes)  3.95 us
  transfers between devices with their start and end apart: 21, of which 18 were waited for; matrix products, arithmetic and copies ran while one was open for 17% of the time, Pallas kernels for 0%

profile of v4, /device:TPU:2, one launch (start us, length us, event | category | flops | bytes accessed | tf_op | source)
XLA Modules:
  0.0 101.2 jit_solution(1539023976106662844)
XLA Ops:
  0.8 0.7 iota_compare_fusion
  1.5 0.7 select_reduce_fusion.1
  2.3 0.7 fusion.130
  3.0 0.8 fusion.107
  4.7 0.8 dynamic-slice.4
  5.5 0.8 dynamic-slice.5
  6.3 1.8 %copy.158 = bf16[2,512,128]{1,2,0:T(8,128)(2,1)} copy(bf16[2,512,128]{2,1,0:T(8,128)(2,1)} %param.12) | data formatting | bytes 524288 | tf_op args[1]
  8.1 0.9 reshape.793
  9.1 3.2 %collective-permute-start.1 = (bf16[2,4,2,284]{3,2,1,0:T(2,128)(2,1)S(1)}, bf16[2,4,2,284]{3,2,1,0:T(2,128)(2,1)S(1)}, u32[]{:S(2)}, u32[]{:S(2)}) collective-permute-start(bf16[2,4,2,284]{3,2,1,0:T(2,128)(2,1)S(1)} %pad_maximum_fusion.8), channel_id=1, source_target_pairs={{0,8},{1,9},{2,10},{3,11},{4,12},{5,13},{6,14},{7,15},{8,0},{9,1},... | collective-permute-start | bytes 27272 | tf_op jit(solution)/shard_map/ppermute | solution.py:21
  12.3 1.7 %collective-permute-done.1 = bf16[2,4,2,284]{3,2,1,0:T(2,128)(2,1)S(1)} collective-permute-done((bf16[2,4,2,284]{3,2,1,0:T(2,128)(2,1)S(1)}, bf16[2,4,2,284]{3,2,1,0:T(2,128)(2,1)S(1)}, u32[]{:S(2)}, u32[]{:S(2)}) %collective-permute-start.1) | collective-permute-done | bytes 9120 | tf_op jit(solution)/shard_map/ppermute | solution.py:21
  14.0 1.9 %collective-permute-start.2 = (bf16[2,2,4,2,284]{4,3,2,1,0:T(2,128)(2,1)S(1)}, bf16[2,2,4,2,284]{4,3,2,1,0:T(2,128)(2,1)S(1)}, u32[]{:S(2)}, u32[]{:S(2)}) collective-permute-start(bf16[2,2,4,2,284]{4,3,2,1,0:T(2,128)(2,1)S(1)} %pad_maximum_fusion.6), channel_id=1, source_target_pairs={{0,4},{1,5},{2,6},{3,7},{4,0},{5,1},{6,2},{7,3},{8,12},{9,13},{10,... | collective-permute-start | bytes 54536 | tf_op jit(solution)/shard_map/ppermute | solution.py:21
  16.0 1.9 %collective-permute-done.2 = bf16[2,2,4,2,284]{4,3,2,1,0:T(2,128)(2,1)S(1)} collective-permute-done((bf16[2,2,4,2,284]{4,3,2,1,0:T(2,128)(2,1)S(1)}, bf16[2,2,4,2,284]{4,3,2,1,0:T(2,128)(2,1)S(1)}, u32[]{:S(2)}, u32[]{:S(2)}) %collective-permute-start.2) | collective-permute-done | bytes 18208 | tf_op jit(solution)/shard_map/ppermute | solution.py:21
  18.0 1.9 %collective-permute-start.3 = (bf16[2,2,2,4,2,284]{5,4,3,2,1,0:T(2,128)(2,1)S(1)}, bf16[2,2,2,4,2,284]{5,4,3,2,1,0:T(2,128)(2,1)S(1)}, u32[]{:S(2)}, u32[]{:S(2)}) collective-permute-start(bf16[2,2,2,4,2,284]{5,4,3,2,1,0:T(2,128)(2,1)S(1)} %pad_maximum_fusion.3), channel_id=1, source_target_pairs={{0,2},{1,3},{2,0},{3,1},{4,6},{5,7},{6,4},{7,5},{8,10},{9,11},{10,... | collective-permute-start | bytes 109064 | tf_op jit(solution)/shard_map/ppermute | solution.py:21
  19.9 2.2 %collective-permute-done.3 = bf16[2,2,2,4,2,284]{5,4,3,2,1,0:T(2,128)(2,1)S(1)} collective-permute-done((bf16[2,2,2,4,2,284]{5,4,3,2,1,0:T(2,128)(2,1)S(1)}, bf16[2,2,2,4,2,284]{5,4,3,2,1,0:T(2,128)(2,1)S(1)}, u32[]{:S(2)}, u32[]{:S(2)}) %collective-permute-start.3) | collective-permute-done | bytes 36384 | tf_op jit(solution)/shard_map/ppermute | solution.py:21
  22.5 1.1 %collective-permute-done.4 = bf16[2,2,2,2,4,2,284]{6,5,4,3,2,1,0:T(2,128)(2,1)S(1)} collective-permute-done((bf16[2,2,2,2,4,2,284]{6,5,4,3,2,1,0:T(2,128)(2,1)S(1)}, bf16[2,2,2,2,4,2,284]{6,5,4,3,2,1,0:T(2,128)(2,1)S(1)}, u32[]{:S(2)}, u32[]{:S(2)}) %collective-permute-start.4) | collective-permute-done | bytes 72736 | tf_op jit(solution)/shard_map/ppermute | solution.py:21
  24.0 0.9 gather_fusion
  26.7 0.6 copy-done.4
  27.7 1.8 %collective-permute-start.5 = (f32[16,412]{1,0:T(8,128)S(1)}, f32[16,412]{1,0:T(8,128)S(1)}, u32[]{:S(2)}, u32[]{:S(2)}) collective-permute-start(f32[16,412]{1,0:T(8,128)S(1)} %pad_maximum_fusion.5), channel_id=1, source_target_pairs={{0,16},{16,0},{1,17},{17,1},{2,18},{18,2},{3,19},{19,3},{4,20},{20... | collective-permute-start | bytes 79112 | tf_op jit(solution)/shard_map/ppermute | solution.py:37
  29.5 3.3 %fusion.185 = f32[16,1136]{1,0:T(8,128)S(1)} fusion(bf16[2272,1136]{1,0:T(8,128)(2,1)} %param.20, f32[16,4544]{1,0:T(8,128)S(1)} %reshape.801, s32[]{:T(128)S(6)} %select_n.420, f32[2272]{0:T(1024)S(1)} %dynamic-slice.5, f32[2272]{0:T(1024)S(1)} %dynamic-slice.4, f32[16]{0:T(128)S(1)} %rsqrt.12, f32[16]{0:T(128)S(1)} %div.134), kind=kOutput, calls=%fused_computation.427 | convolution fusion | flops 82773504 | bytes 5407748 | tf_op jit(solution)/shard_map/dot_general | solution.py:167
  33.4 2.7 %collective-permute-start.7 = (bf16[4,2,284]{2,1,0:T(2,128)(2,1)S(1)}, bf16[4,2,284]{2,1,0:T(2,128)(2,1)S(1)}, u32[]{:S(2)}, u32[]{:S(2)}) collective-permute-start(bf16[4,2,284]{2,1,0:T(2,128)(2,1)S(1)} %constant_dynamic-slice_fusion.1), channel_id=1, source_target_pairs={{0,8},{1,9},{2,10},{3,11},{4,12},{5,13},{6,14},{7,15},{8,0},{9,1},... | collective-permute-start | bytes 13640 | tf_op jit(solution)/shard_map/ppermute | solution.py:21
  36.3 1.7 %collective-permute-done.7 = bf16[4,2,284]{2,1,0:T(2,128)(2,1)S(1)} collective-permute-done((bf16[4,2,284]{2,1,0:T(2,128)(2,1)S(1)}, bf16[4,2,284]{2,1,0:T(2,128)(2,1)S(1)}, u32[]{:S(2)}, u32[]{:S(2)}) %collective-permute-start.7) | collective-permute-done | bytes 4576 | tf_op jit(solution)/shard_map/ppermute | solution.py:21
  38.0 1.6 %collective-permute-start.8 = (bf16[2,4,2,284]{3,2,1,0:T(2,128)(2,1)S(1)}, bf16[2,4,2,284]{3,2,1,0:T(2,128)(2,1)S(1)}, u32[]{:S(2)}, u32[]{:S(2)}) collective-permute-start(bf16[2,4,2,284]{3,2,1,0:T(2,128)(2,1)S(1)} %pad_maximum_fusion.9), channel_id=1, source_target_pairs={{0,4},{1,5},{2,6},{3,7},{4,0},{5,1},{6,2},{7,3},{8,12},{9,13},{10,... | collective-permute-start | bytes 27272 | tf_op jit(solution)/shard_map/ppermute | solution.py:21
  39.7 2.1 %collective-permute-done.8 = bf16[2,4,2,284]{3,2,1,0:T(2,128)(2,1)S(1)} collective-permute-done((bf16[2,4,2,284]{3,2,1,0:T(2,128)(2,1)S(1)}, bf16[2,4,2,284]{3,2,1,0:T(2,128)(2,1)S(1)}, u32[]{:S(2)}, u32[]{:S(2)}) %collective-permute-start.8) | collective-permute-done | bytes 9120 | tf_op jit(solution)/shard_map/ppermute | solution.py:21
  41.8 1.6 %collective-permute-start.9 = (bf16[2,2,4,2,284]{4,3,2,1,0:T(2,128)(2,1)S(1)}, bf16[2,2,4,2,284]{4,3,2,1,0:T(2,128)(2,1)S(1)}, u32[]{:S(2)}, u32[]{:S(2)}) collective-permute-start(bf16[2,2,4,2,284]{4,3,2,1,0:T(2,128)(2,1)S(1)} %pad_maximum_fusion.7), channel_id=1, source_target_pairs={{0,2},{1,3},{2,0},{3,1},{4,6},{5,7},{6,4},{7,5},{8,10},{9,11},{10,... | collective-permute-start | bytes 54536 | tf_op jit(solution)/shard_map/ppermute | solution.py:21
  43.4 2.3 %collective-permute-done.9 = bf16[2,2,4,2,284]{4,3,2,1,0:T(2,128)(2,1)S(1)} collective-permute-done((bf16[2,2,4,2,284]{4,3,2,1,0:T(2,128)(2,1)S(1)}, bf16[2,2,4,2,284]{4,3,2,1,0:T(2,128)(2,1)S(1)}, u32[]{:S(2)}, u32[]{:S(2)}) %collective-permute-start.9) | collective-permute-done | bytes 18208 | tf_op jit(solution)/shard_map/ppermute | solution.py:21
  45.9 1.1 %collective-permute-done.10 = bf16[2,2,2,4,2,284]{5,4,3,2,1,0:T(2,128)(2,1)S(1)} collective-permute-done((bf16[2,2,2,4,2,284]{5,4,3,2,1,0:T(2,128)(2,1)S(1)}, bf16[2,2,2,4,2,284]{5,4,3,2,1,0:T(2,128)(2,1)S(1)}, u32[]{:S(2)}, u32[]{:S(2)}) %collective-permute-start.10) | collective-permute-done | bytes 36384 | tf_op jit(solution)/shard_map/ppermute | solution.py:21
  47.3 0.6 gather_fusion.1
  51.7 0.6 collective-permute-start.6
  53.3 1.6 %collective-permute-start.12 = (bf16[2,284,70]{1,0,2:T(2,128)(2,1)S(1)}, bf16[2,284,70]{1,0,2:T(2,128)(2,1)S(1)}, u32[]{:S(2)}, u32[]{:S(2)}) collective-permute-start(bf16[2,284,70]{1,0,2:T(2,128)(2,1)S(1)} %fusion.15), channel_id=1, source_target_pairs={{0,2},{1,3},{2,0},{3,1},{4,6},{5,7},{6,4},{7,5},{8,10},{9,11},{10,... | collective-permute-start | bytes 238568 | tf_op jit(solution)/shard_map/ppermute | solution.py:82
  54.9 1.3 %collective-permute-done.6 = f32[16,1136]{1,0:T(8,128)S(1)} collective-permute-done((f32[16,1136]{1,0:T(8,128)S(1)}, f32[16,1136]{1,0:T(8,128)S(1)}, u32[]{:S(2)}, u32[]{:S(2)}) %collective-permute-start.6) | collective-permute-done | bytes 72736 | tf_op jit(solution)/shard_map/ppermute | solution.py:37
  56.2 3.4 %fusion.33 = f32[16,2272]{1,0:T(8,128)S(1)} fusion(bf16[1136,2272]{1,0:T(8,128)(2,1)} %param.21, f32[16,1136]{1,0:T(8,128)S(1)} %fusion.185, f32[16,1136]{1,0:T(8,128)S(1)} %collective-permute-done.6), kind=kOutput, calls=%fused_computation.94 | convolution fusion | flops 83791360 | bytes 5452800 | tf_op jit(solution)/shard_map/dot_general | solution.py:173
  60.1 1.6 %collective-permute-start.13 = (bf16[2,284,70]{1,0,2:T(2,128)(2,1)S(1)}, bf16[2,284,70]{1,0,2:T(2,128)(2,1)S(1)}, u32[]{:S(2)}, u32[]{:S(2)}) collective-permute-start(bf16[2,284,70]{1,0,2:T(2,128)(2,1)S(1)} %fusion.16), channel_id=1, source_target_pairs={{0,4},{1,5},{2,6},{3,7},{4,0},{5,1},{6,2},{7,3},{8,12},{9,13},{10,... | collective-permute-start | bytes 238568 | tf_op jit(solution)/shard_map/ppermute | solution.py:82
  61.8 3.1 %collective-permute-done.13 = bf16[2,284,70]{1,0,2:T(2,128)(2,1)S(1)} collective-permute-done((bf16[2,284,70]{1,0,2:T(2,128)(2,1)S(1)}, bf16[2,284,70]{1,0,2:T(2,128)(2,1)S(1)}, u32[]{:S(2)}, u32[]{:S(2)}) %collective-permute-start.13) | collective-permute-done | bytes 79552 | tf_op jit(solution)/shard_map/ppermute | solution.py:82
  65.6 2.7 %collective-permute-start.14 = (bf16[2,284,70]{1,2,0:T(8,128)(2,1)S(1)}, bf16[2,284,70]{1,2,0:T(8,128)(2,1)S(1)}, u32[]{:S(2)}, u32[]{:S(2)}) collective-permute-start(bf16[2,284,70]{1,2,0:T(8,128)(2,1)S(1)} %concatenate.68), channel_id=1, source_target_pairs={{0,8},{1,9},{2,10},{3,11},{4,12},{5,13},{6,14},{7,15},{8,0},{9,1},... | collective-permute-start | bytes 238568 | tf_op jit(solution)/shard_map/ppermute | solution.py:82
  68.2 4.2 %collective-permute-done.14 = bf16[2,284,70]{1,2,0:T(8,128)(2,1)S(1)} collective-permute-done((bf16[2,284,70]{1,2,0:T(8,128)(2,1)S(1)}, bf16[2,284,70]{1,2,0:T(8,128)(2,1)S(1)}, u32[]{:S(2)}, u32[]{:S(2)}) %collective-permute-start.14) | collective-permute-done | bytes 79552 | tf_op jit(solution)/shard_map/ppermute | solution.py:82
  73.6 3.0 %collective-permute-done.15 = bf16[4,2,284]{2,0,1:T(4,128)(2,1)S(1)} collective-permute-done((bf16[4,2,284]{2,0,1:T(4,128)(2,1)S(1)}, bf16[4,2,284]{2,0,1:T(4,128)(2,1)S(1)}, u32[]{:S(2)}, u32[]{:S(2)}) %collective-permute-start.15) | collective-permute-done | bytes 4576 | tf_op jit(solution)/shard_map/ppermute | solution.py:21
  77.8 0.6 gather_fusion.3
  79.0 1.3 %collective-permute-done.16 = f32[2,2,2,4,2,284]{5,4,3,2,1,0:T(2,128)S(1)} collective-permute-done((f32[2,2,2,4,2,284]{5,4,3,2,1,0:T(2,128)S(1)}, f32[2,2,2,4,2,284]{5,4,3,2,1,0:T(2,128)S(1)}, u32[]{:S(2)}, u32[]{:S(2)}) %collective-permute-start.16) | collective-permute-done | bytes 72736 | tf_op jit(solution)/shard_map/ppermute | solution.py:54
  80.3 1.6 %collective-permute-start.17 = (f32[2,2,4,2,284]{4,3,2,1,0:T(2,128)S(1)}, f32[2,2,4,2,284]{4,3,2,1,0:T(2,128)S(1)}, u32[]{:S(2)}, u32[]{:S(2)}) collective-permute-start(f32[2,2,4,2,284]{4,3,2,1,0:T(2,128)S(1)} %fusion.30), channel_id=1, source_target_pairs={{0,2},{1,3},{2,0},{3,1},{4,6},{5,7},{6,4},{7,5},{8,10},{9,11},{10,... | collective-permute-start | bytes 109064 | tf_op jit(solution)/shard_map/ppermute | solution.py:54
  81.9 2.6 %collective-permute-done.17 = f32[2,2,4,2,284]{4,3,2,1,0:T(2,128)S(1)} collective-permute-done((f32[2,2,4,2,284]{4,3,2,1,0:T(2,128)S(1)}, f32[2,2,4,2,284]{4,3,2,1,0:T(2,128)S(1)}, u32[]{:S(2)}, u32[]{:S(2)}) %collective-permute-start.17) | collective-permute-done | bytes 36384 | tf_op jit(solution)/shard_map/ppermute | solution.py:54
  84.6 0.7 collective-permute-start.18
  85.3 3.2 %collective-permute-done.18 = f32[2,4,2,284]{3,2,1,0:T(2,128)S(1)} collective-permute-done((f32[2,4,2,284]{3,2,1,0:T(2,128)S(1)}, f32[2,4,2,284]{3,2,1,0:T(2,128)S(1)}, u32[]{:S(2)}, u32[]{:S(2)}) %collective-permute-start.18) | collective-permute-done | bytes 18208 | tf_op jit(solution)/shard_map/ppermute | solution.py:54
  88.5 2.1 %collective-permute-start.19 = (f32[4,2,284]{2,1,0:T(2,128)S(1)}, f32[4,2,284]{2,1,0:T(2,128)S(1)}, u32[]{:S(2)}, u32[]{:S(2)}) collective-permute-start(f32[4,2,284]{2,1,0:T(2,128)S(1)} %select_bitcast_fusion), channel_id=1, source_target_pairs={{0,8},{1,9},{2,10},{3,11},{4,12},{5,13},{6,14},{7,15},{8,0},{9,1},... | collective-permute-start | bytes 27272 | tf_op jit(solution)/shard_map/ppermute | solution.py:54
  90.6 2.6 %collective-permute-done.19 = f32[4,2,284]{2,1,0:T(2,128)S(1)} collective-permute-done((f32[4,2,284]{2,1,0:T(2,128)S(1)}, f32[4,2,284]{2,1,0:T(2,128)S(1)}, u32[]{:S(2)}, u32[]{:S(2)}) %collective-permute-start.19) | collective-permute-done | bytes 9120 | tf_op jit(solution)/shard_map/ppermute | solution.py:54
  93.2 3.9 %collective-permute-start.20 = (f32[4,2,284]{2,1,0:T(2,128)S(1)}, f32[4,2,284]{2,1,0:T(2,128)S(1)}, u32[]{:S(2)}, u32[]{:S(2)}) collective-permute-start(f32[4,2,284]{2,1,0:T(2,128)S(1)} %bitcast_add_fusion), channel_id=1, source_target_pairs={{0,0},{1,1},{2,2},{3,3},{4,4},{5,5},{6,6},{7,7},{8,16},{9,17},{10,... | collective-permute-start | bytes 27272 | tf_op jit(solution)/shard_map/ppermute | solution.py:242
  97.1 0.8 copy.188
  98.0 2.6 %collective-permute-done.20 = f32[4,2,284]{2,1,0:T(2,128)S(1)} collective-permute-done((f32[4,2,284]{2,1,0:T(2,128)S(1)}, f32[4,2,284]{2,1,0:T(2,128)S(1)}, u32[]{:S(2)}, u32[]{:S(2)}) %collective-permute-start.20) | collective-permute-done | bytes 9120 | tf_op jit(solution)/shard_map/ppermute | solution.py:242
  100.6 0.6 add_convert_fusion
  (175 shorter events, 14.1 us)
Async XLA Ops:
  0.6 76.7 %copy-start = (bf16[284,2272]{1,0:T(8,128)(2,1)S(1)}, bf16[284,2272]{1,0:T(8,128)(2,1)}, u32[]{:S(2)}) copy-start(bf16[284,2272]{1,0:T(8,128)(2,1)} %param.19) | copy-start | bytes 3871492
  0.6 8.4 %copy-start.5 = (bf16[4,2,284]{2,1,0:T(2,128)(2,1)S(1)}, bf16[4,2,284]{2,1,0:T(2,128)(2,1)}, u32[]{:S(2)}) copy-start(bf16[4,2,284]{2,1,0:T(2,128)(2,1)} %param.11) | copy-start | bytes 13636
  0.7 8.4 %collective-permute-start = (bf16[4,2,284]{2,1,0:T(2,128)(2,1)}, bf16[4,2,284]{2,1,0:T(2,128)(2,1)S(1)}, u32[]{:S(2)}, u32[]{:S(2)}) collective-permute-start(bf16[4,2,284]{2,1,0:T(2,128)(2,1)} %param.11), channel_id=1, source_target_pairs={{0,16},{16,0},{1,17},{17,1},{2,18},{18,2},{3,19},{19,3},{4,20},{20... | collective-permute-start | bytes 13640 | tf_op jit(solution)/shard_map/ppermute | solution.py:21
  9.1 4.9 %collective-permute-start.1 = (bf16[2,4,2,284]{3,2,1,0:T(2,128)(2,1)S(1)}, bf16[2,4,2,284]{3,2,1,0:T(2,128)(2,1)S(1)}, u32[]{:S(2)}, u32[]{:S(2)}) collective-permute-start(bf16[2,4,2,284]{3,2,1,0:T(2,128)(2,1)S(1)} %pad_maximum_fusion.8), channel_id=1, source_target_pairs={{0,8},{1,9},{2,10},{3,11},{4,12},{5,13},{6,14},{7,15},{8,0},{9,1},... | collective-permute-start | bytes 27272 | tf_op jit(solution)/shard_map/ppermute | solution.py:21
  14.0 3.9 %collective-permute-start.2 = (bf16[2,2,4,2,284]{4,3,2,1,0:T(2,128)(2,1)S(1)}, bf16[2,2,4,2,284]{4,3,2,1,0:T(2,128)(2,1)S(1)}, u32[]{:S(2)}, u32[]{:S(2)}) collective-permute-start(bf16[2,2,4,2,284]{4,3,2,1,0:T(2,128)(2,1)S(1)} %pad_maximum_fusion.6), channel_id=1, source_target_pairs={{0,4},{1,5},{2,6},{3,7},{4,0},{5,1},{6,2},{7,3},{8,12},{9,13},{10,... | collective-permute-start | bytes 54536 | tf_op jit(solution)/shard_map/ppermute | solution.py:21
  18.0 4.2 %collective-permute-start.3 = (bf16[2,2,2,4,2,284]{5,4,3,2,1,0:T(2,128)(2,1)S(1)}, bf16[2,2,2,4,2,284]{5,4,3,2,1,0:T(2,128)(2,1)S(1)}, u32[]{:S(2)}, u32[]{:S(2)}) collective-permute-start(bf16[2,2,2,4,2,284]{5,4,3,2,1,0:T(2,128)(2,1)S(1)} %pad_maximum_fusion.3), channel_id=1, source_target_pairs={{0,2},{1,3},{2,0},{3,1},{4,6},{5,7},{6,4},{7,5},{8,10},{9,11},{10,... | collective-permute-start | bytes 109064 | tf_op jit(solution)/shard_map/ppermute | solution.py:21
  22.3 1.4 %collective-permute-start.4 = (bf16[2,2,2,2,4,2,284]{6,5,4,3,2,1,0:T(2,128)(2,1)S(1)}, bf16[2,2,2,2,4,2,284]{6,5,4,3,2,1,0:T(2,128)(2,1)S(1)}, u32[]{:S(2)}, u32[]{:S(2)}) collective-permute-start(bf16[2,2,2,2,4,2,284]{6,5,4,3,2,1,0:T(2,128)(2,1)S(1)} %pad_maximum_fusion.1), channel_id=1, source_target_pairs={{0,1},{1,0},{2,3},{3,2},{4,5},{5,4},{6,7},{7,6},{8,9},{9,8},{10,11... | collective-permute-start | bytes 218120 | tf_op jit(solution)/shard_map/ppermute | solution.py:21
  25.0 1.3 %copy-start.1 = (bf16[2272,284]{0,1:T(8,128)(2,1)S(1)}, bf16[2272,284]{0,1:T(8,128)(2,1)}, u32[]{:S(2)}) copy-start(bf16[2272,284]{0,1:T(8,128)(2,1)} %param.17) | copy-start | bytes 3871492
  26.3 1.1 %copy-start.4 = (bf16[2272,128]{1,0:T(8,128)(2,1)S(1)}, bf16[2272,128]{1,0:T(8,128)(2,1)}, u32[]{:S(2)}) copy-start(bf16[2272,128]{1,0:T(8,128)(2,1)} %param.18) | copy-start | bytes 1744900
  27.7 8.3 %copy-start.3 = (bf16[2,512,128]{1,2,0:T(8,128)(2,1)S(1)}, bf16[2,512,128]{1,2,0:T(8,128)(2,1)}, u32[]{:S(2)}) copy-start(bf16[2,512,128]{1,2,0:T(8,128)(2,1)} %copy.158) | copy-start | bytes 786436
  27.7 5.1 %collective-permute-start.5 = (f32[16,412]{1,0:T(8,128)S(1)}, f32[16,412]{1,0:T(8,128)S(1)}, u32[]{:S(2)}, u32[]{:S(2)}) collective-permute-start(f32[16,412]{1,0:T(8,128)S(1)} %pad_maximum_fusion.5), channel_id=1, source_target_pairs={{0,16},{16,0},{1,17},{17,1},{2,18},{18,2},{3,19},{19,3},{4,20},{20... | collective-permute-start | bytes 79112 | tf_op jit(solution)/shard_map/ppermute | solution.py:37
  33.4 4.6 %collective-permute-start.7 = (bf16[4,2,284]{2,1,0:T(2,128)(2,1)S(1)}, bf16[4,2,284]{2,1,0:T(2,128)(2,1)S(1)}, u32[]{:S(2)}, u32[]{:S(2)}) collective-permute-start(bf16[4,2,284]{2,1,0:T(2,128)(2,1)S(1)} %constant_dynamic-slice_fusion.1), channel_id=1, source_target_pairs={{0,8},{1,9},{2,10},{3,11},{4,12},{5,13},{6,14},{7,15},{8,0},{9,1},... | collective-permute-start | bytes 13640 | tf_op jit(solution)/shard_map/ppermute | solution.py:21
  38.0 3.8 %collective-permute-start.8 = (bf16[2,4,2,284]{3,2,1,0:T(2,128)(2,1)S(1)}, bf16[2,4,2,284]{3,2,1,0:T(2,128)(2,1)S(1)}, u32[]{:S(2)}, u32[]{:S(2)}) collective-permute-start(bf16[2,4,2,284]{3,2,1,0:T(2,128)(2,1)S(1)} %pad_maximum_fusion.9), channel_id=1, source_target_pairs={{0,4},{1,5},{2,6},{3,7},{4,0},{5,1},{6,2},{7,3},{8,12},{9,13},{10,... | collective-permute-start | bytes 27272 | tf_op jit(solution)/shard_map/ppermute | solution.py:21
  41.8 3.9 %collective-permute-start.9 = (bf16[2,2,4,2,284]{4,3,2,1,0:T(2,128)(2,1)S(1)}, bf16[2,2,4,2,284]{4,3,2,1,0:T(2,128)(2,1)S(1)}, u32[]{:S(2)}, u32[]{:S(2)}) collective-permute-start(bf16[2,2,4,2,284]{4,3,2,1,0:T(2,128)(2,1)S(1)} %pad_maximum_fusion.7), channel_id=1, source_target_pairs={{0,2},{1,3},{2,0},{3,1},{4,6},{5,7},{6,4},{7,5},{8,10},{9,11},{10,... | collective-permute-start | bytes 54536 | tf_op jit(solution)/shard_map/ppermute | solution.py:21
  45.8 1.3 %collective-permute-start.10 = (bf16[2,2,2,4,2,284]{5,4,3,2,1,0:T(2,128)(2,1)S(1)}, bf16[2,2,2,4,2,284]{5,4,3,2,1,0:T(2,128)(2,1)S(1)}, u32[]{:S(2)}, u32[]{:S(2)}) collective-permute-start(bf16[2,2,2,4,2,284]{5,4,3,2,1,0:T(2,128)(2,1)S(1)} %pad_maximum_fusion.4), channel_id=1, source_target_pairs={{0,1},{1,0},{2,3},{3,2},{4,5},{5,4},{6,7},{7,6},{8,9},{9,8},{10,11... | collective-permute-start | bytes 109064 | tf_op jit(solution)/shard_map/ppermute | solution.py:21
  48.9 1.0 copy-start.2
  51.5 1.4 %collective-permute-start.11 = (bf16[2,284,70]{1,0,2:T(2,128)(2,1)S(1)}, bf16[2,284,70]{1,0,2:T(2,128)(2,1)S(1)}, u32[]{:S(2)}, u32[]{:S(2)}) collective-permute-start(bf16[2,284,70]{1,0,2:T(2,128)(2,1)S(1)} %fusion.14), channel_id=1, source_target_pairs={{0,1},{1,0},{2,3},{3,2},{4,5},{5,4},{6,7},{7,6},{8,9},{9,8},{10,11... | collective-permute-start | bytes 238568 | tf_op jit(solution)/shard_map/ppermute | solution.py:82
  51.7 4.5 %collective-permute-start.6 = (f32[16,1136]{1,0:T(8,128)S(1)}, f32[16,1136]{1,0:T(8,128)S(1)}, u32[]{:S(2)}, u32[]{:S(2)}) collective-permute-start(f32[16,1136]{1,0:T(8,128)S(1)} %fusion.185), channel_id=1, source_target_pairs={{0,16},{16,0},{1,17},{17,1},{2,18},{18,2},{3,19},{19,3},{4,20},{20... | collective-permute-start | bytes 218120 | tf_op jit(solution)/shard_map/ppermute | solution.py:37
  53.3 6.3 %collective-permute-start.12 = (bf16[2,284,70]{1,0,2:T(2,128)(2,1)S(1)}, bf16[2,284,70]{1,0,2:T(2,128)(2,1)S(1)}, u32[]{:S(2)}, u32[]{:S(2)}) collective-permute-start(bf16[2,284,70]{1,0,2:T(2,128)(2,1)S(1)} %fusion.15), channel_id=1, source_target_pairs={{0,2},{1,3},{2,0},{3,1},{4,6},{5,7},{6,4},{7,5},{8,10},{9,11},{10,... | collective-permute-start | bytes 238568 | tf_op jit(solution)/shard_map/ppermute | solution.py:82
  60.1 4.8 %collective-permute-start.13 = (bf16[2,284,70]{1,0,2:T(2,128)(2,1)S(1)}, bf16[2,284,70]{1,0,2:T(2,128)(2,1)S(1)}, u32[]{:S(2)}, u32[]{:S(2)}) collective-permute-start(bf16[2,284,70]{1,0,2:T(2,128)(2,1)S(1)} %fusion.16), channel_id=1, source_target_pairs={{0,4},{1,5},{2,6},{3,7},{4,0},{5,1},{6,2},{7,3},{8,12},{9,13},{10,... | collective-permute-start | bytes 238568 | tf_op jit(solution)/shard_map/ppermute | solution.py:82
  65.6 6.9 %collective-permute-start.14 = (bf16[2,284,70]{1,2,0:T(8,128)(2,1)S(1)}, bf16[2,284,70]{1,2,0:T(8,128)(2,1)S(1)}, u32[]{:S(2)}, u32[]{:S(2)}) collective-permute-start(bf16[2,284,70]{1,2,0:T(8,128)(2,1)S(1)} %concatenate.68), channel_id=1, source_target_pairs={{0,8},{1,9},{2,10},{3,11},{4,12},{5,13},{6,14},{7,15},{8,0},{9,1},... | collective-permute-start | bytes 238568 | tf_op jit(solution)/shard_map/ppermute | solution.py:82
  73.0 3.6 %collective-permute-start.15 = (bf16[4,2,284]{2,0,1:T(4,128)(2,1)S(1)}, bf16[4,2,284]{2,0,1:T(4,128)(2,1)S(1)}, u32[]{:S(2)}, u32[]{:S(2)}) collective-permute-start(bf16[4,2,284]{2,0,1:T(4,128)(2,1)S(1)} %get-tuple-element.51), channel_id=1, source_target_pairs={{0,16},{16,0},{1,17},{17,1},{2,18},{18,2},{3,19},{19,3},{4,20},{20... | collective-permute-start | bytes 13640 | tf_op jit(solution)/shard_map/ppermute | solution.py:21
  78.9 1.4 %collective-permute-start.16 = (f32[2,2,2,4,2,284]{5,4,3,2,1,0:T(2,128)S(1)}, f32[2,2,2,4,2,284]{5,4,3,2,1,0:T(2,128)S(1)}, u32[]{:S(2)}, u32[]{:S(2)}) collective-permute-start(f32[2,2,2,4,2,284]{5,4,3,2,1,0:T(2,128)S(1)} %fusion.13), channel_id=1, source_target_pairs={{0,1},{1,0},{2,3},{3,2},{4,5},{5,4},{6,7},{7,6},{8,9},{9,8},{10,11... | collective-permute-start | bytes 218120 | tf_op jit(solution)/shard_map/ppermute | solution.py:54
  80.3 4.2 %collective-permute-start.17 = (f32[2,2,4,2,284]{4,3,2,1,0:T(2,128)S(1)}, f32[2,2,4,2,284]{4,3,2,1,0:T(2,128)S(1)}, u32[]{:S(2)}, u32[]{:S(2)}) collective-permute-start(f32[2,2,4,2,284]{4,3,2,1,0:T(2,128)S(1)} %fusion.30), channel_id=1, source_target_pairs={{0,2},{1,3},{2,0},{3,1},{4,6},{5,7},{6,4},{7,5},{8,10},{9,11},{10,... | collective-permute-start | bytes 109064 | tf_op jit(solution)/shard_map/ppermute | solution.py:54
  84.6 3.9 %collective-permute-start.18 = (f32[2,4,2,284]{3,2,1,0:T(2,128)S(1)}, f32[2,4,2,284]{3,2,1,0:T(2,128)S(1)}, u32[]{:S(2)}, u32[]{:S(2)}) collective-permute-start(f32[2,4,2,284]{3,2,1,0:T(2,128)S(1)} %fusion.65), channel_id=1, source_target_pairs={{0,4},{1,5},{2,6},{3,7},{4,0},{5,1},{6,2},{7,3},{8,12},{9,13},{10,... | collective-permute-start | bytes 54536 | tf_op jit(solution)/shard_map/ppermute | solution.py:54
  88.5 4.7 %collective-permute-start.19 = (f32[4,2,284]{2,1,0:T(2,128)S(1)}, f32[4,2,284]{2,1,0:T(2,128)S(1)}, u32[]{:S(2)}, u32[]{:S(2)}) collective-permute-start(f32[4,2,284]{2,1,0:T(2,128)S(1)} %select_bitcast_fusion), channel_id=1, source_target_pairs={{0,8},{1,9},{2,10},{3,11},{4,12},{5,13},{6,14},{7,15},{8,0},{9,1},... | collective-permute-start | bytes 27272 | tf_op jit(solution)/shard_map/ppermute | solution.py:54
  93.2 7.4 %collective-permute-start.20 = (f32[4,2,284]{2,1,0:T(2,128)S(1)}, f32[4,2,284]{2,1,0:T(2,128)S(1)}, u32[]{:S(2)}, u32[]{:S(2)}) collective-permute-start(f32[4,2,284]{2,1,0:T(2,128)S(1)} %bitcast_add_fusion), channel_id=1, source_target_pairs={{0,0},{1,1},{2,2},{3,3},{4,4},{5,5},{6,6},{7,7},{8,16},{9,17},{10,... | collective-permute-start | bytes 27272 | tf_op jit(solution)/shard_map/ppermute | solution.py:242

commit v5 on v4

--- a/solution.py
+++ b/solution.py
@@ -13,13 +13,16 @@
     return [(index, index ^ bit) for index in range(size)]
 
 
-def gather_xor(block, axis, size):
+def gather_xor(block, axis, size, riders=None):
     levels = size.bit_length() - 1
+    riders = dict(riders or {})
     stacked = block
     for level in range(levels):
         bit = 2 ** (levels - 1 - level)
         stacked = jnp.stack([stacked, lax.ppermute(stacked, axis, xor_pairs(size, bit))])
-    return stacked.reshape((size,) + block.shape)
+        if level in riders:
+            stacked, riders[level] = lax.optimization_barrier((stacked, riders[level]))
+    return stacked.reshape((size,) + block.shape), riders
 
 
 def xor_slot(offset, size):
@@ -143,21 +146,16 @@
     group_index = lax.axis_index("req")
     shard_index = lax.axis_index("seq")
 
-    request_ids = jnp.arange(total, dtype=jnp.int32)
-    serves = placement[:, None] == request_ids[None, :]
-    own_serves = lax.dynamic_slice_in_dim(serves, group_index * group_rows, group_rows, 0)
-    slot_lengths = jnp.sum(jnp.where(own_serves, lengths[None, :], 0), axis=1)
-    step_offsets = jnp.arange(steps, dtype=jnp.int32)
-    positions = slot_lengths[None, :] + step_offsets[:, None]
     seq_ids = jnp.arange(seq_size, dtype=jnp.int32)
     req_ids = jnp.arange(req_size, dtype=jnp.int32)
     seq_slots = xor_slot(shard_index ^ seq_ids, seq_size)
     req_slots = xor_slot(group_index ^ req_ids, req_size)
 
-    every = gather_xor(gather_xor(states, "req", req_size), "seq", seq_size)
-    slot_req = xor_slot(group_index ^ (placement // group_rows), req_size)
-    current_all = every[seq_slots[None, :], slot_req[:, None], :, (placement % group_rows)[:, None], :]
-    current_all = current_all.transpose(2, 0, 1, 3).reshape(steps, total, model_width)
+    by_request, _ = gather_xor(states, "req", req_size)
+    every, riders = gather_xor(by_request, "seq", seq_size, {0: (norm_gain, norm_bias)})
+    norm_gain, norm_bias = riders[0]
+    every = jnp.take(jnp.take(every, seq_slots, axis=0), req_slots, axis=1)
+    current_all = every.transpose(2, 1, 3, 0, 4).reshape(steps, total, model_width)
     normed = layer_norm(current_all.reshape(rows, model_width), norm_gain, norm_bias)
     normed_part = lax.dynamic_slice_in_dim(normed, group_index * part_width, part_width, 1)
 
@@ -172,15 +170,22 @@
     hidden = jax.nn.gelu(up_part, approximate=False).astype(jnp.bfloat16)
     down_part = jnp.dot(hidden, w_down, preferred_element_type=jnp.float32)
 
-    own_query = lax.dynamic_slice_in_dim(query_raw, group_index * group_rows, group_rows, 1)
-    query_all = jnp.take(gather_xor(own_query, "seq", seq_size), seq_slots, axis=0)
+    request_ids = jnp.arange(total, dtype=jnp.int32)
+    own_requests = lax.dynamic_slice_in_dim(placement, group_index * group_rows, group_rows, 0)
+    slot_lengths = jnp.take(lengths, own_requests, mode="clip")
+    step_offsets = jnp.arange(steps, dtype=jnp.int32)
+    positions = slot_lengths[None, :] + step_offsets[:, None]
+    own_query = jnp.take(query_raw, own_requests, axis=1, mode="clip")
+    query_all, riders = gather_xor(own_query, "seq", seq_size, {0: kv_cache})
+    kv_cache = riders[0]
+    query_all = jnp.take(query_all, seq_slots, axis=0)
     query_all = query_all.transpose(1, 2, 0, 3).reshape(steps, group_rows, model_width)
     flat_positions = positions.reshape(-1)
     query_rows = rotate(
         query_all.astype(jnp.float32).reshape(steps * group_rows, head_count, head_width),
         flat_positions,
     ).astype(jnp.bfloat16)
-    own_keyval = lax.dynamic_slice_in_dim(keyval, group_index * group_rows, group_rows, 1)
+    own_keyval = jnp.take(keyval, own_requests, axis=1, mode="clip")
     own_keyval = own_keyval.reshape(steps * group_rows, 2 * head_width)
     new_key = rotate(own_keyval[:, None, :head_width], flat_positions)[:, 0, :]
     new_entry = jnp.concatenate([new_key, own_keyval[:, head_width:]], axis=-1).astype(jnp.bfloat16)
@@ -224,13 +229,15 @@
         .astype(jnp.bfloat16)
     )
     own_mixed = lax.dynamic_slice_in_dim(mixed, shard_index * slice_width, slice_width, 2)
-    every_mixed = jnp.take(gather_xor(own_mixed, "req", req_size), req_slots, axis=0)
-    mixed_part = every_mixed.transpose(1, 0, 2, 3).reshape(rows, slice_width)
+    every_mixed = jnp.take(gather_xor(own_mixed, "req", req_size)[0], req_slots, axis=0)
+    serves = placement[:, None] == request_ids[None, :]
+    inverse = jnp.sum(jnp.where(serves, request_ids[:, None], 0), axis=0)
+    mixed_part = every_mixed.transpose(1, 0, 2, 3).reshape(steps, total, slice_width)
+    mixed_part = jnp.take(mixed_part, inverse, axis=1, mode="clip").reshape(rows, slice_width)
 
     partial_sum = jnp.dot(mixed_part, w_out, preferred_element_type=jnp.float32) + down_part
-    inverse = jnp.sum(jnp.where(serves, request_ids[:, None], 0), axis=0)
     chunks = seq_size // req_size
-    by_request = jnp.take(partial_sum.reshape(steps, total, part_width), inverse, axis=1)
+    by_request = partial_sum.reshape(steps, total, part_width)
     blocks = by_request.reshape(steps, req_size, group_rows, chunks, slice_width)
     blocks = blocks.transpose(1, 3, 0, 2, 4).reshape(seq_size, steps, group_rows, slice_width)
     reduced = scatter_sum(blocks, "seq", seq_size)

time: 102 us -> 98.8 us (0.969)
  waiting for transfers between devices: 38.6 us -> 36.9 us
  other arithmetic: 8.59 us -> 7.55 us
    gather x5 -> x10, local copies, waits for them, and re-layouts: 2.91 us -> 5.57 us  [the longest x2 1.32 us: shards(): every = jnp.take(jnp.take(every, seq_slots, axis=0), req_slots, axis=1)]
    unnamed x15 -> x18, local copies, waits for them, and re-layouts: 4.26 us -> 2.46 us
    ppermute x10, waiting for transfers between devices: 17.2 us -> 15.5 us  [gather_xor(): lax.ppermute(stacked, axis, xor_pairs(size, bit))]
    dynamic_slice x2, local copies, waits for them, and re-layouts: 1.54 us -> 0.16 us  [shards(): lax.dynamic_slice_in_dim(normed, group_index * part_width, part_width, 1)]
    another operation x17 -> x13, other arithmetic: 1.33 us -> 2.4 us  [gather_xor(): jnp.stack([stacked, lax.ppermute(stacked, axis, xor_pairs(size, bit))])]
  transfers between devices with their start and end apart: 21 -> 21, of which waited for: 18 -> 19; matrix products, arithmetic and copies ran while one was open for 17% -> 14% of each run, Pallas kernels for 0% -> 0%
where the time goes in v5:
time: 98.8 us; the launch traced here: 98.4 us
  waiting for transfers between devices  36.9 us (37%)
  starting transfers between devices  30.2 us (31%)
  local copies, waits for them, and re-layouts  13.6 us (14%)
  matrix products  8.63 us (9%)
  other arithmetic  7.55 us (8%)
  between operations  1.41 us (1%)
    ppermute x10, waiting for transfers between devices, gather_xor(): lax.ppermute(stacked, axis, xor_pairs(size, bit))  15.5 us
    ppermute x10, starting transfers between devices, gather_xor(): lax.ppermute(stacked, axis, xor_pairs(size, bit))  13.4 us
    ppermute x4, waiting for transfers between devices, scatter_sum(): blocks = keep + lax.ppermute(send, axis, xor_pairs(size, bit))  9.56 us
    ppermute x4, waiting for transfers between devices, merge_over(): other = lax.ppermute(sent, axis, xor_pairs(size, bit))  7.99 us
    ppermute x4, starting transfers between devices, merge_over(): other = lax.ppermute(sent, axis, xor_pairs(size, bit))  6.09 us
    ppermute x4, starting transfers between devices, scatter_sum(): blocks = keep + lax.ppermute(send, axis, xor_pairs(size, bit))  4.47 us
    ppermute x1, starting transfers between devices, shards(): own_branch = lax.ppermute(reduced, ALL, routes)  3.94 us
    dot_general x1, matrix products, shards(): down_part = jnp.dot(hidden, w_down, preferred_element_type=jnp.float32)  3.39 us
  transfers between devices with their start and end apart: 21, of which 19 were waited for; matrix products, arithmetic and copies ran while one was open for 14% of the time, Pallas kernels for 0%

profile of v5, /device:TPU:2, one launch (start us, length us, event | category | flops | bytes accessed | tf_op | source)
XLA Modules:
  0.0 98.4 jit_solution(15824421872059690302)
XLA Ops:
  0.8 0.7 select_reduce_fusion.1
  1.5 0.7 dynamic_slice.10
  2.3 1.3 %gather_fusion.2 = s32[2]{0:T(128)S(1)} fusion(s32[4]{0:T(128)} %param.13, s32[1024]{0:T(1024)S(1)} %get-tuple-element.100), kind=kCustom, calls=%fused_computation.2 | custom fusion | bytes 24 | tf_op jit(solution)/shard_map/jit(_take)/gather | solution.py:175
  4.6 0.7 pad_maximum_fusion.8
  5.3 3.0 %collective-permute-start.1 = (bf16[2,4,2,284]{3,2,1,0:T(2,128)(2,1)S(1)}, bf16[2,4,2,284]{3,2,1,0:T(2,128)(2,1)S(1)}, u32[]{:S(2)}, u32[]{:S(2)}) collective-permute-start(bf16[2,4,2,284]{3,2,1,0:T(2,128)(2,1)S(1)} %pad_maximum_fusion.8), channel_id=1, source_target_pairs={{0,8},{1,9},{2,10},{3,11},{4,12},{5,13},{6,14},{7,15},{8,0},{9,1},... | collective-permute-start | bytes 27272 | tf_op jit(solution)/shard_map/ppermute | solution.py:22
  8.3 0.7 fusion.191
  9.0 1.0 %collective-permute-done.1 = bf16[2,4,2,284]{3,2,1,0:T(2,128)(2,1)S(1)} collective-permute-done((bf16[2,4,2,284]{3,2,1,0:T(2,128)(2,1)S(1)}, bf16[2,4,2,284]{3,2,1,0:T(2,128)(2,1)S(1)}, u32[]{:S(2)}, u32[]{:S(2)}) %collective-permute-start.1) | collective-permute-done | bytes 9120 | tf_op jit(solution)/shard_map/ppermute | solution.py:22
  10.1 1.9 %collective-permute-start.2 = (bf16[2,2,4,2,284]{4,3,2,1,0:T(2,128)(2,1)S(1)}, bf16[2,2,4,2,284]{4,3,2,1,0:T(2,128)(2,1)S(1)}, u32[]{:S(2)}, u32[]{:S(2)}) collective-permute-start(bf16[2,2,4,2,284]{4,3,2,1,0:T(2,128)(2,1)S(1)} %pad_maximum_fusion.6), channel_id=1, source_target_pairs={{0,4},{1,5},{2,6},{3,7},{4,0},{5,1},{6,2},{7,3},{8,12},{9,13},{10,... | collective-permute-start | bytes 54536 | tf_op jit(solution)/shard_map/ppermute | solution.py:22
  12.1 0.9 reshape.752
  13.1 0.8 collective-permute-done.2
  14.0 1.8 %collective-permute-start.3 = (bf16[2,2,2,4,2,284]{5,4,3,2,1,0:T(2,128)(2,1)S(1)}, bf16[2,2,2,4,2,284]{5,4,3,2,1,0:T(2,128)(2,1)S(1)}, u32[]{:S(2)}, u32[]{:S(2)}) collective-permute-start(bf16[2,2,2,4,2,284]{5,4,3,2,1,0:T(2,128)(2,1)S(1)} %pad_maximum_fusion.3), channel_id=1, source_target_pairs={{0,2},{1,3},{2,0},{3,1},{4,6},{5,7},{6,4},{7,5},{8,10},{9,11},{10,... | collective-permute-start | bytes 109064 | tf_op jit(solution)/shard_map/ppermute | solution.py:22
  16.0 2.2 %collective-permute-done.3 = bf16[2,2,2,4,2,284]{5,4,3,2,1,0:T(2,128)(2,1)S(1)} collective-permute-done((bf16[2,2,2,4,2,284]{5,4,3,2,1,0:T(2,128)(2,1)S(1)}, bf16[2,2,2,4,2,284]{5,4,3,2,1,0:T(2,128)(2,1)S(1)}, u32[]{:S(2)}, u32[]{:S(2)}) %collective-permute-start.3) | collective-permute-done | bytes 36384 | tf_op jit(solution)/shard_map/ppermute | solution.py:22
  18.6 1.1 %collective-permute-done.4 = bf16[2,2,2,2,4,2,284]{6,5,4,3,2,1,0:T(2,128)(2,1)S(1)} collective-permute-done((bf16[2,2,2,2,4,2,284]{6,5,4,3,2,1,0:T(2,128)(2,1)S(1)}, bf16[2,2,2,2,4,2,284]{6,5,4,3,2,1,0:T(2,128)(2,1)S(1)}, u32[]{:S(2)}, u32[]{:S(2)}) %collective-permute-start.4) | collective-permute-done | bytes 72736 | tf_op jit(solution)/shard_map/ppermute | solution.py:22
  20.1 0.7 gather_fusion
  21.1 0.6 gather_fusion.1
  23.6 0.6 copy-done.3
  24.6 1.8 %collective-permute-start.5 = (f32[16,412]{1,0:T(8,128)S(1)}, f32[16,412]{1,0:T(8,128)S(1)}, u32[]{:S(2)}, u32[]{:S(2)}) collective-permute-start(f32[16,412]{1,0:T(8,128)S(1)} %pad_maximum_fusion.5), channel_id=1, source_target_pairs={{0,16},{16,0},{1,17},{17,1},{2,18},{18,2},{3,19},{19,3},{4,20},{20... | collective-permute-start | bytes 79112 | tf_op jit(solution)/shard_map/ppermute | solution.py:40
  26.4 3.3 %fusion.180 = f32[16,1136]{1,0:T(8,128)S(1)} fusion(bf16[2272,1136]{1,0:T(8,128)(2,1)} %param.20, f32[16,4544]{1,0:T(8,128)S(1)} %reshape.760, s32[]{:T(128)S(6)} %select_n.359, f32[2272]{0:T(1024)S(1)} %dynamic-slice.5, f32[2272]{0:T(1024)S(1)} %dynamic-slice.4, f32[16]{0:T(128)S(1)} %rsqrt.12, f32[16]{0:T(128)S(1)} %div.129), kind=kOutput, calls=%fused_computation.409 | convolution fusion | flops 82773504 | bytes 5407748 | tf_op jit(solution)/shard_map/dot_general | solution.py:165
  31.1 2.6 %collective-permute-start.7 = (bf16[4,2,284]{2,0,1:T(4,128)(2,1)S(1)}, bf16[4,2,284]{2,0,1:T(4,128)(2,1)S(1)}, u32[]{:S(2)}, u32[]{:S(2)}) collective-permute-start(bf16[4,2,284]{2,0,1:T(4,128)(2,1)S(1)} %bitcast.315), channel_id=1, source_target_pairs={{0,8},{1,9},{2,10},{3,11},{4,12},{5,13},{6,14},{7,15},{8,0},{9,1},... | collective-permute-start | bytes 13640 | tf_op jit(solution)/shard_map/ppermute | solution.py:22
  33.9 1.8 %collective-permute-done.7 = bf16[4,2,284]{2,0,1:T(4,128)(2,1)S(1)} collective-permute-done((bf16[4,2,284]{2,0,1:T(4,128)(2,1)S(1)}, bf16[4,2,284]{2,0,1:T(4,128)(2,1)S(1)}, u32[]{:S(2)}, u32[]{:S(2)}) %collective-permute-start.7) | collective-permute-done | bytes 4576 | tf_op jit(solution)/shard_map/ppermute | solution.py:22
  35.7 1.6 %collective-permute-start.8 = (bf16[2,4,2,284]{3,1,2,0:T(4,128)(2,1)S(1)}, bf16[2,4,2,284]{3,1,2,0:T(4,128)(2,1)S(1)}, u32[]{:S(2)}, u32[]{:S(2)}) collective-permute-start(bf16[2,4,2,284]{3,1,2,0:T(4,128)(2,1)S(1)} %pad_maximum_fusion.9), channel_id=1, source_target_pairs={{0,4},{1,5},{2,6},{3,7},{4,0},{5,1},{6,2},{7,3},{8,12},{9,13},{10,... | collective-permute-start | bytes 27272 | tf_op jit(solution)/shard_map/ppermute | solution.py:22
  37.4 2.0 %collective-permute-done.8 = bf16[2,4,2,284]{3,1,2,0:T(4,128)(2,1)S(1)} collective-permute-done((bf16[2,4,2,284]{3,1,2,0:T(4,128)(2,1)S(1)}, bf16[2,4,2,284]{3,1,2,0:T(4,128)(2,1)S(1)}, u32[]{:S(2)}, u32[]{:S(2)}) %collective-permute-start.8) | collective-permute-done | bytes 9120 | tf_op jit(solution)/shard_map/ppermute | solution.py:22
  39.5 1.6 %collective-permute-start.9 = (bf16[2,2,4,2,284]{4,2,3,1,0:T(4,128)(2,1)S(1)}, bf16[2,2,4,2,284]{4,2,3,1,0:T(4,128)(2,1)S(1)}, u32[]{:S(2)}, u32[]{:S(2)}) collective-permute-start(bf16[2,2,4,2,284]{4,2,3,1,0:T(4,128)(2,1)S(1)} %get-tuple-element.69), channel_id=1, source_target_pairs={{0,2},{1,3},{2,0},{3,1},{4,6},{5,7},{6,4},{7,5},{8,10},{9,11},{10,... | collective-permute-start | bytes 54536 | tf_op jit(solution)/shard_map/ppermute | solution.py:22
  41.3 2.1 %collective-permute-done.9 = bf16[2,2,4,2,284]{4,2,3,1,0:T(4,128)(2,1)S(1)} collective-permute-done((bf16[2,2,4,2,284]{4,2,3,1,0:T(4,128)(2,1)S(1)}, bf16[2,2,4,2,284]{4,2,3,1,0:T(4,128)(2,1)S(1)}, u32[]{:S(2)}, u32[]{:S(2)}) %collective-permute-start.9) | collective-permute-done | bytes 18208 | tf_op jit(solution)/shard_map/ppermute | solution.py:22
  43.7 1.0 %collective-permute-done.10 = bf16[2,2,2,4,2,284]{5,3,4,2,1,0:T(4,128)(2,1)S(1)} collective-permute-done((bf16[2,2,2,4,2,284]{5,3,4,2,1,0:T(4,128)(2,1)S(1)}, bf16[2,2,2,4,2,284]{5,3,4,2,1,0:T(4,128)(2,1)S(1)}, u32[]{:S(2)}, u32[]{:S(2)}) %collective-permute-start.10) | collective-permute-done | bytes 36384 | tf_op jit(solution)/shard_map/ppermute | solution.py:22
  44.8 0.6 gather_fusion.4
  49.8 0.6 collective-permute-done.11
  50.9 1.6 %collective-permute-start.12 = (bf16[2,284,70]{1,0,2:T(2,128)(2,1)S(1)}, bf16[2,284,70]{1,0,2:T(2,128)(2,1)S(1)}, u32[]{:S(2)}, u32[]{:S(2)}) collective-permute-start(bf16[2,284,70]{1,0,2:T(2,128)(2,1)S(1)} %fusion.16), channel_id=1, source_target_pairs={{0,2},{1,3},{2,0},{3,1},{4,6},{5,7},{6,4},{7,5},{8,10},{9,11},{10,... | collective-permute-start | bytes 238568 | tf_op jit(solution)/shard_map/ppermute | solution.py:85
  52.4 1.3 %collective-permute-done.6 = f32[16,1136]{1,0:T(8,128)S(1)} collective-permute-done((f32[16,1136]{1,0:T(8,128)S(1)}, f32[16,1136]{1,0:T(8,128)S(1)}, u32[]{:S(2)}, u32[]{:S(2)}) %collective-permute-start.6) | collective-permute-done | bytes 72736 | tf_op jit(solution)/shard_map/ppermute | solution.py:40
  53.8 3.4 %fusion.34 = f32[16,2272]{1,0:T(8,128)S(1)} fusion(bf16[1136,2272]{1,0:T(8,128)(2,1)} %param.21, f32[16,1136]{1,0:T(8,128)S(1)} %fusion.180, f32[16,1136]{1,0:T(8,128)S(1)} %collective-permute-done.6), kind=kOutput, calls=%fused_computation.100 | convolution fusion | flops 83791360 | bytes 5452800 | tf_op jit(solution)/shard_map/dot_general | solution.py:171
  57.6 1.6 %collective-permute-start.13 = (bf16[2,284,70]{1,0,2:T(2,128)(2,1)S(1)}, bf16[2,284,70]{1,0,2:T(2,128)(2,1)S(1)}, u32[]{:S(2)}, u32[]{:S(2)}) collective-permute-start(bf16[2,284,70]{1,0,2:T(2,128)(2,1)S(1)} %fusion.17), channel_id=1, source_target_pairs={{0,4},{1,5},{2,6},{3,7},{4,0},{5,1},{6,2},{7,3},{8,12},{9,13},{10,... | collective-permute-start | bytes 238568 | tf_op jit(solution)/shard_map/ppermute | solution.py:85
  59.3 3.1 %collective-permute-done.13 = bf16[2,284,70]{1,0,2:T(2,128)(2,1)S(1)} collective-permute-done((bf16[2,284,70]{1,0,2:T(2,128)(2,1)S(1)}, bf16[2,284,70]{1,0,2:T(2,128)(2,1)S(1)}, u32[]{:S(2)}, u32[]{:S(2)}) %collective-permute-start.13) | collective-permute-done | bytes 79552 | tf_op jit(solution)/shard_map/ppermute | solution.py:85
  63.1 2.6 %collective-permute-start.14 = (bf16[2,284,70]{1,2,0:T(8,128)(2,1)S(1)}, bf16[2,284,70]{1,2,0:T(8,128)(2,1)S(1)}, u32[]{:S(2)}, u32[]{:S(2)}) collective-permute-start(bf16[2,284,70]{1,2,0:T(8,128)(2,1)S(1)} %concatenate.64), channel_id=1, source_target_pairs={{0,8},{1,9},{2,10},{3,11},{4,12},{5,13},{6,14},{7,15},{8,0},{9,1},... | collective-permute-start | bytes 238568 | tf_op jit(solution)/shard_map/ppermute | solution.py:85
  65.7 4.3 %collective-permute-done.14 = bf16[2,284,70]{1,2,0:T(8,128)(2,1)S(1)} collective-permute-done((bf16[2,284,70]{1,2,0:T(8,128)(2,1)S(1)}, bf16[2,284,70]{1,2,0:T(8,128)(2,1)S(1)}, u32[]{:S(2)}, u32[]{:S(2)}) %collective-permute-start.14) | collective-permute-done | bytes 79552 | tf_op jit(solution)/shard_map/ppermute | solution.py:85
  70.5 0.6 collective-permute-start.15
  71.1 3.1 %collective-permute-done.15 = bf16[4,2,284]{2,0,1:T(4,128)(2,1)S(1)} collective-permute-done((bf16[4,2,284]{2,0,1:T(4,128)(2,1)S(1)}, bf16[4,2,284]{2,0,1:T(4,128)(2,1)S(1)}, u32[]{:S(2)}, u32[]{:S(2)}) %collective-permute-start.15) | collective-permute-done | bytes 4576 | tf_op jit(solution)/shard_map/ppermute | solution.py:22
  74.2 0.6 gather_fusion.6
  76.2 1.3 %collective-permute-done.16 = f32[2,2,2,4,2,284]{5,4,3,2,1,0:T(2,128)S(1)} collective-permute-done((f32[2,2,2,4,2,284]{5,4,3,2,1,0:T(2,128)S(1)}, f32[2,2,2,4,2,284]{5,4,3,2,1,0:T(2,128)S(1)}, u32[]{:S(2)}, u32[]{:S(2)}) %collective-permute-start.16) | collective-permute-done | bytes 72736 | tf_op jit(solution)/shard_map/ppermute | solution.py:57
  77.6 1.6 %collective-permute-start.17 = (f32[2,2,4,2,284]{4,3,2,1,0:T(2,128)S(1)}, f32[2,2,4,2,284]{4,3,2,1,0:T(2,128)S(1)}, u32[]{:S(2)}, u32[]{:S(2)}) collective-permute-start(f32[2,2,4,2,284]{4,3,2,1,0:T(2,128)S(1)} %fusion.31), channel_id=1, source_target_pairs={{0,2},{1,3},{2,0},{3,1},{4,6},{5,7},{6,4},{7,5},{8,10},{9,11},{10,... | collective-permute-start | bytes 109064 | tf_op jit(solution)/shard_map/ppermute | solution.py:57
  79.2 2.6 %collective-permute-done.17 = f32[2,2,4,2,284]{4,3,2,1,0:T(2,128)S(1)} collective-permute-done((f32[2,2,4,2,284]{4,3,2,1,0:T(2,128)S(1)}, f32[2,2,4,2,284]{4,3,2,1,0:T(2,128)S(1)}, u32[]{:S(2)}, u32[]{:S(2)}) %collective-permute-start.17) | collective-permute-done | bytes 36384 | tf_op jit(solution)/shard_map/ppermute | solution.py:57
  81.8 0.7 collective-permute-start.18
  82.5 3.2 %collective-permute-done.18 = f32[2,4,2,284]{3,2,1,0:T(2,128)S(1)} collective-permute-done((f32[2,4,2,284]{3,2,1,0:T(2,128)S(1)}, f32[2,4,2,284]{3,2,1,0:T(2,128)S(1)}, u32[]{:S(2)}, u32[]{:S(2)}) %collective-permute-start.18) | collective-permute-done | bytes 18208 | tf_op jit(solution)/shard_map/ppermute | solution.py:57
  85.7 2.1 %collective-permute-start.19 = (f32[4,2,284]{2,1,0:T(2,128)S(1)}, f32[4,2,284]{2,1,0:T(2,128)S(1)}, u32[]{:S(2)}, u32[]{:S(2)}) collective-permute-start(f32[4,2,284]{2,1,0:T(2,128)S(1)} %select_bitcast_fusion), channel_id=1, source_target_pairs={{0,8},{1,9},{2,10},{3,11},{4,12},{5,13},{6,14},{7,15},{8,0},{9,1},... | collective-permute-start | bytes 27272 | tf_op jit(solution)/shard_map/ppermute | solution.py:57
  87.8 2.6 %collective-permute-done.19 = f32[4,2,284]{2,1,0:T(2,128)S(1)} collective-permute-done((f32[4,2,284]{2,1,0:T(2,128)S(1)}, f32[4,2,284]{2,1,0:T(2,128)S(1)}, u32[]{:S(2)}, u32[]{:S(2)}) %collective-permute-start.19) | collective-permute-done | bytes 9120 | tf_op jit(solution)/shard_map/ppermute | solution.py:57
  90.4 3.9 %collective-permute-start.20 = (f32[4,2,284]{2,1,0:T(2,128)S(1)}, f32[4,2,284]{2,1,0:T(2,128)S(1)}, u32[]{:S(2)}, u32[]{:S(2)}) collective-permute-start(f32[4,2,284]{2,1,0:T(2,128)S(1)} %bitcast_add_fusion), channel_id=1, source_target_pairs={{0,0},{1,1},{2,2},{3,3},{4,4},{5,5},{6,6},{7,7},{8,16},{9,17},{10,... | collective-permute-start | bytes 27272 | tf_op jit(solution)/shard_map/ppermute | solution.py:249
  94.4 0.8 copy.285
  95.2 2.6 %collective-permute-done.20 = f32[4,2,284]{2,1,0:T(2,128)S(1)} collective-permute-done((f32[4,2,284]{2,1,0:T(2,128)S(1)}, f32[4,2,284]{2,1,0:T(2,128)S(1)}, u32[]{:S(2)}, u32[]{:S(2)}) %collective-permute-start.20) | collective-permute-done | bytes 9120 | tf_op jit(solution)/shard_map/ppermute | solution.py:249
  97.8 0.6 add_convert_fusion
  (173 shorter events, 14.7 us)
Async XLA Ops:
  0.6 74.8 %copy-start = (bf16[284,2272]{1,0:T(8,128)(2,1)S(1)}, bf16[284,2272]{1,0:T(8,128)(2,1)}, u32[]{:S(2)}) copy-start(bf16[284,2272]{1,0:T(8,128)(2,1)} %param.19) | copy-start | bytes 3871492
  0.6 12.3 %copy-start.6 = (bf16[4544]{0:T(1024)(128)(2,1)S(1)}, bf16[4544]{0:T(1024)(128)(2,1)}, u32[]{:S(2)}) copy-start(bf16[4544]{0:T(1024)(128)(2,1)} %param.15) | copy-start | bytes 27268
  0.7 12.4 %copy-start.7 = (bf16[4544]{0:T(1024)(128)(2,1)S(1)}, bf16[4544]{0:T(1024)(128)(2,1)}, u32[]{:S(2)}) copy-start(bf16[4544]{0:T(1024)(128)(2,1)} %param.16) | copy-start | bytes 27268
  0.7 3.9 %collective-permute-start = (bf16[4,2,284]{2,1,0:T(2,128)(2,1)}, bf16[4,2,284]{2,1,0:T(2,128)(2,1)S(1)}, u32[]{:S(2)}, u32[]{:S(2)}) collective-permute-start(bf16[4,2,284]{2,1,0:T(2,128)(2,1)} %param.11), channel_id=1, source_target_pairs={{0,16},{16,0},{1,17},{17,1},{2,18},{18,2},{3,19},{19,3},{4,20},{20... | collective-permute-start | bytes 13640 | tf_op jit(solution)/shard_map/ppermute | solution.py:22
  5.3 4.7 %collective-permute-start.1 = (bf16[2,4,2,284]{3,2,1,0:T(2,128)(2,1)S(1)}, bf16[2,4,2,284]{3,2,1,0:T(2,128)(2,1)S(1)}, u32[]{:S(2)}, u32[]{:S(2)}) collective-permute-start(bf16[2,4,2,284]{3,2,1,0:T(2,128)(2,1)S(1)} %pad_maximum_fusion.8), channel_id=1, source_target_pairs={{0,8},{1,9},{2,10},{3,11},{4,12},{5,13},{6,14},{7,15},{8,0},{9,1},... | collective-permute-start | bytes 27272 | tf_op jit(solution)/shard_map/ppermute | solution.py:22
  10.1 3.9 %collective-permute-start.2 = (bf16[2,2,4,2,284]{4,3,2,1,0:T(2,128)(2,1)S(1)}, bf16[2,2,4,2,284]{4,3,2,1,0:T(2,128)(2,1)S(1)}, u32[]{:S(2)}, u32[]{:S(2)}) collective-permute-start(bf16[2,2,4,2,284]{4,3,2,1,0:T(2,128)(2,1)S(1)} %pad_maximum_fusion.6), channel_id=1, source_target_pairs={{0,4},{1,5},{2,6},{3,7},{4,0},{5,1},{6,2},{7,3},{8,12},{9,13},{10,... | collective-permute-start | bytes 54536 | tf_op jit(solution)/shard_map/ppermute | solution.py:22
  14.0 4.2 %collective-permute-start.3 = (bf16[2,2,2,4,2,284]{5,4,3,2,1,0:T(2,128)(2,1)S(1)}, bf16[2,2,2,4,2,284]{5,4,3,2,1,0:T(2,128)(2,1)S(1)}, u32[]{:S(2)}, u32[]{:S(2)}) collective-permute-start(bf16[2,2,2,4,2,284]{5,4,3,2,1,0:T(2,128)(2,1)S(1)} %pad_maximum_fusion.3), channel_id=1, source_target_pairs={{0,2},{1,3},{2,0},{3,1},{4,6},{5,7},{6,4},{7,5},{8,10},{9,11},{10,... | collective-permute-start | bytes 109064 | tf_op jit(solution)/shard_map/ppermute | solution.py:22
  18.3 1.4 %collective-permute-start.4 = (bf16[2,2,2,2,4,2,284]{6,5,4,3,2,1,0:T(2,128)(2,1)S(1)}, bf16[2,2,2,2,4,2,284]{6,5,4,3,2,1,0:T(2,128)(2,1)S(1)}, u32[]{:S(2)}, u32[]{:S(2)}) collective-permute-start(bf16[2,2,2,2,4,2,284]{6,5,4,3,2,1,0:T(2,128)(2,1)S(1)} %pad_maximum_fusion.1), channel_id=1, source_target_pairs={{0,1},{1,0},{2,3},{3,2},{4,5},{5,4},{6,7},{7,6},{8,9},{9,8},{10,11... | collective-permute-start | bytes 218120 | tf_op jit(solution)/shard_map/ppermute | solution.py:22
  21.9 1.3 %copy-start.1 = (bf16[2272,284]{0,1:T(8,128)(2,1)S(1)}, bf16[2272,284]{0,1:T(8,128)(2,1)}, u32[]{:S(2)}) copy-start(bf16[2272,284]{0,1:T(8,128)(2,1)} %param.17) | copy-start | bytes 3871492
  23.2 1.1 %copy-start.3 = (bf16[2272,128]{1,0:T(8,128)(2,1)S(1)}, bf16[2272,128]{1,0:T(8,128)(2,1)}, u32[]{:S(2)}) copy-start(bf16[2272,128]{1,0:T(8,128)(2,1)} %param.18) | copy-start | bytes 1744900
  24.6 16.5 %copy-start.4 = (bf16[2,512,128]{2,1,0:T(8,128)(2,1)S(1)}, bf16[2,512,128]{2,1,0:T(8,128)(2,1)}, u32[]{:S(2)}) copy-start(bf16[2,512,128]{2,1,0:T(8,128)(2,1)} %param.12) | copy-start | bytes 786436
  24.6 5.1 %collective-permute-start.5 = (f32[16,412]{1,0:T(8,128)S(1)}, f32[16,412]{1,0:T(8,128)S(1)}, u32[]{:S(2)}, u32[]{:S(2)}) collective-permute-start(f32[16,412]{1,0:T(8,128)S(1)} %pad_maximum_fusion.5), channel_id=1, source_target_pairs={{0,16},{16,0},{1,17},{17,1},{2,18},{18,2},{3,19},{19,3},{4,20},{20... | collective-permute-start | bytes 79112 | tf_op jit(solution)/shard_map/ppermute | solution.py:40
  31.1 4.6 %collective-permute-start.7 = (bf16[4,2,284]{2,0,1:T(4,128)(2,1)S(1)}, bf16[4,2,284]{2,0,1:T(4,128)(2,1)S(1)}, u32[]{:S(2)}, u32[]{:S(2)}) collective-permute-start(bf16[4,2,284]{2,0,1:T(4,128)(2,1)S(1)} %bitcast.315), channel_id=1, source_target_pairs={{0,8},{1,9},{2,10},{3,11},{4,12},{5,13},{6,14},{7,15},{8,0},{9,1},... | collective-permute-start | bytes 13640 | tf_op jit(solution)/shard_map/ppermute | solution.py:22
  35.7 3.8 %collective-permute-start.8 = (bf16[2,4,2,284]{3,1,2,0:T(4,128)(2,1)S(1)}, bf16[2,4,2,284]{3,1,2,0:T(4,128)(2,1)S(1)}, u32[]{:S(2)}, u32[]{:S(2)}) collective-permute-start(bf16[2,4,2,284]{3,1,2,0:T(4,128)(2,1)S(1)} %pad_maximum_fusion.9), channel_id=1, source_target_pairs={{0,4},{1,5},{2,6},{3,7},{4,0},{5,1},{6,2},{7,3},{8,12},{9,13},{10,... | collective-permute-start | bytes 27272 | tf_op jit(solution)/shard_map/ppermute | solution.py:22
  39.5 3.9 %collective-permute-start.9 = (bf16[2,2,4,2,284]{4,2,3,1,0:T(4,128)(2,1)S(1)}, bf16[2,2,4,2,284]{4,2,3,1,0:T(4,128)(2,1)S(1)}, u32[]{:S(2)}, u32[]{:S(2)}) collective-permute-start(bf16[2,2,4,2,284]{4,2,3,1,0:T(4,128)(2,1)S(1)} %get-tuple-element.69), channel_id=1, source_target_pairs={{0,2},{1,3},{2,0},{3,1},{4,6},{5,7},{6,4},{7,5},{8,10},{9,11},{10,... | collective-permute-start | bytes 54536 | tf_op jit(solution)/shard_map/ppermute | solution.py:22
  43.4 1.3 %collective-permute-start.10 = (bf16[2,2,2,4,2,284]{5,3,4,2,1,0:T(4,128)(2,1)S(1)}, bf16[2,2,2,4,2,284]{5,3,4,2,1,0:T(4,128)(2,1)S(1)}, u32[]{:S(2)}, u32[]{:S(2)}) collective-permute-start(bf16[2,2,2,4,2,284]{5,3,4,2,1,0:T(4,128)(2,1)S(1)} %get-tuple-element.67), channel_id=1, source_target_pairs={{0,1},{1,0},{2,3},{3,2},{4,5},{5,4},{6,7},{7,6},{8,9},{9,8},{10,11... | collective-permute-start | bytes 109064 | tf_op jit(solution)/shard_map/ppermute | solution.py:22
  46.4 1.0 %copy-start.2 = (pred[2,284,512]{2,1,0:T(8,128)(4,1)S(1)}, pred[2,284,512]{2,1,0:T(8,128)(4,1)}, u32[]{:S(2)}) copy-start(pred[2,284,512]{2,1,0:T(8,128)(4,1)} %reshape.752) | copy-start | bytes 872452
  49.0 1.4 %collective-permute-start.11 = (bf16[2,284,70]{1,0,2:T(2,128)(2,1)S(1)}, bf16[2,284,70]{1,0,2:T(2,128)(2,1)S(1)}, u32[]{:S(2)}, u32[]{:S(2)}) collective-permute-start(bf16[2,284,70]{1,0,2:T(2,128)(2,1)S(1)} %fusion.15), channel_id=1, source_target_pairs={{0,1},{1,0},{2,3},{3,2},{4,5},{5,4},{6,7},{7,6},{8,9},{9,8},{10,11... | collective-permute-start | bytes 238568 | tf_op jit(solution)/shard_map/ppermute | solution.py:85
  49.3 4.5 %collective-permute-start.6 = (f32[16,1136]{1,0:T(8,128)S(1)}, f32[16,1136]{1,0:T(8,128)S(1)}, u32[]{:S(2)}, u32[]{:S(2)}) collective-permute-start(f32[16,1136]{1,0:T(8,128)S(1)} %fusion.180), channel_id=1, source_target_pairs={{0,16},{16,0},{1,17},{17,1},{2,18},{18,2},{3,19},{19,3},{4,20},{20... | collective-permute-start | bytes 218120 | tf_op jit(solution)/shard_map/ppermute | solution.py:40
  50.9 6.3 %collective-permute-start.12 = (bf16[2,284,70]{1,0,2:T(2,128)(2,1)S(1)}, bf16[2,284,70]{1,0,2:T(2,128)(2,1)S(1)}, u32[]{:S(2)}, u32[]{:S(2)}) collective-permute-start(bf16[2,284,70]{1,0,2:T(2,128)(2,1)S(1)} %fusion.16), channel_id=1, source_target_pairs={{0,2},{1,3},{2,0},{3,1},{4,6},{5,7},{6,4},{7,5},{8,10},{9,11},{10,... | collective-permute-start | bytes 238568 | tf_op jit(solution)/shard_map/ppermute | solution.py:85
  57.6 4.8 %collective-permute-start.13 = (bf16[2,284,70]{1,0,2:T(2,128)(2,1)S(1)}, bf16[2,284,70]{1,0,2:T(2,128)(2,1)S(1)}, u32[]{:S(2)}, u32[]{:S(2)}) collective-permute-start(bf16[2,284,70]{1,0,2:T(2,128)(2,1)S(1)} %fusion.17), channel_id=1, source_target_pairs={{0,4},{1,5},{2,6},{3,7},{4,0},{5,1},{6,2},{7,3},{8,12},{9,13},{10,... | collective-permute-start | bytes 238568 | tf_op jit(solution)/shard_map/ppermute | solution.py:85
  63.1 6.9 %collective-permute-start.14 = (bf16[2,284,70]{1,2,0:T(8,128)(2,1)S(1)}, bf16[2,284,70]{1,2,0:T(8,128)(2,1)S(1)}, u32[]{:S(2)}, u32[]{:S(2)}) collective-permute-start(bf16[2,284,70]{1,2,0:T(8,128)(2,1)S(1)} %concatenate.64), channel_id=1, source_target_pairs={{0,8},{1,9},{2,10},{3,11},{4,12},{5,13},{6,14},{7,15},{8,0},{9,1},... | collective-permute-start | bytes 238568 | tf_op jit(solution)/shard_map/ppermute | solution.py:85
  70.5 3.6 %collective-permute-start.15 = (bf16[4,2,284]{2,0,1:T(4,128)(2,1)S(1)}, bf16[4,2,284]{2,0,1:T(4,128)(2,1)S(1)}, u32[]{:S(2)}, u32[]{:S(2)}) collective-permute-start(bf16[4,2,284]{2,0,1:T(4,128)(2,1)S(1)} %get-tuple-element.65), channel_id=1, source_target_pairs={{0,16},{16,0},{1,17},{17,1},{2,18},{18,2},{3,19},{19,3},{4,20},{20... | collective-permute-start | bytes 13640 | tf_op jit(solution)/shard_map/ppermute | solution.py:22
  75.9 21.9 %copy-start.5 = (bf16[4,2,284]{2,1,0:T(2,128)(2,1)S(1)}, bf16[4,2,284]{2,1,0:T(2,128)(2,1)}, u32[]{:S(2)}) copy-start(bf16[4,2,284]{2,1,0:T(2,128)(2,1)} %param.11) | copy-start | bytes 13636
  76.1 1.4 %collective-permute-start.16 = (f32[2,2,2,4,2,284]{5,4,3,2,1,0:T(2,128)S(1)}, f32[2,2,2,4,2,284]{5,4,3,2,1,0:T(2,128)S(1)}, u32[]{:S(2)}, u32[]{:S(2)}) collective-permute-start(f32[2,2,2,4,2,284]{5,4,3,2,1,0:T(2,128)S(1)} %fusion.14), channel_id=1, source_target_pairs={{0,1},{1,0},{2,3},{3,2},{4,5},{5,4},{6,7},{7,6},{8,9},{9,8},{10,11... | collective-permute-start | bytes 218120 | tf_op jit(solution)/shard_map/ppermute | solution.py:57
  77.6 4.2 %collective-permute-start.17 = (f32[2,2,4,2,284]{4,3,2,1,0:T(2,128)S(1)}, f32[2,2,4,2,284]{4,3,2,1,0:T(2,128)S(1)}, u32[]{:S(2)}, u32[]{:S(2)}) collective-permute-start(f32[2,2,4,2,284]{4,3,2,1,0:T(2,128)S(1)} %fusion.31), channel_id=1, source_target_pairs={{0,2},{1,3},{2,0},{3,1},{4,6},{5,7},{6,4},{7,5},{8,10},{9,11},{10,... | collective-permute-start | bytes 109064 | tf_op jit(solution)/shard_map/ppermute | solution.py:57
  81.8 3.9 %collective-permute-start.18 = (f32[2,4,2,284]{3,2,1,0:T(2,128)S(1)}, f32[2,4,2,284]{3,2,1,0:T(2,128)S(1)}, u32[]{:S(2)}, u32[]{:S(2)}) collective-permute-start(f32[2,4,2,284]{3,2,1,0:T(2,128)S(1)} %fusion.66), channel_id=1, source_target_pairs={{0,4},{1,5},{2,6},{3,7},{4,0},{5,1},{6,2},{7,3},{8,12},{9,13},{10,... | collective-permute-start | bytes 54536 | tf_op jit(solution)/shard_map/ppermute | solution.py:57
  85.7 4.7 %collective-permute-start.19 = (f32[4,2,284]{2,1,0:T(2,128)S(1)}, f32[4,2,284]{2,1,0:T(2,128)S(1)}, u32[]{:S(2)}, u32[]{:S(2)}) collective-permute-start(f32[4,2,284]{2,1,0:T(2,128)S(1)} %select_bitcast_fusion), channel_id=1, source_target_pairs={{0,8},{1,9},{2,10},{3,11},{4,12},{5,13},{6,14},{7,15},{8,0},{9,1},... | collective-permute-start | bytes 27272 | tf_op jit(solution)/shard_map/ppermute | solution.py:57
  90.4 7.4 %collective-permute-start.20 = (f32[4,2,284]{2,1,0:T(2,128)S(1)}, f32[4,2,284]{2,1,0:T(2,128)S(1)}, u32[]{:S(2)}, u32[]{:S(2)}) collective-permute-start(f32[4,2,284]{2,1,0:T(2,128)S(1)} %bitcast_add_fusion), channel_id=1, source_target_pairs={{0,0},{1,1},{2,2},{3,3},{4,4},{5,5},{6,6},{7,7},{8,16},{9,17},{10,... | collective-permute-start | bytes 27272 | tf_op jit(solution)/shard_map/ppermute | solution.py:249

commit v6 on v5

--- a/solution.py
+++ b/solution.py
@@ -154,7 +154,8 @@
     by_request, _ = gather_xor(states, "req", req_size)
     every, riders = gather_xor(by_request, "seq", seq_size, {0: (norm_gain, norm_bias)})
     norm_gain, norm_bias = riders[0]
-    every = jnp.take(jnp.take(every, seq_slots, axis=0), req_slots, axis=1)
+    every = every.reshape((seq_size * req_size,) + every.shape[2:])
+    every = jnp.take(every, seq_slots[:, None] * req_size + req_slots[None, :], axis=0, mode="clip")
     current_all = every.transpose(2, 1, 3, 0, 4).reshape(steps, total, model_width)
     normed = layer_norm(current_all.reshape(rows, model_width), norm_gain, norm_bias)
     normed_part = lax.dynamic_slice_in_dim(normed, group_index * part_width, part_width, 1)
@@ -164,28 +165,30 @@
     first = sum_over(jnp.concatenate([part_query, part_keyval], axis=1), "req", req_size)
     part_up = jnp.dot(normed_part, w_up, preferred_element_type=jnp.float32)
     first, part_up = lax.optimization_barrier((first, part_up))
-    query_raw = first[:, :slice_width].astype(jnp.bfloat16).reshape(steps, total, slice_width)
-    keyval = first[:, slice_width:].reshape(steps, total, 2 * head_width)
+    request_ids = jnp.arange(total, dtype=jnp.int32)
+    own_requests = lax.dynamic_slice_in_dim(placement, group_index * group_rows, group_rows, 0)
+    own_serves = own_requests[:, None] == request_ids[None, :]
+    slot_lengths = jnp.sum(jnp.where(own_serves, lengths[None, :], 0), axis=1)
+    step_offsets = jnp.arange(steps, dtype=jnp.int32)
+    positions = slot_lengths[None, :] + step_offsets[:, None]
+    own_first = jnp.sum(
+        jnp.where(own_serves[None, :, :, None], first.reshape(steps, 1, total, -1), 0.0), axis=2
+    )
+    own_query = own_first[:, :, :slice_width].astype(jnp.bfloat16)
+    own_keyval = own_first[:, :, slice_width:]
     up_part = sum_over(part_up, "req", req_size)
     hidden = jax.nn.gelu(up_part, approximate=False).astype(jnp.bfloat16)
     down_part = jnp.dot(hidden, w_down, preferred_element_type=jnp.float32)
 
-    request_ids = jnp.arange(total, dtype=jnp.int32)
-    own_requests = lax.dynamic_slice_in_dim(placement, group_index * group_rows, group_rows, 0)
-    slot_lengths = jnp.take(lengths, own_requests, mode="clip")
-    step_offsets = jnp.arange(steps, dtype=jnp.int32)
-    positions = slot_lengths[None, :] + step_offsets[:, None]
-    own_query = jnp.take(query_raw, own_requests, axis=1, mode="clip")
     query_all, riders = gather_xor(own_query, "seq", seq_size, {0: kv_cache})
     kv_cache = riders[0]
-    query_all = jnp.take(query_all, seq_slots, axis=0)
+    query_all = jnp.take(query_all, seq_slots, axis=0, mode="clip")
     query_all = query_all.transpose(1, 2, 0, 3).reshape(steps, group_rows, model_width)
     flat_positions = positions.reshape(-1)
     query_rows = rotate(
         query_all.astype(jnp.float32).reshape(steps * group_rows, head_count, head_width),
         flat_positions,
     ).astype(jnp.bfloat16)
-    own_keyval = jnp.take(keyval, own_requests, axis=1, mode="clip")
     own_keyval = own_keyval.reshape(steps * group_rows, 2 * head_width)
     new_key = rotate(own_keyval[:, None, :head_width], flat_positions)[:, 0, :]
     new_entry = jnp.concatenate([new_key, own_keyval[:, head_width:]], axis=-1).astype(jnp.bfloat16)
@@ -208,10 +211,8 @@
     scores = jnp.einsum(
         "gqd,gsd->gqs", query_heads, key_rows, preferred_element_type=jnp.float32
     ) * head_width ** (-0.5)
-    valid = global_positions[None, None, :] <= positions.T[:, :, None]
-    valid = jnp.broadcast_to(
-        valid[:, :, None, :], (group_rows, steps, head_count, seg_length)
-    ).reshape(group_rows, steps * head_count, seg_length)
+    head_positions = jnp.repeat(positions.T, head_count, axis=1)
+    valid = global_positions[None, None, :] <= head_positions[:, :, None]
     local_peak = jnp.max(jnp.where(valid, scores, NEGATIVE), axis=-1)
     weights = jnp.where(valid, jnp.exp(scores - local_peak[:, :, None]), 0.0)
     local_total = jnp.sum(weights, axis=-1)
@@ -229,11 +230,14 @@
         .astype(jnp.bfloat16)
     )
     own_mixed = lax.dynamic_slice_in_dim(mixed, shard_index * slice_width, slice_width, 2)
-    every_mixed = jnp.take(gather_xor(own_mixed, "req", req_size)[0], req_slots, axis=0)
+    every_mixed = gather_xor(own_mixed, "req", req_size)[0]
     serves = placement[:, None] == request_ids[None, :]
     inverse = jnp.sum(jnp.where(serves, request_ids[:, None], 0), axis=0)
+    mixed_rows = xor_slot(group_index ^ (inverse // group_rows), req_size) * group_rows + (
+        inverse % group_rows
+    )
     mixed_part = every_mixed.transpose(1, 0, 2, 3).reshape(steps, total, slice_width)
-    mixed_part = jnp.take(mixed_part, inverse, axis=1, mode="clip").reshape(rows, slice_width)
+    mixed_part = jnp.take(mixed_part, mixed_rows, axis=1, mode="clip").reshape(rows, slice_width)
 
     partial_sum = jnp.dot(mixed_part, w_out, preferred_element_type=jnp.float32) + down_part
     chunks = seq_size // req_size

time: 98.8 us -> 96.7 us (0.979)
  local copies, waits for them, and re-layouts: 13.6 us -> 9.57 us
  matrix products: 8.63 us -> 9.94 us
  other arithmetic: 7.55 us -> 8.83 us
  starting transfers between devices: 30.2 us -> 29.1 us
    gather x10 -> x4, local copies, waits for them, and re-layouts: 5.57 us -> 2.24 us  [the longest x1 1.01 us: shards(): jnp.take(every, seq_slots[:, None] * req_size + req_slots[None, :], axis=...]
    unnamed x18 -> x10, local copies, waits for them, and re-layouts: 2.46 us -> 1.03 us
    dynamic_slice x2, local copies, waits for them, and re-layouts: 0.16 us -> 1.54 us  [shards(): lax.dynamic_slice_in_dim(normed, group_index * part_width, part_width, 1)]
    dot_general x1, matrix products: 0.43 us -> 1.76 us  [shards(): jnp.dot(normed_part, w_query, preferred_element_type=jnp.float32)]
    another operation x13 -> x15, other arithmetic: 2.4 us -> 2.65 us  [gather_xor(): jnp.stack([stacked, lax.ppermute(stacked, axis, xor_pairs(size, bit))])]
  transfers between devices with their start and end apart: 21 -> 21, of which waited for: 19 -> 19; matrix products, arithmetic and copies ran while one was open for 14% -> 15% of each run, Pallas kernels for 0% -> 0%
where the time goes in v6:
time: 96.7 us; the launch traced here: 96.3 us
  waiting for transfers between devices  37.5 us (39%)
  starting transfers between devices  29.1 us (30%)
  matrix products  9.94 us (10%)
  local copies, waits for them, and re-layouts  9.57 us (10%)
  other arithmetic  8.83 us (9%)
  between operations  1.4 us (1%)
    ppermute x10, waiting for transfers between devices, gather_xor(): lax.ppermute(stacked, axis, xor_pairs(size, bit))  16 us
    ppermute x10, starting transfers between devices, gather_xor(): lax.ppermute(stacked, axis, xor_pairs(size, bit))  12.5 us
    ppermute x4, waiting for transfers between devices, scatter_sum(): blocks = keep + lax.ppermute(send, axis, xor_pairs(size, bit))  9.55 us
    ppermute x4, waiting for transfers between devices, merge_over(): other = lax.ppermute(sent, axis, xor_pairs(size, bit))  7.96 us
    ppermute x4, starting transfers between devices, merge_over(): other = lax.ppermute(sent, axis, xor_pairs(size, bit))  6.1 us
    ppermute x4, starting transfers between devices, scatter_sum(): blocks = keep + lax.ppermute(send, axis, xor_pairs(size, bit))  4.49 us
    ppermute x1, starting transfers between devices, shards(): own_branch = lax.ppermute(reduced, ALL, routes)  3.95 us
    dot_general x1, matrix products, shards(): down_part = jnp.dot(hidden, w_down, preferred_element_type=jnp.float32)  3.39 us
  transfers between devices with their start and end apart: 21, of which 19 were waited for; matrix products, arithmetic and copies ran while one was open for 15% of the time, Pallas kernels for 0%

profile of v6, /device:TPU:2, one launch (start us, length us, event | category | flops | bytes accessed | tf_op | source)
XLA Modules:
  0.0 96.3 jit_solution(5477526903491927943)
XLA Ops:
  0.8 0.8 select_reduce_fusion.1
  1.7 0.7 dynamic_slice.10
  2.5 0.8 select_reduce_fusion.2
  4.5 0.7 pad_maximum_fusion.8
  5.3 2.7 %collective-permute-start.1 = (bf16[2,4,2,284]{3,2,1,0:T(2,128)(2,1)S(1)}, bf16[2,4,2,284]{3,2,1,0:T(2,128)(2,1)S(1)}, u32[]{:S(2)}, u32[]{:S(2)}) collective-permute-start(bf16[2,4,2,284]{3,2,1,0:T(2,128)(2,1)S(1)} %pad_maximum_fusion.8), channel_id=1, source_target_pairs={{0,8},{1,9},{2,10},{3,11},{4,12},{5,13},{6,14},{7,15},{8,0},{9,1},... | collective-permute-start | bytes 27272 | tf_op jit(solution)/shard_map/ppermute | solution.py:22
  7.9 0.7 fusion.197
  8.6 1.3 %collective-permute-done.1 = bf16[2,4,2,284]{3,2,1,0:T(2,128)(2,1)S(1)} collective-permute-done((bf16[2,4,2,284]{3,2,1,0:T(2,128)(2,1)S(1)}, bf16[2,4,2,284]{3,2,1,0:T(2,128)(2,1)S(1)}, u32[]{:S(2)}, u32[]{:S(2)}) %collective-permute-start.1) | collective-permute-done | bytes 9120 | tf_op jit(solution)/shard_map/ppermute | solution.py:22
  10.0 1.6 %collective-permute-start.2 = (bf16[2,2,4,2,284]{4,3,2,1,0:T(2,128)(2,1)S(1)}, bf16[2,2,4,2,284]{4,3,2,1,0:T(2,128)(2,1)S(1)}, u32[]{:S(2)}, u32[]{:S(2)}) collective-permute-start(bf16[2,2,4,2,284]{4,3,2,1,0:T(2,128)(2,1)S(1)} %pad_maximum_fusion.6), channel_id=1, source_target_pairs={{0,4},{1,5},{2,6},{3,7},{4,0},{5,1},{6,2},{7,3},{8,12},{9,13},{10,... | collective-permute-start | bytes 54536 | tf_op jit(solution)/shard_map/ppermute | solution.py:22
  11.8 0.8 dynamic-slice.4
  12.5 0.8 dynamic-slice.5
  13.9 1.6 %collective-permute-start.3 = (bf16[2,2,2,4,2,284]{5,4,3,2,1,0:T(2,128)(2,1)S(1)}, bf16[2,2,2,4,2,284]{5,4,3,2,1,0:T(2,128)(2,1)S(1)}, u32[]{:S(2)}, u32[]{:S(2)}) collective-permute-start(bf16[2,2,2,4,2,284]{5,4,3,2,1,0:T(2,128)(2,1)S(1)} %pad_maximum_fusion.3), channel_id=1, source_target_pairs={{0,2},{1,3},{2,0},{3,1},{4,6},{5,7},{6,4},{7,5},{8,10},{9,11},{10,... | collective-permute-start | bytes 109064 | tf_op jit(solution)/shard_map/ppermute | solution.py:22
  15.6 2.5 %collective-permute-done.3 = bf16[2,2,2,4,2,284]{5,4,3,2,1,0:T(2,128)(2,1)S(1)} collective-permute-done((bf16[2,2,2,4,2,284]{5,4,3,2,1,0:T(2,128)(2,1)S(1)}, bf16[2,2,2,4,2,284]{5,4,3,2,1,0:T(2,128)(2,1)S(1)}, u32[]{:S(2)}, u32[]{:S(2)}) %collective-permute-start.3) | collective-permute-done | bytes 36384 | tf_op jit(solution)/shard_map/ppermute | solution.py:22
  18.5 1.1 %collective-permute-done.4 = bf16[2,2,2,2,4,2,284]{6,5,4,3,2,1,0:T(2,128)(2,1)S(1)} collective-permute-done((bf16[2,2,2,2,4,2,284]{6,5,4,3,2,1,0:T(2,128)(2,1)S(1)}, bf16[2,2,2,2,4,2,284]{6,5,4,3,2,1,0:T(2,128)(2,1)S(1)}, u32[]{:S(2)}, u32[]{:S(2)}) %collective-permute-start.4) | collective-permute-done | bytes 72736 | tf_op jit(solution)/shard_map/ppermute | solution.py:22
  19.9 1.0 %gather_fusion = bf16[32,4,2,284]{3,2,1,0:T(2,128)(2,1)S(1)} fusion(bf16[32,4,2,284]{3,2,1,0:T(2,128)(2,1)S(1)} %bitcast.313, s32[1024]{0:T(1024)S(1)} %pad_clamp_fusion.2), kind=kCustom, calls=%fused_computation | custom fusion | bytes 290944 | tf_op jit(solution)/shard_map/jit(_take)/gather | solution.py:158
  22.4 1.8 %fusion.182 = f32[16,284]{1,0:T(8,128)S(1)} fusion(bf16[2272,284]{0,1:T(8,128)(2,1)} %param.17, f32[16,4544]{1,0:T(8,128)S(1)} %reshape.851, s32[]{:T(128)S(6)} %select_n.330, f32[2272]{0:T(1024)S(1)} %dynamic-slice.5, f32[2272]{0:T(1024)S(1)} %dynamic-slice.4, f32[16]{0:T(128)S(1)} %rsqrt.12, f32[16]{0:T(128)S(1)} %div.131), kind=kOutput, calls=%fused_computation.407 | convolution fusion | flops 20829696 | bytes 1481732 | tf_op jit(solution)/shard_map/dot_general | solution.py:163
  24.5 1.5 %collective-permute-start.5 = (f32[16,412]{1,0:T(8,128)S(1)}, f32[16,412]{1,0:T(8,128)S(1)}, u32[]{:S(2)}, u32[]{:S(2)}) collective-permute-start(f32[16,412]{1,0:T(8,128)S(1)} %pad_maximum_fusion.5), channel_id=1, source_target_pairs={{0,16},{16,0},{1,17},{17,1},{2,18},{18,2},{3,19},{19,3},{4,20},{20... | collective-permute-start | bytes 79112 | tf_op jit(solution)/shard_map/ppermute | solution.py:40
  26.0 3.3 %fusion.184 = f32[16,1136]{1,0:T(8,128)S(1)} fusion(bf16[2272,1136]{1,0:T(8,128)(2,1)} %param.20, f32[16,4544]{1,0:T(8,128)S(1)} %reshape.851, s32[]{:T(128)S(6)} %select_n.330, f32[2272]{0:T(1024)S(1)} %dynamic-slice.5, f32[2272]{0:T(1024)S(1)} %dynamic-slice.4, f32[16]{0:T(128)S(1)} %rsqrt.12, f32[16]{0:T(128)S(1)} %div.131), kind=kOutput, calls=%fused_computation.408 | convolution fusion | flops 82773504 | bytes 5407748 | tf_op jit(solution)/shard_map/dot_general | solution.py:166
  29.8 2.6 %collective-permute-start.7 = (bf16[4,2,284]{2,1,0:T(2,128)(2,1)S(1)}, bf16[4,2,284]{2,1,0:T(2,128)(2,1)S(1)}, u32[]{:S(2)}, u32[]{:S(2)}) collective-permute-start(bf16[4,2,284]{2,1,0:T(2,128)(2,1)S(1)} %slice.429), channel_id=1, source_target_pairs={{0,8},{1,9},{2,10},{3,11},{4,12},{5,13},{6,14},{7,15},{8,0},{9,1},... | collective-permute-start | bytes 13640 | tf_op jit(solution)/shard_map/ppermute | solution.py:22
  32.6 1.8 %collective-permute-done.7 = bf16[4,2,284]{2,1,0:T(2,128)(2,1)S(1)} collective-permute-done((bf16[4,2,284]{2,1,0:T(2,128)(2,1)S(1)}, bf16[4,2,284]{2,1,0:T(2,128)(2,1)S(1)}, u32[]{:S(2)}, u32[]{:S(2)}) %collective-permute-start.7) | collective-permute-done | bytes 4576 | tf_op jit(solution)/shard_map/ppermute | solution.py:22
  34.5 1.6 %collective-permute-start.8 = (bf16[2,4,2,284]{3,2,1,0:T(2,128)(2,1)S(1)}, bf16[2,4,2,284]{3,2,1,0:T(2,128)(2,1)S(1)}, u32[]{:S(2)}, u32[]{:S(2)}) collective-permute-start(bf16[2,4,2,284]{3,2,1,0:T(2,128)(2,1)S(1)} %pad_maximum_fusion.9), channel_id=1, source_target_pairs={{0,4},{1,5},{2,6},{3,7},{4,0},{5,1},{6,2},{7,3},{8,12},{9,13},{10,... | collective-permute-start | bytes 27272 | tf_op jit(solution)/shard_map/ppermute | solution.py:22
  36.4 1.9 %collective-permute-done.8 = bf16[2,4,2,284]{3,2,1,0:T(2,128)(2,1)S(1)} collective-permute-done((bf16[2,4,2,284]{3,2,1,0:T(2,128)(2,1)S(1)}, bf16[2,4,2,284]{3,2,1,0:T(2,128)(2,1)S(1)}, u32[]{:S(2)}, u32[]{:S(2)}) %collective-permute-start.8) | collective-permute-done | bytes 9120 | tf_op jit(solution)/shard_map/ppermute | solution.py:22
  38.3 1.6 %collective-permute-start.9 = (bf16[2,2,4,2,284]{4,3,2,1,0:T(2,128)(2,1)S(1)}, bf16[2,2,4,2,284]{4,3,2,1,0:T(2,128)(2,1)S(1)}, u32[]{:S(2)}, u32[]{:S(2)}) collective-permute-start(bf16[2,2,4,2,284]{4,3,2,1,0:T(2,128)(2,1)S(1)} %pad_maximum_fusion.7), channel_id=1, source_target_pairs={{0,2},{1,3},{2,0},{3,1},{4,6},{5,7},{6,4},{7,5},{8,10},{9,11},{10,... | collective-permute-start | bytes 54536 | tf_op jit(solution)/shard_map/ppermute | solution.py:22
  40.0 2.3 %collective-permute-done.9 = bf16[2,2,4,2,284]{4,3,2,1,0:T(2,128)(2,1)S(1)} collective-permute-done((bf16[2,2,4,2,284]{4,3,2,1,0:T(2,128)(2,1)S(1)}, bf16[2,2,4,2,284]{4,3,2,1,0:T(2,128)(2,1)S(1)}, u32[]{:S(2)}, u32[]{:S(2)}) %collective-permute-start.9) | collective-permute-done | bytes 18208 | tf_op jit(solution)/shard_map/ppermute | solution.py:22
  42.5 1.1 %collective-permute-done.10 = bf16[2,2,2,4,2,284]{5,4,3,2,1,0:T(2,128)(2,1)S(1)} collective-permute-done((bf16[2,2,2,4,2,284]{5,4,3,2,1,0:T(2,128)(2,1)S(1)}, bf16[2,2,2,4,2,284]{5,4,3,2,1,0:T(2,128)(2,1)S(1)}, u32[]{:S(2)}, u32[]{:S(2)}) %collective-permute-start.10) | collective-permute-done | bytes 36384 | tf_op jit(solution)/shard_map/ppermute | solution.py:22
  43.8 0.6 gather_fusion.1
  47.8 0.6 collective-permute-start.6
  48.4 0.6 collective-permute-done.11
  49.4 1.6 %collective-permute-start.12 = (bf16[2,284,70]{1,0,2:T(2,128)(2,1)S(1)}, bf16[2,284,70]{1,0,2:T(2,128)(2,1)S(1)}, u32[]{:S(2)}, u32[]{:S(2)}) collective-permute-start(bf16[2,284,70]{1,0,2:T(2,128)(2,1)S(1)} %fusion.19), channel_id=1, source_target_pairs={{0,2},{1,3},{2,0},{3,1},{4,6},{5,7},{6,4},{7,5},{8,10},{9,11},{10,... | collective-permute-start | bytes 238568 | tf_op jit(solution)/shard_map/ppermute | solution.py:85
  51.0 1.3 %collective-permute-done.6 = f32[16,1136]{1,0:T(8,128)S(1)} collective-permute-done((f32[16,1136]{1,0:T(8,128)S(1)}, f32[16,1136]{1,0:T(8,128)S(1)}, u32[]{:S(2)}, u32[]{:S(2)}) %collective-permute-start.6) | collective-permute-done | bytes 72736 | tf_op jit(solution)/shard_map/ppermute | solution.py:40
  52.3 3.4 %fusion.37 = f32[16,2272]{1,0:T(8,128)S(1)} fusion(bf16[1136,2272]{1,0:T(8,128)(2,1)} %param.21, f32[16,1136]{1,0:T(8,128)S(1)} %fusion.184, f32[16,1136]{1,0:T(8,128)S(1)} %collective-permute-done.6), kind=kOutput, calls=%fused_computation.97 | convolution fusion | flops 83791360 | bytes 5452800 | tf_op jit(solution)/shard_map/dot_general | solution.py:181
  56.2 1.6 %collective-permute-start.13 = (bf16[2,284,70]{1,0,2:T(2,128)(2,1)S(1)}, bf16[2,284,70]{1,0,2:T(2,128)(2,1)S(1)}, u32[]{:S(2)}, u32[]{:S(2)}) collective-permute-start(bf16[2,284,70]{1,0,2:T(2,128)(2,1)S(1)} %fusion.20), channel_id=1, source_target_pairs={{0,4},{1,5},{2,6},{3,7},{4,0},{5,1},{6,2},{7,3},{8,12},{9,13},{10,... | collective-permute-start | bytes 238568 | tf_op jit(solution)/shard_map/ppermute | solution.py:85
  57.8 3.1 %collective-permute-done.13 = bf16[2,284,70]{1,0,2:T(2,128)(2,1)S(1)} collective-permute-done((bf16[2,284,70]{1,0,2:T(2,128)(2,1)S(1)}, bf16[2,284,70]{1,0,2:T(2,128)(2,1)S(1)}, u32[]{:S(2)}, u32[]{:S(2)}) %collective-permute-start.13) | collective-permute-done | bytes 79552 | tf_op jit(solution)/shard_map/ppermute | solution.py:85
  61.7 2.7 %collective-permute-start.14 = (bf16[2,284,70]{1,2,0:T(8,128)(2,1)S(1)}, bf16[2,284,70]{1,2,0:T(8,128)(2,1)S(1)}, u32[]{:S(2)}, u32[]{:S(2)}) collective-permute-start(bf16[2,284,70]{1,2,0:T(8,128)(2,1)S(1)} %concatenate.64), channel_id=1, source_target_pairs={{0,8},{1,9},{2,10},{3,11},{4,12},{5,13},{6,14},{7,15},{8,0},{9,1},... | collective-permute-start | bytes 238568 | tf_op jit(solution)/shard_map/ppermute | solution.py:85
  64.3 4.2 %collective-permute-done.14 = bf16[2,284,70]{1,2,0:T(8,128)(2,1)S(1)} collective-permute-done((bf16[2,284,70]{1,2,0:T(8,128)(2,1)S(1)}, bf16[2,284,70]{1,2,0:T(8,128)(2,1)S(1)}, u32[]{:S(2)}, u32[]{:S(2)}) %collective-permute-start.14) | collective-permute-done | bytes 79552 | tf_op jit(solution)/shard_map/ppermute | solution.py:85
  69.1 0.6 collective-permute-start.15
  69.7 3.1 %collective-permute-done.15 = bf16[4,2,284]{2,0,1:T(4,128)(2,1)S(1)} collective-permute-done((bf16[4,2,284]{2,0,1:T(4,128)(2,1)S(1)}, bf16[4,2,284]{2,0,1:T(4,128)(2,1)S(1)}, u32[]{:S(2)}, u32[]{:S(2)}) %collective-permute-start.15) | collective-permute-done | bytes 4576 | tf_op jit(solution)/shard_map/ppermute | solution.py:22
  72.8 0.6 gather_fusion.2
  74.1 1.3 %collective-permute-done.16 = f32[2,2,2,4,2,284]{5,4,3,2,1,0:T(2,128)S(1)} collective-permute-done((f32[2,2,2,4,2,284]{5,4,3,2,1,0:T(2,128)S(1)}, f32[2,2,2,4,2,284]{5,4,3,2,1,0:T(2,128)S(1)}, u32[]{:S(2)}, u32[]{:S(2)}) %collective-permute-start.16) | collective-permute-done | bytes 72736 | tf_op jit(solution)/shard_map/ppermute | solution.py:57
  75.5 1.6 %collective-permute-start.17 = (f32[2,2,4,2,284]{4,3,2,1,0:T(2,128)S(1)}, f32[2,2,4,2,284]{4,3,2,1,0:T(2,128)S(1)}, u32[]{:S(2)}, u32[]{:S(2)}) collective-permute-start(f32[2,2,4,2,284]{4,3,2,1,0:T(2,128)S(1)} %fusion.34), channel_id=1, source_target_pairs={{0,2},{1,3},{2,0},{3,1},{4,6},{5,7},{6,4},{7,5},{8,10},{9,11},{10,... | collective-permute-start | bytes 109064 | tf_op jit(solution)/shard_map/ppermute | solution.py:57
  77.1 2.6 %collective-permute-done.17 = f32[2,2,4,2,284]{4,3,2,1,0:T(2,128)S(1)} collective-permute-done((f32[2,2,4,2,284]{4,3,2,1,0:T(2,128)S(1)}, f32[2,2,4,2,284]{4,3,2,1,0:T(2,128)S(1)}, u32[]{:S(2)}, u32[]{:S(2)}) %collective-permute-start.17) | collective-permute-done | bytes 36384 | tf_op jit(solution)/shard_map/ppermute | solution.py:57
  79.7 0.7 collective-permute-start.18
  80.4 3.2 %collective-permute-done.18 = f32[2,4,2,284]{3,2,1,0:T(2,128)S(1)} collective-permute-done((f32[2,4,2,284]{3,2,1,0:T(2,128)S(1)}, f32[2,4,2,284]{3,2,1,0:T(2,128)S(1)}, u32[]{:S(2)}, u32[]{:S(2)}) %collective-permute-start.18) | collective-permute-done | bytes 18208 | tf_op jit(solution)/shard_map/ppermute | solution.py:57
  83.6 2.1 %collective-permute-start.19 = (f32[4,2,284]{2,1,0:T(2,128)S(1)}, f32[4,2,284]{2,1,0:T(2,128)S(1)}, u32[]{:S(2)}, u32[]{:S(2)}) collective-permute-start(f32[4,2,284]{2,1,0:T(2,128)S(1)} %select_bitcast_fusion), channel_id=1, source_target_pairs={{0,8},{1,9},{2,10},{3,11},{4,12},{5,13},{6,14},{7,15},{8,0},{9,1},... | collective-permute-start | bytes 27272 | tf_op jit(solution)/shard_map/ppermute | solution.py:57
  85.7 2.6 %collective-permute-done.19 = f32[4,2,284]{2,1,0:T(2,128)S(1)} collective-permute-done((f32[4,2,284]{2,1,0:T(2,128)S(1)}, f32[4,2,284]{2,1,0:T(2,128)S(1)}, u32[]{:S(2)}, u32[]{:S(2)}) %collective-permute-start.19) | collective-permute-done | bytes 9120 | tf_op jit(solution)/shard_map/ppermute | solution.py:57
  88.3 3.9 %collective-permute-start.20 = (f32[4,2,284]{2,1,0:T(2,128)S(1)}, f32[4,2,284]{2,1,0:T(2,128)S(1)}, u32[]{:S(2)}, u32[]{:S(2)}) collective-permute-start(f32[4,2,284]{2,1,0:T(2,128)S(1)} %bitcast_add_fusion), channel_id=1, source_target_pairs={{0,0},{1,1},{2,2},{3,3},{4,4},{5,5},{6,6},{7,7},{8,16},{9,17},{10,... | collective-permute-start | bytes 27272 | tf_op jit(solution)/shard_map/ppermute | solution.py:253
  92.3 0.8 copy.225
  93.1 2.6 %collective-permute-done.20 = f32[4,2,284]{2,1,0:T(2,128)S(1)} collective-permute-done((f32[4,2,284]{2,1,0:T(2,128)S(1)}, f32[4,2,284]{2,1,0:T(2,128)S(1)}, u32[]{:S(2)}, u32[]{:S(2)}) %collective-permute-start.20) | collective-permute-done | bytes 9120 | tf_op jit(solution)/shard_map/ppermute | solution.py:253
  95.7 0.6 add_convert_fusion
  (160 shorter events, 12.3 us)
Async XLA Ops:
  0.6 72.7 %copy-start = (bf16[284,2272]{1,0:T(8,128)(2,1)S(1)}, bf16[284,2272]{1,0:T(8,128)(2,1)}, u32[]{:S(2)}) copy-start(bf16[284,2272]{1,0:T(8,128)(2,1)} %param.19) | copy-start | bytes 3871492
  0.6 3.9 %collective-permute-start = (bf16[4,2,284]{2,1,0:T(2,128)(2,1)}, bf16[4,2,284]{2,1,0:T(2,128)(2,1)S(1)}, u32[]{:S(2)}, u32[]{:S(2)}) collective-permute-start(bf16[4,2,284]{2,1,0:T(2,128)(2,1)} %param.11), channel_id=1, source_target_pairs={{0,16},{16,0},{1,17},{17,1},{2,18},{18,2},{3,19},{19,3},{4,20},{20... | collective-permute-start | bytes 13640 | tf_op jit(solution)/shard_map/ppermute | solution.py:22
  5.3 4.7 %collective-permute-start.1 = (bf16[2,4,2,284]{3,2,1,0:T(2,128)(2,1)S(1)}, bf16[2,4,2,284]{3,2,1,0:T(2,128)(2,1)S(1)}, u32[]{:S(2)}, u32[]{:S(2)}) collective-permute-start(bf16[2,4,2,284]{3,2,1,0:T(2,128)(2,1)S(1)} %pad_maximum_fusion.8), channel_id=1, source_target_pairs={{0,8},{1,9},{2,10},{3,11},{4,12},{5,13},{6,14},{7,15},{8,0},{9,1},... | collective-permute-start | bytes 27272 | tf_op jit(solution)/shard_map/ppermute | solution.py:22
  10.0 3.9 %collective-permute-start.2 = (bf16[2,2,4,2,284]{4,3,2,1,0:T(2,128)(2,1)S(1)}, bf16[2,2,4,2,284]{4,3,2,1,0:T(2,128)(2,1)S(1)}, u32[]{:S(2)}, u32[]{:S(2)}) collective-permute-start(bf16[2,2,4,2,284]{4,3,2,1,0:T(2,128)(2,1)S(1)} %pad_maximum_fusion.6), channel_id=1, source_target_pairs={{0,4},{1,5},{2,6},{3,7},{4,0},{5,1},{6,2},{7,3},{8,12},{9,13},{10,... | collective-permute-start | bytes 54536 | tf_op jit(solution)/shard_map/ppermute | solution.py:22
  13.9 4.2 %collective-permute-start.3 = (bf16[2,2,2,4,2,284]{5,4,3,2,1,0:T(2,128)(2,1)S(1)}, bf16[2,2,2,4,2,284]{5,4,3,2,1,0:T(2,128)(2,1)S(1)}, u32[]{:S(2)}, u32[]{:S(2)}) collective-permute-start(bf16[2,2,2,4,2,284]{5,4,3,2,1,0:T(2,128)(2,1)S(1)} %pad_maximum_fusion.3), channel_id=1, source_target_pairs={{0,2},{1,3},{2,0},{3,1},{4,6},{5,7},{6,4},{7,5},{8,10},{9,11},{10,... | collective-permute-start | bytes 109064 | tf_op jit(solution)/shard_map/ppermute | solution.py:22
  18.3 1.4 %collective-permute-start.4 = (bf16[2,2,2,2,4,2,284]{6,5,4,3,2,1,0:T(2,128)(2,1)S(1)}, bf16[2,2,2,2,4,2,284]{6,5,4,3,2,1,0:T(2,128)(2,1)S(1)}, u32[]{:S(2)}, u32[]{:S(2)}) collective-permute-start(bf16[2,2,2,2,4,2,284]{6,5,4,3,2,1,0:T(2,128)(2,1)S(1)} %pad_maximum_fusion.1), channel_id=1, source_target_pairs={{0,1},{1,0},{2,3},{3,2},{4,5},{5,4},{6,7},{7,6},{8,9},{9,8},{10,11... | collective-permute-start | bytes 218120 | tf_op jit(solution)/shard_map/ppermute | solution.py:22
  22.1 2.0 %copy-start.1 = (bf16[2272,128]{1,0:T(8,128)(2,1)S(1)}, bf16[2272,128]{1,0:T(8,128)(2,1)}, u32[]{:S(2)}) copy-start(bf16[2272,128]{1,0:T(8,128)(2,1)} %param.18) | copy-start | bytes 1744900
  24.5 9.9 %copy-start.2 = (bf16[2,512,128]{2,1,0:T(8,128)(2,1)S(1)}, bf16[2,512,128]{2,1,0:T(8,128)(2,1)}, u32[]{:S(2)}) copy-start(bf16[2,512,128]{2,1,0:T(8,128)(2,1)} %param.12) | copy-start | bytes 786436
  24.5 4.8 %collective-permute-start.5 = (f32[16,412]{1,0:T(8,128)S(1)}, f32[16,412]{1,0:T(8,128)S(1)}, u32[]{:S(2)}, u32[]{:S(2)}) collective-permute-start(f32[16,412]{1,0:T(8,128)S(1)} %pad_maximum_fusion.5), channel_id=1, source_target_pairs={{0,16},{16,0},{1,17},{17,1},{2,18},{18,2},{3,19},{19,3},{4,20},{20... | collective-permute-start | bytes 79112 | tf_op jit(solution)/shard_map/ppermute | solution.py:40
  29.8 4.5 %collective-permute-start.7 = (bf16[4,2,284]{2,1,0:T(2,128)(2,1)S(1)}, bf16[4,2,284]{2,1,0:T(2,128)(2,1)S(1)}, u32[]{:S(2)}, u32[]{:S(2)}) collective-permute-start(bf16[4,2,284]{2,1,0:T(2,128)(2,1)S(1)} %slice.429), channel_id=1, source_target_pairs={{0,8},{1,9},{2,10},{3,11},{4,12},{5,13},{6,14},{7,15},{8,0},{9,1},... | collective-permute-start | bytes 13640 | tf_op jit(solution)/shard_map/ppermute | solution.py:22
  34.5 3.8 %collective-permute-start.8 = (bf16[2,4,2,284]{3,2,1,0:T(2,128)(2,1)S(1)}, bf16[2,4,2,284]{3,2,1,0:T(2,128)(2,1)S(1)}, u32[]{:S(2)}, u32[]{:S(2)}) collective-permute-start(bf16[2,4,2,284]{3,2,1,0:T(2,128)(2,1)S(1)} %pad_maximum_fusion.9), channel_id=1, source_target_pairs={{0,4},{1,5},{2,6},{3,7},{4,0},{5,1},{6,2},{7,3},{8,12},{9,13},{10,... | collective-permute-start | bytes 27272 | tf_op jit(solution)/shard_map/ppermute | solution.py:22
  38.3 3.9 %collective-permute-start.9 = (bf16[2,2,4,2,284]{4,3,2,1,0:T(2,128)(2,1)S(1)}, bf16[2,2,4,2,284]{4,3,2,1,0:T(2,128)(2,1)S(1)}, u32[]{:S(2)}, u32[]{:S(2)}) collective-permute-start(bf16[2,2,4,2,284]{4,3,2,1,0:T(2,128)(2,1)S(1)} %pad_maximum_fusion.7), channel_id=1, source_target_pairs={{0,2},{1,3},{2,0},{3,1},{4,6},{5,7},{6,4},{7,5},{8,10},{9,11},{10,... | collective-permute-start | bytes 54536 | tf_op jit(solution)/shard_map/ppermute | solution.py:22
  42.3 1.3 %collective-permute-start.10 = (bf16[2,2,2,4,2,284]{5,4,3,2,1,0:T(2,128)(2,1)S(1)}, bf16[2,2,2,4,2,284]{5,4,3,2,1,0:T(2,128)(2,1)S(1)}, u32[]{:S(2)}, u32[]{:S(2)}) collective-permute-start(bf16[2,2,2,4,2,284]{5,4,3,2,1,0:T(2,128)(2,1)S(1)} %pad_maximum_fusion.4), channel_id=1, source_target_pairs={{0,1},{1,0},{2,3},{3,2},{4,5},{5,4},{6,7},{7,6},{8,9},{9,8},{10,11... | collective-permute-start | bytes 109064 | tf_op jit(solution)/shard_map/ppermute | solution.py:22
  47.6 1.4 %collective-permute-start.11 = (bf16[2,284,70]{1,0,2:T(2,128)(2,1)S(1)}, bf16[2,284,70]{1,0,2:T(2,128)(2,1)S(1)}, u32[]{:S(2)}, u32[]{:S(2)}) collective-permute-start(bf16[2,284,70]{1,0,2:T(2,128)(2,1)S(1)} %fusion.18), channel_id=1, source_target_pairs={{0,1},{1,0},{2,3},{3,2},{4,5},{5,4},{6,7},{7,6},{8,9},{9,8},{10,11... | collective-permute-start | bytes 238568 | tf_op jit(solution)/shard_map/ppermute | solution.py:85
  47.8 4.5 %collective-permute-start.6 = (f32[16,1136]{1,0:T(8,128)S(1)}, f32[16,1136]{1,0:T(8,128)S(1)}, u32[]{:S(2)}, u32[]{:S(2)}) collective-permute-start(f32[16,1136]{1,0:T(8,128)S(1)} %fusion.184), channel_id=1, source_target_pairs={{0,16},{16,0},{1,17},{17,1},{2,18},{18,2},{3,19},{19,3},{4,20},{20... | collective-permute-start | bytes 218120 | tf_op jit(solution)/shard_map/ppermute | solution.py:40
  49.4 6.3 %collective-permute-start.12 = (bf16[2,284,70]{1,0,2:T(2,128)(2,1)S(1)}, bf16[2,284,70]{1,0,2:T(2,128)(2,1)S(1)}, u32[]{:S(2)}, u32[]{:S(2)}) collective-permute-start(bf16[2,284,70]{1,0,2:T(2,128)(2,1)S(1)} %fusion.19), channel_id=1, source_target_pairs={{0,2},{1,3},{2,0},{3,1},{4,6},{5,7},{6,4},{7,5},{8,10},{9,11},{10,... | collective-permute-start | bytes 238568 | tf_op jit(solution)/shard_map/ppermute | solution.py:85
  56.2 4.8 %collective-permute-start.13 = (bf16[2,284,70]{1,0,2:T(2,128)(2,1)S(1)}, bf16[2,284,70]{1,0,2:T(2,128)(2,1)S(1)}, u32[]{:S(2)}, u32[]{:S(2)}) collective-permute-start(bf16[2,284,70]{1,0,2:T(2,128)(2,1)S(1)} %fusion.20), channel_id=1, source_target_pairs={{0,4},{1,5},{2,6},{3,7},{4,0},{5,1},{6,2},{7,3},{8,12},{9,13},{10,... | collective-permute-start | bytes 238568 | tf_op jit(solution)/shard_map/ppermute | solution.py:85
  61.7 6.9 %collective-permute-start.14 = (bf16[2,284,70]{1,2,0:T(8,128)(2,1)S(1)}, bf16[2,284,70]{1,2,0:T(8,128)(2,1)S(1)}, u32[]{:S(2)}, u32[]{:S(2)}) collective-permute-start(bf16[2,284,70]{1,2,0:T(8,128)(2,1)S(1)} %concatenate.64), channel_id=1, source_target_pairs={{0,8},{1,9},{2,10},{3,11},{4,12},{5,13},{6,14},{7,15},{8,0},{9,1},... | collective-permute-start | bytes 238568 | tf_op jit(solution)/shard_map/ppermute | solution.py:85
  69.1 3.6 %collective-permute-start.15 = (bf16[4,2,284]{2,0,1:T(4,128)(2,1)S(1)}, bf16[4,2,284]{2,0,1:T(4,128)(2,1)S(1)}, u32[]{:S(2)}, u32[]{:S(2)}) collective-permute-start(bf16[4,2,284]{2,0,1:T(4,128)(2,1)S(1)} %get-tuple-element.63), channel_id=1, source_target_pairs={{0,16},{16,0},{1,17},{17,1},{2,18},{18,2},{3,19},{19,3},{4,20},{20... | collective-permute-start | bytes 13640 | tf_op jit(solution)/shard_map/ppermute | solution.py:22
  73.8 21.9 %copy-start.3 = (bf16[4,2,284]{2,1,0:T(2,128)(2,1)S(1)}, bf16[4,2,284]{2,1,0:T(2,128)(2,1)}, u32[]{:S(2)}) copy-start(bf16[4,2,284]{2,1,0:T(2,128)(2,1)} %param.11) | copy-start | bytes 13636
  74.0 1.4 %collective-permute-start.16 = (f32[2,2,2,4,2,284]{5,4,3,2,1,0:T(2,128)S(1)}, f32[2,2,2,4,2,284]{5,4,3,2,1,0:T(2,128)S(1)}, u32[]{:S(2)}, u32[]{:S(2)}) collective-permute-start(f32[2,2,2,4,2,284]{5,4,3,2,1,0:T(2,128)S(1)} %fusion.17), channel_id=1, source_target_pairs={{0,1},{1,0},{2,3},{3,2},{4,5},{5,4},{6,7},{7,6},{8,9},{9,8},{10,11... | collective-permute-start | bytes 218120 | tf_op jit(solution)/shard_map/ppermute | solution.py:57
  75.5 4.2 %collective-permute-start.17 = (f32[2,2,4,2,284]{4,3,2,1,0:T(2,128)S(1)}, f32[2,2,4,2,284]{4,3,2,1,0:T(2,128)S(1)}, u32[]{:S(2)}, u32[]{:S(2)}) collective-permute-start(f32[2,2,4,2,284]{4,3,2,1,0:T(2,128)S(1)} %fusion.34), channel_id=1, source_target_pairs={{0,2},{1,3},{2,0},{3,1},{4,6},{5,7},{6,4},{7,5},{8,10},{9,11},{10,... | collective-permute-start | bytes 109064 | tf_op jit(solution)/shard_map/ppermute | solution.py:57
  79.7 3.9 %collective-permute-start.18 = (f32[2,4,2,284]{3,2,1,0:T(2,128)S(1)}, f32[2,4,2,284]{3,2,1,0:T(2,128)S(1)}, u32[]{:S(2)}, u32[]{:S(2)}) collective-permute-start(f32[2,4,2,284]{3,2,1,0:T(2,128)S(1)} %fusion.69), channel_id=1, source_target_pairs={{0,4},{1,5},{2,6},{3,7},{4,0},{5,1},{6,2},{7,3},{8,12},{9,13},{10,... | collective-permute-start | bytes 54536 | tf_op jit(solution)/shard_map/ppermute | solution.py:57
  83.6 4.7 %collective-permute-start.19 = (f32[4,2,284]{2,1,0:T(2,128)S(1)}, f32[4,2,284]{2,1,0:T(2,128)S(1)}, u32[]{:S(2)}, u32[]{:S(2)}) collective-permute-start(f32[4,2,284]{2,1,0:T(2,128)S(1)} %select_bitcast_fusion), channel_id=1, source_target_pairs={{0,8},{1,9},{2,10},{3,11},{4,12},{5,13},{6,14},{7,15},{8,0},{9,1},... | collective-permute-start | bytes 27272 | tf_op jit(solution)/shard_map/ppermute | solution.py:57
  88.3 7.4 %collective-permute-start.20 = (f32[4,2,284]{2,1,0:T(2,128)S(1)}, f32[4,2,284]{2,1,0:T(2,128)S(1)}, u32[]{:S(2)}, u32[]{:S(2)}) collective-permute-start(f32[4,2,284]{2,1,0:T(2,128)S(1)} %bitcast_add_fusion), channel_id=1, source_target_pairs={{0,0},{1,1},{2,2},{3,3},{4,4},{5,5},{6,6},{7,7},{8,16},{9,17},{10,... | collective-permute-start | bytes 27272 | tf_op jit(solution)/shard_map/ppermute | solution.py:253

commit v7 on v6

--- a/solution.py
+++ b/solution.py
@@ -13,16 +13,16 @@
     return [(index, index ^ bit) for index in range(size)]
 
 
-def gather_xor(block, axis, size, riders=None):
+def gather_xor(block, axis, size, hooks=None, carry=None):
     levels = size.bit_length() - 1
-    riders = dict(riders or {})
+    hooks = hooks or {}
     stacked = block
     for level in range(levels):
+        if level in hooks:
+            stacked, carry = lax.optimization_barrier((stacked, hooks[level](carry)))
         bit = 2 ** (levels - 1 - level)
         stacked = jnp.stack([stacked, lax.ppermute(stacked, axis, xor_pairs(size, bit))])
-        if level in riders:
-            stacked, riders[level] = lax.optimization_barrier((stacked, riders[level]))
-    return stacked.reshape((size,) + block.shape), riders
+    return stacked.reshape((size,) + block.shape), carry
 
 
 def xor_slot(offset, size):
@@ -151,9 +151,33 @@
     seq_slots = xor_slot(shard_index ^ seq_ids, seq_size)
     req_slots = xor_slot(group_index ^ req_ids, req_size)
 
+    request_ids = jnp.arange(total, dtype=jnp.int32)
+    step_offsets = jnp.arange(steps, dtype=jnp.int32)
+
+    def bookkeeping(carried):
+        placement_now, lengths_now = carried
+        own_requests = lax.dynamic_slice_in_dim(
+            placement_now, group_index * group_rows, group_rows, 0
+        )
+        own_serves = own_requests[:, None] == request_ids[None, :]
+        slot_lengths = jnp.sum(jnp.where(own_serves, lengths_now[None, :], 0), axis=1)
+        positions = slot_lengths[None, :] + step_offsets[:, None]
+        serves = placement_now[:, None] == request_ids[None, :]
+        inverse = jnp.sum(jnp.where(serves, request_ids[:, None], 0), axis=0)
+        return own_serves, positions, inverse
+
     by_request, _ = gather_xor(states, "req", req_size)
-    every, riders = gather_xor(by_request, "seq", seq_size, {0: (norm_gain, norm_bias)})
-    norm_gain, norm_bias = riders[0]
+    hooks = {1: lambda carried: carried}
+    if seq_size >= 8:
+        hooks[2] = lambda carried: carried
+        hooks[3] = lambda carried: (carried[0], bookkeeping(carried[1]))
+    every, carried = gather_xor(
+        by_request, "seq", seq_size, hooks, ((norm_gain, norm_bias), (placement, lengths))
+    )
+    (norm_gain, norm_bias), books = carried
+    if seq_size < 8:
+        books = bookkeeping(books)
+    own_serves, positions, inverse = books
     every = every.reshape((seq_size * req_size,) + every.shape[2:])
     every = jnp.take(every, seq_slots[:, None] * req_size + req_slots[None, :], axis=0, mode="clip")
     current_all = every.transpose(2, 1, 3, 0, 4).reshape(steps, total, model_width)
@@ -165,23 +189,22 @@
     first = sum_over(jnp.concatenate([part_query, part_keyval], axis=1), "req", req_size)
     part_up = jnp.dot(normed_part, w_up, preferred_element_type=jnp.float32)
     first, part_up = lax.optimization_barrier((first, part_up))
-    request_ids = jnp.arange(total, dtype=jnp.int32)
-    own_requests = lax.dynamic_slice_in_dim(placement, group_index * group_rows, group_rows, 0)
-    own_serves = own_requests[:, None] == request_ids[None, :]
-    slot_lengths = jnp.sum(jnp.where(own_serves, lengths[None, :], 0), axis=1)
-    step_offsets = jnp.arange(steps, dtype=jnp.int32)
-    positions = slot_lengths[None, :] + step_offsets[:, None]
     own_first = jnp.sum(
         jnp.where(own_serves[None, :, :, None], first.reshape(steps, 1, total, -1), 0.0), axis=2
     )
     own_query = own_first[:, :, :slice_width].astype(jnp.bfloat16)
     own_keyval = own_first[:, :, slice_width:]
-    up_part = sum_over(part_up, "req", req_size)
+
+    query_hooks = {1: lambda carried: carried}
+    if seq_size >= 4:
+        query_hooks[2] = lambda carried: (carried[0], sum_over(carried[1], "req", req_size))
+    query_all, (kv_cache, up_part) = gather_xor(
+        own_query, "seq", seq_size, query_hooks, (kv_cache, part_up)
+    )
+    if seq_size < 4:
+        up_part = sum_over(up_part, "req", req_size)
     hidden = jax.nn.gelu(up_part, approximate=False).astype(jnp.bfloat16)
     down_part = jnp.dot(hidden, w_down, preferred_element_type=jnp.float32)
-
-    query_all, riders = gather_xor(own_query, "seq", seq_size, {0: kv_cache})
-    kv_cache = riders[0]
     query_all = jnp.take(query_all, seq_slots, axis=0, mode="clip")
     query_all = query_all.transpose(1, 2, 0, 3).reshape(steps, group_rows, model_width)
     flat_positions = positions.reshape(-1)
@@ -231,8 +254,6 @@
     )
     own_mixed = lax.dynamic_slice_in_dim(mixed, shard_index * slice_width, slice_width, 2)
     every_mixed = gather_xor(own_mixed, "req", req_size)[0]
-    serves = placement[:, None] == request_ids[None, :]
-    inverse = jnp.sum(jnp.where(serves, request_ids[:, None], 0), axis=0)
     mixed_rows = xor_slot(group_index ^ (inverse // group_rows), req_size) * group_rows + (
         inverse % group_rows
     )

time: 96.7 us -> 98.7 us (1.021)
  waiting for transfers between devices: 37.5 us -> 41.7 us
  matrix products: 9.94 us -> 8.61 us
  starting transfers between devices: 29.1 us -> 27.9 us
    ppermute x4, waiting for transfers between devices: 7.96 us -> 9.69 us  [merge_over(): other = lax.ppermute(sent, axis, xor_pairs(size, bit))]
    dot_general x1, matrix products: 1.76 us -> 0.43 us  [shards(): jnp.dot(normed_part, w_query, preferred_element_type=jnp.float32)]
    ppermute x2, waiting for transfers between devices: 1.35 us -> 2.57 us  [sum_over(): value = value + lax.ppermute(value, axis, xor_pairs(size, bit))]
    ppermute x4, starting transfers between devices: 6.1 us -> 4.99 us  [merge_over(): other = lax.ppermute(sent, axis, xor_pairs(size, bit))]
    ppermute x4, starting transfers between devices: 4.49 us -> 3.43 us  [scatter_sum(): blocks = keep + lax.ppermute(send, axis, xor_pairs(size, bit))]
    ppermute x4, waiting for transfers between devices: 9.55 us -> 10.6 us  [scatter_sum(): blocks = keep + lax.ppermute(send, axis, xor_pairs(size, bit))]
    another operation x15 -> x12, other arithmetic: 2.65 us -> 2.38 us  [gather_xor(): jnp.stack([stacked, lax.ppermute(stacked, axis, xor_pairs(size, bit))])]
  transfers between devices with their start and end apart: 21 -> 21, of which waited for: 19 -> 20; matrix products, arithmetic and copies ran while one was open for 15% -> 12% of each run, Pallas kernels for 0% -> 0%
where the time goes in v7:
time: 98.7 us; the launch traced here: 98.3 us
  waiting for transfers between devices  41.7 us (42%)
  starting transfers between devices  27.9 us (28%)
  local copies, waits for them, and re-layouts  10.3 us (10%)
  matrix products  8.61 us (9%)
  other arithmetic  8.4 us (9%)
  between operations  1.42 us (1%)
    ppermute x10, waiting for transfers between devices, gather_xor(): lax.ppermute(stacked, axis, xor_pairs(size, bit))  16.8 us
    ppermute x10, starting transfers between devices, gather_xor(): lax.ppermute(stacked, axis, xor_pairs(size, bit))  13.4 us
    ppermute x4, waiting for transfers between devices, scatter_sum(): blocks = keep + lax.ppermute(send, axis, xor_pairs(size, bit))  10.6 us
    ppermute x4, waiting for transfers between devices, merge_over(): other = lax.ppermute(sent, axis, xor_pairs(size, bit))  9.69 us
    ppermute x4, starting transfers between devices, merge_over(): other = lax.ppermute(sent, axis, xor_pairs(size, bit))  4.99 us
    ppermute x1, starting transfers between devices, shards(): own_branch = lax.ppermute(reduced, ALL, routes)  4.44 us
    ppermute x4, starting transfers between devices, scatter_sum(): blocks = keep + lax.ppermute(send, axis, xor_pairs(size, bit))  3.43 us
    dot_general x1, matrix products, shards(): down_part = jnp.dot(hidden, w_down, preferred_element_type=jnp.float32)  3.38 us
  transfers between devices with their start and end apart: 21, of which 20 were waited for; matrix products, arithmetic and copies ran while one was open for 12% of the time, Pallas kernels for 0%

profile of v7, /device:TPU:2, one launch (start us, length us, event | category | flops | bytes accessed | tf_op | source)
XLA Modules:
  0.0 98.3 jit_solution(9911541106201456180)
XLA Ops:
  1.0 3.6 %collective-permute-done = bf16[4,2,284]{2,1,0:T(2,128)(2,1)S(1)} collective-permute-done((bf16[4,2,284]{2,1,0:T(2,128)(2,1)}, bf16[4,2,284]{2,1,0:T(2,128)(2,1)S(1)}, u32[]{:S(2)}, u32[]{:S(2)}) %collective-permute-start) | collective-permute-done | bytes 4576 | tf_op jit(solution)/shard_map/ppermute | solution.py:24
  4.5 0.7 pad_maximum_fusion.8
  5.3 2.7 %collective-permute-start.1 = (bf16[2,4,2,284]{3,2,1,0:T(2,128)(2,1)S(1)}, bf16[2,4,2,284]{3,2,1,0:T(2,128)(2,1)S(1)}, u32[]{:S(2)}, u32[]{:S(2)}) collective-permute-start(bf16[2,4,2,284]{3,2,1,0:T(2,128)(2,1)S(1)} %pad_maximum_fusion.8), channel_id=1, source_target_pairs={{0,8},{1,9},{2,10},{3,11},{4,12},{5,13},{6,14},{7,15},{8,0},{9,1},... | collective-permute-start | bytes 27272 | tf_op jit(solution)/shard_map/ppermute | solution.py:24
  7.9 0.7 fusion.192
  8.6 1.3 %collective-permute-done.1 = bf16[2,4,2,284]{3,2,1,0:T(2,128)(2,1)S(1)} collective-permute-done((bf16[2,4,2,284]{3,2,1,0:T(2,128)(2,1)S(1)}, bf16[2,4,2,284]{3,2,1,0:T(2,128)(2,1)S(1)}, u32[]{:S(2)}, u32[]{:S(2)}) %collective-permute-start.1) | collective-permute-done | bytes 9120 | tf_op jit(solution)/shard_map/ppermute | solution.py:24
  10.0 1.6 %collective-permute-start.2 = (bf16[2,2,4,2,284]{4,3,2,1,0:T(2,128)(2,1)S(1)}, bf16[2,2,4,2,284]{4,3,2,1,0:T(2,128)(2,1)S(1)}, u32[]{:S(2)}, u32[]{:S(2)}) collective-permute-start(bf16[2,2,4,2,284]{4,3,2,1,0:T(2,128)(2,1)S(1)} %pad_maximum_fusion.6), channel_id=1, source_target_pairs={{0,4},{1,5},{2,6},{3,7},{4,0},{5,1},{6,2},{7,3},{8,12},{9,13},{10,... | collective-permute-start | bytes 54536 | tf_op jit(solution)/shard_map/ppermute | solution.py:24
  11.6 2.2 %collective-permute-done.2 = bf16[2,2,4,2,284]{4,3,2,1,0:T(2,128)(2,1)S(1)} collective-permute-done((bf16[2,2,4,2,284]{4,3,2,1,0:T(2,128)(2,1)S(1)}, bf16[2,2,4,2,284]{4,3,2,1,0:T(2,128)(2,1)S(1)}, u32[]{:S(2)}, u32[]{:S(2)}) %collective-permute-start.2) | collective-permute-done | bytes 18208 | tf_op jit(solution)/shard_map/ppermute | solution.py:24
  13.9 0.7 dynamic_slice.9
  14.8 0.8 select_reduce_fusion.2
  15.6 1.6 %collective-permute-start.3 = (bf16[2,2,2,4,2,284]{5,4,3,2,1,0:T(2,128)(2,1)S(1)}, bf16[2,2,2,4,2,284]{5,4,3,2,1,0:T(2,128)(2,1)S(1)}, u32[]{:S(2)}, u32[]{:S(2)}) collective-permute-start(bf16[2,2,2,4,2,284]{5,4,3,2,1,0:T(2,128)(2,1)S(1)} %pad_maximum_fusion.3), channel_id=1, source_target_pairs={{0,2},{1,3},{2,0},{3,1},{4,6},{5,7},{6,4},{7,5},{8,10},{9,11},{10,... | collective-permute-start | bytes 109064 | tf_op jit(solution)/shard_map/ppermute | solution.py:24
  17.2 0.7 select_reduce_fusion.1
  17.9 1.8 %collective-permute-done.3 = bf16[2,2,2,4,2,284]{5,4,3,2,1,0:T(2,128)(2,1)S(1)} collective-permute-done((bf16[2,2,2,4,2,284]{5,4,3,2,1,0:T(2,128)(2,1)S(1)}, bf16[2,2,2,4,2,284]{5,4,3,2,1,0:T(2,128)(2,1)S(1)}, u32[]{:S(2)}, u32[]{:S(2)}) %collective-permute-start.3) | collective-permute-done | bytes 36384 | tf_op jit(solution)/shard_map/ppermute | solution.py:24
  20.0 0.8 dynamic-slice.4
  20.8 0.8 dynamic-slice.5
  22.7 1.0 %gather_fusion = bf16[32,4,2,284]{3,2,1,0:T(2,128)(2,1)S(1)} fusion(bf16[32,4,2,284]{3,2,1,0:T(2,128)(2,1)S(1)} %bitcast.294, s32[1024]{0:T(1024)S(1)} %pad_clamp_fusion.2), kind=kCustom, calls=%fused_computation | custom fusion | bytes 290944 | tf_op jit(solution)/shard_map/jit(_take)/gather | solution.py:182
  25.5 0.6 copy-done.2
  26.7 3.3 %fusion.182 = f32[16,1136]{1,0:T(8,128)S(1)} fusion(bf16[2272,1136]{1,0:T(8,128)(2,1)} %param.20, f32[16,4544]{1,0:T(8,128)S(1)} %reshape.715, s32[]{:T(128)S(6)} %select_n.311, f32[2272]{0:T(1024)S(1)} %dynamic-slice.5, f32[2272]{0:T(1024)S(1)} %dynamic-slice.4, f32[16]{0:T(128)S(1)} %rsqrt.12, f32[16]{0:T(128)S(1)} %div.131), kind=kOutput, calls=%fused_computation.404 | convolution fusion | flops 82773504 | bytes 5407748 | tf_op jit(solution)/shard_map/dot_general | solution.py:190
  30.9 2.6 %collective-permute-start.6 = (bf16[4,2,284]{2,1,0:T(2,128)(2,1)S(1)}, bf16[4,2,284]{2,1,0:T(2,128)(2,1)S(1)}, u32[]{:S(2)}, u32[]{:S(2)}) collective-permute-start(bf16[4,2,284]{2,1,0:T(2,128)(2,1)S(1)} %slice.429), channel_id=1, source_target_pairs={{0,8},{1,9},{2,10},{3,11},{4,12},{5,13},{6,14},{7,15},{8,0},{9,1},... | collective-permute-start | bytes 13640 | tf_op jit(solution)/shard_map/ppermute | solution.py:24
  33.7 1.8 %collective-permute-done.6 = bf16[4,2,284]{2,1,0:T(2,128)(2,1)S(1)} collective-permute-done((bf16[4,2,284]{2,1,0:T(2,128)(2,1)S(1)}, bf16[4,2,284]{2,1,0:T(2,128)(2,1)S(1)}, u32[]{:S(2)}, u32[]{:S(2)}) %collective-permute-start.6) | collective-permute-done | bytes 4576 | tf_op jit(solution)/shard_map/ppermute | solution.py:24
  35.5 1.6 %collective-permute-start.7 = (bf16[2,4,2,284]{3,2,1,0:T(2,128)(2,1)S(1)}, bf16[2,4,2,284]{3,2,1,0:T(2,128)(2,1)S(1)}, u32[]{:S(2)}, u32[]{:S(2)}) collective-permute-start(bf16[2,4,2,284]{3,2,1,0:T(2,128)(2,1)S(1)} %pad_maximum_fusion.9), channel_id=1, source_target_pairs={{0,4},{1,5},{2,6},{3,7},{4,0},{5,1},{6,2},{7,3},{8,12},{9,13},{10,... | collective-permute-start | bytes 27272 | tf_op jit(solution)/shard_map/ppermute | solution.py:24
  37.1 1.4 %collective-permute-start.8 = (f32[16,1136]{1,0:T(8,128)S(1)}, f32[16,1136]{1,0:T(8,128)S(1)}, u32[]{:S(2)}, u32[]{:S(2)}) collective-permute-start(f32[16,1136]{1,0:T(8,128)S(1)} %fusion.182), channel_id=1, source_target_pairs={{0,16},{16,0},{1,17},{17,1},{2,18},{18,2},{3,19},{19,3},{4,20},{20... | collective-permute-start | bytes 218120 | tf_op jit(solution)/shard_map/ppermute | solution.py:40
  38.6 0.7 collective-permute-done.7
  39.3 2.2 %collective-permute-done.8 = f32[16,1136]{1,0:T(8,128)S(1)} collective-permute-done((f32[16,1136]{1,0:T(8,128)S(1)}, f32[16,1136]{1,0:T(8,128)S(1)}, u32[]{:S(2)}, u32[]{:S(2)}) %collective-permute-start.8) | collective-permute-done | bytes 72736 | tf_op jit(solution)/shard_map/ppermute | solution.py:40
  41.6 1.6 %collective-permute-start.9 = (bf16[2,2,4,2,284]{4,3,2,1,0:T(2,128)(2,1)S(1)}, bf16[2,2,4,2,284]{4,3,2,1,0:T(2,128)(2,1)S(1)}, u32[]{:S(2)}, u32[]{:S(2)}) collective-permute-start(bf16[2,2,4,2,284]{4,3,2,1,0:T(2,128)(2,1)S(1)} %pad_maximum_fusion.7), channel_id=1, source_target_pairs={{0,2},{1,3},{2,0},{3,1},{4,6},{5,7},{6,4},{7,5},{8,10},{9,11},{10,... | collective-permute-start | bytes 54536 | tf_op jit(solution)/shard_map/ppermute | solution.py:24
  43.4 2.1 %collective-permute-done.9 = bf16[2,2,4,2,284]{4,3,2,1,0:T(2,128)(2,1)S(1)} collective-permute-done((bf16[2,2,4,2,284]{4,3,2,1,0:T(2,128)(2,1)S(1)}, bf16[2,2,4,2,284]{4,3,2,1,0:T(2,128)(2,1)S(1)}, u32[]{:S(2)}, u32[]{:S(2)}) %collective-permute-start.9) | collective-permute-done | bytes 18208 | tf_op jit(solution)/shard_map/ppermute | solution.py:24
  45.8 1.1 %collective-permute-done.10 = bf16[2,2,2,4,2,284]{5,4,3,2,1,0:T(2,128)(2,1)S(1)} collective-permute-done((bf16[2,2,2,4,2,284]{5,4,3,2,1,0:T(2,128)(2,1)S(1)}, bf16[2,2,2,4,2,284]{5,4,3,2,1,0:T(2,128)(2,1)S(1)}, u32[]{:S(2)}, u32[]{:S(2)}) %collective-permute-start.10) | collective-permute-done | bytes 36384 | tf_op jit(solution)/shard_map/ppermute | solution.py:24
  47.1 0.6 gather_fusion.1
  49.3 0.5 fusion
  51.1 1.2 %collective-permute-done.11 = bf16[2,284,70]{1,0,2:T(2,128)(2,1)S(1)} collective-permute-done((bf16[2,284,70]{1,0,2:T(2,128)(2,1)S(1)}, bf16[2,284,70]{1,0,2:T(2,128)(2,1)S(1)}, u32[]{:S(2)}, u32[]{:S(2)}) %collective-permute-start.11) | collective-permute-done | bytes 79552 | tf_op jit(solution)/shard_map/ppermute | solution.py:85
  52.7 1.6 %collective-permute-start.12 = (bf16[2,284,70]{1,0,2:T(2,128)(2,1)S(1)}, bf16[2,284,70]{1,0,2:T(2,128)(2,1)S(1)}, u32[]{:S(2)}, u32[]{:S(2)}) collective-permute-start(bf16[2,284,70]{1,0,2:T(2,128)(2,1)S(1)} %fusion.19), channel_id=1, source_target_pairs={{0,2},{1,3},{2,0},{3,1},{4,6},{5,7},{6,4},{7,5},{8,10},{9,11},{10,... | collective-permute-start | bytes 238568 | tf_op jit(solution)/shard_map/ppermute | solution.py:85
  54.3 3.4 %fusion.37 = f32[16,2272]{1,0:T(8,128)S(1)} fusion(bf16[1136,2272]{1,0:T(8,128)(2,1)} %param.21, f32[16,1136]{1,0:T(8,128)S(1)} %add.459), kind=kOutput, calls=%fused_computation.97 | convolution fusion | flops 83773184 | bytes 5380096 | tf_op jit(solution)/shard_map/dot_general | solution.py:207
  58.3 0.5 collective-permute-start.13
  58.8 4.3 %collective-permute-done.13 = bf16[2,284,70]{1,0,2:T(2,128)(2,1)S(1)} collective-permute-done((bf16[2,284,70]{1,0,2:T(2,128)(2,1)S(1)}, bf16[2,284,70]{1,0,2:T(2,128)(2,1)S(1)}, u32[]{:S(2)}, u32[]{:S(2)}) %collective-permute-start.13) | collective-permute-done | bytes 79552 | tf_op jit(solution)/shard_map/ppermute | solution.py:85
  63.8 2.7 %collective-permute-start.14 = (bf16[2,284,70]{1,2,0:T(8,128)(2,1)S(1)}, bf16[2,284,70]{1,2,0:T(8,128)(2,1)S(1)}, u32[]{:S(2)}, u32[]{:S(2)}) collective-permute-start(bf16[2,284,70]{1,2,0:T(8,128)(2,1)S(1)} %concatenate.64), channel_id=1, source_target_pairs={{0,8},{1,9},{2,10},{3,11},{4,12},{5,13},{6,14},{7,15},{8,0},{9,1},... | collective-permute-start | bytes 238568 | tf_op jit(solution)/shard_map/ppermute | solution.py:85
  66.4 4.1 %collective-permute-done.14 = bf16[2,284,70]{1,2,0:T(8,128)(2,1)S(1)} collective-permute-done((bf16[2,284,70]{1,2,0:T(8,128)(2,1)S(1)}, bf16[2,284,70]{1,2,0:T(8,128)(2,1)S(1)}, u32[]{:S(2)}, u32[]{:S(2)}) %collective-permute-start.14) | collective-permute-done | bytes 79552 | tf_op jit(solution)/shard_map/ppermute | solution.py:85
  71.1 1.5 %collective-permute-start.15 = (bf16[4,2,284]{2,0,1:T(4,128)(2,1)S(1)}, bf16[4,2,284]{2,0,1:T(4,128)(2,1)S(1)}, u32[]{:S(2)}, u32[]{:S(2)}) collective-permute-start(bf16[4,2,284]{2,0,1:T(4,128)(2,1)S(1)} %get-tuple-element.97), channel_id=1, source_target_pairs={{0,16},{16,0},{1,17},{17,1},{2,18},{18,2},{3,19},{19,3},{4,20},{20... | collective-permute-start | bytes 13640 | tf_op jit(solution)/shard_map/ppermute | solution.py:24
  72.5 2.2 %collective-permute-done.15 = bf16[4,2,284]{2,0,1:T(4,128)(2,1)S(1)} collective-permute-done((bf16[4,2,284]{2,0,1:T(4,128)(2,1)S(1)}, bf16[4,2,284]{2,0,1:T(4,128)(2,1)S(1)}, u32[]{:S(2)}, u32[]{:S(2)}) %collective-permute-start.15) | collective-permute-done | bytes 4576 | tf_op jit(solution)/shard_map/ppermute | solution.py:24
  74.7 0.6 gather_fusion.2
  76.1 1.3 %collective-permute-done.16 = f32[2,2,2,4,2,284]{5,4,3,2,1,0:T(2,128)S(1)} collective-permute-done((f32[2,2,2,4,2,284]{5,4,3,2,1,0:T(2,128)S(1)}, f32[2,2,2,4,2,284]{5,4,3,2,1,0:T(2,128)S(1)}, u32[]{:S(2)}, u32[]{:S(2)}) %collective-permute-start.16) | collective-permute-done | bytes 72736 | tf_op jit(solution)/shard_map/ppermute | solution.py:57
  77.5 1.6 %collective-permute-start.17 = (f32[2,2,4,2,284]{4,3,2,1,0:T(2,128)S(1)}, f32[2,2,4,2,284]{4,3,2,1,0:T(2,128)S(1)}, u32[]{:S(2)}, u32[]{:S(2)}) collective-permute-start(f32[2,2,4,2,284]{4,3,2,1,0:T(2,128)S(1)} %fusion.34), channel_id=1, source_target_pairs={{0,2},{1,3},{2,0},{3,1},{4,6},{5,7},{6,4},{7,5},{8,10},{9,11},{10,... | collective-permute-start | bytes 109064 | tf_op jit(solution)/shard_map/ppermute | solution.py:57
  79.1 2.6 %collective-permute-done.17 = f32[2,2,4,2,284]{4,3,2,1,0:T(2,128)S(1)} collective-permute-done((f32[2,2,4,2,284]{4,3,2,1,0:T(2,128)S(1)}, f32[2,2,4,2,284]{4,3,2,1,0:T(2,128)S(1)}, u32[]{:S(2)}, u32[]{:S(2)}) %collective-permute-start.17) | collective-permute-done | bytes 36384 | tf_op jit(solution)/shard_map/ppermute | solution.py:57
  81.8 3.8 %collective-permute-done.18 = f32[2,4,2,284]{3,2,1,0:T(2,128)S(1)} collective-permute-done((f32[2,4,2,284]{3,2,1,0:T(2,128)S(1)}, f32[2,4,2,284]{3,2,1,0:T(2,128)S(1)}, u32[]{:S(2)}, u32[]{:S(2)}) %collective-permute-start.18) | collective-permute-done | bytes 18208 | tf_op jit(solution)/shard_map/ppermute | solution.py:57
  85.6 1.7 %collective-permute-start.19 = (f32[4,2,284]{2,1,0:T(2,128)S(1)}, f32[4,2,284]{2,1,0:T(2,128)S(1)}, u32[]{:S(2)}, u32[]{:S(2)}) collective-permute-start(f32[4,2,284]{2,1,0:T(2,128)S(1)} %select_bitcast_fusion), channel_id=1, source_target_pairs={{0,8},{1,9},{2,10},{3,11},{4,12},{5,13},{6,14},{7,15},{8,0},{9,1},... | collective-permute-start | bytes 27272 | tf_op jit(solution)/shard_map/ppermute | solution.py:57
  87.3 3.0 %collective-permute-done.19 = f32[4,2,284]{2,1,0:T(2,128)S(1)} collective-permute-done((f32[4,2,284]{2,1,0:T(2,128)S(1)}, f32[4,2,284]{2,1,0:T(2,128)S(1)}, u32[]{:S(2)}, u32[]{:S(2)}) %collective-permute-start.19) | collective-permute-done | bytes 9120 | tf_op jit(solution)/shard_map/ppermute | solution.py:57
  90.3 4.4 %collective-permute-start.20 = (f32[4,2,284]{2,1,0:T(2,128)S(1)}, f32[4,2,284]{2,1,0:T(2,128)S(1)}, u32[]{:S(2)}, u32[]{:S(2)}) collective-permute-start(f32[4,2,284]{2,1,0:T(2,128)S(1)} %bitcast_add_fusion), channel_id=1, source_target_pairs={{0,0},{1,1},{2,2},{3,3},{4,4},{5,5},{6,6},{7,7},{8,16},{9,17},{10,... | collective-permute-start | bytes 27272 | tf_op jit(solution)/shard_map/ppermute | solution.py:274
  94.8 0.8 copy.231
  95.6 2.1 %collective-permute-done.20 = f32[4,2,284]{2,1,0:T(2,128)S(1)} collective-permute-done((f32[4,2,284]{2,1,0:T(2,128)S(1)}, f32[4,2,284]{2,1,0:T(2,128)S(1)}, u32[]{:S(2)}, u32[]{:S(2)}) %collective-permute-start.20) | collective-permute-done | bytes 9120 | tf_op jit(solution)/shard_map/ppermute | solution.py:274
  97.7 0.6 add_convert_fusion
  (161 shorter events, 11.8 us)
Async XLA Ops:
  0.6 74.7 %copy-start = (bf16[284,2272]{1,0:T(8,128)(2,1)S(1)}, bf16[284,2272]{1,0:T(8,128)(2,1)}, u32[]{:S(2)}) copy-start(bf16[284,2272]{1,0:T(8,128)(2,1)} %param.19) | copy-start | bytes 3871492
  0.6 3.9 %collective-permute-start = (bf16[4,2,284]{2,1,0:T(2,128)(2,1)}, bf16[4,2,284]{2,1,0:T(2,128)(2,1)S(1)}, u32[]{:S(2)}, u32[]{:S(2)}) collective-permute-start(bf16[4,2,284]{2,1,0:T(2,128)(2,1)} %param.11), channel_id=1, source_target_pairs={{0,16},{16,0},{1,17},{17,1},{2,18},{18,2},{3,19},{19,3},{4,20},{20... | collective-permute-start | bytes 13640 | tf_op jit(solution)/shard_map/ppermute | solution.py:24
  5.3 4.7 %collective-permute-start.1 = (bf16[2,4,2,284]{3,2,1,0:T(2,128)(2,1)S(1)}, bf16[2,4,2,284]{3,2,1,0:T(2,128)(2,1)S(1)}, u32[]{:S(2)}, u32[]{:S(2)}) collective-permute-start(bf16[2,4,2,284]{3,2,1,0:T(2,128)(2,1)S(1)} %pad_maximum_fusion.8), channel_id=1, source_target_pairs={{0,8},{1,9},{2,10},{3,11},{4,12},{5,13},{6,14},{7,15},{8,0},{9,1},... | collective-permute-start | bytes 27272 | tf_op jit(solution)/shard_map/ppermute | solution.py:24
  10.0 3.9 %collective-permute-start.2 = (bf16[2,2,4,2,284]{4,3,2,1,0:T(2,128)(2,1)S(1)}, bf16[2,2,4,2,284]{4,3,2,1,0:T(2,128)(2,1)S(1)}, u32[]{:S(2)}, u32[]{:S(2)}) collective-permute-start(bf16[2,2,4,2,284]{4,3,2,1,0:T(2,128)(2,1)S(1)} %pad_maximum_fusion.6), channel_id=1, source_target_pairs={{0,4},{1,5},{2,6},{3,7},{4,0},{5,1},{6,2},{7,3},{8,12},{9,13},{10,... | collective-permute-start | bytes 54536 | tf_op jit(solution)/shard_map/ppermute | solution.py:24
  15.6 4.2 %collective-permute-start.3 = (bf16[2,2,2,4,2,284]{5,4,3,2,1,0:T(2,128)(2,1)S(1)}, bf16[2,2,2,4,2,284]{5,4,3,2,1,0:T(2,128)(2,1)S(1)}, u32[]{:S(2)}, u32[]{:S(2)}) collective-permute-start(bf16[2,2,2,4,2,284]{5,4,3,2,1,0:T(2,128)(2,1)S(1)} %pad_maximum_fusion.3), channel_id=1, source_target_pairs={{0,2},{1,3},{2,0},{3,1},{4,6},{5,7},{6,4},{7,5},{8,10},{9,11},{10,... | collective-permute-start | bytes 109064 | tf_op jit(solution)/shard_map/ppermute | solution.py:24
  19.9 2.4 %collective-permute-start.4 = (bf16[2,2,2,2,4,2,284]{6,5,4,3,2,1,0:T(2,128)(2,1)S(1)}, bf16[2,2,2,2,4,2,284]{6,5,4,3,2,1,0:T(2,128)(2,1)S(1)}, u32[]{:S(2)}, u32[]{:S(2)}) collective-permute-start(bf16[2,2,2,2,4,2,284]{6,5,4,3,2,1,0:T(2,128)(2,1)S(1)} %pad_maximum_fusion.1), channel_id=1, source_target_pairs={{0,1},{1,0},{2,3},{3,2},{4,5},{5,4},{6,7},{7,6},{8,9},{9,8},{10,11... | collective-permute-start | bytes 218120 | tf_op jit(solution)/shard_map/ppermute | solution.py:24
  23.7 1.4 %copy-start.1 = (bf16[2272,284]{0,1:T(8,128)(2,1)S(1)}, bf16[2272,284]{0,1:T(8,128)(2,1)}, u32[]{:S(2)}) copy-start(bf16[2272,284]{0,1:T(8,128)(2,1)} %param.17) | copy-start | bytes 3871492
  25.1 1.1 %copy-start.2 = (bf16[2272,128]{1,0:T(8,128)(2,1)S(1)}, bf16[2272,128]{1,0:T(8,128)(2,1)}, u32[]{:S(2)}) copy-start(bf16[2272,128]{1,0:T(8,128)(2,1)} %param.18) | copy-start | bytes 1744900
  26.5 15.0 %copy-start.3 = (bf16[2,512,128]{2,1,0:T(8,128)(2,1)S(1)}, bf16[2,512,128]{2,1,0:T(8,128)(2,1)}, u32[]{:S(2)}) copy-start(bf16[2,512,128]{2,1,0:T(8,128)(2,1)} %param.12) | copy-start | bytes 786436
  26.5 3.9 %collective-permute-start.5 = (f32[16,412]{1,0:T(8,128)S(1)}, f32[16,412]{1,0:T(8,128)S(1)}, u32[]{:S(2)}, u32[]{:S(2)}) collective-permute-start(f32[16,412]{1,0:T(8,128)S(1)} %pad_maximum_fusion.5), channel_id=1, source_target_pairs={{0,16},{16,0},{1,17},{17,1},{2,18},{18,2},{3,19},{19,3},{4,20},{20... | collective-permute-start | bytes 79112 | tf_op jit(solution)/shard_map/ppermute | solution.py:40
  30.9 4.5 %collective-permute-start.6 = (bf16[4,2,284]{2,1,0:T(2,128)(2,1)S(1)}, bf16[4,2,284]{2,1,0:T(2,128)(2,1)S(1)}, u32[]{:S(2)}, u32[]{:S(2)}) collective-permute-start(bf16[4,2,284]{2,1,0:T(2,128)(2,1)S(1)} %slice.429), channel_id=1, source_target_pairs={{0,8},{1,9},{2,10},{3,11},{4,12},{5,13},{6,14},{7,15},{8,0},{9,1},... | collective-permute-start | bytes 13640 | tf_op jit(solution)/shard_map/ppermute | solution.py:24
  35.5 3.8 %collective-permute-start.7 = (bf16[2,4,2,284]{3,2,1,0:T(2,128)(2,1)S(1)}, bf16[2,4,2,284]{3,2,1,0:T(2,128)(2,1)S(1)}, u32[]{:S(2)}, u32[]{:S(2)}) collective-permute-start(bf16[2,4,2,284]{3,2,1,0:T(2,128)(2,1)S(1)} %pad_maximum_fusion.9), channel_id=1, source_target_pairs={{0,4},{1,5},{2,6},{3,7},{4,0},{5,1},{6,2},{7,3},{8,12},{9,13},{10,... | collective-permute-start | bytes 27272 | tf_op jit(solution)/shard_map/ppermute | solution.py:24
  37.1 4.4 %collective-permute-start.8 = (f32[16,1136]{1,0:T(8,128)S(1)}, f32[16,1136]{1,0:T(8,128)S(1)}, u32[]{:S(2)}, u32[]{:S(2)}) collective-permute-start(f32[16,1136]{1,0:T(8,128)S(1)} %fusion.182), channel_id=1, source_target_pairs={{0,16},{16,0},{1,17},{17,1},{2,18},{18,2},{3,19},{19,3},{4,20},{20... | collective-permute-start | bytes 218120 | tf_op jit(solution)/shard_map/ppermute | solution.py:40
  41.6 3.9 %collective-permute-start.9 = (bf16[2,2,4,2,284]{4,3,2,1,0:T(2,128)(2,1)S(1)}, bf16[2,2,4,2,284]{4,3,2,1,0:T(2,128)(2,1)S(1)}, u32[]{:S(2)}, u32[]{:S(2)}) collective-permute-start(bf16[2,2,4,2,284]{4,3,2,1,0:T(2,128)(2,1)S(1)} %pad_maximum_fusion.7), channel_id=1, source_target_pairs={{0,2},{1,3},{2,0},{3,1},{4,6},{5,7},{6,4},{7,5},{8,10},{9,11},{10,... | collective-permute-start | bytes 54536 | tf_op jit(solution)/shard_map/ppermute | solution.py:24
  45.6 1.3 %collective-permute-start.10 = (bf16[2,2,2,4,2,284]{5,4,3,2,1,0:T(2,128)(2,1)S(1)}, bf16[2,2,2,4,2,284]{5,4,3,2,1,0:T(2,128)(2,1)S(1)}, u32[]{:S(2)}, u32[]{:S(2)}) collective-permute-start(bf16[2,2,2,4,2,284]{5,4,3,2,1,0:T(2,128)(2,1)S(1)} %pad_maximum_fusion.4), channel_id=1, source_target_pairs={{0,1},{1,0},{2,3},{3,2},{4,5},{5,4},{6,7},{7,6},{8,9},{9,8},{10,11... | collective-permute-start | bytes 109064 | tf_op jit(solution)/shard_map/ppermute | solution.py:24
  50.9 1.4 %collective-permute-start.11 = (bf16[2,284,70]{1,0,2:T(2,128)(2,1)S(1)}, bf16[2,284,70]{1,0,2:T(2,128)(2,1)S(1)}, u32[]{:S(2)}, u32[]{:S(2)}) collective-permute-start(bf16[2,284,70]{1,0,2:T(2,128)(2,1)S(1)} %fusion.18), channel_id=1, source_target_pairs={{0,1},{1,0},{2,3},{3,2},{4,5},{5,4},{6,7},{7,6},{8,9},{9,8},{10,11... | collective-permute-start | bytes 238568 | tf_op jit(solution)/shard_map/ppermute | solution.py:85
  52.7 5.1 %collective-permute-start.12 = (bf16[2,284,70]{1,0,2:T(2,128)(2,1)S(1)}, bf16[2,284,70]{1,0,2:T(2,128)(2,1)S(1)}, u32[]{:S(2)}, u32[]{:S(2)}) collective-permute-start(bf16[2,284,70]{1,0,2:T(2,128)(2,1)S(1)} %fusion.19), channel_id=1, source_target_pairs={{0,2},{1,3},{2,0},{3,1},{4,6},{5,7},{6,4},{7,5},{8,10},{9,11},{10,... | collective-permute-start | bytes 238568 | tf_op jit(solution)/shard_map/ppermute | solution.py:85
  58.3 4.8 %collective-permute-start.13 = (bf16[2,284,70]{1,0,2:T(2,128)(2,1)S(1)}, bf16[2,284,70]{1,0,2:T(2,128)(2,1)S(1)}, u32[]{:S(2)}, u32[]{:S(2)}) collective-permute-start(bf16[2,284,70]{1,0,2:T(2,128)(2,1)S(1)} %fusion.20), channel_id=1, source_target_pairs={{0,4},{1,5},{2,6},{3,7},{4,0},{5,1},{6,2},{7,3},{8,12},{9,13},{10,... | collective-permute-start | bytes 238568 | tf_op jit(solution)/shard_map/ppermute | solution.py:85
  63.8 6.8 %collective-permute-start.14 = (bf16[2,284,70]{1,2,0:T(8,128)(2,1)S(1)}, bf16[2,284,70]{1,2,0:T(8,128)(2,1)S(1)}, u32[]{:S(2)}, u32[]{:S(2)}) collective-permute-start(bf16[2,284,70]{1,2,0:T(8,128)(2,1)S(1)} %concatenate.64), channel_id=1, source_target_pairs={{0,8},{1,9},{2,10},{3,11},{4,12},{5,13},{6,14},{7,15},{8,0},{9,1},... | collective-permute-start | bytes 238568 | tf_op jit(solution)/shard_map/ppermute | solution.py:85
  71.1 3.6 %collective-permute-start.15 = (bf16[4,2,284]{2,0,1:T(4,128)(2,1)S(1)}, bf16[4,2,284]{2,0,1:T(4,128)(2,1)S(1)}, u32[]{:S(2)}, u32[]{:S(2)}) collective-permute-start(bf16[4,2,284]{2,0,1:T(4,128)(2,1)S(1)} %get-tuple-element.97), channel_id=1, source_target_pairs={{0,16},{16,0},{1,17},{17,1},{2,18},{18,2},{3,19},{19,3},{4,20},{20... | collective-permute-start | bytes 13640 | tf_op jit(solution)/shard_map/ppermute | solution.py:24
  75.8 21.9 %copy-start.4 = (bf16[4,2,284]{2,1,0:T(2,128)(2,1)S(1)}, bf16[4,2,284]{2,1,0:T(2,128)(2,1)}, u32[]{:S(2)}) copy-start(bf16[4,2,284]{2,1,0:T(2,128)(2,1)} %param.11) | copy-start | bytes 13636
  76.0 1.4 %collective-permute-start.16 = (f32[2,2,2,4,2,284]{5,4,3,2,1,0:T(2,128)S(1)}, f32[2,2,2,4,2,284]{5,4,3,2,1,0:T(2,128)S(1)}, u32[]{:S(2)}, u32[]{:S(2)}) collective-permute-start(f32[2,2,2,4,2,284]{5,4,3,2,1,0:T(2,128)S(1)} %fusion.17), channel_id=1, source_target_pairs={{0,1},{1,0},{2,3},{3,2},{4,5},{5,4},{6,7},{7,6},{8,9},{9,8},{10,11... | collective-permute-start | bytes 218120 | tf_op jit(solution)/shard_map/ppermute | solution.py:57
  77.5 4.2 %collective-permute-start.17 = (f32[2,2,4,2,284]{4,3,2,1,0:T(2,128)S(1)}, f32[2,2,4,2,284]{4,3,2,1,0:T(2,128)S(1)}, u32[]{:S(2)}, u32[]{:S(2)}) collective-permute-start(f32[2,2,4,2,284]{4,3,2,1,0:T(2,128)S(1)} %fusion.34), channel_id=1, source_target_pairs={{0,2},{1,3},{2,0},{3,1},{4,6},{5,7},{6,4},{7,5},{8,10},{9,11},{10,... | collective-permute-start | bytes 109064 | tf_op jit(solution)/shard_map/ppermute | solution.py:57
  81.7 3.9 %collective-permute-start.18 = (f32[2,4,2,284]{3,2,1,0:T(2,128)S(1)}, f32[2,4,2,284]{3,2,1,0:T(2,128)S(1)}, u32[]{:S(2)}, u32[]{:S(2)}) collective-permute-start(f32[2,4,2,284]{3,2,1,0:T(2,128)S(1)} %fusion.69), channel_id=1, source_target_pairs={{0,4},{1,5},{2,6},{3,7},{4,0},{5,1},{6,2},{7,3},{8,12},{9,13},{10,... | collective-permute-start | bytes 54536 | tf_op jit(solution)/shard_map/ppermute | solution.py:57
  85.6 4.7 %collective-permute-start.19 = (f32[4,2,284]{2,1,0:T(2,128)S(1)}, f32[4,2,284]{2,1,0:T(2,128)S(1)}, u32[]{:S(2)}, u32[]{:S(2)}) collective-permute-start(f32[4,2,284]{2,1,0:T(2,128)S(1)} %select_bitcast_fusion), channel_id=1, source_target_pairs={{0,8},{1,9},{2,10},{3,11},{4,12},{5,13},{6,14},{7,15},{8,0},{9,1},... | collective-permute-start | bytes 27272 | tf_op jit(solution)/shard_map/ppermute | solution.py:57
  90.3 7.4 %collective-permute-start.20 = (f32[4,2,284]{2,1,0:T(2,128)S(1)}, f32[4,2,284]{2,1,0:T(2,128)S(1)}, u32[]{:S(2)}, u32[]{:S(2)}) collective-permute-start(f32[4,2,284]{2,1,0:T(2,128)S(1)} %bitcast_add_fusion), channel_id=1, source_target_pairs={{0,0},{1,1},{2,2},{3,3},{4,4},{5,5},{6,6},{7,7},{8,16},{9,17},{10,... | collective-permute-start | bytes 27272 | tf_op jit(solution)/shard_map/ppermute | solution.py:274

commit v8 on v6

--- a/solution.py
+++ b/solution.py
@@ -71,29 +71,59 @@
     return (pieces[..., 0] + pieces[..., 1]) + pieces[..., 2]
 
 
-def merge_over(peak, total, weighted, axis, size, carried):
+def pack_merge(peak, total, weighted):
+    return jnp.concatenate(
+        [jnp.stack(split_exact(peak) + split_exact(total), axis=-1), weighted.astype(jnp.bfloat16)],
+        axis=-1,
+    )
+
+
+def merge_pair(peak, total, weighted, other):
+    peak_second = join_exact(other[..., 0:3])
+    total_second = join_exact(other[..., 3:6])
+    weighted_second = other[..., 6:].astype(jnp.float32)
+    merged_peak = jnp.maximum(peak, peak_second)
+    scale_first = jnp.exp(peak - merged_peak)
+    scale_second = jnp.exp(peak_second - merged_peak)
+    total = total * scale_first + total_second * scale_second
+    weighted = weighted * scale_first[..., None] + weighted_second * scale_second[..., None]
+    return merged_peak, total, weighted
+
+
+def merge_over(peak, total, weighted, axis, size, carried, steps, chunk_width):
+    index = lax.axis_index(axis)
+    group_rows, step_heads, head_width = weighted.shape
+    head_count = step_heads // steps
+    span = min(head_count, (chunk_width + 2 * head_width - 2) // head_width)
     bit = 1
-    while bit < size:
+    while bit < size // 2:
         if bit == 4:
             carried, peak, total, weighted = lax.optimization_barrier(
                 (carried, peak, total, weighted)
             )
-        sent = jnp.concatenate(
-            [jnp.stack(split_exact(peak) + split_exact(total), axis=-1), weighted.astype(jnp.bfloat16)],
-            axis=-1,
-        )
-        other = lax.ppermute(sent, axis, xor_pairs(size, bit))
-        peak_second = join_exact(other[..., 0:3])
-        total_second = join_exact(other[..., 3:6])
-        weighted_second = other[..., 6:].astype(jnp.float32)
-        merged_peak = jnp.maximum(peak, peak_second)
-        scale_first = jnp.exp(peak - merged_peak)
-        scale_second = jnp.exp(peak_second - merged_peak)
-        total = total * scale_first + total_second * scale_second
-        weighted = weighted * scale_first[..., None] + weighted_second * scale_second[..., None]
-        peak = merged_peak
+        other = lax.ppermute(pack_merge(peak, total, weighted), axis, xor_pairs(size, bit))
+        peak, total, weighted = merge_pair(peak, total, weighted, other)
         bit *= 2
-    return peak, total, weighted, carried
+
+    def first_head(position):
+        return jnp.minimum((position * chunk_width) // head_width, head_count - span)
+
+    def window(value, start):
+        value = value.reshape((group_rows, steps, head_count) + value.shape[2:])
+        return lax.dynamic_slice_in_dim(value, start, span, 2)
+
+    partner_start = first_head(index ^ bit)
+    own_start = first_head(index)
+    sent = pack_merge(
+        window(peak, partner_start), window(total, partner_start), window(weighted, partner_start)
+    )
+    other = lax.ppermute(sent, axis, xor_pairs(size, bit))
+    _, total, weighted = merge_pair(
+        window(peak, own_start), window(total, own_start), window(weighted, own_start), other
+    )
+    mixed = (weighted / total[..., None]).reshape(group_rows, steps, span * head_width)
+    offset = index * chunk_width - own_start * head_width
+    return lax.dynamic_slice_in_dim(mixed, offset, chunk_width, 2), carried
 
 
 def layer_norm(row_block, norm_gain, norm_bias):
@@ -220,16 +250,10 @@
         "gqs,gsd->gqd", weights, value_rows, preferred_element_type=jnp.float32
     )
 
-    _, merged_total, merged_weighted, down_part = merge_over(
-        local_peak, local_total, local_weighted, "seq", seq_size, down_part
-    )
-    mixed = merged_weighted / merged_total[:, :, None]
-    mixed = (
-        mixed.reshape(group_rows, steps, model_width)
-        .transpose(1, 0, 2)
-        .astype(jnp.bfloat16)
-    )
-    own_mixed = lax.dynamic_slice_in_dim(mixed, shard_index * slice_width, slice_width, 2)
+    own_mixed, down_part = merge_over(
+        local_peak, local_total, local_weighted, "seq", seq_size, down_part, steps, slice_width
+    )
+    own_mixed = own_mixed.transpose(1, 0, 2).astype(jnp.bfloat16)
     every_mixed = gather_xor(own_mixed, "req", req_size)[0]
     serves = placement[:, None] == request_ids[None, :]
     inverse = jnp.sum(jnp.where(serves, request_ids[:, None], 0), axis=0)

time: 96.7 us -> 96.6 us (level)
  waiting for transfers between devices: 37.5 us -> 33 us
  starting transfers between devices: 29.1 us -> 31.1 us
  local copies, waits for them, and re-layouts: 9.57 us -> 11.3 us
    ppermute x4 -> x1, waiting for transfers between devices: 7.96 us -> 1.71 us  [merge_over(): other = lax.ppermute(sent, axis, xor_pairs(size, bit))]
    ppermute x0 -> x3, waiting for transfers between devices: none -> 3.76 us  [merge_over(): lax.ppermute(pack_merge(peak, total, weighted), axis, xor_pairs(size, bit))]
    ppermute x0 -> x3, starting transfers between devices: none -> 3.45 us  [merge_over(): lax.ppermute(pack_merge(peak, total, weighted), axis, xor_pairs(size, bit))]
    ppermute x4 -> x1, starting transfers between devices: 6.1 us -> 2.66 us  [merge_over(): other = lax.ppermute(sent, axis, xor_pairs(size, bit))]
    ppermute x4, starting transfers between devices: 4.49 us -> 5.95 us  [scatter_sum(): blocks = keep + lax.ppermute(send, axis, xor_pairs(size, bit))]
    ppermute x4, waiting for transfers between devices: 9.55 us -> 8.08 us  [scatter_sum(): blocks = keep + lax.ppermute(send, axis, xor_pairs(size, bit))]
where the time goes in v8:
time: 96.6 us; the launch traced here: 96.1 us
  waiting for transfers between devices  33 us (34%)
  starting transfers between devices  31.1 us (32%)
  local copies, waits for them, and re-layouts  11.3 us (12%)
  matrix products  9.94 us (10%)
  other arithmetic  9.38 us (10%)
  between operations  1.41 us (1%)
    ppermute x10, waiting for transfers between devices, gather_xor(): lax.ppermute(stacked, axis, xor_pairs(size, bit))  16 us
    ppermute x10, starting transfers between devices, gather_xor(): lax.ppermute(stacked, axis, xor_pairs(size, bit))  12.5 us
    ppermute x4, waiting for transfers between devices, scatter_sum(): blocks = keep + lax.ppermute(send, axis, xor_pairs(size, bit))  8.08 us
    ppermute x4, starting transfers between devices, scatter_sum(): blocks = keep + lax.ppermute(send, axis, xor_pairs(size, bit))  5.95 us
    ppermute x1, starting transfers between devices, shards(): own_branch = lax.ppermute(reduced, ALL, routes)  4.5 us
    ppermute x3, waiting for transfers between devices, merge_over(): lax.ppermute(pack_merge(peak, total, weighted), axis, xor_pairs(size, bit))  3.76 us
    ppermute x3, starting transfers between devices, merge_over(): lax.ppermute(pack_merge(peak, total, weighted), axis, xor_pairs(size, bit))  3.45 us
    dot_general x1, matrix products, shards(): down_part = jnp.dot(hidden, w_down, preferred_element_type=jnp.float32)  3.39 us
  transfers between devices with their start and end apart: 21, of which 19 were waited for; matrix products, arithmetic and copies ran while one was open for 15% of the time, Pallas kernels for 0%

profile of v8, /device:TPU:2, one launch (start us, length us, event | category | flops | bytes accessed | tf_op | source)
XLA Modules:
  0.0 96.1 jit_solution(10986791525077841444)
XLA Ops:
  0.8 0.8 select_reduce_fusion.1
  1.7 0.7 dynamic_slice.28
  2.5 0.8 select_reduce_fusion.2
  4.5 0.7 pad_maximum_fusion.8
  5.3 2.7 %collective-permute-start.1 = (bf16[2,4,2,284]{3,2,1,0:T(2,128)(2,1)S(1)}, bf16[2,4,2,284]{3,2,1,0:T(2,128)(2,1)S(1)}, u32[]{:S(2)}, u32[]{:S(2)}) collective-permute-start(bf16[2,4,2,284]{3,2,1,0:T(2,128)(2,1)S(1)} %pad_maximum_fusion.8), channel_id=1, source_target_pairs={{0,8},{1,9},{2,10},{3,11},{4,12},{5,13},{6,14},{7,15},{8,0},{9,1},... | collective-permute-start | bytes 27272 | tf_op jit(solution)/shard_map/ppermute | solution.py:22
  7.9 0.7 fusion.198
  8.6 1.3 %collective-permute-done.1 = bf16[2,4,2,284]{3,2,1,0:T(2,128)(2,1)S(1)} collective-permute-done((bf16[2,4,2,284]{3,2,1,0:T(2,128)(2,1)S(1)}, bf16[2,4,2,284]{3,2,1,0:T(2,128)(2,1)S(1)}, u32[]{:S(2)}, u32[]{:S(2)}) %collective-permute-start.1) | collective-permute-done | bytes 9120 | tf_op jit(solution)/shard_map/ppermute | solution.py:22
  10.0 1.6 %collective-permute-start.2 = (bf16[2,2,4,2,284]{4,3,2,1,0:T(2,128)(2,1)S(1)}, bf16[2,2,4,2,284]{4,3,2,1,0:T(2,128)(2,1)S(1)}, u32[]{:S(2)}, u32[]{:S(2)}) collective-permute-start(bf16[2,2,4,2,284]{4,3,2,1,0:T(2,128)(2,1)S(1)} %pad_maximum_fusion.6), channel_id=1, source_target_pairs={{0,4},{1,5},{2,6},{3,7},{4,0},{5,1},{6,2},{7,3},{8,12},{9,13},{10,... | collective-permute-start | bytes 54536 | tf_op jit(solution)/shard_map/ppermute | solution.py:22
  11.8 0.8 dynamic-slice
  12.5 0.8 dynamic-slice.1
  13.9 1.6 %collective-permute-start.3 = (bf16[2,2,2,4,2,284]{5,4,3,2,1,0:T(2,128)(2,1)S(1)}, bf16[2,2,2,4,2,284]{5,4,3,2,1,0:T(2,128)(2,1)S(1)}, u32[]{:S(2)}, u32[]{:S(2)}) collective-permute-start(bf16[2,2,2,4,2,284]{5,4,3,2,1,0:T(2,128)(2,1)S(1)} %pad_maximum_fusion.3), channel_id=1, source_target_pairs={{0,2},{1,3},{2,0},{3,1},{4,6},{5,7},{6,4},{7,5},{8,10},{9,11},{10,... | collective-permute-start | bytes 109064 | tf_op jit(solution)/shard_map/ppermute | solution.py:22
  15.6 2.5 %collective-permute-done.3 = bf16[2,2,2,4,2,284]{5,4,3,2,1,0:T(2,128)(2,1)S(1)} collective-permute-done((bf16[2,2,2,4,2,284]{5,4,3,2,1,0:T(2,128)(2,1)S(1)}, bf16[2,2,2,4,2,284]{5,4,3,2,1,0:T(2,128)(2,1)S(1)}, u32[]{:S(2)}, u32[]{:S(2)}) %collective-permute-start.3) | collective-permute-done | bytes 36384 | tf_op jit(solution)/shard_map/ppermute | solution.py:22
  18.5 1.1 %collective-permute-done.4 = bf16[2,2,2,2,4,2,284]{6,5,4,3,2,1,0:T(2,128)(2,1)S(1)} collective-permute-done((bf16[2,2,2,2,4,2,284]{6,5,4,3,2,1,0:T(2,128)(2,1)S(1)}, bf16[2,2,2,2,4,2,284]{6,5,4,3,2,1,0:T(2,128)(2,1)S(1)}, u32[]{:S(2)}, u32[]{:S(2)}) %collective-permute-start.4) | collective-permute-done | bytes 72736 | tf_op jit(solution)/shard_map/ppermute | solution.py:22
  19.9 1.0 %gather_fusion = bf16[32,4,2,284]{3,2,1,0:T(2,128)(2,1)S(1)} fusion(bf16[32,4,2,284]{3,2,1,0:T(2,128)(2,1)S(1)} %bitcast.296, s32[1024]{0:T(1024)S(1)} %pad_clamp_fusion.2), kind=kCustom, calls=%fused_computation | custom fusion | bytes 290944 | tf_op jit(solution)/shard_map/jit(_take)/gather | solution.py:188
  22.4 1.8 %fusion.183 = f32[16,284]{1,0:T(8,128)S(1)} fusion(bf16[2272,284]{0,1:T(8,128)(2,1)} %param.17, f32[16,4544]{1,0:T(8,128)S(1)} %reshape.868, s32[]{:T(128)S(6)} %select_n.346, f32[2272]{0:T(1024)S(1)} %dynamic-slice.1, f32[2272]{0:T(1024)S(1)} %dynamic-slice, f32[16]{0:T(128)S(1)} %rsqrt.12, f32[16]{0:T(128)S(1)} %div.145), kind=kOutput, calls=%fused_computation.403 | convolution fusion | flops 20829696 | bytes 1481732 | tf_op jit(solution)/shard_map/dot_general | solution.py:193
  24.5 1.5 %collective-permute-start.5 = (f32[16,412]{1,0:T(8,128)S(1)}, f32[16,412]{1,0:T(8,128)S(1)}, u32[]{:S(2)}, u32[]{:S(2)}) collective-permute-start(f32[16,412]{1,0:T(8,128)S(1)} %pad_maximum_fusion.5), channel_id=1, source_target_pairs={{0,16},{16,0},{1,17},{17,1},{2,18},{18,2},{3,19},{19,3},{4,20},{20... | collective-permute-start | bytes 79112 | tf_op jit(solution)/shard_map/ppermute | solution.py:40
  26.0 3.3 %fusion.185 = f32[16,1136]{1,0:T(8,128)S(1)} fusion(bf16[2272,1136]{1,0:T(8,128)(2,1)} %param.20, f32[16,4544]{1,0:T(8,128)S(1)} %reshape.868, s32[]{:T(128)S(6)} %select_n.346, f32[2272]{0:T(1024)S(1)} %dynamic-slice.1, f32[2272]{0:T(1024)S(1)} %dynamic-slice, f32[16]{0:T(128)S(1)} %rsqrt.12, f32[16]{0:T(128)S(1)} %div.145), kind=kOutput, calls=%fused_computation.404 | convolution fusion | flops 82773504 | bytes 5407748 | tf_op jit(solution)/shard_map/dot_general | solution.py:196
  29.8 2.6 %collective-permute-start.7 = (bf16[4,2,284]{2,1,0:T(2,128)(2,1)S(1)}, bf16[4,2,284]{2,1,0:T(2,128)(2,1)S(1)}, u32[]{:S(2)}, u32[]{:S(2)}) collective-permute-start(bf16[4,2,284]{2,1,0:T(2,128)(2,1)S(1)} %slice.413), channel_id=1, source_target_pairs={{0,8},{1,9},{2,10},{3,11},{4,12},{5,13},{6,14},{7,15},{8,0},{9,1},... | collective-permute-start | bytes 13640 | tf_op jit(solution)/shard_map/ppermute | solution.py:22
  32.6 1.8 %collective-permute-done.7 = bf16[4,2,284]{2,1,0:T(2,128)(2,1)S(1)} collective-permute-done((bf16[4,2,284]{2,1,0:T(2,128)(2,1)S(1)}, bf16[4,2,284]{2,1,0:T(2,128)(2,1)S(1)}, u32[]{:S(2)}, u32[]{:S(2)}) %collective-permute-start.7) | collective-permute-done | bytes 4576 | tf_op jit(solution)/shard_map/ppermute | solution.py:22
  34.5 1.6 %collective-permute-start.8 = (bf16[2,4,2,284]{3,2,1,0:T(2,128)(2,1)S(1)}, bf16[2,4,2,284]{3,2,1,0:T(2,128)(2,1)S(1)}, u32[]{:S(2)}, u32[]{:S(2)}) collective-permute-start(bf16[2,4,2,284]{3,2,1,0:T(2,128)(2,1)S(1)} %pad_maximum_fusion.9), channel_id=1, source_target_pairs={{0,4},{1,5},{2,6},{3,7},{4,0},{5,1},{6,2},{7,3},{8,12},{9,13},{10,... | collective-permute-start | bytes 27272 | tf_op jit(solution)/shard_map/ppermute | solution.py:22
  36.4 1.9 %collective-permute-done.8 = bf16[2,4,2,284]{3,2,1,0:T(2,128)(2,1)S(1)} collective-permute-done((bf16[2,4,2,284]{3,2,1,0:T(2,128)(2,1)S(1)}, bf16[2,4,2,284]{3,2,1,0:T(2,128)(2,1)S(1)}, u32[]{:S(2)}, u32[]{:S(2)}) %collective-permute-start.8) | collective-permute-done | bytes 9120 | tf_op jit(solution)/shard_map/ppermute | solution.py:22
  38.3 1.6 %collective-permute-start.9 = (bf16[2,2,4,2,284]{4,3,2,1,0:T(2,128)(2,1)S(1)}, bf16[2,2,4,2,284]{4,3,2,1,0:T(2,128)(2,1)S(1)}, u32[]{:S(2)}, u32[]{:S(2)}) collective-permute-start(bf16[2,2,4,2,284]{4,3,2,1,0:T(2,128)(2,1)S(1)} %pad_maximum_fusion.7), channel_id=1, source_target_pairs={{0,2},{1,3},{2,0},{3,1},{4,6},{5,7},{6,4},{7,5},{8,10},{9,11},{10,... | collective-permute-start | bytes 54536 | tf_op jit(solution)/shard_map/ppermute | solution.py:22
  40.0 2.3 %collective-permute-done.9 = bf16[2,2,4,2,284]{4,3,2,1,0:T(2,128)(2,1)S(1)} collective-permute-done((bf16[2,2,4,2,284]{4,3,2,1,0:T(2,128)(2,1)S(1)}, bf16[2,2,4,2,284]{4,3,2,1,0:T(2,128)(2,1)S(1)}, u32[]{:S(2)}, u32[]{:S(2)}) %collective-permute-start.9) | collective-permute-done | bytes 18208 | tf_op jit(solution)/shard_map/ppermute | solution.py:22
  42.5 1.1 %collective-permute-done.10 = bf16[2,2,2,4,2,284]{5,4,3,2,1,0:T(2,128)(2,1)S(1)} collective-permute-done((bf16[2,2,2,4,2,284]{5,4,3,2,1,0:T(2,128)(2,1)S(1)}, bf16[2,2,2,4,2,284]{5,4,3,2,1,0:T(2,128)(2,1)S(1)}, u32[]{:S(2)}, u32[]{:S(2)}) %collective-permute-start.10) | collective-permute-done | bytes 36384 | tf_op jit(solution)/shard_map/ppermute | solution.py:22
  43.8 0.6 gather_fusion.1
  48.4 0.6 collective-permute-done.11
  49.4 1.6 %collective-permute-start.12 = (bf16[2,284,70]{1,0,2:T(2,128)(2,1)S(1)}, bf16[2,284,70]{1,0,2:T(2,128)(2,1)S(1)}, u32[]{:S(2)}, u32[]{:S(2)}) collective-permute-start(bf16[2,284,70]{1,0,2:T(2,128)(2,1)S(1)} %fusion.19), channel_id=1, source_target_pairs={{0,2},{1,3},{2,0},{3,1},{4,6},{5,7},{6,4},{7,5},{8,10},{9,11},{10,... | collective-permute-start | bytes 238568 | tf_op jit(solution)/shard_map/ppermute | solution.py:104
  51.0 1.3 %collective-permute-done.6 = f32[16,1136]{1,0:T(8,128)S(1)} collective-permute-done((f32[16,1136]{1,0:T(8,128)S(1)}, f32[16,1136]{1,0:T(8,128)S(1)}, u32[]{:S(2)}, u32[]{:S(2)}) %collective-permute-start.6) | collective-permute-done | bytes 72736 | tf_op jit(solution)/shard_map/ppermute | solution.py:40
  52.3 3.4 %fusion.35 = f32[16,2272]{1,0:T(8,128)S(1)} fusion(bf16[1136,2272]{1,0:T(8,128)(2,1)} %param.21, f32[16,1136]{1,0:T(8,128)S(1)} %fusion.185, f32[16,1136]{1,0:T(8,128)S(1)} %collective-permute-done.6), kind=kOutput, calls=%fused_computation.74 | convolution fusion | flops 83791360 | bytes 5452800 | tf_op jit(solution)/shard_map/dot_general | solution.py:211
  56.1 0.6 concatenate.63
  56.7 1.6 %collective-permute-start.13 = (bf16[2,284,70]{1,2,0:T(8,128)(2,1)S(1)}, bf16[2,284,70]{1,2,0:T(8,128)(2,1)S(1)}, u32[]{:S(2)}, u32[]{:S(2)}) collective-permute-start(bf16[2,284,70]{1,2,0:T(8,128)(2,1)S(1)} %concatenate.63), channel_id=1, source_target_pairs={{0,4},{1,5},{2,6},{3,7},{4,0},{5,1},{6,2},{7,3},{8,12},{9,13},{10,... | collective-permute-start | bytes 238568 | tf_op jit(solution)/shard_map/ppermute | solution.py:104
  58.3 3.2 %collective-permute-done.13 = bf16[2,284,70]{1,2,0:T(8,128)(2,1)S(1)} collective-permute-done((bf16[2,284,70]{1,2,0:T(8,128)(2,1)S(1)}, bf16[2,284,70]{1,2,0:T(8,128)(2,1)S(1)}, u32[]{:S(2)}, u32[]{:S(2)}) %collective-permute-start.13) | collective-permute-done | bytes 79552 | tf_op jit(solution)/shard_map/ppermute | solution.py:104
  63.4 2.7 %collective-permute-start.14 = (bf16[2,4,6,70]{3,2,1,0:T(8,128)(2,1)S(1)}, bf16[2,4,6,70]{3,2,1,0:T(8,128)(2,1)S(1)}, u32[]{:S(2)}, u32[]{:S(2)}) collective-permute-start(bf16[2,4,6,70]{3,2,1,0:T(8,128)(2,1)S(1)} %concatenate.64), channel_id=1, source_target_pairs={{0,8},{1,9},{2,10},{3,11},{4,12},{5,13},{6,14},{7,15},{8,0},{9,1},... | collective-permute-start | bytes 20168 | tf_op jit(solution)/shard_map/ppermute | solution.py:120
  66.4 1.7 %collective-permute-done.14 = bf16[2,4,6,70]{3,2,1,0:T(8,128)(2,1)S(1)} collective-permute-done((bf16[2,4,6,70]{3,2,1,0:T(8,128)(2,1)S(1)}, bf16[2,4,6,70]{3,2,1,0:T(8,128)(2,1)S(1)}, u32[]{:S(2)}, u32[]{:S(2)}) %collective-permute-start.14) | collective-permute-done | bytes 6752 | tf_op jit(solution)/shard_map/ppermute | solution.py:120
  68.9 0.6 collective-permute-start.15
  69.5 3.1 %collective-permute-done.15 = bf16[4,2,284]{2,0,1:T(4,128)(2,1)S(1)} collective-permute-done((bf16[4,2,284]{2,0,1:T(4,128)(2,1)S(1)}, bf16[4,2,284]{2,0,1:T(4,128)(2,1)S(1)}, u32[]{:S(2)}, u32[]{:S(2)}) %collective-permute-start.15) | collective-permute-done | bytes 4576 | tf_op jit(solution)/shard_map/ppermute | solution.py:22
  72.6 0.6 gather_fusion.2
  73.9 1.3 %collective-permute-done.16 = f32[2,2,2,4,2,284]{5,4,3,2,1,0:T(2,128)S(1)} collective-permute-done((f32[2,2,2,4,2,284]{5,4,3,2,1,0:T(2,128)S(1)}, f32[2,2,2,4,2,284]{5,4,3,2,1,0:T(2,128)S(1)}, u32[]{:S(2)}, u32[]{:S(2)}) %collective-permute-start.16) | collective-permute-done | bytes 72736 | tf_op jit(solution)/shard_map/ppermute | solution.py:57
  75.3 1.6 %collective-permute-start.17 = (f32[2,2,4,2,284]{4,3,2,1,0:T(2,128)S(1)}, f32[2,2,4,2,284]{4,3,2,1,0:T(2,128)S(1)}, u32[]{:S(2)}, u32[]{:S(2)}) collective-permute-start(f32[2,2,4,2,284]{4,3,2,1,0:T(2,128)S(1)} %fusion.32), channel_id=1, source_target_pairs={{0,2},{1,3},{2,0},{3,1},{4,6},{5,7},{6,4},{7,5},{8,10},{9,11},{10,... | collective-permute-start | bytes 109064 | tf_op jit(solution)/shard_map/ppermute | solution.py:57
  76.9 2.6 %collective-permute-done.17 = f32[2,2,4,2,284]{4,3,2,1,0:T(2,128)S(1)} collective-permute-done((f32[2,2,4,2,284]{4,3,2,1,0:T(2,128)S(1)}, f32[2,2,4,2,284]{4,3,2,1,0:T(2,128)S(1)}, u32[]{:S(2)}, u32[]{:S(2)}) %collective-permute-start.17) | collective-permute-done | bytes 36384 | tf_op jit(solution)/shard_map/ppermute | solution.py:57
  79.5 1.6 %collective-permute-start.18 = (f32[2,4,2,284]{3,2,1,0:T(2,128)S(1)}, f32[2,4,2,284]{3,2,1,0:T(2,128)S(1)}, u32[]{:S(2)}, u32[]{:S(2)}) collective-permute-start(f32[2,4,2,284]{3,2,1,0:T(2,128)S(1)} %fusion.69), channel_id=1, source_target_pairs={{0,4},{1,5},{2,6},{3,7},{4,0},{5,1},{6,2},{7,3},{8,12},{9,13},{10,... | collective-permute-start | bytes 54536 | tf_op jit(solution)/shard_map/ppermute | solution.py:57
  81.2 2.3 %collective-permute-done.18 = f32[2,4,2,284]{3,2,1,0:T(2,128)S(1)} collective-permute-done((f32[2,4,2,284]{3,2,1,0:T(2,128)S(1)}, f32[2,4,2,284]{3,2,1,0:T(2,128)S(1)}, u32[]{:S(2)}, u32[]{:S(2)}) %collective-permute-start.18) | collective-permute-done | bytes 18208 | tf_op jit(solution)/shard_map/ppermute | solution.py:57
  83.5 2.7 %collective-permute-start.19 = (f32[4,2,284]{2,1,0:T(2,128)S(1)}, f32[4,2,284]{2,1,0:T(2,128)S(1)}, u32[]{:S(2)}, u32[]{:S(2)}) collective-permute-start(f32[4,2,284]{2,1,0:T(2,128)S(1)} %select_bitcast_fusion), channel_id=1, source_target_pairs={{0,8},{1,9},{2,10},{3,11},{4,12},{5,13},{6,14},{7,15},{8,0},{9,1},... | collective-permute-start | bytes 27272 | tf_op jit(solution)/shard_map/ppermute | solution.py:57
  86.1 2.0 %collective-permute-done.19 = f32[4,2,284]{2,1,0:T(2,128)S(1)} collective-permute-done((f32[4,2,284]{2,1,0:T(2,128)S(1)}, f32[4,2,284]{2,1,0:T(2,128)S(1)}, u32[]{:S(2)}, u32[]{:S(2)}) %collective-permute-start.19) | collective-permute-done | bytes 9120 | tf_op jit(solution)/shard_map/ppermute | solution.py:57
  88.1 4.5 %collective-permute-start.20 = (f32[4,2,284]{2,1,0:T(2,128)S(1)}, f32[4,2,284]{2,1,0:T(2,128)S(1)}, u32[]{:S(2)}, u32[]{:S(2)}) collective-permute-start(f32[4,2,284]{2,1,0:T(2,128)S(1)} %bitcast_add_fusion), channel_id=1, source_target_pairs={{0,0},{1,1},{2,2},{3,3},{4,4},{5,5},{6,6},{7,7},{8,16},{9,17},{10,... | collective-permute-start | bytes 27272 | tf_op jit(solution)/shard_map/ppermute | solution.py:277
  92.6 0.8 copy.250
  93.5 2.0 %collective-permute-done.20 = f32[4,2,284]{2,1,0:T(2,128)S(1)} collective-permute-done((f32[4,2,284]{2,1,0:T(2,128)S(1)}, f32[4,2,284]{2,1,0:T(2,128)S(1)}, u32[]{:S(2)}, u32[]{:S(2)}) %collective-permute-start.20) | collective-permute-done | bytes 9120 | tf_op jit(solution)/shard_map/ppermute | solution.py:277
  95.5 0.6 add_convert_fusion
  (170 shorter events, 14.6 us)
Async XLA Ops:
  0.6 72.6 %copy-start = (bf16[284,2272]{1,0:T(8,128)(2,1)S(1)}, bf16[284,2272]{1,0:T(8,128)(2,1)}, u32[]{:S(2)}) copy-start(bf16[284,2272]{1,0:T(8,128)(2,1)} %param.19) | copy-start | bytes 3871492
  0.6 3.9 %collective-permute-start = (bf16[4,2,284]{2,1,0:T(2,128)(2,1)}, bf16[4,2,284]{2,1,0:T(2,128)(2,1)S(1)}, u32[]{:S(2)}, u32[]{:S(2)}) collective-permute-start(bf16[4,2,284]{2,1,0:T(2,128)(2,1)} %param.11), channel_id=1, source_target_pairs={{0,16},{16,0},{1,17},{17,1},{2,18},{18,2},{3,19},{19,3},{4,20},{20... | collective-permute-start | bytes 13640 | tf_op jit(solution)/shard_map/ppermute | solution.py:22
  5.3 4.7 %collective-permute-start.1 = (bf16[2,4,2,284]{3,2,1,0:T(2,128)(2,1)S(1)}, bf16[2,4,2,284]{3,2,1,0:T(2,128)(2,1)S(1)}, u32[]{:S(2)}, u32[]{:S(2)}) collective-permute-start(bf16[2,4,2,284]{3,2,1,0:T(2,128)(2,1)S(1)} %pad_maximum_fusion.8), channel_id=1, source_target_pairs={{0,8},{1,9},{2,10},{3,11},{4,12},{5,13},{6,14},{7,15},{8,0},{9,1},... | collective-permute-start | bytes 27272 | tf_op jit(solution)/shard_map/ppermute | solution.py:22
  10.0 3.9 %collective-permute-start.2 = (bf16[2,2,4,2,284]{4,3,2,1,0:T(2,128)(2,1)S(1)}, bf16[2,2,4,2,284]{4,3,2,1,0:T(2,128)(2,1)S(1)}, u32[]{:S(2)}, u32[]{:S(2)}) collective-permute-start(bf16[2,2,4,2,284]{4,3,2,1,0:T(2,128)(2,1)S(1)} %pad_maximum_fusion.6), channel_id=1, source_target_pairs={{0,4},{1,5},{2,6},{3,7},{4,0},{5,1},{6,2},{7,3},{8,12},{9,13},{10,... | collective-permute-start | bytes 54536 | tf_op jit(solution)/shard_map/ppermute | solution.py:22
  13.9 4.2 %collective-permute-start.3 = (bf16[2,2,2,4,2,284]{5,4,3,2,1,0:T(2,128)(2,1)S(1)}, bf16[2,2,2,4,2,284]{5,4,3,2,1,0:T(2,128)(2,1)S(1)}, u32[]{:S(2)}, u32[]{:S(2)}) collective-permute-start(bf16[2,2,2,4,2,284]{5,4,3,2,1,0:T(2,128)(2,1)S(1)} %pad_maximum_fusion.3), channel_id=1, source_target_pairs={{0,2},{1,3},{2,0},{3,1},{4,6},{5,7},{6,4},{7,5},{8,10},{9,11},{10,... | collective-permute-start | bytes 109064 | tf_op jit(solution)/shard_map/ppermute | solution.py:22
  18.3 1.4 %collective-permute-start.4 = (bf16[2,2,2,2,4,2,284]{6,5,4,3,2,1,0:T(2,128)(2,1)S(1)}, bf16[2,2,2,2,4,2,284]{6,5,4,3,2,1,0:T(2,128)(2,1)S(1)}, u32[]{:S(2)}, u32[]{:S(2)}) collective-permute-start(bf16[2,2,2,2,4,2,284]{6,5,4,3,2,1,0:T(2,128)(2,1)S(1)} %pad_maximum_fusion.1), channel_id=1, source_target_pairs={{0,1},{1,0},{2,3},{3,2},{4,5},{5,4},{6,7},{7,6},{8,9},{9,8},{10,11... | collective-permute-start | bytes 218120 | tf_op jit(solution)/shard_map/ppermute | solution.py:22
  22.1 2.0 %copy-start.1 = (bf16[2272,128]{1,0:T(8,128)(2,1)S(1)}, bf16[2272,128]{1,0:T(8,128)(2,1)}, u32[]{:S(2)}) copy-start(bf16[2272,128]{1,0:T(8,128)(2,1)} %param.18) | copy-start | bytes 1744900
  24.5 9.9 %copy-start.2 = (bf16[2,512,128]{2,1,0:T(8,128)(2,1)S(1)}, bf16[2,512,128]{2,1,0:T(8,128)(2,1)}, u32[]{:S(2)}) copy-start(bf16[2,512,128]{2,1,0:T(8,128)(2,1)} %param.12) | copy-start | bytes 786436
  24.5 4.8 %collective-permute-start.5 = (f32[16,412]{1,0:T(8,128)S(1)}, f32[16,412]{1,0:T(8,128)S(1)}, u32[]{:S(2)}, u32[]{:S(2)}) collective-permute-start(f32[16,412]{1,0:T(8,128)S(1)} %pad_maximum_fusion.5), channel_id=1, source_target_pairs={{0,16},{16,0},{1,17},{17,1},{2,18},{18,2},{3,19},{19,3},{4,20},{20... | collective-permute-start | bytes 79112 | tf_op jit(solution)/shard_map/ppermute | solution.py:40
  29.8 4.5 %collective-permute-start.7 = (bf16[4,2,284]{2,1,0:T(2,128)(2,1)S(1)}, bf16[4,2,284]{2,1,0:T(2,128)(2,1)S(1)}, u32[]{:S(2)}, u32[]{:S(2)}) collective-permute-start(bf16[4,2,284]{2,1,0:T(2,128)(2,1)S(1)} %slice.413), channel_id=1, source_target_pairs={{0,8},{1,9},{2,10},{3,11},{4,12},{5,13},{6,14},{7,15},{8,0},{9,1},... | collective-permute-start | bytes 13640 | tf_op jit(solution)/shard_map/ppermute | solution.py:22
  34.5 3.8 %collective-permute-start.8 = (bf16[2,4,2,284]{3,2,1,0:T(2,128)(2,1)S(1)}, bf16[2,4,2,284]{3,2,1,0:T(2,128)(2,1)S(1)}, u32[]{:S(2)}, u32[]{:S(2)}) collective-permute-start(bf16[2,4,2,284]{3,2,1,0:T(2,128)(2,1)S(1)} %pad_maximum_fusion.9), channel_id=1, source_target_pairs={{0,4},{1,5},{2,6},{3,7},{4,0},{5,1},{6,2},{7,3},{8,12},{9,13},{10,... | collective-permute-start | bytes 27272 | tf_op jit(solution)/shard_map/ppermute | solution.py:22
  38.3 3.9 %collective-permute-start.9 = (bf16[2,2,4,2,284]{4,3,2,1,0:T(2,128)(2,1)S(1)}, bf16[2,2,4,2,284]{4,3,2,1,0:T(2,128)(2,1)S(1)}, u32[]{:S(2)}, u32[]{:S(2)}) collective-permute-start(bf16[2,2,4,2,284]{4,3,2,1,0:T(2,128)(2,1)S(1)} %pad_maximum_fusion.7), channel_id=1, source_target_pairs={{0,2},{1,3},{2,0},{3,1},{4,6},{5,7},{6,4},{7,5},{8,10},{9,11},{10,... | collective-permute-start | bytes 54536 | tf_op jit(solution)/shard_map/ppermute | solution.py:22
  42.3 1.3 %collective-permute-start.10 = (bf16[2,2,2,4,2,284]{5,4,3,2,1,0:T(2,128)(2,1)S(1)}, bf16[2,2,2,4,2,284]{5,4,3,2,1,0:T(2,128)(2,1)S(1)}, u32[]{:S(2)}, u32[]{:S(2)}) collective-permute-start(bf16[2,2,2,4,2,284]{5,4,3,2,1,0:T(2,128)(2,1)S(1)} %pad_maximum_fusion.4), channel_id=1, source_target_pairs={{0,1},{1,0},{2,3},{3,2},{4,5},{5,4},{6,7},{7,6},{8,9},{9,8},{10,11... | collective-permute-start | bytes 109064 | tf_op jit(solution)/shard_map/ppermute | solution.py:22
  47.6 1.4 %collective-permute-start.11 = (bf16[2,284,70]{1,0,2:T(2,128)(2,1)S(1)}, bf16[2,284,70]{1,0,2:T(2,128)(2,1)S(1)}, u32[]{:S(2)}, u32[]{:S(2)}) collective-permute-start(bf16[2,284,70]{1,0,2:T(2,128)(2,1)S(1)} %fusion.18), channel_id=1, source_target_pairs={{0,1},{1,0},{2,3},{3,2},{4,5},{5,4},{6,7},{7,6},{8,9},{9,8},{10,11... | collective-permute-start | bytes 238568 | tf_op jit(solution)/shard_map/ppermute | solution.py:104
  47.8 4.5 %collective-permute-start.6 = (f32[16,1136]{1,0:T(8,128)S(1)}, f32[16,1136]{1,0:T(8,128)S(1)}, u32[]{:S(2)}, u32[]{:S(2)}) collective-permute-start(f32[16,1136]{1,0:T(8,128)S(1)} %fusion.185), channel_id=1, source_target_pairs={{0,16},{16,0},{1,17},{17,1},{2,18},{18,2},{3,19},{19,3},{4,20},{20... | collective-permute-start | bytes 218120 | tf_op jit(solution)/shard_map/ppermute | solution.py:40
  49.4 6.3 %collective-permute-start.12 = (bf16[2,284,70]{1,0,2:T(2,128)(2,1)S(1)}, bf16[2,284,70]{1,0,2:T(2,128)(2,1)S(1)}, u32[]{:S(2)}, u32[]{:S(2)}) collective-permute-start(bf16[2,284,70]{1,0,2:T(2,128)(2,1)S(1)} %fusion.19), channel_id=1, source_target_pairs={{0,2},{1,3},{2,0},{3,1},{4,6},{5,7},{6,4},{7,5},{8,10},{9,11},{10,... | collective-permute-start | bytes 238568 | tf_op jit(solution)/shard_map/ppermute | solution.py:104
  56.7 4.8 %collective-permute-start.13 = (bf16[2,284,70]{1,2,0:T(8,128)(2,1)S(1)}, bf16[2,284,70]{1,2,0:T(8,128)(2,1)S(1)}, u32[]{:S(2)}, u32[]{:S(2)}) collective-permute-start(bf16[2,284,70]{1,2,0:T(8,128)(2,1)S(1)} %concatenate.63), channel_id=1, source_target_pairs={{0,4},{1,5},{2,6},{3,7},{4,0},{5,1},{6,2},{7,3},{8,12},{9,13},{10,... | collective-permute-start | bytes 238568 | tf_op jit(solution)/shard_map/ppermute | solution.py:104
  63.4 4.7 %collective-permute-start.14 = (bf16[2,4,6,70]{3,2,1,0:T(8,128)(2,1)S(1)}, bf16[2,4,6,70]{3,2,1,0:T(8,128)(2,1)S(1)}, u32[]{:S(2)}, u32[]{:S(2)}) collective-permute-start(bf16[2,4,6,70]{3,2,1,0:T(8,128)(2,1)S(1)} %concatenate.64), channel_id=1, source_target_pairs={{0,8},{1,9},{2,10},{3,11},{4,12},{5,13},{6,14},{7,15},{8,0},{9,1},... | collective-permute-start | bytes 20168 | tf_op jit(solution)/shard_map/ppermute | solution.py:120
  68.9 3.6 %collective-permute-start.15 = (bf16[4,2,284]{2,0,1:T(4,128)(2,1)S(1)}, bf16[4,2,284]{2,0,1:T(4,128)(2,1)S(1)}, u32[]{:S(2)}, u32[]{:S(2)}) collective-permute-start(bf16[4,2,284]{2,0,1:T(4,128)(2,1)S(1)} %get-tuple-element.64), channel_id=1, source_target_pairs={{0,16},{16,0},{1,17},{17,1},{2,18},{18,2},{3,19},{19,3},{4,20},{20... | collective-permute-start | bytes 13640 | tf_op jit(solution)/shard_map/ppermute | solution.py:22
  73.6 21.9 %copy-start.3 = (bf16[4,2,284]{2,1,0:T(2,128)(2,1)S(1)}, bf16[4,2,284]{2,1,0:T(2,128)(2,1)}, u32[]{:S(2)}) copy-start(bf16[4,2,284]{2,1,0:T(2,128)(2,1)} %param.11) | copy-start | bytes 13636
  73.8 1.4 %collective-permute-start.16 = (f32[2,2,2,4,2,284]{5,4,3,2,1,0:T(2,128)S(1)}, f32[2,2,2,4,2,284]{5,4,3,2,1,0:T(2,128)S(1)}, u32[]{:S(2)}, u32[]{:S(2)}) collective-permute-start(f32[2,2,2,4,2,284]{5,4,3,2,1,0:T(2,128)S(1)} %fusion.17), channel_id=1, source_target_pairs={{0,1},{1,0},{2,3},{3,2},{4,5},{5,4},{6,7},{7,6},{8,9},{9,8},{10,11... | collective-permute-start | bytes 218120 | tf_op jit(solution)/shard_map/ppermute | solution.py:57
  75.3 4.2 %collective-permute-start.17 = (f32[2,2,4,2,284]{4,3,2,1,0:T(2,128)S(1)}, f32[2,2,4,2,284]{4,3,2,1,0:T(2,128)S(1)}, u32[]{:S(2)}, u32[]{:S(2)}) collective-permute-start(f32[2,2,4,2,284]{4,3,2,1,0:T(2,128)S(1)} %fusion.32), channel_id=1, source_target_pairs={{0,2},{1,3},{2,0},{3,1},{4,6},{5,7},{6,4},{7,5},{8,10},{9,11},{10,... | collective-permute-start | bytes 109064 | tf_op jit(solution)/shard_map/ppermute | solution.py:57
  79.5 3.9 %collective-permute-start.18 = (f32[2,4,2,284]{3,2,1,0:T(2,128)S(1)}, f32[2,4,2,284]{3,2,1,0:T(2,128)S(1)}, u32[]{:S(2)}, u32[]{:S(2)}) collective-permute-start(f32[2,4,2,284]{3,2,1,0:T(2,128)S(1)} %fusion.69), channel_id=1, source_target_pairs={{0,4},{1,5},{2,6},{3,7},{4,0},{5,1},{6,2},{7,3},{8,12},{9,13},{10,... | collective-permute-start | bytes 54536 | tf_op jit(solution)/shard_map/ppermute | solution.py:57
  83.5 4.7 %collective-permute-start.19 = (f32[4,2,284]{2,1,0:T(2,128)S(1)}, f32[4,2,284]{2,1,0:T(2,128)S(1)}, u32[]{:S(2)}, u32[]{:S(2)}) collective-permute-start(f32[4,2,284]{2,1,0:T(2,128)S(1)} %select_bitcast_fusion), channel_id=1, source_target_pairs={{0,8},{1,9},{2,10},{3,11},{4,12},{5,13},{6,14},{7,15},{8,0},{9,1},... | collective-permute-start | bytes 27272 | tf_op jit(solution)/shard_map/ppermute | solution.py:57
  88.1 7.4 %collective-permute-start.20 = (f32[4,2,284]{2,1,0:T(2,128)S(1)}, f32[4,2,284]{2,1,0:T(2,128)S(1)}, u32[]{:S(2)}, u32[]{:S(2)}) collective-permute-start(f32[4,2,284]{2,1,0:T(2,128)S(1)} %bitcast_add_fusion), channel_id=1, source_target_pairs={{0,0},{1,1},{2,2},{3,3},{4,4},{5,5},{6,6},{7,7},{8,16},{9,17},{10,... | collective-permute-start | bytes 27272 | tf_op jit(solution)/shard_map/ppermute | solution.py:277

commit v9 on v8

--- a/solution.py
+++ b/solution.py
@@ -114,9 +114,7 @@
 
     partner_start = first_head(index ^ bit)
     own_start = first_head(index)
-    sent = pack_merge(
-        window(peak, partner_start), window(total, partner_start), window(weighted, partner_start)
-    )
+    sent = window(pack_merge(peak, total, weighted), partner_start)
     other = lax.ppermute(sent, axis, xor_pairs(size, bit))
     _, total, weighted = merge_pair(
         window(peak, own_start), window(total, own_start), window(weighted, own_start), other

time: 96.6 us -> 97.3 us (level)
  waiting for transfers between devices: 33 us -> 30.9 us
  starting transfers between devices: 31.1 us -> 32.7 us
  local copies, waits for them, and re-layouts: 11.3 us -> 12.4 us
    concatenate x4 -> x12, local copies, waits for them, and re-layouts: 1.07 us -> 3.2 us  [pack_merge(): jnp.concatenate([jnp.stack(split_exact(peak) + split_exact(total), axis=-...]
  transfers between devices with their start and end apart: 21 -> 21, of which waited for: 19 -> 18; matrix products, arithmetic and copies ran while one was open for 15% -> 15% of each run, Pallas kernels for 0% -> 0%
where the time goes in v9:
time: 97.3 us; the launch traced here: 95.9 us
  starting transfers between devices  32.7 us (34%)
  waiting for transfers between devices  30.9 us (32%)
  local copies, waits for them, and re-layouts  12.4 us (13%)
  matrix products  9.94 us (10%)
  other arithmetic  8.49 us (9%)
  between operations  1.52 us (2%)
    ppermute x10, waiting for transfers between devices, gather_xor(): lax.ppermute(stacked, axis, xor_pairs(size, bit))  16 us
    ppermute x10, starting transfers between devices, gather_xor(): lax.ppermute(stacked, axis, xor_pairs(size, bit))  13.3 us
    ppermute x4, waiting for transfers between devices, scatter_sum(): blocks = keep + lax.ppermute(send, axis, xor_pairs(size, bit))  8.09 us
    ppermute x4, starting transfers between devices, scatter_sum(): blocks = keep + lax.ppermute(send, axis, xor_pairs(size, bit))  5.95 us
    ppermute x1, starting transfers between devices, shards(): own_branch = lax.ppermute(reduced, ALL, routes)  5.31 us
    ppermute x3, starting transfers between devices, merge_over(): lax.ppermute(pack_merge(peak, total, weighted), axis, xor_pairs(size, bit))  3.45 us
    dot_general x1, matrix products, shards(): down_part = jnp.dot(hidden, w_down, preferred_element_type=jnp.float32)  3.39 us
    dot_general x1, matrix products, shards(): part_up = jnp.dot(normed_part, w_up, preferred_element_type=jnp.float32)  3.32 us
  transfers between devices with their start and end apart: 21, of which 18 were waited for; matrix products, arithmetic and copies ran while one was open for 15% of the time, Pallas kernels for 0%

profile of v9, /device:TPU:2, one launch (start us, length us, event | category | flops | bytes accessed | tf_op | source)
XLA Modules:
  0.0 95.9 jit_solution(4918925318099940343)
XLA Ops:
  0.8 0.8 dynamic_slice.22
  1.7 0.8 select_reduce_fusion.2
  3.3 1.3 %collective-permute-done = bf16[4,2,284]{2,1,0:T(2,128)(2,1)S(1)} collective-permute-done((bf16[4,2,284]{2,1,0:T(2,128)(2,1)}, bf16[4,2,284]{2,1,0:T(2,128)(2,1)S(1)}, u32[]{:S(2)}, u32[]{:S(2)}) %collective-permute-start) | collective-permute-done | bytes 4576 | tf_op jit(solution)/shard_map/ppermute | solution.py:22
  4.5 0.7 pad_maximum_fusion.8
  5.3 2.7 %collective-permute-start.1 = (bf16[2,4,2,284]{3,2,1,0:T(2,128)(2,1)S(1)}, bf16[2,4,2,284]{3,2,1,0:T(2,128)(2,1)S(1)}, u32[]{:S(2)}, u32[]{:S(2)}) collective-permute-start(bf16[2,4,2,284]{3,2,1,0:T(2,128)(2,1)S(1)} %pad_maximum_fusion.8), channel_id=1, source_target_pairs={{0,8},{1,9},{2,10},{3,11},{4,12},{5,13},{6,14},{7,15},{8,0},{9,1},... | collective-permute-start | bytes 27272 | tf_op jit(solution)/shard_map/ppermute | solution.py:22
  7.9 0.7 fusion.194
  8.6 1.3 %collective-permute-done.1 = bf16[2,4,2,284]{3,2,1,0:T(2,128)(2,1)S(1)} collective-permute-done((bf16[2,4,2,284]{3,2,1,0:T(2,128)(2,1)S(1)}, bf16[2,4,2,284]{3,2,1,0:T(2,128)(2,1)S(1)}, u32[]{:S(2)}, u32[]{:S(2)}) %collective-permute-start.1) | collective-permute-done | bytes 9120 | tf_op jit(solution)/shard_map/ppermute | solution.py:22
  10.0 1.6 %collective-permute-start.2 = (bf16[2,2,4,2,284]{4,3,2,1,0:T(2,128)(2,1)S(1)}, bf16[2,2,4,2,284]{4,3,2,1,0:T(2,128)(2,1)S(1)}, u32[]{:S(2)}, u32[]{:S(2)}) collective-permute-start(bf16[2,2,4,2,284]{4,3,2,1,0:T(2,128)(2,1)S(1)} %pad_maximum_fusion.6), channel_id=1, source_target_pairs={{0,4},{1,5},{2,6},{3,7},{4,0},{5,1},{6,2},{7,3},{8,12},{9,13},{10,... | collective-permute-start | bytes 54536 | tf_op jit(solution)/shard_map/ppermute | solution.py:22
  11.8 0.8 dynamic-slice
  12.6 0.8 dynamic-slice.1
  13.9 1.6 %collective-permute-start.3 = (bf16[2,2,2,4,2,284]{5,4,3,2,1,0:T(2,128)(2,1)S(1)}, bf16[2,2,2,4,2,284]{5,4,3,2,1,0:T(2,128)(2,1)S(1)}, u32[]{:S(2)}, u32[]{:S(2)}) collective-permute-start(bf16[2,2,2,4,2,284]{5,4,3,2,1,0:T(2,128)(2,1)S(1)} %pad_maximum_fusion.3), channel_id=1, source_target_pairs={{0,2},{1,3},{2,0},{3,1},{4,6},{5,7},{6,4},{7,5},{8,10},{9,11},{10,... | collective-permute-start | bytes 109064 | tf_op jit(solution)/shard_map/ppermute | solution.py:22
  15.6 2.5 %collective-permute-done.3 = bf16[2,2,2,4,2,284]{5,4,3,2,1,0:T(2,128)(2,1)S(1)} collective-permute-done((bf16[2,2,2,4,2,284]{5,4,3,2,1,0:T(2,128)(2,1)S(1)}, bf16[2,2,2,4,2,284]{5,4,3,2,1,0:T(2,128)(2,1)S(1)}, u32[]{:S(2)}, u32[]{:S(2)}) %collective-permute-start.3) | collective-permute-done | bytes 36384 | tf_op jit(solution)/shard_map/ppermute | solution.py:22
  18.5 1.1 %collective-permute-done.4 = bf16[2,2,2,2,4,2,284]{6,5,4,3,2,1,0:T(2,128)(2,1)S(1)} collective-permute-done((bf16[2,2,2,2,4,2,284]{6,5,4,3,2,1,0:T(2,128)(2,1)S(1)}, bf16[2,2,2,2,4,2,284]{6,5,4,3,2,1,0:T(2,128)(2,1)S(1)}, u32[]{:S(2)}, u32[]{:S(2)}) %collective-permute-start.4) | collective-permute-done | bytes 72736 | tf_op jit(solution)/shard_map/ppermute | solution.py:22
  19.9 1.0 %gather_fusion = bf16[32,4,2,284]{3,2,1,0:T(2,128)(2,1)S(1)} fusion(bf16[32,4,2,284]{3,2,1,0:T(2,128)(2,1)S(1)} %bitcast.287, s32[1024]{0:T(1024)S(1)} %get-tuple-element.102), kind=kCustom, calls=%fused_computation | custom fusion | bytes 290944 | tf_op jit(solution)/shard_map/jit(_take)/gather | solution.py:186
  22.4 1.8 %fusion.179 = f32[16,284]{1,0:T(8,128)S(1)} fusion(bf16[2272,284]{0,1:T(8,128)(2,1)} %param.17, f32[16,4544]{1,0:T(8,128)S(1)} %reshape.879, s32[]{:T(128)S(6)} %select_n.344, f32[2272]{0:T(1024)S(1)} %dynamic-slice.1, f32[2272]{0:T(1024)S(1)} %dynamic-slice, f32[16]{0:T(128)S(1)} %rsqrt.12, f32[16]{0:T(128)S(1)} %div.145), kind=kOutput, calls=%fused_computation.398 | convolution fusion | flops 20829696 | bytes 1481732 | tf_op jit(solution)/shard_map/dot_general | solution.py:191
  24.5 0.7 collective-permute-start.5
  25.2 3.3 %fusion.181 = f32[16,1136]{1,0:T(8,128)S(1)} fusion(bf16[2272,1136]{1,0:T(8,128)(2,1)} %param.20, f32[16,4544]{1,0:T(8,128)S(1)} %reshape.879, s32[]{:T(128)S(6)} %select_n.344, f32[2272]{0:T(1024)S(1)} %dynamic-slice.1, f32[2272]{0:T(1024)S(1)} %dynamic-slice, f32[16]{0:T(128)S(1)} %rsqrt.12, f32[16]{0:T(128)S(1)} %div.145), kind=kOutput, calls=%fused_computation.399 | convolution fusion | flops 82773504 | bytes 5407748 | tf_op jit(solution)/shard_map/dot_general | solution.py:194
  29.0 2.6 %collective-permute-start.7 = (bf16[4,2,284]{2,1,0:T(2,128)(2,1)S(1)}, bf16[4,2,284]{2,1,0:T(2,128)(2,1)S(1)}, u32[]{:S(2)}, u32[]{:S(2)}) collective-permute-start(bf16[4,2,284]{2,1,0:T(2,128)(2,1)S(1)} %slice.413), channel_id=1, source_target_pairs={{0,8},{1,9},{2,10},{3,11},{4,12},{5,13},{6,14},{7,15},{8,0},{9,1},... | collective-permute-start | bytes 13640 | tf_op jit(solution)/shard_map/ppermute | solution.py:22
  31.7 1.8 %collective-permute-done.7 = bf16[4,2,284]{2,1,0:T(2,128)(2,1)S(1)} collective-permute-done((bf16[4,2,284]{2,1,0:T(2,128)(2,1)S(1)}, bf16[4,2,284]{2,1,0:T(2,128)(2,1)S(1)}, u32[]{:S(2)}, u32[]{:S(2)}) %collective-permute-start.7) | collective-permute-done | bytes 4576 | tf_op jit(solution)/shard_map/ppermute | solution.py:22
  33.7 1.6 %collective-permute-start.8 = (bf16[2,4,2,284]{3,2,1,0:T(2,128)(2,1)S(1)}, bf16[2,4,2,284]{3,2,1,0:T(2,128)(2,1)S(1)}, u32[]{:S(2)}, u32[]{:S(2)}) collective-permute-start(bf16[2,4,2,284]{3,2,1,0:T(2,128)(2,1)S(1)} %pad_maximum_fusion.9), channel_id=1, source_target_pairs={{0,4},{1,5},{2,6},{3,7},{4,0},{5,1},{6,2},{7,3},{8,12},{9,13},{10,... | collective-permute-start | bytes 27272 | tf_op jit(solution)/shard_map/ppermute | solution.py:22
  35.6 1.9 %collective-permute-done.8 = bf16[2,4,2,284]{3,2,1,0:T(2,128)(2,1)S(1)} collective-permute-done((bf16[2,4,2,284]{3,2,1,0:T(2,128)(2,1)S(1)}, bf16[2,4,2,284]{3,2,1,0:T(2,128)(2,1)S(1)}, u32[]{:S(2)}, u32[]{:S(2)}) %collective-permute-start.8) | collective-permute-done | bytes 9120 | tf_op jit(solution)/shard_map/ppermute | solution.py:22
  37.5 1.6 %collective-permute-start.9 = (bf16[2,2,4,2,284]{4,3,2,1,0:T(2,128)(2,1)S(1)}, bf16[2,2,4,2,284]{4,3,2,1,0:T(2,128)(2,1)S(1)}, u32[]{:S(2)}, u32[]{:S(2)}) collective-permute-start(bf16[2,2,4,2,284]{4,3,2,1,0:T(2,128)(2,1)S(1)} %pad_maximum_fusion.7), channel_id=1, source_target_pairs={{0,2},{1,3},{2,0},{3,1},{4,6},{5,7},{6,4},{7,5},{8,10},{9,11},{10,... | collective-permute-start | bytes 54536 | tf_op jit(solution)/shard_map/ppermute | solution.py:22
  39.1 2.3 %collective-permute-done.9 = bf16[2,2,4,2,284]{4,3,2,1,0:T(2,128)(2,1)S(1)} collective-permute-done((bf16[2,2,4,2,284]{4,3,2,1,0:T(2,128)(2,1)S(1)}, bf16[2,2,4,2,284]{4,3,2,1,0:T(2,128)(2,1)S(1)}, u32[]{:S(2)}, u32[]{:S(2)}) %collective-permute-start.9) | collective-permute-done | bytes 18208 | tf_op jit(solution)/shard_map/ppermute | solution.py:22
  41.6 1.1 %collective-permute-done.10 = bf16[2,2,2,4,2,284]{5,4,3,2,1,0:T(2,128)(2,1)S(1)} collective-permute-done((bf16[2,2,2,4,2,284]{5,4,3,2,1,0:T(2,128)(2,1)S(1)}, bf16[2,2,2,4,2,284]{5,4,3,2,1,0:T(2,128)(2,1)S(1)}, u32[]{:S(2)}, u32[]{:S(2)}) %collective-permute-start.10) | collective-permute-done | bytes 36384 | tf_op jit(solution)/shard_map/ppermute | solution.py:22
  43.0 0.6 gather_fusion.1
  47.1 1.4 %collective-permute-start.6 = (f32[16,1136]{1,0:T(8,128)S(1)}, f32[16,1136]{1,0:T(8,128)S(1)}, u32[]{:S(2)}, u32[]{:S(2)}) collective-permute-start(f32[16,1136]{1,0:T(8,128)S(1)} %fusion.181), channel_id=1, source_target_pairs={{0,16},{16,0},{1,17},{17,1},{2,18},{18,2},{3,19},{19,3},{4,20},{20... | collective-permute-start | bytes 218120 | tf_op jit(solution)/shard_map/ppermute | solution.py:40
  48.9 1.6 %collective-permute-start.12 = (bf16[2,284,70]{1,0,2:T(2,128)(2,1)S(1)}, bf16[2,284,70]{1,0,2:T(2,128)(2,1)S(1)}, u32[]{:S(2)}, u32[]{:S(2)}) collective-permute-start(bf16[2,284,70]{1,0,2:T(2,128)(2,1)S(1)} %fusion.19), channel_id=1, source_target_pairs={{0,2},{1,3},{2,0},{3,1},{4,6},{5,7},{6,4},{7,5},{8,10},{9,11},{10,... | collective-permute-start | bytes 238568 | tf_op jit(solution)/shard_map/ppermute | solution.py:104
  50.5 1.1 %collective-permute-done.6 = f32[16,1136]{1,0:T(8,128)S(1)} collective-permute-done((f32[16,1136]{1,0:T(8,128)S(1)}, f32[16,1136]{1,0:T(8,128)S(1)}, u32[]{:S(2)}, u32[]{:S(2)}) %collective-permute-start.6) | collective-permute-done | bytes 72736 | tf_op jit(solution)/shard_map/ppermute | solution.py:40
  51.6 3.4 %fusion.35 = f32[16,2272]{1,0:T(8,128)S(1)} fusion(bf16[1136,2272]{1,0:T(8,128)(2,1)} %param.21, f32[16,1136]{1,0:T(8,128)S(1)} %fusion.181, f32[16,1136]{1,0:T(8,128)S(1)} %collective-permute-done.6), kind=kOutput, calls=%fused_computation.74 | convolution fusion | flops 83791360 | bytes 5452800 | tf_op jit(solution)/shard_map/dot_general | solution.py:209
  55.4 0.6 concatenate.78
  55.9 1.6 %collective-permute-start.13 = (bf16[2,284,70]{1,2,0:T(8,128)(2,1)S(1)}, bf16[2,284,70]{1,2,0:T(8,128)(2,1)S(1)}, u32[]{:S(2)}, u32[]{:S(2)}) collective-permute-start(bf16[2,284,70]{1,2,0:T(8,128)(2,1)S(1)} %concatenate.78), channel_id=1, source_target_pairs={{0,4},{1,5},{2,6},{3,7},{4,0},{5,1},{6,2},{7,3},{8,12},{9,13},{10,... | collective-permute-start | bytes 238568 | tf_op jit(solution)/shard_map/ppermute | solution.py:104
  57.7 3.1 %collective-permute-done.13 = bf16[2,284,70]{1,2,0:T(8,128)(2,1)S(1)} collective-permute-done((bf16[2,284,70]{1,2,0:T(8,128)(2,1)S(1)}, bf16[2,284,70]{1,2,0:T(8,128)(2,1)S(1)}, u32[]{:S(2)}, u32[]{:S(2)}) %collective-permute-start.13) | collective-permute-done | bytes 79552 | tf_op jit(solution)/shard_map/ppermute | solution.py:104
  63.2 2.6 %collective-permute-start.14 = (bf16[2,4,6,70]{3,2,1,0:T(8,128)(2,1)S(1)}, bf16[2,4,6,70]{3,2,1,0:T(8,128)(2,1)S(1)}, u32[]{:S(2)}, u32[]{:S(2)}) collective-permute-start(bf16[2,4,6,70]{3,2,1,0:T(8,128)(2,1)S(1)} %constant_dynamic-slice_fusion), channel_id=1, source_target_pairs={{0,8},{1,9},{2,10},{3,11},{4,12},{5,13},{6,14},{7,15},{8,0},{9,1},... | collective-permute-start | bytes 20168 | tf_op jit(solution)/shard_map/ppermute | solution.py:118
  66.6 1.4 %collective-permute-done.14 = bf16[2,4,6,70]{3,2,1,0:T(8,128)(2,1)S(1)} collective-permute-done((bf16[2,4,6,70]{3,2,1,0:T(8,128)(2,1)S(1)}, bf16[2,4,6,70]{3,2,1,0:T(8,128)(2,1)S(1)}, u32[]{:S(2)}, u32[]{:S(2)}) %collective-permute-start.14) | collective-permute-done | bytes 6752 | tf_op jit(solution)/shard_map/ppermute | solution.py:118
  68.7 1.4 %collective-permute-start.15 = (bf16[4,2,284]{2,0,1:T(4,128)(2,1)S(1)}, bf16[4,2,284]{2,0,1:T(4,128)(2,1)S(1)}, u32[]{:S(2)}, u32[]{:S(2)}) collective-permute-start(bf16[4,2,284]{2,0,1:T(4,128)(2,1)S(1)} %get-tuple-element.67), channel_id=1, source_target_pairs={{0,16},{16,0},{1,17},{17,1},{2,18},{18,2},{3,19},{19,3},{4,20},{20... | collective-permute-start | bytes 13640 | tf_op jit(solution)/shard_map/ppermute | solution.py:22
  70.1 2.2 %collective-permute-done.15 = bf16[4,2,284]{2,0,1:T(4,128)(2,1)S(1)} collective-permute-done((bf16[4,2,284]{2,0,1:T(4,128)(2,1)S(1)}, bf16[4,2,284]{2,0,1:T(4,128)(2,1)S(1)}, u32[]{:S(2)}, u32[]{:S(2)}) %collective-permute-start.15) | collective-permute-done | bytes 4576 | tf_op jit(solution)/shard_map/ppermute | solution.py:22
  72.4 0.6 gather_fusion.2
  73.8 1.3 %collective-permute-done.16 = f32[2,2,2,4,2,284]{5,4,3,2,1,0:T(2,128)S(1)} collective-permute-done((f32[2,2,2,4,2,284]{5,4,3,2,1,0:T(2,128)S(1)}, f32[2,2,2,4,2,284]{5,4,3,2,1,0:T(2,128)S(1)}, u32[]{:S(2)}, u32[]{:S(2)}) %collective-permute-start.16) | collective-permute-done | bytes 72736 | tf_op jit(solution)/shard_map/ppermute | solution.py:57
  75.1 1.6 %collective-permute-start.17 = (f32[2,2,4,2,284]{4,3,2,1,0:T(2,128)S(1)}, f32[2,2,4,2,284]{4,3,2,1,0:T(2,128)S(1)}, u32[]{:S(2)}, u32[]{:S(2)}) collective-permute-start(f32[2,2,4,2,284]{4,3,2,1,0:T(2,128)S(1)} %fusion.32), channel_id=1, source_target_pairs={{0,2},{1,3},{2,0},{3,1},{4,6},{5,7},{6,4},{7,5},{8,10},{9,11},{10,... | collective-permute-start | bytes 109064 | tf_op jit(solution)/shard_map/ppermute | solution.py:57
  76.7 2.6 %collective-permute-done.17 = f32[2,2,4,2,284]{4,3,2,1,0:T(2,128)S(1)} collective-permute-done((f32[2,2,4,2,284]{4,3,2,1,0:T(2,128)S(1)}, f32[2,2,4,2,284]{4,3,2,1,0:T(2,128)S(1)}, u32[]{:S(2)}, u32[]{:S(2)}) %collective-permute-start.17) | collective-permute-done | bytes 36384 | tf_op jit(solution)/shard_map/ppermute | solution.py:57
  79.3 1.6 %collective-permute-start.18 = (f32[2,4,2,284]{3,2,1,0:T(2,128)S(1)}, f32[2,4,2,284]{3,2,1,0:T(2,128)S(1)}, u32[]{:S(2)}, u32[]{:S(2)}) collective-permute-start(f32[2,4,2,284]{3,2,1,0:T(2,128)S(1)} %fusion.69), channel_id=1, source_target_pairs={{0,4},{1,5},{2,6},{3,7},{4,0},{5,1},{6,2},{7,3},{8,12},{9,13},{10,... | collective-permute-start | bytes 54536 | tf_op jit(solution)/shard_map/ppermute | solution.py:57
  81.0 2.2 %collective-permute-done.18 = f32[2,4,2,284]{3,2,1,0:T(2,128)S(1)} collective-permute-done((f32[2,4,2,284]{3,2,1,0:T(2,128)S(1)}, f32[2,4,2,284]{3,2,1,0:T(2,128)S(1)}, u32[]{:S(2)}, u32[]{:S(2)}) %collective-permute-start.18) | collective-permute-done | bytes 18208 | tf_op jit(solution)/shard_map/ppermute | solution.py:57
  83.3 2.6 %collective-permute-start.19 = (f32[4,2,284]{2,1,0:T(2,128)S(1)}, f32[4,2,284]{2,1,0:T(2,128)S(1)}, u32[]{:S(2)}, u32[]{:S(2)}) collective-permute-start(f32[4,2,284]{2,1,0:T(2,128)S(1)} %select_bitcast_fusion), channel_id=1, source_target_pairs={{0,8},{1,9},{2,10},{3,11},{4,12},{5,13},{6,14},{7,15},{8,0},{9,1},... | collective-permute-start | bytes 27272 | tf_op jit(solution)/shard_map/ppermute | solution.py:57
  85.9 2.0 %collective-permute-done.19 = f32[4,2,284]{2,1,0:T(2,128)S(1)} collective-permute-done((f32[4,2,284]{2,1,0:T(2,128)S(1)}, f32[4,2,284]{2,1,0:T(2,128)S(1)}, u32[]{:S(2)}, u32[]{:S(2)}) %collective-permute-start.19) | collective-permute-done | bytes 9120 | tf_op jit(solution)/shard_map/ppermute | solution.py:57
  88.0 5.3 %collective-permute-start.20 = (f32[4,2,284]{2,1,0:T(2,128)S(1)}, f32[4,2,284]{2,1,0:T(2,128)S(1)}, u32[]{:S(2)}, u32[]{:S(2)}) collective-permute-start(f32[4,2,284]{2,1,0:T(2,128)S(1)} %bitcast_add_fusion), channel_id=1, source_target_pairs={{0,0},{1,1},{2,2},{3,3},{4,4},{5,5},{6,6},{7,7},{8,16},{9,17},{10,... | collective-permute-start | bytes 27272 | tf_op jit(solution)/shard_map/ppermute | solution.py:275
  93.3 0.8 copy.250
  94.1 1.2 %collective-permute-done.20 = f32[4,2,284]{2,1,0:T(2,128)S(1)} collective-permute-done((f32[4,2,284]{2,1,0:T(2,128)S(1)}, f32[4,2,284]{2,1,0:T(2,128)S(1)}, u32[]{:S(2)}, u32[]{:S(2)}) %collective-permute-start.20) | collective-permute-done | bytes 9120 | tf_op jit(solution)/shard_map/ppermute | solution.py:275
  95.3 0.6 add_convert_fusion
  (173 shorter events, 14.5 us)
Async XLA Ops:
  0.6 72.4 %copy-start = (bf16[284,2272]{1,0:T(8,128)(2,1)S(1)}, bf16[284,2272]{1,0:T(8,128)(2,1)}, u32[]{:S(2)}) copy-start(bf16[284,2272]{1,0:T(8,128)(2,1)} %param.19) | copy-start | bytes 3871492
  0.6 3.9 %collective-permute-start = (bf16[4,2,284]{2,1,0:T(2,128)(2,1)}, bf16[4,2,284]{2,1,0:T(2,128)(2,1)S(1)}, u32[]{:S(2)}, u32[]{:S(2)}) collective-permute-start(bf16[4,2,284]{2,1,0:T(2,128)(2,1)} %param.11), channel_id=1, source_target_pairs={{0,16},{16,0},{1,17},{17,1},{2,18},{18,2},{3,19},{19,3},{4,20},{20... | collective-permute-start | bytes 13640 | tf_op jit(solution)/shard_map/ppermute | solution.py:22
  5.3 4.7 %collective-permute-start.1 = (bf16[2,4,2,284]{3,2,1,0:T(2,128)(2,1)S(1)}, bf16[2,4,2,284]{3,2,1,0:T(2,128)(2,1)S(1)}, u32[]{:S(2)}, u32[]{:S(2)}) collective-permute-start(bf16[2,4,2,284]{3,2,1,0:T(2,128)(2,1)S(1)} %pad_maximum_fusion.8), channel_id=1, source_target_pairs={{0,8},{1,9},{2,10},{3,11},{4,12},{5,13},{6,14},{7,15},{8,0},{9,1},... | collective-permute-start | bytes 27272 | tf_op jit(solution)/shard_map/ppermute | solution.py:22
  10.0 3.9 %collective-permute-start.2 = (bf16[2,2,4,2,284]{4,3,2,1,0:T(2,128)(2,1)S(1)}, bf16[2,2,4,2,284]{4,3,2,1,0:T(2,128)(2,1)S(1)}, u32[]{:S(2)}, u32[]{:S(2)}) collective-permute-start(bf16[2,2,4,2,284]{4,3,2,1,0:T(2,128)(2,1)S(1)} %pad_maximum_fusion.6), channel_id=1, source_target_pairs={{0,4},{1,5},{2,6},{3,7},{4,0},{5,1},{6,2},{7,3},{8,12},{9,13},{10,... | collective-permute-start | bytes 54536 | tf_op jit(solution)/shard_map/ppermute | solution.py:22
  13.9 4.2 %collective-permute-start.3 = (bf16[2,2,2,4,2,284]{5,4,3,2,1,0:T(2,128)(2,1)S(1)}, bf16[2,2,2,4,2,284]{5,4,3,2,1,0:T(2,128)(2,1)S(1)}, u32[]{:S(2)}, u32[]{:S(2)}) collective-permute-start(bf16[2,2,2,4,2,284]{5,4,3,2,1,0:T(2,128)(2,1)S(1)} %pad_maximum_fusion.3), channel_id=1, source_target_pairs={{0,2},{1,3},{2,0},{3,1},{4,6},{5,7},{6,4},{7,5},{8,10},{9,11},{10,... | collective-permute-start | bytes 109064 | tf_op jit(solution)/shard_map/ppermute | solution.py:22
  18.3 1.4 %collective-permute-start.4 = (bf16[2,2,2,2,4,2,284]{6,5,4,3,2,1,0:T(2,128)(2,1)S(1)}, bf16[2,2,2,2,4,2,284]{6,5,4,3,2,1,0:T(2,128)(2,1)S(1)}, u32[]{:S(2)}, u32[]{:S(2)}) collective-permute-start(bf16[2,2,2,2,4,2,284]{6,5,4,3,2,1,0:T(2,128)(2,1)S(1)} %pad_maximum_fusion.1), channel_id=1, source_target_pairs={{0,1},{1,0},{2,3},{3,2},{4,5},{5,4},{6,7},{7,6},{8,9},{9,8},{10,11... | collective-permute-start | bytes 218120 | tf_op jit(solution)/shard_map/ppermute | solution.py:22
  22.1 2.0 %copy-start.1 = (bf16[2272,128]{1,0:T(8,128)(2,1)S(1)}, bf16[2272,128]{1,0:T(8,128)(2,1)}, u32[]{:S(2)}) copy-start(bf16[2272,128]{1,0:T(8,128)(2,1)} %param.18) | copy-start | bytes 1744900
  24.5 9.0 %copy-start.2 = (bf16[2,512,128]{2,1,0:T(8,128)(2,1)S(1)}, bf16[2,512,128]{2,1,0:T(8,128)(2,1)}, u32[]{:S(2)}) copy-start(bf16[2,512,128]{2,1,0:T(8,128)(2,1)} %param.12) | copy-start | bytes 786436
  24.5 4.0 %collective-permute-start.5 = (f32[16,412]{1,0:T(8,128)S(1)}, f32[16,412]{1,0:T(8,128)S(1)}, u32[]{:S(2)}, u32[]{:S(2)}) collective-permute-start(f32[16,412]{1,0:T(8,128)S(1)} %pad_maximum_fusion.5), channel_id=1, source_target_pairs={{0,16},{16,0},{1,17},{17,1},{2,18},{18,2},{3,19},{19,3},{4,20},{20... | collective-permute-start | bytes 79112 | tf_op jit(solution)/shard_map/ppermute | solution.py:40
  29.0 4.5 %collective-permute-start.7 = (bf16[4,2,284]{2,1,0:T(2,128)(2,1)S(1)}, bf16[4,2,284]{2,1,0:T(2,128)(2,1)S(1)}, u32[]{:S(2)}, u32[]{:S(2)}) collective-permute-start(bf16[4,2,284]{2,1,0:T(2,128)(2,1)S(1)} %slice.413), channel_id=1, source_target_pairs={{0,8},{1,9},{2,10},{3,11},{4,12},{5,13},{6,14},{7,15},{8,0},{9,1},... | collective-permute-start | bytes 13640 | tf_op jit(solution)/shard_map/ppermute | solution.py:22
  33.7 3.8 %collective-permute-start.8 = (bf16[2,4,2,284]{3,2,1,0:T(2,128)(2,1)S(1)}, bf16[2,4,2,284]{3,2,1,0:T(2,128)(2,1)S(1)}, u32[]{:S(2)}, u32[]{:S(2)}) collective-permute-start(bf16[2,4,2,284]{3,2,1,0:T(2,128)(2,1)S(1)} %pad_maximum_fusion.9), channel_id=1, source_target_pairs={{0,4},{1,5},{2,6},{3,7},{4,0},{5,1},{6,2},{7,3},{8,12},{9,13},{10,... | collective-permute-start | bytes 27272 | tf_op jit(solution)/shard_map/ppermute | solution.py:22
  37.5 3.9 %collective-permute-start.9 = (bf16[2,2,4,2,284]{4,3,2,1,0:T(2,128)(2,1)S(1)}, bf16[2,2,4,2,284]{4,3,2,1,0:T(2,128)(2,1)S(1)}, u32[]{:S(2)}, u32[]{:S(2)}) collective-permute-start(bf16[2,2,4,2,284]{4,3,2,1,0:T(2,128)(2,1)S(1)} %pad_maximum_fusion.7), channel_id=1, source_target_pairs={{0,2},{1,3},{2,0},{3,1},{4,6},{5,7},{6,4},{7,5},{8,10},{9,11},{10,... | collective-permute-start | bytes 54536 | tf_op jit(solution)/shard_map/ppermute | solution.py:22
  41.5 1.3 %collective-permute-start.10 = (bf16[2,2,2,4,2,284]{5,4,3,2,1,0:T(2,128)(2,1)S(1)}, bf16[2,2,2,4,2,284]{5,4,3,2,1,0:T(2,128)(2,1)S(1)}, u32[]{:S(2)}, u32[]{:S(2)}) collective-permute-start(bf16[2,2,2,4,2,284]{5,4,3,2,1,0:T(2,128)(2,1)S(1)} %pad_maximum_fusion.4), channel_id=1, source_target_pairs={{0,1},{1,0},{2,3},{3,2},{4,5},{5,4},{6,7},{7,6},{8,9},{9,8},{10,11... | collective-permute-start | bytes 109064 | tf_op jit(solution)/shard_map/ppermute | solution.py:22
  46.1 0.9 copy-start.4
  46.8 1.7 %collective-permute-start.11 = (bf16[2,284,70]{1,0,2:T(2,128)(2,1)S(1)}, bf16[2,284,70]{1,0,2:T(2,128)(2,1)S(1)}, u32[]{:S(2)}, u32[]{:S(2)}) collective-permute-start(bf16[2,284,70]{1,0,2:T(2,128)(2,1)S(1)} %fusion.18), channel_id=1, source_target_pairs={{0,1},{1,0},{2,3},{3,2},{4,5},{5,4},{6,7},{7,6},{8,9},{9,8},{10,11... | collective-permute-start | bytes 238568 | tf_op jit(solution)/shard_map/ppermute | solution.py:104
  47.1 4.5 %collective-permute-start.6 = (f32[16,1136]{1,0:T(8,128)S(1)}, f32[16,1136]{1,0:T(8,128)S(1)}, u32[]{:S(2)}, u32[]{:S(2)}) collective-permute-start(f32[16,1136]{1,0:T(8,128)S(1)} %fusion.181), channel_id=1, source_target_pairs={{0,16},{16,0},{1,17},{17,1},{2,18},{18,2},{3,19},{19,3},{4,20},{20... | collective-permute-start | bytes 218120 | tf_op jit(solution)/shard_map/ppermute | solution.py:40
  48.9 6.1 %collective-permute-start.12 = (bf16[2,284,70]{1,0,2:T(2,128)(2,1)S(1)}, bf16[2,284,70]{1,0,2:T(2,128)(2,1)S(1)}, u32[]{:S(2)}, u32[]{:S(2)}) collective-permute-start(bf16[2,284,70]{1,0,2:T(2,128)(2,1)S(1)} %fusion.19), channel_id=1, source_target_pairs={{0,2},{1,3},{2,0},{3,1},{4,6},{5,7},{6,4},{7,5},{8,10},{9,11},{10,... | collective-permute-start | bytes 238568 | tf_op jit(solution)/shard_map/ppermute | solution.py:104
  55.9 4.8 %collective-permute-start.13 = (bf16[2,284,70]{1,2,0:T(8,128)(2,1)S(1)}, bf16[2,284,70]{1,2,0:T(8,128)(2,1)S(1)}, u32[]{:S(2)}, u32[]{:S(2)}) collective-permute-start(bf16[2,284,70]{1,2,0:T(8,128)(2,1)S(1)} %concatenate.78), channel_id=1, source_target_pairs={{0,4},{1,5},{2,6},{3,7},{4,0},{5,1},{6,2},{7,3},{8,12},{9,13},{10,... | collective-permute-start | bytes 238568 | tf_op jit(solution)/shard_map/ppermute | solution.py:104
  63.2 4.7 %collective-permute-start.14 = (bf16[2,4,6,70]{3,2,1,0:T(8,128)(2,1)S(1)}, bf16[2,4,6,70]{3,2,1,0:T(8,128)(2,1)S(1)}, u32[]{:S(2)}, u32[]{:S(2)}) collective-permute-start(bf16[2,4,6,70]{3,2,1,0:T(8,128)(2,1)S(1)} %constant_dynamic-slice_fusion), channel_id=1, source_target_pairs={{0,8},{1,9},{2,10},{3,11},{4,12},{5,13},{6,14},{7,15},{8,0},{9,1},... | collective-permute-start | bytes 20168 | tf_op jit(solution)/shard_map/ppermute | solution.py:118
  68.7 3.6 %collective-permute-start.15 = (bf16[4,2,284]{2,0,1:T(4,128)(2,1)S(1)}, bf16[4,2,284]{2,0,1:T(4,128)(2,1)S(1)}, u32[]{:S(2)}, u32[]{:S(2)}) collective-permute-start(bf16[4,2,284]{2,0,1:T(4,128)(2,1)S(1)} %get-tuple-element.67), channel_id=1, source_target_pairs={{0,16},{16,0},{1,17},{17,1},{2,18},{18,2},{3,19},{19,3},{4,20},{20... | collective-permute-start | bytes 13640 | tf_op jit(solution)/shard_map/ppermute | solution.py:22
  73.5 21.9 %copy-start.3 = (bf16[4,2,284]{2,1,0:T(2,128)(2,1)S(1)}, bf16[4,2,284]{2,1,0:T(2,128)(2,1)}, u32[]{:S(2)}) copy-start(bf16[4,2,284]{2,1,0:T(2,128)(2,1)} %param.11) | copy-start | bytes 13636
  73.7 1.4 %collective-permute-start.16 = (f32[2,2,2,4,2,284]{5,4,3,2,1,0:T(2,128)S(1)}, f32[2,2,2,4,2,284]{5,4,3,2,1,0:T(2,128)S(1)}, u32[]{:S(2)}, u32[]{:S(2)}) collective-permute-start(f32[2,2,2,4,2,284]{5,4,3,2,1,0:T(2,128)S(1)} %fusion.17), channel_id=1, source_target_pairs={{0,1},{1,0},{2,3},{3,2},{4,5},{5,4},{6,7},{7,6},{8,9},{9,8},{10,11... | collective-permute-start | bytes 218120 | tf_op jit(solution)/shard_map/ppermute | solution.py:57
  75.1 4.2 %collective-permute-start.17 = (f32[2,2,4,2,284]{4,3,2,1,0:T(2,128)S(1)}, f32[2,2,4,2,284]{4,3,2,1,0:T(2,128)S(1)}, u32[]{:S(2)}, u32[]{:S(2)}) collective-permute-start(f32[2,2,4,2,284]{4,3,2,1,0:T(2,128)S(1)} %fusion.32), channel_id=1, source_target_pairs={{0,2},{1,3},{2,0},{3,1},{4,6},{5,7},{6,4},{7,5},{8,10},{9,11},{10,... | collective-permute-start | bytes 109064 | tf_op jit(solution)/shard_map/ppermute | solution.py:57
  79.3 3.9 %collective-permute-start.18 = (f32[2,4,2,284]{3,2,1,0:T(2,128)S(1)}, f32[2,4,2,284]{3,2,1,0:T(2,128)S(1)}, u32[]{:S(2)}, u32[]{:S(2)}) collective-permute-start(f32[2,4,2,284]{3,2,1,0:T(2,128)S(1)} %fusion.69), channel_id=1, source_target_pairs={{0,4},{1,5},{2,6},{3,7},{4,0},{5,1},{6,2},{7,3},{8,12},{9,13},{10,... | collective-permute-start | bytes 54536 | tf_op jit(solution)/shard_map/ppermute | solution.py:57
  83.3 4.7 %collective-permute-start.19 = (f32[4,2,284]{2,1,0:T(2,128)S(1)}, f32[4,2,284]{2,1,0:T(2,128)S(1)}, u32[]{:S(2)}, u32[]{:S(2)}) collective-permute-start(f32[4,2,284]{2,1,0:T(2,128)S(1)} %select_bitcast_fusion), channel_id=1, source_target_pairs={{0,8},{1,9},{2,10},{3,11},{4,12},{5,13},{6,14},{7,15},{8,0},{9,1},... | collective-permute-start | bytes 27272 | tf_op jit(solution)/shard_map/ppermute | solution.py:57
  88.0 7.4 %collective-permute-start.20 = (f32[4,2,284]{2,1,0:T(2,128)S(1)}, f32[4,2,284]{2,1,0:T(2,128)S(1)}, u32[]{:S(2)}, u32[]{:S(2)}) collective-permute-start(f32[4,2,284]{2,1,0:T(2,128)S(1)} %bitcast_add_fusion), channel_id=1, source_target_pairs={{0,0},{1,1},{2,2},{3,3},{4,4},{5,5},{6,6},{7,7},{8,16},{9,17},{10,... | collective-permute-start | bytes 27272 | tf_op jit(solution)/shard_map/ppermute | solution.py:275

commit v10 on v9

--- a/solution.py
+++ b/solution.py
@@ -42,11 +42,11 @@
     return value
 
 
-def scatter_sum(blocks, axis, size):
+def scatter_sum(blocks, axis, size, rounds):
     index = lax.axis_index(axis)
     levels = size.bit_length() - 1
     blocks = blocks.reshape((2,) * levels + blocks.shape[1:])
-    for level in range(levels):
+    for level in range(rounds):
         bit = 2 ** level
         place = levels - 1 - level
         high = (index // bit) % 2 == 1
@@ -266,13 +266,25 @@
     by_request = partial_sum.reshape(steps, total, part_width)
     blocks = by_request.reshape(steps, req_size, group_rows, chunks, slice_width)
     blocks = blocks.transpose(1, 3, 0, 2, 4).reshape(seq_size, steps, group_rows, slice_width)
-    reduced = scatter_sum(blocks, "seq", seq_size)
-    routes = []
+    levels = seq_size.bit_length() - 1
+    half = seq_size // 2
+    pair = scatter_sum(blocks, "seq", seq_size, levels - 1)
+    high = shard_index >= half
+    own_block = jnp.where(high, pair[1], pair[0])
+    other_block = jnp.where(high, pair[0], pair[1])
+
+    def owner(source_group, block):
+        return (block // chunks) * seq_size + source_group * chunks + block % chunks
+
+    own_routes, other_routes = [], []
     for source_group in range(req_size):
         for block in range(seq_size):
-            target = (block // chunks) * seq_size + source_group * chunks + block % chunks
-            routes.append((source_group * seq_size + block, target))
-    own_branch = lax.ppermute(reduced, ALL, routes)
+            source = source_group * seq_size + block
+            own_routes.append((source, owner(source_group, block)))
+            other_routes.append((source, owner(source_group, block ^ half)))
+    own_branch = lax.ppermute(own_block, ALL, own_routes) + lax.ppermute(
+        other_block, ALL, other_routes
+    )
     new_states = (states.astype(jnp.float32) + own_branch).astype(jnp.bfloat16)
     return (new_states, cache_now)
 

time: 97.3 us -> 94 us (0.966)
  starting transfers between devices: 32.7 us -> 30.1 us
    ppermute x4 -> x3, starting transfers between devices: 5.95 us -> 3.3 us  [scatter_sum(): blocks = keep + lax.ppermute(send, axis, xor_pairs(size, bit))]
    ppermute x4 -> x3, waiting for transfers between devices: 8.09 us -> 6.07 us  [scatter_sum(): blocks = keep + lax.ppermute(send, axis, xor_pairs(size, bit))]
    ppermute x1 -> x2, waiting for transfers between devices: 1.23 us -> 2.84 us  [the longest x1 1.68 us: shards(): lax.ppermute(other_block, ALL, other_routes)]
    ppermute x1 -> x2, starting transfers between devices: 5.31 us -> 5.37 us  [the longest x1 5.31 us: shards(): lax.ppermute(own_block, ALL, own_routes)]
where the time goes in v10:
time: 94 us; the launch traced here: 93 us
  waiting for transfers between devices  30.5 us (32%)
  starting transfers between devices  30.1 us (32%)
  local copies, waits for them, and re-layouts  12.4 us (13%)
  matrix products  9.94 us (11%)
  other arithmetic  8.48 us (9%)
  between operations  1.52 us (2%)
    ppermute x10, waiting for transfers between devices, gather_xor(): lax.ppermute(stacked, axis, xor_pairs(size, bit))  16 us
    ppermute x10, starting transfers between devices, gather_xor(): lax.ppermute(stacked, axis, xor_pairs(size, bit))  13.3 us
    ppermute x3, waiting for transfers between devices, scatter_sum(): blocks = keep + lax.ppermute(send, axis, xor_pairs(size, bit))  6.07 us
    ppermute x1, starting transfers between devices, shards(): lax.ppermute(own_block, ALL, own_routes)  5.31 us
    ppermute x3, starting transfers between devices, merge_over(): lax.ppermute(pack_merge(peak, total, weighted), axis, xor_pairs(size, bit))  3.45 us
    dot_general x1, matrix products, shards(): down_part = jnp.dot(hidden, w_down, preferred_element_type=jnp.float32)  3.39 us
    dot_general x1, matrix products, shards(): part_up = jnp.dot(normed_part, w_up, preferred_element_type=jnp.float32)  3.32 us
    ppermute x3, starting transfers between devices, scatter_sum(): blocks = keep + lax.ppermute(send, axis, xor_pairs(size, bit))  3.3 us
  transfers between devices with their start and end apart: 21, of which 18 were waited for; matrix products, arithmetic and copies ran while one was open for 15% of the time, Pallas kernels for 0%

profile of v10, /device:TPU:2, one launch (start us, length us, event | category | flops | bytes accessed | tf_op | source)
XLA Modules:
  0.0 93.0 jit_solution(6587920878363397503)
XLA Ops:
  0.8 0.8 dynamic_slice.22
  1.7 0.8 select_reduce_fusion.2
  3.3 1.3 %collective-permute-done = bf16[4,2,284]{2,1,0:T(2,128)(2,1)S(1)} collective-permute-done((bf16[4,2,284]{2,1,0:T(2,128)(2,1)}, bf16[4,2,284]{2,1,0:T(2,128)(2,1)S(1)}, u32[]{:S(2)}, u32[]{:S(2)}) %collective-permute-start) | collective-permute-done | bytes 4576 | tf_op jit(solution)/shard_map/ppermute | solution.py:22
  4.5 0.7 pad_maximum_fusion.8
  5.3 2.7 %collective-permute-start.1 = (bf16[2,4,2,284]{3,2,1,0:T(2,128)(2,1)S(1)}, bf16[2,4,2,284]{3,2,1,0:T(2,128)(2,1)S(1)}, u32[]{:S(2)}, u32[]{:S(2)}) collective-permute-start(bf16[2,4,2,284]{3,2,1,0:T(2,128)(2,1)S(1)} %pad_maximum_fusion.8), channel_id=1, source_target_pairs={{0,8},{1,9},{2,10},{3,11},{4,12},{5,13},{6,14},{7,15},{8,0},{9,1},... | collective-permute-start | bytes 27272 | tf_op jit(solution)/shard_map/ppermute | solution.py:22
  7.9 0.7 fusion.194
  8.6 1.3 %collective-permute-done.1 = bf16[2,4,2,284]{3,2,1,0:T(2,128)(2,1)S(1)} collective-permute-done((bf16[2,4,2,284]{3,2,1,0:T(2,128)(2,1)S(1)}, bf16[2,4,2,284]{3,2,1,0:T(2,128)(2,1)S(1)}, u32[]{:S(2)}, u32[]{:S(2)}) %collective-permute-start.1) | collective-permute-done | bytes 9120 | tf_op jit(solution)/shard_map/ppermute | solution.py:22
  10.0 1.6 %collective-permute-start.2 = (bf16[2,2,4,2,284]{4,3,2,1,0:T(2,128)(2,1)S(1)}, bf16[2,2,4,2,284]{4,3,2,1,0:T(2,128)(2,1)S(1)}, u32[]{:S(2)}, u32[]{:S(2)}) collective-permute-start(bf16[2,2,4,2,284]{4,3,2,1,0:T(2,128)(2,1)S(1)} %pad_maximum_fusion.6), channel_id=1, source_target_pairs={{0,4},{1,5},{2,6},{3,7},{4,0},{5,1},{6,2},{7,3},{8,12},{9,13},{10,... | collective-permute-start | bytes 54536 | tf_op jit(solution)/shard_map/ppermute | solution.py:22
  11.8 0.8 dynamic-slice
  12.6 0.8 dynamic-slice.1
  13.9 1.6 %collective-permute-start.3 = (bf16[2,2,2,4,2,284]{5,4,3,2,1,0:T(2,128)(2,1)S(1)}, bf16[2,2,2,4,2,284]{5,4,3,2,1,0:T(2,128)(2,1)S(1)}, u32[]{:S(2)}, u32[]{:S(2)}) collective-permute-start(bf16[2,2,2,4,2,284]{5,4,3,2,1,0:T(2,128)(2,1)S(1)} %pad_maximum_fusion.3), channel_id=1, source_target_pairs={{0,2},{1,3},{2,0},{3,1},{4,6},{5,7},{6,4},{7,5},{8,10},{9,11},{10,... | collective-permute-start | bytes 109064 | tf_op jit(solution)/shard_map/ppermute | solution.py:22
  15.6 2.5 %collective-permute-done.3 = bf16[2,2,2,4,2,284]{5,4,3,2,1,0:T(2,128)(2,1)S(1)} collective-permute-done((bf16[2,2,2,4,2,284]{5,4,3,2,1,0:T(2,128)(2,1)S(1)}, bf16[2,2,2,4,2,284]{5,4,3,2,1,0:T(2,128)(2,1)S(1)}, u32[]{:S(2)}, u32[]{:S(2)}) %collective-permute-start.3) | collective-permute-done | bytes 36384 | tf_op jit(solution)/shard_map/ppermute | solution.py:22
  18.5 1.1 %collective-permute-done.4 = bf16[2,2,2,2,4,2,284]{6,5,4,3,2,1,0:T(2,128)(2,1)S(1)} collective-permute-done((bf16[2,2,2,2,4,2,284]{6,5,4,3,2,1,0:T(2,128)(2,1)S(1)}, bf16[2,2,2,2,4,2,284]{6,5,4,3,2,1,0:T(2,128)(2,1)S(1)}, u32[]{:S(2)}, u32[]{:S(2)}) %collective-permute-start.4) | collective-permute-done | bytes 72736 | tf_op jit(solution)/shard_map/ppermute | solution.py:22
  19.9 1.0 %gather_fusion = bf16[32,4,2,284]{3,2,1,0:T(2,128)(2,1)S(1)} fusion(bf16[32,4,2,284]{3,2,1,0:T(2,128)(2,1)S(1)} %bitcast.287, s32[1024]{0:T(1024)S(1)} %get-tuple-element.104), kind=kCustom, calls=%fused_computation | custom fusion | bytes 290944 | tf_op jit(solution)/shard_map/jit(_take)/gather | solution.py:186
  22.4 1.8 %fusion.179 = f32[16,284]{1,0:T(8,128)S(1)} fusion(bf16[2272,284]{0,1:T(8,128)(2,1)} %param.17, f32[16,4544]{1,0:T(8,128)S(1)} %reshape.879, s32[]{:T(128)S(6)} %select_n.335, f32[2272]{0:T(1024)S(1)} %dynamic-slice.1, f32[2272]{0:T(1024)S(1)} %dynamic-slice, f32[16]{0:T(128)S(1)} %rsqrt.12, f32[16]{0:T(128)S(1)} %div.135), kind=kOutput, calls=%fused_computation.398 | convolution fusion | flops 20829696 | bytes 1481732 | tf_op jit(solution)/shard_map/dot_general | solution.py:191
  24.5 0.7 collective-permute-start.5
  25.2 3.3 %fusion.181 = f32[16,1136]{1,0:T(8,128)S(1)} fusion(bf16[2272,1136]{1,0:T(8,128)(2,1)} %param.20, f32[16,4544]{1,0:T(8,128)S(1)} %reshape.879, s32[]{:T(128)S(6)} %select_n.335, f32[2272]{0:T(1024)S(1)} %dynamic-slice.1, f32[2272]{0:T(1024)S(1)} %dynamic-slice, f32[16]{0:T(128)S(1)} %rsqrt.12, f32[16]{0:T(128)S(1)} %div.135), kind=kOutput, calls=%fused_computation.399 | convolution fusion | flops 82773504 | bytes 5407748 | tf_op jit(solution)/shard_map/dot_general | solution.py:194
  29.0 2.6 %collective-permute-start.7 = (bf16[4,2,284]{2,1,0:T(2,128)(2,1)S(1)}, bf16[4,2,284]{2,1,0:T(2,128)(2,1)S(1)}, u32[]{:S(2)}, u32[]{:S(2)}) collective-permute-start(bf16[4,2,284]{2,1,0:T(2,128)(2,1)S(1)} %slice.415), channel_id=1, source_target_pairs={{0,8},{1,9},{2,10},{3,11},{4,12},{5,13},{6,14},{7,15},{8,0},{9,1},... | collective-permute-start | bytes 13640 | tf_op jit(solution)/shard_map/ppermute | solution.py:22
  31.7 1.8 %collective-permute-done.7 = bf16[4,2,284]{2,1,0:T(2,128)(2,1)S(1)} collective-permute-done((bf16[4,2,284]{2,1,0:T(2,128)(2,1)S(1)}, bf16[4,2,284]{2,1,0:T(2,128)(2,1)S(1)}, u32[]{:S(2)}, u32[]{:S(2)}) %collective-permute-start.7) | collective-permute-done | bytes 4576 | tf_op jit(solution)/shard_map/ppermute | solution.py:22
  33.7 1.6 %collective-permute-start.8 = (bf16[2,4,2,284]{3,2,1,0:T(2,128)(2,1)S(1)}, bf16[2,4,2,284]{3,2,1,0:T(2,128)(2,1)S(1)}, u32[]{:S(2)}, u32[]{:S(2)}) collective-permute-start(bf16[2,4,2,284]{3,2,1,0:T(2,128)(2,1)S(1)} %pad_maximum_fusion.9), channel_id=1, source_target_pairs={{0,4},{1,5},{2,6},{3,7},{4,0},{5,1},{6,2},{7,3},{8,12},{9,13},{10,... | collective-permute-start | bytes 27272 | tf_op jit(solution)/shard_map/ppermute | solution.py:22
  35.6 1.9 %collective-permute-done.8 = bf16[2,4,2,284]{3,2,1,0:T(2,128)(2,1)S(1)} collective-permute-done((bf16[2,4,2,284]{3,2,1,0:T(2,128)(2,1)S(1)}, bf16[2,4,2,284]{3,2,1,0:T(2,128)(2,1)S(1)}, u32[]{:S(2)}, u32[]{:S(2)}) %collective-permute-start.8) | collective-permute-done | bytes 9120 | tf_op jit(solution)/shard_map/ppermute | solution.py:22
  37.5 1.6 %collective-permute-start.9 = (bf16[2,2,4,2,284]{4,3,2,1,0:T(2,128)(2,1)S(1)}, bf16[2,2,4,2,284]{4,3,2,1,0:T(2,128)(2,1)S(1)}, u32[]{:S(2)}, u32[]{:S(2)}) collective-permute-start(bf16[2,2,4,2,284]{4,3,2,1,0:T(2,128)(2,1)S(1)} %pad_maximum_fusion.7), channel_id=1, source_target_pairs={{0,2},{1,3},{2,0},{3,1},{4,6},{5,7},{6,4},{7,5},{8,10},{9,11},{10,... | collective-permute-start | bytes 54536 | tf_op jit(solution)/shard_map/ppermute | solution.py:22
  39.1 2.3 %collective-permute-done.9 = bf16[2,2,4,2,284]{4,3,2,1,0:T(2,128)(2,1)S(1)} collective-permute-done((bf16[2,2,4,2,284]{4,3,2,1,0:T(2,128)(2,1)S(1)}, bf16[2,2,4,2,284]{4,3,2,1,0:T(2,128)(2,1)S(1)}, u32[]{:S(2)}, u32[]{:S(2)}) %collective-permute-start.9) | collective-permute-done | bytes 18208 | tf_op jit(solution)/shard_map/ppermute | solution.py:22
  41.6 1.1 %collective-permute-done.10 = bf16[2,2,2,4,2,284]{5,4,3,2,1,0:T(2,128)(2,1)S(1)} collective-permute-done((bf16[2,2,2,4,2,284]{5,4,3,2,1,0:T(2,128)(2,1)S(1)}, bf16[2,2,2,4,2,284]{5,4,3,2,1,0:T(2,128)(2,1)S(1)}, u32[]{:S(2)}, u32[]{:S(2)}) %collective-permute-start.10) | collective-permute-done | bytes 36384 | tf_op jit(solution)/shard_map/ppermute | solution.py:22
  43.0 0.6 gather_fusion.1
  47.1 1.4 %collective-permute-start.6 = (f32[16,1136]{1,0:T(8,128)S(1)}, f32[16,1136]{1,0:T(8,128)S(1)}, u32[]{:S(2)}, u32[]{:S(2)}) collective-permute-start(f32[16,1136]{1,0:T(8,128)S(1)} %fusion.181), channel_id=1, source_target_pairs={{0,16},{16,0},{1,17},{17,1},{2,18},{18,2},{3,19},{19,3},{4,20},{20... | collective-permute-start | bytes 218120 | tf_op jit(solution)/shard_map/ppermute | solution.py:40
  48.9 1.6 %collective-permute-start.12 = (bf16[2,284,70]{1,0,2:T(2,128)(2,1)S(1)}, bf16[2,284,70]{1,0,2:T(2,128)(2,1)S(1)}, u32[]{:S(2)}, u32[]{:S(2)}) collective-permute-start(bf16[2,284,70]{1,0,2:T(2,128)(2,1)S(1)} %fusion.19), channel_id=1, source_target_pairs={{0,2},{1,3},{2,0},{3,1},{4,6},{5,7},{6,4},{7,5},{8,10},{9,11},{10,... | collective-permute-start | bytes 238568 | tf_op jit(solution)/shard_map/ppermute | solution.py:104
  50.5 1.1 %collective-permute-done.6 = f32[16,1136]{1,0:T(8,128)S(1)} collective-permute-done((f32[16,1136]{1,0:T(8,128)S(1)}, f32[16,1136]{1,0:T(8,128)S(1)}, u32[]{:S(2)}, u32[]{:S(2)}) %collective-permute-start.6) | collective-permute-done | bytes 72736 | tf_op jit(solution)/shard_map/ppermute | solution.py:40
  51.6 3.4 %fusion.35 = f32[16,2272]{1,0:T(8,128)S(1)} fusion(bf16[1136,2272]{1,0:T(8,128)(2,1)} %param.21, f32[16,1136]{1,0:T(8,128)S(1)} %fusion.181, f32[16,1136]{1,0:T(8,128)S(1)} %collective-permute-done.6), kind=kOutput, calls=%fused_computation.74 | convolution fusion | flops 83791360 | bytes 5452800 | tf_op jit(solution)/shard_map/dot_general | solution.py:209
  55.4 0.6 concatenate.78
  55.9 1.6 %collective-permute-start.13 = (bf16[2,284,70]{1,2,0:T(8,128)(2,1)S(1)}, bf16[2,284,70]{1,2,0:T(8,128)(2,1)S(1)}, u32[]{:S(2)}, u32[]{:S(2)}) collective-permute-start(bf16[2,284,70]{1,2,0:T(8,128)(2,1)S(1)} %concatenate.78), channel_id=1, source_target_pairs={{0,4},{1,5},{2,6},{3,7},{4,0},{5,1},{6,2},{7,3},{8,12},{9,13},{10,... | collective-permute-start | bytes 238568 | tf_op jit(solution)/shard_map/ppermute | solution.py:104
  57.7 3.1 %collective-permute-done.13 = bf16[2,284,70]{1,2,0:T(8,128)(2,1)S(1)} collective-permute-done((bf16[2,284,70]{1,2,0:T(8,128)(2,1)S(1)}, bf16[2,284,70]{1,2,0:T(8,128)(2,1)S(1)}, u32[]{:S(2)}, u32[]{:S(2)}) %collective-permute-start.13) | collective-permute-done | bytes 79552 | tf_op jit(solution)/shard_map/ppermute | solution.py:104
  62.7 0.5 concatenate.86
  63.2 2.6 %collective-permute-start.14 = (bf16[2,4,6,70]{3,2,1,0:T(8,128)(2,1)S(1)}, bf16[2,4,6,70]{3,2,1,0:T(8,128)(2,1)S(1)}, u32[]{:S(2)}, u32[]{:S(2)}) collective-permute-start(bf16[2,4,6,70]{3,2,1,0:T(8,128)(2,1)S(1)} %constant_dynamic-slice_fusion), channel_id=1, source_target_pairs={{0,8},{1,9},{2,10},{3,11},{4,12},{5,13},{6,14},{7,15},{8,0},{9,1},... | collective-permute-start | bytes 20168 | tf_op jit(solution)/shard_map/ppermute | solution.py:118
  66.6 1.4 %collective-permute-done.14 = bf16[2,4,6,70]{3,2,1,0:T(8,128)(2,1)S(1)} collective-permute-done((bf16[2,4,6,70]{3,2,1,0:T(8,128)(2,1)S(1)}, bf16[2,4,6,70]{3,2,1,0:T(8,128)(2,1)S(1)}, u32[]{:S(2)}, u32[]{:S(2)}) %collective-permute-start.14) | collective-permute-done | bytes 6752 | tf_op jit(solution)/shard_map/ppermute | solution.py:118
  68.7 1.4 %collective-permute-start.15 = (bf16[4,2,284]{2,0,1:T(4,128)(2,1)S(1)}, bf16[4,2,284]{2,0,1:T(4,128)(2,1)S(1)}, u32[]{:S(2)}, u32[]{:S(2)}) collective-permute-start(bf16[4,2,284]{2,0,1:T(4,128)(2,1)S(1)} %get-tuple-element.69), channel_id=1, source_target_pairs={{0,16},{16,0},{1,17},{17,1},{2,18},{18,2},{3,19},{19,3},{4,20},{20... | collective-permute-start | bytes 13640 | tf_op jit(solution)/shard_map/ppermute | solution.py:22
  70.1 2.2 %collective-permute-done.15 = bf16[4,2,284]{2,0,1:T(4,128)(2,1)S(1)} collective-permute-done((bf16[4,2,284]{2,0,1:T(4,128)(2,1)S(1)}, bf16[4,2,284]{2,0,1:T(4,128)(2,1)S(1)}, u32[]{:S(2)}, u32[]{:S(2)}) %collective-permute-start.15) | collective-permute-done | bytes 4576 | tf_op jit(solution)/shard_map/ppermute | solution.py:22
  72.4 0.6 gather_fusion.2
  73.8 1.3 %collective-permute-done.16 = f32[2,2,2,4,2,284]{5,4,3,2,1,0:T(2,128)S(1)} collective-permute-done((f32[2,2,2,4,2,284]{5,4,3,2,1,0:T(2,128)S(1)}, f32[2,2,2,4,2,284]{5,4,3,2,1,0:T(2,128)S(1)}, u32[]{:S(2)}, u32[]{:S(2)}) %collective-permute-start.16) | collective-permute-done | bytes 72736 | tf_op jit(solution)/shard_map/ppermute | solution.py:57
  75.1 1.6 %collective-permute-start.17 = (f32[2,2,4,2,284]{4,3,2,1,0:T(2,128)S(1)}, f32[2,2,4,2,284]{4,3,2,1,0:T(2,128)S(1)}, u32[]{:S(2)}, u32[]{:S(2)}) collective-permute-start(f32[2,2,4,2,284]{4,3,2,1,0:T(2,128)S(1)} %fusion.32), channel_id=1, source_target_pairs={{0,2},{1,3},{2,0},{3,1},{4,6},{5,7},{6,4},{7,5},{8,10},{9,11},{10,... | collective-permute-start | bytes 109064 | tf_op jit(solution)/shard_map/ppermute | solution.py:57
  76.7 2.6 %collective-permute-done.17 = f32[2,2,4,2,284]{4,3,2,1,0:T(2,128)S(1)} collective-permute-done((f32[2,2,4,2,284]{4,3,2,1,0:T(2,128)S(1)}, f32[2,2,4,2,284]{4,3,2,1,0:T(2,128)S(1)}, u32[]{:S(2)}, u32[]{:S(2)}) %collective-permute-start.17) | collective-permute-done | bytes 36384 | tf_op jit(solution)/shard_map/ppermute | solution.py:57
  79.3 1.6 %collective-permute-start.18 = (f32[2,4,2,284]{3,2,1,0:T(2,128)S(1)}, f32[2,4,2,284]{3,2,1,0:T(2,128)S(1)}, u32[]{:S(2)}, u32[]{:S(2)}) collective-permute-start(f32[2,4,2,284]{3,2,1,0:T(2,128)S(1)} %fusion.69), channel_id=1, source_target_pairs={{0,4},{1,5},{2,6},{3,7},{4,0},{5,1},{6,2},{7,3},{8,12},{9,13},{10,... | collective-permute-start | bytes 54536 | tf_op jit(solution)/shard_map/ppermute | solution.py:57
  81.0 2.2 %collective-permute-done.18 = f32[2,4,2,284]{3,2,1,0:T(2,128)S(1)} collective-permute-done((f32[2,4,2,284]{3,2,1,0:T(2,128)S(1)}, f32[2,4,2,284]{3,2,1,0:T(2,128)S(1)}, u32[]{:S(2)}, u32[]{:S(2)}) %collective-permute-start.18) | collective-permute-done | bytes 18208 | tf_op jit(solution)/shard_map/ppermute | solution.py:57
  83.3 5.3 %collective-permute-start.19 = (f32[4,2,284]{2,1,0:T(2,128)S(1)}, f32[4,2,284]{2,1,0:T(2,128)S(1)}, u32[]{:S(2)}, u32[]{:S(2)}) collective-permute-start(f32[4,2,284]{2,1,0:T(2,128)S(1)} %get-tuple-element.63), channel_id=1, source_target_pairs={{0,0},{1,1},{2,2},{3,3},{4,4},{5,5},{6,6},{7,7},{8,16},{9,17},{10,... | collective-permute-start | bytes 27272 | tf_op jit(solution)/shard_map/ppermute | solution.py:285
  88.7 0.8 copy.250
  89.5 1.2 %collective-permute-done.19 = f32[4,2,284]{2,1,0:T(2,128)S(1)} collective-permute-done((f32[4,2,284]{2,1,0:T(2,128)S(1)}, f32[4,2,284]{2,1,0:T(2,128)S(1)}, u32[]{:S(2)}, u32[]{:S(2)}) %collective-permute-start.19) | collective-permute-done | bytes 9120 | tf_op jit(solution)/shard_map/ppermute | solution.py:285
  90.7 1.7 %collective-permute-done.20 = f32[4,2,284]{2,1,0:T(2,128)S(1)} collective-permute-done((f32[4,2,284]{2,1,0:T(2,128)S(1)}, f32[4,2,284]{2,1,0:T(2,128)S(1)}, u32[]{:S(2)}, u32[]{:S(2)}) %collective-permute-start.20) | collective-permute-done | bytes 9120 | tf_op jit(solution)/shard_map/ppermute | solution.py:285
  92.4 0.6 add_convert_fusion
  (172 shorter events, 14.0 us)
Async XLA Ops:
  0.6 72.4 %copy-start = (bf16[284,2272]{1,0:T(8,128)(2,1)S(1)}, bf16[284,2272]{1,0:T(8,128)(2,1)}, u32[]{:S(2)}) copy-start(bf16[284,2272]{1,0:T(8,128)(2,1)} %param.19) | copy-start | bytes 3871492
  0.6 3.9 %collective-permute-start = (bf16[4,2,284]{2,1,0:T(2,128)(2,1)}, bf16[4,2,284]{2,1,0:T(2,128)(2,1)S(1)}, u32[]{:S(2)}, u32[]{:S(2)}) collective-permute-start(bf16[4,2,284]{2,1,0:T(2,128)(2,1)} %param.11), channel_id=1, source_target_pairs={{0,16},{16,0},{1,17},{17,1},{2,18},{18,2},{3,19},{19,3},{4,20},{20... | collective-permute-start | bytes 13640 | tf_op jit(solution)/shard_map/ppermute | solution.py:22
  5.3 4.7 %collective-permute-start.1 = (bf16[2,4,2,284]{3,2,1,0:T(2,128)(2,1)S(1)}, bf16[2,4,2,284]{3,2,1,0:T(2,128)(2,1)S(1)}, u32[]{:S(2)}, u32[]{:S(2)}) collective-permute-start(bf16[2,4,2,284]{3,2,1,0:T(2,128)(2,1)S(1)} %pad_maximum_fusion.8), channel_id=1, source_target_pairs={{0,8},{1,9},{2,10},{3,11},{4,12},{5,13},{6,14},{7,15},{8,0},{9,1},... | collective-permute-start | bytes 27272 | tf_op jit(solution)/shard_map/ppermute | solution.py:22
  10.0 3.9 %collective-permute-start.2 = (bf16[2,2,4,2,284]{4,3,2,1,0:T(2,128)(2,1)S(1)}, bf16[2,2,4,2,284]{4,3,2,1,0:T(2,128)(2,1)S(1)}, u32[]{:S(2)}, u32[]{:S(2)}) collective-permute-start(bf16[2,2,4,2,284]{4,3,2,1,0:T(2,128)(2,1)S(1)} %pad_maximum_fusion.6), channel_id=1, source_target_pairs={{0,4},{1,5},{2,6},{3,7},{4,0},{5,1},{6,2},{7,3},{8,12},{9,13},{10,... | collective-permute-start | bytes 54536 | tf_op jit(solution)/shard_map/ppermute | solution.py:22
  13.9 4.2 %collective-permute-start.3 = (bf16[2,2,2,4,2,284]{5,4,3,2,1,0:T(2,128)(2,1)S(1)}, bf16[2,2,2,4,2,284]{5,4,3,2,1,0:T(2,128)(2,1)S(1)}, u32[]{:S(2)}, u32[]{:S(2)}) collective-permute-start(bf16[2,2,2,4,2,284]{5,4,3,2,1,0:T(2,128)(2,1)S(1)} %pad_maximum_fusion.3), channel_id=1, source_target_pairs={{0,2},{1,3},{2,0},{3,1},{4,6},{5,7},{6,4},{7,5},{8,10},{9,11},{10,... | collective-permute-start | bytes 109064 | tf_op jit(solution)/shard_map/ppermute | solution.py:22
  18.3 1.4 %collective-permute-start.4 = (bf16[2,2,2,2,4,2,284]{6,5,4,3,2,1,0:T(2,128)(2,1)S(1)}, bf16[2,2,2,2,4,2,284]{6,5,4,3,2,1,0:T(2,128)(2,1)S(1)}, u32[]{:S(2)}, u32[]{:S(2)}) collective-permute-start(bf16[2,2,2,2,4,2,284]{6,5,4,3,2,1,0:T(2,128)(2,1)S(1)} %pad_maximum_fusion.1), channel_id=1, source_target_pairs={{0,1},{1,0},{2,3},{3,2},{4,5},{5,4},{6,7},{7,6},{8,9},{9,8},{10,11... | collective-permute-start | bytes 218120 | tf_op jit(solution)/shard_map/ppermute | solution.py:22
  22.1 2.0 %copy-start.1 = (bf16[2272,128]{1,0:T(8,128)(2,1)S(1)}, bf16[2272,128]{1,0:T(8,128)(2,1)}, u32[]{:S(2)}) copy-start(bf16[2272,128]{1,0:T(8,128)(2,1)} %param.18) | copy-start | bytes 1744900
  24.5 9.0 %copy-start.2 = (bf16[2,512,128]{2,1,0:T(8,128)(2,1)S(1)}, bf16[2,512,128]{2,1,0:T(8,128)(2,1)}, u32[]{:S(2)}) copy-start(bf16[2,512,128]{2,1,0:T(8,128)(2,1)} %param.12) | copy-start | bytes 786436
  24.5 4.0 %collective-permute-start.5 = (f32[16,412]{1,0:T(8,128)S(1)}, f32[16,412]{1,0:T(8,128)S(1)}, u32[]{:S(2)}, u32[]{:S(2)}) collective-permute-start(f32[16,412]{1,0:T(8,128)S(1)} %pad_maximum_fusion.5), channel_id=1, source_target_pairs={{0,16},{16,0},{1,17},{17,1},{2,18},{18,2},{3,19},{19,3},{4,20},{20... | collective-permute-start | bytes 79112 | tf_op jit(solution)/shard_map/ppermute | solution.py:40
  29.0 4.5 %collective-permute-start.7 = (bf16[4,2,284]{2,1,0:T(2,128)(2,1)S(1)}, bf16[4,2,284]{2,1,0:T(2,128)(2,1)S(1)}, u32[]{:S(2)}, u32[]{:S(2)}) collective-permute-start(bf16[4,2,284]{2,1,0:T(2,128)(2,1)S(1)} %slice.415), channel_id=1, source_target_pairs={{0,8},{1,9},{2,10},{3,11},{4,12},{5,13},{6,14},{7,15},{8,0},{9,1},... | collective-permute-start | bytes 13640 | tf_op jit(solution)/shard_map/ppermute | solution.py:22
  33.7 3.8 %collective-permute-start.8 = (bf16[2,4,2,284]{3,2,1,0:T(2,128)(2,1)S(1)}, bf16[2,4,2,284]{3,2,1,0:T(2,128)(2,1)S(1)}, u32[]{:S(2)}, u32[]{:S(2)}) collective-permute-start(bf16[2,4,2,284]{3,2,1,0:T(2,128)(2,1)S(1)} %pad_maximum_fusion.9), channel_id=1, source_target_pairs={{0,4},{1,5},{2,6},{3,7},{4,0},{5,1},{6,2},{7,3},{8,12},{9,13},{10,... | collective-permute-start | bytes 27272 | tf_op jit(solution)/shard_map/ppermute | solution.py:22
  37.5 3.9 %collective-permute-start.9 = (bf16[2,2,4,2,284]{4,3,2,1,0:T(2,128)(2,1)S(1)}, bf16[2,2,4,2,284]{4,3,2,1,0:T(2,128)(2,1)S(1)}, u32[]{:S(2)}, u32[]{:S(2)}) collective-permute-start(bf16[2,2,4,2,284]{4,3,2,1,0:T(2,128)(2,1)S(1)} %pad_maximum_fusion.7), channel_id=1, source_target_pairs={{0,2},{1,3},{2,0},{3,1},{4,6},{5,7},{6,4},{7,5},{8,10},{9,11},{10,... | collective-permute-start | bytes 54536 | tf_op jit(solution)/shard_map/ppermute | solution.py:22
  41.5 1.3 %collective-permute-start.10 = (bf16[2,2,2,4,2,284]{5,4,3,2,1,0:T(2,128)(2,1)S(1)}, bf16[2,2,2,4,2,284]{5,4,3,2,1,0:T(2,128)(2,1)S(1)}, u32[]{:S(2)}, u32[]{:S(2)}) collective-permute-start(bf16[2,2,2,4,2,284]{5,4,3,2,1,0:T(2,128)(2,1)S(1)} %pad_maximum_fusion.4), channel_id=1, source_target_pairs={{0,1},{1,0},{2,3},{3,2},{4,5},{5,4},{6,7},{7,6},{8,9},{9,8},{10,11... | collective-permute-start | bytes 109064 | tf_op jit(solution)/shard_map/ppermute | solution.py:22
  46.1 0.9 copy-start.4
  46.8 1.7 %collective-permute-start.11 = (bf16[2,284,70]{1,0,2:T(2,128)(2,1)S(1)}, bf16[2,284,70]{1,0,2:T(2,128)(2,1)S(1)}, u32[]{:S(2)}, u32[]{:S(2)}) collective-permute-start(bf16[2,284,70]{1,0,2:T(2,128)(2,1)S(1)} %fusion.18), channel_id=1, source_target_pairs={{0,1},{1,0},{2,3},{3,2},{4,5},{5,4},{6,7},{7,6},{8,9},{9,8},{10,11... | collective-permute-start | bytes 238568 | tf_op jit(solution)/shard_map/ppermute | solution.py:104
  47.1 4.5 %collective-permute-start.6 = (f32[16,1136]{1,0:T(8,128)S(1)}, f32[16,1136]{1,0:T(8,128)S(1)}, u32[]{:S(2)}, u32[]{:S(2)}) collective-permute-start(f32[16,1136]{1,0:T(8,128)S(1)} %fusion.181), channel_id=1, source_target_pairs={{0,16},{16,0},{1,17},{17,1},{2,18},{18,2},{3,19},{19,3},{4,20},{20... | collective-permute-start | bytes 218120 | tf_op jit(solution)/shard_map/ppermute | solution.py:40
  48.9 6.1 %collective-permute-start.12 = (bf16[2,284,70]{1,0,2:T(2,128)(2,1)S(1)}, bf16[2,284,70]{1,0,2:T(2,128)(2,1)S(1)}, u32[]{:S(2)}, u32[]{:S(2)}) collective-permute-start(bf16[2,284,70]{1,0,2:T(2,128)(2,1)S(1)} %fusion.19), channel_id=1, source_target_pairs={{0,2},{1,3},{2,0},{3,1},{4,6},{5,7},{6,4},{7,5},{8,10},{9,11},{10,... | collective-permute-start | bytes 238568 | tf_op jit(solution)/shard_map/ppermute | solution.py:104
  55.9 4.8 %collective-permute-start.13 = (bf16[2,284,70]{1,2,0:T(8,128)(2,1)S(1)}, bf16[2,284,70]{1,2,0:T(8,128)(2,1)S(1)}, u32[]{:S(2)}, u32[]{:S(2)}) collective-permute-start(bf16[2,284,70]{1,2,0:T(8,128)(2,1)S(1)} %concatenate.78), channel_id=1, source_target_pairs={{0,4},{1,5},{2,6},{3,7},{4,0},{5,1},{6,2},{7,3},{8,12},{9,13},{10,... | collective-permute-start | bytes 238568 | tf_op jit(solution)/shard_map/ppermute | solution.py:104
  63.2 4.7 %collective-permute-start.14 = (bf16[2,4,6,70]{3,2,1,0:T(8,128)(2,1)S(1)}, bf16[2,4,6,70]{3,2,1,0:T(8,128)(2,1)S(1)}, u32[]{:S(2)}, u32[]{:S(2)}) collective-permute-start(bf16[2,4,6,70]{3,2,1,0:T(8,128)(2,1)S(1)} %constant_dynamic-slice_fusion), channel_id=1, source_target_pairs={{0,8},{1,9},{2,10},{3,11},{4,12},{5,13},{6,14},{7,15},{8,0},{9,1},... | collective-permute-start | bytes 20168 | tf_op jit(solution)/shard_map/ppermute | solution.py:118
  68.7 3.6 %collective-permute-start.15 = (bf16[4,2,284]{2,0,1:T(4,128)(2,1)S(1)}, bf16[4,2,284]{2,0,1:T(4,128)(2,1)S(1)}, u32[]{:S(2)}, u32[]{:S(2)}) collective-permute-start(bf16[4,2,284]{2,0,1:T(4,128)(2,1)S(1)} %get-tuple-element.69), channel_id=1, source_target_pairs={{0,16},{16,0},{1,17},{17,1},{2,18},{18,2},{3,19},{19,3},{4,20},{20... | collective-permute-start | bytes 13640 | tf_op jit(solution)/shard_map/ppermute | solution.py:22
  73.5 18.9 %copy-start.3 = (bf16[4,2,284]{2,1,0:T(2,128)(2,1)S(1)}, bf16[4,2,284]{2,1,0:T(2,128)(2,1)}, u32[]{:S(2)}) copy-start(bf16[4,2,284]{2,1,0:T(2,128)(2,1)} %param.11) | copy-start | bytes 13636
  73.7 1.4 %collective-permute-start.16 = (f32[2,2,2,4,2,284]{5,4,3,2,1,0:T(2,128)S(1)}, f32[2,2,2,4,2,284]{5,4,3,2,1,0:T(2,128)S(1)}, u32[]{:S(2)}, u32[]{:S(2)}) collective-permute-start(f32[2,2,2,4,2,284]{5,4,3,2,1,0:T(2,128)S(1)} %fusion.17), channel_id=1, source_target_pairs={{0,1},{1,0},{2,3},{3,2},{4,5},{5,4},{6,7},{7,6},{8,9},{9,8},{10,11... | collective-permute-start | bytes 218120 | tf_op jit(solution)/shard_map/ppermute | solution.py:57
  75.1 4.2 %collective-permute-start.17 = (f32[2,2,4,2,284]{4,3,2,1,0:T(2,128)S(1)}, f32[2,2,4,2,284]{4,3,2,1,0:T(2,128)S(1)}, u32[]{:S(2)}, u32[]{:S(2)}) collective-permute-start(f32[2,2,4,2,284]{4,3,2,1,0:T(2,128)S(1)} %fusion.32), channel_id=1, source_target_pairs={{0,2},{1,3},{2,0},{3,1},{4,6},{5,7},{6,4},{7,5},{8,10},{9,11},{10,... | collective-permute-start | bytes 109064 | tf_op jit(solution)/shard_map/ppermute | solution.py:57
  79.3 3.9 %collective-permute-start.18 = (f32[2,4,2,284]{3,2,1,0:T(2,128)S(1)}, f32[2,4,2,284]{3,2,1,0:T(2,128)S(1)}, u32[]{:S(2)}, u32[]{:S(2)}) collective-permute-start(f32[2,4,2,284]{3,2,1,0:T(2,128)S(1)} %fusion.69), channel_id=1, source_target_pairs={{0,4},{1,5},{2,6},{3,7},{4,0},{5,1},{6,2},{7,3},{8,12},{9,13},{10,... | collective-permute-start | bytes 54536 | tf_op jit(solution)/shard_map/ppermute | solution.py:57
  83.3 7.4 %collective-permute-start.19 = (f32[4,2,284]{2,1,0:T(2,128)S(1)}, f32[4,2,284]{2,1,0:T(2,128)S(1)}, u32[]{:S(2)}, u32[]{:S(2)}) collective-permute-start(f32[4,2,284]{2,1,0:T(2,128)S(1)} %get-tuple-element.63), channel_id=1, source_target_pairs={{0,0},{1,1},{2,2},{3,3},{4,4},{5,5},{6,6},{7,7},{8,16},{9,17},{10,... | collective-permute-start | bytes 27272 | tf_op jit(solution)/shard_map/ppermute | solution.py:285
  88.6 3.7 %collective-permute-start.20 = (f32[4,2,284]{2,1,0:T(2,128)S(1)}, f32[4,2,284]{2,1,0:T(2,128)S(1)}, u32[]{:S(2)}, u32[]{:S(2)}) collective-permute-start(f32[4,2,284]{2,1,0:T(2,128)S(1)} %get-tuple-element.62), channel_id=1, source_target_pairs={{0,16},{1,17},{2,18},{3,19},{4,20},{5,21},{6,22},{7,23},{8,0},{9,1... | collective-permute-start | bytes 27272 | tf_op jit(solution)/shard_map/ppermute | solution.py:285

commit v11 on v10

--- a/solution.py
+++ b/solution.py
@@ -90,7 +90,7 @@
     return merged_peak, total, weighted
 
 
-def merge_over(peak, total, weighted, axis, size, carried, steps, chunk_width):
+def merge_over(peak, total, weighted, axis, size, carried, steps, chunk_width, cross=False):
     index = lax.axis_index(axis)
     group_rows, step_heads, head_width = weighted.shape
     head_count = step_heads // steps
@@ -112,16 +112,44 @@
         value = value.reshape((group_rows, steps, head_count) + value.shape[2:])
         return lax.dynamic_slice_in_dim(value, start, span, 2)
 
+    def finish(total, weighted):
+        mixed = (weighted / total[..., None]).reshape(group_rows, steps, span * head_width)
+        offset = index * chunk_width - own_start * head_width
+        return lax.dynamic_slice_in_dim(mixed, offset, chunk_width, 2)
+
     partner_start = first_head(index ^ bit)
     own_start = first_head(index)
     sent = window(pack_merge(peak, total, weighted), partner_start)
     other = lax.ppermute(sent, axis, xor_pairs(size, bit))
-    _, total, weighted = merge_pair(
+    results = []
+    if cross:
+        def whole(start):
+            return jnp.concatenate(
+                [window(peak, start)[..., None], window(total, start)[..., None], window(weighted, start)],
+                axis=-1,
+            )
+
+        same_routes = [(g * size + s, (1 - g) * size + s) for g in range(2) for s in range(size)]
+        partner_routes = [
+            (g * size + s, (1 - g) * size + (s ^ bit)) for g in range(2) for s in range(size)
+        ]
+        cross_same = lax.ppermute(whole(own_start), ALL, same_routes)
+        cross_partner = lax.ppermute(whole(partner_start), ALL, partner_routes)
+    _, own_total, own_weighted = merge_pair(
         window(peak, own_start), window(total, own_start), window(weighted, own_start), other
     )
-    mixed = (weighted / total[..., None]).reshape(group_rows, steps, span * head_width)
-    offset = index * chunk_width - own_start * head_width
-    return lax.dynamic_slice_in_dim(mixed, offset, chunk_width, 2), carried
+    results.append(finish(own_total, own_weighted))
+    if cross:
+        peak_first, peak_second = cross_same[..., 0], cross_partner[..., 0]
+        merged_peak = jnp.maximum(peak_first, peak_second)
+        scale_first = jnp.exp(peak_first - merged_peak)
+        scale_second = jnp.exp(peak_second - merged_peak)
+        cross_total = cross_same[..., 1] * scale_first + cross_partner[..., 1] * scale_second
+        cross_weighted = (
+            cross_same[..., 2:] * scale_first[..., None] + cross_partner[..., 2:] * scale_second[..., None]
+        )
+        results.append(finish(cross_total, cross_weighted))
+    return results, carried
 
 
 def layer_norm(row_block, norm_gain, norm_bias):
@@ -248,16 +276,26 @@
         "gqs,gsd->gqd", weights, value_rows, preferred_element_type=jnp.float32
     )
 
-    own_mixed, down_part = merge_over(
-        local_peak, local_total, local_weighted, "seq", seq_size, down_part, steps, slice_width
-    )
-    own_mixed = own_mixed.transpose(1, 0, 2).astype(jnp.bfloat16)
-    every_mixed = gather_xor(own_mixed, "req", req_size)[0]
+    fold = req_size == 2
+    chunk_mixed, down_part = merge_over(
+        local_peak, local_total, local_weighted, "seq", seq_size, down_part, steps, slice_width, fold
+    )
+    chunk_mixed = [part.transpose(1, 0, 2).astype(jnp.bfloat16) for part in chunk_mixed]
     serves = placement[:, None] == request_ids[None, :]
     inverse = jnp.sum(jnp.where(serves, request_ids[:, None], 0), axis=0)
-    mixed_rows = xor_slot(group_index ^ (inverse // group_rows), req_size) * group_rows + (
-        inverse % group_rows
-    )
+    if fold:
+        own_mixed, other_mixed = chunk_mixed
+        every_mixed = jnp.where(
+            group_index == 0,
+            jnp.stack([own_mixed, other_mixed]),
+            jnp.stack([other_mixed, own_mixed]),
+        )
+        mixed_rows = inverse
+    else:
+        every_mixed = gather_xor(chunk_mixed[0], "req", req_size)[0]
+        mixed_rows = xor_slot(group_index ^ (inverse // group_rows), req_size) * group_rows + (
+            inverse % group_rows
+        )
     mixed_part = every_mixed.transpose(1, 0, 2, 3).reshape(steps, total, slice_width)
     mixed_part = jnp.take(mixed_part, mixed_rows, axis=1, mode="clip").reshape(rows, slice_width)
 

time: 94 us -> 98 us (1.043)
  starting transfers between devices: 30.1 us -> 32.2 us
  local copies, waits for them, and re-layouts: 12.4 us -> 13.4 us
    ppermute x0 -> x2, starting transfers between devices: none -> 4.17 us  [the longest x1 2.73 us: merge_over(): cross_partner = lax.ppermute(whole(partner_start), ALL, partner_routes)]
    ppermute x0 -> x2, waiting for transfers between devices: none -> 2.97 us  [the longest x1 2.97 us: merge_over(): cross_partner = lax.ppermute(whole(partner_start), ALL, partner_routes)]
    ppermute x10 -> x9, waiting for transfers between devices: 16 us -> 13.7 us  [gather_xor(): lax.ppermute(stacked, axis, xor_pairs(size, bit))]
    ppermute x10 -> x9, starting transfers between devices: 13.3 us -> 11.9 us  [gather_xor(): lax.ppermute(stacked, axis, xor_pairs(size, bit))]
    another operation x15 -> x14, other arithmetic: 2.65 us -> 2.63 us  [gather_xor(): jnp.stack([stacked, lax.ppermute(stacked, axis, xor_pairs(size, bit))])]
  transfers between devices with their start and end apart: 21 -> 22, of which waited for: 18 -> 18; matrix products, arithmetic and copies ran while one was open for 15% -> 16% of each run, Pallas kernels for 0% -> 0%
where the time goes in v11:
time: 98 us; the launch traced here: 96.9 us
  starting transfers between devices  32.2 us (33%)
  waiting for transfers between devices  31 us (32%)
  local copies, waits for them, and re-layouts  13.4 us (14%)
  matrix products  9.94 us (10%)
  other arithmetic  8.92 us (9%)
  between operations  1.51 us (2%)
    ppermute x9, waiting for transfers between devices, gather_xor(): lax.ppermute(stacked, axis, xor_pairs(size, bit))  13.7 us
    ppermute x9, starting transfers between devices, gather_xor(): lax.ppermute(stacked, axis, xor_pairs(size, bit))  11.9 us
    ppermute x3, waiting for transfers between devices, scatter_sum(): blocks = keep + lax.ppermute(send, axis, xor_pairs(size, bit))  6.08 us
    ppermute x1, starting transfers between devices, shards(): lax.ppermute(own_block, ALL, own_routes)  4.59 us
    ppermute x3, starting transfers between devices, merge_over(): lax.ppermute(pack_merge(peak, total, weighted), axis, xor_pairs(size, bit))  3.45 us
    dot_general x1, matrix products, shards(): down_part = jnp.dot(hidden, w_down, preferred_element_type=jnp.float32)  3.39 us
    dot_general x1, matrix products, shards(): part_up = jnp.dot(normed_part, w_up, preferred_element_type=jnp.float32)  3.32 us
    ppermute x3, starting transfers between devices, scatter_sum(): blocks = keep + lax.ppermute(send, axis, xor_pairs(size, bit))  3.3 us
  transfers between devices with their start and end apart: 22, of which 18 were waited for; matrix products, arithmetic and copies ran while one was open for 16% of the time, Pallas kernels for 0%

profile of v11, /device:TPU:2, one launch (start us, length us, event | category | flops | bytes accessed | tf_op | source)
XLA Modules:
  0.0 96.9 jit_solution(18416063735811282578)
XLA Ops:
  0.8 0.8 dynamic_slice.37
  1.7 0.8 select_reduce_fusion.2
  3.3 1.3 %collective-permute-done = bf16[4,2,284]{2,1,0:T(2,128)(2,1)S(1)} collective-permute-done((bf16[4,2,284]{2,1,0:T(2,128)(2,1)}, bf16[4,2,284]{2,1,0:T(2,128)(2,1)S(1)}, u32[]{:S(2)}, u32[]{:S(2)}) %collective-permute-start) | collective-permute-done | bytes 4576 | tf_op jit(solution)/shard_map/ppermute | solution.py:22
  4.5 0.7 pad_maximum_fusion.10
  5.3 2.7 %collective-permute-start.1 = (bf16[2,4,2,284]{3,2,1,0:T(2,128)(2,1)S(1)}, bf16[2,4,2,284]{3,2,1,0:T(2,128)(2,1)S(1)}, u32[]{:S(2)}, u32[]{:S(2)}) collective-permute-start(bf16[2,4,2,284]{3,2,1,0:T(2,128)(2,1)S(1)} %pad_maximum_fusion.10), channel_id=1, source_target_pairs={{0,8},{1,9},{2,10},{3,11},{4,12},{5,13},{6,14},{7,15},{8,0},{9,1},... | collective-permute-start | bytes 27272 | tf_op jit(solution)/shard_map/ppermute | solution.py:22
  7.9 0.7 fusion.198
  8.6 1.3 %collective-permute-done.1 = bf16[2,4,2,284]{3,2,1,0:T(2,128)(2,1)S(1)} collective-permute-done((bf16[2,4,2,284]{3,2,1,0:T(2,128)(2,1)S(1)}, bf16[2,4,2,284]{3,2,1,0:T(2,128)(2,1)S(1)}, u32[]{:S(2)}, u32[]{:S(2)}) %collective-permute-start.1) | collective-permute-done | bytes 9120 | tf_op jit(solution)/shard_map/ppermute | solution.py:22
  10.0 1.6 %collective-permute-start.2 = (bf16[2,2,4,2,284]{4,3,2,1,0:T(2,128)(2,1)S(1)}, bf16[2,2,4,2,284]{4,3,2,1,0:T(2,128)(2,1)S(1)}, u32[]{:S(2)}, u32[]{:S(2)}) collective-permute-start(bf16[2,2,4,2,284]{4,3,2,1,0:T(2,128)(2,1)S(1)} %pad_maximum_fusion.8), channel_id=1, source_target_pairs={{0,4},{1,5},{2,6},{3,7},{4,0},{5,1},{6,2},{7,3},{8,12},{9,13},{10,... | collective-permute-start | bytes 54536 | tf_op jit(solution)/shard_map/ppermute | solution.py:22
  11.8 0.8 dynamic-slice
  12.6 0.8 dynamic-slice.1
  13.9 1.6 %collective-permute-start.3 = (bf16[2,2,2,4,2,284]{5,4,3,2,1,0:T(2,128)(2,1)S(1)}, bf16[2,2,2,4,2,284]{5,4,3,2,1,0:T(2,128)(2,1)S(1)}, u32[]{:S(2)}, u32[]{:S(2)}) collective-permute-start(bf16[2,2,2,4,2,284]{5,4,3,2,1,0:T(2,128)(2,1)S(1)} %pad_maximum_fusion.3), channel_id=1, source_target_pairs={{0,2},{1,3},{2,0},{3,1},{4,6},{5,7},{6,4},{7,5},{8,10},{9,11},{10,... | collective-permute-start | bytes 109064 | tf_op jit(solution)/shard_map/ppermute | solution.py:22
  15.6 2.5 %collective-permute-done.3 = bf16[2,2,2,4,2,284]{5,4,3,2,1,0:T(2,128)(2,1)S(1)} collective-permute-done((bf16[2,2,2,4,2,284]{5,4,3,2,1,0:T(2,128)(2,1)S(1)}, bf16[2,2,2,4,2,284]{5,4,3,2,1,0:T(2,128)(2,1)S(1)}, u32[]{:S(2)}, u32[]{:S(2)}) %collective-permute-start.3) | collective-permute-done | bytes 36384 | tf_op jit(solution)/shard_map/ppermute | solution.py:22
  18.5 1.1 %collective-permute-done.4 = bf16[2,2,2,2,4,2,284]{6,5,4,3,2,1,0:T(2,128)(2,1)S(1)} collective-permute-done((bf16[2,2,2,2,4,2,284]{6,5,4,3,2,1,0:T(2,128)(2,1)S(1)}, bf16[2,2,2,2,4,2,284]{6,5,4,3,2,1,0:T(2,128)(2,1)S(1)}, u32[]{:S(2)}, u32[]{:S(2)}) %collective-permute-start.4) | collective-permute-done | bytes 72736 | tf_op jit(solution)/shard_map/ppermute | solution.py:22
  19.9 1.0 %gather_fusion = bf16[32,4,2,284]{3,2,1,0:T(2,128)(2,1)S(1)} fusion(bf16[32,4,2,284]{3,2,1,0:T(2,128)(2,1)S(1)} %bitcast.280, s32[1024]{0:T(1024)S(1)} %get-tuple-element.111), kind=kCustom, calls=%fused_computation | custom fusion | bytes 290944 | tf_op jit(solution)/shard_map/jit(_take)/gather | solution.py:214
  22.4 1.8 %fusion.183 = f32[16,284]{1,0:T(8,128)S(1)} fusion(bf16[2272,284]{0,1:T(8,128)(2,1)} %param.17, f32[16,4544]{1,0:T(8,128)S(1)} %reshape.779, s32[]{:T(128)S(6)} %select_n.313, f32[2272]{0:T(1024)S(1)} %dynamic-slice.1, f32[2272]{0:T(1024)S(1)} %dynamic-slice, f32[16]{0:T(128)S(1)} %rsqrt.12, f32[16]{0:T(128)S(1)} %div.133), kind=kOutput, calls=%fused_computation.407 | convolution fusion | flops 20829696 | bytes 1481732 | tf_op jit(solution)/shard_map/dot_general | solution.py:219
  24.5 0.7 collective-permute-start.5
  25.2 3.3 %fusion.185 = f32[16,1136]{1,0:T(8,128)S(1)} fusion(bf16[2272,1136]{1,0:T(8,128)(2,1)} %param.20, f32[16,4544]{1,0:T(8,128)S(1)} %reshape.779, s32[]{:T(128)S(6)} %select_n.313, f32[2272]{0:T(1024)S(1)} %dynamic-slice.1, f32[2272]{0:T(1024)S(1)} %dynamic-slice, f32[16]{0:T(128)S(1)} %rsqrt.12, f32[16]{0:T(128)S(1)} %div.133), kind=kOutput, calls=%fused_computation.408 | convolution fusion | flops 82773504 | bytes 5407748 | tf_op jit(solution)/shard_map/dot_general | solution.py:222
  29.0 2.6 %collective-permute-start.7 = (bf16[4,2,284]{2,1,0:T(2,128)(2,1)S(1)}, bf16[4,2,284]{2,1,0:T(2,128)(2,1)S(1)}, u32[]{:S(2)}, u32[]{:S(2)}) collective-permute-start(bf16[4,2,284]{2,1,0:T(2,128)(2,1)S(1)} %slice.481), channel_id=1, source_target_pairs={{0,8},{1,9},{2,10},{3,11},{4,12},{5,13},{6,14},{7,15},{8,0},{9,1},... | collective-permute-start | bytes 13640 | tf_op jit(solution)/shard_map/ppermute | solution.py:22
  31.7 1.8 %collective-permute-done.7 = bf16[4,2,284]{2,1,0:T(2,128)(2,1)S(1)} collective-permute-done((bf16[4,2,284]{2,1,0:T(2,128)(2,1)S(1)}, bf16[4,2,284]{2,1,0:T(2,128)(2,1)S(1)}, u32[]{:S(2)}, u32[]{:S(2)}) %collective-permute-start.7) | collective-permute-done | bytes 4576 | tf_op jit(solution)/shard_map/ppermute | solution.py:22
  33.7 1.6 %collective-permute-start.8 = (bf16[2,4,2,284]{3,2,1,0:T(2,128)(2,1)S(1)}, bf16[2,4,2,284]{3,2,1,0:T(2,128)(2,1)S(1)}, u32[]{:S(2)}, u32[]{:S(2)}) collective-permute-start(bf16[2,4,2,284]{3,2,1,0:T(2,128)(2,1)S(1)} %pad_maximum_fusion.11), channel_id=1, source_target_pairs={{0,4},{1,5},{2,6},{3,7},{4,0},{5,1},{6,2},{7,3},{8,12},{9,13},{10,... | collective-permute-start | bytes 27272 | tf_op jit(solution)/shard_map/ppermute | solution.py:22
  35.6 1.9 %collective-permute-done.8 = bf16[2,4,2,284]{3,2,1,0:T(2,128)(2,1)S(1)} collective-permute-done((bf16[2,4,2,284]{3,2,1,0:T(2,128)(2,1)S(1)}, bf16[2,4,2,284]{3,2,1,0:T(2,128)(2,1)S(1)}, u32[]{:S(2)}, u32[]{:S(2)}) %collective-permute-start.8) | collective-permute-done | bytes 9120 | tf_op jit(solution)/shard_map/ppermute | solution.py:22
  37.5 1.6 %collective-permute-start.9 = (bf16[2,2,4,2,284]{4,3,2,1,0:T(2,128)(2,1)S(1)}, bf16[2,2,4,2,284]{4,3,2,1,0:T(2,128)(2,1)S(1)}, u32[]{:S(2)}, u32[]{:S(2)}) collective-permute-start(bf16[2,2,4,2,284]{4,3,2,1,0:T(2,128)(2,1)S(1)} %pad_maximum_fusion.9), channel_id=1, source_target_pairs={{0,2},{1,3},{2,0},{3,1},{4,6},{5,7},{6,4},{7,5},{8,10},{9,11},{10,... | collective-permute-start | bytes 54536 | tf_op jit(solution)/shard_map/ppermute | solution.py:22
  39.1 2.3 %collective-permute-done.9 = bf16[2,2,4,2,284]{4,3,2,1,0:T(2,128)(2,1)S(1)} collective-permute-done((bf16[2,2,4,2,284]{4,3,2,1,0:T(2,128)(2,1)S(1)}, bf16[2,2,4,2,284]{4,3,2,1,0:T(2,128)(2,1)S(1)}, u32[]{:S(2)}, u32[]{:S(2)}) %collective-permute-start.9) | collective-permute-done | bytes 18208 | tf_op jit(solution)/shard_map/ppermute | solution.py:22
  41.6 1.1 %collective-permute-done.10 = bf16[2,2,2,4,2,284]{5,4,3,2,1,0:T(2,128)(2,1)S(1)} collective-permute-done((bf16[2,2,2,4,2,284]{5,4,3,2,1,0:T(2,128)(2,1)S(1)}, bf16[2,2,2,4,2,284]{5,4,3,2,1,0:T(2,128)(2,1)S(1)}, u32[]{:S(2)}, u32[]{:S(2)}) %collective-permute-start.10) | collective-permute-done | bytes 36384 | tf_op jit(solution)/shard_map/ppermute | solution.py:22
  43.0 0.6 gather_fusion.1
  47.1 1.4 %collective-permute-start.6 = (f32[16,1136]{1,0:T(8,128)S(1)}, f32[16,1136]{1,0:T(8,128)S(1)}, u32[]{:S(2)}, u32[]{:S(2)}) collective-permute-start(f32[16,1136]{1,0:T(8,128)S(1)} %fusion.185), channel_id=1, source_target_pairs={{0,16},{16,0},{1,17},{17,1},{2,18},{18,2},{3,19},{19,3},{4,20},{20... | collective-permute-start | bytes 218120 | tf_op jit(solution)/shard_map/ppermute | solution.py:40
  48.9 1.6 %collective-permute-start.12 = (bf16[2,284,70]{1,0,2:T(2,128)(2,1)S(1)}, bf16[2,284,70]{1,0,2:T(2,128)(2,1)S(1)}, u32[]{:S(2)}, u32[]{:S(2)}) collective-permute-start(bf16[2,284,70]{1,0,2:T(2,128)(2,1)S(1)} %fusion.19), channel_id=1, source_target_pairs={{0,2},{1,3},{2,0},{3,1},{4,6},{5,7},{6,4},{7,5},{8,10},{9,11},{10,... | collective-permute-start | bytes 238568 | tf_op jit(solution)/shard_map/ppermute | solution.py:104
  50.5 1.1 %collective-permute-done.6 = f32[16,1136]{1,0:T(8,128)S(1)} collective-permute-done((f32[16,1136]{1,0:T(8,128)S(1)}, f32[16,1136]{1,0:T(8,128)S(1)}, u32[]{:S(2)}, u32[]{:S(2)}) %collective-permute-start.6) | collective-permute-done | bytes 72736 | tf_op jit(solution)/shard_map/ppermute | solution.py:40
  51.6 3.4 %fusion.35 = f32[16,2272]{1,0:T(8,128)S(1)} fusion(bf16[1136,2272]{1,0:T(8,128)(2,1)} %param.21, f32[16,1136]{1,0:T(8,128)S(1)} %fusion.185, f32[16,1136]{1,0:T(8,128)S(1)} %collective-permute-done.6), kind=kOutput, calls=%fused_computation.76 | convolution fusion | flops 83791360 | bytes 5452800 | tf_op jit(solution)/shard_map/dot_general | solution.py:237
  55.4 0.6 concatenate.84
  55.9 1.6 %collective-permute-start.13 = (bf16[2,284,70]{1,2,0:T(8,128)(2,1)S(1)}, bf16[2,284,70]{1,2,0:T(8,128)(2,1)S(1)}, u32[]{:S(2)}, u32[]{:S(2)}) collective-permute-start(bf16[2,284,70]{1,2,0:T(8,128)(2,1)S(1)} %concatenate.84), channel_id=1, source_target_pairs={{0,4},{1,5},{2,6},{3,7},{4,0},{5,1},{6,2},{7,3},{8,12},{9,13},{10,... | collective-permute-start | bytes 238568 | tf_op jit(solution)/shard_map/ppermute | solution.py:104
  57.6 3.2 %collective-permute-done.13 = bf16[2,284,70]{1,2,0:T(8,128)(2,1)S(1)} collective-permute-done((bf16[2,284,70]{1,2,0:T(8,128)(2,1)S(1)}, bf16[2,284,70]{1,2,0:T(8,128)(2,1)S(1)}, u32[]{:S(2)}, u32[]{:S(2)}) %collective-permute-start.13) | collective-permute-done | bytes 79552 | tf_op jit(solution)/shard_map/ppermute | solution.py:104
  63.2 2.6 %collective-permute-start.14 = (bf16[2,4,6,70]{3,2,1,0:T(8,128)(2,1)S(1)}, bf16[2,4,6,70]{3,2,1,0:T(8,128)(2,1)S(1)}, u32[]{:S(2)}, u32[]{:S(2)}) collective-permute-start(bf16[2,4,6,70]{3,2,1,0:T(8,128)(2,1)S(1)} %constant_dynamic-slice_fusion.1), channel_id=1, source_target_pairs={{0,8},{1,9},{2,10},{3,11},{4,12},{5,13},{6,14},{7,15},{8,0},{9,1},... | collective-permute-start | bytes 20168 | tf_op jit(solution)/shard_map/ppermute | solution.py:123
  66.9 1.1 %collective-permute-done.14 = bf16[2,4,6,70]{3,2,1,0:T(8,128)(2,1)S(1)} collective-permute-done((bf16[2,4,6,70]{3,2,1,0:T(8,128)(2,1)S(1)}, bf16[2,4,6,70]{3,2,1,0:T(8,128)(2,1)S(1)}, u32[]{:S(2)}, u32[]{:S(2)}) %collective-permute-start.14) | collective-permute-done | bytes 6752 | tf_op jit(solution)/shard_map/ppermute | solution.py:123
  69.0 1.4 %collective-permute-start.15 = (f32[2,4,6,66]{3,2,1,0:T(8,128)S(1)}, f32[2,4,6,66]{3,2,1,0:T(8,128)S(1)}, u32[]{:S(2)}, u32[]{:S(2)}) collective-permute-start(f32[2,4,6,66]{3,2,1,0:T(8,128)S(1)} %pad_maximum_fusion.6), channel_id=1, source_target_pairs={{0,16},{1,17},{2,18},{3,19},{4,20},{5,21},{6,22},{7,23},{8,24},{9,... | collective-permute-start | bytes 38024 | tf_op jit(solution)/shard_map/ppermute | solution.py:136
  70.8 2.7 %collective-permute-start.16 = (f32[2,4,6,66]{3,2,1,0:T(8,128)S(1)}, f32[2,4,6,66]{3,2,1,0:T(8,128)S(1)}, u32[]{:S(2)}, u32[]{:S(2)}) collective-permute-start(f32[2,4,6,66]{3,2,1,0:T(8,128)S(1)} %pad_maximum_fusion.7), channel_id=1, source_target_pairs={{0,24},{1,25},{2,26},{3,27},{4,28},{5,29},{6,30},{7,31},{8,16},{9,... | collective-permute-start | bytes 38024 | tf_op jit(solution)/shard_map/ppermute | solution.py:137
  73.6 3.0 %collective-permute-done.16 = f32[2,4,6,66]{3,2,1,0:T(8,128)S(1)} collective-permute-done((f32[2,4,6,66]{3,2,1,0:T(8,128)S(1)}, f32[2,4,6,66]{3,2,1,0:T(8,128)S(1)}, u32[]{:S(2)}, u32[]{:S(2)}) %collective-permute-start.16) | collective-permute-done | bytes 12704 | tf_op jit(solution)/shard_map/ppermute | solution.py:137
  77.1 0.6 gather_fusion.2
  78.5 1.3 %collective-permute-done.17 = f32[2,2,2,4,2,284]{5,4,3,2,1,0:T(2,128)S(1)} collective-permute-done((f32[2,2,2,4,2,284]{5,4,3,2,1,0:T(2,128)S(1)}, f32[2,2,2,4,2,284]{5,4,3,2,1,0:T(2,128)S(1)}, u32[]{:S(2)}, u32[]{:S(2)}) %collective-permute-start.17) | collective-permute-done | bytes 72736 | tf_op jit(solution)/shard_map/ppermute | solution.py:57
  79.8 1.6 %collective-permute-start.18 = (f32[2,2,4,2,284]{4,3,2,1,0:T(2,128)S(1)}, f32[2,2,4,2,284]{4,3,2,1,0:T(2,128)S(1)}, u32[]{:S(2)}, u32[]{:S(2)}) collective-permute-start(f32[2,2,4,2,284]{4,3,2,1,0:T(2,128)S(1)} %fusion.32), channel_id=1, source_target_pairs={{0,2},{1,3},{2,0},{3,1},{4,6},{5,7},{6,4},{7,5},{8,10},{9,11},{10,... | collective-permute-start | bytes 109064 | tf_op jit(solution)/shard_map/ppermute | solution.py:57
  81.4 2.6 %collective-permute-done.18 = f32[2,2,4,2,284]{4,3,2,1,0:T(2,128)S(1)} collective-permute-done((f32[2,2,4,2,284]{4,3,2,1,0:T(2,128)S(1)}, f32[2,2,4,2,284]{4,3,2,1,0:T(2,128)S(1)}, u32[]{:S(2)}, u32[]{:S(2)}) %collective-permute-start.18) | collective-permute-done | bytes 36384 | tf_op jit(solution)/shard_map/ppermute | solution.py:57
  84.0 1.6 %collective-permute-start.19 = (f32[2,4,2,284]{3,2,1,0:T(2,128)S(1)}, f32[2,4,2,284]{3,2,1,0:T(2,128)S(1)}, u32[]{:S(2)}, u32[]{:S(2)}) collective-permute-start(f32[2,4,2,284]{3,2,1,0:T(2,128)S(1)} %fusion.75), channel_id=1, source_target_pairs={{0,4},{1,5},{2,6},{3,7},{4,0},{5,1},{6,2},{7,3},{8,12},{9,13},{10,... | collective-permute-start | bytes 54536 | tf_op jit(solution)/shard_map/ppermute | solution.py:57
  85.7 2.3 %collective-permute-done.19 = f32[2,4,2,284]{3,2,1,0:T(2,128)S(1)} collective-permute-done((f32[2,4,2,284]{3,2,1,0:T(2,128)S(1)}, f32[2,4,2,284]{3,2,1,0:T(2,128)S(1)}, u32[]{:S(2)}, u32[]{:S(2)}) %collective-permute-start.19) | collective-permute-done | bytes 18208 | tf_op jit(solution)/shard_map/ppermute | solution.py:57
  88.0 4.6 %collective-permute-start.20 = (f32[4,2,284]{2,1,0:T(2,128)S(1)}, f32[4,2,284]{2,1,0:T(2,128)S(1)}, u32[]{:S(2)}, u32[]{:S(2)}) collective-permute-start(f32[4,2,284]{2,1,0:T(2,128)S(1)} %get-tuple-element.68), channel_id=1, source_target_pairs={{0,0},{1,1},{2,2},{3,3},{4,4},{5,5},{6,6},{7,7},{8,16},{9,17},{10,... | collective-permute-start | bytes 27272 | tf_op jit(solution)/shard_map/ppermute | solution.py:323
  92.6 0.8 copy.276
  93.5 1.9 %collective-permute-done.20 = f32[4,2,284]{2,1,0:T(2,128)S(1)} collective-permute-done((f32[4,2,284]{2,1,0:T(2,128)S(1)}, f32[4,2,284]{2,1,0:T(2,128)S(1)}, u32[]{:S(2)}, u32[]{:S(2)}) %collective-permute-start.20) | collective-permute-done | bytes 9120 | tf_op jit(solution)/shard_map/ppermute | solution.py:323
  95.4 1.0 collective-permute-done.21
  96.3 0.6 add_convert_fusion
  (184 shorter events, 16.0 us)
Async XLA Ops:
  0.6 77.1 %copy-start = (bf16[284,2272]{1,0:T(8,128)(2,1)S(1)}, bf16[284,2272]{1,0:T(8,128)(2,1)}, u32[]{:S(2)}) copy-start(bf16[284,2272]{1,0:T(8,128)(2,1)} %param.19) | copy-start | bytes 3871492
  0.6 3.9 %collective-permute-start = (bf16[4,2,284]{2,1,0:T(2,128)(2,1)}, bf16[4,2,284]{2,1,0:T(2,128)(2,1)S(1)}, u32[]{:S(2)}, u32[]{:S(2)}) collective-permute-start(bf16[4,2,284]{2,1,0:T(2,128)(2,1)} %param.11), channel_id=1, source_target_pairs={{0,16},{16,0},{1,17},{17,1},{2,18},{18,2},{3,19},{19,3},{4,20},{20... | collective-permute-start | bytes 13640 | tf_op jit(solution)/shard_map/ppermute | solution.py:22
  5.3 4.7 %collective-permute-start.1 = (bf16[2,4,2,284]{3,2,1,0:T(2,128)(2,1)S(1)}, bf16[2,4,2,284]{3,2,1,0:T(2,128)(2,1)S(1)}, u32[]{:S(2)}, u32[]{:S(2)}) collective-permute-start(bf16[2,4,2,284]{3,2,1,0:T(2,128)(2,1)S(1)} %pad_maximum_fusion.10), channel_id=1, source_target_pairs={{0,8},{1,9},{2,10},{3,11},{4,12},{5,13},{6,14},{7,15},{8,0},{9,1},... | collective-permute-start | bytes 27272 | tf_op jit(solution)/shard_map/ppermute | solution.py:22
  10.0 3.9 %collective-permute-start.2 = (bf16[2,2,4,2,284]{4,3,2,1,0:T(2,128)(2,1)S(1)}, bf16[2,2,4,2,284]{4,3,2,1,0:T(2,128)(2,1)S(1)}, u32[]{:S(2)}, u32[]{:S(2)}) collective-permute-start(bf16[2,2,4,2,284]{4,3,2,1,0:T(2,128)(2,1)S(1)} %pad_maximum_fusion.8), channel_id=1, source_target_pairs={{0,4},{1,5},{2,6},{3,7},{4,0},{5,1},{6,2},{7,3},{8,12},{9,13},{10,... | collective-permute-start | bytes 54536 | tf_op jit(solution)/shard_map/ppermute | solution.py:22
  13.9 4.2 %collective-permute-start.3 = (bf16[2,2,2,4,2,284]{5,4,3,2,1,0:T(2,128)(2,1)S(1)}, bf16[2,2,2,4,2,284]{5,4,3,2,1,0:T(2,128)(2,1)S(1)}, u32[]{:S(2)}, u32[]{:S(2)}) collective-permute-start(bf16[2,2,2,4,2,284]{5,4,3,2,1,0:T(2,128)(2,1)S(1)} %pad_maximum_fusion.3), channel_id=1, source_target_pairs={{0,2},{1,3},{2,0},{3,1},{4,6},{5,7},{6,4},{7,5},{8,10},{9,11},{10,... | collective-permute-start | bytes 109064 | tf_op jit(solution)/shard_map/ppermute | solution.py:22
  18.3 1.4 %collective-permute-start.4 = (bf16[2,2,2,2,4,2,284]{6,5,4,3,2,1,0:T(2,128)(2,1)S(1)}, bf16[2,2,2,2,4,2,284]{6,5,4,3,2,1,0:T(2,128)(2,1)S(1)}, u32[]{:S(2)}, u32[]{:S(2)}) collective-permute-start(bf16[2,2,2,2,4,2,284]{6,5,4,3,2,1,0:T(2,128)(2,1)S(1)} %pad_maximum_fusion.1), channel_id=1, source_target_pairs={{0,1},{1,0},{2,3},{3,2},{4,5},{5,4},{6,7},{7,6},{8,9},{9,8},{10,11... | collective-permute-start | bytes 218120 | tf_op jit(solution)/shard_map/ppermute | solution.py:22
  22.1 2.0 %copy-start.1 = (bf16[2272,128]{1,0:T(8,128)(2,1)S(1)}, bf16[2272,128]{1,0:T(8,128)(2,1)}, u32[]{:S(2)}) copy-start(bf16[2272,128]{1,0:T(8,128)(2,1)} %param.18) | copy-start | bytes 1744900
  24.5 9.0 %copy-start.2 = (bf16[2,512,128]{2,1,0:T(8,128)(2,1)S(1)}, bf16[2,512,128]{2,1,0:T(8,128)(2,1)}, u32[]{:S(2)}) copy-start(bf16[2,512,128]{2,1,0:T(8,128)(2,1)} %param.12) | copy-start | bytes 786436
  24.5 4.0 %collective-permute-start.5 = (f32[16,412]{1,0:T(8,128)S(1)}, f32[16,412]{1,0:T(8,128)S(1)}, u32[]{:S(2)}, u32[]{:S(2)}) collective-permute-start(f32[16,412]{1,0:T(8,128)S(1)} %pad_maximum_fusion.5), channel_id=1, source_target_pairs={{0,16},{16,0},{1,17},{17,1},{2,18},{18,2},{3,19},{19,3},{4,20},{20... | collective-permute-start | bytes 79112 | tf_op jit(solution)/shard_map/ppermute | solution.py:40
  29.0 4.5 %collective-permute-start.7 = (bf16[4,2,284]{2,1,0:T(2,128)(2,1)S(1)}, bf16[4,2,284]{2,1,0:T(2,128)(2,1)S(1)}, u32[]{:S(2)}, u32[]{:S(2)}) collective-permute-start(bf16[4,2,284]{2,1,0:T(2,128)(2,1)S(1)} %slice.481), channel_id=1, source_target_pairs={{0,8},{1,9},{2,10},{3,11},{4,12},{5,13},{6,14},{7,15},{8,0},{9,1},... | collective-permute-start | bytes 13640 | tf_op jit(solution)/shard_map/ppermute | solution.py:22
  33.7 3.8 %collective-permute-start.8 = (bf16[2,4,2,284]{3,2,1,0:T(2,128)(2,1)S(1)}, bf16[2,4,2,284]{3,2,1,0:T(2,128)(2,1)S(1)}, u32[]{:S(2)}, u32[]{:S(2)}) collective-permute-start(bf16[2,4,2,284]{3,2,1,0:T(2,128)(2,1)S(1)} %pad_maximum_fusion.11), channel_id=1, source_target_pairs={{0,4},{1,5},{2,6},{3,7},{4,0},{5,1},{6,2},{7,3},{8,12},{9,13},{10,... | collective-permute-start | bytes 27272 | tf_op jit(solution)/shard_map/ppermute | solution.py:22
  37.5 3.9 %collective-permute-start.9 = (bf16[2,2,4,2,284]{4,3,2,1,0:T(2,128)(2,1)S(1)}, bf16[2,2,4,2,284]{4,3,2,1,0:T(2,128)(2,1)S(1)}, u32[]{:S(2)}, u32[]{:S(2)}) collective-permute-start(bf16[2,2,4,2,284]{4,3,2,1,0:T(2,128)(2,1)S(1)} %pad_maximum_fusion.9), channel_id=1, source_target_pairs={{0,2},{1,3},{2,0},{3,1},{4,6},{5,7},{6,4},{7,5},{8,10},{9,11},{10,... | collective-permute-start | bytes 54536 | tf_op jit(solution)/shard_map/ppermute | solution.py:22
  41.5 1.3 %collective-permute-start.10 = (bf16[2,2,2,4,2,284]{5,4,3,2,1,0:T(2,128)(2,1)S(1)}, bf16[2,2,2,4,2,284]{5,4,3,2,1,0:T(2,128)(2,1)S(1)}, u32[]{:S(2)}, u32[]{:S(2)}) collective-permute-start(bf16[2,2,2,4,2,284]{5,4,3,2,1,0:T(2,128)(2,1)S(1)} %pad_maximum_fusion.4), channel_id=1, source_target_pairs={{0,1},{1,0},{2,3},{3,2},{4,5},{5,4},{6,7},{7,6},{8,9},{9,8},{10,11... | collective-permute-start | bytes 109064 | tf_op jit(solution)/shard_map/ppermute | solution.py:22
  46.1 0.9 copy-start.4
  46.8 1.7 %collective-permute-start.11 = (bf16[2,284,70]{1,0,2:T(2,128)(2,1)S(1)}, bf16[2,284,70]{1,0,2:T(2,128)(2,1)S(1)}, u32[]{:S(2)}, u32[]{:S(2)}) collective-permute-start(bf16[2,284,70]{1,0,2:T(2,128)(2,1)S(1)} %fusion.18), channel_id=1, source_target_pairs={{0,1},{1,0},{2,3},{3,2},{4,5},{5,4},{6,7},{7,6},{8,9},{9,8},{10,11... | collective-permute-start | bytes 238568 | tf_op jit(solution)/shard_map/ppermute | solution.py:104
  47.1 4.5 %collective-permute-start.6 = (f32[16,1136]{1,0:T(8,128)S(1)}, f32[16,1136]{1,0:T(8,128)S(1)}, u32[]{:S(2)}, u32[]{:S(2)}) collective-permute-start(f32[16,1136]{1,0:T(8,128)S(1)} %fusion.185), channel_id=1, source_target_pairs={{0,16},{16,0},{1,17},{17,1},{2,18},{18,2},{3,19},{19,3},{4,20},{20... | collective-permute-start | bytes 218120 | tf_op jit(solution)/shard_map/ppermute | solution.py:40
  48.9 6.1 %collective-permute-start.12 = (bf16[2,284,70]{1,0,2:T(2,128)(2,1)S(1)}, bf16[2,284,70]{1,0,2:T(2,128)(2,1)S(1)}, u32[]{:S(2)}, u32[]{:S(2)}) collective-permute-start(bf16[2,284,70]{1,0,2:T(2,128)(2,1)S(1)} %fusion.19), channel_id=1, source_target_pairs={{0,2},{1,3},{2,0},{3,1},{4,6},{5,7},{6,4},{7,5},{8,10},{9,11},{10,... | collective-permute-start | bytes 238568 | tf_op jit(solution)/shard_map/ppermute | solution.py:104
  55.9 4.8 %collective-permute-start.13 = (bf16[2,284,70]{1,2,0:T(8,128)(2,1)S(1)}, bf16[2,284,70]{1,2,0:T(8,128)(2,1)S(1)}, u32[]{:S(2)}, u32[]{:S(2)}) collective-permute-start(bf16[2,284,70]{1,2,0:T(8,128)(2,1)S(1)} %concatenate.84), channel_id=1, source_target_pairs={{0,4},{1,5},{2,6},{3,7},{4,0},{5,1},{6,2},{7,3},{8,12},{9,13},{10,... | collective-permute-start | bytes 238568 | tf_op jit(solution)/shard_map/ppermute | solution.py:104
  63.2 4.7 %collective-permute-start.14 = (bf16[2,4,6,70]{3,2,1,0:T(8,128)(2,1)S(1)}, bf16[2,4,6,70]{3,2,1,0:T(8,128)(2,1)S(1)}, u32[]{:S(2)}, u32[]{:S(2)}) collective-permute-start(bf16[2,4,6,70]{3,2,1,0:T(8,128)(2,1)S(1)} %constant_dynamic-slice_fusion.1), channel_id=1, source_target_pairs={{0,8},{1,9},{2,10},{3,11},{4,12},{5,13},{6,14},{7,15},{8,0},{9,1},... | collective-permute-start | bytes 20168 | tf_op jit(solution)/shard_map/ppermute | solution.py:123
  69.0 4.6 %collective-permute-start.15 = (f32[2,4,6,66]{3,2,1,0:T(8,128)S(1)}, f32[2,4,6,66]{3,2,1,0:T(8,128)S(1)}, u32[]{:S(2)}, u32[]{:S(2)}) collective-permute-start(f32[2,4,6,66]{3,2,1,0:T(8,128)S(1)} %pad_maximum_fusion.6), channel_id=1, source_target_pairs={{0,16},{1,17},{2,18},{3,19},{4,20},{5,21},{6,22},{7,23},{8,24},{9,... | collective-permute-start | bytes 38024 | tf_op jit(solution)/shard_map/ppermute | solution.py:136
  70.8 5.8 %collective-permute-start.16 = (f32[2,4,6,66]{3,2,1,0:T(8,128)S(1)}, f32[2,4,6,66]{3,2,1,0:T(8,128)S(1)}, u32[]{:S(2)}, u32[]{:S(2)}) collective-permute-start(f32[2,4,6,66]{3,2,1,0:T(8,128)S(1)} %pad_maximum_fusion.7), channel_id=1, source_target_pairs={{0,24},{1,25},{2,26},{3,27},{4,28},{5,29},{6,30},{7,31},{8,16},{9,... | collective-permute-start | bytes 38024 | tf_op jit(solution)/shard_map/ppermute | solution.py:137
  78.2 18.2 %copy-start.3 = (bf16[4,2,284]{2,1,0:T(2,128)(2,1)S(1)}, bf16[4,2,284]{2,1,0:T(2,128)(2,1)}, u32[]{:S(2)}) copy-start(bf16[4,2,284]{2,1,0:T(2,128)(2,1)} %param.11) | copy-start | bytes 13636
  78.3 1.4 %collective-permute-start.17 = (f32[2,2,2,4,2,284]{5,4,3,2,1,0:T(2,128)S(1)}, f32[2,2,2,4,2,284]{5,4,3,2,1,0:T(2,128)S(1)}, u32[]{:S(2)}, u32[]{:S(2)}) collective-permute-start(f32[2,2,2,4,2,284]{5,4,3,2,1,0:T(2,128)S(1)} %fusion.17), channel_id=1, source_target_pairs={{0,1},{1,0},{2,3},{3,2},{4,5},{5,4},{6,7},{7,6},{8,9},{9,8},{10,11... | collective-permute-start | bytes 218120 | tf_op jit(solution)/shard_map/ppermute | solution.py:57
  79.8 4.2 %collective-permute-start.18 = (f32[2,2,4,2,284]{4,3,2,1,0:T(2,128)S(1)}, f32[2,2,4,2,284]{4,3,2,1,0:T(2,128)S(1)}, u32[]{:S(2)}, u32[]{:S(2)}) collective-permute-start(f32[2,2,4,2,284]{4,3,2,1,0:T(2,128)S(1)} %fusion.32), channel_id=1, source_target_pairs={{0,2},{1,3},{2,0},{3,1},{4,6},{5,7},{6,4},{7,5},{8,10},{9,11},{10,... | collective-permute-start | bytes 109064 | tf_op jit(solution)/shard_map/ppermute | solution.py:57
  84.0 3.9 %collective-permute-start.19 = (f32[2,4,2,284]{3,2,1,0:T(2,128)S(1)}, f32[2,4,2,284]{3,2,1,0:T(2,128)S(1)}, u32[]{:S(2)}, u32[]{:S(2)}) collective-permute-start(f32[2,4,2,284]{3,2,1,0:T(2,128)S(1)} %fusion.75), channel_id=1, source_target_pairs={{0,4},{1,5},{2,6},{3,7},{4,0},{5,1},{6,2},{7,3},{8,12},{9,13},{10,... | collective-permute-start | bytes 54536 | tf_op jit(solution)/shard_map/ppermute | solution.py:57
  88.0 7.4 %collective-permute-start.20 = (f32[4,2,284]{2,1,0:T(2,128)S(1)}, f32[4,2,284]{2,1,0:T(2,128)S(1)}, u32[]{:S(2)}, u32[]{:S(2)}) collective-permute-start(f32[4,2,284]{2,1,0:T(2,128)S(1)} %get-tuple-element.68), channel_id=1, source_target_pairs={{0,0},{1,1},{2,2},{3,3},{4,4},{5,5},{6,6},{7,7},{8,16},{9,17},{10,... | collective-permute-start | bytes 27272 | tf_op jit(solution)/shard_map/ppermute | solution.py:323
  92.6 3.7 %collective-permute-start.21 = (f32[4,2,284]{2,1,0:T(2,128)S(1)}, f32[4,2,284]{2,1,0:T(2,128)S(1)}, u32[]{:S(2)}, u32[]{:S(2)}) collective-permute-start(f32[4,2,284]{2,1,0:T(2,128)S(1)} %get-tuple-element.67), channel_id=1, source_target_pairs={{0,16},{1,17},{2,18},{3,19},{4,20},{5,21},{6,22},{7,23},{8,0},{9,1... | collective-permute-start | bytes 27272 | tf_op jit(solution)/shard_map/ppermute | solution.py:323

commit v12 on v10

--- a/solution.py
+++ b/solution.py
@@ -179,11 +179,23 @@
     seq_slots = xor_slot(shard_index ^ seq_ids, seq_size)
     req_slots = xor_slot(group_index ^ req_ids, req_size)
 
-    by_request, _ = gather_xor(states, "req", req_size)
-    every, riders = gather_xor(by_request, "seq", seq_size, {0: (norm_gain, norm_bias)})
-    norm_gain, norm_bias = riders[0]
-    every = every.reshape((seq_size * req_size,) + every.shape[2:])
-    every = jnp.take(every, seq_slots[:, None] * req_size + req_slots[None, :], axis=0, mode="clip")
+    rounds = [("seq", seq_size, 1)] + [("req", req_size, 2 ** b) for b in range(req_size.bit_length() - 2, -1, -1)]
+    rounds += [("seq", seq_size, 2 ** b) for b in range(seq_size.bit_length() - 2, 0, -1)]
+    stacked = states
+    for number, (axis, size, bit) in enumerate(rounds):
+        stacked = jnp.stack([stacked, lax.ppermute(stacked, axis, xor_pairs(size, bit))])
+        if number == 1:
+            stacked, (norm_gain, norm_bias) = lax.optimization_barrier(
+                (stacked, (norm_gain, norm_bias))
+            )
+    every = stacked.reshape((2 ** len(rounds),) + states.shape)
+    seq_offsets = shard_index ^ seq_ids
+    req_offsets = group_index ^ req_ids
+    positions_all = jnp.zeros((seq_size, req_size), jnp.int32)
+    for number, (axis, size, bit) in enumerate(rounds):
+        offsets = seq_offsets[:, None] if axis == "seq" else req_offsets[None, :]
+        positions_all = positions_all + ((offsets // bit) % 2) * (2 ** number)
+    every = jnp.take(every, positions_all, axis=0, mode="clip")
     current_all = every.transpose(2, 1, 3, 0, 4).reshape(steps, total, model_width)
     normed = layer_norm(current_all.reshape(rows, model_width), norm_gain, norm_bias)
     normed_part = lax.dynamic_slice_in_dim(normed, group_index * part_width, part_width, 1)

time: 94 us -> 96.2 us (1.023)
  waiting for transfers between devices: 30.5 us -> 32.9 us
    ppermute x0 -> x5, waiting for transfers between devices: none -> 8.81 us  [shards(): lax.ppermute(stacked, axis, xor_pairs(size, bit))]
    ppermute x10 -> x5, waiting for transfers between devices: 16 us -> 9.24 us  [gather_xor(): lax.ppermute(stacked, axis, xor_pairs(size, bit))]
    ppermute x0 -> x5, starting transfers between devices: none -> 6.02 us  [shards(): lax.ppermute(stacked, axis, xor_pairs(size, bit))]
    ppermute x10 -> x5, starting transfers between devices: 13.3 us -> 7.35 us  [gather_xor(): lax.ppermute(stacked, axis, xor_pairs(size, bit))]
    another operation x2 -> x10, other arithmetic: 0.08 us -> 2.31 us  [the longest x8 2.23 us: shards(): jnp.stack([stacked, lax.ppermute(stacked, axis, xor_pairs(size, bit))])]
    another operation x15 -> x7, other arithmetic: 2.65 us -> 0.42 us  [gather_xor(): jnp.stack([stacked, lax.ppermute(stacked, axis, xor_pairs(size, bit))])]
where the time goes in v12:
time: 96.2 us; the launch traced here: 95.2 us
  waiting for transfers between devices  32.9 us (34%)
  starting transfers between devices  29.9 us (31%)
  local copies, waits for them, and re-layouts  12.4 us (13%)
  matrix products  9.94 us (10%)
  other arithmetic  8.51 us (9%)
  between operations  1.52 us (2%)
    ppermute x5, waiting for transfers between devices, gather_xor(): lax.ppermute(stacked, axis, xor_pairs(size, bit))  9.24 us
    ppermute x5, waiting for transfers between devices, shards(): lax.ppermute(stacked, axis, xor_pairs(size, bit))  8.81 us
    ppermute x5, starting transfers between devices, gather_xor(): lax.ppermute(stacked, axis, xor_pairs(size, bit))  7.35 us
    ppermute x3, waiting for transfers between devices, scatter_sum(): blocks = keep + lax.ppermute(send, axis, xor_pairs(size, bit))  6.08 us
    ppermute x5, starting transfers between devices, shards(): lax.ppermute(stacked, axis, xor_pairs(size, bit))  6.02 us
    ppermute x1, starting transfers between devices, shards(): lax.ppermute(own_block, ALL, own_routes)  5.39 us
    ppermute x3, starting transfers between devices, merge_over(): lax.ppermute(pack_merge(peak, total, weighted), axis, xor_pairs(size, bit))  3.44 us
    dot_general x1, matrix products, shards(): down_part = jnp.dot(hidden, w_down, preferred_element_type=jnp.float32)  3.39 us
  transfers between devices with their start and end apart: 21, of which 18 were waited for; matrix products, arithmetic and copies ran while one was open for 15% of the time, Pallas kernels for 0%

profile of v12, /device:TPU:2, one launch (start us, length us, event | category | flops | bytes accessed | tf_op | source)
XLA Modules:
  0.0 95.2 jit_solution(11579451121506831259)
XLA Ops:
  0.8 0.8 dynamic_slice.22
  1.7 0.8 select_reduce_fusion.2
  3.4 0.7 pad_maximum_fusion.8
  4.2 0.7 fusion.192
  4.9 3.0 %collective-permute-done.1 = bf16[2,4,2,284]{3,2,1,0:T(2,128)(2,1)S(1)} collective-permute-done((bf16[2,4,2,284]{3,2,1,0:T(2,128)(2,1)S(1)}, bf16[2,4,2,284]{3,2,1,0:T(2,128)(2,1)S(1)}, u32[]{:S(2)}, u32[]{:S(2)}) %collective-permute-start.1) | collective-permute-done | bytes 9120 | tf_op jit(solution)/shard_map/ppermute | solution.py:186
  7.9 2.7 %collective-permute-start.2 = (bf16[2,2,4,2,284]{4,3,2,1,0:T(2,128)(2,1)S(1)}, bf16[2,2,4,2,284]{4,3,2,1,0:T(2,128)(2,1)S(1)}, u32[]{:S(2)}, u32[]{:S(2)}) collective-permute-start(bf16[2,2,4,2,284]{4,3,2,1,0:T(2,128)(2,1)S(1)} %pad_maximum_fusion.6), channel_id=1, source_target_pairs={{0,8},{1,9},{2,10},{3,11},{4,12},{5,13},{6,14},{7,15},{8,0},{9,1},... | collective-permute-start | bytes 54536 | tf_op jit(solution)/shard_map/ppermute | solution.py:186
  10.8 0.8 dynamic-slice
  11.5 0.8 dynamic-slice.1
  12.8 1.6 %collective-permute-start.3 = (bf16[2,2,2,4,2,284]{5,4,3,2,1,0:T(2,128)(2,1)S(1)}, bf16[2,2,2,4,2,284]{5,4,3,2,1,0:T(2,128)(2,1)S(1)}, u32[]{:S(2)}, u32[]{:S(2)}) collective-permute-start(bf16[2,2,2,4,2,284]{5,4,3,2,1,0:T(2,128)(2,1)S(1)} %pad_maximum_fusion.3), channel_id=1, source_target_pairs={{0,4},{1,5},{2,6},{3,7},{4,0},{5,1},{6,2},{7,3},{8,12},{9,13},{10,... | collective-permute-start | bytes 109064 | tf_op jit(solution)/shard_map/ppermute | solution.py:186
  14.5 2.4 %collective-permute-done.3 = bf16[2,2,2,4,2,284]{5,4,3,2,1,0:T(2,128)(2,1)S(1)} collective-permute-done((bf16[2,2,2,4,2,284]{5,4,3,2,1,0:T(2,128)(2,1)S(1)}, bf16[2,2,2,4,2,284]{5,4,3,2,1,0:T(2,128)(2,1)S(1)}, u32[]{:S(2)}, u32[]{:S(2)}) %collective-permute-start.3) | collective-permute-done | bytes 36384 | tf_op jit(solution)/shard_map/ppermute | solution.py:186
  17.1 1.6 %collective-permute-start.4 = (bf16[2,2,2,2,4,2,284]{6,5,4,3,2,1,0:T(2,128)(2,1)S(1)}, bf16[2,2,2,2,4,2,284]{6,5,4,3,2,1,0:T(2,128)(2,1)S(1)}, u32[]{:S(2)}, u32[]{:S(2)}) collective-permute-start(bf16[2,2,2,2,4,2,284]{6,5,4,3,2,1,0:T(2,128)(2,1)S(1)} %pad_maximum_fusion.1), channel_id=1, source_target_pairs={{0,2},{1,3},{2,0},{3,1},{4,6},{5,7},{6,4},{7,5},{8,10},{9,11},{10,... | collective-permute-start | bytes 218120 | tf_op jit(solution)/shard_map/ppermute | solution.py:186
  18.9 2.9 %collective-permute-done.4 = bf16[2,2,2,2,4,2,284]{6,5,4,3,2,1,0:T(2,128)(2,1)S(1)} collective-permute-done((bf16[2,2,2,2,4,2,284]{6,5,4,3,2,1,0:T(2,128)(2,1)S(1)}, bf16[2,2,2,2,4,2,284]{6,5,4,3,2,1,0:T(2,128)(2,1)S(1)}, u32[]{:S(2)}, u32[]{:S(2)}) %collective-permute-start.4) | collective-permute-done | bytes 72736 | tf_op jit(solution)/shard_map/ppermute | solution.py:186
  22.1 1.0 %gather_fusion = bf16[32,4,2,284]{3,2,1,0:T(2,128)(2,1)S(1)} fusion(bf16[32,4,2,284]{3,2,1,0:T(2,128)(2,1)S(1)} %bitcast.287, s32[1024]{0:T(1024)S(1)} %pad_clamp_fusion.2), kind=kCustom, calls=%fused_computation | custom fusion | bytes 290944 | tf_op jit(solution)/shard_map/jit(_take)/gather | solution.py:198
  24.5 1.8 %fusion.177 = f32[16,284]{1,0:T(8,128)S(1)} fusion(bf16[2272,284]{0,1:T(8,128)(2,1)} %param.17, f32[16,4544]{1,0:T(8,128)S(1)} %reshape.1072, s32[]{:T(128)S(6)} %select_n.361, f32[2272]{0:T(1024)S(1)} %dynamic-slice.1, f32[2272]{0:T(1024)S(1)} %dynamic-slice, f32[16]{0:T(128)S(1)} %rsqrt.12, f32[16]{0:T(128)S(1)} %div.145), kind=kOutput, calls=%fused_computation.398 | convolution fusion | flops 20829696 | bytes 1481732 | tf_op jit(solution)/shard_map/dot_general | solution.py:203
  26.9 3.3 %fusion.179 = f32[16,1136]{1,0:T(8,128)S(1)} fusion(bf16[2272,1136]{1,0:T(8,128)(2,1)} %param.20, f32[16,4544]{1,0:T(8,128)S(1)} %reshape.1072, s32[]{:T(128)S(6)} %select_n.361, f32[2272]{0:T(1024)S(1)} %dynamic-slice.1, f32[2272]{0:T(1024)S(1)} %dynamic-slice, f32[16]{0:T(128)S(1)} %rsqrt.12, f32[16]{0:T(128)S(1)} %div.145), kind=kOutput, calls=%fused_computation.399 | convolution fusion | flops 82773504 | bytes 5407748 | tf_op jit(solution)/shard_map/dot_general | solution.py:206
  31.1 2.6 %collective-permute-start.7 = (bf16[4,2,284]{2,1,0:T(2,128)(2,1)S(1)}, bf16[4,2,284]{2,1,0:T(2,128)(2,1)S(1)}, u32[]{:S(2)}, u32[]{:S(2)}) collective-permute-start(bf16[4,2,284]{2,1,0:T(2,128)(2,1)S(1)} %slice.415), channel_id=1, source_target_pairs={{0,8},{1,9},{2,10},{3,11},{4,12},{5,13},{6,14},{7,15},{8,0},{9,1},... | collective-permute-start | bytes 13640 | tf_op jit(solution)/shard_map/ppermute | solution.py:22
  33.9 1.8 %collective-permute-done.7 = bf16[4,2,284]{2,1,0:T(2,128)(2,1)S(1)} collective-permute-done((bf16[4,2,284]{2,1,0:T(2,128)(2,1)S(1)}, bf16[4,2,284]{2,1,0:T(2,128)(2,1)S(1)}, u32[]{:S(2)}, u32[]{:S(2)}) %collective-permute-start.7) | collective-permute-done | bytes 4576 | tf_op jit(solution)/shard_map/ppermute | solution.py:22
  35.8 1.6 %collective-permute-start.8 = (bf16[2,4,2,284]{3,2,1,0:T(2,128)(2,1)S(1)}, bf16[2,4,2,284]{3,2,1,0:T(2,128)(2,1)S(1)}, u32[]{:S(2)}, u32[]{:S(2)}) collective-permute-start(bf16[2,4,2,284]{3,2,1,0:T(2,128)(2,1)S(1)} %pad_maximum_fusion.9), channel_id=1, source_target_pairs={{0,4},{1,5},{2,6},{3,7},{4,0},{5,1},{6,2},{7,3},{8,12},{9,13},{10,... | collective-permute-start | bytes 27272 | tf_op jit(solution)/shard_map/ppermute | solution.py:22
  37.7 1.9 %collective-permute-done.8 = bf16[2,4,2,284]{3,2,1,0:T(2,128)(2,1)S(1)} collective-permute-done((bf16[2,4,2,284]{3,2,1,0:T(2,128)(2,1)S(1)}, bf16[2,4,2,284]{3,2,1,0:T(2,128)(2,1)S(1)}, u32[]{:S(2)}, u32[]{:S(2)}) %collective-permute-start.8) | collective-permute-done | bytes 9120 | tf_op jit(solution)/shard_map/ppermute | solution.py:22
  39.6 1.6 %collective-permute-start.9 = (bf16[2,2,4,2,284]{4,3,2,1,0:T(2,128)(2,1)S(1)}, bf16[2,2,4,2,284]{4,3,2,1,0:T(2,128)(2,1)S(1)}, u32[]{:S(2)}, u32[]{:S(2)}) collective-permute-start(bf16[2,2,4,2,284]{4,3,2,1,0:T(2,128)(2,1)S(1)} %pad_maximum_fusion.7), channel_id=1, source_target_pairs={{0,2},{1,3},{2,0},{3,1},{4,6},{5,7},{6,4},{7,5},{8,10},{9,11},{10,... | collective-permute-start | bytes 54536 | tf_op jit(solution)/shard_map/ppermute | solution.py:22
  41.3 2.3 %collective-permute-done.9 = bf16[2,2,4,2,284]{4,3,2,1,0:T(2,128)(2,1)S(1)} collective-permute-done((bf16[2,2,4,2,284]{4,3,2,1,0:T(2,128)(2,1)S(1)}, bf16[2,2,4,2,284]{4,3,2,1,0:T(2,128)(2,1)S(1)}, u32[]{:S(2)}, u32[]{:S(2)}) %collective-permute-start.9) | collective-permute-done | bytes 18208 | tf_op jit(solution)/shard_map/ppermute | solution.py:22
  43.8 1.1 %collective-permute-done.10 = bf16[2,2,2,4,2,284]{5,4,3,2,1,0:T(2,128)(2,1)S(1)} collective-permute-done((bf16[2,2,2,4,2,284]{5,4,3,2,1,0:T(2,128)(2,1)S(1)}, bf16[2,2,2,4,2,284]{5,4,3,2,1,0:T(2,128)(2,1)S(1)}, u32[]{:S(2)}, u32[]{:S(2)}) %collective-permute-start.10) | collective-permute-done | bytes 36384 | tf_op jit(solution)/shard_map/ppermute | solution.py:22
  45.1 0.6 gather_fusion.1
  47.3 0.5 fusion
  47.7 0.4 fusion.1
  49.2 1.5 %collective-permute-start.6 = (f32[16,1136]{1,0:T(8,128)S(1)}, f32[16,1136]{1,0:T(8,128)S(1)}, u32[]{:S(2)}, u32[]{:S(2)}) collective-permute-start(f32[16,1136]{1,0:T(8,128)S(1)} %fusion.179), channel_id=1, source_target_pairs={{0,16},{16,0},{1,17},{17,1},{2,18},{18,2},{3,19},{19,3},{4,20},{20... | collective-permute-start | bytes 218120 | tf_op jit(solution)/shard_map/ppermute | solution.py:40
  51.1 1.6 %collective-permute-start.12 = (bf16[2,284,70]{1,0,2:T(2,128)(2,1)S(1)}, bf16[2,284,70]{1,0,2:T(2,128)(2,1)S(1)}, u32[]{:S(2)}, u32[]{:S(2)}) collective-permute-start(bf16[2,284,70]{1,0,2:T(2,128)(2,1)S(1)} %fusion.19), channel_id=1, source_target_pairs={{0,2},{1,3},{2,0},{3,1},{4,6},{5,7},{6,4},{7,5},{8,10},{9,11},{10,... | collective-permute-start | bytes 238568 | tf_op jit(solution)/shard_map/ppermute | solution.py:104
  52.7 1.0 %collective-permute-done.6 = f32[16,1136]{1,0:T(8,128)S(1)} collective-permute-done((f32[16,1136]{1,0:T(8,128)S(1)}, f32[16,1136]{1,0:T(8,128)S(1)}, u32[]{:S(2)}, u32[]{:S(2)}) %collective-permute-start.6) | collective-permute-done | bytes 72736 | tf_op jit(solution)/shard_map/ppermute | solution.py:40
  53.7 3.4 %fusion.35 = f32[16,2272]{1,0:T(8,128)S(1)} fusion(bf16[1136,2272]{1,0:T(8,128)(2,1)} %param.21, f32[16,1136]{1,0:T(8,128)S(1)} %fusion.179, f32[16,1136]{1,0:T(8,128)S(1)} %collective-permute-done.6), kind=kOutput, calls=%fused_computation.74 | convolution fusion | flops 83791360 | bytes 5452800 | tf_op jit(solution)/shard_map/dot_general | solution.py:221
  57.5 0.6 concatenate.78
  58.1 1.6 %collective-permute-start.13 = (bf16[2,284,70]{1,2,0:T(8,128)(2,1)S(1)}, bf16[2,284,70]{1,2,0:T(8,128)(2,1)S(1)}, u32[]{:S(2)}, u32[]{:S(2)}) collective-permute-start(bf16[2,284,70]{1,2,0:T(8,128)(2,1)S(1)} %concatenate.78), channel_id=1, source_target_pairs={{0,4},{1,5},{2,6},{3,7},{4,0},{5,1},{6,2},{7,3},{8,12},{9,13},{10,... | collective-permute-start | bytes 238568 | tf_op jit(solution)/shard_map/ppermute | solution.py:104
  59.8 3.1 %collective-permute-done.13 = bf16[2,284,70]{1,2,0:T(8,128)(2,1)S(1)} collective-permute-done((bf16[2,284,70]{1,2,0:T(8,128)(2,1)S(1)}, bf16[2,284,70]{1,2,0:T(8,128)(2,1)S(1)}, u32[]{:S(2)}, u32[]{:S(2)}) %collective-permute-start.13) | collective-permute-done | bytes 79552 | tf_op jit(solution)/shard_map/ppermute | solution.py:104
  64.8 0.5 concatenate.86
  65.4 2.7 %collective-permute-start.14 = (bf16[2,4,6,70]{3,2,1,0:T(8,128)(2,1)S(1)}, bf16[2,4,6,70]{3,2,1,0:T(8,128)(2,1)S(1)}, u32[]{:S(2)}, u32[]{:S(2)}) collective-permute-start(bf16[2,4,6,70]{3,2,1,0:T(8,128)(2,1)S(1)} %constant_dynamic-slice_fusion), channel_id=1, source_target_pairs={{0,8},{1,9},{2,10},{3,11},{4,12},{5,13},{6,14},{7,15},{8,0},{9,1},... | collective-permute-start | bytes 20168 | tf_op jit(solution)/shard_map/ppermute | solution.py:118
  68.7 1.3 %collective-permute-done.14 = bf16[2,4,6,70]{3,2,1,0:T(8,128)(2,1)S(1)} collective-permute-done((bf16[2,4,6,70]{3,2,1,0:T(8,128)(2,1)S(1)}, bf16[2,4,6,70]{3,2,1,0:T(8,128)(2,1)S(1)}, u32[]{:S(2)}, u32[]{:S(2)}) %collective-permute-start.14) | collective-permute-done | bytes 6752 | tf_op jit(solution)/shard_map/ppermute | solution.py:118
  70.9 1.5 %collective-permute-start.15 = (bf16[4,2,284]{2,0,1:T(4,128)(2,1)S(1)}, bf16[4,2,284]{2,0,1:T(4,128)(2,1)S(1)}, u32[]{:S(2)}, u32[]{:S(2)}) collective-permute-start(bf16[4,2,284]{2,0,1:T(4,128)(2,1)S(1)} %get-tuple-element.69), channel_id=1, source_target_pairs={{0,16},{16,0},{1,17},{17,1},{2,18},{18,2},{3,19},{19,3},{4,20},{20... | collective-permute-start | bytes 13640 | tf_op jit(solution)/shard_map/ppermute | solution.py:22
  72.3 2.2 %collective-permute-done.15 = bf16[4,2,284]{2,0,1:T(4,128)(2,1)S(1)} collective-permute-done((bf16[4,2,284]{2,0,1:T(4,128)(2,1)S(1)}, bf16[4,2,284]{2,0,1:T(4,128)(2,1)S(1)}, u32[]{:S(2)}, u32[]{:S(2)}) %collective-permute-start.15) | collective-permute-done | bytes 4576 | tf_op jit(solution)/shard_map/ppermute | solution.py:22
  74.5 0.6 gather_fusion.2
  75.9 1.3 %collective-permute-done.16 = f32[2,2,2,4,2,284]{5,4,3,2,1,0:T(2,128)S(1)} collective-permute-done((f32[2,2,2,4,2,284]{5,4,3,2,1,0:T(2,128)S(1)}, f32[2,2,2,4,2,284]{5,4,3,2,1,0:T(2,128)S(1)}, u32[]{:S(2)}, u32[]{:S(2)}) %collective-permute-start.16) | collective-permute-done | bytes 72736 | tf_op jit(solution)/shard_map/ppermute | solution.py:57
  77.2 1.6 %collective-permute-start.17 = (f32[2,2,4,2,284]{4,3,2,1,0:T(2,128)S(1)}, f32[2,2,4,2,284]{4,3,2,1,0:T(2,128)S(1)}, u32[]{:S(2)}, u32[]{:S(2)}) collective-permute-start(f32[2,2,4,2,284]{4,3,2,1,0:T(2,128)S(1)} %fusion.32), channel_id=1, source_target_pairs={{0,2},{1,3},{2,0},{3,1},{4,6},{5,7},{6,4},{7,5},{8,10},{9,11},{10,... | collective-permute-start | bytes 109064 | tf_op jit(solution)/shard_map/ppermute | solution.py:57
  78.8 2.6 %collective-permute-done.17 = f32[2,2,4,2,284]{4,3,2,1,0:T(2,128)S(1)} collective-permute-done((f32[2,2,4,2,284]{4,3,2,1,0:T(2,128)S(1)}, f32[2,2,4,2,284]{4,3,2,1,0:T(2,128)S(1)}, u32[]{:S(2)}, u32[]{:S(2)}) %collective-permute-start.17) | collective-permute-done | bytes 36384 | tf_op jit(solution)/shard_map/ppermute | solution.py:57
  81.5 1.6 %collective-permute-start.18 = (f32[2,4,2,284]{3,2,1,0:T(2,128)S(1)}, f32[2,4,2,284]{3,2,1,0:T(2,128)S(1)}, u32[]{:S(2)}, u32[]{:S(2)}) collective-permute-start(f32[2,4,2,284]{3,2,1,0:T(2,128)S(1)} %fusion.69), channel_id=1, source_target_pairs={{0,4},{1,5},{2,6},{3,7},{4,0},{5,1},{6,2},{7,3},{8,12},{9,13},{10,... | collective-permute-start | bytes 54536 | tf_op jit(solution)/shard_map/ppermute | solution.py:57
  83.1 2.3 %collective-permute-done.18 = f32[2,4,2,284]{3,2,1,0:T(2,128)S(1)} collective-permute-done((f32[2,4,2,284]{3,2,1,0:T(2,128)S(1)}, f32[2,4,2,284]{3,2,1,0:T(2,128)S(1)}, u32[]{:S(2)}, u32[]{:S(2)}) %collective-permute-start.18) | collective-permute-done | bytes 18208 | tf_op jit(solution)/shard_map/ppermute | solution.py:57
  85.4 5.4 %collective-permute-start.19 = (f32[4,2,284]{2,1,0:T(2,128)S(1)}, f32[4,2,284]{2,1,0:T(2,128)S(1)}, u32[]{:S(2)}, u32[]{:S(2)}) collective-permute-start(f32[4,2,284]{2,1,0:T(2,128)S(1)} %get-tuple-element.63), channel_id=1, source_target_pairs={{0,0},{1,1},{2,2},{3,3},{4,4},{5,5},{6,6},{7,7},{8,16},{9,17},{10,... | collective-permute-start | bytes 27272 | tf_op jit(solution)/shard_map/ppermute | solution.py:297
  90.9 0.8 copy.250
  91.7 1.1 %collective-permute-done.19 = f32[4,2,284]{2,1,0:T(2,128)S(1)} collective-permute-done((f32[4,2,284]{2,1,0:T(2,128)S(1)}, f32[4,2,284]{2,1,0:T(2,128)S(1)}, u32[]{:S(2)}, u32[]{:S(2)}) %collective-permute-start.19) | collective-permute-done | bytes 9120 | tf_op jit(solution)/shard_map/ppermute | solution.py:297
  92.8 1.8 %collective-permute-done.20 = f32[4,2,284]{2,1,0:T(2,128)S(1)} collective-permute-done((f32[4,2,284]{2,1,0:T(2,128)S(1)}, f32[4,2,284]{2,1,0:T(2,128)S(1)}, u32[]{:S(2)}, u32[]{:S(2)}) %collective-permute-start.20) | collective-permute-done | bytes 9120 | tf_op jit(solution)/shard_map/ppermute | solution.py:297
  94.6 0.6 add_convert_fusion
  (174 shorter events, 13.7 us)
Async XLA Ops:
  0.6 74.5 %copy-start = (bf16[284,2272]{1,0:T(8,128)(2,1)S(1)}, bf16[284,2272]{1,0:T(8,128)(2,1)}, u32[]{:S(2)}) copy-start(bf16[284,2272]{1,0:T(8,128)(2,1)} %param.19) | copy-start | bytes 3871492
  0.6 2.7 %collective-permute-start = (bf16[4,2,284]{2,1,0:T(2,128)(2,1)}, bf16[4,2,284]{2,1,0:T(2,128)(2,1)S(1)}, u32[]{:S(2)}, u32[]{:S(2)}) collective-permute-start(bf16[4,2,284]{2,1,0:T(2,128)(2,1)} %param.11), channel_id=1, source_target_pairs={{0,1},{1,0},{2,3},{3,2},{4,5},{5,4},{6,7},{7,6},{8,9},{9,8},{10,11... | collective-permute-start | bytes 13640 | tf_op jit(solution)/shard_map/ppermute | solution.py:186
  4.1 3.8 %collective-permute-start.1 = (bf16[2,4,2,284]{3,2,1,0:T(2,128)(2,1)S(1)}, bf16[2,4,2,284]{3,2,1,0:T(2,128)(2,1)S(1)}, u32[]{:S(2)}, u32[]{:S(2)}) collective-permute-start(bf16[2,4,2,284]{3,2,1,0:T(2,128)(2,1)S(1)} %pad_maximum_fusion.8), channel_id=1, source_target_pairs={{0,16},{16,0},{1,17},{17,1},{2,18},{18,2},{3,19},{19,3},{4,20},{20... | collective-permute-start | bytes 27272 | tf_op jit(solution)/shard_map/ppermute | solution.py:186
  7.9 4.8 %collective-permute-start.2 = (bf16[2,2,4,2,284]{4,3,2,1,0:T(2,128)(2,1)S(1)}, bf16[2,2,4,2,284]{4,3,2,1,0:T(2,128)(2,1)S(1)}, u32[]{:S(2)}, u32[]{:S(2)}) collective-permute-start(bf16[2,2,4,2,284]{4,3,2,1,0:T(2,128)(2,1)S(1)} %pad_maximum_fusion.6), channel_id=1, source_target_pairs={{0,8},{1,9},{2,10},{3,11},{4,12},{5,13},{6,14},{7,15},{8,0},{9,1},... | collective-permute-start | bytes 54536 | tf_op jit(solution)/shard_map/ppermute | solution.py:186
  12.8 4.2 %collective-permute-start.3 = (bf16[2,2,2,4,2,284]{5,4,3,2,1,0:T(2,128)(2,1)S(1)}, bf16[2,2,2,4,2,284]{5,4,3,2,1,0:T(2,128)(2,1)S(1)}, u32[]{:S(2)}, u32[]{:S(2)}) collective-permute-start(bf16[2,2,2,4,2,284]{5,4,3,2,1,0:T(2,128)(2,1)S(1)} %pad_maximum_fusion.3), channel_id=1, source_target_pairs={{0,4},{1,5},{2,6},{3,7},{4,0},{5,1},{6,2},{7,3},{8,12},{9,13},{10,... | collective-permute-start | bytes 109064 | tf_op jit(solution)/shard_map/ppermute | solution.py:186
  17.1 4.7 %collective-permute-start.4 = (bf16[2,2,2,2,4,2,284]{6,5,4,3,2,1,0:T(2,128)(2,1)S(1)}, bf16[2,2,2,2,4,2,284]{6,5,4,3,2,1,0:T(2,128)(2,1)S(1)}, u32[]{:S(2)}, u32[]{:S(2)}) collective-permute-start(bf16[2,2,2,2,4,2,284]{6,5,4,3,2,1,0:T(2,128)(2,1)S(1)} %pad_maximum_fusion.1), channel_id=1, source_target_pairs={{0,2},{1,3},{2,0},{3,1},{4,6},{5,7},{6,4},{7,5},{8,10},{9,11},{10,... | collective-permute-start | bytes 218120 | tf_op jit(solution)/shard_map/ppermute | solution.py:186
  24.3 2.0 %copy-start.1 = (bf16[2272,128]{1,0:T(8,128)(2,1)S(1)}, bf16[2272,128]{1,0:T(8,128)(2,1)}, u32[]{:S(2)}) copy-start(bf16[2272,128]{1,0:T(8,128)(2,1)} %param.18) | copy-start | bytes 1744900
  26.7 9.0 %copy-start.2 = (bf16[2,512,128]{2,1,0:T(8,128)(2,1)S(1)}, bf16[2,512,128]{2,1,0:T(8,128)(2,1)}, u32[]{:S(2)}) copy-start(bf16[2,512,128]{2,1,0:T(8,128)(2,1)} %param.12) | copy-start | bytes 786436
  26.7 3.9 %collective-permute-start.5 = (f32[16,412]{1,0:T(8,128)S(1)}, f32[16,412]{1,0:T(8,128)S(1)}, u32[]{:S(2)}, u32[]{:S(2)}) collective-permute-start(f32[16,412]{1,0:T(8,128)S(1)} %pad_maximum_fusion.5), channel_id=1, source_target_pairs={{0,16},{16,0},{1,17},{17,1},{2,18},{18,2},{3,19},{19,3},{4,20},{20... | collective-permute-start | bytes 79112 | tf_op jit(solution)/shard_map/ppermute | solution.py:40
  31.1 4.5 %collective-permute-start.7 = (bf16[4,2,284]{2,1,0:T(2,128)(2,1)S(1)}, bf16[4,2,284]{2,1,0:T(2,128)(2,1)S(1)}, u32[]{:S(2)}, u32[]{:S(2)}) collective-permute-start(bf16[4,2,284]{2,1,0:T(2,128)(2,1)S(1)} %slice.415), channel_id=1, source_target_pairs={{0,8},{1,9},{2,10},{3,11},{4,12},{5,13},{6,14},{7,15},{8,0},{9,1},... | collective-permute-start | bytes 13640 | tf_op jit(solution)/shard_map/ppermute | solution.py:22
  35.8 3.8 %collective-permute-start.8 = (bf16[2,4,2,284]{3,2,1,0:T(2,128)(2,1)S(1)}, bf16[2,4,2,284]{3,2,1,0:T(2,128)(2,1)S(1)}, u32[]{:S(2)}, u32[]{:S(2)}) collective-permute-start(bf16[2,4,2,284]{3,2,1,0:T(2,128)(2,1)S(1)} %pad_maximum_fusion.9), channel_id=1, source_target_pairs={{0,4},{1,5},{2,6},{3,7},{4,0},{5,1},{6,2},{7,3},{8,12},{9,13},{10,... | collective-permute-start | bytes 27272 | tf_op jit(solution)/shard_map/ppermute | solution.py:22
  39.6 3.9 %collective-permute-start.9 = (bf16[2,2,4,2,284]{4,3,2,1,0:T(2,128)(2,1)S(1)}, bf16[2,2,4,2,284]{4,3,2,1,0:T(2,128)(2,1)S(1)}, u32[]{:S(2)}, u32[]{:S(2)}) collective-permute-start(bf16[2,2,4,2,284]{4,3,2,1,0:T(2,128)(2,1)S(1)} %pad_maximum_fusion.7), channel_id=1, source_target_pairs={{0,2},{1,3},{2,0},{3,1},{4,6},{5,7},{6,4},{7,5},{8,10},{9,11},{10,... | collective-permute-start | bytes 54536 | tf_op jit(solution)/shard_map/ppermute | solution.py:22
  43.6 1.3 %collective-permute-start.10 = (bf16[2,2,2,4,2,284]{5,4,3,2,1,0:T(2,128)(2,1)S(1)}, bf16[2,2,2,4,2,284]{5,4,3,2,1,0:T(2,128)(2,1)S(1)}, u32[]{:S(2)}, u32[]{:S(2)}) collective-permute-start(bf16[2,2,2,4,2,284]{5,4,3,2,1,0:T(2,128)(2,1)S(1)} %pad_maximum_fusion.4), channel_id=1, source_target_pairs={{0,1},{1,0},{2,3},{3,2},{4,5},{5,4},{6,7},{7,6},{8,9},{9,8},{10,11... | collective-permute-start | bytes 109064 | tf_op jit(solution)/shard_map/ppermute | solution.py:22
  48.2 0.9 copy-start.4
  48.9 1.8 %collective-permute-start.11 = (bf16[2,284,70]{1,0,2:T(2,128)(2,1)S(1)}, bf16[2,284,70]{1,0,2:T(2,128)(2,1)S(1)}, u32[]{:S(2)}, u32[]{:S(2)}) collective-permute-start(bf16[2,284,70]{1,0,2:T(2,128)(2,1)S(1)} %fusion.18), channel_id=1, source_target_pairs={{0,1},{1,0},{2,3},{3,2},{4,5},{5,4},{6,7},{7,6},{8,9},{9,8},{10,11... | collective-permute-start | bytes 238568 | tf_op jit(solution)/shard_map/ppermute | solution.py:104
  49.2 4.5 %collective-permute-start.6 = (f32[16,1136]{1,0:T(8,128)S(1)}, f32[16,1136]{1,0:T(8,128)S(1)}, u32[]{:S(2)}, u32[]{:S(2)}) collective-permute-start(f32[16,1136]{1,0:T(8,128)S(1)} %fusion.179), channel_id=1, source_target_pairs={{0,16},{16,0},{1,17},{17,1},{2,18},{18,2},{3,19},{19,3},{4,20},{20... | collective-permute-start | bytes 218120 | tf_op jit(solution)/shard_map/ppermute | solution.py:40
  51.1 6.0 %collective-permute-start.12 = (bf16[2,284,70]{1,0,2:T(2,128)(2,1)S(1)}, bf16[2,284,70]{1,0,2:T(2,128)(2,1)S(1)}, u32[]{:S(2)}, u32[]{:S(2)}) collective-permute-start(bf16[2,284,70]{1,0,2:T(2,128)(2,1)S(1)} %fusion.19), channel_id=1, source_target_pairs={{0,2},{1,3},{2,0},{3,1},{4,6},{5,7},{6,4},{7,5},{8,10},{9,11},{10,... | collective-permute-start | bytes 238568 | tf_op jit(solution)/shard_map/ppermute | solution.py:104
  58.1 4.8 %collective-permute-start.13 = (bf16[2,284,70]{1,2,0:T(8,128)(2,1)S(1)}, bf16[2,284,70]{1,2,0:T(8,128)(2,1)S(1)}, u32[]{:S(2)}, u32[]{:S(2)}) collective-permute-start(bf16[2,284,70]{1,2,0:T(8,128)(2,1)S(1)} %concatenate.78), channel_id=1, source_target_pairs={{0,4},{1,5},{2,6},{3,7},{4,0},{5,1},{6,2},{7,3},{8,12},{9,13},{10,... | collective-permute-start | bytes 238568 | tf_op jit(solution)/shard_map/ppermute | solution.py:104
  65.4 4.7 %collective-permute-start.14 = (bf16[2,4,6,70]{3,2,1,0:T(8,128)(2,1)S(1)}, bf16[2,4,6,70]{3,2,1,0:T(8,128)(2,1)S(1)}, u32[]{:S(2)}, u32[]{:S(2)}) collective-permute-start(bf16[2,4,6,70]{3,2,1,0:T(8,128)(2,1)S(1)} %constant_dynamic-slice_fusion), channel_id=1, source_target_pairs={{0,8},{1,9},{2,10},{3,11},{4,12},{5,13},{6,14},{7,15},{8,0},{9,1},... | collective-permute-start | bytes 20168 | tf_op jit(solution)/shard_map/ppermute | solution.py:118
  70.9 3.6 %collective-permute-start.15 = (bf16[4,2,284]{2,0,1:T(4,128)(2,1)S(1)}, bf16[4,2,284]{2,0,1:T(4,128)(2,1)S(1)}, u32[]{:S(2)}, u32[]{:S(2)}) collective-permute-start(bf16[4,2,284]{2,0,1:T(4,128)(2,1)S(1)} %get-tuple-element.69), channel_id=1, source_target_pairs={{0,16},{16,0},{1,17},{17,1},{2,18},{18,2},{3,19},{19,3},{4,20},{20... | collective-permute-start | bytes 13640 | tf_op jit(solution)/shard_map/ppermute | solution.py:22
  75.6 19.0 %copy-start.3 = (bf16[4,2,284]{2,1,0:T(2,128)(2,1)S(1)}, bf16[4,2,284]{2,1,0:T(2,128)(2,1)}, u32[]{:S(2)}) copy-start(bf16[4,2,284]{2,1,0:T(2,128)(2,1)} %param.11) | copy-start | bytes 13636
  75.8 1.4 %collective-permute-start.16 = (f32[2,2,2,4,2,284]{5,4,3,2,1,0:T(2,128)S(1)}, f32[2,2,2,4,2,284]{5,4,3,2,1,0:T(2,128)S(1)}, u32[]{:S(2)}, u32[]{:S(2)}) collective-permute-start(f32[2,2,2,4,2,284]{5,4,3,2,1,0:T(2,128)S(1)} %fusion.17), channel_id=1, source_target_pairs={{0,1},{1,0},{2,3},{3,2},{4,5},{5,4},{6,7},{7,6},{8,9},{9,8},{10,11... | collective-permute-start | bytes 218120 | tf_op jit(solution)/shard_map/ppermute | solution.py:57
  77.2 4.2 %collective-permute-start.17 = (f32[2,2,4,2,284]{4,3,2,1,0:T(2,128)S(1)}, f32[2,2,4,2,284]{4,3,2,1,0:T(2,128)S(1)}, u32[]{:S(2)}, u32[]{:S(2)}) collective-permute-start(f32[2,2,4,2,284]{4,3,2,1,0:T(2,128)S(1)} %fusion.32), channel_id=1, source_target_pairs={{0,2},{1,3},{2,0},{3,1},{4,6},{5,7},{6,4},{7,5},{8,10},{9,11},{10,... | collective-permute-start | bytes 109064 | tf_op jit(solution)/shard_map/ppermute | solution.py:57
  81.5 3.9 %collective-permute-start.18 = (f32[2,4,2,284]{3,2,1,0:T(2,128)S(1)}, f32[2,4,2,284]{3,2,1,0:T(2,128)S(1)}, u32[]{:S(2)}, u32[]{:S(2)}) collective-permute-start(f32[2,4,2,284]{3,2,1,0:T(2,128)S(1)} %fusion.69), channel_id=1, source_target_pairs={{0,4},{1,5},{2,6},{3,7},{4,0},{5,1},{6,2},{7,3},{8,12},{9,13},{10,... | collective-permute-start | bytes 54536 | tf_op jit(solution)/shard_map/ppermute | solution.py:57
  85.4 7.4 %collective-permute-start.19 = (f32[4,2,284]{2,1,0:T(2,128)S(1)}, f32[4,2,284]{2,1,0:T(2,128)S(1)}, u32[]{:S(2)}, u32[]{:S(2)}) collective-permute-start(f32[4,2,284]{2,1,0:T(2,128)S(1)} %get-tuple-element.63), channel_id=1, source_target_pairs={{0,0},{1,1},{2,2},{3,3},{4,4},{5,5},{6,6},{7,7},{8,16},{9,17},{10,... | collective-permute-start | bytes 27272 | tf_op jit(solution)/shard_map/ppermute | solution.py:297
  90.8 3.7 %collective-permute-start.20 = (f32[4,2,284]{2,1,0:T(2,128)S(1)}, f32[4,2,284]{2,1,0:T(2,128)S(1)}, u32[]{:S(2)}, u32[]{:S(2)}) collective-permute-start(f32[4,2,284]{2,1,0:T(2,128)S(1)} %get-tuple-element.62), channel_id=1, source_target_pairs={{0,16},{1,17},{2,18},{3,19},{4,20},{5,21},{6,22},{7,23},{8,0},{9,1... | collective-permute-start | bytes 27272 | tf_op jit(solution)/shard_map/ppermute | solution.py:297

commit v13 on v10

--- a/solution.py
+++ b/solution.py
@@ -98,8 +98,8 @@
     bit = 1
     while bit < size // 2:
         if bit == 4:
-            carried, peak, total, weighted = lax.optimization_barrier(
-                (carried, peak, total, weighted)
+            carried[0], peak, total, weighted = lax.optimization_barrier(
+                (carried[0], peak, total, weighted)
             )
         other = lax.ppermute(pack_merge(peak, total, weighted), axis, xor_pairs(size, bit))
         peak, total, weighted = merge_pair(peak, total, weighted, other)
@@ -112,6 +112,10 @@
         value = value.reshape((group_rows, steps, head_count) + value.shape[2:])
         return lax.dynamic_slice_in_dim(value, start, span, 2)
 
+    if size >= 16:
+        carried[1], peak, total, weighted = lax.optimization_barrier(
+            (carried[1], peak, total, weighted)
+        )
     partner_start = first_head(index ^ bit)
     own_start = first_head(index)
     sent = window(pack_merge(peak, total, weighted), partner_start)
@@ -206,7 +210,11 @@
     own_keyval = own_first[:, :, slice_width:]
     up_part = sum_over(part_up, "req", req_size)
     hidden = jax.nn.gelu(up_part, approximate=False).astype(jnp.bfloat16)
-    down_part = jnp.dot(hidden, w_down, preferred_element_type=jnp.float32)
+    down_half = w_down.shape[1] // 2
+    down_parts = [
+        jnp.dot(hidden, w_down[:, :down_half], preferred_element_type=jnp.float32),
+        jnp.dot(hidden, w_down[:, down_half:], preferred_element_type=jnp.float32),
+    ]
 
     query_all, riders = gather_xor(own_query, "seq", seq_size, {0: kv_cache})
     kv_cache = riders[0]
@@ -248,8 +256,8 @@
         "gqs,gsd->gqd", weights, value_rows, preferred_element_type=jnp.float32
     )
 
-    own_mixed, down_part = merge_over(
-        local_peak, local_total, local_weighted, "seq", seq_size, down_part, steps, slice_width
+    own_mixed, down_parts = merge_over(
+        local_peak, local_total, local_weighted, "seq", seq_size, down_parts, steps, slice_width
     )
     own_mixed = own_mixed.transpose(1, 0, 2).astype(jnp.bfloat16)
     every_mixed = gather_xor(own_mixed, "req", req_size)[0]
@@ -261,6 +269,7 @@
     mixed_part = every_mixed.transpose(1, 0, 2, 3).reshape(steps, total, slice_width)
     mixed_part = jnp.take(mixed_part, mixed_rows, axis=1, mode="clip").reshape(rows, slice_width)
 
+    down_part = jnp.concatenate(down_parts, axis=1)
     partial_sum = jnp.dot(mixed_part, w_out, preferred_element_type=jnp.float32) + down_part
     chunks = seq_size // req_size
     by_request = partial_sum.reshape(steps, total, part_width)

time: 94 us -> 93.2 us (level)
  waiting for transfers between devices: 30.5 us -> 28.5 us
  matrix products: 9.94 us -> 11.8 us
  starting transfers between devices: 30.1 us -> 28.8 us
    ppermute x3, waiting for transfers between devices: 3.1 us -> 0.62 us  [merge_over(): lax.ppermute(pack_merge(peak, total, weighted), axis, xor_pairs(size, bit))]
    dot_general x1 -> x2, matrix products: 3.39 us -> 5.22 us  [the longest x1 2.93 us: shards(): jnp.dot(hidden, w_down[:, down_half:], preferred_element_type=jnp.float32)]
  transfers between devices with their start and end apart: 21 -> 21, of which waited for: 18 -> 19; matrix products, arithmetic and copies ran while one was open for 15% -> 18% of each run, Pallas kernels for 0% -> 0%
where the time goes in v13:
time: 93.2 us; the launch traced here: 92.2 us
  starting transfers between devices  28.8 us (31%)
  waiting for transfers between devices  28.5 us (31%)
  local copies, waits for them, and re-layouts  12.4 us (13%)
  matrix products  11.8 us (13%)
  other arithmetic  9.15 us (10%)
  between operations  1.53 us (2%)
    ppermute x10, waiting for transfers between devices, gather_xor(): lax.ppermute(stacked, axis, xor_pairs(size, bit))  15.9 us
    ppermute x10, starting transfers between devices, gather_xor(): lax.ppermute(stacked, axis, xor_pairs(size, bit))  12.6 us
    ppermute x3, waiting for transfers between devices, scatter_sum(): blocks = keep + lax.ppermute(send, axis, xor_pairs(size, bit))  6.08 us
    ppermute x1, starting transfers between devices, shards(): lax.ppermute(own_block, ALL, own_routes)  4.61 us
    ppermute x3, starting transfers between devices, merge_over(): lax.ppermute(pack_merge(peak, total, weighted), axis, xor_pairs(size, bit))  3.44 us
    dot_general x1, matrix products, shards(): part_up = jnp.dot(normed_part, w_up, preferred_element_type=jnp.float32)  3.32 us
    ppermute x3, starting transfers between devices, scatter_sum(): blocks = keep + lax.ppermute(send, axis, xor_pairs(size, bit))  3.3 us
    concatenate x12, local copies, waits for them, and re-layouts, pack_merge(): jnp.concatenate([jnp.stack(split_exact(peak) + split_exact(total), axis=-...  3.19 us
  transfers between devices with their start and end apart: 21, of which 19 were waited for; matrix products, arithmetic and copies ran while one was open for 18% of the time, Pallas kernels for 0%

profile of v13, /device:TPU:2, one launch (start us, length us, event | category | flops | bytes accessed | tf_op | source)
XLA Modules:
  0.0 92.2 jit_solution(754379091206135997)
XLA Ops:
  0.8 0.8 dynamic_slice.22
  1.7 0.8 select_reduce_fusion.2
  2.6 0.7 select_reduce_fusion.1
  4.5 0.7 pad_maximum_fusion.8
  5.3 2.7 %collective-permute-start.1 = (bf16[2,4,2,284]{3,2,1,0:T(2,128)(2,1)S(1)}, bf16[2,4,2,284]{3,2,1,0:T(2,128)(2,1)S(1)}, u32[]{:S(2)}, u32[]{:S(2)}) collective-permute-start(bf16[2,4,2,284]{3,2,1,0:T(2,128)(2,1)S(1)} %pad_maximum_fusion.8), channel_id=1, source_target_pairs={{0,8},{1,9},{2,10},{3,11},{4,12},{5,13},{6,14},{7,15},{8,0},{9,1},... | collective-permute-start | bytes 27272 | tf_op jit(solution)/shard_map/ppermute | solution.py:22
  7.9 0.7 fusion.135
  8.6 1.3 %collective-permute-done.1 = bf16[2,4,2,284]{3,2,1,0:T(2,128)(2,1)S(1)} collective-permute-done((bf16[2,4,2,284]{3,2,1,0:T(2,128)(2,1)S(1)}, bf16[2,4,2,284]{3,2,1,0:T(2,128)(2,1)S(1)}, u32[]{:S(2)}, u32[]{:S(2)}) %collective-permute-start.1) | collective-permute-done | bytes 9120 | tf_op jit(solution)/shard_map/ppermute | solution.py:22
  10.0 1.6 %collective-permute-start.2 = (bf16[2,2,4,2,284]{4,3,2,1,0:T(2,128)(2,1)S(1)}, bf16[2,2,4,2,284]{4,3,2,1,0:T(2,128)(2,1)S(1)}, u32[]{:S(2)}, u32[]{:S(2)}) collective-permute-start(bf16[2,2,4,2,284]{4,3,2,1,0:T(2,128)(2,1)S(1)} %pad_maximum_fusion.6), channel_id=1, source_target_pairs={{0,4},{1,5},{2,6},{3,7},{4,0},{5,1},{6,2},{7,3},{8,12},{9,13},{10,... | collective-permute-start | bytes 54536 | tf_op jit(solution)/shard_map/ppermute | solution.py:22
  11.8 0.8 dynamic-slice
  12.6 0.8 dynamic-slice.1
  13.9 1.6 %collective-permute-start.3 = (bf16[2,2,2,4,2,284]{5,4,3,2,1,0:T(2,128)(2,1)S(1)}, bf16[2,2,2,4,2,284]{5,4,3,2,1,0:T(2,128)(2,1)S(1)}, u32[]{:S(2)}, u32[]{:S(2)}) collective-permute-start(bf16[2,2,2,4,2,284]{5,4,3,2,1,0:T(2,128)(2,1)S(1)} %pad_maximum_fusion.3), channel_id=1, source_target_pairs={{0,2},{1,3},{2,0},{3,1},{4,6},{5,7},{6,4},{7,5},{8,10},{9,11},{10,... | collective-permute-start | bytes 109064 | tf_op jit(solution)/shard_map/ppermute | solution.py:22
  15.6 2.5 %collective-permute-done.3 = bf16[2,2,2,4,2,284]{5,4,3,2,1,0:T(2,128)(2,1)S(1)} collective-permute-done((bf16[2,2,2,4,2,284]{5,4,3,2,1,0:T(2,128)(2,1)S(1)}, bf16[2,2,2,4,2,284]{5,4,3,2,1,0:T(2,128)(2,1)S(1)}, u32[]{:S(2)}, u32[]{:S(2)}) %collective-permute-start.3) | collective-permute-done | bytes 36384 | tf_op jit(solution)/shard_map/ppermute | solution.py:22
  18.5 1.1 %collective-permute-done.4 = bf16[2,2,2,2,4,2,284]{6,5,4,3,2,1,0:T(2,128)(2,1)S(1)} collective-permute-done((bf16[2,2,2,2,4,2,284]{6,5,4,3,2,1,0:T(2,128)(2,1)S(1)}, bf16[2,2,2,2,4,2,284]{6,5,4,3,2,1,0:T(2,128)(2,1)S(1)}, u32[]{:S(2)}, u32[]{:S(2)}) %collective-permute-start.4) | collective-permute-done | bytes 72736 | tf_op jit(solution)/shard_map/ppermute | solution.py:22
  19.9 1.0 %gather_fusion = bf16[32,4,2,284]{3,2,1,0:T(2,128)(2,1)S(1)} fusion(bf16[32,4,2,284]{3,2,1,0:T(2,128)(2,1)S(1)} %bitcast.285, s32[1024]{0:T(1024)S(1)} %get-tuple-element.110), kind=kCustom, calls=%fused_computation | custom fusion | bytes 290944 | tf_op jit(solution)/shard_map/jit(_take)/gather | solution.py:190
  22.4 1.8 %fusion.121 = f32[16,284]{1,0:T(8,128)S(1)} fusion(bf16[2272,284]{0,1:T(8,128)(2,1)} %param.17, f32[16,4544]{1,0:T(8,128)S(1)} %reshape.879, s32[]{:T(128)S(6)} %select_n.335, f32[2272]{0:T(1024)S(1)} %dynamic-slice.1, f32[2272]{0:T(1024)S(1)} %dynamic-slice, f32[16]{0:T(128)S(1)} %rsqrt.12, f32[16]{0:T(128)S(1)} %div.135), kind=kOutput, calls=%fused_computation.340 | convolution fusion | flops 20829696 | bytes 1481732 | tf_op jit(solution)/shard_map/dot_general | solution.py:195
  24.5 1.4 %collective-permute-start.5 = (f32[16,412]{1,0:T(8,128)S(1)}, f32[16,412]{1,0:T(8,128)S(1)}, u32[]{:S(2)}, u32[]{:S(2)}) collective-permute-start(f32[16,412]{1,0:T(8,128)S(1)} %pad_maximum_fusion.5), channel_id=1, source_target_pairs={{0,16},{16,0},{1,17},{17,1},{2,18},{18,2},{3,19},{19,3},{4,20},{20... | collective-permute-start | bytes 79112 | tf_op jit(solution)/shard_map/ppermute | solution.py:40
  25.9 3.3 %fusion.123 = f32[16,1136]{1,0:T(8,128)S(1)} fusion(bf16[2272,1136]{1,0:T(8,128)(2,1)} %param.20, f32[16,4544]{1,0:T(8,128)S(1)} %reshape.879, s32[]{:T(128)S(6)} %select_n.335, f32[2272]{0:T(1024)S(1)} %dynamic-slice.1, f32[2272]{0:T(1024)S(1)} %dynamic-slice, f32[16]{0:T(128)S(1)} %rsqrt.12, f32[16]{0:T(128)S(1)} %div.135), kind=kOutput, calls=%fused_computation.341 | convolution fusion | flops 82773504 | bytes 5407748 | tf_op jit(solution)/shard_map/dot_general | solution.py:198
  29.7 2.6 %collective-permute-start.7 = (bf16[4,2,284]{2,1,0:T(2,128)(2,1)S(1)}, bf16[4,2,284]{2,1,0:T(2,128)(2,1)S(1)}, u32[]{:S(2)}, u32[]{:S(2)}) collective-permute-start(bf16[4,2,284]{2,1,0:T(2,128)(2,1)S(1)} %slice.427), channel_id=1, source_target_pairs={{0,8},{1,9},{2,10},{3,11},{4,12},{5,13},{6,14},{7,15},{8,0},{9,1},... | collective-permute-start | bytes 13640 | tf_op jit(solution)/shard_map/ppermute | solution.py:22
  32.5 1.8 %collective-permute-done.7 = bf16[4,2,284]{2,1,0:T(2,128)(2,1)S(1)} collective-permute-done((bf16[4,2,284]{2,1,0:T(2,128)(2,1)S(1)}, bf16[4,2,284]{2,1,0:T(2,128)(2,1)S(1)}, u32[]{:S(2)}, u32[]{:S(2)}) %collective-permute-start.7) | collective-permute-done | bytes 4576 | tf_op jit(solution)/shard_map/ppermute | solution.py:22
  34.5 1.6 %collective-permute-start.8 = (bf16[2,4,2,284]{3,2,1,0:T(2,128)(2,1)S(1)}, bf16[2,4,2,284]{3,2,1,0:T(2,128)(2,1)S(1)}, u32[]{:S(2)}, u32[]{:S(2)}) collective-permute-start(bf16[2,4,2,284]{3,2,1,0:T(2,128)(2,1)S(1)} %pad_maximum_fusion.9), channel_id=1, source_target_pairs={{0,4},{1,5},{2,6},{3,7},{4,0},{5,1},{6,2},{7,3},{8,12},{9,13},{10,... | collective-permute-start | bytes 27272 | tf_op jit(solution)/shard_map/ppermute | solution.py:22
  36.3 1.9 %collective-permute-done.8 = bf16[2,4,2,284]{3,2,1,0:T(2,128)(2,1)S(1)} collective-permute-done((bf16[2,4,2,284]{3,2,1,0:T(2,128)(2,1)S(1)}, bf16[2,4,2,284]{3,2,1,0:T(2,128)(2,1)S(1)}, u32[]{:S(2)}, u32[]{:S(2)}) %collective-permute-start.8) | collective-permute-done | bytes 9120 | tf_op jit(solution)/shard_map/ppermute | solution.py:22
  38.3 1.6 %collective-permute-start.9 = (bf16[2,2,4,2,284]{4,3,2,1,0:T(2,128)(2,1)S(1)}, bf16[2,2,4,2,284]{4,3,2,1,0:T(2,128)(2,1)S(1)}, u32[]{:S(2)}, u32[]{:S(2)}) collective-permute-start(bf16[2,2,4,2,284]{4,3,2,1,0:T(2,128)(2,1)S(1)} %pad_maximum_fusion.7), channel_id=1, source_target_pairs={{0,2},{1,3},{2,0},{3,1},{4,6},{5,7},{6,4},{7,5},{8,10},{9,11},{10,... | collective-permute-start | bytes 54536 | tf_op jit(solution)/shard_map/ppermute | solution.py:22
  39.9 2.3 %collective-permute-done.9 = bf16[2,2,4,2,284]{4,3,2,1,0:T(2,128)(2,1)S(1)} collective-permute-done((bf16[2,2,4,2,284]{4,3,2,1,0:T(2,128)(2,1)S(1)}, bf16[2,2,4,2,284]{4,3,2,1,0:T(2,128)(2,1)S(1)}, u32[]{:S(2)}, u32[]{:S(2)}) %collective-permute-start.9) | collective-permute-done | bytes 18208 | tf_op jit(solution)/shard_map/ppermute | solution.py:22
  42.4 1.1 %collective-permute-done.10 = bf16[2,2,2,4,2,284]{5,4,3,2,1,0:T(2,128)(2,1)S(1)} collective-permute-done((bf16[2,2,2,4,2,284]{5,4,3,2,1,0:T(2,128)(2,1)S(1)}, bf16[2,2,2,4,2,284]{5,4,3,2,1,0:T(2,128)(2,1)S(1)}, u32[]{:S(2)}, u32[]{:S(2)}) %collective-permute-start.10) | collective-permute-done | bytes 36384 | tf_op jit(solution)/shard_map/ppermute | solution.py:22
  43.7 0.6 gather_fusion.1
  47.8 0.7 collective-permute-start.6
  49.3 1.6 %collective-permute-start.12 = (bf16[2,284,70]{1,0,2:T(2,128)(2,1)S(1)}, bf16[2,284,70]{1,0,2:T(2,128)(2,1)S(1)}, u32[]{:S(2)}, u32[]{:S(2)}) collective-permute-start(bf16[2,284,70]{1,0,2:T(2,128)(2,1)S(1)} %fusion.23), channel_id=1, source_target_pairs={{0,2},{1,3},{2,0},{3,1},{4,6},{5,7},{6,4},{7,5},{8,10},{9,11},{10,... | collective-permute-start | bytes 238568 | tf_op jit(solution)/shard_map/ppermute | solution.py:104
  50.9 1.5 %collective-permute-done.6 = f32[16,1136]{1,0:T(8,128)S(1)} collective-permute-done((f32[16,1136]{1,0:T(8,128)S(1)}, f32[16,1136]{1,0:T(8,128)S(1)}, u32[]{:S(2)}, u32[]{:S(2)}) %collective-permute-start.6) | collective-permute-done | bytes 72736 | tf_op jit(solution)/shard_map/ppermute | solution.py:40
  52.4 2.3 %fusion = f32[16,1136]{1,0:T(8,128)S(1)} fusion(bf16[1136,2272]{1,0:T(8,128)(2,1)} %param.21, f32[16,1136]{1,0:T(8,128)S(1)} %fusion.123, f32[16,1136]{1,0:T(8,128)S(1)} %collective-permute-done.6), kind=kOutput, calls=%fused_computation.4 | convolution fusion | flops 42495488 | bytes 2835456 | tf_op jit(solution)/shard_map/dot_general | solution.py:215
  55.0 0.6 concatenate.81
  55.6 1.6 %collective-permute-start.13 = (bf16[2,284,70]{1,2,0:T(8,128)(2,1)S(1)}, bf16[2,284,70]{1,2,0:T(8,128)(2,1)S(1)}, u32[]{:S(2)}, u32[]{:S(2)}) collective-permute-start(bf16[2,284,70]{1,2,0:T(8,128)(2,1)S(1)} %concatenate.81), channel_id=1, source_target_pairs={{0,4},{1,5},{2,6},{3,7},{4,0},{5,1},{6,2},{7,3},{8,12},{9,13},{10,... | collective-permute-start | bytes 238568 | tf_op jit(solution)/shard_map/ppermute | solution.py:104
  57.3 2.9 %fusion.2 = f32[16,1136]{1,0:T(8,128)S(1)} fusion(bf16[1136,2272]{1,0:T(8,128)(2,1)} %param.21, f32[16,1136]{1,0:T(8,128)S(1)} %fusion.123, f32[16,1136]{1,0:T(8,128)S(1)} %collective-permute-done.6), kind=kOutput, calls=%fused_computation.6 | convolution fusion | flops 42495488 | bytes 2835456 | tf_op jit(solution)/shard_map/dot_general | solution.py:216
  62.6 0.5 concatenate.89
  63.1 2.7 %collective-permute-start.14 = (bf16[2,4,6,70]{3,2,1,0:T(8,128)(2,1)S(1)}, bf16[2,4,6,70]{3,2,1,0:T(8,128)(2,1)S(1)}, u32[]{:S(2)}, u32[]{:S(2)}) collective-permute-start(bf16[2,4,6,70]{3,2,1,0:T(8,128)(2,1)S(1)} %constant_dynamic-slice_fusion), channel_id=1, source_target_pairs={{0,8},{1,9},{2,10},{3,11},{4,12},{5,13},{6,14},{7,15},{8,0},{9,1},... | collective-permute-start | bytes 20168 | tf_op jit(solution)/shard_map/ppermute | solution.py:122
  66.3 1.5 %collective-permute-done.14 = bf16[2,4,6,70]{3,2,1,0:T(8,128)(2,1)S(1)} collective-permute-done((bf16[2,4,6,70]{3,2,1,0:T(8,128)(2,1)S(1)}, bf16[2,4,6,70]{3,2,1,0:T(8,128)(2,1)S(1)}, u32[]{:S(2)}, u32[]{:S(2)}) %collective-permute-start.14) | collective-permute-done | bytes 6752 | tf_op jit(solution)/shard_map/ppermute | solution.py:122
  68.6 0.7 collective-permute-start.15
  69.3 3.0 %collective-permute-done.15 = bf16[4,2,284]{2,0,1:T(4,128)(2,1)S(1)} collective-permute-done((bf16[4,2,284]{2,0,1:T(4,128)(2,1)S(1)}, bf16[4,2,284]{2,0,1:T(4,128)(2,1)S(1)}, u32[]{:S(2)}, u32[]{:S(2)}) %collective-permute-start.15) | collective-permute-done | bytes 4576 | tf_op jit(solution)/shard_map/ppermute | solution.py:22
  72.3 0.6 gather_fusion.2
  73.7 1.3 %collective-permute-done.16 = f32[2,2,2,4,2,284]{5,4,3,2,1,0:T(2,128)S(1)} collective-permute-done((f32[2,2,2,4,2,284]{5,4,3,2,1,0:T(2,128)S(1)}, f32[2,2,2,4,2,284]{5,4,3,2,1,0:T(2,128)S(1)}, u32[]{:S(2)}, u32[]{:S(2)}) %collective-permute-start.16) | collective-permute-done | bytes 72736 | tf_op jit(solution)/shard_map/ppermute | solution.py:57
  75.0 1.6 %collective-permute-start.17 = (f32[2,2,4,2,284]{4,3,2,1,0:T(2,128)S(1)}, f32[2,2,4,2,284]{4,3,2,1,0:T(2,128)S(1)}, u32[]{:S(2)}, u32[]{:S(2)}) collective-permute-start(f32[2,2,4,2,284]{4,3,2,1,0:T(2,128)S(1)} %fusion.36), channel_id=1, source_target_pairs={{0,2},{1,3},{2,0},{3,1},{4,6},{5,7},{6,4},{7,5},{8,10},{9,11},{10,... | collective-permute-start | bytes 109064 | tf_op jit(solution)/shard_map/ppermute | solution.py:57
  76.6 2.6 %collective-permute-done.17 = f32[2,2,4,2,284]{4,3,2,1,0:T(2,128)S(1)} collective-permute-done((f32[2,2,4,2,284]{4,3,2,1,0:T(2,128)S(1)}, f32[2,2,4,2,284]{4,3,2,1,0:T(2,128)S(1)}, u32[]{:S(2)}, u32[]{:S(2)}) %collective-permute-start.17) | collective-permute-done | bytes 36384 | tf_op jit(solution)/shard_map/ppermute | solution.py:57
  79.2 1.6 %collective-permute-start.18 = (f32[2,4,2,284]{3,2,1,0:T(2,128)S(1)}, f32[2,4,2,284]{3,2,1,0:T(2,128)S(1)}, u32[]{:S(2)}, u32[]{:S(2)}) collective-permute-start(f32[2,4,2,284]{3,2,1,0:T(2,128)S(1)} %fusion.41), channel_id=1, source_target_pairs={{0,4},{1,5},{2,6},{3,7},{4,0},{5,1},{6,2},{7,3},{8,12},{9,13},{10,... | collective-permute-start | bytes 54536 | tf_op jit(solution)/shard_map/ppermute | solution.py:57
  80.9 2.2 %collective-permute-done.18 = f32[2,4,2,284]{3,2,1,0:T(2,128)S(1)} collective-permute-done((f32[2,4,2,284]{3,2,1,0:T(2,128)S(1)}, f32[2,4,2,284]{3,2,1,0:T(2,128)S(1)}, u32[]{:S(2)}, u32[]{:S(2)}) %collective-permute-start.18) | collective-permute-done | bytes 18208 | tf_op jit(solution)/shard_map/ppermute | solution.py:57
  83.2 4.6 %collective-permute-start.19 = (f32[4,2,284]{2,1,0:T(2,128)S(1)}, f32[4,2,284]{2,1,0:T(2,128)S(1)}, u32[]{:S(2)}, u32[]{:S(2)}) collective-permute-start(f32[4,2,284]{2,1,0:T(2,128)S(1)} %get-tuple-element.68), channel_id=1, source_target_pairs={{0,0},{1,1},{2,2},{3,3},{4,4},{5,5},{6,6},{7,7},{8,16},{9,17},{10,... | collective-permute-start | bytes 27272 | tf_op jit(solution)/shard_map/ppermute | solution.py:294
  87.9 0.8 copy.250
  88.7 1.9 %collective-permute-done.19 = f32[4,2,284]{2,1,0:T(2,128)S(1)} collective-permute-done((f32[4,2,284]{2,1,0:T(2,128)S(1)}, f32[4,2,284]{2,1,0:T(2,128)S(1)}, u32[]{:S(2)}, u32[]{:S(2)}) %collective-permute-start.19) | collective-permute-done | bytes 9120 | tf_op jit(solution)/shard_map/ppermute | solution.py:294
  90.6 1.0 %collective-permute-done.20 = f32[4,2,284]{2,1,0:T(2,128)S(1)} collective-permute-done((f32[4,2,284]{2,1,0:T(2,128)S(1)}, f32[4,2,284]{2,1,0:T(2,128)S(1)}, u32[]{:S(2)}, u32[]{:S(2)}) %collective-permute-start.20) | collective-permute-done | bytes 9120 | tf_op jit(solution)/shard_map/ppermute | solution.py:294
  91.5 0.6 add_convert_fusion
  (172 shorter events, 15.1 us)
Async XLA Ops:
  0.6 72.3 %copy-start = (bf16[284,2272]{1,0:T(8,128)(2,1)S(1)}, bf16[284,2272]{1,0:T(8,128)(2,1)}, u32[]{:S(2)}) copy-start(bf16[284,2272]{1,0:T(8,128)(2,1)} %param.19) | copy-start | bytes 3871492
  0.6 3.9 %collective-permute-start = (bf16[4,2,284]{2,1,0:T(2,128)(2,1)}, bf16[4,2,284]{2,1,0:T(2,128)(2,1)S(1)}, u32[]{:S(2)}, u32[]{:S(2)}) collective-permute-start(bf16[4,2,284]{2,1,0:T(2,128)(2,1)} %param.11), channel_id=1, source_target_pairs={{0,16},{16,0},{1,17},{17,1},{2,18},{18,2},{3,19},{19,3},{4,20},{20... | collective-permute-start | bytes 13640 | tf_op jit(solution)/shard_map/ppermute | solution.py:22
  5.3 4.7 %collective-permute-start.1 = (bf16[2,4,2,284]{3,2,1,0:T(2,128)(2,1)S(1)}, bf16[2,4,2,284]{3,2,1,0:T(2,128)(2,1)S(1)}, u32[]{:S(2)}, u32[]{:S(2)}) collective-permute-start(bf16[2,4,2,284]{3,2,1,0:T(2,128)(2,1)S(1)} %pad_maximum_fusion.8), channel_id=1, source_target_pairs={{0,8},{1,9},{2,10},{3,11},{4,12},{5,13},{6,14},{7,15},{8,0},{9,1},... | collective-permute-start | bytes 27272 | tf_op jit(solution)/shard_map/ppermute | solution.py:22
  10.0 3.9 %collective-permute-start.2 = (bf16[2,2,4,2,284]{4,3,2,1,0:T(2,128)(2,1)S(1)}, bf16[2,2,4,2,284]{4,3,2,1,0:T(2,128)(2,1)S(1)}, u32[]{:S(2)}, u32[]{:S(2)}) collective-permute-start(bf16[2,2,4,2,284]{4,3,2,1,0:T(2,128)(2,1)S(1)} %pad_maximum_fusion.6), channel_id=1, source_target_pairs={{0,4},{1,5},{2,6},{3,7},{4,0},{5,1},{6,2},{7,3},{8,12},{9,13},{10,... | collective-permute-start | bytes 54536 | tf_op jit(solution)/shard_map/ppermute | solution.py:22
  13.9 4.2 %collective-permute-start.3 = (bf16[2,2,2,4,2,284]{5,4,3,2,1,0:T(2,128)(2,1)S(1)}, bf16[2,2,2,4,2,284]{5,4,3,2,1,0:T(2,128)(2,1)S(1)}, u32[]{:S(2)}, u32[]{:S(2)}) collective-permute-start(bf16[2,2,2,4,2,284]{5,4,3,2,1,0:T(2,128)(2,1)S(1)} %pad_maximum_fusion.3), channel_id=1, source_target_pairs={{0,2},{1,3},{2,0},{3,1},{4,6},{5,7},{6,4},{7,5},{8,10},{9,11},{10,... | collective-permute-start | bytes 109064 | tf_op jit(solution)/shard_map/ppermute | solution.py:22
  18.3 1.4 %collective-permute-start.4 = (bf16[2,2,2,2,4,2,284]{6,5,4,3,2,1,0:T(2,128)(2,1)S(1)}, bf16[2,2,2,2,4,2,284]{6,5,4,3,2,1,0:T(2,128)(2,1)S(1)}, u32[]{:S(2)}, u32[]{:S(2)}) collective-permute-start(bf16[2,2,2,2,4,2,284]{6,5,4,3,2,1,0:T(2,128)(2,1)S(1)} %pad_maximum_fusion.1), channel_id=1, source_target_pairs={{0,1},{1,0},{2,3},{3,2},{4,5},{5,4},{6,7},{7,6},{8,9},{9,8},{10,11... | collective-permute-start | bytes 218120 | tf_op jit(solution)/shard_map/ppermute | solution.py:22
  22.1 2.0 %copy-start.1 = (bf16[2272,128]{1,0:T(8,128)(2,1)S(1)}, bf16[2272,128]{1,0:T(8,128)(2,1)}, u32[]{:S(2)}) copy-start(bf16[2272,128]{1,0:T(8,128)(2,1)} %param.18) | copy-start | bytes 1744900
  24.5 9.8 %copy-start.2 = (bf16[2,512,128]{2,1,0:T(8,128)(2,1)S(1)}, bf16[2,512,128]{2,1,0:T(8,128)(2,1)}, u32[]{:S(2)}) copy-start(bf16[2,512,128]{2,1,0:T(8,128)(2,1)} %param.12) | copy-start | bytes 786436
  24.5 4.7 %collective-permute-start.5 = (f32[16,412]{1,0:T(8,128)S(1)}, f32[16,412]{1,0:T(8,128)S(1)}, u32[]{:S(2)}, u32[]{:S(2)}) collective-permute-start(f32[16,412]{1,0:T(8,128)S(1)} %pad_maximum_fusion.5), channel_id=1, source_target_pairs={{0,16},{16,0},{1,17},{17,1},{2,18},{18,2},{3,19},{19,3},{4,20},{20... | collective-permute-start | bytes 79112 | tf_op jit(solution)/shard_map/ppermute | solution.py:40
  29.7 4.5 %collective-permute-start.7 = (bf16[4,2,284]{2,1,0:T(2,128)(2,1)S(1)}, bf16[4,2,284]{2,1,0:T(2,128)(2,1)S(1)}, u32[]{:S(2)}, u32[]{:S(2)}) collective-permute-start(bf16[4,2,284]{2,1,0:T(2,128)(2,1)S(1)} %slice.427), channel_id=1, source_target_pairs={{0,8},{1,9},{2,10},{3,11},{4,12},{5,13},{6,14},{7,15},{8,0},{9,1},... | collective-permute-start | bytes 13640 | tf_op jit(solution)/shard_map/ppermute | solution.py:22
  34.5 3.8 %collective-permute-start.8 = (bf16[2,4,2,284]{3,2,1,0:T(2,128)(2,1)S(1)}, bf16[2,4,2,284]{3,2,1,0:T(2,128)(2,1)S(1)}, u32[]{:S(2)}, u32[]{:S(2)}) collective-permute-start(bf16[2,4,2,284]{3,2,1,0:T(2,128)(2,1)S(1)} %pad_maximum_fusion.9), channel_id=1, source_target_pairs={{0,4},{1,5},{2,6},{3,7},{4,0},{5,1},{6,2},{7,3},{8,12},{9,13},{10,... | collective-permute-start | bytes 27272 | tf_op jit(solution)/shard_map/ppermute | solution.py:22
  38.3 3.9 %collective-permute-start.9 = (bf16[2,2,4,2,284]{4,3,2,1,0:T(2,128)(2,1)S(1)}, bf16[2,2,4,2,284]{4,3,2,1,0:T(2,128)(2,1)S(1)}, u32[]{:S(2)}, u32[]{:S(2)}) collective-permute-start(bf16[2,2,4,2,284]{4,3,2,1,0:T(2,128)(2,1)S(1)} %pad_maximum_fusion.7), channel_id=1, source_target_pairs={{0,2},{1,3},{2,0},{3,1},{4,6},{5,7},{6,4},{7,5},{8,10},{9,11},{10,... | collective-permute-start | bytes 54536 | tf_op jit(solution)/shard_map/ppermute | solution.py:22
  42.2 1.3 %collective-permute-start.10 = (bf16[2,2,2,4,2,284]{5,4,3,2,1,0:T(2,128)(2,1)S(1)}, bf16[2,2,2,4,2,284]{5,4,3,2,1,0:T(2,128)(2,1)S(1)}, u32[]{:S(2)}, u32[]{:S(2)}) collective-permute-start(bf16[2,2,2,4,2,284]{5,4,3,2,1,0:T(2,128)(2,1)S(1)} %pad_maximum_fusion.4), channel_id=1, source_target_pairs={{0,1},{1,0},{2,3},{3,2},{4,5},{5,4},{6,7},{7,6},{8,9},{9,8},{10,11... | collective-permute-start | bytes 109064 | tf_op jit(solution)/shard_map/ppermute | solution.py:22
  47.5 1.4 %collective-permute-start.11 = (bf16[2,284,70]{1,0,2:T(2,128)(2,1)S(1)}, bf16[2,284,70]{1,0,2:T(2,128)(2,1)S(1)}, u32[]{:S(2)}, u32[]{:S(2)}) collective-permute-start(bf16[2,284,70]{1,0,2:T(2,128)(2,1)S(1)} %fusion.22), channel_id=1, source_target_pairs={{0,1},{1,0},{2,3},{3,2},{4,5},{5,4},{6,7},{7,6},{8,9},{9,8},{10,11... | collective-permute-start | bytes 238568 | tf_op jit(solution)/shard_map/ppermute | solution.py:104
  47.8 4.6 %collective-permute-start.6 = (f32[16,1136]{1,0:T(8,128)S(1)}, f32[16,1136]{1,0:T(8,128)S(1)}, u32[]{:S(2)}, u32[]{:S(2)}) collective-permute-start(f32[16,1136]{1,0:T(8,128)S(1)} %fusion.123), channel_id=1, source_target_pairs={{0,16},{16,0},{1,17},{17,1},{2,18},{18,2},{3,19},{19,3},{4,20},{20... | collective-permute-start | bytes 218120 | tf_op jit(solution)/shard_map/ppermute | solution.py:40
  49.3 5.4 %collective-permute-start.12 = (bf16[2,284,70]{1,0,2:T(2,128)(2,1)S(1)}, bf16[2,284,70]{1,0,2:T(2,128)(2,1)S(1)}, u32[]{:S(2)}, u32[]{:S(2)}) collective-permute-start(bf16[2,284,70]{1,0,2:T(2,128)(2,1)S(1)} %fusion.23), channel_id=1, source_target_pairs={{0,2},{1,3},{2,0},{3,1},{4,6},{5,7},{6,4},{7,5},{8,10},{9,11},{10,... | collective-permute-start | bytes 238568 | tf_op jit(solution)/shard_map/ppermute | solution.py:104
  55.6 4.8 %collective-permute-start.13 = (bf16[2,284,70]{1,2,0:T(8,128)(2,1)S(1)}, bf16[2,284,70]{1,2,0:T(8,128)(2,1)S(1)}, u32[]{:S(2)}, u32[]{:S(2)}) collective-permute-start(bf16[2,284,70]{1,2,0:T(8,128)(2,1)S(1)} %concatenate.81), channel_id=1, source_target_pairs={{0,4},{1,5},{2,6},{3,7},{4,0},{5,1},{6,2},{7,3},{8,12},{9,13},{10,... | collective-permute-start | bytes 238568 | tf_op jit(solution)/shard_map/ppermute | solution.py:104
  63.1 4.7 %collective-permute-start.14 = (bf16[2,4,6,70]{3,2,1,0:T(8,128)(2,1)S(1)}, bf16[2,4,6,70]{3,2,1,0:T(8,128)(2,1)S(1)}, u32[]{:S(2)}, u32[]{:S(2)}) collective-permute-start(bf16[2,4,6,70]{3,2,1,0:T(8,128)(2,1)S(1)} %constant_dynamic-slice_fusion), channel_id=1, source_target_pairs={{0,8},{1,9},{2,10},{3,11},{4,12},{5,13},{6,14},{7,15},{8,0},{9,1},... | collective-permute-start | bytes 20168 | tf_op jit(solution)/shard_map/ppermute | solution.py:122
  68.6 3.6 %collective-permute-start.15 = (bf16[4,2,284]{2,0,1:T(4,128)(2,1)S(1)}, bf16[4,2,284]{2,0,1:T(4,128)(2,1)S(1)}, u32[]{:S(2)}, u32[]{:S(2)}) collective-permute-start(bf16[4,2,284]{2,0,1:T(4,128)(2,1)S(1)} %get-tuple-element.74), channel_id=1, source_target_pairs={{0,16},{16,0},{1,17},{17,1},{2,18},{18,2},{3,19},{19,3},{4,20},{20... | collective-permute-start | bytes 13640 | tf_op jit(solution)/shard_map/ppermute | solution.py:22
  73.4 18.2 %copy-start.3 = (bf16[4,2,284]{2,1,0:T(2,128)(2,1)S(1)}, bf16[4,2,284]{2,1,0:T(2,128)(2,1)}, u32[]{:S(2)}) copy-start(bf16[4,2,284]{2,1,0:T(2,128)(2,1)} %param.11) | copy-start | bytes 13636
  73.5 1.4 %collective-permute-start.16 = (f32[2,2,2,4,2,284]{5,4,3,2,1,0:T(2,128)S(1)}, f32[2,2,2,4,2,284]{5,4,3,2,1,0:T(2,128)S(1)}, u32[]{:S(2)}, u32[]{:S(2)}) collective-permute-start(f32[2,2,2,4,2,284]{5,4,3,2,1,0:T(2,128)S(1)} %fusion.21), channel_id=1, source_target_pairs={{0,1},{1,0},{2,3},{3,2},{4,5},{5,4},{6,7},{7,6},{8,9},{9,8},{10,11... | collective-permute-start | bytes 218120 | tf_op jit(solution)/shard_map/ppermute | solution.py:57
  75.0 4.2 %collective-permute-start.17 = (f32[2,2,4,2,284]{4,3,2,1,0:T(2,128)S(1)}, f32[2,2,4,2,284]{4,3,2,1,0:T(2,128)S(1)}, u32[]{:S(2)}, u32[]{:S(2)}) collective-permute-start(f32[2,2,4,2,284]{4,3,2,1,0:T(2,128)S(1)} %fusion.36), channel_id=1, source_target_pairs={{0,2},{1,3},{2,0},{3,1},{4,6},{5,7},{6,4},{7,5},{8,10},{9,11},{10,... | collective-permute-start | bytes 109064 | tf_op jit(solution)/shard_map/ppermute | solution.py:57
  79.2 3.9 %collective-permute-start.18 = (f32[2,4,2,284]{3,2,1,0:T(2,128)S(1)}, f32[2,4,2,284]{3,2,1,0:T(2,128)S(1)}, u32[]{:S(2)}, u32[]{:S(2)}) collective-permute-start(f32[2,4,2,284]{3,2,1,0:T(2,128)S(1)} %fusion.41), channel_id=1, source_target_pairs={{0,4},{1,5},{2,6},{3,7},{4,0},{5,1},{6,2},{7,3},{8,12},{9,13},{10,... | collective-permute-start | bytes 54536 | tf_op jit(solution)/shard_map/ppermute | solution.py:57
  83.2 7.4 %collective-permute-start.19 = (f32[4,2,284]{2,1,0:T(2,128)S(1)}, f32[4,2,284]{2,1,0:T(2,128)S(1)}, u32[]{:S(2)}, u32[]{:S(2)}) collective-permute-start(f32[4,2,284]{2,1,0:T(2,128)S(1)} %get-tuple-element.68), channel_id=1, source_target_pairs={{0,0},{1,1},{2,2},{3,3},{4,4},{5,5},{6,6},{7,7},{8,16},{9,17},{10,... | collective-permute-start | bytes 27272 | tf_op jit(solution)/shard_map/ppermute | solution.py:294
  87.8 3.7 %collective-permute-start.20 = (f32[4,2,284]{2,1,0:T(2,128)S(1)}, f32[4,2,284]{2,1,0:T(2,128)S(1)}, u32[]{:S(2)}, u32[]{:S(2)}) collective-permute-start(f32[4,2,284]{2,1,0:T(2,128)S(1)} %get-tuple-element.67), channel_id=1, source_target_pairs={{0,16},{1,17},{2,18},{3,19},{4,20},{5,21},{6,22},{7,23},{8,0},{9,1... | collective-permute-start | bytes 27272 | tf_op jit(solution)/shard_map/ppermute | solution.py:294

commit v14 on v13

--- a/solution.py
+++ b/solution.py
@@ -208,16 +208,27 @@
     )
     own_query = own_first[:, :, :slice_width].astype(jnp.bfloat16)
     own_keyval = own_first[:, :, slice_width:]
-    up_part = sum_over(part_up, "req", req_size)
+    query_levels = seq_size.bit_length() - 1
+    query_all = own_query
+    up_part = None
+    for level in range(query_levels):
+        bit = 2 ** (query_levels - 1 - level)
+        query_all = jnp.stack([query_all, lax.ppermute(query_all, "seq", xor_pairs(seq_size, bit))])
+        if level == 0:
+            query_all, (kv_cache, part_up) = lax.optimization_barrier((query_all, (kv_cache, part_up)))
+        if level == 1:
+            query_all, up_part = lax.optimization_barrier(
+                (query_all, sum_over(part_up, "req", req_size))
+            )
+    if up_part is None:
+        up_part = sum_over(part_up, "req", req_size)
+    query_all = query_all.reshape((seq_size,) + own_query.shape)
     hidden = jax.nn.gelu(up_part, approximate=False).astype(jnp.bfloat16)
     down_half = w_down.shape[1] // 2
     down_parts = [
         jnp.dot(hidden, w_down[:, :down_half], preferred_element_type=jnp.float32),
         jnp.dot(hidden, w_down[:, down_half:], preferred_element_type=jnp.float32),
     ]
-
-    query_all, riders = gather_xor(own_query, "seq", seq_size, {0: kv_cache})
-    kv_cache = riders[0]
     query_all = jnp.take(query_all, seq_slots, axis=0, mode="clip")
     query_all = query_all.transpose(1, 2, 0, 3).reshape(steps, group_rows, model_width)
     flat_positions = positions.reshape(-1)

time: 93.2 us -> 95.4 us (1.024)
  waiting for transfers between devices: 28.5 us -> 33 us
  starting transfers between devices: 28.8 us -> 26.4 us
    ppermute x10 -> x6, waiting for transfers between devices: 15.9 us -> 8.9 us  [gather_xor(): lax.ppermute(stacked, axis, xor_pairs(size, bit))]
    ppermute x0 -> x4, waiting for transfers between devices: none -> 6.26 us  [shards(): lax.ppermute(query_all, 'seq', xor_pairs(seq_size, bit))]
    ppermute x10 -> x6, starting transfers between devices: 12.6 us -> 6.67 us  [gather_xor(): lax.ppermute(stacked, axis, xor_pairs(size, bit))]
    ppermute x0 -> x4, starting transfers between devices: none -> 5.89 us  [shards(): lax.ppermute(query_all, 'seq', xor_pairs(seq_size, bit))]
    ppermute x3, waiting for transfers between devices: 0.62 us -> 3.7 us  [merge_over(): lax.ppermute(pack_merge(peak, total, weighted), axis, xor_pairs(size, bit))]
    ppermute x3, starting transfers between devices: 3.3 us -> 2.11 us  [scatter_sum(): blocks = keep + lax.ppermute(send, axis, xor_pairs(size, bit))]
    ppermute x3, waiting for transfers between devices: 6.08 us -> 7.27 us  [scatter_sum(): blocks = keep + lax.ppermute(send, axis, xor_pairs(size, bit))]
    ppermute x3, starting transfers between devices: 3.44 us -> 2.33 us  [merge_over(): lax.ppermute(pack_merge(peak, total, weighted), axis, xor_pairs(size, bit))]
  transfers between devices with their start and end apart: 21 -> 21, of which waited for: 19 -> 20; matrix products, arithmetic and copies ran while one was open for 18% -> 17% of each run, Pallas kernels for 0% -> 0%
where the time goes in v14:
time: 95.4 us; the launch traced here: 94.1 us
  waiting for transfers between devices  33 us (35%)
  starting transfers between devices  26.4 us (28%)
  local copies, waits for them, and re-layouts  12.4 us (13%)
  matrix products  11.7 us (12%)
  other arithmetic  9.12 us (10%)
  between operations  1.51 us (2%)
    ppermute x6, waiting for transfers between devices, gather_xor(): lax.ppermute(stacked, axis, xor_pairs(size, bit))  8.9 us
    ppermute x3, waiting for transfers between devices, scatter_sum(): blocks = keep + lax.ppermute(send, axis, xor_pairs(size, bit))  7.27 us
    ppermute x6, starting transfers between devices, gather_xor(): lax.ppermute(stacked, axis, xor_pairs(size, bit))  6.67 us
    ppermute x4, waiting for transfers between devices, shards(): lax.ppermute(query_all, 'seq', xor_pairs(seq_size, bit))  6.26 us
    ppermute x4, starting transfers between devices, shards(): lax.ppermute(query_all, 'seq', xor_pairs(seq_size, bit))  5.89 us
    ppermute x1, starting transfers between devices, shards(): lax.ppermute(own_block, ALL, own_routes)  4.53 us
    ppermute x3, waiting for transfers between devices, merge_over(): lax.ppermute(pack_merge(peak, total, weighted), axis, xor_pairs(size, bit))  3.7 us
    dot_general x1, matrix products, shards(): part_up = jnp.dot(normed_part, w_up, preferred_element_type=jnp.float32)  3.32 us
  transfers between devices with their start and end apart: 21, of which 20 were waited for; matrix products, arithmetic and copies ran while one was open for 17% of the time, Pallas kernels for 0%

profile of v14, /device:TPU:2, one launch (start us, length us, event | category | flops | bytes accessed | tf_op | source)
XLA Modules:
  0.0 94.1 jit_solution(9968052991421154871)
XLA Ops:
  0.8 0.8 dynamic_slice.21
  1.7 0.8 select_reduce_fusion.2
  2.6 0.7 select_reduce_fusion.1
  4.5 0.7 pad_maximum_fusion.8
  5.3 2.7 %collective-permute-start.1 = (bf16[2,4,2,284]{3,2,1,0:T(2,128)(2,1)S(1)}, bf16[2,4,2,284]{3,2,1,0:T(2,128)(2,1)S(1)}, u32[]{:S(2)}, u32[]{:S(2)}) collective-permute-start(bf16[2,4,2,284]{3,2,1,0:T(2,128)(2,1)S(1)} %pad_maximum_fusion.8), channel_id=1, source_target_pairs={{0,8},{1,9},{2,10},{3,11},{4,12},{5,13},{6,14},{7,15},{8,0},{9,1},... | collective-permute-start | bytes 27272 | tf_op jit(solution)/shard_map/ppermute | solution.py:22
  7.9 0.7 fusion.134
  8.6 1.3 %collective-permute-done.1 = bf16[2,4,2,284]{3,2,1,0:T(2,128)(2,1)S(1)} collective-permute-done((bf16[2,4,2,284]{3,2,1,0:T(2,128)(2,1)S(1)}, bf16[2,4,2,284]{3,2,1,0:T(2,128)(2,1)S(1)}, u32[]{:S(2)}, u32[]{:S(2)}) %collective-permute-start.1) | collective-permute-done | bytes 9120 | tf_op jit(solution)/shard_map/ppermute | solution.py:22
  10.0 1.6 %collective-permute-start.2 = (bf16[2,2,4,2,284]{4,3,2,1,0:T(2,128)(2,1)S(1)}, bf16[2,2,4,2,284]{4,3,2,1,0:T(2,128)(2,1)S(1)}, u32[]{:S(2)}, u32[]{:S(2)}) collective-permute-start(bf16[2,2,4,2,284]{4,3,2,1,0:T(2,128)(2,1)S(1)} %pad_maximum_fusion.6), channel_id=1, source_target_pairs={{0,4},{1,5},{2,6},{3,7},{4,0},{5,1},{6,2},{7,3},{8,12},{9,13},{10,... | collective-permute-start | bytes 54536 | tf_op jit(solution)/shard_map/ppermute | solution.py:22
  11.8 0.8 dynamic-slice
  12.6 0.8 dynamic-slice.1
  13.9 1.6 %collective-permute-start.3 = (bf16[2,2,2,4,2,284]{5,4,3,2,1,0:T(2,128)(2,1)S(1)}, bf16[2,2,2,4,2,284]{5,4,3,2,1,0:T(2,128)(2,1)S(1)}, u32[]{:S(2)}, u32[]{:S(2)}) collective-permute-start(bf16[2,2,2,4,2,284]{5,4,3,2,1,0:T(2,128)(2,1)S(1)} %pad_maximum_fusion.3), channel_id=1, source_target_pairs={{0,2},{1,3},{2,0},{3,1},{4,6},{5,7},{6,4},{7,5},{8,10},{9,11},{10,... | collective-permute-start | bytes 109064 | tf_op jit(solution)/shard_map/ppermute | solution.py:22
  15.6 2.5 %collective-permute-done.3 = bf16[2,2,2,4,2,284]{5,4,3,2,1,0:T(2,128)(2,1)S(1)} collective-permute-done((bf16[2,2,2,4,2,284]{5,4,3,2,1,0:T(2,128)(2,1)S(1)}, bf16[2,2,2,4,2,284]{5,4,3,2,1,0:T(2,128)(2,1)S(1)}, u32[]{:S(2)}, u32[]{:S(2)}) %collective-permute-start.3) | collective-permute-done | bytes 36384 | tf_op jit(solution)/shard_map/ppermute | solution.py:22
  18.5 1.1 %collective-permute-done.4 = bf16[2,2,2,2,4,2,284]{6,5,4,3,2,1,0:T(2,128)(2,1)S(1)} collective-permute-done((bf16[2,2,2,2,4,2,284]{6,5,4,3,2,1,0:T(2,128)(2,1)S(1)}, bf16[2,2,2,2,4,2,284]{6,5,4,3,2,1,0:T(2,128)(2,1)S(1)}, u32[]{:S(2)}, u32[]{:S(2)}) %collective-permute-start.4) | collective-permute-done | bytes 72736 | tf_op jit(solution)/shard_map/ppermute | solution.py:22
  19.9 1.0 %gather_fusion = bf16[32,4,2,284]{3,2,1,0:T(2,128)(2,1)S(1)} fusion(bf16[32,4,2,284]{3,2,1,0:T(2,128)(2,1)S(1)} %bitcast.284, s32[1024]{0:T(1024)S(1)} %get-tuple-element.116), kind=kCustom, calls=%fused_computation | custom fusion | bytes 290944 | tf_op jit(solution)/shard_map/jit(_take)/gather | solution.py:190
  22.4 1.8 %fusion.121 = f32[16,284]{1,0:T(8,128)S(1)} fusion(bf16[2272,284]{0,1:T(8,128)(2,1)} %param.17, f32[16,4544]{1,0:T(8,128)S(1)} %reshape.880, s32[]{:T(128)S(6)} %select_n.336, f32[2272]{0:T(1024)S(1)} %dynamic-slice.1, f32[2272]{0:T(1024)S(1)} %dynamic-slice, f32[16]{0:T(128)S(1)} %rsqrt.12, f32[16]{0:T(128)S(1)} %div.135), kind=kOutput, calls=%fused_computation.340 | convolution fusion | flops 20829696 | bytes 1481732 | tf_op jit(solution)/shard_map/dot_general | solution.py:195
  24.5 1.4 %collective-permute-start.5 = (f32[16,412]{1,0:T(8,128)S(1)}, f32[16,412]{1,0:T(8,128)S(1)}, u32[]{:S(2)}, u32[]{:S(2)}) collective-permute-start(f32[16,412]{1,0:T(8,128)S(1)} %pad_maximum_fusion.5), channel_id=1, source_target_pairs={{0,16},{16,0},{1,17},{17,1},{2,18},{18,2},{3,19},{19,3},{4,20},{20... | collective-permute-start | bytes 79112 | tf_op jit(solution)/shard_map/ppermute | solution.py:40
  25.9 3.3 %fusion.123 = f32[16,1136]{1,0:T(8,128)S(1)} fusion(bf16[2272,1136]{1,0:T(8,128)(2,1)} %param.20, f32[16,4544]{1,0:T(8,128)S(1)} %reshape.880, s32[]{:T(128)S(6)} %select_n.336, f32[2272]{0:T(1024)S(1)} %dynamic-slice.1, f32[2272]{0:T(1024)S(1)} %dynamic-slice, f32[16]{0:T(128)S(1)} %rsqrt.12, f32[16]{0:T(128)S(1)} %div.135), kind=kOutput, calls=%fused_computation.341 | convolution fusion | flops 82773504 | bytes 5407748 | tf_op jit(solution)/shard_map/dot_general | solution.py:198
  29.7 2.6 %collective-permute-start.6 = (bf16[4,2,284]{2,1,0:T(2,128)(2,1)S(1)}, bf16[4,2,284]{2,1,0:T(2,128)(2,1)S(1)}, u32[]{:S(2)}, u32[]{:S(2)}) collective-permute-start(bf16[4,2,284]{2,1,0:T(2,128)(2,1)S(1)} %slice.427), channel_id=1, source_target_pairs={{0,8},{1,9},{2,10},{3,11},{4,12},{5,13},{6,14},{7,15},{8,0},{9,1},... | collective-permute-start | bytes 13640 | tf_op jit(solution)/shard_map/ppermute | solution.py:216
  32.5 1.8 %collective-permute-done.6 = bf16[4,2,284]{2,1,0:T(2,128)(2,1)S(1)} collective-permute-done((bf16[4,2,284]{2,1,0:T(2,128)(2,1)S(1)}, bf16[4,2,284]{2,1,0:T(2,128)(2,1)S(1)}, u32[]{:S(2)}, u32[]{:S(2)}) %collective-permute-start.6) | collective-permute-done | bytes 4576 | tf_op jit(solution)/shard_map/ppermute | solution.py:216
  34.3 1.6 %collective-permute-start.7 = (bf16[2,4,2,284]{3,2,1,0:T(2,128)(2,1)S(1)}, bf16[2,4,2,284]{3,2,1,0:T(2,128)(2,1)S(1)}, u32[]{:S(2)}, u32[]{:S(2)}) collective-permute-start(bf16[2,4,2,284]{3,2,1,0:T(2,128)(2,1)S(1)} %pad_maximum_fusion.9), channel_id=1, source_target_pairs={{0,4},{1,5},{2,6},{3,7},{4,0},{5,1},{6,2},{7,3},{8,12},{9,13},{10,... | collective-permute-start | bytes 27272 | tf_op jit(solution)/shard_map/ppermute | solution.py:216
  36.1 0.7 collective-permute-start.8
  36.8 1.2 %collective-permute-done.7 = bf16[2,4,2,284]{3,2,1,0:T(2,128)(2,1)S(1)} collective-permute-done((bf16[2,4,2,284]{3,2,1,0:T(2,128)(2,1)S(1)}, bf16[2,4,2,284]{3,2,1,0:T(2,128)(2,1)S(1)}, u32[]{:S(2)}, u32[]{:S(2)}) %collective-permute-start.7) | collective-permute-done | bytes 9120 | tf_op jit(solution)/shard_map/ppermute | solution.py:216
  38.1 2.4 %collective-permute-done.8 = f32[16,1136]{1,0:T(8,128)S(1)} collective-permute-done((f32[16,1136]{1,0:T(8,128)S(1)}, f32[16,1136]{1,0:T(8,128)S(1)}, u32[]{:S(2)}, u32[]{:S(2)}) %collective-permute-start.8) | collective-permute-done | bytes 72736 | tf_op jit(solution)/shard_map/ppermute | solution.py:40
  40.5 1.6 %collective-permute-start.9 = (bf16[2,2,4,2,284]{4,3,2,1,0:T(2,128)(2,1)S(1)}, bf16[2,2,4,2,284]{4,3,2,1,0:T(2,128)(2,1)S(1)}, u32[]{:S(2)}, u32[]{:S(2)}) collective-permute-start(bf16[2,2,4,2,284]{4,3,2,1,0:T(2,128)(2,1)S(1)} %pad_maximum_fusion.7), channel_id=1, source_target_pairs={{0,2},{1,3},{2,0},{3,1},{4,6},{5,7},{6,4},{7,5},{8,10},{9,11},{10,... | collective-permute-start | bytes 54536 | tf_op jit(solution)/shard_map/ppermute | solution.py:216
  42.3 2.1 %collective-permute-done.9 = bf16[2,2,4,2,284]{4,3,2,1,0:T(2,128)(2,1)S(1)} collective-permute-done((bf16[2,2,4,2,284]{4,3,2,1,0:T(2,128)(2,1)S(1)}, bf16[2,2,4,2,284]{4,3,2,1,0:T(2,128)(2,1)S(1)}, u32[]{:S(2)}, u32[]{:S(2)}) %collective-permute-start.9) | collective-permute-done | bytes 18208 | tf_op jit(solution)/shard_map/ppermute | solution.py:216
  44.7 1.1 %collective-permute-done.10 = bf16[2,2,2,4,2,284]{5,4,3,2,1,0:T(2,128)(2,1)S(1)} collective-permute-done((bf16[2,2,2,4,2,284]{5,4,3,2,1,0:T(2,128)(2,1)S(1)}, bf16[2,2,2,4,2,284]{5,4,3,2,1,0:T(2,128)(2,1)S(1)}, u32[]{:S(2)}, u32[]{:S(2)}) %collective-permute-start.10) | collective-permute-done | bytes 36384 | tf_op jit(solution)/shard_map/ppermute | solution.py:216
  46.0 0.6 gather_fusion.1
  50.1 1.1 %collective-permute-done.11 = bf16[2,284,70]{1,0,2:T(2,128)(2,1)S(1)} collective-permute-done((bf16[2,284,70]{1,0,2:T(2,128)(2,1)S(1)}, bf16[2,284,70]{1,0,2:T(2,128)(2,1)S(1)}, u32[]{:S(2)}, u32[]{:S(2)}) %collective-permute-start.11) | collective-permute-done | bytes 79552 | tf_op jit(solution)/shard_map/ppermute | solution.py:104
  51.6 1.6 %collective-permute-start.12 = (bf16[2,284,70]{1,0,2:T(2,128)(2,1)S(1)}, bf16[2,284,70]{1,0,2:T(2,128)(2,1)S(1)}, u32[]{:S(2)}, u32[]{:S(2)}) collective-permute-start(bf16[2,284,70]{1,0,2:T(2,128)(2,1)S(1)} %fusion.23), channel_id=1, source_target_pairs={{0,2},{1,3},{2,0},{3,1},{4,6},{5,7},{6,4},{7,5},{8,10},{9,11},{10,... | collective-permute-start | bytes 238568 | tf_op jit(solution)/shard_map/ppermute | solution.py:104
  53.2 2.3 %fusion = f32[16,1136]{1,0:T(8,128)S(1)} fusion(bf16[1136,2272]{1,0:T(8,128)(2,1)} %param.21, f32[16,1136]{1,0:T(8,128)S(1)} %add.504), kind=kOutput, calls=%fused_computation.4 | convolution fusion | flops 42477312 | bytes 2762752 | tf_op jit(solution)/shard_map/dot_general | solution.py:229
  55.5 1.2 %collective-permute-done.12 = bf16[2,284,70]{1,0,2:T(2,128)(2,1)S(1)} collective-permute-done((bf16[2,284,70]{1,0,2:T(2,128)(2,1)S(1)}, bf16[2,284,70]{1,0,2:T(2,128)(2,1)S(1)}, u32[]{:S(2)}, u32[]{:S(2)}) %collective-permute-start.12) | collective-permute-done | bytes 79552 | tf_op jit(solution)/shard_map/ppermute | solution.py:104
  57.1 0.6 concatenate.81
  58.2 2.9 %fusion.2 = f32[16,1136]{1,0:T(8,128)S(1)} fusion(bf16[1136,2272]{1,0:T(8,128)(2,1)} %param.21, f32[16,1136]{1,0:T(8,128)S(1)} %add.504), kind=kOutput, calls=%fused_computation.6 | convolution fusion | flops 42477312 | bytes 2762752 | tf_op jit(solution)/shard_map/dot_general | solution.py:230
  61.1 1.4 %collective-permute-done.13 = bf16[2,284,70]{1,2,0:T(8,128)(2,1)S(1)} collective-permute-done((bf16[2,284,70]{1,2,0:T(8,128)(2,1)S(1)}, bf16[2,284,70]{1,2,0:T(8,128)(2,1)S(1)}, u32[]{:S(2)}, u32[]{:S(2)}) %collective-permute-start.13) | collective-permute-done | bytes 79552 | tf_op jit(solution)/shard_map/ppermute | solution.py:104
  65.2 2.7 %collective-permute-start.14 = (bf16[2,4,6,70]{3,2,1,0:T(8,128)(2,1)S(1)}, bf16[2,4,6,70]{3,2,1,0:T(8,128)(2,1)S(1)}, u32[]{:S(2)}, u32[]{:S(2)}) collective-permute-start(bf16[2,4,6,70]{3,2,1,0:T(8,128)(2,1)S(1)} %constant_dynamic-slice_fusion), channel_id=1, source_target_pairs={{0,8},{1,9},{2,10},{3,11},{4,12},{5,13},{6,14},{7,15},{8,0},{9,1},... | collective-permute-start | bytes 20168 | tf_op jit(solution)/shard_map/ppermute | solution.py:122
  68.3 1.6 %collective-permute-done.14 = bf16[2,4,6,70]{3,2,1,0:T(8,128)(2,1)S(1)} collective-permute-done((bf16[2,4,6,70]{3,2,1,0:T(8,128)(2,1)S(1)}, bf16[2,4,6,70]{3,2,1,0:T(8,128)(2,1)S(1)}, u32[]{:S(2)}, u32[]{:S(2)}) %collective-permute-start.14) | collective-permute-done | bytes 6752 | tf_op jit(solution)/shard_map/ppermute | solution.py:122
  70.7 0.6 collective-permute-start.15
  71.4 3.0 %collective-permute-done.15 = bf16[4,2,284]{2,0,1:T(4,128)(2,1)S(1)} collective-permute-done((bf16[4,2,284]{2,0,1:T(4,128)(2,1)S(1)}, bf16[4,2,284]{2,0,1:T(4,128)(2,1)S(1)}, u32[]{:S(2)}, u32[]{:S(2)}) %collective-permute-start.15) | collective-permute-done | bytes 4576 | tf_op jit(solution)/shard_map/ppermute | solution.py:22
  74.4 0.6 gather_fusion.2
  75.7 1.3 %collective-permute-done.16 = f32[2,2,2,4,2,284]{5,4,3,2,1,0:T(2,128)S(1)} collective-permute-done((f32[2,2,2,4,2,284]{5,4,3,2,1,0:T(2,128)S(1)}, f32[2,2,2,4,2,284]{5,4,3,2,1,0:T(2,128)S(1)}, u32[]{:S(2)}, u32[]{:S(2)}) %collective-permute-start.16) | collective-permute-done | bytes 72736 | tf_op jit(solution)/shard_map/ppermute | solution.py:57
  77.1 1.6 %collective-permute-start.17 = (f32[2,2,4,2,284]{4,3,2,1,0:T(2,128)S(1)}, f32[2,2,4,2,284]{4,3,2,1,0:T(2,128)S(1)}, u32[]{:S(2)}, u32[]{:S(2)}) collective-permute-start(f32[2,2,4,2,284]{4,3,2,1,0:T(2,128)S(1)} %fusion.36), channel_id=1, source_target_pairs={{0,2},{1,3},{2,0},{3,1},{4,6},{5,7},{6,4},{7,5},{8,10},{9,11},{10,... | collective-permute-start | bytes 109064 | tf_op jit(solution)/shard_map/ppermute | solution.py:57
  78.7 2.6 %collective-permute-done.17 = f32[2,2,4,2,284]{4,3,2,1,0:T(2,128)S(1)} collective-permute-done((f32[2,2,4,2,284]{4,3,2,1,0:T(2,128)S(1)}, f32[2,2,4,2,284]{4,3,2,1,0:T(2,128)S(1)}, u32[]{:S(2)}, u32[]{:S(2)}) %collective-permute-start.17) | collective-permute-done | bytes 36384 | tf_op jit(solution)/shard_map/ppermute | solution.py:57
  81.8 3.4 %collective-permute-done.18 = f32[2,4,2,284]{3,2,1,0:T(2,128)S(1)} collective-permute-done((f32[2,4,2,284]{3,2,1,0:T(2,128)S(1)}, f32[2,4,2,284]{3,2,1,0:T(2,128)S(1)}, u32[]{:S(2)}, u32[]{:S(2)}) %collective-permute-start.18) | collective-permute-done | bytes 18208 | tf_op jit(solution)/shard_map/ppermute | solution.py:57
  85.3 4.5 %collective-permute-start.19 = (f32[4,2,284]{2,1,0:T(2,128)S(1)}, f32[4,2,284]{2,1,0:T(2,128)S(1)}, u32[]{:S(2)}, u32[]{:S(2)}) collective-permute-start(f32[4,2,284]{2,1,0:T(2,128)S(1)} %get-tuple-element.74), channel_id=1, source_target_pairs={{0,0},{1,1},{2,2},{3,3},{4,4},{5,5},{6,6},{7,7},{8,16},{9,17},{10,... | collective-permute-start | bytes 27272 | tf_op jit(solution)/shard_map/ppermute | solution.py:305
  89.9 0.8 copy.250
  90.7 2.0 %collective-permute-done.19 = f32[4,2,284]{2,1,0:T(2,128)S(1)} collective-permute-done((f32[4,2,284]{2,1,0:T(2,128)S(1)}, f32[4,2,284]{2,1,0:T(2,128)S(1)}, u32[]{:S(2)}, u32[]{:S(2)}) %collective-permute-start.19) | collective-permute-done | bytes 9120 | tf_op jit(solution)/shard_map/ppermute | solution.py:305
  92.7 0.8 collective-permute-done.20
  93.5 0.6 add_convert_fusion
  (172 shorter events, 15.9 us)
Async XLA Ops:
  0.6 74.3 %copy-start = (bf16[284,2272]{1,0:T(8,128)(2,1)S(1)}, bf16[284,2272]{1,0:T(8,128)(2,1)}, u32[]{:S(2)}) copy-start(bf16[284,2272]{1,0:T(8,128)(2,1)} %param.19) | copy-start | bytes 3871492
  0.6 3.9 %collective-permute-start = (bf16[4,2,284]{2,1,0:T(2,128)(2,1)}, bf16[4,2,284]{2,1,0:T(2,128)(2,1)S(1)}, u32[]{:S(2)}, u32[]{:S(2)}) collective-permute-start(bf16[4,2,284]{2,1,0:T(2,128)(2,1)} %param.11), channel_id=1, source_target_pairs={{0,16},{16,0},{1,17},{17,1},{2,18},{18,2},{3,19},{19,3},{4,20},{20... | collective-permute-start | bytes 13640 | tf_op jit(solution)/shard_map/ppermute | solution.py:22
  5.3 4.7 %collective-permute-start.1 = (bf16[2,4,2,284]{3,2,1,0:T(2,128)(2,1)S(1)}, bf16[2,4,2,284]{3,2,1,0:T(2,128)(2,1)S(1)}, u32[]{:S(2)}, u32[]{:S(2)}) collective-permute-start(bf16[2,4,2,284]{3,2,1,0:T(2,128)(2,1)S(1)} %pad_maximum_fusion.8), channel_id=1, source_target_pairs={{0,8},{1,9},{2,10},{3,11},{4,12},{5,13},{6,14},{7,15},{8,0},{9,1},... | collective-permute-start | bytes 27272 | tf_op jit(solution)/shard_map/ppermute | solution.py:22
  10.0 3.9 %collective-permute-start.2 = (bf16[2,2,4,2,284]{4,3,2,1,0:T(2,128)(2,1)S(1)}, bf16[2,2,4,2,284]{4,3,2,1,0:T(2,128)(2,1)S(1)}, u32[]{:S(2)}, u32[]{:S(2)}) collective-permute-start(bf16[2,2,4,2,284]{4,3,2,1,0:T(2,128)(2,1)S(1)} %pad_maximum_fusion.6), channel_id=1, source_target_pairs={{0,4},{1,5},{2,6},{3,7},{4,0},{5,1},{6,2},{7,3},{8,12},{9,13},{10,... | collective-permute-start | bytes 54536 | tf_op jit(solution)/shard_map/ppermute | solution.py:22
  13.9 4.2 %collective-permute-start.3 = (bf16[2,2,2,4,2,284]{5,4,3,2,1,0:T(2,128)(2,1)S(1)}, bf16[2,2,2,4,2,284]{5,4,3,2,1,0:T(2,128)(2,1)S(1)}, u32[]{:S(2)}, u32[]{:S(2)}) collective-permute-start(bf16[2,2,2,4,2,284]{5,4,3,2,1,0:T(2,128)(2,1)S(1)} %pad_maximum_fusion.3), channel_id=1, source_target_pairs={{0,2},{1,3},{2,0},{3,1},{4,6},{5,7},{6,4},{7,5},{8,10},{9,11},{10,... | collective-permute-start | bytes 109064 | tf_op jit(solution)/shard_map/ppermute | solution.py:22
  18.3 1.4 %collective-permute-start.4 = (bf16[2,2,2,2,4,2,284]{6,5,4,3,2,1,0:T(2,128)(2,1)S(1)}, bf16[2,2,2,2,4,2,284]{6,5,4,3,2,1,0:T(2,128)(2,1)S(1)}, u32[]{:S(2)}, u32[]{:S(2)}) collective-permute-start(bf16[2,2,2,2,4,2,284]{6,5,4,3,2,1,0:T(2,128)(2,1)S(1)} %pad_maximum_fusion.1), channel_id=1, source_target_pairs={{0,1},{1,0},{2,3},{3,2},{4,5},{5,4},{6,7},{7,6},{8,9},{9,8},{10,11... | collective-permute-start | bytes 218120 | tf_op jit(solution)/shard_map/ppermute | solution.py:22
  22.1 2.0 %copy-start.1 = (bf16[2272,128]{1,0:T(8,128)(2,1)S(1)}, bf16[2272,128]{1,0:T(8,128)(2,1)}, u32[]{:S(2)}) copy-start(bf16[2272,128]{1,0:T(8,128)(2,1)} %param.18) | copy-start | bytes 1744900
  24.5 11.4 %copy-start.2 = (bf16[2,512,128]{2,1,0:T(8,128)(2,1)S(1)}, bf16[2,512,128]{2,1,0:T(8,128)(2,1)}, u32[]{:S(2)}) copy-start(bf16[2,512,128]{2,1,0:T(8,128)(2,1)} %param.12) | copy-start | bytes 786436
  24.5 4.7 %collective-permute-start.5 = (f32[16,412]{1,0:T(8,128)S(1)}, f32[16,412]{1,0:T(8,128)S(1)}, u32[]{:S(2)}, u32[]{:S(2)}) collective-permute-start(f32[16,412]{1,0:T(8,128)S(1)} %pad_maximum_fusion.5), channel_id=1, source_target_pairs={{0,16},{16,0},{1,17},{17,1},{2,18},{18,2},{3,19},{19,3},{4,20},{20... | collective-permute-start | bytes 79112 | tf_op jit(solution)/shard_map/ppermute | solution.py:40
  29.7 4.5 %collective-permute-start.6 = (bf16[4,2,284]{2,1,0:T(2,128)(2,1)S(1)}, bf16[4,2,284]{2,1,0:T(2,128)(2,1)S(1)}, u32[]{:S(2)}, u32[]{:S(2)}) collective-permute-start(bf16[4,2,284]{2,1,0:T(2,128)(2,1)S(1)} %slice.427), channel_id=1, source_target_pairs={{0,8},{1,9},{2,10},{3,11},{4,12},{5,13},{6,14},{7,15},{8,0},{9,1},... | collective-permute-start | bytes 13640 | tf_op jit(solution)/shard_map/ppermute | solution.py:216
  34.3 3.8 %collective-permute-start.7 = (bf16[2,4,2,284]{3,2,1,0:T(2,128)(2,1)S(1)}, bf16[2,4,2,284]{3,2,1,0:T(2,128)(2,1)S(1)}, u32[]{:S(2)}, u32[]{:S(2)}) collective-permute-start(bf16[2,4,2,284]{3,2,1,0:T(2,128)(2,1)S(1)} %pad_maximum_fusion.9), channel_id=1, source_target_pairs={{0,4},{1,5},{2,6},{3,7},{4,0},{5,1},{6,2},{7,3},{8,12},{9,13},{10,... | collective-permute-start | bytes 27272 | tf_op jit(solution)/shard_map/ppermute | solution.py:216
  36.1 4.4 %collective-permute-start.8 = (f32[16,1136]{1,0:T(8,128)S(1)}, f32[16,1136]{1,0:T(8,128)S(1)}, u32[]{:S(2)}, u32[]{:S(2)}) collective-permute-start(f32[16,1136]{1,0:T(8,128)S(1)} %fusion.123), channel_id=1, source_target_pairs={{0,16},{16,0},{1,17},{17,1},{2,18},{18,2},{3,19},{19,3},{4,20},{20... | collective-permute-start | bytes 218120 | tf_op jit(solution)/shard_map/ppermute | solution.py:40
  40.5 3.9 %collective-permute-start.9 = (bf16[2,2,4,2,284]{4,3,2,1,0:T(2,128)(2,1)S(1)}, bf16[2,2,4,2,284]{4,3,2,1,0:T(2,128)(2,1)S(1)}, u32[]{:S(2)}, u32[]{:S(2)}) collective-permute-start(bf16[2,2,4,2,284]{4,3,2,1,0:T(2,128)(2,1)S(1)} %pad_maximum_fusion.7), channel_id=1, source_target_pairs={{0,2},{1,3},{2,0},{3,1},{4,6},{5,7},{6,4},{7,5},{8,10},{9,11},{10,... | collective-permute-start | bytes 54536 | tf_op jit(solution)/shard_map/ppermute | solution.py:216
  44.5 1.3 %collective-permute-start.10 = (bf16[2,2,2,4,2,284]{5,4,3,2,1,0:T(2,128)(2,1)S(1)}, bf16[2,2,2,4,2,284]{5,4,3,2,1,0:T(2,128)(2,1)S(1)}, u32[]{:S(2)}, u32[]{:S(2)}) collective-permute-start(bf16[2,2,2,4,2,284]{5,4,3,2,1,0:T(2,128)(2,1)S(1)} %pad_maximum_fusion.4), channel_id=1, source_target_pairs={{0,1},{1,0},{2,3},{3,2},{4,5},{5,4},{6,7},{7,6},{8,9},{9,8},{10,11... | collective-permute-start | bytes 109064 | tf_op jit(solution)/shard_map/ppermute | solution.py:216
  49.8 1.4 %collective-permute-start.11 = (bf16[2,284,70]{1,0,2:T(2,128)(2,1)S(1)}, bf16[2,284,70]{1,0,2:T(2,128)(2,1)S(1)}, u32[]{:S(2)}, u32[]{:S(2)}) collective-permute-start(bf16[2,284,70]{1,0,2:T(2,128)(2,1)S(1)} %fusion.22), channel_id=1, source_target_pairs={{0,1},{1,0},{2,3},{3,2},{4,5},{5,4},{6,7},{7,6},{8,9},{9,8},{10,11... | collective-permute-start | bytes 238568 | tf_op jit(solution)/shard_map/ppermute | solution.py:104
  51.6 5.1 %collective-permute-start.12 = (bf16[2,284,70]{1,0,2:T(2,128)(2,1)S(1)}, bf16[2,284,70]{1,0,2:T(2,128)(2,1)S(1)}, u32[]{:S(2)}, u32[]{:S(2)}) collective-permute-start(bf16[2,284,70]{1,0,2:T(2,128)(2,1)S(1)} %fusion.23), channel_id=1, source_target_pairs={{0,2},{1,3},{2,0},{3,1},{4,6},{5,7},{6,4},{7,5},{8,10},{9,11},{10,... | collective-permute-start | bytes 238568 | tf_op jit(solution)/shard_map/ppermute | solution.py:104
  57.7 4.8 %collective-permute-start.13 = (bf16[2,284,70]{1,2,0:T(8,128)(2,1)S(1)}, bf16[2,284,70]{1,2,0:T(8,128)(2,1)S(1)}, u32[]{:S(2)}, u32[]{:S(2)}) collective-permute-start(bf16[2,284,70]{1,2,0:T(8,128)(2,1)S(1)} %concatenate.81), channel_id=1, source_target_pairs={{0,4},{1,5},{2,6},{3,7},{4,0},{5,1},{6,2},{7,3},{8,12},{9,13},{10,... | collective-permute-start | bytes 238568 | tf_op jit(solution)/shard_map/ppermute | solution.py:104
  65.2 4.8 %collective-permute-start.14 = (bf16[2,4,6,70]{3,2,1,0:T(8,128)(2,1)S(1)}, bf16[2,4,6,70]{3,2,1,0:T(8,128)(2,1)S(1)}, u32[]{:S(2)}, u32[]{:S(2)}) collective-permute-start(bf16[2,4,6,70]{3,2,1,0:T(8,128)(2,1)S(1)} %constant_dynamic-slice_fusion), channel_id=1, source_target_pairs={{0,8},{1,9},{2,10},{3,11},{4,12},{5,13},{6,14},{7,15},{8,0},{9,1},... | collective-permute-start | bytes 20168 | tf_op jit(solution)/shard_map/ppermute | solution.py:122
  70.7 3.6 %collective-permute-start.15 = (bf16[4,2,284]{2,0,1:T(4,128)(2,1)S(1)}, bf16[4,2,284]{2,0,1:T(4,128)(2,1)S(1)}, u32[]{:S(2)}, u32[]{:S(2)}) collective-permute-start(bf16[4,2,284]{2,0,1:T(4,128)(2,1)S(1)} %get-tuple-element.80), channel_id=1, source_target_pairs={{0,16},{16,0},{1,17},{17,1},{2,18},{18,2},{3,19},{19,3},{4,20},{20... | collective-permute-start | bytes 13640 | tf_op jit(solution)/shard_map/ppermute | solution.py:22
  75.4 18.1 %copy-start.3 = (bf16[4,2,284]{2,1,0:T(2,128)(2,1)S(1)}, bf16[4,2,284]{2,1,0:T(2,128)(2,1)}, u32[]{:S(2)}) copy-start(bf16[4,2,284]{2,1,0:T(2,128)(2,1)} %param.11) | copy-start | bytes 13636
  75.6 1.4 %collective-permute-start.16 = (f32[2,2,2,4,2,284]{5,4,3,2,1,0:T(2,128)S(1)}, f32[2,2,2,4,2,284]{5,4,3,2,1,0:T(2,128)S(1)}, u32[]{:S(2)}, u32[]{:S(2)}) collective-permute-start(f32[2,2,2,4,2,284]{5,4,3,2,1,0:T(2,128)S(1)} %fusion.21), channel_id=1, source_target_pairs={{0,1},{1,0},{2,3},{3,2},{4,5},{5,4},{6,7},{7,6},{8,9},{9,8},{10,11... | collective-permute-start | bytes 218120 | tf_op jit(solution)/shard_map/ppermute | solution.py:57
  77.1 4.2 %collective-permute-start.17 = (f32[2,2,4,2,284]{4,3,2,1,0:T(2,128)S(1)}, f32[2,2,4,2,284]{4,3,2,1,0:T(2,128)S(1)}, u32[]{:S(2)}, u32[]{:S(2)}) collective-permute-start(f32[2,2,4,2,284]{4,3,2,1,0:T(2,128)S(1)} %fusion.36), channel_id=1, source_target_pairs={{0,2},{1,3},{2,0},{3,1},{4,6},{5,7},{6,4},{7,5},{8,10},{9,11},{10,... | collective-permute-start | bytes 109064 | tf_op jit(solution)/shard_map/ppermute | solution.py:57
  81.3 3.9 %collective-permute-start.18 = (f32[2,4,2,284]{3,2,1,0:T(2,128)S(1)}, f32[2,4,2,284]{3,2,1,0:T(2,128)S(1)}, u32[]{:S(2)}, u32[]{:S(2)}) collective-permute-start(f32[2,4,2,284]{3,2,1,0:T(2,128)S(1)} %fusion.41), channel_id=1, source_target_pairs={{0,4},{1,5},{2,6},{3,7},{4,0},{5,1},{6,2},{7,3},{8,12},{9,13},{10,... | collective-permute-start | bytes 54536 | tf_op jit(solution)/shard_map/ppermute | solution.py:57
  85.3 7.5 %collective-permute-start.19 = (f32[4,2,284]{2,1,0:T(2,128)S(1)}, f32[4,2,284]{2,1,0:T(2,128)S(1)}, u32[]{:S(2)}, u32[]{:S(2)}) collective-permute-start(f32[4,2,284]{2,1,0:T(2,128)S(1)} %get-tuple-element.74), channel_id=1, source_target_pairs={{0,0},{1,1},{2,2},{3,3},{4,4},{5,5},{6,6},{7,7},{8,16},{9,17},{10,... | collective-permute-start | bytes 27272 | tf_op jit(solution)/shard_map/ppermute | solution.py:305
  89.8 3.7 %collective-permute-start.20 = (f32[4,2,284]{2,1,0:T(2,128)S(1)}, f32[4,2,284]{2,1,0:T(2,128)S(1)}, u32[]{:S(2)}, u32[]{:S(2)}) collective-permute-start(f32[4,2,284]{2,1,0:T(2,128)S(1)} %get-tuple-element.73), channel_id=1, source_target_pairs={{0,16},{1,17},{2,18},{3,19},{4,20},{5,21},{6,22},{7,23},{8,0},{9,1... | collective-permute-start | bytes 27272 | tf_op jit(solution)/shard_map/ppermute | solution.py:305

commit v15 on v13

--- a/solution.py
+++ b/solution.py
@@ -216,6 +216,7 @@
         jnp.dot(hidden, w_down[:, down_half:], preferred_element_type=jnp.float32),
     ]
 
+    cache_input = kv_cache
     query_all, riders = gather_xor(own_query, "seq", seq_size, {0: kv_cache})
     kv_cache = riders[0]
     query_all = jnp.take(query_all, seq_slots, axis=0, mode="clip")
@@ -237,6 +238,11 @@
         write_mask = global_positions[None, :] == positions[step_index][:, None]
         cache_now = jnp.where(write_mask[:, :, None], new_entry[step_index][:, None, :], cache_now)
 
+    cache_out = cache_input
+    for step_index in range(steps):
+        write_mask = global_positions[None, :] == positions[step_index][:, None]
+        cache_out = jnp.where(write_mask[:, :, None], new_entry[step_index][:, None, :], cache_out)
+
     key_rows = cache_now[:, :, :head_width]
     value_rows = cache_now[:, :, head_width:]
     query_heads = (
@@ -295,7 +301,7 @@
         other_block, ALL, other_routes
     )
     new_states = (states.astype(jnp.float32) + own_branch).astype(jnp.bfloat16)
-    return (new_states, cache_now)
+    return (new_states, cache_out)
 
 
 def solution(mesh):

time: 93.2 us -> 93.9 us (level)
  starting transfers between devices: 28.8 us -> 26.9 us
  waiting for transfers between devices: 28.5 us -> 29.9 us
  local copies, waits for them, and re-layouts: 12.4 us -> 13.5 us
    unnamed x11 -> x12, local copies, waits for them, and re-layouts: 1.16 us -> 2.25 us
  transfers between devices with their start and end apart: 21 -> 21, of which waited for: 19 -> 18; matrix products, arithmetic and copies ran while one was open for 18% -> 19% of each run, Pallas kernels for 0% -> 0%
where the time goes in v15:
time: 93.9 us; the launch traced here: 92.8 us
  waiting for transfers between devices  29.9 us (32%)
  starting transfers between devices  26.9 us (29%)
  local copies, waits for them, and re-layouts  13.5 us (14%)
  matrix products  11.8 us (13%)
  other arithmetic  9.15 us (10%)
  between operations  1.55 us (2%)
    ppermute x10, waiting for transfers between devices, gather_xor(): lax.ppermute(stacked, axis, xor_pairs(size, bit))  16.1 us
    ppermute x10, starting transfers between devices, gather_xor(): lax.ppermute(stacked, axis, xor_pairs(size, bit))  12 us
    ppermute x3, waiting for transfers between devices, scatter_sum(): blocks = keep + lax.ppermute(send, axis, xor_pairs(size, bit))  6.7 us
    ppermute x1, starting transfers between devices, shards(): lax.ppermute(own_block, ALL, own_routes)  4.62 us
    dot_general x1, matrix products, shards(): part_up = jnp.dot(normed_part, w_up, preferred_element_type=jnp.float32)  3.32 us
    concatenate x12, local copies, waits for them, and re-layouts, pack_merge(): jnp.concatenate([jnp.stack(split_exact(peak) + split_exact(total), axis=-...  3.19 us
    dot_general x1, matrix products, shards(): jnp.dot(hidden, w_down[:, down_half:], preferred_element_type=jnp.float32)  2.93 us
    ppermute x3, starting transfers between devices, merge_over(): lax.ppermute(pack_merge(peak, total, weighted), axis, xor_pairs(size, bit))  2.82 us
  transfers between devices with their start and end apart: 21, of which 18 were waited for; matrix products, arithmetic and copies ran while one was open for 19% of the time, Pallas kernels for 0%

profile of v15, /device:TPU:2, one launch (start us, length us, event | category | flops | bytes accessed | tf_op | source)
XLA Modules:
  0.0 92.8 jit_solution(1213049980375336833)
XLA Ops:
  0.8 0.8 dynamic_slice.22
  1.7 0.8 select_reduce_fusion.2
  2.6 0.7 select_reduce_fusion.1
  4.5 0.7 pad_maximum_fusion.8
  5.3 2.7 %collective-permute-start.1 = (bf16[2,4,2,284]{3,2,1,0:T(2,128)(2,1)S(1)}, bf16[2,4,2,284]{3,2,1,0:T(2,128)(2,1)S(1)}, u32[]{:S(2)}, u32[]{:S(2)}) collective-permute-start(bf16[2,4,2,284]{3,2,1,0:T(2,128)(2,1)S(1)} %pad_maximum_fusion.8), channel_id=1, source_target_pairs={{0,8},{1,9},{2,10},{3,11},{4,12},{5,13},{6,14},{7,15},{8,0},{9,1},... | collective-permute-start | bytes 27272 | tf_op jit(solution)/shard_map/ppermute | solution.py:22
  7.9 0.7 fusion.135
  8.6 1.3 %collective-permute-done.1 = bf16[2,4,2,284]{3,2,1,0:T(2,128)(2,1)S(1)} collective-permute-done((bf16[2,4,2,284]{3,2,1,0:T(2,128)(2,1)S(1)}, bf16[2,4,2,284]{3,2,1,0:T(2,128)(2,1)S(1)}, u32[]{:S(2)}, u32[]{:S(2)}) %collective-permute-start.1) | collective-permute-done | bytes 9120 | tf_op jit(solution)/shard_map/ppermute | solution.py:22
  10.0 1.6 %collective-permute-start.2 = (bf16[2,2,4,2,284]{4,3,2,1,0:T(2,128)(2,1)S(1)}, bf16[2,2,4,2,284]{4,3,2,1,0:T(2,128)(2,1)S(1)}, u32[]{:S(2)}, u32[]{:S(2)}) collective-permute-start(bf16[2,2,4,2,284]{4,3,2,1,0:T(2,128)(2,1)S(1)} %pad_maximum_fusion.6), channel_id=1, source_target_pairs={{0,4},{1,5},{2,6},{3,7},{4,0},{5,1},{6,2},{7,3},{8,12},{9,13},{10,... | collective-permute-start | bytes 54536 | tf_op jit(solution)/shard_map/ppermute | solution.py:22
  11.7 1.1 %copy.255 = bf16[2,512,128]{1,2,0:T(8,128)(2,1)S(1)} copy(bf16[2,512,128]{2,1,0:T(8,128)(2,1)} %param.12) | data formatting | bytes 524288 | tf_op args[1]
  12.9 0.8 dynamic-slice
  13.7 0.8 dynamic-slice.1
  14.6 1.6 %collective-permute-start.3 = (bf16[2,2,2,4,2,284]{5,4,3,2,1,0:T(2,128)(2,1)S(1)}, bf16[2,2,2,4,2,284]{5,4,3,2,1,0:T(2,128)(2,1)S(1)}, u32[]{:S(2)}, u32[]{:S(2)}) collective-permute-start(bf16[2,2,2,4,2,284]{5,4,3,2,1,0:T(2,128)(2,1)S(1)} %pad_maximum_fusion.3), channel_id=1, source_target_pairs={{0,2},{1,3},{2,0},{3,1},{4,6},{5,7},{6,4},{7,5},{8,10},{9,11},{10,... | collective-permute-start | bytes 109064 | tf_op jit(solution)/shard_map/ppermute | solution.py:22
  16.2 2.5 %collective-permute-done.3 = bf16[2,2,2,4,2,284]{5,4,3,2,1,0:T(2,128)(2,1)S(1)} collective-permute-done((bf16[2,2,2,4,2,284]{5,4,3,2,1,0:T(2,128)(2,1)S(1)}, bf16[2,2,2,4,2,284]{5,4,3,2,1,0:T(2,128)(2,1)S(1)}, u32[]{:S(2)}, u32[]{:S(2)}) %collective-permute-start.3) | collective-permute-done | bytes 36384 | tf_op jit(solution)/shard_map/ppermute | solution.py:22
  19.1 1.1 %collective-permute-done.4 = bf16[2,2,2,2,4,2,284]{6,5,4,3,2,1,0:T(2,128)(2,1)S(1)} collective-permute-done((bf16[2,2,2,2,4,2,284]{6,5,4,3,2,1,0:T(2,128)(2,1)S(1)}, bf16[2,2,2,2,4,2,284]{6,5,4,3,2,1,0:T(2,128)(2,1)S(1)}, u32[]{:S(2)}, u32[]{:S(2)}) %collective-permute-start.4) | collective-permute-done | bytes 72736 | tf_op jit(solution)/shard_map/ppermute | solution.py:22
  20.5 1.0 %gather_fusion = bf16[32,4,2,284]{3,2,1,0:T(2,128)(2,1)S(1)} fusion(bf16[32,4,2,284]{3,2,1,0:T(2,128)(2,1)S(1)} %bitcast.285, s32[1024]{0:T(1024)S(1)} %get-tuple-element.112), kind=kCustom, calls=%fused_computation | custom fusion | bytes 290944 | tf_op jit(solution)/shard_map/jit(_take)/gather | solution.py:190
  23.0 1.8 %fusion.121 = f32[16,284]{1,0:T(8,128)S(1)} fusion(bf16[2272,284]{0,1:T(8,128)(2,1)} %param.17, f32[16,4544]{1,0:T(8,128)S(1)} %reshape.879, s32[]{:T(128)S(6)} %select_n.347, f32[2272]{0:T(1024)S(1)} %dynamic-slice.1, f32[2272]{0:T(1024)S(1)} %dynamic-slice, f32[16]{0:T(128)S(1)} %rsqrt.12, f32[16]{0:T(128)S(1)} %div.135), kind=kOutput, calls=%fused_computation.341 | convolution fusion | flops 20829696 | bytes 1481732 | tf_op jit(solution)/shard_map/dot_general | solution.py:195
  25.1 1.4 %collective-permute-start.5 = (f32[16,412]{1,0:T(8,128)S(1)}, f32[16,412]{1,0:T(8,128)S(1)}, u32[]{:S(2)}, u32[]{:S(2)}) collective-permute-start(f32[16,412]{1,0:T(8,128)S(1)} %pad_maximum_fusion.5), channel_id=1, source_target_pairs={{0,16},{16,0},{1,17},{17,1},{2,18},{18,2},{3,19},{19,3},{4,20},{20... | collective-permute-start | bytes 79112 | tf_op jit(solution)/shard_map/ppermute | solution.py:40
  26.5 3.3 %fusion.123 = f32[16,1136]{1,0:T(8,128)S(1)} fusion(bf16[2272,1136]{1,0:T(8,128)(2,1)} %param.20, f32[16,4544]{1,0:T(8,128)S(1)} %reshape.879, s32[]{:T(128)S(6)} %select_n.347, f32[2272]{0:T(1024)S(1)} %dynamic-slice.1, f32[2272]{0:T(1024)S(1)} %dynamic-slice, f32[16]{0:T(128)S(1)} %rsqrt.12, f32[16]{0:T(128)S(1)} %div.135), kind=kOutput, calls=%fused_computation.342 | convolution fusion | flops 82773504 | bytes 5407748 | tf_op jit(solution)/shard_map/dot_general | solution.py:198
  30.4 2.6 %collective-permute-start.7 = (bf16[4,2,284]{2,1,0:T(2,128)(2,1)S(1)}, bf16[4,2,284]{2,1,0:T(2,128)(2,1)S(1)}, u32[]{:S(2)}, u32[]{:S(2)}) collective-permute-start(bf16[4,2,284]{2,1,0:T(2,128)(2,1)S(1)} %slice.435), channel_id=1, source_target_pairs={{0,8},{1,9},{2,10},{3,11},{4,12},{5,13},{6,14},{7,15},{8,0},{9,1},... | collective-permute-start | bytes 13640 | tf_op jit(solution)/shard_map/ppermute | solution.py:22
  33.1 1.8 %collective-permute-done.7 = bf16[4,2,284]{2,1,0:T(2,128)(2,1)S(1)} collective-permute-done((bf16[4,2,284]{2,1,0:T(2,128)(2,1)S(1)}, bf16[4,2,284]{2,1,0:T(2,128)(2,1)S(1)}, u32[]{:S(2)}, u32[]{:S(2)}) %collective-permute-start.7) | collective-permute-done | bytes 4576 | tf_op jit(solution)/shard_map/ppermute | solution.py:22
  35.1 1.0 %collective-permute-start.8 = (bf16[2,4,2,284]{3,2,1,0:T(2,128)(2,1)S(1)}, bf16[2,4,2,284]{3,2,1,0:T(2,128)(2,1)S(1)}, u32[]{:S(2)}, u32[]{:S(2)}) collective-permute-start(bf16[2,4,2,284]{3,2,1,0:T(2,128)(2,1)S(1)} %pad_maximum_fusion.9), channel_id=1, source_target_pairs={{0,4},{1,5},{2,6},{3,7},{4,0},{5,1},{6,2},{7,3},{8,12},{9,13},{10,... | collective-permute-start | bytes 27272 | tf_op jit(solution)/shard_map/ppermute | solution.py:22
  36.3 2.5 %collective-permute-done.8 = bf16[2,4,2,284]{3,2,1,0:T(2,128)(2,1)S(1)} collective-permute-done((bf16[2,4,2,284]{3,2,1,0:T(2,128)(2,1)S(1)}, bf16[2,4,2,284]{3,2,1,0:T(2,128)(2,1)S(1)}, u32[]{:S(2)}, u32[]{:S(2)}) %collective-permute-start.8) | collective-permute-done | bytes 9120 | tf_op jit(solution)/shard_map/ppermute | solution.py:22
  38.9 1.6 %collective-permute-start.9 = (bf16[2,2,4,2,284]{4,3,2,1,0:T(2,128)(2,1)S(1)}, bf16[2,2,4,2,284]{4,3,2,1,0:T(2,128)(2,1)S(1)}, u32[]{:S(2)}, u32[]{:S(2)}) collective-permute-start(bf16[2,2,4,2,284]{4,3,2,1,0:T(2,128)(2,1)S(1)} %pad_maximum_fusion.7), channel_id=1, source_target_pairs={{0,2},{1,3},{2,0},{3,1},{4,6},{5,7},{6,4},{7,5},{8,10},{9,11},{10,... | collective-permute-start | bytes 54536 | tf_op jit(solution)/shard_map/ppermute | solution.py:22
  40.5 2.3 %collective-permute-done.9 = bf16[2,2,4,2,284]{4,3,2,1,0:T(2,128)(2,1)S(1)} collective-permute-done((bf16[2,2,4,2,284]{4,3,2,1,0:T(2,128)(2,1)S(1)}, bf16[2,2,4,2,284]{4,3,2,1,0:T(2,128)(2,1)S(1)}, u32[]{:S(2)}, u32[]{:S(2)}) %collective-permute-start.9) | collective-permute-done | bytes 18208 | tf_op jit(solution)/shard_map/ppermute | solution.py:22
  43.0 1.1 %collective-permute-done.10 = bf16[2,2,2,4,2,284]{5,4,3,2,1,0:T(2,128)(2,1)S(1)} collective-permute-done((bf16[2,2,2,4,2,284]{5,4,3,2,1,0:T(2,128)(2,1)S(1)}, bf16[2,2,2,4,2,284]{5,4,3,2,1,0:T(2,128)(2,1)S(1)}, u32[]{:S(2)}, u32[]{:S(2)}) %collective-permute-start.10) | collective-permute-done | bytes 36384 | tf_op jit(solution)/shard_map/ppermute | solution.py:22
  44.4 0.6 gather_fusion.1
  48.5 0.7 collective-permute-start.6
  50.0 1.6 %collective-permute-start.12 = (bf16[2,284,70]{1,0,2:T(2,128)(2,1)S(1)}, bf16[2,284,70]{1,0,2:T(2,128)(2,1)S(1)}, u32[]{:S(2)}, u32[]{:S(2)}) collective-permute-start(bf16[2,284,70]{1,0,2:T(2,128)(2,1)S(1)} %fusion.23), channel_id=1, source_target_pairs={{0,2},{1,3},{2,0},{3,1},{4,6},{5,7},{6,4},{7,5},{8,10},{9,11},{10,... | collective-permute-start | bytes 238568 | tf_op jit(solution)/shard_map/ppermute | solution.py:104
  51.6 1.5 %collective-permute-done.6 = f32[16,1136]{1,0:T(8,128)S(1)} collective-permute-done((f32[16,1136]{1,0:T(8,128)S(1)}, f32[16,1136]{1,0:T(8,128)S(1)}, u32[]{:S(2)}, u32[]{:S(2)}) %collective-permute-start.6) | collective-permute-done | bytes 72736 | tf_op jit(solution)/shard_map/ppermute | solution.py:40
  53.0 2.3 %fusion = f32[16,1136]{1,0:T(8,128)S(1)} fusion(bf16[1136,2272]{1,0:T(8,128)(2,1)} %param.21, f32[16,1136]{1,0:T(8,128)S(1)} %fusion.123, f32[16,1136]{1,0:T(8,128)S(1)} %collective-permute-done.6), kind=kOutput, calls=%fused_computation.4 | convolution fusion | flops 42495488 | bytes 2835456 | tf_op jit(solution)/shard_map/dot_general | solution.py:215
  55.7 0.6 concatenate.81
  56.3 1.0 %collective-permute-start.13 = (bf16[2,284,70]{1,2,0:T(8,128)(2,1)S(1)}, bf16[2,284,70]{1,2,0:T(8,128)(2,1)S(1)}, u32[]{:S(2)}, u32[]{:S(2)}) collective-permute-start(bf16[2,284,70]{1,2,0:T(8,128)(2,1)S(1)} %concatenate.81), channel_id=1, source_target_pairs={{0,4},{1,5},{2,6},{3,7},{4,0},{5,1},{6,2},{7,3},{8,12},{9,13},{10,... | collective-permute-start | bytes 238568 | tf_op jit(solution)/shard_map/ppermute | solution.py:104
  57.3 2.9 %fusion.2 = f32[16,1136]{1,0:T(8,128)S(1)} fusion(bf16[1136,2272]{1,0:T(8,128)(2,1)} %param.21, f32[16,1136]{1,0:T(8,128)S(1)} %fusion.123, f32[16,1136]{1,0:T(8,128)S(1)} %collective-permute-done.6), kind=kOutput, calls=%fused_computation.6 | convolution fusion | flops 42495488 | bytes 2835456 | tf_op jit(solution)/shard_map/dot_general | solution.py:216
  60.2 0.9 collective-permute-done.13
  63.8 2.7 %collective-permute-start.14 = (bf16[2,4,6,70]{3,2,1,0:T(8,128)(2,1)S(1)}, bf16[2,4,6,70]{3,2,1,0:T(8,128)(2,1)S(1)}, u32[]{:S(2)}, u32[]{:S(2)}) collective-permute-start(bf16[2,4,6,70]{3,2,1,0:T(8,128)(2,1)S(1)} %constant_dynamic-slice_fusion), channel_id=1, source_target_pairs={{0,8},{1,9},{2,10},{3,11},{4,12},{5,13},{6,14},{7,15},{8,0},{9,1},... | collective-permute-start | bytes 20168 | tf_op jit(solution)/shard_map/ppermute | solution.py:122
  66.9 1.5 %collective-permute-done.14 = bf16[2,4,6,70]{3,2,1,0:T(8,128)(2,1)S(1)} collective-permute-done((bf16[2,4,6,70]{3,2,1,0:T(8,128)(2,1)S(1)}, bf16[2,4,6,70]{3,2,1,0:T(8,128)(2,1)S(1)}, u32[]{:S(2)}, u32[]{:S(2)}) %collective-permute-start.14) | collective-permute-done | bytes 6752 | tf_op jit(solution)/shard_map/ppermute | solution.py:122
  69.3 0.7 collective-permute-start.15
  70.0 3.0 %collective-permute-done.15 = bf16[4,2,284]{2,0,1:T(4,128)(2,1)S(1)} collective-permute-done((bf16[4,2,284]{2,0,1:T(4,128)(2,1)S(1)}, bf16[4,2,284]{2,0,1:T(4,128)(2,1)S(1)}, u32[]{:S(2)}, u32[]{:S(2)}) %collective-permute-start.15) | collective-permute-done | bytes 4576 | tf_op jit(solution)/shard_map/ppermute | solution.py:22
  74.3 1.3 %collective-permute-done.16 = f32[2,2,2,4,2,284]{5,4,3,2,1,0:T(2,128)S(1)} collective-permute-done((f32[2,2,2,4,2,284]{5,4,3,2,1,0:T(2,128)S(1)}, f32[2,2,2,4,2,284]{5,4,3,2,1,0:T(2,128)S(1)}, u32[]{:S(2)}, u32[]{:S(2)}) %collective-permute-start.16) | collective-permute-done | bytes 72736 | tf_op jit(solution)/shard_map/ppermute | solution.py:57
  75.7 1.6 %collective-permute-start.17 = (f32[2,2,4,2,284]{4,3,2,1,0:T(2,128)S(1)}, f32[2,2,4,2,284]{4,3,2,1,0:T(2,128)S(1)}, u32[]{:S(2)}, u32[]{:S(2)}) collective-permute-start(f32[2,2,4,2,284]{4,3,2,1,0:T(2,128)S(1)} %fusion.36), channel_id=1, source_target_pairs={{0,2},{1,3},{2,0},{3,1},{4,6},{5,7},{6,4},{7,5},{8,10},{9,11},{10,... | collective-permute-start | bytes 109064 | tf_op jit(solution)/shard_map/ppermute | solution.py:57
  77.2 2.6 %collective-permute-done.17 = f32[2,2,4,2,284]{4,3,2,1,0:T(2,128)S(1)} collective-permute-done((f32[2,2,4,2,284]{4,3,2,1,0:T(2,128)S(1)}, f32[2,2,4,2,284]{4,3,2,1,0:T(2,128)S(1)}, u32[]{:S(2)}, u32[]{:S(2)}) %collective-permute-start.17) | collective-permute-done | bytes 36384 | tf_op jit(solution)/shard_map/ppermute | solution.py:57
  79.9 1.0 %collective-permute-start.18 = (f32[2,4,2,284]{3,2,1,0:T(2,128)S(1)}, f32[2,4,2,284]{3,2,1,0:T(2,128)S(1)}, u32[]{:S(2)}, u32[]{:S(2)}) collective-permute-start(f32[2,4,2,284]{3,2,1,0:T(2,128)S(1)} %fusion.41), channel_id=1, source_target_pairs={{0,4},{1,5},{2,6},{3,7},{4,0},{5,1},{6,2},{7,3},{8,12},{9,13},{10,... | collective-permute-start | bytes 54536 | tf_op jit(solution)/shard_map/ppermute | solution.py:57
  80.9 2.9 %collective-permute-done.18 = f32[2,4,2,284]{3,2,1,0:T(2,128)S(1)} collective-permute-done((f32[2,4,2,284]{3,2,1,0:T(2,128)S(1)}, f32[2,4,2,284]{3,2,1,0:T(2,128)S(1)}, u32[]{:S(2)}, u32[]{:S(2)}) %collective-permute-start.18) | collective-permute-done | bytes 18208 | tf_op jit(solution)/shard_map/ppermute | solution.py:57
  83.8 4.6 %collective-permute-start.19 = (f32[4,2,284]{2,1,0:T(2,128)S(1)}, f32[4,2,284]{2,1,0:T(2,128)S(1)}, u32[]{:S(2)}, u32[]{:S(2)}) collective-permute-start(f32[4,2,284]{2,1,0:T(2,128)S(1)} %get-tuple-element.68), channel_id=1, source_target_pairs={{0,0},{1,1},{2,2},{3,3},{4,4},{5,5},{6,6},{7,7},{8,16},{9,17},{10,... | collective-permute-start | bytes 27272 | tf_op jit(solution)/shard_map/ppermute | solution.py:300
  88.5 0.8 copy.256
  89.4 1.8 %collective-permute-done.19 = f32[4,2,284]{2,1,0:T(2,128)S(1)} collective-permute-done((f32[4,2,284]{2,1,0:T(2,128)S(1)}, f32[4,2,284]{2,1,0:T(2,128)S(1)}, u32[]{:S(2)}, u32[]{:S(2)}) %collective-permute-start.19) | collective-permute-done | bytes 9120 | tf_op jit(solution)/shard_map/ppermute | solution.py:300
  91.2 1.0 %collective-permute-done.20 = f32[4,2,284]{2,1,0:T(2,128)S(1)} collective-permute-done((f32[4,2,284]{2,1,0:T(2,128)S(1)}, f32[4,2,284]{2,1,0:T(2,128)S(1)}, u32[]{:S(2)}, u32[]{:S(2)}) %collective-permute-start.20) | collective-permute-done | bytes 9120 | tf_op jit(solution)/shard_map/ppermute | solution.py:300
  92.2 0.6 add_convert_fusion
  (173 shorter events, 15.5 us)
Async XLA Ops:
  0.6 72.9 %copy-start = (bf16[284,2272]{1,0:T(8,128)(2,1)S(1)}, bf16[284,2272]{1,0:T(8,128)(2,1)}, u32[]{:S(2)}) copy-start(bf16[284,2272]{1,0:T(8,128)(2,1)} %param.19) | copy-start | bytes 3871492
  0.6 3.9 %collective-permute-start = (bf16[4,2,284]{2,1,0:T(2,128)(2,1)}, bf16[4,2,284]{2,1,0:T(2,128)(2,1)S(1)}, u32[]{:S(2)}, u32[]{:S(2)}) collective-permute-start(bf16[4,2,284]{2,1,0:T(2,128)(2,1)} %param.11), channel_id=1, source_target_pairs={{0,16},{16,0},{1,17},{17,1},{2,18},{18,2},{3,19},{19,3},{4,20},{20... | collective-permute-start | bytes 13640 | tf_op jit(solution)/shard_map/ppermute | solution.py:22
  5.3 4.7 %collective-permute-start.1 = (bf16[2,4,2,284]{3,2,1,0:T(2,128)(2,1)S(1)}, bf16[2,4,2,284]{3,2,1,0:T(2,128)(2,1)S(1)}, u32[]{:S(2)}, u32[]{:S(2)}) collective-permute-start(bf16[2,4,2,284]{3,2,1,0:T(2,128)(2,1)S(1)} %pad_maximum_fusion.8), channel_id=1, source_target_pairs={{0,8},{1,9},{2,10},{3,11},{4,12},{5,13},{6,14},{7,15},{8,0},{9,1},... | collective-permute-start | bytes 27272 | tf_op jit(solution)/shard_map/ppermute | solution.py:22
  10.0 4.5 %collective-permute-start.2 = (bf16[2,2,4,2,284]{4,3,2,1,0:T(2,128)(2,1)S(1)}, bf16[2,2,4,2,284]{4,3,2,1,0:T(2,128)(2,1)S(1)}, u32[]{:S(2)}, u32[]{:S(2)}) collective-permute-start(bf16[2,2,4,2,284]{4,3,2,1,0:T(2,128)(2,1)S(1)} %pad_maximum_fusion.6), channel_id=1, source_target_pairs={{0,4},{1,5},{2,6},{3,7},{4,0},{5,1},{6,2},{7,3},{8,12},{9,13},{10,... | collective-permute-start | bytes 54536 | tf_op jit(solution)/shard_map/ppermute | solution.py:22
  14.6 4.2 %collective-permute-start.3 = (bf16[2,2,2,4,2,284]{5,4,3,2,1,0:T(2,128)(2,1)S(1)}, bf16[2,2,2,4,2,284]{5,4,3,2,1,0:T(2,128)(2,1)S(1)}, u32[]{:S(2)}, u32[]{:S(2)}) collective-permute-start(bf16[2,2,2,4,2,284]{5,4,3,2,1,0:T(2,128)(2,1)S(1)} %pad_maximum_fusion.3), channel_id=1, source_target_pairs={{0,2},{1,3},{2,0},{3,1},{4,6},{5,7},{6,4},{7,5},{8,10},{9,11},{10,... | collective-permute-start | bytes 109064 | tf_op jit(solution)/shard_map/ppermute | solution.py:22
  18.9 1.4 %collective-permute-start.4 = (bf16[2,2,2,2,4,2,284]{6,5,4,3,2,1,0:T(2,128)(2,1)S(1)}, bf16[2,2,2,2,4,2,284]{6,5,4,3,2,1,0:T(2,128)(2,1)S(1)}, u32[]{:S(2)}, u32[]{:S(2)}) collective-permute-start(bf16[2,2,2,2,4,2,284]{6,5,4,3,2,1,0:T(2,128)(2,1)S(1)} %pad_maximum_fusion.1), channel_id=1, source_target_pairs={{0,1},{1,0},{2,3},{3,2},{4,5},{5,4},{6,7},{7,6},{8,9},{9,8},{10,11... | collective-permute-start | bytes 218120 | tf_op jit(solution)/shard_map/ppermute | solution.py:22
  22.8 2.0 %copy-start.2 = (bf16[2272,128]{1,0:T(8,128)(2,1)S(1)}, bf16[2272,128]{1,0:T(8,128)(2,1)}, u32[]{:S(2)}) copy-start(bf16[2272,128]{1,0:T(8,128)(2,1)} %param.18) | copy-start | bytes 1744900
  25.1 9.8 %copy-start.1 = (bf16[2,512,128]{2,1,0:T(8,128)(2,1)S(1)}, bf16[2,512,128]{2,1,0:T(8,128)(2,1)}, u32[]{:S(2)}) copy-start(bf16[2,512,128]{2,1,0:T(8,128)(2,1)} %param.12) | copy-start | bytes 786436
  25.1 4.7 %collective-permute-start.5 = (f32[16,412]{1,0:T(8,128)S(1)}, f32[16,412]{1,0:T(8,128)S(1)}, u32[]{:S(2)}, u32[]{:S(2)}) collective-permute-start(f32[16,412]{1,0:T(8,128)S(1)} %pad_maximum_fusion.5), channel_id=1, source_target_pairs={{0,16},{16,0},{1,17},{17,1},{2,18},{18,2},{3,19},{19,3},{4,20},{20... | collective-permute-start | bytes 79112 | tf_op jit(solution)/shard_map/ppermute | solution.py:40
  30.4 4.5 %collective-permute-start.7 = (bf16[4,2,284]{2,1,0:T(2,128)(2,1)S(1)}, bf16[4,2,284]{2,1,0:T(2,128)(2,1)S(1)}, u32[]{:S(2)}, u32[]{:S(2)}) collective-permute-start(bf16[4,2,284]{2,1,0:T(2,128)(2,1)S(1)} %slice.435), channel_id=1, source_target_pairs={{0,8},{1,9},{2,10},{3,11},{4,12},{5,13},{6,14},{7,15},{8,0},{9,1},... | collective-permute-start | bytes 13640 | tf_op jit(solution)/shard_map/ppermute | solution.py:22
  35.1 3.8 %collective-permute-start.8 = (bf16[2,4,2,284]{3,2,1,0:T(2,128)(2,1)S(1)}, bf16[2,4,2,284]{3,2,1,0:T(2,128)(2,1)S(1)}, u32[]{:S(2)}, u32[]{:S(2)}) collective-permute-start(bf16[2,4,2,284]{3,2,1,0:T(2,128)(2,1)S(1)} %pad_maximum_fusion.9), channel_id=1, source_target_pairs={{0,4},{1,5},{2,6},{3,7},{4,0},{5,1},{6,2},{7,3},{8,12},{9,13},{10,... | collective-permute-start | bytes 27272 | tf_op jit(solution)/shard_map/ppermute | solution.py:22
  38.9 3.9 %collective-permute-start.9 = (bf16[2,2,4,2,284]{4,3,2,1,0:T(2,128)(2,1)S(1)}, bf16[2,2,4,2,284]{4,3,2,1,0:T(2,128)(2,1)S(1)}, u32[]{:S(2)}, u32[]{:S(2)}) collective-permute-start(bf16[2,2,4,2,284]{4,3,2,1,0:T(2,128)(2,1)S(1)} %pad_maximum_fusion.7), channel_id=1, source_target_pairs={{0,2},{1,3},{2,0},{3,1},{4,6},{5,7},{6,4},{7,5},{8,10},{9,11},{10,... | collective-permute-start | bytes 54536 | tf_op jit(solution)/shard_map/ppermute | solution.py:22
  42.9 1.3 %collective-permute-start.10 = (bf16[2,2,2,4,2,284]{5,4,3,2,1,0:T(2,128)(2,1)S(1)}, bf16[2,2,2,4,2,284]{5,4,3,2,1,0:T(2,128)(2,1)S(1)}, u32[]{:S(2)}, u32[]{:S(2)}) collective-permute-start(bf16[2,2,2,4,2,284]{5,4,3,2,1,0:T(2,128)(2,1)S(1)} %pad_maximum_fusion.4), channel_id=1, source_target_pairs={{0,1},{1,0},{2,3},{3,2},{4,5},{5,4},{6,7},{7,6},{8,9},{9,8},{10,11... | collective-permute-start | bytes 109064 | tf_op jit(solution)/shard_map/ppermute | solution.py:22
  48.2 1.4 %collective-permute-start.11 = (bf16[2,284,70]{1,0,2:T(2,128)(2,1)S(1)}, bf16[2,284,70]{1,0,2:T(2,128)(2,1)S(1)}, u32[]{:S(2)}, u32[]{:S(2)}) collective-permute-start(bf16[2,284,70]{1,0,2:T(2,128)(2,1)S(1)} %fusion.22), channel_id=1, source_target_pairs={{0,1},{1,0},{2,3},{3,2},{4,5},{5,4},{6,7},{7,6},{8,9},{9,8},{10,11... | collective-permute-start | bytes 238568 | tf_op jit(solution)/shard_map/ppermute | solution.py:104
  48.5 4.6 %collective-permute-start.6 = (f32[16,1136]{1,0:T(8,128)S(1)}, f32[16,1136]{1,0:T(8,128)S(1)}, u32[]{:S(2)}, u32[]{:S(2)}) collective-permute-start(f32[16,1136]{1,0:T(8,128)S(1)} %fusion.123), channel_id=1, source_target_pairs={{0,16},{16,0},{1,17},{17,1},{2,18},{18,2},{3,19},{19,3},{4,20},{20... | collective-permute-start | bytes 218120 | tf_op jit(solution)/shard_map/ppermute | solution.py:40
  50.0 5.4 %collective-permute-start.12 = (bf16[2,284,70]{1,0,2:T(2,128)(2,1)S(1)}, bf16[2,284,70]{1,0,2:T(2,128)(2,1)S(1)}, u32[]{:S(2)}, u32[]{:S(2)}) collective-permute-start(bf16[2,284,70]{1,0,2:T(2,128)(2,1)S(1)} %fusion.23), channel_id=1, source_target_pairs={{0,2},{1,3},{2,0},{3,1},{4,6},{5,7},{6,4},{7,5},{8,10},{9,11},{10,... | collective-permute-start | bytes 238568 | tf_op jit(solution)/shard_map/ppermute | solution.py:104
  56.3 4.8 %collective-permute-start.13 = (bf16[2,284,70]{1,2,0:T(8,128)(2,1)S(1)}, bf16[2,284,70]{1,2,0:T(8,128)(2,1)S(1)}, u32[]{:S(2)}, u32[]{:S(2)}) collective-permute-start(bf16[2,284,70]{1,2,0:T(8,128)(2,1)S(1)} %concatenate.81), channel_id=1, source_target_pairs={{0,4},{1,5},{2,6},{3,7},{4,0},{5,1},{6,2},{7,3},{8,12},{9,13},{10,... | collective-permute-start | bytes 238568 | tf_op jit(solution)/shard_map/ppermute | solution.py:104
  63.8 4.7 %collective-permute-start.14 = (bf16[2,4,6,70]{3,2,1,0:T(8,128)(2,1)S(1)}, bf16[2,4,6,70]{3,2,1,0:T(8,128)(2,1)S(1)}, u32[]{:S(2)}, u32[]{:S(2)}) collective-permute-start(bf16[2,4,6,70]{3,2,1,0:T(8,128)(2,1)S(1)} %constant_dynamic-slice_fusion), channel_id=1, source_target_pairs={{0,8},{1,9},{2,10},{3,11},{4,12},{5,13},{6,14},{7,15},{8,0},{9,1},... | collective-permute-start | bytes 20168 | tf_op jit(solution)/shard_map/ppermute | solution.py:122
  69.3 3.6 %collective-permute-start.15 = (bf16[4,2,284]{2,0,1:T(4,128)(2,1)S(1)}, bf16[4,2,284]{2,0,1:T(4,128)(2,1)S(1)}, u32[]{:S(2)}, u32[]{:S(2)}) collective-permute-start(bf16[4,2,284]{2,0,1:T(4,128)(2,1)S(1)} %get-tuple-element.76), channel_id=1, source_target_pairs={{0,16},{16,0},{1,17},{17,1},{2,18},{18,2},{3,19},{19,3},{4,20},{20... | collective-permute-start | bytes 13640 | tf_op jit(solution)/shard_map/ppermute | solution.py:22
  74.0 18.2 %copy-start.3 = (bf16[4,2,284]{2,1,0:T(2,128)(2,1)S(1)}, bf16[4,2,284]{2,1,0:T(2,128)(2,1)}, u32[]{:S(2)}) copy-start(bf16[4,2,284]{2,1,0:T(2,128)(2,1)} %param.11) | copy-start | bytes 13636
  74.2 1.4 %collective-permute-start.16 = (f32[2,2,2,4,2,284]{5,4,3,2,1,0:T(2,128)S(1)}, f32[2,2,2,4,2,284]{5,4,3,2,1,0:T(2,128)S(1)}, u32[]{:S(2)}, u32[]{:S(2)}) collective-permute-start(f32[2,2,2,4,2,284]{5,4,3,2,1,0:T(2,128)S(1)} %fusion.21), channel_id=1, source_target_pairs={{0,1},{1,0},{2,3},{3,2},{4,5},{5,4},{6,7},{7,6},{8,9},{9,8},{10,11... | collective-permute-start | bytes 218120 | tf_op jit(solution)/shard_map/ppermute | solution.py:57
  75.7 4.2 %collective-permute-start.17 = (f32[2,2,4,2,284]{4,3,2,1,0:T(2,128)S(1)}, f32[2,2,4,2,284]{4,3,2,1,0:T(2,128)S(1)}, u32[]{:S(2)}, u32[]{:S(2)}) collective-permute-start(f32[2,2,4,2,284]{4,3,2,1,0:T(2,128)S(1)} %fusion.36), channel_id=1, source_target_pairs={{0,2},{1,3},{2,0},{3,1},{4,6},{5,7},{6,4},{7,5},{8,10},{9,11},{10,... | collective-permute-start | bytes 109064 | tf_op jit(solution)/shard_map/ppermute | solution.py:57
  79.9 3.9 %collective-permute-start.18 = (f32[2,4,2,284]{3,2,1,0:T(2,128)S(1)}, f32[2,4,2,284]{3,2,1,0:T(2,128)S(1)}, u32[]{:S(2)}, u32[]{:S(2)}) collective-permute-start(f32[2,4,2,284]{3,2,1,0:T(2,128)S(1)} %fusion.41), channel_id=1, source_target_pairs={{0,4},{1,5},{2,6},{3,7},{4,0},{5,1},{6,2},{7,3},{8,12},{9,13},{10,... | collective-permute-start | bytes 54536 | tf_op jit(solution)/shard_map/ppermute | solution.py:57
  83.8 7.4 %collective-permute-start.19 = (f32[4,2,284]{2,1,0:T(2,128)S(1)}, f32[4,2,284]{2,1,0:T(2,128)S(1)}, u32[]{:S(2)}, u32[]{:S(2)}) collective-permute-start(f32[4,2,284]{2,1,0:T(2,128)S(1)} %get-tuple-element.68), channel_id=1, source_target_pairs={{0,0},{1,1},{2,2},{3,3},{4,4},{5,5},{6,6},{7,7},{8,16},{9,17},{10,... | collective-permute-start | bytes 27272 | tf_op jit(solution)/shard_map/ppermute | solution.py:300
  88.4 3.7 %collective-permute-start.20 = (f32[4,2,284]{2,1,0:T(2,128)S(1)}, f32[4,2,284]{2,1,0:T(2,128)S(1)}, u32[]{:S(2)}, u32[]{:S(2)}) collective-permute-start(f32[4,2,284]{2,1,0:T(2,128)S(1)} %get-tuple-element.67), channel_id=1, source_target_pairs={{0,16},{1,17},{2,18},{3,19},{4,20},{5,21},{6,22},{7,23},{8,0},{9,1... | collective-permute-start | bytes 27272 | tf_op jit(solution)/shard_map/ppermute | solution.py:300

commit v16 on v13

--- a/solution.py
+++ b/solution.py
@@ -120,6 +120,7 @@
     own_start = first_head(index)
     sent = window(pack_merge(peak, total, weighted), partner_start)
     other = lax.ppermute(sent, axis, xor_pairs(size, bit))
+    other, carried[2] = lax.optimization_barrier((other, carried[2]))
     _, total, weighted = merge_pair(
         window(peak, own_start), window(total, own_start), window(weighted, own_start), other
     )
@@ -210,10 +211,10 @@
     own_keyval = own_first[:, :, slice_width:]
     up_part = sum_over(part_up, "req", req_size)
     hidden = jax.nn.gelu(up_part, approximate=False).astype(jnp.bfloat16)
-    down_half = w_down.shape[1] // 2
+    down_cuts = [0, w_down.shape[1] * 3 // 8, w_down.shape[1] * 3 // 4, w_down.shape[1]]
     down_parts = [
-        jnp.dot(hidden, w_down[:, :down_half], preferred_element_type=jnp.float32),
-        jnp.dot(hidden, w_down[:, down_half:], preferred_element_type=jnp.float32),
+        jnp.dot(hidden, w_down[:, start:stop], preferred_element_type=jnp.float32)
+        for start, stop in zip(down_cuts[:-1], down_cuts[1:])
     ]
 
     query_all, riders = gather_xor(own_query, "seq", seq_size, {0: kv_cache})

time: 93.2 us -> 94.2 us (1.011)
  matrix products: 11.8 us -> 13.3 us
    ppermute x3, waiting for transfers between devices: 0.62 us -> 2.18 us  [merge_over(): lax.ppermute(pack_merge(peak, total, weighted), axis, xor_pairs(size, bit))]
    dot_general x2 -> x3, matrix products: 5.22 us -> 6.75 us  [shards(): jnp.dot(hidden, w_down[:, start:stop], preferred_element_type=jnp.float32)]
    ppermute x2, waiting for transfers between devices: 1.48 us -> 0.01 us  [sum_over(): value = value + lax.ppermute(value, axis, xor_pairs(size, bit))]
  transfers between devices with their start and end apart: 21 -> 21, of which waited for: 19 -> 18; matrix products, arithmetic and copies ran while one was open for 18% -> 24% of each run, Pallas kernels for 0% -> 0%
where the time goes in v16:
time: 94.2 us; the launch traced here: 93 us
  starting transfers between devices  28.6 us (30%)
  waiting for transfers between devices  27.9 us (30%)
  matrix products  13.3 us (14%)
  local copies, waits for them, and re-layouts  12.5 us (13%)
  other arithmetic  9.18 us (10%)
  between operations  1.5 us (2%)
    ppermute x10, waiting for transfers between devices, gather_xor(): lax.ppermute(stacked, axis, xor_pairs(size, bit))  15.2 us
    ppermute x10, starting transfers between devices, gather_xor(): lax.ppermute(stacked, axis, xor_pairs(size, bit))  12.5 us
    dot_general x3, matrix products, shards(): jnp.dot(hidden, w_down[:, start:stop], preferred_element_type=jnp.float32)  6.75 us
    ppermute x3, waiting for transfers between devices, scatter_sum(): blocks = keep + lax.ppermute(send, axis, xor_pairs(size, bit))  6.07 us
    ppermute x1, starting transfers between devices, shards(): lax.ppermute(own_block, ALL, own_routes)  4.56 us
    ppermute x3, starting transfers between devices, merge_over(): lax.ppermute(pack_merge(peak, total, weighted), axis, xor_pairs(size, bit))  3.46 us
    dot_general x1, matrix products, shards(): part_up = jnp.dot(normed_part, w_up, preferred_element_type=jnp.float32)  3.32 us
    ppermute x3, starting transfers between devices, scatter_sum(): blocks = keep + lax.ppermute(send, axis, xor_pairs(size, bit))  3.3 us
  transfers between devices with their start and end apart: 21, of which 18 were waited for; matrix products, arithmetic and copies ran while one was open for 24% of the time, Pallas kernels for 0%

profile of v16, /device:TPU:2, one launch (start us, length us, event | category | flops | bytes accessed | tf_op | source)
XLA Modules:
  0.0 93.0 jit_solution(1814761776414204534)
XLA Ops:
  0.8 0.8 dynamic_slice.22
  1.7 0.8 select_reduce_fusion.2
  2.6 0.7 select_reduce_fusion.1
  4.5 0.7 pad_maximum_fusion.8
  5.3 2.7 %collective-permute-start.1 = (bf16[2,4,2,284]{3,2,1,0:T(2,128)(2,1)S(1)}, bf16[2,4,2,284]{3,2,1,0:T(2,128)(2,1)S(1)}, u32[]{:S(2)}, u32[]{:S(2)}) collective-permute-start(bf16[2,4,2,284]{3,2,1,0:T(2,128)(2,1)S(1)} %pad_maximum_fusion.8), channel_id=1, source_target_pairs={{0,8},{1,9},{2,10},{3,11},{4,12},{5,13},{6,14},{7,15},{8,0},{9,1},... | collective-permute-start | bytes 27272 | tf_op jit(solution)/shard_map/ppermute | solution.py:22
  7.9 0.7 fusion.139
  8.6 1.3 %collective-permute-done.1 = bf16[2,4,2,284]{3,2,1,0:T(2,128)(2,1)S(1)} collective-permute-done((bf16[2,4,2,284]{3,2,1,0:T(2,128)(2,1)S(1)}, bf16[2,4,2,284]{3,2,1,0:T(2,128)(2,1)S(1)}, u32[]{:S(2)}, u32[]{:S(2)}) %collective-permute-start.1) | collective-permute-done | bytes 9120 | tf_op jit(solution)/shard_map/ppermute | solution.py:22
  10.0 1.6 %collective-permute-start.2 = (bf16[2,2,4,2,284]{4,3,2,1,0:T(2,128)(2,1)S(1)}, bf16[2,2,4,2,284]{4,3,2,1,0:T(2,128)(2,1)S(1)}, u32[]{:S(2)}, u32[]{:S(2)}) collective-permute-start(bf16[2,2,4,2,284]{4,3,2,1,0:T(2,128)(2,1)S(1)} %pad_maximum_fusion.6), channel_id=1, source_target_pairs={{0,4},{1,5},{2,6},{3,7},{4,0},{5,1},{6,2},{7,3},{8,12},{9,13},{10,... | collective-permute-start | bytes 54536 | tf_op jit(solution)/shard_map/ppermute | solution.py:22
  11.8 0.8 dynamic-slice
  12.6 0.8 dynamic-slice.1
  13.9 1.6 %collective-permute-start.3 = (bf16[2,2,2,4,2,284]{5,4,3,2,1,0:T(2,128)(2,1)S(1)}, bf16[2,2,2,4,2,284]{5,4,3,2,1,0:T(2,128)(2,1)S(1)}, u32[]{:S(2)}, u32[]{:S(2)}) collective-permute-start(bf16[2,2,2,4,2,284]{5,4,3,2,1,0:T(2,128)(2,1)S(1)} %pad_maximum_fusion.3), channel_id=1, source_target_pairs={{0,2},{1,3},{2,0},{3,1},{4,6},{5,7},{6,4},{7,5},{8,10},{9,11},{10,... | collective-permute-start | bytes 109064 | tf_op jit(solution)/shard_map/ppermute | solution.py:22
  15.6 2.5 %collective-permute-done.3 = bf16[2,2,2,4,2,284]{5,4,3,2,1,0:T(2,128)(2,1)S(1)} collective-permute-done((bf16[2,2,2,4,2,284]{5,4,3,2,1,0:T(2,128)(2,1)S(1)}, bf16[2,2,2,4,2,284]{5,4,3,2,1,0:T(2,128)(2,1)S(1)}, u32[]{:S(2)}, u32[]{:S(2)}) %collective-permute-start.3) | collective-permute-done | bytes 36384 | tf_op jit(solution)/shard_map/ppermute | solution.py:22
  18.5 1.1 %collective-permute-done.4 = bf16[2,2,2,2,4,2,284]{6,5,4,3,2,1,0:T(2,128)(2,1)S(1)} collective-permute-done((bf16[2,2,2,2,4,2,284]{6,5,4,3,2,1,0:T(2,128)(2,1)S(1)}, bf16[2,2,2,2,4,2,284]{6,5,4,3,2,1,0:T(2,128)(2,1)S(1)}, u32[]{:S(2)}, u32[]{:S(2)}) %collective-permute-start.4) | collective-permute-done | bytes 72736 | tf_op jit(solution)/shard_map/ppermute | solution.py:22
  19.9 1.0 %gather_fusion = bf16[32,4,2,284]{3,2,1,0:T(2,128)(2,1)S(1)} fusion(bf16[32,4,2,284]{3,2,1,0:T(2,128)(2,1)S(1)} %bitcast.285, s32[1024]{0:T(1024)S(1)} %get-tuple-element.114), kind=kCustom, calls=%fused_computation | custom fusion | bytes 290944 | tf_op jit(solution)/shard_map/jit(_take)/gather | solution.py:191
  22.4 1.8 %fusion.124 = f32[16,284]{1,0:T(8,128)S(1)} fusion(bf16[2272,284]{0,1:T(8,128)(2,1)} %param.17, f32[16,4544]{1,0:T(8,128)S(1)} %reshape.879, s32[]{:T(128)S(6)} %select_n.335, f32[2272]{0:T(1024)S(1)} %dynamic-slice.1, f32[2272]{0:T(1024)S(1)} %dynamic-slice, f32[16]{0:T(128)S(1)} %rsqrt.12, f32[16]{0:T(128)S(1)} %div.135), kind=kOutput, calls=%fused_computation.341 | convolution fusion | flops 20829696 | bytes 1481732 | tf_op jit(solution)/shard_map/dot_general | solution.py:196
  24.5 1.4 %collective-permute-start.5 = (f32[16,412]{1,0:T(8,128)S(1)}, f32[16,412]{1,0:T(8,128)S(1)}, u32[]{:S(2)}, u32[]{:S(2)}) collective-permute-start(f32[16,412]{1,0:T(8,128)S(1)} %pad_maximum_fusion.5), channel_id=1, source_target_pairs={{0,16},{16,0},{1,17},{17,1},{2,18},{18,2},{3,19},{19,3},{4,20},{20... | collective-permute-start | bytes 79112 | tf_op jit(solution)/shard_map/ppermute | solution.py:40
  25.9 3.3 %fusion.126 = f32[16,1136]{1,0:T(8,128)S(1)} fusion(bf16[2272,1136]{1,0:T(8,128)(2,1)} %param.20, f32[16,4544]{1,0:T(8,128)S(1)} %reshape.879, s32[]{:T(128)S(6)} %select_n.335, f32[2272]{0:T(1024)S(1)} %dynamic-slice.1, f32[2272]{0:T(1024)S(1)} %dynamic-slice, f32[16]{0:T(128)S(1)} %rsqrt.12, f32[16]{0:T(128)S(1)} %div.135), kind=kOutput, calls=%fused_computation.342 | convolution fusion | flops 82773504 | bytes 5407748 | tf_op jit(solution)/shard_map/dot_general | solution.py:199
  29.8 2.6 %collective-permute-start.7 = (bf16[4,2,284]{2,1,0:T(2,128)(2,1)S(1)}, bf16[4,2,284]{2,1,0:T(2,128)(2,1)S(1)}, u32[]{:S(2)}, u32[]{:S(2)}) collective-permute-start(bf16[4,2,284]{2,1,0:T(2,128)(2,1)S(1)} %slice.430), channel_id=1, source_target_pairs={{0,8},{1,9},{2,10},{3,11},{4,12},{5,13},{6,14},{7,15},{8,0},{9,1},... | collective-permute-start | bytes 13640 | tf_op jit(solution)/shard_map/ppermute | solution.py:22
  32.5 0.6 collective-permute-start.6
  33.1 1.1 %collective-permute-done.7 = bf16[4,2,284]{2,1,0:T(2,128)(2,1)S(1)} collective-permute-done((bf16[4,2,284]{2,1,0:T(2,128)(2,1)S(1)}, bf16[4,2,284]{2,1,0:T(2,128)(2,1)S(1)}, u32[]{:S(2)}, u32[]{:S(2)}) %collective-permute-start.7) | collective-permute-done | bytes 4576 | tf_op jit(solution)/shard_map/ppermute | solution.py:22
  34.5 1.6 %collective-permute-start.8 = (bf16[2,4,2,284]{3,2,1,0:T(2,128)(2,1)S(1)}, bf16[2,4,2,284]{3,2,1,0:T(2,128)(2,1)S(1)}, u32[]{:S(2)}, u32[]{:S(2)}) collective-permute-start(bf16[2,4,2,284]{3,2,1,0:T(2,128)(2,1)S(1)} %pad_maximum_fusion.9), channel_id=1, source_target_pairs={{0,4},{1,5},{2,6},{3,7},{4,0},{5,1},{6,2},{7,3},{8,12},{9,13},{10,... | collective-permute-start | bytes 27272 | tf_op jit(solution)/shard_map/ppermute | solution.py:22
  36.3 1.9 %collective-permute-done.8 = bf16[2,4,2,284]{3,2,1,0:T(2,128)(2,1)S(1)} collective-permute-done((bf16[2,4,2,284]{3,2,1,0:T(2,128)(2,1)S(1)}, bf16[2,4,2,284]{3,2,1,0:T(2,128)(2,1)S(1)}, u32[]{:S(2)}, u32[]{:S(2)}) %collective-permute-start.8) | collective-permute-done | bytes 9120 | tf_op jit(solution)/shard_map/ppermute | solution.py:22
  38.3 1.6 %collective-permute-start.9 = (bf16[2,2,4,2,284]{4,3,2,1,0:T(2,128)(2,1)S(1)}, bf16[2,2,4,2,284]{4,3,2,1,0:T(2,128)(2,1)S(1)}, u32[]{:S(2)}, u32[]{:S(2)}) collective-permute-start(bf16[2,2,4,2,284]{4,3,2,1,0:T(2,128)(2,1)S(1)} %pad_maximum_fusion.7), channel_id=1, source_target_pairs={{0,2},{1,3},{2,0},{3,1},{4,6},{5,7},{6,4},{7,5},{8,10},{9,11},{10,... | collective-permute-start | bytes 54536 | tf_op jit(solution)/shard_map/ppermute | solution.py:22
  39.9 2.3 %collective-permute-done.9 = bf16[2,2,4,2,284]{4,3,2,1,0:T(2,128)(2,1)S(1)} collective-permute-done((bf16[2,2,4,2,284]{4,3,2,1,0:T(2,128)(2,1)S(1)}, bf16[2,2,4,2,284]{4,3,2,1,0:T(2,128)(2,1)S(1)}, u32[]{:S(2)}, u32[]{:S(2)}) %collective-permute-start.9) | collective-permute-done | bytes 18208 | tf_op jit(solution)/shard_map/ppermute | solution.py:22
  42.4 1.1 %collective-permute-done.10 = bf16[2,2,2,4,2,284]{5,4,3,2,1,0:T(2,128)(2,1)S(1)} collective-permute-done((bf16[2,2,2,4,2,284]{5,4,3,2,1,0:T(2,128)(2,1)S(1)}, bf16[2,2,2,4,2,284]{5,4,3,2,1,0:T(2,128)(2,1)S(1)}, u32[]{:S(2)}, u32[]{:S(2)}) %collective-permute-start.10) | collective-permute-done | bytes 36384 | tf_op jit(solution)/shard_map/ppermute | solution.py:22
  43.7 0.6 gather_fusion.1
  47.8 2.0 %fusion = f32[16,852]{1,0:T(8,128)S(1)} fusion(bf16[1136,2272]{1,0:T(8,128)(2,1)} %param.21, f32[16,1136]{1,0:T(8,128)S(1)} %fusion.126, f32[16,1136]{1,0:T(8,128)S(1)} %collective-permute-done.6), kind=kOutput, calls=%fused_computation.3 | convolution fusion | flops 32171520 | bytes 2235648 | tf_op jit(solution)/shard_map/dot_general | solution.py:216
  50.3 1.6 %collective-permute-start.12 = (bf16[2,284,70]{1,0,2:T(2,128)(2,1)S(1)}, bf16[2,284,70]{1,0,2:T(2,128)(2,1)S(1)}, u32[]{:S(2)}, u32[]{:S(2)}) collective-permute-start(bf16[2,284,70]{1,0,2:T(2,128)(2,1)S(1)} %fusion.25), channel_id=1, source_target_pairs={{0,2},{1,3},{2,0},{3,1},{4,6},{5,7},{6,4},{7,5},{8,10},{9,11},{10,... | collective-permute-start | bytes 238568 | tf_op jit(solution)/shard_map/ppermute | solution.py:104
  51.9 2.6 %fusion.2 = f32[16,852]{1,0:T(8,128)S(1)} fusion(bf16[1136,2272]{1,0:T(8,128)(2,1)} %param.21, f32[16,1136]{1,0:T(8,128)S(1)} %fusion.126, f32[16,1136]{1,0:T(8,128)S(1)} %collective-permute-done.6), kind=kOutput, calls=%fused_computation.5 | convolution fusion | flops 32171520 | bytes 2235648 | tf_op jit(solution)/shard_map/dot_general | solution.py:216
  54.5 1.1 %collective-permute-done.12 = bf16[2,284,70]{1,0,2:T(2,128)(2,1)S(1)} collective-permute-done((bf16[2,284,70]{1,0,2:T(2,128)(2,1)S(1)}, bf16[2,284,70]{1,0,2:T(2,128)(2,1)S(1)}, u32[]{:S(2)}, u32[]{:S(2)}) %collective-permute-start.12) | collective-permute-done | bytes 79552 | tf_op jit(solution)/shard_map/ppermute | solution.py:104
  55.9 0.6 concatenate.81
  56.5 1.6 %collective-permute-start.13 = (bf16[2,284,70]{1,2,0:T(8,128)(2,1)S(1)}, bf16[2,284,70]{1,2,0:T(8,128)(2,1)S(1)}, u32[]{:S(2)}, u32[]{:S(2)}) collective-permute-start(bf16[2,284,70]{1,2,0:T(8,128)(2,1)S(1)} %concatenate.81), channel_id=1, source_target_pairs={{0,4},{1,5},{2,6},{3,7},{4,0},{5,1},{6,2},{7,3},{8,12},{9,13},{10,... | collective-permute-start | bytes 238568 | tf_op jit(solution)/shard_map/ppermute | solution.py:104
  58.2 2.1 %fusion.4 = f32[16,568]{1,0:T(8,128)S(1)} fusion(bf16[1136,2272]{1,0:T(8,128)(2,1)} %param.21, f32[16,1136]{1,0:T(8,128)S(1)} %fusion.126, f32[16,1136]{1,0:T(8,128)S(1)} %collective-permute-done.6), kind=kOutput, calls=%fused_computation.9 | convolution fusion | flops 21847552 | bytes 1635840 | tf_op jit(solution)/shard_map/dot_general | solution.py:216
  60.3 1.1 %collective-permute-done.13 = bf16[2,284,70]{1,2,0:T(8,128)(2,1)S(1)} collective-permute-done((bf16[2,284,70]{1,2,0:T(8,128)(2,1)S(1)}, bf16[2,284,70]{1,2,0:T(8,128)(2,1)S(1)}, u32[]{:S(2)}, u32[]{:S(2)}) %collective-permute-start.13) | collective-permute-done | bytes 79552 | tf_op jit(solution)/shard_map/ppermute | solution.py:104
  64.0 2.7 %collective-permute-start.14 = (bf16[2,4,6,70]{3,2,1,0:T(8,128)(2,1)S(1)}, bf16[2,4,6,70]{3,2,1,0:T(8,128)(2,1)S(1)}, u32[]{:S(2)}, u32[]{:S(2)}) collective-permute-start(bf16[2,4,6,70]{3,2,1,0:T(8,128)(2,1)S(1)} %constant_dynamic-slice_fusion), channel_id=1, source_target_pairs={{0,8},{1,9},{2,10},{3,11},{4,12},{5,13},{6,14},{7,15},{8,0},{9,1},... | collective-permute-start | bytes 20168 | tf_op jit(solution)/shard_map/ppermute | solution.py:122
  67.2 1.5 %collective-permute-done.14 = bf16[2,4,6,70]{3,2,1,0:T(8,128)(2,1)S(1)} collective-permute-done((bf16[2,4,6,70]{3,2,1,0:T(8,128)(2,1)S(1)}, bf16[2,4,6,70]{3,2,1,0:T(8,128)(2,1)S(1)}, u32[]{:S(2)}, u32[]{:S(2)}) %collective-permute-start.14) | collective-permute-done | bytes 6752 | tf_op jit(solution)/shard_map/ppermute | solution.py:122
  69.5 0.6 collective-permute-start.15
  70.3 2.9 %collective-permute-done.15 = bf16[4,2,284]{2,0,1:T(4,128)(2,1)S(1)} collective-permute-done((bf16[4,2,284]{2,0,1:T(4,128)(2,1)S(1)}, bf16[4,2,284]{2,0,1:T(4,128)(2,1)S(1)}, u32[]{:S(2)}, u32[]{:S(2)}) %collective-permute-start.15) | collective-permute-done | bytes 4576 | tf_op jit(solution)/shard_map/ppermute | solution.py:22
  74.6 1.3 %collective-permute-done.16 = f32[2,2,2,4,2,284]{5,4,3,2,1,0:T(2,128)S(1)} collective-permute-done((f32[2,2,2,4,2,284]{5,4,3,2,1,0:T(2,128)S(1)}, f32[2,2,2,4,2,284]{5,4,3,2,1,0:T(2,128)S(1)}, u32[]{:S(2)}, u32[]{:S(2)}) %collective-permute-start.16) | collective-permute-done | bytes 72736 | tf_op jit(solution)/shard_map/ppermute | solution.py:57
  75.9 1.6 %collective-permute-start.17 = (f32[2,2,4,2,284]{4,3,2,1,0:T(2,128)S(1)}, f32[2,2,4,2,284]{4,3,2,1,0:T(2,128)S(1)}, u32[]{:S(2)}, u32[]{:S(2)}) collective-permute-start(f32[2,2,4,2,284]{4,3,2,1,0:T(2,128)S(1)} %fusion.38), channel_id=1, source_target_pairs={{0,2},{1,3},{2,0},{3,1},{4,6},{5,7},{6,4},{7,5},{8,10},{9,11},{10,... | collective-permute-start | bytes 109064 | tf_op jit(solution)/shard_map/ppermute | solution.py:57
  77.5 2.6 %collective-permute-done.17 = f32[2,2,4,2,284]{4,3,2,1,0:T(2,128)S(1)} collective-permute-done((f32[2,2,4,2,284]{4,3,2,1,0:T(2,128)S(1)}, f32[2,2,4,2,284]{4,3,2,1,0:T(2,128)S(1)}, u32[]{:S(2)}, u32[]{:S(2)}) %collective-permute-start.17) | collective-permute-done | bytes 36384 | tf_op jit(solution)/shard_map/ppermute | solution.py:57
  80.1 1.6 %collective-permute-start.18 = (f32[2,4,2,284]{3,2,1,0:T(2,128)S(1)}, f32[2,4,2,284]{3,2,1,0:T(2,128)S(1)}, u32[]{:S(2)}, u32[]{:S(2)}) collective-permute-start(f32[2,4,2,284]{3,2,1,0:T(2,128)S(1)} %fusion.43), channel_id=1, source_target_pairs={{0,4},{1,5},{2,6},{3,7},{4,0},{5,1},{6,2},{7,3},{8,12},{9,13},{10,... | collective-permute-start | bytes 54536 | tf_op jit(solution)/shard_map/ppermute | solution.py:57
  81.8 2.3 %collective-permute-done.18 = f32[2,4,2,284]{3,2,1,0:T(2,128)S(1)} collective-permute-done((f32[2,4,2,284]{3,2,1,0:T(2,128)S(1)}, f32[2,4,2,284]{3,2,1,0:T(2,128)S(1)}, u32[]{:S(2)}, u32[]{:S(2)}) %collective-permute-start.18) | collective-permute-done | bytes 18208 | tf_op jit(solution)/shard_map/ppermute | solution.py:57
  84.1 4.6 %collective-permute-start.19 = (f32[4,2,284]{2,1,0:T(2,128)S(1)}, f32[4,2,284]{2,1,0:T(2,128)S(1)}, u32[]{:S(2)}, u32[]{:S(2)}) collective-permute-start(f32[4,2,284]{2,1,0:T(2,128)S(1)} %get-tuple-element.72), channel_id=1, source_target_pairs={{0,0},{1,1},{2,2},{3,3},{4,4},{5,5},{6,6},{7,7},{8,16},{9,17},{10,... | collective-permute-start | bytes 27272 | tf_op jit(solution)/shard_map/ppermute | solution.py:295
  88.7 0.8 copy.250
  89.6 1.9 %collective-permute-done.19 = f32[4,2,284]{2,1,0:T(2,128)S(1)} collective-permute-done((f32[4,2,284]{2,1,0:T(2,128)S(1)}, f32[4,2,284]{2,1,0:T(2,128)S(1)}, u32[]{:S(2)}, u32[]{:S(2)}) %collective-permute-start.19) | collective-permute-done | bytes 9120 | tf_op jit(solution)/shard_map/ppermute | solution.py:295
  91.5 0.9 collective-permute-done.20
  92.4 0.6 add_convert_fusion
  (175 shorter events, 15.7 us)
Async XLA Ops:
  0.6 73.2 %copy-start = (bf16[284,2272]{1,0:T(8,128)(2,1)S(1)}, bf16[284,2272]{1,0:T(8,128)(2,1)}, u32[]{:S(2)}) copy-start(bf16[284,2272]{1,0:T(8,128)(2,1)} %param.19) | copy-start | bytes 3871492
  0.6 3.9 %collective-permute-start = (bf16[4,2,284]{2,1,0:T(2,128)(2,1)}, bf16[4,2,284]{2,1,0:T(2,128)(2,1)S(1)}, u32[]{:S(2)}, u32[]{:S(2)}) collective-permute-start(bf16[4,2,284]{2,1,0:T(2,128)(2,1)} %param.11), channel_id=1, source_target_pairs={{0,16},{16,0},{1,17},{17,1},{2,18},{18,2},{3,19},{19,3},{4,20},{20... | collective-permute-start | bytes 13640 | tf_op jit(solution)/shard_map/ppermute | solution.py:22
  5.3 4.7 %collective-permute-start.1 = (bf16[2,4,2,284]{3,2,1,0:T(2,128)(2,1)S(1)}, bf16[2,4,2,284]{3,2,1,0:T(2,128)(2,1)S(1)}, u32[]{:S(2)}, u32[]{:S(2)}) collective-permute-start(bf16[2,4,2,284]{3,2,1,0:T(2,128)(2,1)S(1)} %pad_maximum_fusion.8), channel_id=1, source_target_pairs={{0,8},{1,9},{2,10},{3,11},{4,12},{5,13},{6,14},{7,15},{8,0},{9,1},... | collective-permute-start | bytes 27272 | tf_op jit(solution)/shard_map/ppermute | solution.py:22
  10.0 3.9 %collective-permute-start.2 = (bf16[2,2,4,2,284]{4,3,2,1,0:T(2,128)(2,1)S(1)}, bf16[2,2,4,2,284]{4,3,2,1,0:T(2,128)(2,1)S(1)}, u32[]{:S(2)}, u32[]{:S(2)}) collective-permute-start(bf16[2,2,4,2,284]{4,3,2,1,0:T(2,128)(2,1)S(1)} %pad_maximum_fusion.6), channel_id=1, source_target_pairs={{0,4},{1,5},{2,6},{3,7},{4,0},{5,1},{6,2},{7,3},{8,12},{9,13},{10,... | collective-permute-start | bytes 54536 | tf_op jit(solution)/shard_map/ppermute | solution.py:22
  13.9 4.2 %collective-permute-start.3 = (bf16[2,2,2,4,2,284]{5,4,3,2,1,0:T(2,128)(2,1)S(1)}, bf16[2,2,2,4,2,284]{5,4,3,2,1,0:T(2,128)(2,1)S(1)}, u32[]{:S(2)}, u32[]{:S(2)}) collective-permute-start(bf16[2,2,2,4,2,284]{5,4,3,2,1,0:T(2,128)(2,1)S(1)} %pad_maximum_fusion.3), channel_id=1, source_target_pairs={{0,2},{1,3},{2,0},{3,1},{4,6},{5,7},{6,4},{7,5},{8,10},{9,11},{10,... | collective-permute-start | bytes 109064 | tf_op jit(solution)/shard_map/ppermute | solution.py:22
  18.3 1.4 %collective-permute-start.4 = (bf16[2,2,2,2,4,2,284]{6,5,4,3,2,1,0:T(2,128)(2,1)S(1)}, bf16[2,2,2,2,4,2,284]{6,5,4,3,2,1,0:T(2,128)(2,1)S(1)}, u32[]{:S(2)}, u32[]{:S(2)}) collective-permute-start(bf16[2,2,2,2,4,2,284]{6,5,4,3,2,1,0:T(2,128)(2,1)S(1)} %pad_maximum_fusion.1), channel_id=1, source_target_pairs={{0,1},{1,0},{2,3},{3,2},{4,5},{5,4},{6,7},{7,6},{8,9},{9,8},{10,11... | collective-permute-start | bytes 218120 | tf_op jit(solution)/shard_map/ppermute | solution.py:22
  22.1 2.0 %copy-start.1 = (bf16[2272,128]{1,0:T(8,128)(2,1)S(1)}, bf16[2272,128]{1,0:T(8,128)(2,1)}, u32[]{:S(2)}) copy-start(bf16[2272,128]{1,0:T(8,128)(2,1)} %param.18) | copy-start | bytes 1744900
  24.5 9.8 %copy-start.2 = (bf16[2,512,128]{2,1,0:T(8,128)(2,1)S(1)}, bf16[2,512,128]{2,1,0:T(8,128)(2,1)}, u32[]{:S(2)}) copy-start(bf16[2,512,128]{2,1,0:T(8,128)(2,1)} %param.12) | copy-start | bytes 786436
  24.5 4.8 %collective-permute-start.5 = (f32[16,412]{1,0:T(8,128)S(1)}, f32[16,412]{1,0:T(8,128)S(1)}, u32[]{:S(2)}, u32[]{:S(2)}) collective-permute-start(f32[16,412]{1,0:T(8,128)S(1)} %pad_maximum_fusion.5), channel_id=1, source_target_pairs={{0,16},{16,0},{1,17},{17,1},{2,18},{18,2},{3,19},{19,3},{4,20},{20... | collective-permute-start | bytes 79112 | tf_op jit(solution)/shard_map/ppermute | solution.py:40
  29.8 4.5 %collective-permute-start.7 = (bf16[4,2,284]{2,1,0:T(2,128)(2,1)S(1)}, bf16[4,2,284]{2,1,0:T(2,128)(2,1)S(1)}, u32[]{:S(2)}, u32[]{:S(2)}) collective-permute-start(bf16[4,2,284]{2,1,0:T(2,128)(2,1)S(1)} %slice.430), channel_id=1, source_target_pairs={{0,8},{1,9},{2,10},{3,11},{4,12},{5,13},{6,14},{7,15},{8,0},{9,1},... | collective-permute-start | bytes 13640 | tf_op jit(solution)/shard_map/ppermute | solution.py:22
  32.5 15.3 %collective-permute-start.6 = (f32[16,1136]{1,0:T(8,128)S(1)}, f32[16,1136]{1,0:T(8,128)S(1)}, u32[]{:S(2)}, u32[]{:S(2)}) collective-permute-start(f32[16,1136]{1,0:T(8,128)S(1)} %fusion.126), channel_id=1, source_target_pairs={{0,16},{16,0},{1,17},{17,1},{2,18},{18,2},{3,19},{19,3},{4,20},{20... | collective-permute-start | bytes 218120 | tf_op jit(solution)/shard_map/ppermute | solution.py:40
  34.5 3.8 %collective-permute-start.8 = (bf16[2,4,2,284]{3,2,1,0:T(2,128)(2,1)S(1)}, bf16[2,4,2,284]{3,2,1,0:T(2,128)(2,1)S(1)}, u32[]{:S(2)}, u32[]{:S(2)}) collective-permute-start(bf16[2,4,2,284]{3,2,1,0:T(2,128)(2,1)S(1)} %pad_maximum_fusion.9), channel_id=1, source_target_pairs={{0,4},{1,5},{2,6},{3,7},{4,0},{5,1},{6,2},{7,3},{8,12},{9,13},{10,... | collective-permute-start | bytes 27272 | tf_op jit(solution)/shard_map/ppermute | solution.py:22
  38.3 3.9 %collective-permute-start.9 = (bf16[2,2,4,2,284]{4,3,2,1,0:T(2,128)(2,1)S(1)}, bf16[2,2,4,2,284]{4,3,2,1,0:T(2,128)(2,1)S(1)}, u32[]{:S(2)}, u32[]{:S(2)}) collective-permute-start(bf16[2,2,4,2,284]{4,3,2,1,0:T(2,128)(2,1)S(1)} %pad_maximum_fusion.7), channel_id=1, source_target_pairs={{0,2},{1,3},{2,0},{3,1},{4,6},{5,7},{6,4},{7,5},{8,10},{9,11},{10,... | collective-permute-start | bytes 54536 | tf_op jit(solution)/shard_map/ppermute | solution.py:22
  42.2 1.3 %collective-permute-start.10 = (bf16[2,2,2,4,2,284]{5,4,3,2,1,0:T(2,128)(2,1)S(1)}, bf16[2,2,2,4,2,284]{5,4,3,2,1,0:T(2,128)(2,1)S(1)}, u32[]{:S(2)}, u32[]{:S(2)}) collective-permute-start(bf16[2,2,2,4,2,284]{5,4,3,2,1,0:T(2,128)(2,1)S(1)} %pad_maximum_fusion.4), channel_id=1, source_target_pairs={{0,1},{1,0},{2,3},{3,2},{4,5},{5,4},{6,7},{7,6},{8,9},{9,8},{10,11... | collective-permute-start | bytes 109064 | tf_op jit(solution)/shard_map/ppermute | solution.py:22
  47.5 2.3 %collective-permute-start.11 = (bf16[2,284,70]{1,0,2:T(2,128)(2,1)S(1)}, bf16[2,284,70]{1,0,2:T(2,128)(2,1)S(1)}, u32[]{:S(2)}, u32[]{:S(2)}) collective-permute-start(bf16[2,284,70]{1,0,2:T(2,128)(2,1)S(1)} %fusion.24), channel_id=1, source_target_pairs={{0,1},{1,0},{2,3},{3,2},{4,5},{5,4},{6,7},{7,6},{8,9},{9,8},{10,11... | collective-permute-start | bytes 238568 | tf_op jit(solution)/shard_map/ppermute | solution.py:104
  50.3 5.3 %collective-permute-start.12 = (bf16[2,284,70]{1,0,2:T(2,128)(2,1)S(1)}, bf16[2,284,70]{1,0,2:T(2,128)(2,1)S(1)}, u32[]{:S(2)}, u32[]{:S(2)}) collective-permute-start(bf16[2,284,70]{1,0,2:T(2,128)(2,1)S(1)} %fusion.25), channel_id=1, source_target_pairs={{0,2},{1,3},{2,0},{3,1},{4,6},{5,7},{6,4},{7,5},{8,10},{9,11},{10,... | collective-permute-start | bytes 238568 | tf_op jit(solution)/shard_map/ppermute | solution.py:104
  56.5 4.8 %collective-permute-start.13 = (bf16[2,284,70]{1,2,0:T(8,128)(2,1)S(1)}, bf16[2,284,70]{1,2,0:T(8,128)(2,1)S(1)}, u32[]{:S(2)}, u32[]{:S(2)}) collective-permute-start(bf16[2,284,70]{1,2,0:T(8,128)(2,1)S(1)} %concatenate.81), channel_id=1, source_target_pairs={{0,4},{1,5},{2,6},{3,7},{4,0},{5,1},{6,2},{7,3},{8,12},{9,13},{10,... | collective-permute-start | bytes 238568 | tf_op jit(solution)/shard_map/ppermute | solution.py:104
  64.0 4.7 %collective-permute-start.14 = (bf16[2,4,6,70]{3,2,1,0:T(8,128)(2,1)S(1)}, bf16[2,4,6,70]{3,2,1,0:T(8,128)(2,1)S(1)}, u32[]{:S(2)}, u32[]{:S(2)}) collective-permute-start(bf16[2,4,6,70]{3,2,1,0:T(8,128)(2,1)S(1)} %constant_dynamic-slice_fusion), channel_id=1, source_target_pairs={{0,8},{1,9},{2,10},{3,11},{4,12},{5,13},{6,14},{7,15},{8,0},{9,1},... | collective-permute-start | bytes 20168 | tf_op jit(solution)/shard_map/ppermute | solution.py:122
  69.5 3.6 %collective-permute-start.15 = (bf16[4,2,284]{2,0,1:T(4,128)(2,1)S(1)}, bf16[4,2,284]{2,0,1:T(4,128)(2,1)S(1)}, u32[]{:S(2)}, u32[]{:S(2)}) collective-permute-start(bf16[4,2,284]{2,0,1:T(4,128)(2,1)S(1)} %get-tuple-element.78), channel_id=1, source_target_pairs={{0,16},{16,0},{1,17},{17,1},{2,18},{18,2},{3,19},{19,3},{4,20},{20... | collective-permute-start | bytes 13640 | tf_op jit(solution)/shard_map/ppermute | solution.py:22
  74.3 18.1 %copy-start.3 = (bf16[4,2,284]{2,1,0:T(2,128)(2,1)S(1)}, bf16[4,2,284]{2,1,0:T(2,128)(2,1)}, u32[]{:S(2)}) copy-start(bf16[4,2,284]{2,1,0:T(2,128)(2,1)} %param.11) | copy-start | bytes 13636
  74.5 1.4 %collective-permute-start.16 = (f32[2,2,2,4,2,284]{5,4,3,2,1,0:T(2,128)S(1)}, f32[2,2,2,4,2,284]{5,4,3,2,1,0:T(2,128)S(1)}, u32[]{:S(2)}, u32[]{:S(2)}) collective-permute-start(f32[2,2,2,4,2,284]{5,4,3,2,1,0:T(2,128)S(1)} %fusion.23), channel_id=1, source_target_pairs={{0,1},{1,0},{2,3},{3,2},{4,5},{5,4},{6,7},{7,6},{8,9},{9,8},{10,11... | collective-permute-start | bytes 218120 | tf_op jit(solution)/shard_map/ppermute | solution.py:57
  75.9 4.2 %collective-permute-start.17 = (f32[2,2,4,2,284]{4,3,2,1,0:T(2,128)S(1)}, f32[2,2,4,2,284]{4,3,2,1,0:T(2,128)S(1)}, u32[]{:S(2)}, u32[]{:S(2)}) collective-permute-start(f32[2,2,4,2,284]{4,3,2,1,0:T(2,128)S(1)} %fusion.38), channel_id=1, source_target_pairs={{0,2},{1,3},{2,0},{3,1},{4,6},{5,7},{6,4},{7,5},{8,10},{9,11},{10,... | collective-permute-start | bytes 109064 | tf_op jit(solution)/shard_map/ppermute | solution.py:57
  80.1 3.9 %collective-permute-start.18 = (f32[2,4,2,284]{3,2,1,0:T(2,128)S(1)}, f32[2,4,2,284]{3,2,1,0:T(2,128)S(1)}, u32[]{:S(2)}, u32[]{:S(2)}) collective-permute-start(f32[2,4,2,284]{3,2,1,0:T(2,128)S(1)} %fusion.43), channel_id=1, source_target_pairs={{0,4},{1,5},{2,6},{3,7},{4,0},{5,1},{6,2},{7,3},{8,12},{9,13},{10,... | collective-permute-start | bytes 54536 | tf_op jit(solution)/shard_map/ppermute | solution.py:57
  84.1 7.4 %collective-permute-start.19 = (f32[4,2,284]{2,1,0:T(2,128)S(1)}, f32[4,2,284]{2,1,0:T(2,128)S(1)}, u32[]{:S(2)}, u32[]{:S(2)}) collective-permute-start(f32[4,2,284]{2,1,0:T(2,128)S(1)} %get-tuple-element.72), channel_id=1, source_target_pairs={{0,0},{1,1},{2,2},{3,3},{4,4},{5,5},{6,6},{7,7},{8,16},{9,17},{10,... | collective-permute-start | bytes 27272 | tf_op jit(solution)/shard_map/ppermute | solution.py:295
  88.6 3.7 %collective-permute-start.20 = (f32[4,2,284]{2,1,0:T(2,128)S(1)}, f32[4,2,284]{2,1,0:T(2,128)S(1)}, u32[]{:S(2)}, u32[]{:S(2)}) collective-permute-start(f32[4,2,284]{2,1,0:T(2,128)S(1)} %get-tuple-element.71), channel_id=1, source_target_pairs={{0,16},{1,17},{2,18},{3,19},{4,20},{5,21},{6,22},{7,23},{8,0},{9,1... | collective-permute-start | bytes 27272 | tf_op jit(solution)/shard_map/ppermute | solution.py:295

commit v17 on v13

--- a/solution.py
+++ b/solution.py
@@ -184,8 +184,9 @@
     req_slots = xor_slot(group_index ^ req_ids, req_size)
 
     by_request, _ = gather_xor(states, "req", req_size)
-    every, riders = gather_xor(by_request, "seq", seq_size, {0: (norm_gain, norm_bias)})
-    norm_gain, norm_bias = riders[0]
+    gain_level = min(1, seq_size.bit_length() - 2)
+    every, riders = gather_xor(by_request, "seq", seq_size, {gain_level: (norm_gain, norm_bias)})
+    norm_gain, norm_bias = riders[gain_level]
     every = every.reshape((seq_size * req_size,) + every.shape[2:])
     every = jnp.take(every, seq_slots[:, None] * req_size + req_slots[None, :], axis=0, mode="clip")
     current_all = every.transpose(2, 1, 3, 0, 4).reshape(steps, total, model_width)

time: 93.2 us -> 93.2 us (level)
  no operation moved by 1% of the time
where the time goes in v17:
time: 93.2 us; the launch traced here: 92.2 us
  starting transfers between devices  28.8 us (31%)
  waiting for transfers between devices  28.5 us (31%)
  local copies, waits for them, and re-layouts  12.4 us (13%)
  matrix products  11.8 us (13%)
  other arithmetic  9.12 us (10%)
  between operations  1.53 us (2%)
    ppermute x10, waiting for transfers between devices, gather_xor(): lax.ppermute(stacked, axis, xor_pairs(size, bit))  16 us
    ppermute x10, starting transfers between devices, gather_xor(): lax.ppermute(stacked, axis, xor_pairs(size, bit))  12.6 us
    ppermute x3, waiting for transfers between devices, scatter_sum(): blocks = keep + lax.ppermute(send, axis, xor_pairs(size, bit))  6.08 us
    ppermute x1, starting transfers between devices, shards(): lax.ppermute(own_block, ALL, own_routes)  4.61 us
    ppermute x3, starting transfers between devices, merge_over(): lax.ppermute(pack_merge(peak, total, weighted), axis, xor_pairs(size, bit))  3.44 us
    dot_general x1, matrix products, shards(): part_up = jnp.dot(normed_part, w_up, preferred_element_type=jnp.float32)  3.32 us
    ppermute x3, starting transfers between devices, scatter_sum(): blocks = keep + lax.ppermute(send, axis, xor_pairs(size, bit))  3.3 us
    concatenate x12, local copies, waits for them, and re-layouts, pack_merge(): jnp.concatenate([jnp.stack(split_exact(peak) + split_exact(total), axis=-...  3.19 us
  transfers between devices with their start and end apart: 21, of which 19 were waited for; matrix products, arithmetic and copies ran while one was open for 18% of the time, Pallas kernels for 0%

profile of v17, /device:TPU:2, one launch (start us, length us, event | category | flops | bytes accessed | tf_op | source)
XLA Modules:
  0.0 92.2 jit_solution(6727607688444523744)
XLA Ops:
  0.8 0.8 dynamic_slice.22
  1.7 0.8 select_reduce_fusion.2
  2.6 0.7 select_reduce_fusion.1
  4.5 0.7 pad_maximum_fusion.8
  5.3 2.7 %collective-permute-start.1 = (bf16[2,4,2,284]{3,2,1,0:T(2,128)(2,1)S(1)}, bf16[2,4,2,284]{3,2,1,0:T(2,128)(2,1)S(1)}, u32[]{:S(2)}, u32[]{:S(2)}) collective-permute-start(bf16[2,4,2,284]{3,2,1,0:T(2,128)(2,1)S(1)} %pad_maximum_fusion.8), channel_id=1, source_target_pairs={{0,8},{1,9},{2,10},{3,11},{4,12},{5,13},{6,14},{7,15},{8,0},{9,1},... | collective-permute-start | bytes 27272 | tf_op jit(solution)/shard_map/ppermute | solution.py:22
  7.9 0.7 fusion.135
  8.6 1.3 %collective-permute-done.1 = bf16[2,4,2,284]{3,2,1,0:T(2,128)(2,1)S(1)} collective-permute-done((bf16[2,4,2,284]{3,2,1,0:T(2,128)(2,1)S(1)}, bf16[2,4,2,284]{3,2,1,0:T(2,128)(2,1)S(1)}, u32[]{:S(2)}, u32[]{:S(2)}) %collective-permute-start.1) | collective-permute-done | bytes 9120 | tf_op jit(solution)/shard_map/ppermute | solution.py:22
  10.0 1.6 %collective-permute-start.2 = (bf16[2,2,4,2,284]{4,3,2,1,0:T(2,128)(2,1)S(1)}, bf16[2,2,4,2,284]{4,3,2,1,0:T(2,128)(2,1)S(1)}, u32[]{:S(2)}, u32[]{:S(2)}) collective-permute-start(bf16[2,2,4,2,284]{4,3,2,1,0:T(2,128)(2,1)S(1)} %pad_maximum_fusion.6), channel_id=1, source_target_pairs={{0,4},{1,5},{2,6},{3,7},{4,0},{5,1},{6,2},{7,3},{8,12},{9,13},{10,... | collective-permute-start | bytes 54536 | tf_op jit(solution)/shard_map/ppermute | solution.py:22
  11.7 2.2 %collective-permute-done.2 = bf16[2,2,4,2,284]{4,3,2,1,0:T(2,128)(2,1)S(1)} collective-permute-done((bf16[2,2,4,2,284]{4,3,2,1,0:T(2,128)(2,1)S(1)}, bf16[2,2,4,2,284]{4,3,2,1,0:T(2,128)(2,1)S(1)}, u32[]{:S(2)}, u32[]{:S(2)}) %collective-permute-start.2) | collective-permute-done | bytes 18208 | tf_op jit(solution)/shard_map/ppermute | solution.py:22
  13.9 1.6 %collective-permute-start.3 = (bf16[2,2,2,4,2,284]{5,4,3,2,1,0:T(2,128)(2,1)S(1)}, bf16[2,2,2,4,2,284]{5,4,3,2,1,0:T(2,128)(2,1)S(1)}, u32[]{:S(2)}, u32[]{:S(2)}) collective-permute-start(bf16[2,2,2,4,2,284]{5,4,3,2,1,0:T(2,128)(2,1)S(1)} %pad_maximum_fusion.3), channel_id=1, source_target_pairs={{0,2},{1,3},{2,0},{3,1},{4,6},{5,7},{6,4},{7,5},{8,10},{9,11},{10,... | collective-permute-start | bytes 109064 | tf_op jit(solution)/shard_map/ppermute | solution.py:22
  15.8 0.8 dynamic-slice
  16.5 0.8 dynamic-slice.1
  17.3 0.8 collective-permute-done.3
  18.5 1.1 %collective-permute-done.4 = bf16[2,2,2,2,4,2,284]{6,5,4,3,2,1,0:T(2,128)(2,1)S(1)} collective-permute-done((bf16[2,2,2,2,4,2,284]{6,5,4,3,2,1,0:T(2,128)(2,1)S(1)}, bf16[2,2,2,2,4,2,284]{6,5,4,3,2,1,0:T(2,128)(2,1)S(1)}, u32[]{:S(2)}, u32[]{:S(2)}) %collective-permute-start.4) | collective-permute-done | bytes 72736 | tf_op jit(solution)/shard_map/ppermute | solution.py:22
  19.9 1.0 %gather_fusion = bf16[32,4,2,284]{3,2,1,0:T(2,128)(2,1)S(1)} fusion(bf16[32,4,2,284]{3,2,1,0:T(2,128)(2,1)S(1)} %bitcast.285, s32[1024]{0:T(1024)S(1)} %get-tuple-element.110), kind=kCustom, calls=%fused_computation | custom fusion | bytes 290944 | tf_op jit(solution)/shard_map/jit(_take)/gather | solution.py:191
  22.4 1.8 %fusion.121 = f32[16,284]{1,0:T(8,128)S(1)} fusion(bf16[2272,284]{0,1:T(8,128)(2,1)} %param.17, f32[16,4544]{1,0:T(8,128)S(1)} %reshape.879, s32[]{:T(128)S(6)} %select_n.335, f32[2272]{0:T(1024)S(1)} %dynamic-slice.1, f32[2272]{0:T(1024)S(1)} %dynamic-slice, f32[16]{0:T(128)S(1)} %rsqrt.12, f32[16]{0:T(128)S(1)} %div.135), kind=kOutput, calls=%fused_computation.340 | convolution fusion | flops 20829696 | bytes 1481732 | tf_op jit(solution)/shard_map/dot_general | solution.py:196
  24.5 1.4 %collective-permute-start.5 = (f32[16,412]{1,0:T(8,128)S(1)}, f32[16,412]{1,0:T(8,128)S(1)}, u32[]{:S(2)}, u32[]{:S(2)}) collective-permute-start(f32[16,412]{1,0:T(8,128)S(1)} %pad_maximum_fusion.5), channel_id=1, source_target_pairs={{0,16},{16,0},{1,17},{17,1},{2,18},{18,2},{3,19},{19,3},{4,20},{20... | collective-permute-start | bytes 79112 | tf_op jit(solution)/shard_map/ppermute | solution.py:40
  25.9 3.3 %fusion.123 = f32[16,1136]{1,0:T(8,128)S(1)} fusion(bf16[2272,1136]{1,0:T(8,128)(2,1)} %param.20, f32[16,4544]{1,0:T(8,128)S(1)} %reshape.879, s32[]{:T(128)S(6)} %select_n.335, f32[2272]{0:T(1024)S(1)} %dynamic-slice.1, f32[2272]{0:T(1024)S(1)} %dynamic-slice, f32[16]{0:T(128)S(1)} %rsqrt.12, f32[16]{0:T(128)S(1)} %div.135), kind=kOutput, calls=%fused_computation.341 | convolution fusion | flops 82773504 | bytes 5407748 | tf_op jit(solution)/shard_map/dot_general | solution.py:199
  29.7 2.6 %collective-permute-start.7 = (bf16[4,2,284]{2,1,0:T(2,128)(2,1)S(1)}, bf16[4,2,284]{2,1,0:T(2,128)(2,1)S(1)}, u32[]{:S(2)}, u32[]{:S(2)}) collective-permute-start(bf16[4,2,284]{2,1,0:T(2,128)(2,1)S(1)} %slice.427), channel_id=1, source_target_pairs={{0,8},{1,9},{2,10},{3,11},{4,12},{5,13},{6,14},{7,15},{8,0},{9,1},... | collective-permute-start | bytes 13640 | tf_op jit(solution)/shard_map/ppermute | solution.py:22
  32.5 1.8 %collective-permute-done.7 = bf16[4,2,284]{2,1,0:T(2,128)(2,1)S(1)} collective-permute-done((bf16[4,2,284]{2,1,0:T(2,128)(2,1)S(1)}, bf16[4,2,284]{2,1,0:T(2,128)(2,1)S(1)}, u32[]{:S(2)}, u32[]{:S(2)}) %collective-permute-start.7) | collective-permute-done | bytes 4576 | tf_op jit(solution)/shard_map/ppermute | solution.py:22
  34.5 1.6 %collective-permute-start.8 = (bf16[2,4,2,284]{3,2,1,0:T(2,128)(2,1)S(1)}, bf16[2,4,2,284]{3,2,1,0:T(2,128)(2,1)S(1)}, u32[]{:S(2)}, u32[]{:S(2)}) collective-permute-start(bf16[2,4,2,284]{3,2,1,0:T(2,128)(2,1)S(1)} %pad_maximum_fusion.9), channel_id=1, source_target_pairs={{0,4},{1,5},{2,6},{3,7},{4,0},{5,1},{6,2},{7,3},{8,12},{9,13},{10,... | collective-permute-start | bytes 27272 | tf_op jit(solution)/shard_map/ppermute | solution.py:22
  36.3 1.9 %collective-permute-done.8 = bf16[2,4,2,284]{3,2,1,0:T(2,128)(2,1)S(1)} collective-permute-done((bf16[2,4,2,284]{3,2,1,0:T(2,128)(2,1)S(1)}, bf16[2,4,2,284]{3,2,1,0:T(2,128)(2,1)S(1)}, u32[]{:S(2)}, u32[]{:S(2)}) %collective-permute-start.8) | collective-permute-done | bytes 9120 | tf_op jit(solution)/shard_map/ppermute | solution.py:22
  38.3 1.6 %collective-permute-start.9 = (bf16[2,2,4,2,284]{4,3,2,1,0:T(2,128)(2,1)S(1)}, bf16[2,2,4,2,284]{4,3,2,1,0:T(2,128)(2,1)S(1)}, u32[]{:S(2)}, u32[]{:S(2)}) collective-permute-start(bf16[2,2,4,2,284]{4,3,2,1,0:T(2,128)(2,1)S(1)} %pad_maximum_fusion.7), channel_id=1, source_target_pairs={{0,2},{1,3},{2,0},{3,1},{4,6},{5,7},{6,4},{7,5},{8,10},{9,11},{10,... | collective-permute-start | bytes 54536 | tf_op jit(solution)/shard_map/ppermute | solution.py:22
  39.9 2.3 %collective-permute-done.9 = bf16[2,2,4,2,284]{4,3,2,1,0:T(2,128)(2,1)S(1)} collective-permute-done((bf16[2,2,4,2,284]{4,3,2,1,0:T(2,128)(2,1)S(1)}, bf16[2,2,4,2,284]{4,3,2,1,0:T(2,128)(2,1)S(1)}, u32[]{:S(2)}, u32[]{:S(2)}) %collective-permute-start.9) | collective-permute-done | bytes 18208 | tf_op jit(solution)/shard_map/ppermute | solution.py:22
  42.4 1.1 %collective-permute-done.10 = bf16[2,2,2,4,2,284]{5,4,3,2,1,0:T(2,128)(2,1)S(1)} collective-permute-done((bf16[2,2,2,4,2,284]{5,4,3,2,1,0:T(2,128)(2,1)S(1)}, bf16[2,2,2,4,2,284]{5,4,3,2,1,0:T(2,128)(2,1)S(1)}, u32[]{:S(2)}, u32[]{:S(2)}) %collective-permute-start.10) | collective-permute-done | bytes 36384 | tf_op jit(solution)/shard_map/ppermute | solution.py:22
  43.7 0.6 gather_fusion.1
  47.8 0.7 collective-permute-start.6
  49.3 1.6 %collective-permute-start.12 = (bf16[2,284,70]{1,0,2:T(2,128)(2,1)S(1)}, bf16[2,284,70]{1,0,2:T(2,128)(2,1)S(1)}, u32[]{:S(2)}, u32[]{:S(2)}) collective-permute-start(bf16[2,284,70]{1,0,2:T(2,128)(2,1)S(1)} %fusion.23), channel_id=1, source_target_pairs={{0,2},{1,3},{2,0},{3,1},{4,6},{5,7},{6,4},{7,5},{8,10},{9,11},{10,... | collective-permute-start | bytes 238568 | tf_op jit(solution)/shard_map/ppermute | solution.py:104
  50.9 1.5 %collective-permute-done.6 = f32[16,1136]{1,0:T(8,128)S(1)} collective-permute-done((f32[16,1136]{1,0:T(8,128)S(1)}, f32[16,1136]{1,0:T(8,128)S(1)}, u32[]{:S(2)}, u32[]{:S(2)}) %collective-permute-start.6) | collective-permute-done | bytes 72736 | tf_op jit(solution)/shard_map/ppermute | solution.py:40
  52.4 2.3 %fusion = f32[16,1136]{1,0:T(8,128)S(1)} fusion(bf16[1136,2272]{1,0:T(8,128)(2,1)} %param.21, f32[16,1136]{1,0:T(8,128)S(1)} %fusion.123, f32[16,1136]{1,0:T(8,128)S(1)} %collective-permute-done.6), kind=kOutput, calls=%fused_computation.4 | convolution fusion | flops 42495488 | bytes 2835456 | tf_op jit(solution)/shard_map/dot_general | solution.py:216
  55.0 0.6 concatenate.81
  55.6 1.6 %collective-permute-start.13 = (bf16[2,284,70]{1,2,0:T(8,128)(2,1)S(1)}, bf16[2,284,70]{1,2,0:T(8,128)(2,1)S(1)}, u32[]{:S(2)}, u32[]{:S(2)}) collective-permute-start(bf16[2,284,70]{1,2,0:T(8,128)(2,1)S(1)} %concatenate.81), channel_id=1, source_target_pairs={{0,4},{1,5},{2,6},{3,7},{4,0},{5,1},{6,2},{7,3},{8,12},{9,13},{10,... | collective-permute-start | bytes 238568 | tf_op jit(solution)/shard_map/ppermute | solution.py:104
  57.3 2.9 %fusion.2 = f32[16,1136]{1,0:T(8,128)S(1)} fusion(bf16[1136,2272]{1,0:T(8,128)(2,1)} %param.21, f32[16,1136]{1,0:T(8,128)S(1)} %fusion.123, f32[16,1136]{1,0:T(8,128)S(1)} %collective-permute-done.6), kind=kOutput, calls=%fused_computation.6 | convolution fusion | flops 42495488 | bytes 2835456 | tf_op jit(solution)/shard_map/dot_general | solution.py:217
  63.1 2.7 %collective-permute-start.14 = (bf16[2,4,6,70]{3,2,1,0:T(8,128)(2,1)S(1)}, bf16[2,4,6,70]{3,2,1,0:T(8,128)(2,1)S(1)}, u32[]{:S(2)}, u32[]{:S(2)}) collective-permute-start(bf16[2,4,6,70]{3,2,1,0:T(8,128)(2,1)S(1)} %constant_dynamic-slice_fusion), channel_id=1, source_target_pairs={{0,8},{1,9},{2,10},{3,11},{4,12},{5,13},{6,14},{7,15},{8,0},{9,1},... | collective-permute-start | bytes 20168 | tf_op jit(solution)/shard_map/ppermute | solution.py:122
  66.3 1.5 %collective-permute-done.14 = bf16[2,4,6,70]{3,2,1,0:T(8,128)(2,1)S(1)} collective-permute-done((bf16[2,4,6,70]{3,2,1,0:T(8,128)(2,1)S(1)}, bf16[2,4,6,70]{3,2,1,0:T(8,128)(2,1)S(1)}, u32[]{:S(2)}, u32[]{:S(2)}) %collective-permute-start.14) | collective-permute-done | bytes 6752 | tf_op jit(solution)/shard_map/ppermute | solution.py:122
  68.6 0.7 collective-permute-start.15
  69.3 3.0 %collective-permute-done.15 = bf16[4,2,284]{2,0,1:T(4,128)(2,1)S(1)} collective-permute-done((bf16[4,2,284]{2,0,1:T(4,128)(2,1)S(1)}, bf16[4,2,284]{2,0,1:T(4,128)(2,1)S(1)}, u32[]{:S(2)}, u32[]{:S(2)}) %collective-permute-start.15) | collective-permute-done | bytes 4576 | tf_op jit(solution)/shard_map/ppermute | solution.py:22
  72.3 0.6 gather_fusion.2
  73.7 1.3 %collective-permute-done.16 = f32[2,2,2,4,2,284]{5,4,3,2,1,0:T(2,128)S(1)} collective-permute-done((f32[2,2,2,4,2,284]{5,4,3,2,1,0:T(2,128)S(1)}, f32[2,2,2,4,2,284]{5,4,3,2,1,0:T(2,128)S(1)}, u32[]{:S(2)}, u32[]{:S(2)}) %collective-permute-start.16) | collective-permute-done | bytes 72736 | tf_op jit(solution)/shard_map/ppermute | solution.py:57
  75.0 1.6 %collective-permute-start.17 = (f32[2,2,4,2,284]{4,3,2,1,0:T(2,128)S(1)}, f32[2,2,4,2,284]{4,3,2,1,0:T(2,128)S(1)}, u32[]{:S(2)}, u32[]{:S(2)}) collective-permute-start(f32[2,2,4,2,284]{4,3,2,1,0:T(2,128)S(1)} %fusion.36), channel_id=1, source_target_pairs={{0,2},{1,3},{2,0},{3,1},{4,6},{5,7},{6,4},{7,5},{8,10},{9,11},{10,... | collective-permute-start | bytes 109064 | tf_op jit(solution)/shard_map/ppermute | solution.py:57
  76.6 2.6 %collective-permute-done.17 = f32[2,2,4,2,284]{4,3,2,1,0:T(2,128)S(1)} collective-permute-done((f32[2,2,4,2,284]{4,3,2,1,0:T(2,128)S(1)}, f32[2,2,4,2,284]{4,3,2,1,0:T(2,128)S(1)}, u32[]{:S(2)}, u32[]{:S(2)}) %collective-permute-start.17) | collective-permute-done | bytes 36384 | tf_op jit(solution)/shard_map/ppermute | solution.py:57
  79.2 1.6 %collective-permute-start.18 = (f32[2,4,2,284]{3,2,1,0:T(2,128)S(1)}, f32[2,4,2,284]{3,2,1,0:T(2,128)S(1)}, u32[]{:S(2)}, u32[]{:S(2)}) collective-permute-start(f32[2,4,2,284]{3,2,1,0:T(2,128)S(1)} %fusion.41), channel_id=1, source_target_pairs={{0,4},{1,5},{2,6},{3,7},{4,0},{5,1},{6,2},{7,3},{8,12},{9,13},{10,... | collective-permute-start | bytes 54536 | tf_op jit(solution)/shard_map/ppermute | solution.py:57
  80.9 2.2 %collective-permute-done.18 = f32[2,4,2,284]{3,2,1,0:T(2,128)S(1)} collective-permute-done((f32[2,4,2,284]{3,2,1,0:T(2,128)S(1)}, f32[2,4,2,284]{3,2,1,0:T(2,128)S(1)}, u32[]{:S(2)}, u32[]{:S(2)}) %collective-permute-start.18) | collective-permute-done | bytes 18208 | tf_op jit(solution)/shard_map/ppermute | solution.py:57
  83.2 4.6 %collective-permute-start.19 = (f32[4,2,284]{2,1,0:T(2,128)S(1)}, f32[4,2,284]{2,1,0:T(2,128)S(1)}, u32[]{:S(2)}, u32[]{:S(2)}) collective-permute-start(f32[4,2,284]{2,1,0:T(2,128)S(1)} %get-tuple-element.68), channel_id=1, source_target_pairs={{0,0},{1,1},{2,2},{3,3},{4,4},{5,5},{6,6},{7,7},{8,16},{9,17},{10,... | collective-permute-start | bytes 27272 | tf_op jit(solution)/shard_map/ppermute | solution.py:295
  87.9 0.8 copy.250
  88.7 1.9 %collective-permute-done.19 = f32[4,2,284]{2,1,0:T(2,128)S(1)} collective-permute-done((f32[4,2,284]{2,1,0:T(2,128)S(1)}, f32[4,2,284]{2,1,0:T(2,128)S(1)}, u32[]{:S(2)}, u32[]{:S(2)}) %collective-permute-start.19) | collective-permute-done | bytes 9120 | tf_op jit(solution)/shard_map/ppermute | solution.py:295
  90.6 1.0 %collective-permute-done.20 = f32[4,2,284]{2,1,0:T(2,128)S(1)} collective-permute-done((f32[4,2,284]{2,1,0:T(2,128)S(1)}, f32[4,2,284]{2,1,0:T(2,128)S(1)}, u32[]{:S(2)}, u32[]{:S(2)}) %collective-permute-start.20) | collective-permute-done | bytes 9120 | tf_op jit(solution)/shard_map/ppermute | solution.py:295
  91.5 0.6 add_convert_fusion
  (172 shorter events, 15.1 us)
Async XLA Ops:
  0.6 72.3 %copy-start = (bf16[284,2272]{1,0:T(8,128)(2,1)S(1)}, bf16[284,2272]{1,0:T(8,128)(2,1)}, u32[]{:S(2)}) copy-start(bf16[284,2272]{1,0:T(8,128)(2,1)} %param.19) | copy-start | bytes 3871492
  0.6 3.9 %collective-permute-start = (bf16[4,2,284]{2,1,0:T(2,128)(2,1)}, bf16[4,2,284]{2,1,0:T(2,128)(2,1)S(1)}, u32[]{:S(2)}, u32[]{:S(2)}) collective-permute-start(bf16[4,2,284]{2,1,0:T(2,128)(2,1)} %param.11), channel_id=1, source_target_pairs={{0,16},{16,0},{1,17},{17,1},{2,18},{18,2},{3,19},{19,3},{4,20},{20... | collective-permute-start | bytes 13640 | tf_op jit(solution)/shard_map/ppermute | solution.py:22
  5.3 4.7 %collective-permute-start.1 = (bf16[2,4,2,284]{3,2,1,0:T(2,128)(2,1)S(1)}, bf16[2,4,2,284]{3,2,1,0:T(2,128)(2,1)S(1)}, u32[]{:S(2)}, u32[]{:S(2)}) collective-permute-start(bf16[2,4,2,284]{3,2,1,0:T(2,128)(2,1)S(1)} %pad_maximum_fusion.8), channel_id=1, source_target_pairs={{0,8},{1,9},{2,10},{3,11},{4,12},{5,13},{6,14},{7,15},{8,0},{9,1},... | collective-permute-start | bytes 27272 | tf_op jit(solution)/shard_map/ppermute | solution.py:22
  10.0 3.9 %collective-permute-start.2 = (bf16[2,2,4,2,284]{4,3,2,1,0:T(2,128)(2,1)S(1)}, bf16[2,2,4,2,284]{4,3,2,1,0:T(2,128)(2,1)S(1)}, u32[]{:S(2)}, u32[]{:S(2)}) collective-permute-start(bf16[2,2,4,2,284]{4,3,2,1,0:T(2,128)(2,1)S(1)} %pad_maximum_fusion.6), channel_id=1, source_target_pairs={{0,4},{1,5},{2,6},{3,7},{4,0},{5,1},{6,2},{7,3},{8,12},{9,13},{10,... | collective-permute-start | bytes 54536 | tf_op jit(solution)/shard_map/ppermute | solution.py:22
  13.9 4.2 %collective-permute-start.3 = (bf16[2,2,2,4,2,284]{5,4,3,2,1,0:T(2,128)(2,1)S(1)}, bf16[2,2,2,4,2,284]{5,4,3,2,1,0:T(2,128)(2,1)S(1)}, u32[]{:S(2)}, u32[]{:S(2)}) collective-permute-start(bf16[2,2,2,4,2,284]{5,4,3,2,1,0:T(2,128)(2,1)S(1)} %pad_maximum_fusion.3), channel_id=1, source_target_pairs={{0,2},{1,3},{2,0},{3,1},{4,6},{5,7},{6,4},{7,5},{8,10},{9,11},{10,... | collective-permute-start | bytes 109064 | tf_op jit(solution)/shard_map/ppermute | solution.py:22
  18.3 1.4 %collective-permute-start.4 = (bf16[2,2,2,2,4,2,284]{6,5,4,3,2,1,0:T(2,128)(2,1)S(1)}, bf16[2,2,2,2,4,2,284]{6,5,4,3,2,1,0:T(2,128)(2,1)S(1)}, u32[]{:S(2)}, u32[]{:S(2)}) collective-permute-start(bf16[2,2,2,2,4,2,284]{6,5,4,3,2,1,0:T(2,128)(2,1)S(1)} %pad_maximum_fusion.1), channel_id=1, source_target_pairs={{0,1},{1,0},{2,3},{3,2},{4,5},{5,4},{6,7},{7,6},{8,9},{9,8},{10,11... | collective-permute-start | bytes 218120 | tf_op jit(solution)/shard_map/ppermute | solution.py:22
  22.1 2.0 %copy-start.1 = (bf16[2272,128]{1,0:T(8,128)(2,1)S(1)}, bf16[2272,128]{1,0:T(8,128)(2,1)}, u32[]{:S(2)}) copy-start(bf16[2272,128]{1,0:T(8,128)(2,1)} %param.18) | copy-start | bytes 1744900
  24.5 9.8 %copy-start.2 = (bf16[2,512,128]{2,1,0:T(8,128)(2,1)S(1)}, bf16[2,512,128]{2,1,0:T(8,128)(2,1)}, u32[]{:S(2)}) copy-start(bf16[2,512,128]{2,1,0:T(8,128)(2,1)} %param.12) | copy-start | bytes 786436
  24.5 4.7 %collective-permute-start.5 = (f32[16,412]{1,0:T(8,128)S(1)}, f32[16,412]{1,0:T(8,128)S(1)}, u32[]{:S(2)}, u32[]{:S(2)}) collective-permute-start(f32[16,412]{1,0:T(8,128)S(1)} %pad_maximum_fusion.5), channel_id=1, source_target_pairs={{0,16},{16,0},{1,17},{17,1},{2,18},{18,2},{3,19},{19,3},{4,20},{20... | collective-permute-start | bytes 79112 | tf_op jit(solution)/shard_map/ppermute | solution.py:40
  29.7 4.5 %collective-permute-start.7 = (bf16[4,2,284]{2,1,0:T(2,128)(2,1)S(1)}, bf16[4,2,284]{2,1,0:T(2,128)(2,1)S(1)}, u32[]{:S(2)}, u32[]{:S(2)}) collective-permute-start(bf16[4,2,284]{2,1,0:T(2,128)(2,1)S(1)} %slice.427), channel_id=1, source_target_pairs={{0,8},{1,9},{2,10},{3,11},{4,12},{5,13},{6,14},{7,15},{8,0},{9,1},... | collective-permute-start | bytes 13640 | tf_op jit(solution)/shard_map/ppermute | solution.py:22
  34.5 3.8 %collective-permute-start.8 = (bf16[2,4,2,284]{3,2,1,0:T(2,128)(2,1)S(1)}, bf16[2,4,2,284]{3,2,1,0:T(2,128)(2,1)S(1)}, u32[]{:S(2)}, u32[]{:S(2)}) collective-permute-start(bf16[2,4,2,284]{3,2,1,0:T(2,128)(2,1)S(1)} %pad_maximum_fusion.9), channel_id=1, source_target_pairs={{0,4},{1,5},{2,6},{3,7},{4,0},{5,1},{6,2},{7,3},{8,12},{9,13},{10,... | collective-permute-start | bytes 27272 | tf_op jit(solution)/shard_map/ppermute | solution.py:22
  38.3 3.9 %collective-permute-start.9 = (bf16[2,2,4,2,284]{4,3,2,1,0:T(2,128)(2,1)S(1)}, bf16[2,2,4,2,284]{4,3,2,1,0:T(2,128)(2,1)S(1)}, u32[]{:S(2)}, u32[]{:S(2)}) collective-permute-start(bf16[2,2,4,2,284]{4,3,2,1,0:T(2,128)(2,1)S(1)} %pad_maximum_fusion.7), channel_id=1, source_target_pairs={{0,2},{1,3},{2,0},{3,1},{4,6},{5,7},{6,4},{7,5},{8,10},{9,11},{10,... | collective-permute-start | bytes 54536 | tf_op jit(solution)/shard_map/ppermute | solution.py:22
  42.2 1.3 %collective-permute-start.10 = (bf16[2,2,2,4,2,284]{5,4,3,2,1,0:T(2,128)(2,1)S(1)}, bf16[2,2,2,4,2,284]{5,4,3,2,1,0:T(2,128)(2,1)S(1)}, u32[]{:S(2)}, u32[]{:S(2)}) collective-permute-start(bf16[2,2,2,4,2,284]{5,4,3,2,1,0:T(2,128)(2,1)S(1)} %pad_maximum_fusion.4), channel_id=1, source_target_pairs={{0,1},{1,0},{2,3},{3,2},{4,5},{5,4},{6,7},{7,6},{8,9},{9,8},{10,11... | collective-permute-start | bytes 109064 | tf_op jit(solution)/shard_map/ppermute | solution.py:22
  47.5 1.4 %collective-permute-start.11 = (bf16[2,284,70]{1,0,2:T(2,128)(2,1)S(1)}, bf16[2,284,70]{1,0,2:T(2,128)(2,1)S(1)}, u32[]{:S(2)}, u32[]{:S(2)}) collective-permute-start(bf16[2,284,70]{1,0,2:T(2,128)(2,1)S(1)} %fusion.22), channel_id=1, source_target_pairs={{0,1},{1,0},{2,3},{3,2},{4,5},{5,4},{6,7},{7,6},{8,9},{9,8},{10,11... | collective-permute-start | bytes 238568 | tf_op jit(solution)/shard_map/ppermute | solution.py:104
  47.8 4.6 %collective-permute-start.6 = (f32[16,1136]{1,0:T(8,128)S(1)}, f32[16,1136]{1,0:T(8,128)S(1)}, u32[]{:S(2)}, u32[]{:S(2)}) collective-permute-start(f32[16,1136]{1,0:T(8,128)S(1)} %fusion.123), channel_id=1, source_target_pairs={{0,16},{16,0},{1,17},{17,1},{2,18},{18,2},{3,19},{19,3},{4,20},{20... | collective-permute-start | bytes 218120 | tf_op jit(solution)/shard_map/ppermute | solution.py:40
  49.3 5.4 %collective-permute-start.12 = (bf16[2,284,70]{1,0,2:T(2,128)(2,1)S(1)}, bf16[2,284,70]{1,0,2:T(2,128)(2,1)S(1)}, u32[]{:S(2)}, u32[]{:S(2)}) collective-permute-start(bf16[2,284,70]{1,0,2:T(2,128)(2,1)S(1)} %fusion.23), channel_id=1, source_target_pairs={{0,2},{1,3},{2,0},{3,1},{4,6},{5,7},{6,4},{7,5},{8,10},{9,11},{10,... | collective-permute-start | bytes 238568 | tf_op jit(solution)/shard_map/ppermute | solution.py:104
  55.6 4.8 %collective-permute-start.13 = (bf16[2,284,70]{1,2,0:T(8,128)(2,1)S(1)}, bf16[2,284,70]{1,2,0:T(8,128)(2,1)S(1)}, u32[]{:S(2)}, u32[]{:S(2)}) collective-permute-start(bf16[2,284,70]{1,2,0:T(8,128)(2,1)S(1)} %concatenate.81), channel_id=1, source_target_pairs={{0,4},{1,5},{2,6},{3,7},{4,0},{5,1},{6,2},{7,3},{8,12},{9,13},{10,... | collective-permute-start | bytes 238568 | tf_op jit(solution)/shard_map/ppermute | solution.py:104
  63.1 4.7 %collective-permute-start.14 = (bf16[2,4,6,70]{3,2,1,0:T(8,128)(2,1)S(1)}, bf16[2,4,6,70]{3,2,1,0:T(8,128)(2,1)S(1)}, u32[]{:S(2)}, u32[]{:S(2)}) collective-permute-start(bf16[2,4,6,70]{3,2,1,0:T(8,128)(2,1)S(1)} %constant_dynamic-slice_fusion), channel_id=1, source_target_pairs={{0,8},{1,9},{2,10},{3,11},{4,12},{5,13},{6,14},{7,15},{8,0},{9,1},... | collective-permute-start | bytes 20168 | tf_op jit(solution)/shard_map/ppermute | solution.py:122
  68.6 3.6 %collective-permute-start.15 = (bf16[4,2,284]{2,0,1:T(4,128)(2,1)S(1)}, bf16[4,2,284]{2,0,1:T(4,128)(2,1)S(1)}, u32[]{:S(2)}, u32[]{:S(2)}) collective-permute-start(bf16[4,2,284]{2,0,1:T(4,128)(2,1)S(1)} %get-tuple-element.74), channel_id=1, source_target_pairs={{0,16},{16,0},{1,17},{17,1},{2,18},{18,2},{3,19},{19,3},{4,20},{20... | collective-permute-start | bytes 13640 | tf_op jit(solution)/shard_map/ppermute | solution.py:22
  73.4 18.2 %copy-start.3 = (bf16[4,2,284]{2,1,0:T(2,128)(2,1)S(1)}, bf16[4,2,284]{2,1,0:T(2,128)(2,1)}, u32[]{:S(2)}) copy-start(bf16[4,2,284]{2,1,0:T(2,128)(2,1)} %param.11) | copy-start | bytes 13636
  73.5 1.4 %collective-permute-start.16 = (f32[2,2,2,4,2,284]{5,4,3,2,1,0:T(2,128)S(1)}, f32[2,2,2,4,2,284]{5,4,3,2,1,0:T(2,128)S(1)}, u32[]{:S(2)}, u32[]{:S(2)}) collective-permute-start(f32[2,2,2,4,2,284]{5,4,3,2,1,0:T(2,128)S(1)} %fusion.21), channel_id=1, source_target_pairs={{0,1},{1,0},{2,3},{3,2},{4,5},{5,4},{6,7},{7,6},{8,9},{9,8},{10,11... | collective-permute-start | bytes 218120 | tf_op jit(solution)/shard_map/ppermute | solution.py:57
  75.0 4.2 %collective-permute-start.17 = (f32[2,2,4,2,284]{4,3,2,1,0:T(2,128)S(1)}, f32[2,2,4,2,284]{4,3,2,1,0:T(2,128)S(1)}, u32[]{:S(2)}, u32[]{:S(2)}) collective-permute-start(f32[2,2,4,2,284]{4,3,2,1,0:T(2,128)S(1)} %fusion.36), channel_id=1, source_target_pairs={{0,2},{1,3},{2,0},{3,1},{4,6},{5,7},{6,4},{7,5},{8,10},{9,11},{10,... | collective-permute-start | bytes 109064 | tf_op jit(solution)/shard_map/ppermute | solution.py:57
  79.2 3.9 %collective-permute-start.18 = (f32[2,4,2,284]{3,2,1,0:T(2,128)S(1)}, f32[2,4,2,284]{3,2,1,0:T(2,128)S(1)}, u32[]{:S(2)}, u32[]{:S(2)}) collective-permute-start(f32[2,4,2,284]{3,2,1,0:T(2,128)S(1)} %fusion.41), channel_id=1, source_target_pairs={{0,4},{1,5},{2,6},{3,7},{4,0},{5,1},{6,2},{7,3},{8,12},{9,13},{10,... | collective-permute-start | bytes 54536 | tf_op jit(solution)/shard_map/ppermute | solution.py:57
  83.2 7.4 %collective-permute-start.19 = (f32[4,2,284]{2,1,0:T(2,128)S(1)}, f32[4,2,284]{2,1,0:T(2,128)S(1)}, u32[]{:S(2)}, u32[]{:S(2)}) collective-permute-start(f32[4,2,284]{2,1,0:T(2,128)S(1)} %get-tuple-element.68), channel_id=1, source_target_pairs={{0,0},{1,1},{2,2},{3,3},{4,4},{5,5},{6,6},{7,7},{8,16},{9,17},{10,... | collective-permute-start | bytes 27272 | tf_op jit(solution)/shard_map/ppermute | solution.py:295
  87.8 3.7 %collective-permute-start.20 = (f32[4,2,284]{2,1,0:T(2,128)S(1)}, f32[4,2,284]{2,1,0:T(2,128)S(1)}, u32[]{:S(2)}, u32[]{:S(2)}) collective-permute-start(f32[4,2,284]{2,1,0:T(2,128)S(1)} %get-tuple-element.67), channel_id=1, source_target_pairs={{0,16},{1,17},{2,18},{3,19},{4,20},{5,21},{6,22},{7,23},{8,0},{9,1... | collective-permute-start | bytes 27272 | tf_op jit(solution)/shard_map/ppermute | solution.py:295

commit v18 on v17

--- a/solution.py
+++ b/solution.py
@@ -184,7 +184,7 @@
     req_slots = xor_slot(group_index ^ req_ids, req_size)
 
     by_request, _ = gather_xor(states, "req", req_size)
-    gain_level = min(1, seq_size.bit_length() - 2)
+    gain_level = min(2, seq_size.bit_length() - 2)
     every, riders = gather_xor(by_request, "seq", seq_size, {gain_level: (norm_gain, norm_bias)})
     norm_gain, norm_bias = riders[gain_level]
     every = every.reshape((seq_size * req_size,) + every.shape[2:])

time: 93.2 us -> 93.7 us (level)
  transfers between devices with their start and end apart: 21 -> 21, of which waited for: 19 -> 18; matrix products, arithmetic and copies ran while one was open for 18% -> 18% of each run, Pallas kernels for 0% -> 0%
where the time goes in v18:
time: 93.7 us; the launch traced here: 92.6 us
  starting transfers between devices  29.1 us (31%)
  waiting for transfers between devices  28.8 us (31%)
  local copies, waits for them, and re-layouts  12.4 us (13%)
  matrix products  11.8 us (13%)
  other arithmetic  9.04 us (10%)
  between operations  1.54 us (2%)
    ppermute x10, waiting for transfers between devices, gather_xor(): lax.ppermute(stacked, axis, xor_pairs(size, bit))  16.2 us
    ppermute x10, starting transfers between devices, gather_xor(): lax.ppermute(stacked, axis, xor_pairs(size, bit))  12.7 us
    ppermute x3, waiting for transfers between devices, scatter_sum(): blocks = keep + lax.ppermute(send, axis, xor_pairs(size, bit))  6.07 us
    ppermute x1, starting transfers between devices, shards(): lax.ppermute(own_block, ALL, own_routes)  4.61 us
    ppermute x3, starting transfers between devices, merge_over(): lax.ppermute(pack_merge(peak, total, weighted), axis, xor_pairs(size, bit))  3.46 us
    dot_general x1, matrix products, shards(): part_up = jnp.dot(normed_part, w_up, preferred_element_type=jnp.float32)  3.32 us
    ppermute x3, starting transfers between devices, scatter_sum(): blocks = keep + lax.ppermute(send, axis, xor_pairs(size, bit))  3.3 us
    concatenate x12, local copies, waits for them, and re-layouts, pack_merge(): jnp.concatenate([jnp.stack(split_exact(peak) + split_exact(total), axis=-...  3.19 us
  transfers between devices with their start and end apart: 21, of which 18 were waited for; matrix products, arithmetic and copies ran while one was open for 18% of the time, Pallas kernels for 0%

profile of v18, /device:TPU:2, one launch (start us, length us, event | category | flops | bytes accessed | tf_op | source)
XLA Modules:
  0.0 92.6 jit_solution(392418473909698485)
XLA Ops:
  0.8 0.8 dynamic_slice.22
  1.7 0.8 select_reduce_fusion.2
  2.6 0.7 select_reduce_fusion.1
  4.5 0.7 pad_maximum_fusion.8
  5.3 2.7 %collective-permute-start.1 = (bf16[2,4,2,284]{3,2,1,0:T(2,128)(2,1)S(1)}, bf16[2,4,2,284]{3,2,1,0:T(2,128)(2,1)S(1)}, u32[]{:S(2)}, u32[]{:S(2)}) collective-permute-start(bf16[2,4,2,284]{3,2,1,0:T(2,128)(2,1)S(1)} %pad_maximum_fusion.8), channel_id=1, source_target_pairs={{0,8},{1,9},{2,10},{3,11},{4,12},{5,13},{6,14},{7,15},{8,0},{9,1},... | collective-permute-start | bytes 27272 | tf_op jit(solution)/shard_map/ppermute | solution.py:22
  8.0 0.7 fusion.135
  8.7 1.2 %collective-permute-done.1 = bf16[2,4,2,284]{3,2,1,0:T(2,128)(2,1)S(1)} collective-permute-done((bf16[2,4,2,284]{3,2,1,0:T(2,128)(2,1)S(1)}, bf16[2,4,2,284]{3,2,1,0:T(2,128)(2,1)S(1)}, u32[]{:S(2)}, u32[]{:S(2)}) %collective-permute-start.1) | collective-permute-done | bytes 9120 | tf_op jit(solution)/shard_map/ppermute | solution.py:22
  10.0 1.7 %collective-permute-start.2 = (bf16[2,2,4,2,284]{4,3,2,1,0:T(2,128)(2,1)S(1)}, bf16[2,2,4,2,284]{4,3,2,1,0:T(2,128)(2,1)S(1)}, u32[]{:S(2)}, u32[]{:S(2)}) collective-permute-start(bf16[2,2,4,2,284]{4,3,2,1,0:T(2,128)(2,1)S(1)} %pad_maximum_fusion.6), channel_id=1, source_target_pairs={{0,4},{1,5},{2,6},{3,7},{4,0},{5,1},{6,2},{7,3},{8,12},{9,13},{10,... | collective-permute-start | bytes 54536 | tf_op jit(solution)/shard_map/ppermute | solution.py:22
  11.7 2.2 %collective-permute-done.2 = bf16[2,2,4,2,284]{4,3,2,1,0:T(2,128)(2,1)S(1)} collective-permute-done((bf16[2,2,4,2,284]{4,3,2,1,0:T(2,128)(2,1)S(1)}, bf16[2,2,4,2,284]{4,3,2,1,0:T(2,128)(2,1)S(1)}, u32[]{:S(2)}, u32[]{:S(2)}) %collective-permute-start.2) | collective-permute-done | bytes 18208 | tf_op jit(solution)/shard_map/ppermute | solution.py:22
  13.9 1.6 %collective-permute-start.3 = (bf16[2,2,2,4,2,284]{5,4,3,2,1,0:T(2,128)(2,1)S(1)}, bf16[2,2,2,4,2,284]{5,4,3,2,1,0:T(2,128)(2,1)S(1)}, u32[]{:S(2)}, u32[]{:S(2)}) collective-permute-start(bf16[2,2,2,4,2,284]{5,4,3,2,1,0:T(2,128)(2,1)S(1)} %pad_maximum_fusion.3), channel_id=1, source_target_pairs={{0,2},{1,3},{2,0},{3,1},{4,6},{5,7},{6,4},{7,5},{8,10},{9,11},{10,... | collective-permute-start | bytes 109064 | tf_op jit(solution)/shard_map/ppermute | solution.py:22
  15.7 2.4 %collective-permute-done.3 = bf16[2,2,2,4,2,284]{5,4,3,2,1,0:T(2,128)(2,1)S(1)} collective-permute-done((bf16[2,2,2,4,2,284]{5,4,3,2,1,0:T(2,128)(2,1)S(1)}, bf16[2,2,2,4,2,284]{5,4,3,2,1,0:T(2,128)(2,1)S(1)}, u32[]{:S(2)}, u32[]{:S(2)}) %collective-permute-start.3) | collective-permute-done | bytes 36384 | tf_op jit(solution)/shard_map/ppermute | solution.py:22
  18.4 0.8 dynamic-slice
  19.2 0.8 dynamic-slice.1
  20.3 1.0 %gather_fusion = bf16[32,4,2,284]{3,2,1,0:T(2,128)(2,1)S(1)} fusion(bf16[32,4,2,284]{3,2,1,0:T(2,128)(2,1)S(1)} %bitcast.285, s32[1024]{0:T(1024)S(1)} %get-tuple-element.110), kind=kCustom, calls=%fused_computation | custom fusion | bytes 290944 | tf_op jit(solution)/shard_map/jit(_take)/gather | solution.py:191
  22.7 1.8 %fusion.121 = f32[16,284]{1,0:T(8,128)S(1)} fusion(bf16[2272,284]{0,1:T(8,128)(2,1)} %param.17, f32[16,4544]{1,0:T(8,128)S(1)} %reshape.879, s32[]{:T(128)S(6)} %select_n.335, f32[2272]{0:T(1024)S(1)} %dynamic-slice.1, f32[2272]{0:T(1024)S(1)} %dynamic-slice, f32[16]{0:T(128)S(1)} %rsqrt.12, f32[16]{0:T(128)S(1)} %div.135), kind=kOutput, calls=%fused_computation.340 | convolution fusion | flops 20829696 | bytes 1481732 | tf_op jit(solution)/shard_map/dot_general | solution.py:196
  24.8 1.6 %collective-permute-start.5 = (f32[16,412]{1,0:T(8,128)S(1)}, f32[16,412]{1,0:T(8,128)S(1)}, u32[]{:S(2)}, u32[]{:S(2)}) collective-permute-start(f32[16,412]{1,0:T(8,128)S(1)} %pad_maximum_fusion.5), channel_id=1, source_target_pairs={{0,16},{16,0},{1,17},{17,1},{2,18},{18,2},{3,19},{19,3},{4,20},{20... | collective-permute-start | bytes 79112 | tf_op jit(solution)/shard_map/ppermute | solution.py:40
  26.4 3.3 %fusion.123 = f32[16,1136]{1,0:T(8,128)S(1)} fusion(bf16[2272,1136]{1,0:T(8,128)(2,1)} %param.20, f32[16,4544]{1,0:T(8,128)S(1)} %reshape.879, s32[]{:T(128)S(6)} %select_n.335, f32[2272]{0:T(1024)S(1)} %dynamic-slice.1, f32[2272]{0:T(1024)S(1)} %dynamic-slice, f32[16]{0:T(128)S(1)} %rsqrt.12, f32[16]{0:T(128)S(1)} %div.135), kind=kOutput, calls=%fused_computation.341 | convolution fusion | flops 82773504 | bytes 5407748 | tf_op jit(solution)/shard_map/dot_general | solution.py:199
  30.2 2.6 %collective-permute-start.7 = (bf16[4,2,284]{2,1,0:T(2,128)(2,1)S(1)}, bf16[4,2,284]{2,1,0:T(2,128)(2,1)S(1)}, u32[]{:S(2)}, u32[]{:S(2)}) collective-permute-start(bf16[4,2,284]{2,1,0:T(2,128)(2,1)S(1)} %slice.427), channel_id=1, source_target_pairs={{0,8},{1,9},{2,10},{3,11},{4,12},{5,13},{6,14},{7,15},{8,0},{9,1},... | collective-permute-start | bytes 13640 | tf_op jit(solution)/shard_map/ppermute | solution.py:22
  33.0 1.8 %collective-permute-done.7 = bf16[4,2,284]{2,1,0:T(2,128)(2,1)S(1)} collective-permute-done((bf16[4,2,284]{2,1,0:T(2,128)(2,1)S(1)}, bf16[4,2,284]{2,1,0:T(2,128)(2,1)S(1)}, u32[]{:S(2)}, u32[]{:S(2)}) %collective-permute-start.7) | collective-permute-done | bytes 4576 | tf_op jit(solution)/shard_map/ppermute | solution.py:22
  35.0 1.6 %collective-permute-start.8 = (bf16[2,4,2,284]{3,2,1,0:T(2,128)(2,1)S(1)}, bf16[2,4,2,284]{3,2,1,0:T(2,128)(2,1)S(1)}, u32[]{:S(2)}, u32[]{:S(2)}) collective-permute-start(bf16[2,4,2,284]{3,2,1,0:T(2,128)(2,1)S(1)} %pad_maximum_fusion.9), channel_id=1, source_target_pairs={{0,4},{1,5},{2,6},{3,7},{4,0},{5,1},{6,2},{7,3},{8,12},{9,13},{10,... | collective-permute-start | bytes 27272 | tf_op jit(solution)/shard_map/ppermute | solution.py:22
  36.8 1.9 %collective-permute-done.8 = bf16[2,4,2,284]{3,2,1,0:T(2,128)(2,1)S(1)} collective-permute-done((bf16[2,4,2,284]{3,2,1,0:T(2,128)(2,1)S(1)}, bf16[2,4,2,284]{3,2,1,0:T(2,128)(2,1)S(1)}, u32[]{:S(2)}, u32[]{:S(2)}) %collective-permute-start.8) | collective-permute-done | bytes 9120 | tf_op jit(solution)/shard_map/ppermute | solution.py:22
  38.8 1.6 %collective-permute-start.9 = (bf16[2,2,4,2,284]{4,3,2,1,0:T(2,128)(2,1)S(1)}, bf16[2,2,4,2,284]{4,3,2,1,0:T(2,128)(2,1)S(1)}, u32[]{:S(2)}, u32[]{:S(2)}) collective-permute-start(bf16[2,2,4,2,284]{4,3,2,1,0:T(2,128)(2,1)S(1)} %pad_maximum_fusion.7), channel_id=1, source_target_pairs={{0,2},{1,3},{2,0},{3,1},{4,6},{5,7},{6,4},{7,5},{8,10},{9,11},{10,... | collective-permute-start | bytes 54536 | tf_op jit(solution)/shard_map/ppermute | solution.py:22
  40.4 2.3 %collective-permute-done.9 = bf16[2,2,4,2,284]{4,3,2,1,0:T(2,128)(2,1)S(1)} collective-permute-done((bf16[2,2,4,2,284]{4,3,2,1,0:T(2,128)(2,1)S(1)}, bf16[2,2,4,2,284]{4,3,2,1,0:T(2,128)(2,1)S(1)}, u32[]{:S(2)}, u32[]{:S(2)}) %collective-permute-start.9) | collective-permute-done | bytes 18208 | tf_op jit(solution)/shard_map/ppermute | solution.py:22
  42.9 1.1 %collective-permute-done.10 = bf16[2,2,2,4,2,284]{5,4,3,2,1,0:T(2,128)(2,1)S(1)} collective-permute-done((bf16[2,2,2,4,2,284]{5,4,3,2,1,0:T(2,128)(2,1)S(1)}, bf16[2,2,2,4,2,284]{5,4,3,2,1,0:T(2,128)(2,1)S(1)}, u32[]{:S(2)}, u32[]{:S(2)}) %collective-permute-start.10) | collective-permute-done | bytes 36384 | tf_op jit(solution)/shard_map/ppermute | solution.py:22
  44.2 0.6 gather_fusion.1
  48.3 0.6 collective-permute-start.6
  49.8 1.6 %collective-permute-start.12 = (bf16[2,284,70]{1,0,2:T(2,128)(2,1)S(1)}, bf16[2,284,70]{1,0,2:T(2,128)(2,1)S(1)}, u32[]{:S(2)}, u32[]{:S(2)}) collective-permute-start(bf16[2,284,70]{1,0,2:T(2,128)(2,1)S(1)} %fusion.23), channel_id=1, source_target_pairs={{0,2},{1,3},{2,0},{3,1},{4,6},{5,7},{6,4},{7,5},{8,10},{9,11},{10,... | collective-permute-start | bytes 238568 | tf_op jit(solution)/shard_map/ppermute | solution.py:104
  51.4 1.5 %collective-permute-done.6 = f32[16,1136]{1,0:T(8,128)S(1)} collective-permute-done((f32[16,1136]{1,0:T(8,128)S(1)}, f32[16,1136]{1,0:T(8,128)S(1)}, u32[]{:S(2)}, u32[]{:S(2)}) %collective-permute-start.6) | collective-permute-done | bytes 72736 | tf_op jit(solution)/shard_map/ppermute | solution.py:40
  52.9 2.3 %fusion = f32[16,1136]{1,0:T(8,128)S(1)} fusion(bf16[1136,2272]{1,0:T(8,128)(2,1)} %param.21, f32[16,1136]{1,0:T(8,128)S(1)} %fusion.123, f32[16,1136]{1,0:T(8,128)S(1)} %collective-permute-done.6), kind=kOutput, calls=%fused_computation.4 | convolution fusion | flops 42495488 | bytes 2835456 | tf_op jit(solution)/shard_map/dot_general | solution.py:216
  55.5 0.6 concatenate.81
  56.1 1.6 %collective-permute-start.13 = (bf16[2,284,70]{1,2,0:T(8,128)(2,1)S(1)}, bf16[2,284,70]{1,2,0:T(8,128)(2,1)S(1)}, u32[]{:S(2)}, u32[]{:S(2)}) collective-permute-start(bf16[2,284,70]{1,2,0:T(8,128)(2,1)S(1)} %concatenate.81), channel_id=1, source_target_pairs={{0,4},{1,5},{2,6},{3,7},{4,0},{5,1},{6,2},{7,3},{8,12},{9,13},{10,... | collective-permute-start | bytes 238568 | tf_op jit(solution)/shard_map/ppermute | solution.py:104
  57.8 2.9 %fusion.2 = f32[16,1136]{1,0:T(8,128)S(1)} fusion(bf16[1136,2272]{1,0:T(8,128)(2,1)} %param.21, f32[16,1136]{1,0:T(8,128)S(1)} %fusion.123, f32[16,1136]{1,0:T(8,128)S(1)} %collective-permute-done.6), kind=kOutput, calls=%fused_computation.6 | convolution fusion | flops 42495488 | bytes 2835456 | tf_op jit(solution)/shard_map/dot_general | solution.py:217
  63.1 0.5 concatenate.89
  63.6 2.7 %collective-permute-start.14 = (bf16[2,4,6,70]{3,2,1,0:T(8,128)(2,1)S(1)}, bf16[2,4,6,70]{3,2,1,0:T(8,128)(2,1)S(1)}, u32[]{:S(2)}, u32[]{:S(2)}) collective-permute-start(bf16[2,4,6,70]{3,2,1,0:T(8,128)(2,1)S(1)} %constant_dynamic-slice_fusion), channel_id=1, source_target_pairs={{0,8},{1,9},{2,10},{3,11},{4,12},{5,13},{6,14},{7,15},{8,0},{9,1},... | collective-permute-start | bytes 20168 | tf_op jit(solution)/shard_map/ppermute | solution.py:122
  66.8 1.5 %collective-permute-done.14 = bf16[2,4,6,70]{3,2,1,0:T(8,128)(2,1)S(1)} collective-permute-done((bf16[2,4,6,70]{3,2,1,0:T(8,128)(2,1)S(1)}, bf16[2,4,6,70]{3,2,1,0:T(8,128)(2,1)S(1)}, u32[]{:S(2)}, u32[]{:S(2)}) %collective-permute-start.14) | collective-permute-done | bytes 6752 | tf_op jit(solution)/shard_map/ppermute | solution.py:122
  69.1 0.7 collective-permute-start.15
  69.8 3.0 %collective-permute-done.15 = bf16[4,2,284]{2,0,1:T(4,128)(2,1)S(1)} collective-permute-done((bf16[4,2,284]{2,0,1:T(4,128)(2,1)S(1)}, bf16[4,2,284]{2,0,1:T(4,128)(2,1)S(1)}, u32[]{:S(2)}, u32[]{:S(2)}) %collective-permute-start.15) | collective-permute-done | bytes 4576 | tf_op jit(solution)/shard_map/ppermute | solution.py:22
  72.8 0.6 gather_fusion.2
  74.2 1.3 %collective-permute-done.16 = f32[2,2,2,4,2,284]{5,4,3,2,1,0:T(2,128)S(1)} collective-permute-done((f32[2,2,2,4,2,284]{5,4,3,2,1,0:T(2,128)S(1)}, f32[2,2,2,4,2,284]{5,4,3,2,1,0:T(2,128)S(1)}, u32[]{:S(2)}, u32[]{:S(2)}) %collective-permute-start.16) | collective-permute-done | bytes 72736 | tf_op jit(solution)/shard_map/ppermute | solution.py:57
  75.5 1.6 %collective-permute-start.17 = (f32[2,2,4,2,284]{4,3,2,1,0:T(2,128)S(1)}, f32[2,2,4,2,284]{4,3,2,1,0:T(2,128)S(1)}, u32[]{:S(2)}, u32[]{:S(2)}) collective-permute-start(f32[2,2,4,2,284]{4,3,2,1,0:T(2,128)S(1)} %fusion.36), channel_id=1, source_target_pairs={{0,2},{1,3},{2,0},{3,1},{4,6},{5,7},{6,4},{7,5},{8,10},{9,11},{10,... | collective-permute-start | bytes 109064 | tf_op jit(solution)/shard_map/ppermute | solution.py:57
  77.1 2.6 %collective-permute-done.17 = f32[2,2,4,2,284]{4,3,2,1,0:T(2,128)S(1)} collective-permute-done((f32[2,2,4,2,284]{4,3,2,1,0:T(2,128)S(1)}, f32[2,2,4,2,284]{4,3,2,1,0:T(2,128)S(1)}, u32[]{:S(2)}, u32[]{:S(2)}) %collective-permute-start.17) | collective-permute-done | bytes 36384 | tf_op jit(solution)/shard_map/ppermute | solution.py:57
  79.7 1.6 %collective-permute-start.18 = (f32[2,4,2,284]{3,2,1,0:T(2,128)S(1)}, f32[2,4,2,284]{3,2,1,0:T(2,128)S(1)}, u32[]{:S(2)}, u32[]{:S(2)}) collective-permute-start(f32[2,4,2,284]{3,2,1,0:T(2,128)S(1)} %fusion.41), channel_id=1, source_target_pairs={{0,4},{1,5},{2,6},{3,7},{4,0},{5,1},{6,2},{7,3},{8,12},{9,13},{10,... | collective-permute-start | bytes 54536 | tf_op jit(solution)/shard_map/ppermute | solution.py:57
  81.4 2.2 %collective-permute-done.18 = f32[2,4,2,284]{3,2,1,0:T(2,128)S(1)} collective-permute-done((f32[2,4,2,284]{3,2,1,0:T(2,128)S(1)}, f32[2,4,2,284]{3,2,1,0:T(2,128)S(1)}, u32[]{:S(2)}, u32[]{:S(2)}) %collective-permute-start.18) | collective-permute-done | bytes 18208 | tf_op jit(solution)/shard_map/ppermute | solution.py:57
  83.7 4.6 %collective-permute-start.19 = (f32[4,2,284]{2,1,0:T(2,128)S(1)}, f32[4,2,284]{2,1,0:T(2,128)S(1)}, u32[]{:S(2)}, u32[]{:S(2)}) collective-permute-start(f32[4,2,284]{2,1,0:T(2,128)S(1)} %get-tuple-element.68), channel_id=1, source_target_pairs={{0,0},{1,1},{2,2},{3,3},{4,4},{5,5},{6,6},{7,7},{8,16},{9,17},{10,... | collective-permute-start | bytes 27272 | tf_op jit(solution)/shard_map/ppermute | solution.py:295
  88.4 0.8 copy.250
  89.2 1.9 %collective-permute-done.19 = f32[4,2,284]{2,1,0:T(2,128)S(1)} collective-permute-done((f32[4,2,284]{2,1,0:T(2,128)S(1)}, f32[4,2,284]{2,1,0:T(2,128)S(1)}, u32[]{:S(2)}, u32[]{:S(2)}) %collective-permute-start.19) | collective-permute-done | bytes 9120 | tf_op jit(solution)/shard_map/ppermute | solution.py:295
  91.1 1.0 %collective-permute-done.20 = f32[4,2,284]{2,1,0:T(2,128)S(1)} collective-permute-done((f32[4,2,284]{2,1,0:T(2,128)S(1)}, f32[4,2,284]{2,1,0:T(2,128)S(1)}, u32[]{:S(2)}, u32[]{:S(2)}) %collective-permute-start.20) | collective-permute-done | bytes 9120 | tf_op jit(solution)/shard_map/ppermute | solution.py:295
  92.0 0.6 add_convert_fusion
  (172 shorter events, 14.4 us)
Async XLA Ops:
  0.6 72.8 %copy-start = (bf16[284,2272]{1,0:T(8,128)(2,1)S(1)}, bf16[284,2272]{1,0:T(8,128)(2,1)}, u32[]{:S(2)}) copy-start(bf16[284,2272]{1,0:T(8,128)(2,1)} %param.19) | copy-start | bytes 3871492
  0.6 3.9 %collective-permute-start = (bf16[4,2,284]{2,1,0:T(2,128)(2,1)}, bf16[4,2,284]{2,1,0:T(2,128)(2,1)S(1)}, u32[]{:S(2)}, u32[]{:S(2)}) collective-permute-start(bf16[4,2,284]{2,1,0:T(2,128)(2,1)} %param.11), channel_id=1, source_target_pairs={{0,16},{16,0},{1,17},{17,1},{2,18},{18,2},{3,19},{19,3},{4,20},{20... | collective-permute-start | bytes 13640 | tf_op jit(solution)/shard_map/ppermute | solution.py:22
  5.3 4.7 %collective-permute-start.1 = (bf16[2,4,2,284]{3,2,1,0:T(2,128)(2,1)S(1)}, bf16[2,4,2,284]{3,2,1,0:T(2,128)(2,1)S(1)}, u32[]{:S(2)}, u32[]{:S(2)}) collective-permute-start(bf16[2,4,2,284]{3,2,1,0:T(2,128)(2,1)S(1)} %pad_maximum_fusion.8), channel_id=1, source_target_pairs={{0,8},{1,9},{2,10},{3,11},{4,12},{5,13},{6,14},{7,15},{8,0},{9,1},... | collective-permute-start | bytes 27272 | tf_op jit(solution)/shard_map/ppermute | solution.py:22
  10.0 3.9 %collective-permute-start.2 = (bf16[2,2,4,2,284]{4,3,2,1,0:T(2,128)(2,1)S(1)}, bf16[2,2,4,2,284]{4,3,2,1,0:T(2,128)(2,1)S(1)}, u32[]{:S(2)}, u32[]{:S(2)}) collective-permute-start(bf16[2,2,4,2,284]{4,3,2,1,0:T(2,128)(2,1)S(1)} %pad_maximum_fusion.6), channel_id=1, source_target_pairs={{0,4},{1,5},{2,6},{3,7},{4,0},{5,1},{6,2},{7,3},{8,12},{9,13},{10,... | collective-permute-start | bytes 54536 | tf_op jit(solution)/shard_map/ppermute | solution.py:22
  13.9 4.2 %collective-permute-start.3 = (bf16[2,2,2,4,2,284]{5,4,3,2,1,0:T(2,128)(2,1)S(1)}, bf16[2,2,2,4,2,284]{5,4,3,2,1,0:T(2,128)(2,1)S(1)}, u32[]{:S(2)}, u32[]{:S(2)}) collective-permute-start(bf16[2,2,2,4,2,284]{5,4,3,2,1,0:T(2,128)(2,1)S(1)} %pad_maximum_fusion.3), channel_id=1, source_target_pairs={{0,2},{1,3},{2,0},{3,1},{4,6},{5,7},{6,4},{7,5},{8,10},{9,11},{10,... | collective-permute-start | bytes 109064 | tf_op jit(solution)/shard_map/ppermute | solution.py:22
  18.3 1.7 %collective-permute-start.4 = (bf16[2,2,2,2,4,2,284]{6,5,4,3,2,1,0:T(2,128)(2,1)S(1)}, bf16[2,2,2,2,4,2,284]{6,5,4,3,2,1,0:T(2,128)(2,1)S(1)}, u32[]{:S(2)}, u32[]{:S(2)}) collective-permute-start(bf16[2,2,2,2,4,2,284]{6,5,4,3,2,1,0:T(2,128)(2,1)S(1)} %pad_maximum_fusion.1), channel_id=1, source_target_pairs={{0,1},{1,0},{2,3},{3,2},{4,5},{5,4},{6,7},{7,6},{8,9},{9,8},{10,11... | collective-permute-start | bytes 218120 | tf_op jit(solution)/shard_map/ppermute | solution.py:22
  22.5 2.0 %copy-start.1 = (bf16[2272,128]{1,0:T(8,128)(2,1)S(1)}, bf16[2272,128]{1,0:T(8,128)(2,1)}, u32[]{:S(2)}) copy-start(bf16[2272,128]{1,0:T(8,128)(2,1)} %param.18) | copy-start | bytes 1744900
  24.8 10.0 %copy-start.2 = (bf16[2,512,128]{2,1,0:T(8,128)(2,1)S(1)}, bf16[2,512,128]{2,1,0:T(8,128)(2,1)}, u32[]{:S(2)}) copy-start(bf16[2,512,128]{2,1,0:T(8,128)(2,1)} %param.12) | copy-start | bytes 786436
  24.8 4.9 %collective-permute-start.5 = (f32[16,412]{1,0:T(8,128)S(1)}, f32[16,412]{1,0:T(8,128)S(1)}, u32[]{:S(2)}, u32[]{:S(2)}) collective-permute-start(f32[16,412]{1,0:T(8,128)S(1)} %pad_maximum_fusion.5), channel_id=1, source_target_pairs={{0,16},{16,0},{1,17},{17,1},{2,18},{18,2},{3,19},{19,3},{4,20},{20... | collective-permute-start | bytes 79112 | tf_op jit(solution)/shard_map/ppermute | solution.py:40
  30.2 4.5 %collective-permute-start.7 = (bf16[4,2,284]{2,1,0:T(2,128)(2,1)S(1)}, bf16[4,2,284]{2,1,0:T(2,128)(2,1)S(1)}, u32[]{:S(2)}, u32[]{:S(2)}) collective-permute-start(bf16[4,2,284]{2,1,0:T(2,128)(2,1)S(1)} %slice.427), channel_id=1, source_target_pairs={{0,8},{1,9},{2,10},{3,11},{4,12},{5,13},{6,14},{7,15},{8,0},{9,1},... | collective-permute-start | bytes 13640 | tf_op jit(solution)/shard_map/ppermute | solution.py:22
  35.0 3.8 %collective-permute-start.8 = (bf16[2,4,2,284]{3,2,1,0:T(2,128)(2,1)S(1)}, bf16[2,4,2,284]{3,2,1,0:T(2,128)(2,1)S(1)}, u32[]{:S(2)}, u32[]{:S(2)}) collective-permute-start(bf16[2,4,2,284]{3,2,1,0:T(2,128)(2,1)S(1)} %pad_maximum_fusion.9), channel_id=1, source_target_pairs={{0,4},{1,5},{2,6},{3,7},{4,0},{5,1},{6,2},{7,3},{8,12},{9,13},{10,... | collective-permute-start | bytes 27272 | tf_op jit(solution)/shard_map/ppermute | solution.py:22
  38.8 3.9 %collective-permute-start.9 = (bf16[2,2,4,2,284]{4,3,2,1,0:T(2,128)(2,1)S(1)}, bf16[2,2,4,2,284]{4,3,2,1,0:T(2,128)(2,1)S(1)}, u32[]{:S(2)}, u32[]{:S(2)}) collective-permute-start(bf16[2,2,4,2,284]{4,3,2,1,0:T(2,128)(2,1)S(1)} %pad_maximum_fusion.7), channel_id=1, source_target_pairs={{0,2},{1,3},{2,0},{3,1},{4,6},{5,7},{6,4},{7,5},{8,10},{9,11},{10,... | collective-permute-start | bytes 54536 | tf_op jit(solution)/shard_map/ppermute | solution.py:22
  42.7 1.3 %collective-permute-start.10 = (bf16[2,2,2,4,2,284]{5,4,3,2,1,0:T(2,128)(2,1)S(1)}, bf16[2,2,2,4,2,284]{5,4,3,2,1,0:T(2,128)(2,1)S(1)}, u32[]{:S(2)}, u32[]{:S(2)}) collective-permute-start(bf16[2,2,2,4,2,284]{5,4,3,2,1,0:T(2,128)(2,1)S(1)} %pad_maximum_fusion.4), channel_id=1, source_target_pairs={{0,1},{1,0},{2,3},{3,2},{4,5},{5,4},{6,7},{7,6},{8,9},{9,8},{10,11... | collective-permute-start | bytes 109064 | tf_op jit(solution)/shard_map/ppermute | solution.py:22
  48.0 1.4 %collective-permute-start.11 = (bf16[2,284,70]{1,0,2:T(2,128)(2,1)S(1)}, bf16[2,284,70]{1,0,2:T(2,128)(2,1)S(1)}, u32[]{:S(2)}, u32[]{:S(2)}) collective-permute-start(bf16[2,284,70]{1,0,2:T(2,128)(2,1)S(1)} %fusion.22), channel_id=1, source_target_pairs={{0,1},{1,0},{2,3},{3,2},{4,5},{5,4},{6,7},{7,6},{8,9},{9,8},{10,11... | collective-permute-start | bytes 238568 | tf_op jit(solution)/shard_map/ppermute | solution.py:104
  48.3 4.6 %collective-permute-start.6 = (f32[16,1136]{1,0:T(8,128)S(1)}, f32[16,1136]{1,0:T(8,128)S(1)}, u32[]{:S(2)}, u32[]{:S(2)}) collective-permute-start(f32[16,1136]{1,0:T(8,128)S(1)} %fusion.123), channel_id=1, source_target_pairs={{0,16},{16,0},{1,17},{17,1},{2,18},{18,2},{3,19},{19,3},{4,20},{20... | collective-permute-start | bytes 218120 | tf_op jit(solution)/shard_map/ppermute | solution.py:40
  49.8 5.4 %collective-permute-start.12 = (bf16[2,284,70]{1,0,2:T(2,128)(2,1)S(1)}, bf16[2,284,70]{1,0,2:T(2,128)(2,1)S(1)}, u32[]{:S(2)}, u32[]{:S(2)}) collective-permute-start(bf16[2,284,70]{1,0,2:T(2,128)(2,1)S(1)} %fusion.23), channel_id=1, source_target_pairs={{0,2},{1,3},{2,0},{3,1},{4,6},{5,7},{6,4},{7,5},{8,10},{9,11},{10,... | collective-permute-start | bytes 238568 | tf_op jit(solution)/shard_map/ppermute | solution.py:104
  56.1 4.8 %collective-permute-start.13 = (bf16[2,284,70]{1,2,0:T(8,128)(2,1)S(1)}, bf16[2,284,70]{1,2,0:T(8,128)(2,1)S(1)}, u32[]{:S(2)}, u32[]{:S(2)}) collective-permute-start(bf16[2,284,70]{1,2,0:T(8,128)(2,1)S(1)} %concatenate.81), channel_id=1, source_target_pairs={{0,4},{1,5},{2,6},{3,7},{4,0},{5,1},{6,2},{7,3},{8,12},{9,13},{10,... | collective-permute-start | bytes 238568 | tf_op jit(solution)/shard_map/ppermute | solution.py:104
  63.6 4.7 %collective-permute-start.14 = (bf16[2,4,6,70]{3,2,1,0:T(8,128)(2,1)S(1)}, bf16[2,4,6,70]{3,2,1,0:T(8,128)(2,1)S(1)}, u32[]{:S(2)}, u32[]{:S(2)}) collective-permute-start(bf16[2,4,6,70]{3,2,1,0:T(8,128)(2,1)S(1)} %constant_dynamic-slice_fusion), channel_id=1, source_target_pairs={{0,8},{1,9},{2,10},{3,11},{4,12},{5,13},{6,14},{7,15},{8,0},{9,1},... | collective-permute-start | bytes 20168 | tf_op jit(solution)/shard_map/ppermute | solution.py:122
  69.1 3.6 %collective-permute-start.15 = (bf16[4,2,284]{2,0,1:T(4,128)(2,1)S(1)}, bf16[4,2,284]{2,0,1:T(4,128)(2,1)S(1)}, u32[]{:S(2)}, u32[]{:S(2)}) collective-permute-start(bf16[4,2,284]{2,0,1:T(4,128)(2,1)S(1)} %get-tuple-element.74), channel_id=1, source_target_pairs={{0,16},{16,0},{1,17},{17,1},{2,18},{18,2},{3,19},{19,3},{4,20},{20... | collective-permute-start | bytes 13640 | tf_op jit(solution)/shard_map/ppermute | solution.py:22
  73.9 18.2 %copy-start.3 = (bf16[4,2,284]{2,1,0:T(2,128)(2,1)S(1)}, bf16[4,2,284]{2,1,0:T(2,128)(2,1)}, u32[]{:S(2)}) copy-start(bf16[4,2,284]{2,1,0:T(2,128)(2,1)} %param.11) | copy-start | bytes 13636
  74.0 1.4 %collective-permute-start.16 = (f32[2,2,2,4,2,284]{5,4,3,2,1,0:T(2,128)S(1)}, f32[2,2,2,4,2,284]{5,4,3,2,1,0:T(2,128)S(1)}, u32[]{:S(2)}, u32[]{:S(2)}) collective-permute-start(f32[2,2,2,4,2,284]{5,4,3,2,1,0:T(2,128)S(1)} %fusion.21), channel_id=1, source_target_pairs={{0,1},{1,0},{2,3},{3,2},{4,5},{5,4},{6,7},{7,6},{8,9},{9,8},{10,11... | collective-permute-start | bytes 218120 | tf_op jit(solution)/shard_map/ppermute | solution.py:57
  75.5 4.2 %collective-permute-start.17 = (f32[2,2,4,2,284]{4,3,2,1,0:T(2,128)S(1)}, f32[2,2,4,2,284]{4,3,2,1,0:T(2,128)S(1)}, u32[]{:S(2)}, u32[]{:S(2)}) collective-permute-start(f32[2,2,4,2,284]{4,3,2,1,0:T(2,128)S(1)} %fusion.36), channel_id=1, source_target_pairs={{0,2},{1,3},{2,0},{3,1},{4,6},{5,7},{6,4},{7,5},{8,10},{9,11},{10,... | collective-permute-start | bytes 109064 | tf_op jit(solution)/shard_map/ppermute | solution.py:57
  79.7 3.9 %collective-permute-start.18 = (f32[2,4,2,284]{3,2,1,0:T(2,128)S(1)}, f32[2,4,2,284]{3,2,1,0:T(2,128)S(1)}, u32[]{:S(2)}, u32[]{:S(2)}) collective-permute-start(f32[2,4,2,284]{3,2,1,0:T(2,128)S(1)} %fusion.41), channel_id=1, source_target_pairs={{0,4},{1,5},{2,6},{3,7},{4,0},{5,1},{6,2},{7,3},{8,12},{9,13},{10,... | collective-permute-start | bytes 54536 | tf_op jit(solution)/shard_map/ppermute | solution.py:57
  83.7 7.4 %collective-permute-start.19 = (f32[4,2,284]{2,1,0:T(2,128)S(1)}, f32[4,2,284]{2,1,0:T(2,128)S(1)}, u32[]{:S(2)}, u32[]{:S(2)}) collective-permute-start(f32[4,2,284]{2,1,0:T(2,128)S(1)} %get-tuple-element.68), channel_id=1, source_target_pairs={{0,0},{1,1},{2,2},{3,3},{4,4},{5,5},{6,6},{7,7},{8,16},{9,17},{10,... | collective-permute-start | bytes 27272 | tf_op jit(solution)/shard_map/ppermute | solution.py:295
  88.3 3.7 %collective-permute-start.20 = (f32[4,2,284]{2,1,0:T(2,128)S(1)}, f32[4,2,284]{2,1,0:T(2,128)S(1)}, u32[]{:S(2)}, u32[]{:S(2)}) collective-permute-start(f32[4,2,284]{2,1,0:T(2,128)S(1)} %get-tuple-element.67), channel_id=1, source_target_pairs={{0,16},{1,17},{2,18},{3,19},{4,20},{5,21},{6,22},{7,23},{8,0},{9,1... | collective-permute-start | bytes 27272 | tf_op jit(solution)/shard_map/ppermute | solution.py:295

commit v19 on v17

--- a/solution.py
+++ b/solution.py
@@ -217,8 +217,9 @@
         jnp.dot(hidden, w_down[:, down_half:], preferred_element_type=jnp.float32),
     ]
 
-    query_all, riders = gather_xor(own_query, "seq", seq_size, {0: kv_cache})
-    kv_cache = riders[0]
+    cache_level = min(1, seq_size.bit_length() - 2)
+    query_all, riders = gather_xor(own_query, "seq", seq_size, {cache_level: kv_cache})
+    kv_cache = riders[cache_level]
     query_all = jnp.take(query_all, seq_slots, axis=0, mode="clip")
     query_all = query_all.transpose(1, 2, 0, 3).reshape(steps, group_rows, model_width)
     flat_positions = positions.reshape(-1)

time: 93.2 us -> 93.2 us (level)
  no operation moved by 1% of the time
where the time goes in v19:
time: 93.2 us; the launch traced here: 92.2 us
  starting transfers between devices  28.8 us (31%)
  waiting for transfers between devices  28.6 us (31%)
  local copies, waits for them, and re-layouts  12.4 us (13%)
  matrix products  11.8 us (13%)
  other arithmetic  9.1 us (10%)
  between operations  1.53 us (2%)
    ppermute x10, waiting for transfers between devices, gather_xor(): lax.ppermute(stacked, axis, xor_pairs(size, bit))  16 us
    ppermute x10, starting transfers between devices, gather_xor(): lax.ppermute(stacked, axis, xor_pairs(size, bit))  12.6 us
    ppermute x3, waiting for transfers between devices, scatter_sum(): blocks = keep + lax.ppermute(send, axis, xor_pairs(size, bit))  6.08 us
    ppermute x1, starting transfers between devices, shards(): lax.ppermute(own_block, ALL, own_routes)  4.61 us
    ppermute x3, starting transfers between devices, merge_over(): lax.ppermute(pack_merge(peak, total, weighted), axis, xor_pairs(size, bit))  3.44 us
    dot_general x1, matrix products, shards(): part_up = jnp.dot(normed_part, w_up, preferred_element_type=jnp.float32)  3.32 us
    ppermute x3, starting transfers between devices, scatter_sum(): blocks = keep + lax.ppermute(send, axis, xor_pairs(size, bit))  3.3 us
    concatenate x12, local copies, waits for them, and re-layouts, pack_merge(): jnp.concatenate([jnp.stack(split_exact(peak) + split_exact(total), axis=-...  3.19 us
  transfers between devices with their start and end apart: 21, of which 19 were waited for; matrix products, arithmetic and copies ran while one was open for 18% of the time, Pallas kernels for 0%

profile of v19, /device:TPU:2, one launch (start us, length us, event | category | flops | bytes accessed | tf_op | source)
XLA Modules:
  0.0 92.2 jit_solution(11801779297452214229)
XLA Ops:
  0.8 0.8 dynamic_slice.22
  1.7 0.8 select_reduce_fusion.2
  2.6 0.7 select_reduce_fusion.1
  4.5 0.7 pad_maximum_fusion.8
  5.3 2.7 %collective-permute-start.1 = (bf16[2,4,2,284]{3,2,1,0:T(2,128)(2,1)S(1)}, bf16[2,4,2,284]{3,2,1,0:T(2,128)(2,1)S(1)}, u32[]{:S(2)}, u32[]{:S(2)}) collective-permute-start(bf16[2,4,2,284]{3,2,1,0:T(2,128)(2,1)S(1)} %pad_maximum_fusion.8), channel_id=1, source_target_pairs={{0,8},{1,9},{2,10},{3,11},{4,12},{5,13},{6,14},{7,15},{8,0},{9,1},... | collective-permute-start | bytes 27272 | tf_op jit(solution)/shard_map/ppermute | solution.py:22
  7.9 0.7 fusion.135
  8.6 1.3 %collective-permute-done.1 = bf16[2,4,2,284]{3,2,1,0:T(2,128)(2,1)S(1)} collective-permute-done((bf16[2,4,2,284]{3,2,1,0:T(2,128)(2,1)S(1)}, bf16[2,4,2,284]{3,2,1,0:T(2,128)(2,1)S(1)}, u32[]{:S(2)}, u32[]{:S(2)}) %collective-permute-start.1) | collective-permute-done | bytes 9120 | tf_op jit(solution)/shard_map/ppermute | solution.py:22
  10.0 1.6 %collective-permute-start.2 = (bf16[2,2,4,2,284]{4,3,2,1,0:T(2,128)(2,1)S(1)}, bf16[2,2,4,2,284]{4,3,2,1,0:T(2,128)(2,1)S(1)}, u32[]{:S(2)}, u32[]{:S(2)}) collective-permute-start(bf16[2,2,4,2,284]{4,3,2,1,0:T(2,128)(2,1)S(1)} %pad_maximum_fusion.6), channel_id=1, source_target_pairs={{0,4},{1,5},{2,6},{3,7},{4,0},{5,1},{6,2},{7,3},{8,12},{9,13},{10,... | collective-permute-start | bytes 54536 | tf_op jit(solution)/shard_map/ppermute | solution.py:22
  11.7 2.2 %collective-permute-done.2 = bf16[2,2,4,2,284]{4,3,2,1,0:T(2,128)(2,1)S(1)} collective-permute-done((bf16[2,2,4,2,284]{4,3,2,1,0:T(2,128)(2,1)S(1)}, bf16[2,2,4,2,284]{4,3,2,1,0:T(2,128)(2,1)S(1)}, u32[]{:S(2)}, u32[]{:S(2)}) %collective-permute-start.2) | collective-permute-done | bytes 18208 | tf_op jit(solution)/shard_map/ppermute | solution.py:22
  13.9 1.6 %collective-permute-start.3 = (bf16[2,2,2,4,2,284]{5,4,3,2,1,0:T(2,128)(2,1)S(1)}, bf16[2,2,2,4,2,284]{5,4,3,2,1,0:T(2,128)(2,1)S(1)}, u32[]{:S(2)}, u32[]{:S(2)}) collective-permute-start(bf16[2,2,2,4,2,284]{5,4,3,2,1,0:T(2,128)(2,1)S(1)} %pad_maximum_fusion.3), channel_id=1, source_target_pairs={{0,2},{1,3},{2,0},{3,1},{4,6},{5,7},{6,4},{7,5},{8,10},{9,11},{10,... | collective-permute-start | bytes 109064 | tf_op jit(solution)/shard_map/ppermute | solution.py:22
  15.8 0.8 dynamic-slice
  16.5 0.8 dynamic-slice.1
  17.3 0.8 collective-permute-done.3
  18.5 1.1 %collective-permute-done.4 = bf16[2,2,2,2,4,2,284]{6,5,4,3,2,1,0:T(2,128)(2,1)S(1)} collective-permute-done((bf16[2,2,2,2,4,2,284]{6,5,4,3,2,1,0:T(2,128)(2,1)S(1)}, bf16[2,2,2,2,4,2,284]{6,5,4,3,2,1,0:T(2,128)(2,1)S(1)}, u32[]{:S(2)}, u32[]{:S(2)}) %collective-permute-start.4) | collective-permute-done | bytes 72736 | tf_op jit(solution)/shard_map/ppermute | solution.py:22
  19.9 1.0 %gather_fusion = bf16[32,4,2,284]{3,2,1,0:T(2,128)(2,1)S(1)} fusion(bf16[32,4,2,284]{3,2,1,0:T(2,128)(2,1)S(1)} %bitcast.285, s32[1024]{0:T(1024)S(1)} %get-tuple-element.110), kind=kCustom, calls=%fused_computation | custom fusion | bytes 290944 | tf_op jit(solution)/shard_map/jit(_take)/gather | solution.py:191
  22.4 1.8 %fusion.121 = f32[16,284]{1,0:T(8,128)S(1)} fusion(bf16[2272,284]{0,1:T(8,128)(2,1)} %param.17, f32[16,4544]{1,0:T(8,128)S(1)} %reshape.879, s32[]{:T(128)S(6)} %select_n.335, f32[2272]{0:T(1024)S(1)} %dynamic-slice.1, f32[2272]{0:T(1024)S(1)} %dynamic-slice, f32[16]{0:T(128)S(1)} %rsqrt.12, f32[16]{0:T(128)S(1)} %div.135), kind=kOutput, calls=%fused_computation.340 | convolution fusion | flops 20829696 | bytes 1481732 | tf_op jit(solution)/shard_map/dot_general | solution.py:196
  24.5 1.4 %collective-permute-start.5 = (f32[16,412]{1,0:T(8,128)S(1)}, f32[16,412]{1,0:T(8,128)S(1)}, u32[]{:S(2)}, u32[]{:S(2)}) collective-permute-start(f32[16,412]{1,0:T(8,128)S(1)} %pad_maximum_fusion.5), channel_id=1, source_target_pairs={{0,16},{16,0},{1,17},{17,1},{2,18},{18,2},{3,19},{19,3},{4,20},{20... | collective-permute-start | bytes 79112 | tf_op jit(solution)/shard_map/ppermute | solution.py:40
  25.9 3.3 %fusion.123 = f32[16,1136]{1,0:T(8,128)S(1)} fusion(bf16[2272,1136]{1,0:T(8,128)(2,1)} %param.20, f32[16,4544]{1,0:T(8,128)S(1)} %reshape.879, s32[]{:T(128)S(6)} %select_n.335, f32[2272]{0:T(1024)S(1)} %dynamic-slice.1, f32[2272]{0:T(1024)S(1)} %dynamic-slice, f32[16]{0:T(128)S(1)} %rsqrt.12, f32[16]{0:T(128)S(1)} %div.135), kind=kOutput, calls=%fused_computation.341 | convolution fusion | flops 82773504 | bytes 5407748 | tf_op jit(solution)/shard_map/dot_general | solution.py:199
  29.7 2.6 %collective-permute-start.7 = (bf16[4,2,284]{2,1,0:T(2,128)(2,1)S(1)}, bf16[4,2,284]{2,1,0:T(2,128)(2,1)S(1)}, u32[]{:S(2)}, u32[]{:S(2)}) collective-permute-start(bf16[4,2,284]{2,1,0:T(2,128)(2,1)S(1)} %slice.427), channel_id=1, source_target_pairs={{0,8},{1,9},{2,10},{3,11},{4,12},{5,13},{6,14},{7,15},{8,0},{9,1},... | collective-permute-start | bytes 13640 | tf_op jit(solution)/shard_map/ppermute | solution.py:22
  32.5 1.8 %collective-permute-done.7 = bf16[4,2,284]{2,1,0:T(2,128)(2,1)S(1)} collective-permute-done((bf16[4,2,284]{2,1,0:T(2,128)(2,1)S(1)}, bf16[4,2,284]{2,1,0:T(2,128)(2,1)S(1)}, u32[]{:S(2)}, u32[]{:S(2)}) %collective-permute-start.7) | collective-permute-done | bytes 4576 | tf_op jit(solution)/shard_map/ppermute | solution.py:22
  34.3 1.6 %collective-permute-start.8 = (bf16[2,4,2,284]{3,2,1,0:T(2,128)(2,1)S(1)}, bf16[2,4,2,284]{3,2,1,0:T(2,128)(2,1)S(1)}, u32[]{:S(2)}, u32[]{:S(2)}) collective-permute-start(bf16[2,4,2,284]{3,2,1,0:T(2,128)(2,1)S(1)} %pad_maximum_fusion.9), channel_id=1, source_target_pairs={{0,4},{1,5},{2,6},{3,7},{4,0},{5,1},{6,2},{7,3},{8,12},{9,13},{10,... | collective-permute-start | bytes 27272 | tf_op jit(solution)/shard_map/ppermute | solution.py:22
  36.0 2.1 %collective-permute-done.8 = bf16[2,4,2,284]{3,2,1,0:T(2,128)(2,1)S(1)} collective-permute-done((bf16[2,4,2,284]{3,2,1,0:T(2,128)(2,1)S(1)}, bf16[2,4,2,284]{3,2,1,0:T(2,128)(2,1)S(1)}, u32[]{:S(2)}, u32[]{:S(2)}) %collective-permute-start.8) | collective-permute-done | bytes 9120 | tf_op jit(solution)/shard_map/ppermute | solution.py:22
  38.3 1.6 %collective-permute-start.9 = (bf16[2,2,4,2,284]{4,3,2,1,0:T(2,128)(2,1)S(1)}, bf16[2,2,4,2,284]{4,3,2,1,0:T(2,128)(2,1)S(1)}, u32[]{:S(2)}, u32[]{:S(2)}) collective-permute-start(bf16[2,2,4,2,284]{4,3,2,1,0:T(2,128)(2,1)S(1)} %pad_maximum_fusion.7), channel_id=1, source_target_pairs={{0,2},{1,3},{2,0},{3,1},{4,6},{5,7},{6,4},{7,5},{8,10},{9,11},{10,... | collective-permute-start | bytes 54536 | tf_op jit(solution)/shard_map/ppermute | solution.py:22
  40.0 2.1 %collective-permute-done.9 = bf16[2,2,4,2,284]{4,3,2,1,0:T(2,128)(2,1)S(1)} collective-permute-done((bf16[2,2,4,2,284]{4,3,2,1,0:T(2,128)(2,1)S(1)}, bf16[2,2,4,2,284]{4,3,2,1,0:T(2,128)(2,1)S(1)}, u32[]{:S(2)}, u32[]{:S(2)}) %collective-permute-start.9) | collective-permute-done | bytes 18208 | tf_op jit(solution)/shard_map/ppermute | solution.py:22
  42.4 1.1 %collective-permute-done.10 = bf16[2,2,2,4,2,284]{5,4,3,2,1,0:T(2,128)(2,1)S(1)} collective-permute-done((bf16[2,2,2,4,2,284]{5,4,3,2,1,0:T(2,128)(2,1)S(1)}, bf16[2,2,2,4,2,284]{5,4,3,2,1,0:T(2,128)(2,1)S(1)}, u32[]{:S(2)}, u32[]{:S(2)}) %collective-permute-start.10) | collective-permute-done | bytes 36384 | tf_op jit(solution)/shard_map/ppermute | solution.py:22
  43.7 0.6 gather_fusion.1
  47.8 0.7 collective-permute-start.6
  49.3 1.6 %collective-permute-start.12 = (bf16[2,284,70]{1,0,2:T(2,128)(2,1)S(1)}, bf16[2,284,70]{1,0,2:T(2,128)(2,1)S(1)}, u32[]{:S(2)}, u32[]{:S(2)}) collective-permute-start(bf16[2,284,70]{1,0,2:T(2,128)(2,1)S(1)} %fusion.23), channel_id=1, source_target_pairs={{0,2},{1,3},{2,0},{3,1},{4,6},{5,7},{6,4},{7,5},{8,10},{9,11},{10,... | collective-permute-start | bytes 238568 | tf_op jit(solution)/shard_map/ppermute | solution.py:104
  50.9 1.5 %collective-permute-done.6 = f32[16,1136]{1,0:T(8,128)S(1)} collective-permute-done((f32[16,1136]{1,0:T(8,128)S(1)}, f32[16,1136]{1,0:T(8,128)S(1)}, u32[]{:S(2)}, u32[]{:S(2)}) %collective-permute-start.6) | collective-permute-done | bytes 72736 | tf_op jit(solution)/shard_map/ppermute | solution.py:40
  52.4 2.3 %fusion = f32[16,1136]{1,0:T(8,128)S(1)} fusion(bf16[1136,2272]{1,0:T(8,128)(2,1)} %param.21, f32[16,1136]{1,0:T(8,128)S(1)} %fusion.123, f32[16,1136]{1,0:T(8,128)S(1)} %collective-permute-done.6), kind=kOutput, calls=%fused_computation.4 | convolution fusion | flops 42495488 | bytes 2835456 | tf_op jit(solution)/shard_map/dot_general | solution.py:216
  55.0 0.6 concatenate.81
  55.6 1.6 %collective-permute-start.13 = (bf16[2,284,70]{1,2,0:T(8,128)(2,1)S(1)}, bf16[2,284,70]{1,2,0:T(8,128)(2,1)S(1)}, u32[]{:S(2)}, u32[]{:S(2)}) collective-permute-start(bf16[2,284,70]{1,2,0:T(8,128)(2,1)S(1)} %concatenate.81), channel_id=1, source_target_pairs={{0,4},{1,5},{2,6},{3,7},{4,0},{5,1},{6,2},{7,3},{8,12},{9,13},{10,... | collective-permute-start | bytes 238568 | tf_op jit(solution)/shard_map/ppermute | solution.py:104
  57.3 2.9 %fusion.2 = f32[16,1136]{1,0:T(8,128)S(1)} fusion(bf16[1136,2272]{1,0:T(8,128)(2,1)} %param.21, f32[16,1136]{1,0:T(8,128)S(1)} %fusion.123, f32[16,1136]{1,0:T(8,128)S(1)} %collective-permute-done.6), kind=kOutput, calls=%fused_computation.6 | convolution fusion | flops 42495488 | bytes 2835456 | tf_op jit(solution)/shard_map/dot_general | solution.py:217
  63.1 2.7 %collective-permute-start.14 = (bf16[2,4,6,70]{3,2,1,0:T(8,128)(2,1)S(1)}, bf16[2,4,6,70]{3,2,1,0:T(8,128)(2,1)S(1)}, u32[]{:S(2)}, u32[]{:S(2)}) collective-permute-start(bf16[2,4,6,70]{3,2,1,0:T(8,128)(2,1)S(1)} %constant_dynamic-slice_fusion), channel_id=1, source_target_pairs={{0,8},{1,9},{2,10},{3,11},{4,12},{5,13},{6,14},{7,15},{8,0},{9,1},... | collective-permute-start | bytes 20168 | tf_op jit(solution)/shard_map/ppermute | solution.py:122
  66.3 1.5 %collective-permute-done.14 = bf16[2,4,6,70]{3,2,1,0:T(8,128)(2,1)S(1)} collective-permute-done((bf16[2,4,6,70]{3,2,1,0:T(8,128)(2,1)S(1)}, bf16[2,4,6,70]{3,2,1,0:T(8,128)(2,1)S(1)}, u32[]{:S(2)}, u32[]{:S(2)}) %collective-permute-start.14) | collective-permute-done | bytes 6752 | tf_op jit(solution)/shard_map/ppermute | solution.py:122
  68.6 0.7 collective-permute-start.15
  69.3 3.0 %collective-permute-done.15 = bf16[4,2,284]{2,0,1:T(4,128)(2,1)S(1)} collective-permute-done((bf16[4,2,284]{2,0,1:T(4,128)(2,1)S(1)}, bf16[4,2,284]{2,0,1:T(4,128)(2,1)S(1)}, u32[]{:S(2)}, u32[]{:S(2)}) %collective-permute-start.15) | collective-permute-done | bytes 4576 | tf_op jit(solution)/shard_map/ppermute | solution.py:22
  72.3 0.6 gather_fusion.2
  73.7 1.3 %collective-permute-done.16 = f32[2,2,2,4,2,284]{5,4,3,2,1,0:T(2,128)S(1)} collective-permute-done((f32[2,2,2,4,2,284]{5,4,3,2,1,0:T(2,128)S(1)}, f32[2,2,2,4,2,284]{5,4,3,2,1,0:T(2,128)S(1)}, u32[]{:S(2)}, u32[]{:S(2)}) %collective-permute-start.16) | collective-permute-done | bytes 72736 | tf_op jit(solution)/shard_map/ppermute | solution.py:57
  75.0 1.6 %collective-permute-start.17 = (f32[2,2,4,2,284]{4,3,2,1,0:T(2,128)S(1)}, f32[2,2,4,2,284]{4,3,2,1,0:T(2,128)S(1)}, u32[]{:S(2)}, u32[]{:S(2)}) collective-permute-start(f32[2,2,4,2,284]{4,3,2,1,0:T(2,128)S(1)} %fusion.36), channel_id=1, source_target_pairs={{0,2},{1,3},{2,0},{3,1},{4,6},{5,7},{6,4},{7,5},{8,10},{9,11},{10,... | collective-permute-start | bytes 109064 | tf_op jit(solution)/shard_map/ppermute | solution.py:57
  76.6 2.6 %collective-permute-done.17 = f32[2,2,4,2,284]{4,3,2,1,0:T(2,128)S(1)} collective-permute-done((f32[2,2,4,2,284]{4,3,2,1,0:T(2,128)S(1)}, f32[2,2,4,2,284]{4,3,2,1,0:T(2,128)S(1)}, u32[]{:S(2)}, u32[]{:S(2)}) %collective-permute-start.17) | collective-permute-done | bytes 36384 | tf_op jit(solution)/shard_map/ppermute | solution.py:57
  79.2 1.6 %collective-permute-start.18 = (f32[2,4,2,284]{3,2,1,0:T(2,128)S(1)}, f32[2,4,2,284]{3,2,1,0:T(2,128)S(1)}, u32[]{:S(2)}, u32[]{:S(2)}) collective-permute-start(f32[2,4,2,284]{3,2,1,0:T(2,128)S(1)} %fusion.41), channel_id=1, source_target_pairs={{0,4},{1,5},{2,6},{3,7},{4,0},{5,1},{6,2},{7,3},{8,12},{9,13},{10,... | collective-permute-start | bytes 54536 | tf_op jit(solution)/shard_map/ppermute | solution.py:57
  80.9 2.2 %collective-permute-done.18 = f32[2,4,2,284]{3,2,1,0:T(2,128)S(1)} collective-permute-done((f32[2,4,2,284]{3,2,1,0:T(2,128)S(1)}, f32[2,4,2,284]{3,2,1,0:T(2,128)S(1)}, u32[]{:S(2)}, u32[]{:S(2)}) %collective-permute-start.18) | collective-permute-done | bytes 18208 | tf_op jit(solution)/shard_map/ppermute | solution.py:57
  83.2 4.6 %collective-permute-start.19 = (f32[4,2,284]{2,1,0:T(2,128)S(1)}, f32[4,2,284]{2,1,0:T(2,128)S(1)}, u32[]{:S(2)}, u32[]{:S(2)}) collective-permute-start(f32[4,2,284]{2,1,0:T(2,128)S(1)} %get-tuple-element.68), channel_id=1, source_target_pairs={{0,0},{1,1},{2,2},{3,3},{4,4},{5,5},{6,6},{7,7},{8,16},{9,17},{10,... | collective-permute-start | bytes 27272 | tf_op jit(solution)/shard_map/ppermute | solution.py:296
  87.9 0.8 copy.250
  88.7 1.9 %collective-permute-done.19 = f32[4,2,284]{2,1,0:T(2,128)S(1)} collective-permute-done((f32[4,2,284]{2,1,0:T(2,128)S(1)}, f32[4,2,284]{2,1,0:T(2,128)S(1)}, u32[]{:S(2)}, u32[]{:S(2)}) %collective-permute-start.19) | collective-permute-done | bytes 9120 | tf_op jit(solution)/shard_map/ppermute | solution.py:296
  90.6 1.0 %collective-permute-done.20 = f32[4,2,284]{2,1,0:T(2,128)S(1)} collective-permute-done((f32[4,2,284]{2,1,0:T(2,128)S(1)}, f32[4,2,284]{2,1,0:T(2,128)S(1)}, u32[]{:S(2)}, u32[]{:S(2)}) %collective-permute-start.20) | collective-permute-done | bytes 9120 | tf_op jit(solution)/shard_map/ppermute | solution.py:296
  91.5 0.6 add_convert_fusion
  (172 shorter events, 15.1 us)
Async XLA Ops:
  0.6 72.3 %copy-start = (bf16[284,2272]{1,0:T(8,128)(2,1)S(1)}, bf16[284,2272]{1,0:T(8,128)(2,1)}, u32[]{:S(2)}) copy-start(bf16[284,2272]{1,0:T(8,128)(2,1)} %param.19) | copy-start | bytes 3871492
  0.6 3.9 %collective-permute-start = (bf16[4,2,284]{2,1,0:T(2,128)(2,1)}, bf16[4,2,284]{2,1,0:T(2,128)(2,1)S(1)}, u32[]{:S(2)}, u32[]{:S(2)}) collective-permute-start(bf16[4,2,284]{2,1,0:T(2,128)(2,1)} %param.11), channel_id=1, source_target_pairs={{0,16},{16,0},{1,17},{17,1},{2,18},{18,2},{3,19},{19,3},{4,20},{20... | collective-permute-start | bytes 13640 | tf_op jit(solution)/shard_map/ppermute | solution.py:22
  5.3 4.7 %collective-permute-start.1 = (bf16[2,4,2,284]{3,2,1,0:T(2,128)(2,1)S(1)}, bf16[2,4,2,284]{3,2,1,0:T(2,128)(2,1)S(1)}, u32[]{:S(2)}, u32[]{:S(2)}) collective-permute-start(bf16[2,4,2,284]{3,2,1,0:T(2,128)(2,1)S(1)} %pad_maximum_fusion.8), channel_id=1, source_target_pairs={{0,8},{1,9},{2,10},{3,11},{4,12},{5,13},{6,14},{7,15},{8,0},{9,1},... | collective-permute-start | bytes 27272 | tf_op jit(solution)/shard_map/ppermute | solution.py:22
  10.0 3.9 %collective-permute-start.2 = (bf16[2,2,4,2,284]{4,3,2,1,0:T(2,128)(2,1)S(1)}, bf16[2,2,4,2,284]{4,3,2,1,0:T(2,128)(2,1)S(1)}, u32[]{:S(2)}, u32[]{:S(2)}) collective-permute-start(bf16[2,2,4,2,284]{4,3,2,1,0:T(2,128)(2,1)S(1)} %pad_maximum_fusion.6), channel_id=1, source_target_pairs={{0,4},{1,5},{2,6},{3,7},{4,0},{5,1},{6,2},{7,3},{8,12},{9,13},{10,... | collective-permute-start | bytes 54536 | tf_op jit(solution)/shard_map/ppermute | solution.py:22
  13.9 4.2 %collective-permute-start.3 = (bf16[2,2,2,4,2,284]{5,4,3,2,1,0:T(2,128)(2,1)S(1)}, bf16[2,2,2,4,2,284]{5,4,3,2,1,0:T(2,128)(2,1)S(1)}, u32[]{:S(2)}, u32[]{:S(2)}) collective-permute-start(bf16[2,2,2,4,2,284]{5,4,3,2,1,0:T(2,128)(2,1)S(1)} %pad_maximum_fusion.3), channel_id=1, source_target_pairs={{0,2},{1,3},{2,0},{3,1},{4,6},{5,7},{6,4},{7,5},{8,10},{9,11},{10,... | collective-permute-start | bytes 109064 | tf_op jit(solution)/shard_map/ppermute | solution.py:22
  18.3 1.4 %collective-permute-start.4 = (bf16[2,2,2,2,4,2,284]{6,5,4,3,2,1,0:T(2,128)(2,1)S(1)}, bf16[2,2,2,2,4,2,284]{6,5,4,3,2,1,0:T(2,128)(2,1)S(1)}, u32[]{:S(2)}, u32[]{:S(2)}) collective-permute-start(bf16[2,2,2,2,4,2,284]{6,5,4,3,2,1,0:T(2,128)(2,1)S(1)} %pad_maximum_fusion.1), channel_id=1, source_target_pairs={{0,1},{1,0},{2,3},{3,2},{4,5},{5,4},{6,7},{7,6},{8,9},{9,8},{10,11... | collective-permute-start | bytes 218120 | tf_op jit(solution)/shard_map/ppermute | solution.py:22
  22.1 2.0 %copy-start.1 = (bf16[2272,128]{1,0:T(8,128)(2,1)S(1)}, bf16[2272,128]{1,0:T(8,128)(2,1)}, u32[]{:S(2)}) copy-start(bf16[2272,128]{1,0:T(8,128)(2,1)} %param.18) | copy-start | bytes 1744900
  24.5 13.6 %copy-start.2 = (bf16[2,512,128]{2,1,0:T(8,128)(2,1)S(1)}, bf16[2,512,128]{2,1,0:T(8,128)(2,1)}, u32[]{:S(2)}) copy-start(bf16[2,512,128]{2,1,0:T(8,128)(2,1)} %param.12) | copy-start | bytes 786436
  24.5 4.7 %collective-permute-start.5 = (f32[16,412]{1,0:T(8,128)S(1)}, f32[16,412]{1,0:T(8,128)S(1)}, u32[]{:S(2)}, u32[]{:S(2)}) collective-permute-start(f32[16,412]{1,0:T(8,128)S(1)} %pad_maximum_fusion.5), channel_id=1, source_target_pairs={{0,16},{16,0},{1,17},{17,1},{2,18},{18,2},{3,19},{19,3},{4,20},{20... | collective-permute-start | bytes 79112 | tf_op jit(solution)/shard_map/ppermute | solution.py:40
  29.7 4.5 %collective-permute-start.7 = (bf16[4,2,284]{2,1,0:T(2,128)(2,1)S(1)}, bf16[4,2,284]{2,1,0:T(2,128)(2,1)S(1)}, u32[]{:S(2)}, u32[]{:S(2)}) collective-permute-start(bf16[4,2,284]{2,1,0:T(2,128)(2,1)S(1)} %slice.427), channel_id=1, source_target_pairs={{0,8},{1,9},{2,10},{3,11},{4,12},{5,13},{6,14},{7,15},{8,0},{9,1},... | collective-permute-start | bytes 13640 | tf_op jit(solution)/shard_map/ppermute | solution.py:22
  34.3 3.8 %collective-permute-start.8 = (bf16[2,4,2,284]{3,2,1,0:T(2,128)(2,1)S(1)}, bf16[2,4,2,284]{3,2,1,0:T(2,128)(2,1)S(1)}, u32[]{:S(2)}, u32[]{:S(2)}) collective-permute-start(bf16[2,4,2,284]{3,2,1,0:T(2,128)(2,1)S(1)} %pad_maximum_fusion.9), channel_id=1, source_target_pairs={{0,4},{1,5},{2,6},{3,7},{4,0},{5,1},{6,2},{7,3},{8,12},{9,13},{10,... | collective-permute-start | bytes 27272 | tf_op jit(solution)/shard_map/ppermute | solution.py:22
  38.3 3.9 %collective-permute-start.9 = (bf16[2,2,4,2,284]{4,3,2,1,0:T(2,128)(2,1)S(1)}, bf16[2,2,4,2,284]{4,3,2,1,0:T(2,128)(2,1)S(1)}, u32[]{:S(2)}, u32[]{:S(2)}) collective-permute-start(bf16[2,2,4,2,284]{4,3,2,1,0:T(2,128)(2,1)S(1)} %pad_maximum_fusion.7), channel_id=1, source_target_pairs={{0,2},{1,3},{2,0},{3,1},{4,6},{5,7},{6,4},{7,5},{8,10},{9,11},{10,... | collective-permute-start | bytes 54536 | tf_op jit(solution)/shard_map/ppermute | solution.py:22
  42.2 1.3 %collective-permute-start.10 = (bf16[2,2,2,4,2,284]{5,4,3,2,1,0:T(2,128)(2,1)S(1)}, bf16[2,2,2,4,2,284]{5,4,3,2,1,0:T(2,128)(2,1)S(1)}, u32[]{:S(2)}, u32[]{:S(2)}) collective-permute-start(bf16[2,2,2,4,2,284]{5,4,3,2,1,0:T(2,128)(2,1)S(1)} %pad_maximum_fusion.4), channel_id=1, source_target_pairs={{0,1},{1,0},{2,3},{3,2},{4,5},{5,4},{6,7},{7,6},{8,9},{9,8},{10,11... | collective-permute-start | bytes 109064 | tf_op jit(solution)/shard_map/ppermute | solution.py:22
  47.5 1.4 %collective-permute-start.11 = (bf16[2,284,70]{1,0,2:T(2,128)(2,1)S(1)}, bf16[2,284,70]{1,0,2:T(2,128)(2,1)S(1)}, u32[]{:S(2)}, u32[]{:S(2)}) collective-permute-start(bf16[2,284,70]{1,0,2:T(2,128)(2,1)S(1)} %fusion.22), channel_id=1, source_target_pairs={{0,1},{1,0},{2,3},{3,2},{4,5},{5,4},{6,7},{7,6},{8,9},{9,8},{10,11... | collective-permute-start | bytes 238568 | tf_op jit(solution)/shard_map/ppermute | solution.py:104
  47.8 4.6 %collective-permute-start.6 = (f32[16,1136]{1,0:T(8,128)S(1)}, f32[16,1136]{1,0:T(8,128)S(1)}, u32[]{:S(2)}, u32[]{:S(2)}) collective-permute-start(f32[16,1136]{1,0:T(8,128)S(1)} %fusion.123), channel_id=1, source_target_pairs={{0,16},{16,0},{1,17},{17,1},{2,18},{18,2},{3,19},{19,3},{4,20},{20... | collective-permute-start | bytes 218120 | tf_op jit(solution)/shard_map/ppermute | solution.py:40
  49.3 5.4 %collective-permute-start.12 = (bf16[2,284,70]{1,0,2:T(2,128)(2,1)S(1)}, bf16[2,284,70]{1,0,2:T(2,128)(2,1)S(1)}, u32[]{:S(2)}, u32[]{:S(2)}) collective-permute-start(bf16[2,284,70]{1,0,2:T(2,128)(2,1)S(1)} %fusion.23), channel_id=1, source_target_pairs={{0,2},{1,3},{2,0},{3,1},{4,6},{5,7},{6,4},{7,5},{8,10},{9,11},{10,... | collective-permute-start | bytes 238568 | tf_op jit(solution)/shard_map/ppermute | solution.py:104
  55.6 4.8 %collective-permute-start.13 = (bf16[2,284,70]{1,2,0:T(8,128)(2,1)S(1)}, bf16[2,284,70]{1,2,0:T(8,128)(2,1)S(1)}, u32[]{:S(2)}, u32[]{:S(2)}) collective-permute-start(bf16[2,284,70]{1,2,0:T(8,128)(2,1)S(1)} %concatenate.81), channel_id=1, source_target_pairs={{0,4},{1,5},{2,6},{3,7},{4,0},{5,1},{6,2},{7,3},{8,12},{9,13},{10,... | collective-permute-start | bytes 238568 | tf_op jit(solution)/shard_map/ppermute | solution.py:104
  63.1 4.7 %collective-permute-start.14 = (bf16[2,4,6,70]{3,2,1,0:T(8,128)(2,1)S(1)}, bf16[2,4,6,70]{3,2,1,0:T(8,128)(2,1)S(1)}, u32[]{:S(2)}, u32[]{:S(2)}) collective-permute-start(bf16[2,4,6,70]{3,2,1,0:T(8,128)(2,1)S(1)} %constant_dynamic-slice_fusion), channel_id=1, source_target_pairs={{0,8},{1,9},{2,10},{3,11},{4,12},{5,13},{6,14},{7,15},{8,0},{9,1},... | collective-permute-start | bytes 20168 | tf_op jit(solution)/shard_map/ppermute | solution.py:122
  68.6 3.6 %collective-permute-start.15 = (bf16[4,2,284]{2,0,1:T(4,128)(2,1)S(1)}, bf16[4,2,284]{2,0,1:T(4,128)(2,1)S(1)}, u32[]{:S(2)}, u32[]{:S(2)}) collective-permute-start(bf16[4,2,284]{2,0,1:T(4,128)(2,1)S(1)} %get-tuple-element.74), channel_id=1, source_target_pairs={{0,16},{16,0},{1,17},{17,1},{2,18},{18,2},{3,19},{19,3},{4,20},{20... | collective-permute-start | bytes 13640 | tf_op jit(solution)/shard_map/ppermute | solution.py:22
  73.4 18.2 %copy-start.3 = (bf16[4,2,284]{2,1,0:T(2,128)(2,1)S(1)}, bf16[4,2,284]{2,1,0:T(2,128)(2,1)}, u32[]{:S(2)}) copy-start(bf16[4,2,284]{2,1,0:T(2,128)(2,1)} %param.11) | copy-start | bytes 13636
  73.5 1.4 %collective-permute-start.16 = (f32[2,2,2,4,2,284]{5,4,3,2,1,0:T(2,128)S(1)}, f32[2,2,2,4,2,284]{5,4,3,2,1,0:T(2,128)S(1)}, u32[]{:S(2)}, u32[]{:S(2)}) collective-permute-start(f32[2,2,2,4,2,284]{5,4,3,2,1,0:T(2,128)S(1)} %fusion.21), channel_id=1, source_target_pairs={{0,1},{1,0},{2,3},{3,2},{4,5},{5,4},{6,7},{7,6},{8,9},{9,8},{10,11... | collective-permute-start | bytes 218120 | tf_op jit(solution)/shard_map/ppermute | solution.py:57
  75.0 4.2 %collective-permute-start.17 = (f32[2,2,4,2,284]{4,3,2,1,0:T(2,128)S(1)}, f32[2,2,4,2,284]{4,3,2,1,0:T(2,128)S(1)}, u32[]{:S(2)}, u32[]{:S(2)}) collective-permute-start(f32[2,2,4,2,284]{4,3,2,1,0:T(2,128)S(1)} %fusion.36), channel_id=1, source_target_pairs={{0,2},{1,3},{2,0},{3,1},{4,6},{5,7},{6,4},{7,5},{8,10},{9,11},{10,... | collective-permute-start | bytes 109064 | tf_op jit(solution)/shard_map/ppermute | solution.py:57
  79.2 3.9 %collective-permute-start.18 = (f32[2,4,2,284]{3,2,1,0:T(2,128)S(1)}, f32[2,4,2,284]{3,2,1,0:T(2,128)S(1)}, u32[]{:S(2)}, u32[]{:S(2)}) collective-permute-start(f32[2,4,2,284]{3,2,1,0:T(2,128)S(1)} %fusion.41), channel_id=1, source_target_pairs={{0,4},{1,5},{2,6},{3,7},{4,0},{5,1},{6,2},{7,3},{8,12},{9,13},{10,... | collective-permute-start | bytes 54536 | tf_op jit(solution)/shard_map/ppermute | solution.py:57
  83.2 7.4 %collective-permute-start.19 = (f32[4,2,284]{2,1,0:T(2,128)S(1)}, f32[4,2,284]{2,1,0:T(2,128)S(1)}, u32[]{:S(2)}, u32[]{:S(2)}) collective-permute-start(f32[4,2,284]{2,1,0:T(2,128)S(1)} %get-tuple-element.68), channel_id=1, source_target_pairs={{0,0},{1,1},{2,2},{3,3},{4,4},{5,5},{6,6},{7,7},{8,16},{9,17},{10,... | collective-permute-start | bytes 27272 | tf_op jit(solution)/shard_map/ppermute | solution.py:296
  87.8 3.7 %collective-permute-start.20 = (f32[4,2,284]{2,1,0:T(2,128)S(1)}, f32[4,2,284]{2,1,0:T(2,128)S(1)}, u32[]{:S(2)}, u32[]{:S(2)}) collective-permute-start(f32[4,2,284]{2,1,0:T(2,128)S(1)} %get-tuple-element.67), channel_id=1, source_target_pairs={{0,16},{1,17},{2,18},{3,19},{4,20},{5,21},{6,22},{7,23},{8,0},{9,1... | collective-permute-start | bytes 27272 | tf_op jit(solution)/shard_map/ppermute | solution.py:296
